TPU v7x, 32 devices: a whole 2x2x4 slice. The times are simulated.
32 devices in a mesh: grp: 2 (over x), row: 16 (over z, y, core).
Axes of the slice: x: 2, y: 2, z: 4, core: 2. Of those that a mesh axis runs over, the one named last changes fastest.
Arguments:
- panels: bfloat16 [3, 8192, 1536], P(None, 'row'), may hold values from -0.099436891 to 0.099436891, as said below
- first_f: bfloat16 [1536, 512], P('row', 'grp'), parts along dimension 1, may hold values from -6 to 6
- first_g: bfloat16 [1536, 512], P('row', 'grp'), parts along dimension 1, may hold values from -6 to 6
- phase: float32 [4, 1536], P('grp'), parts along dimension 0, may hold values from -3.140625 to 3.140625
- wavenum: float32 [4, 1536], P('grp'), parts along dimension 0, may hold values from 0.5 to 2
Outputs:
- final_f: float32 [1536, 512], P('row', 'grp'), parts along dimension 1
- final_g: float32 [1536, 512], P('row', 'grp'), parts along dimension 1
There are 2 independent parts, one for each index of `grp`. A program takes and returns all parts, laid end to end along the dimension named above; an argument that names none is the same for every part. Nothing has to cross between parts.
Inputs may be any that keep to these rules, and one draw needn't show every extreme that they name: `panels`: consecutive sectors' surface functions share part of their shape.
All inputs are finite; a program needn't handle non-finite values.
Results may differ from a plain program's by a relative error of at most 0.013.
Values may be sent and summed in bfloat16 or wider, within the bound.
No kernel may reach another device: no remote copies, remote signals or barrier semaphores. Data moves between devices by JAX's collectives and lax.ppermute only.
A program may use at most 64 MiB of HBM per device.

v0:
```python
import jax
import jax.numpy as jnp
from jax import lax
from jax.sharding import PartitionSpec as P

SECTORS = 2


def contract_rows(left, right):
    return lax.dot_general(
        left, right, (((0,), (0,)), ((), ())), preferred_element_type=jnp.float32
    )


def shards(panels, first_f, first_g, phase, wavenum):
    chan_rows = first_f.shape[0]
    width = first_f.shape[1]
    all_channels = chan_rows * lax.axis_size("row")
    first_row = lax.axis_index("row") * chan_rows
    state = jnp.concatenate([first_f, first_g], axis=1).astype(jnp.float32)
    for sector in range(SECTORS):
        current = panels[sector]
        following = panels[sector + 1]
        solutions = state.astype(jnp.bfloat16)
        flipped = lax.psum_scatter(
            contract_rows(following, current), "row", scatter_dimension=0, tiled=True
        ).astype(jnp.bfloat16)
        rotated = jnp.dot(
            flipped,
            lax.all_gather(solutions, "row", axis=0, tiled=True),
            preferred_element_type=jnp.float32,
        )
        rot_amp = rotated[:, :width]
        rot_der = rotated[:, width:]
        angle_rows = lax.dynamic_slice_in_dim(phase[sector], first_row, chan_rows, 0)
        wave_rows = lax.dynamic_slice_in_dim(wavenum[sector], first_row, chan_rows, 0)
        cosine = jnp.cos(angle_rows)[:, None]
        sine = jnp.sin(angle_rows)[:, None]
        wave = wave_rows[:, None]
        new_amp = cosine * rot_amp + sine / wave * rot_der
        new_der = -wave * sine * rot_amp + cosine * rot_der
        local_norm = jnp.sum(new_amp * new_amp, axis=0) + jnp.sum(new_der * new_der, axis=0)
        norm = lax.psum(local_norm, "row")
        scale = 1.0 / jnp.sqrt(norm / (2.0 * all_channels) + 1e-06)
        state = jnp.concatenate([new_amp * scale[None, :], new_der * scale[None, :]], axis=1)
    return (state[:, :width], state[:, width:])


def solution(mesh):
    in_specs = (
        P(None, "row", None),
        P("row", "grp"),
        P("row", "grp"),
        P("grp", None),
        P("grp", None),
    )
    out_specs = (P("row", "grp"), P("row", "grp"))
    return jax.shard_map(shards, mesh=mesh, in_specs=in_specs, out_specs=out_specs, check_vma=False)
```

profile of v0, /device:TPU:0, one launch (start us, length us, event | category | flops | bytes accessed | tf_op | source)
XLA Modules:
  0.0 366.6 jit_solution(17294964851320102471)
XLA Ops:
  7.2 0.0 all-gather.3.cloned.1.call-start
  7.2 1.5 pad_maximum_fusion
  8.7 0.0 all-gather.3.cloned.1.call-update
  8.7 0.0 reduce-scatter.5.cloned.1.call-start
  8.8 8.2 %fusion = f32[1536,1536]{1,0:T(8,128)} fusion(bf16[3,512,1536]{2,1,0:T(8,128)(2,1)} %param.5), kind=kOutput, calls=%fused_computation | convolution fusion | flops 2415919104 | bytes 12582912 | tf_op jit(solution)/shard_map/dot_general | solution.py:10
  16.9 0.0 reduce-scatter.5.cloned.1.call-update
  17.0 0.0 reduce-scatter.3.cloned.1.call-start
  17.0 8.2 %fusion.3 = f32[1536,1536]{1,0:T(8,128)} fusion(bf16[3,512,1536]{2,1,0:T(8,128)(2,1)} %param.5), kind=kOutput, calls=%fused_computation.3 | convolution fusion | flops 2415919104 | bytes 12582912 | tf_op jit(solution)/shard_map/dot_general | solution.py:10
  25.2 0.0 copy-start
  25.2 0.0 copy-start.1
  25.2 0.0 reduce-scatter.3.cloned.1.call-update
  25.2 0.0 all-gather.5.cloned.1.call-start
  25.3 0.6 copy-done
  25.9 0.0 copy-done.1
  25.9 0.1 cosine_bitcast_fusion
  26.0 0.1 bitcast_divide_fusion.1
  26.2 27.1 %all-gather.3.cloned.1.call-done = bf16[1536,512]{1,0:T(8,128)(2,1)} async-done(((bf16[96,512]{1,0:T(8,128)(2,1)}), bf16[1536,512]{1,0:T(8,128)(2,1)}) %all-gather.3.cloned.1.call-update) | async-done | bytes 1572880 | tf_op jit(solution)/shard_map/all_gather | solution.py:30
  53.3 114.4 %reduce-scatter.5.cloned.1.call-done = f32[96,1536]{1,0:T(8,128)} async-done(((f32[1536,1536]{1,0:T(8,128)}), f32[96,1536]{1,0:T(8,128)}) %reduce-scatter.5.cloned.1.call-update) | async-done | bytes 589840 | tf_op jit(solution)/shard_map/reduce_scatter | solution.py:25
  167.6 2.0 fusion.10
  169.6 0.1 multiply_reduce_fusion.2
  169.7 32.2 %psum.14 = f32[256]{0:T(256)S(1)} all-reduce(f32[256]{0:T(256)S(1)} %add.41), channel_id=1, replica_groups=mesh['grp'=2,'row'=16] {'row'}, use_global_device_ids=true, to_apply=%region_4.0 | all-reduce | flops 256 | bytes 2048 | tf_op jit(solution)/shard_map/psum | solution.py:43
  202.0 0.1 multiply_convert_fusion.1
  202.1 0.6 pad_maximum_fusion.1
  202.7 0.0 all-gather.5.cloned.1.call-update
  202.8 0.1 cosine_bitcast_fusion.1
  202.9 0.1 bitcast_divide_fusion
  203.0 80.4 %reduce-scatter.3.cloned.1.call-done = f32[96,1536]{1,0:T(8,128)} async-done(((f32[1536,1536]{1,0:T(8,128)}), f32[96,1536]{1,0:T(8,128)}) %reduce-scatter.3.cloned.1.call-update) | async-done | bytes 589840 | tf_op jit(solution)/shard_map/reduce_scatter | solution.py:25
  283.4 42.2 %all-gather.5.cloned.1.call-done = bf16[1536,512]{1,0:T(8,128)(2,1)} async-done(((bf16[96,512]{1,0:T(8,128)(2,1)}), bf16[1536,512]{1,0:T(8,128)(2,1)}) %all-gather.5.cloned.1.call-update) | async-done | bytes 1572880 | tf_op jit(solution)/shard_map/all_gather | solution.py:30
  325.6 2.0 fusion.12
  327.6 0.1 multiply_reduce_fusion
  327.7 31.6 %psum.15 = f32[256]{0:T(256)S(1)} all-reduce(f32[256]{0:T(256)S(1)} %add.45), channel_id=1, replica_groups=mesh['grp'=2,'row'=16] {'row'}, use_global_device_ids=true, to_apply=%region_7.0 | all-reduce | flops 256 | bytes 2048 | tf_op jit(solution)/shard_map/psum | solution.py:43
  359.3 0.8 broadcast_multiply_fusion
  (5 shorter events, 0.0 us)
Async XLA Ops:
  7.2 46.1 %all-gather.3.cloned.1.call-start = ((), (), s32[]{:S(2)}) async-start(), calls=%async_computation.4 | async-start | bytes 1671168 | tf_op jit(solution)/shard_map/all_gather | solution.py:30
  8.7 158.9 %reduce-scatter.5.cloned.1.call-start = ((), (), s32[]{:S(2)}) async-start(), calls=%async_computation.3 | async-start | bytes 10027008 | tf_op jit(solution)/shard_map/reduce_scatter | solution.py:25
  17.0 266.4 %reduce-scatter.3.cloned.1.call-start = ((), (), s32[]{:S(2)}) async-start(), calls=%async_computation.2 | async-start | bytes 10027008 | tf_op jit(solution)/shard_map/reduce_scatter | solution.py:25
  25.2 0.7 copy-start
  25.2 0.7 copy-start.1
  25.2 300.4 %all-gather.5.cloned.1.call-start = ((), (), s32[]{:S(2)}) async-start(), calls=%async_computation.5 | async-start | bytes 1671168 | tf_op jit(solution)/shard_map/all_gather | solution.py:30
Sparse Core Ops, SparseCore 0:
  10.9 42.3 all-gather.2
  57.4 110.2 reduce-scatter.4
  172.3 111.0 reduce-scatter.2
  286.1 39.4 all-gather.4
where the time goes:
time: 367 us
  waiting for transfers between devices  264 us (72%)
  blocking collectives  63.8 us (17%)
  matrix products  20.3 us (6%)
  between operations  13.8 us (4%)
    reduce_scatter x2, waiting for transfers between devices, shards(): lax.psum_scatter(contract_rows(following, current), 'row', scatter_dimens...  195 us
    all_gather x2, waiting for transfers between devices, shards(): lax.all_gather(solutions, 'row', axis=0, tiled=True)  69.3 us
    psum x2, blocking collectives, shards(): norm = lax.psum(local_norm, 'row')  63.8 us
    dot_general x2, matrix products, contract_rows(): lax.dot_general(left, right, (((0,), (0,)), ((), ())), preferred_element_...  16.3 us
  transfers between devices with their start and end apart: 4, of which 4 were waited for; matrix products, arithmetic and copies ran while one was open for 5% of the time, Pallas kernels for 0%

commit v1 on v0

v1 whole, which is shorter than its diff:
```python
import jax
import jax.numpy as jnp
from jax import lax
from jax.sharding import PartitionSpec as P

SECTORS = 2


def contract_rows(left, right):
    return lax.dot_general(
        left, right, (((0,), (0,)), ((), ())), preferred_element_type=jnp.float32
    )


def shards(panels, first_f, first_g, phase, wavenum):
    chan_rows = first_f.shape[0]
    width = first_f.shape[1]
    all_channels = chan_rows * lax.axis_size("row")
    first_row = lax.axis_index("row") * chan_rows
    solutions = lax.all_gather(
        jnp.concatenate([first_f, first_g], axis=1), "row", axis=0, tiled=True
    )
    for sector in range(SECTORS):
        projected = jnp.dot(
            panels[sector], solutions, preferred_element_type=jnp.float32
        ).astype(jnp.bfloat16)
        rotated = lax.psum(contract_rows(panels[sector + 1], projected), "row")
        rot_amp = rotated[:, :width]
        rot_der = rotated[:, width:]
        cosine = jnp.cos(phase[sector])[:, None]
        sine = jnp.sin(phase[sector])[:, None]
        wave = wavenum[sector][:, None]
        new_amp = cosine * rot_amp + sine / wave * rot_der
        new_der = -wave * sine * rot_amp + cosine * rot_der
        norm = jnp.sum(new_amp * new_amp, axis=0) + jnp.sum(new_der * new_der, axis=0)
        scale = 1.0 / jnp.sqrt(norm / (2.0 * all_channels) + 1e-06)
        amp = new_amp * scale[None, :]
        der = new_der * scale[None, :]
        solutions = jnp.concatenate([amp, der], axis=1).astype(jnp.bfloat16)
    amp = lax.dynamic_slice_in_dim(amp, first_row, chan_rows, 0)
    der = lax.dynamic_slice_in_dim(der, first_row, chan_rows, 0)
    return (amp, der)


def solution(mesh):
    in_specs = (
        P(None, "row", None),
        P("row", "grp"),
        P("row", "grp"),
        P("grp", None),
        P("grp", None),
    )
    out_specs = (P("row", "grp"), P("row", "grp"))
    return jax.shard_map(shards, mesh=mesh, in_specs=in_specs, out_specs=out_specs, check_vma=False)
```

time: 367 us -> 284 us (0.77)
  blocking collectives: 63.8 us -> 0 us
  waiting for transfers between devices: 264 us -> 249 us
  matrix products: 20.3 us -> 11.3 us
  other arithmetic: 3.53 us -> 7.44 us
    psum x0 -> x2, waiting for transfers between devices: none -> 204 us  [shards(): rotated = lax.psum(contract_rows(panels[sector + 1], projected), 'row')]
    reduce_scatter x2 -> x0, waiting for transfers between devices: 195 us -> none  [shards(): lax.psum_scatter(contract_rows(following, current), 'row', scatter_dimens...]
    psum x2 -> x0, blocking collectives: 63.8 us -> none  [shards(): norm = lax.psum(local_norm, 'row')]
    all_gather x2 -> x1, waiting for transfers between devices: 69.3 us -> 44.5 us  [shards(): lax.all_gather(jnp.concatenate([first_f, first_g], axis=1), 'row', axis=0...]
    dot_general x2, matrix products: 16.3 us -> 11.3 us  [contract_rows(): lax.dot_general(left, right, (((0,), (0,)), ((), ())), preferred_element_...]
    reduce_sum x2, other arithmetic: 0.25 us -> 5.21 us  [shards(): jnp.sum(new_der * new_der, axis=0)]
    dot_general x2 -> x0, matrix products: 3.95 us -> none  [shards(): jnp.dot(flipped, lax.all_gather(solutions, 'row', axis=0, tiled=True), pr...]
  transfers between devices with their start and end apart: 4 -> 3, of which waited for: 4 -> 3; matrix products, arithmetic and copies ran while one was open for 5% -> 0% of each run, Pallas kernels for 0% -> 0%
where the time goes in v1:
time: 284 us
  waiting for transfers between devices  249 us (88%)
  between operations  13.8 us (5%)
  matrix products  11.3 us (4%)
  other arithmetic  7.44 us (3%)
    psum x2, waiting for transfers between devices, shards(): rotated = lax.psum(contract_rows(panels[sector + 1], projected), 'row')  204 us
    all_gather x1, waiting for transfers between devices, shards(): lax.all_gather(jnp.concatenate([first_f, first_g], axis=1), 'row', axis=0...  44.5 us
    dot_general x2, matrix products, contract_rows(): lax.dot_general(left, right, (((0,), (0,)), ((), ())), preferred_element_...  11.3 us
  transfers between devices with their start and end apart: 3, of which 3 were waited for; matrix products, arithmetic and copies ran while one was open for 0% of the time, Pallas kernels for 0%

profile of v1, /device:TPU:0, one launch (start us, length us, event | category | flops | bytes accessed | tf_op | source)
XLA Modules:
  0.0 283.9 jit_solution(17807892676333385672)
XLA Ops:
  7.2 0.0 all-gather.2.cloned.1.call-start
  7.2 1.5 pad_maximum_fusion
  8.7 0.0 all-gather.2.cloned.1.call-update
  8.7 0.0 all-reduce.3.cloned.1.call-start
  8.8 44.5 %all-gather.2.cloned.1.call-done = bf16[1536,512]{1,0:T(8,128)(2,1)} async-done(((bf16[96,512]{1,0:T(8,128)(2,1)}), bf16[1536,512]{1,0:T(8,128)(2,1)}) %all-gather.2.cloned.1.call-update) | async-done | bytes 1572880 | tf_op jit(solution)/shard_map/all_gather | solution.py:20
  53.3 5.9 %convolution_bitcast_fusion.1 = f32[1536,512]{0,1:T(8,128)} fusion(bf16[3,512,1536]{2,1,0:T(8,128)(2,1)} %param.5, bf16[1536,512]{1,0:T(8,128)(2,1)} %all-gather.2.cloned.1.call-done), kind=kOutput, calls=%fused_computation.1 | convolution fusion | flops 1610874880 | bytes 7864320 | tf_op jit(solution)/shard_map/dot_general | solution.py:10
  59.1 0.0 copy-start.1
  59.1 0.0 copy-start.2
  59.1 0.0 all-reduce.3.cloned.1.call-update
  59.2 0.0 all-reduce.5.cloned.1.call-start
  59.2 0.6 copy-done.1
  59.9 0.0 copy-done.2
  59.9 0.4 cosine_reduce_fusion.1
  60.3 101.2 %all-reduce.3.cloned.1.call-done = f32[1536,512]{0,1:T(8,128)} async-done(((f32[1536,512]{0,1:T(8,128)}), f32[1536,512]{0,1:T(8,128)}) %all-reduce.3.cloned.1.call-update) | async-done | bytes 3145744 | tf_op jit(solution)/shard_map/psum | solution.py:27
  161.5 0.0 copy-start
  161.5 2.7 multiply_reduce_fusion.2
  164.2 0.2 copy-done
  164.3 0.5 multiply_convert_fusion.1
  164.9 5.4 %convolution_bitcast_fusion = f32[1536,512]{0,1:T(8,128)} fusion(bf16[3,512,1536]{2,1,0:T(8,128)(2,1)} %param.5, bf16[1536,256]{0,1:T(8,128)(2,1)S(1)} %get-tuple-element.17, bf16[1536,256]{0,1:T(8,128)(2,1)S(1)} %get-tuple-element.16), kind=kOutput, calls=%fused_computation | convolution fusion | flops 1614020608 | bytes 7864320 | tf_op jit(solution)/shard_map/dot_general | solution.py:10
  170.3 0.0 all-reduce.5.cloned.1.call-update
  170.3 102.9 %all-reduce.5.cloned.1.call-done = f32[1536,512]{0,1:T(8,128)} async-done(((f32[1536,512]{0,1:T(8,128)}), f32[1536,512]{0,1:T(8,128)}) %all-reduce.5.cloned.1.call-update) | async-done | bytes 3145744 | tf_op jit(solution)/shard_map/psum | solution.py:27
  273.2 2.5 multiply_reduce_fusion
  275.7 0.2 dynamic-slice_multiply_fusion
  275.9 0.7 copy.7
  276.6 0.7 copy.8
  (5 shorter events, 0.1 us)
Async XLA Ops:
  7.2 46.1 %all-gather.2.cloned.1.call-start = ((), (), s32[]{:S(2)}) async-start(), calls=%async_computation | async-start | bytes 1671168 | tf_op jit(solution)/shard_map/all_gather | solution.py:20
  8.7 152.8 %all-reduce.3.cloned.1.call-start = ((), (), s32[]{:S(2)}) async-start(), calls=%async_computation.1 | async-start | bytes 6291456 | tf_op jit(solution)/shard_map/psum | solution.py:27
  59.1 0.7 copy-start.1
  59.1 0.7 copy-start.2
  59.2 214.0 %all-reduce.5.cloned.1.call-start = ((), (), s32[]{:S(2)}) async-start(), calls=%async_computation.2 | async-start | bytes 6291456 | tf_op jit(solution)/shard_map/psum | solution.py:27
  161.5 2.8 copy-start
Sparse Core Ops, SparseCore 0:
  10.9 42.3 all-gather.1
  59.3 102.1 all-reduce.2
  170.4 102.7 all-reduce.4

commit v2 on v0

v2 whole, which is shorter than its diff:
```python
import jax
import jax.numpy as jnp
from jax import lax
from jax.sharding import PartitionSpec as P

SECTORS = 2


def contract_rows(left, right):
    return lax.dot_general(
        left, right, (((0,), (0,)), ((), ())), preferred_element_type=jnp.float32
    )


def exchange(x, distance, devices):
    return lax.ppermute(x, "row", [(i, i ^ distance) for i in range(devices)])


def halving_reduce_scatter(z, devices):
    bits = devices.bit_length() - 1
    me = lax.axis_index("row")
    cur = z.reshape((2,) * bits + (z.shape[0] // devices, z.shape[1]))
    for bit in range(bits):
        axis = bits - 1 - bit
        mine = (me >> bit) & 1
        keep = lax.dynamic_index_in_dim(cur, mine, axis=axis, keepdims=False)
        send = lax.dynamic_index_in_dim(cur, 1 - mine, axis=axis, keepdims=False)
        cur = keep + exchange(send, 1 << bit, devices)
    return cur


def doubling_all_gather(x, devices):
    bits = devices.bit_length() - 1
    me = lax.axis_index("row")
    cur = x
    for step in range(bits):
        bit = bits - 1 - step
        other = exchange(cur, 1 << bit, devices)
        low = (me >> bit) & 1 == 0
        cur = jnp.stack(
            [jnp.where(low, cur, other), jnp.where(low, other, cur)], axis=step
        )
    return cur.reshape((-1, x.shape[-1]))


def doubling_all_reduce(x, devices):
    bits = devices.bit_length() - 1
    for bit in range(bits):
        x = x + exchange(x, 1 << bit, devices)
    return x


def shards(panels, first_f, first_g, phase, wavenum):
    chan_rows = first_f.shape[0]
    width = first_f.shape[1]
    devices = lax.axis_size("row")
    all_channels = chan_rows * devices
    first_row = lax.axis_index("row") * chan_rows
    solutions = doubling_all_gather(
        jnp.concatenate([first_f, first_g], axis=1), devices
    )
    scale = None
    for sector in range(SECTORS):
        projected = jnp.dot(panels[sector], solutions, preferred_element_type=jnp.float32)
        if scale is not None:
            projected = projected * jnp.concatenate([scale, scale])[None, :]
        rotated = halving_reduce_scatter(
            contract_rows(panels[sector + 1], projected.astype(jnp.bfloat16)), devices
        )
        rot_amp = rotated[:, :width]
        rot_der = rotated[:, width:]
        angle_rows = lax.dynamic_slice_in_dim(phase[sector], first_row, chan_rows, 0)
        wave_rows = lax.dynamic_slice_in_dim(wavenum[sector], first_row, chan_rows, 0)
        cosine = jnp.cos(angle_rows)[:, None]
        sine = jnp.sin(angle_rows)[:, None]
        wave = wave_rows[:, None]
        new_amp = cosine * rot_amp + sine / wave * rot_der
        new_der = -wave * sine * rot_amp + cosine * rot_der
        if sector + 1 < SECTORS:
            solutions = doubling_all_gather(
                jnp.concatenate([new_amp, new_der], axis=1).astype(jnp.bfloat16), devices
            )
            full = solutions.astype(jnp.float32)
            norm = jnp.sum(full[:, :width] * full[:, :width], axis=0) + jnp.sum(
                full[:, width:] * full[:, width:], axis=0
            )
        else:
            local_norm = jnp.sum(new_amp * new_amp, axis=0) + jnp.sum(new_der * new_der, axis=0)
            norm = doubling_all_reduce(local_norm, devices)
        scale = 1.0 / jnp.sqrt(norm / (2.0 * all_channels) + 1e-06)
    return (new_amp * scale[None, :], new_der * scale[None, :])


def solution(mesh):
    in_specs = (
        P(None, "row", None),
        P("row", "grp"),
        P("row", "grp"),
        P("grp", None),
        P("grp", None),
    )
    out_specs = (P("row", "grp"), P("row", "grp"))
    return jax.shard_map(shards, mesh=mesh, in_specs=in_specs, out_specs=out_specs, check_vma=False)
```

time: 367 us -> 180 us (0.49)
  waiting for transfers between devices: 264 us -> 130 us
  blocking collectives: 63.8 us -> 0 us
  starting transfers between devices: 0.16 us -> 21.5 us
  between operations: 13.8 us -> 0.95 us
  matrix products: 20.3 us -> 10.7 us
  local copies, waits for them, and re-layouts: 0.89 us -> 9.7 us
    reduce_scatter x2 -> x0, waiting for transfers between devices: 195 us -> none  [shards(): lax.psum_scatter(contract_rows(following, current), 'row', scatter_dimens...]
    ppermute x0 -> x20, waiting for transfers between devices: none -> 130 us  [exchange(): return lax.ppermute(x, 'row', [(i, i ^ distance) for i in range(devices)])]
    all_gather x2 -> x0, waiting for transfers between devices: 69.3 us -> none  [shards(): lax.all_gather(solutions, 'row', axis=0, tiled=True)]
    psum x2 -> x0, blocking collectives: 63.8 us -> none  [shards(): norm = lax.psum(local_norm, 'row')]
    ppermute x0 -> x20, starting transfers between devices: none -> 21.5 us  [exchange(): return lax.ppermute(x, 'row', [(i, i ^ distance) for i in range(devices)])]
    dot_general x2, matrix products: 16.3 us -> 10.7 us  [contract_rows(): lax.dot_general(left, right, (((0,), (0,)), ((), ())), preferred_element_...]
    dot_general x0 -> x2, local copies, waits for them, and re-layouts: none -> 4.75 us  [contract_rows(): lax.dot_general(left, right, (((0,), (0,)), ((), ())), preferred_element_...]
    dot_general x2 -> x0, matrix products: 3.95 us -> none  [shards(): jnp.dot(flipped, lax.all_gather(solutions, 'row', axis=0, tiled=True), pr...]
  transfers between devices with their start and end apart: 4 -> 20, of which waited for: 4 -> 20; matrix products, arithmetic and copies ran while one was open for 5% -> 0% of each run, Pallas kernels for 0% -> 0%
where the time goes in v2:
time: 180 us
  waiting for transfers between devices  130 us (72%)
  starting transfers between devices  21.5 us (12%)
  matrix products  10.7 us (6%)
  local copies, waits for them, and re-layouts  9.7 us (5%)
  other arithmetic  6.81 us (4%)
    ppermute x20, waiting for transfers between devices, exchange(): return lax.ppermute(x, 'row', [(i, i ^ distance) for i in range(devices)])  130 us
    ppermute x20, starting transfers between devices, exchange(): return lax.ppermute(x, 'row', [(i, i ^ distance) for i in range(devices)])  21.5 us
    dot_general x2, matrix products, contract_rows(): lax.dot_general(left, right, (((0,), (0,)), ((), ())), preferred_element_...  10.7 us
    dot_general x2, local copies, waits for them, and re-layouts, contract_rows(): lax.dot_general(left, right, (((0,), (0,)), ((), ())), preferred_element_...  4.75 us
    add x8, other arithmetic, halving_reduce_scatter(): cur = keep + exchange(send, 1 << bit, devices)  3.72 us
  transfers between devices with their start and end apart: 20, of which 20 were waited for; matrix products, arithmetic and copies ran while one was open for 0% of the time, Pallas kernels for 0%

profile of v2, /device:TPU:0, one launch (start us, length us, event | category | flops | bytes accessed | tf_op | source)
XLA Modules:
  0.0 179.9 jit_solution(12605038978951768705)
XLA Ops:
  0.6 0.8 constant_dynamic-update-slice_fusion.1
  1.4 0.8 constant_dynamic-update-slice_fusion
  2.2 4.0 %collective-permute-start = (bf16[96,512]{1,0:T(8,128)(2,1)S(1)}, bf16[96,512]{1,0:T(8,128)(2,1)S(1)}, u32[]{:S(2)}, u32[]{:S(2)}) collective-permute-start(bf16[96,512]{1,0:T(8,128)(2,1)S(1)} %constant_dynamic-update-slice_fusion), channel_id=1, source_target_pairs={{0,8},{1,9},{2,10},{3,11},{4,12},{5,13},{6,14},{7,15},{8,0},{9,1},... | collective-permute-start | bytes 294920 | tf_op jit(solution)/shard_map/ppermute | solution.py:16
  6.3 4.9 %collective-permute-done = bf16[96,512]{1,0:T(8,128)(2,1)S(1)} collective-permute-done((bf16[96,512]{1,0:T(8,128)(2,1)S(1)}, bf16[96,512]{1,0:T(8,128)(2,1)S(1)}, u32[]{:S(2)}, u32[]{:S(2)}) %collective-permute-start) | collective-permute-done | bytes 98336 | tf_op jit(solution)/shard_map/ppermute | solution.py:16
  11.2 0.8 collective-permute-start.1
  12.0 5.4 %collective-permute-done.1 = bf16[2,96,512]{2,1,0:T(8,128)(2,1)S(1)} collective-permute-done((bf16[2,96,512]{2,1,0:T(8,128)(2,1)S(1)}, bf16[2,96,512]{2,1,0:T(8,128)(2,1)S(1)}, u32[]{:S(2)}, u32[]{:S(2)}) %collective-permute-start.1) | collective-permute-done | bytes 196640 | tf_op jit(solution)/shard_map/ppermute | solution.py:16
  17.5 1.3 collective-permute-start.2
  18.8 8.1 %collective-permute-done.2 = bf16[2,2,96,512]{3,2,1,0:T(8,128)(2,1)S(1)} collective-permute-done((bf16[2,2,96,512]{3,2,1,0:T(8,128)(2,1)S(1)}, bf16[2,2,96,512]{3,2,1,0:T(8,128)(2,1)S(1)}, u32[]{:S(2)}, u32[]{:S(2)}) %collective-permute-start.2) | collective-permute-done | bytes 393248 | tf_op jit(solution)/shard_map/ppermute | solution.py:16
  27.0 0.1 pad_maximum_fusion.2
  27.1 2.3 %collective-permute-done.3 = bf16[2,2,2,96,512]{4,3,2,1,0:T(8,128)(2,1)S(1)} collective-permute-done((bf16[2,2,2,96,512]{4,3,2,1,0:T(8,128)(2,1)S(1)}, bf16[2,2,2,96,512]{4,3,2,1,0:T(8,128)(2,1)S(1)}, u32[]{:S(2)}, u32[]{:S(2)}) %collective-permute-start.3) | collective-permute-done | bytes 786464 | tf_op jit(solution)/shard_map/ppermute | solution.py:16
  29.4 0.1 select_bitcast_fusion.3
  29.5 0.2 pad_maximum_fusion
  29.7 5.4 %convolution_bitcast_fusion.1 = f32[1536,512]{0,1:T(8,128)} fusion(bf16[3,512,1536]{2,1,0:T(8,128)(2,1)} %param.5, bf16[1536,512]{1,0:T(8,128)(2,1)S(1)} %bitcast.137), kind=kOutput, calls=%fused_computation.1 | convolution fusion | flops 1610874880 | bytes 7864320 | tf_op jit(solution)/shard_map/dot_general | solution.py:10
  35.0 2.4 %copy.21 = f32[1536,512]{1,0:T(8,128)S(1)} copy(f32[1536,512]{0,1:T(8,128)} %convolution_bitcast_fusion.1) | data formatting | bytes 6291456 | tf_op jit(solution)/shard_map/dot_general | solution.py:10
  37.4 1.4 dynamic-slice_bitcast_fusion.1
  38.8 0.1 collective-permute-start.4
  38.9 3.6 %collective-permute-done.4 = f32[2,2,2,96,512]{4,3,2,1,0:T(8,128)} collective-permute-done((f32[2,2,2,96,512]{4,3,2,1,0:T(8,128)}, f32[2,2,2,96,512]{4,3,2,1,0:T(8,128)}, u32[]{:S(2)}, u32[]{:S(2)}) %collective-permute-start.4) | collective-permute-done | bytes 1572896 | tf_op jit(solution)/shard_map/ppermute | solution.py:16
  42.5 1.8 bitcast_add_fusion.1
  44.3 1.2 copy-done
  45.5 1.4 collective-permute-start.5
  46.9 18.3 %collective-permute-done.5 = f32[2,2,96,512]{3,2,1,0:T(8,128)S(1)} collective-permute-done((f32[2,2,96,512]{3,2,1,0:T(8,128)S(1)}, f32[2,2,96,512]{3,2,1,0:T(8,128)S(1)}, u32[]{:S(2)}, u32[]{:S(2)}) %collective-permute-start.5) | collective-permute-done | bytes 786464 | tf_op jit(solution)/shard_map/ppermute | solution.py:16
  65.2 1.3 bitcast_add_fusion.3
  66.5 2.3 %collective-permute-start.6 = (f32[2,96,512]{2,1,0:T(8,128)S(1)}, f32[2,96,512]{2,1,0:T(8,128)S(1)}, u32[]{:S(2)}, u32[]{:S(2)}) collective-permute-start(f32[2,96,512]{2,1,0:T(8,128)S(1)} %dynamic-slice_bitcast_fusion.5), channel_id=1, source_target_pairs={{0,4},{1,5},{2,6},{3,7},{4,0},{5,1},{6,2},{7,3},{8,12},{9,13},{10,... | collective-permute-start | bytes 1179656 | tf_op jit(solution)/shard_map/ppermute | solution.py:16
  68.9 8.6 %collective-permute-done.6 = f32[2,96,512]{2,1,0:T(8,128)S(1)} collective-permute-done((f32[2,96,512]{2,1,0:T(8,128)S(1)}, f32[2,96,512]{2,1,0:T(8,128)S(1)}, u32[]{:S(2)}, u32[]{:S(2)}) %collective-permute-start.6) | collective-permute-done | bytes 393248 | tf_op jit(solution)/shard_map/ppermute | solution.py:16
  77.4 0.1 bitcast_add_fusion.5
  77.5 3.8 %collective-permute-start.7 = (f32[96,512]{1,0:T(8,128)S(1)}, f32[96,512]{1,0:T(8,128)S(1)}, u32[]{:S(2)}, u32[]{:S(2)}) collective-permute-start(f32[96,512]{1,0:T(8,128)S(1)} %dynamic-slice_bitcast_fusion.7), channel_id=1, source_target_pairs={{0,8},{1,9},{2,10},{3,11},{4,12},{5,13},{6,14},{7,15},{8,0},{9,1},... | collective-permute-start | bytes 589832 | tf_op jit(solution)/shard_map/ppermute | solution.py:16
  81.3 0.1 cosine_bitcast_fusion
  81.4 0.1 bitcast_divide_fusion.1
  81.5 7.4 %collective-permute-done.7 = f32[96,512]{1,0:T(8,128)S(1)} collective-permute-done((f32[96,512]{1,0:T(8,128)S(1)}, f32[96,512]{1,0:T(8,128)S(1)}, u32[]{:S(2)}, u32[]{:S(2)}) %collective-permute-start.7) | collective-permute-done | bytes 196640 | tf_op jit(solution)/shard_map/ppermute | solution.py:16
  89.0 0.1 add_convert_fusion.1
  89.2 7.1 %collective-permute-done.8 = bf16[96,512]{1,0:T(8,128)(2,1)S(1)} collective-permute-done((bf16[96,512]{1,0:T(8,128)(2,1)S(1)}, bf16[96,512]{1,0:T(8,128)(2,1)S(1)}, u32[]{:S(2)}, u32[]{:S(2)}) %collective-permute-start.8) | collective-permute-done | bytes 98336 | tf_op jit(solution)/shard_map/ppermute | solution.py:16
  96.5 5.7 %collective-permute-done.9 = bf16[2,96,512]{2,1,0:T(8,128)(2,1)S(1)} collective-permute-done((bf16[2,96,512]{2,1,0:T(8,128)(2,1)S(1)}, bf16[2,96,512]{2,1,0:T(8,128)(2,1)S(1)}, u32[]{:S(2)}, u32[]{:S(2)}) %collective-permute-start.9) | collective-permute-done | bytes 196640 | tf_op jit(solution)/shard_map/ppermute | solution.py:16
  102.2 1.6 collective-permute-start.10
  103.8 6.3 %collective-permute-done.10 = bf16[2,2,96,512]{3,2,1,0:T(8,128)(2,1)S(1)} collective-permute-done((bf16[2,2,96,512]{3,2,1,0:T(8,128)(2,1)S(1)}, bf16[2,2,96,512]{3,2,1,0:T(8,128)(2,1)S(1)}, u32[]{:S(2)}, u32[]{:S(2)}) %collective-permute-start.10) | collective-permute-done | bytes 393248 | tf_op jit(solution)/shard_map/ppermute | solution.py:16
  110.1 0.1 pad_maximum_fusion.3
  110.3 2.3 %collective-permute-done.11 = bf16[2,2,2,96,512]{4,3,2,1,0:T(8,128)(2,1)S(1)} collective-permute-done((bf16[2,2,2,96,512]{4,3,2,1,0:T(8,128)(2,1)S(1)}, bf16[2,2,2,96,512]{4,3,2,1,0:T(8,128)(2,1)S(1)}, u32[]{:S(2)}, u32[]{:S(2)}) %collective-permute-start.11) | collective-permute-done | bytes 786464 | tf_op jit(solution)/shard_map/ppermute | solution.py:16
  112.6 0.1 select_bitcast_fusion.1
  112.7 0.1 pad_maximum_fusion.1
  112.8 0.1 copy.25
  113.0 0.5 bitcast_convert_fusion
  113.5 0.3 fusion
  113.8 5.4 %convolution_bitcast_fusion = f32[1536,512]{0,1:T(8,128)} fusion(bf16[3,512,1536]{2,1,0:T(8,128)(2,1)} %param.5, bf16[1536,512]{1,0:T(8,128)(2,1)S(1)} %bitcast.136, f32[512]{0:T(512)S(1)} %pad_maximum_fusion.9), kind=kOutput, calls=%fused_computation | convolution fusion | flops 1611137024 | bytes 7866368 | tf_op jit(solution)/shard_map/dot_general | solution.py:10
  119.1 2.4 %copy.26 = f32[1536,512]{1,0:T(8,128)S(1)} copy(f32[1536,512]{0,1:T(8,128)} %convolution_bitcast_fusion) | data formatting | bytes 6291456 | tf_op jit(solution)/shard_map/dot_general | solution.py:10
  121.5 0.2 dynamic-slice_bitcast_fusion
  121.7 0.2 collective-permute-start.12
  121.9 3.3 %collective-permute-done.12 = f32[2,2,2,96,512]{4,3,2,1,0:T(8,128)S(1)} collective-permute-done((f32[2,2,2,96,512]{4,3,2,1,0:T(8,128)S(1)}, f32[2,2,2,96,512]{4,3,2,1,0:T(8,128)S(1)}, u32[]{:S(2)}, u32[]{:S(2)}) %collective-permute-start.12) | collective-permute-done | bytes 1572896 | tf_op jit(solution)/shard_map/ppermute | solution.py:16
  125.2 0.3 bitcast_add_fusion
  125.6 1.6 collective-permute-start.13
  127.2 18.1 %collective-permute-done.13 = f32[2,2,96,512]{3,2,1,0:T(8,128)S(1)} collective-permute-done((f32[2,2,96,512]{3,2,1,0:T(8,128)S(1)}, f32[2,2,96,512]{3,2,1,0:T(8,128)S(1)}, u32[]{:S(2)}, u32[]{:S(2)}) %collective-permute-start.13) | collective-permute-done | bytes 786464 | tf_op jit(solution)/shard_map/ppermute | solution.py:16
  145.2 0.1 bitcast_add_fusion.2
  145.4 0.4 collective-permute-start.14
  145.9 10.0 %collective-permute-done.14 = f32[2,96,512]{2,1,0:T(8,128)S(1)} collective-permute-done((f32[2,96,512]{2,1,0:T(8,128)S(1)}, f32[2,96,512]{2,1,0:T(8,128)S(1)}, u32[]{:S(2)}, u32[]{:S(2)}) %collective-permute-start.14) | collective-permute-done | bytes 393248 | tf_op jit(solution)/shard_map/ppermute | solution.py:16
  155.9 1.3 collective-permute-start.15
  157.2 0.1 cosine_bitcast_fusion.1
  157.3 0.1 bitcast_divide_fusion
  157.4 8.7 %collective-permute-done.15 = f32[96,512]{1,0:T(8,128)S(1)} collective-permute-done((f32[96,512]{1,0:T(8,128)S(1)}, f32[96,512]{1,0:T(8,128)S(1)}, u32[]{:S(2)}, u32[]{:S(2)}) %collective-permute-start.15) | collective-permute-done | bytes 196640 | tf_op jit(solution)/shard_map/ppermute | solution.py:16
  166.1 0.1 multiply_reduce_fusion
  166.4 1.1 collective-permute-done.16
  167.5 1.5 collective-permute-start.17
  169.0 2.0 %collective-permute-done.17 = f32[256]{0:T(256)S(1)} collective-permute-done((f32[256]{0:T(256)S(1)}, f32[256]{0:T(256)S(1)}, u32[]{:S(2)}, u32[]{:S(2)}) %collective-permute-start.17) | collective-permute-done | bytes 1056 | tf_op jit(solution)/shard_map/ppermute | solution.py:16
  171.1 3.6 %collective-permute-done.18 = f32[256]{0:T(256)S(1)} collective-permute-done((f32[256]{0:T(256)S(1)}, f32[256]{0:T(256)S(1)}, u32[]{:S(2)}, u32[]{:S(2)}) %collective-permute-start.18) | collective-permute-done | bytes 1056 | tf_op jit(solution)/shard_map/ppermute | solution.py:16
  174.6 0.8 collective-permute-start.19
  175.5 3.6 %collective-permute-done.19 = f32[256]{0:T(256)S(1)} collective-permute-done((f32[256]{0:T(256)S(1)}, f32[256]{0:T(256)S(1)}, u32[]{:S(2)}, u32[]{:S(2)}) %collective-permute-start.19) | collective-permute-done | bytes 1056 | tf_op jit(solution)/shard_map/ppermute | solution.py:16
  179.1 0.8 broadcast_multiply_fusion
  (39 shorter events, 1.2 us)
Async XLA Ops:
  2.2 8.9 %collective-permute-start = (bf16[96,512]{1,0:T(8,128)(2,1)S(1)}, bf16[96,512]{1,0:T(8,128)(2,1)S(1)}, u32[]{:S(2)}, u32[]{:S(2)}) collective-permute-start(bf16[96,512]{1,0:T(8,128)(2,1)S(1)} %constant_dynamic-update-slice_fusion), channel_id=1, source_target_pairs={{0,8},{1,9},{2,10},{3,11},{4,12},{5,13},{6,14},{7,15},{8,0},{9,1},... | collective-permute-start | bytes 294920 | tf_op jit(solution)/shard_map/ppermute | solution.py:16
  11.2 6.2 %collective-permute-start.1 = (bf16[2,96,512]{2,1,0:T(8,128)(2,1)S(1)}, bf16[2,96,512]{2,1,0:T(8,128)(2,1)S(1)}, u32[]{:S(2)}, u32[]{:S(2)}) collective-permute-start(bf16[2,96,512]{2,1,0:T(8,128)(2,1)S(1)} %pad_maximum_fusion.6), channel_id=1, source_target_pairs={{0,4},{1,5},{2,6},{3,7},{4,0},{5,1},{6,2},{7,3},{8,12},{9,13},{10,... | collective-permute-start | bytes 589832 | tf_op jit(solution)/shard_map/ppermute | solution.py:16
  17.5 9.4 %collective-permute-start.2 = (bf16[2,2,96,512]{3,2,1,0:T(8,128)(2,1)S(1)}, bf16[2,2,96,512]{3,2,1,0:T(8,128)(2,1)S(1)}, u32[]{:S(2)}, u32[]{:S(2)}) collective-permute-start(bf16[2,2,96,512]{3,2,1,0:T(8,128)(2,1)S(1)} %pad_maximum_fusion.4), channel_id=1, source_target_pairs={{0,2},{1,3},{2,0},{3,1},{4,6},{5,7},{6,4},{7,5},{8,10},{9,11},{10,... | collective-permute-start | bytes 1179656 | tf_op jit(solution)/shard_map/ppermute | solution.py:16
  27.0 2.4 %collective-permute-start.3 = (bf16[2,2,2,96,512]{4,3,2,1,0:T(8,128)(2,1)S(1)}, bf16[2,2,2,96,512]{4,3,2,1,0:T(8,128)(2,1)S(1)}, u32[]{:S(2)}, u32[]{:S(2)}) collective-permute-start(bf16[2,2,2,96,512]{4,3,2,1,0:T(8,128)(2,1)S(1)} %pad_maximum_fusion.2), channel_id=1, source_target_pairs={{0,1},{1,0},{2,3},{3,2},{4,5},{5,4},{6,7},{7,6},{8,9},{9,8},{10,11... | collective-permute-start | bytes 2359304 | tf_op jit(solution)/shard_map/ppermute | solution.py:16
  38.8 3.8 %collective-permute-start.4 = (f32[2,2,2,96,512]{4,3,2,1,0:T(8,128)}, f32[2,2,2,96,512]{4,3,2,1,0:T(8,128)}, u32[]{:S(2)}, u32[]{:S(2)}) collective-permute-start(f32[2,2,2,96,512]{4,3,2,1,0:T(8,128)} %dynamic-slice_bitcast_fusion.1), channel_id=1, source_target_pairs={{0,1},{1,0},{2,3},{3,2},{4,5},{5,4},{6,7},{7,6},{8,9},{9,8},{10,11... | collective-permute-start | bytes 4718600 | tf_op jit(solution)/shard_map/ppermute | solution.py:16
  44.3 1.2 copy-start
  45.5 19.6 %collective-permute-start.5 = (f32[2,2,96,512]{3,2,1,0:T(8,128)S(1)}, f32[2,2,96,512]{3,2,1,0:T(8,128)S(1)}, u32[]{:S(2)}, u32[]{:S(2)}) collective-permute-start(f32[2,2,96,512]{3,2,1,0:T(8,128)S(1)} %dynamic-slice_bitcast_fusion.3), channel_id=1, source_target_pairs={{0,2},{1,3},{2,0},{3,1},{4,6},{5,7},{6,4},{7,5},{8,10},{9,11},{10,... | collective-permute-start | bytes 2359304 | tf_op jit(solution)/shard_map/ppermute | solution.py:16
  46.9 21.9 %copy-start.1 = (f32[2,1536]{1,0:T(2,128)S(1)}, f32[2,1536]{1,0:T(2,128)}, u32[]{:S(2)}) copy-start(f32[2,1536]{1,0:T(2,128)} %param.9) | copy-start | bytes 36868
  46.9 21.9 %copy-start.2 = (f32[2,1536]{1,0:T(2,128)S(1)}, f32[2,1536]{1,0:T(2,128)}, u32[]{:S(2)}) copy-start(f32[2,1536]{1,0:T(2,128)} %param.8) | copy-start | bytes 36868
  66.5 10.9 %collective-permute-start.6 = (f32[2,96,512]{2,1,0:T(8,128)S(1)}, f32[2,96,512]{2,1,0:T(8,128)S(1)}, u32[]{:S(2)}, u32[]{:S(2)}) collective-permute-start(f32[2,96,512]{2,1,0:T(8,128)S(1)} %dynamic-slice_bitcast_fusion.5), channel_id=1, source_target_pairs={{0,4},{1,5},{2,6},{3,7},{4,0},{5,1},{6,2},{7,3},{8,12},{9,13},{10,... | collective-permute-start | bytes 1179656 | tf_op jit(solution)/shard_map/ppermute | solution.py:16
  77.5 11.4 %collective-permute-start.7 = (f32[96,512]{1,0:T(8,128)S(1)}, f32[96,512]{1,0:T(8,128)S(1)}, u32[]{:S(2)}, u32[]{:S(2)}) collective-permute-start(f32[96,512]{1,0:T(8,128)S(1)} %dynamic-slice_bitcast_fusion.7), channel_id=1, source_target_pairs={{0,8},{1,9},{2,10},{3,11},{4,12},{5,13},{6,14},{7,15},{8,0},{9,1},... | collective-permute-start | bytes 589832 | tf_op jit(solution)/shard_map/ppermute | solution.py:16
  89.1 7.2 %collective-permute-start.8 = (bf16[96,512]{1,0:T(8,128)(2,1)S(1)}, bf16[96,512]{1,0:T(8,128)(2,1)S(1)}, u32[]{:S(2)}, u32[]{:S(2)}) collective-permute-start(bf16[96,512]{1,0:T(8,128)(2,1)S(1)} %pad_maximum_fusion.8), channel_id=1, source_target_pairs={{0,8},{1,9},{2,10},{3,11},{4,12},{5,13},{6,14},{7,15},{8,0},{9,1},... | collective-permute-start | bytes 294920 | tf_op jit(solution)/shard_map/ppermute | solution.py:16
  96.4 5.7 %collective-permute-start.9 = (bf16[2,96,512]{2,1,0:T(8,128)(2,1)S(1)}, bf16[2,96,512]{2,1,0:T(8,128)(2,1)S(1)}, u32[]{:S(2)}, u32[]{:S(2)}) collective-permute-start(bf16[2,96,512]{2,1,0:T(8,128)(2,1)S(1)} %pad_maximum_fusion.7), channel_id=1, source_target_pairs={{0,4},{1,5},{2,6},{3,7},{4,0},{5,1},{6,2},{7,3},{8,12},{9,13},{10,... | collective-permute-start | bytes 589832 | tf_op jit(solution)/shard_map/ppermute | solution.py:16
  102.2 7.8 %collective-permute-start.10 = (bf16[2,2,96,512]{3,2,1,0:T(8,128)(2,1)S(1)}, bf16[2,2,96,512]{3,2,1,0:T(8,128)(2,1)S(1)}, u32[]{:S(2)}, u32[]{:S(2)}) collective-permute-start(bf16[2,2,96,512]{3,2,1,0:T(8,128)(2,1)S(1)} %pad_maximum_fusion.5), channel_id=1, source_target_pairs={{0,2},{1,3},{2,0},{3,1},{4,6},{5,7},{6,4},{7,5},{8,10},{9,11},{10,... | collective-permute-start | bytes 1179656 | tf_op jit(solution)/shard_map/ppermute | solution.py:16
  110.2 2.4 %collective-permute-start.11 = (bf16[2,2,2,96,512]{4,3,2,1,0:T(8,128)(2,1)S(1)}, bf16[2,2,2,96,512]{4,3,2,1,0:T(8,128)(2,1)S(1)}, u32[]{:S(2)}, u32[]{:S(2)}) collective-permute-start(bf16[2,2,2,96,512]{4,3,2,1,0:T(8,128)(2,1)S(1)} %pad_maximum_fusion.3), channel_id=1, source_target_pairs={{0,1},{1,0},{2,3},{3,2},{4,5},{5,4},{6,7},{7,6},{8,9},{9,8},{10,11... | collective-permute-start | bytes 2359304 | tf_op jit(solution)/shard_map/ppermute | solution.py:16
  121.7 3.5 %collective-permute-start.12 = (f32[2,2,2,96,512]{4,3,2,1,0:T(8,128)S(1)}, f32[2,2,2,96,512]{4,3,2,1,0:T(8,128)S(1)}, u32[]{:S(2)}, u32[]{:S(2)}) collective-permute-start(f32[2,2,2,96,512]{4,3,2,1,0:T(8,128)S(1)} %dynamic-slice_bitcast_fusion), channel_id=1, source_target_pairs={{0,1},{1,0},{2,3},{3,2},{4,5},{5,4},{6,7},{7,6},{8,9},{9,8},{10,11... | collective-permute-start | bytes 4718600 | tf_op jit(solution)/shard_map/ppermute | solution.py:16
  125.6 19.6 %collective-permute-start.13 = (f32[2,2,96,512]{3,2,1,0:T(8,128)S(1)}, f32[2,2,96,512]{3,2,1,0:T(8,128)S(1)}, u32[]{:S(2)}, u32[]{:S(2)}) collective-permute-start(f32[2,2,96,512]{3,2,1,0:T(8,128)S(1)} %dynamic-slice_bitcast_fusion.2), channel_id=1, source_target_pairs={{0,2},{1,3},{2,0},{3,1},{4,6},{5,7},{6,4},{7,5},{8,10},{9,11},{10,... | collective-permute-start | bytes 2359304 | tf_op jit(solution)/shard_map/ppermute | solution.py:16
  145.4 10.4 %collective-permute-start.14 = (f32[2,96,512]{2,1,0:T(8,128)S(1)}, f32[2,96,512]{2,1,0:T(8,128)S(1)}, u32[]{:S(2)}, u32[]{:S(2)}) collective-permute-start(f32[2,96,512]{2,1,0:T(8,128)S(1)} %dynamic-slice_bitcast_fusion.4), channel_id=1, source_target_pairs={{0,4},{1,5},{2,6},{3,7},{4,0},{5,1},{6,2},{7,3},{8,12},{9,13},{10,... | collective-permute-start | bytes 1179656 | tf_op jit(solution)/shard_map/ppermute | solution.py:16
  155.9 10.2 %collective-permute-start.15 = (f32[96,512]{1,0:T(8,128)S(1)}, f32[96,512]{1,0:T(8,128)S(1)}, u32[]{:S(2)}, u32[]{:S(2)}) collective-permute-start(f32[96,512]{1,0:T(8,128)S(1)} %dynamic-slice_bitcast_fusion.6), channel_id=1, source_target_pairs={{0,8},{1,9},{2,10},{3,11},{4,12},{5,13},{6,14},{7,15},{8,0},{9,1},... | collective-permute-start | bytes 589832 | tf_op jit(solution)/shard_map/ppermute | solution.py:16
  166.3 1.2 collective-permute-start.16
  167.5 3.6 %collective-permute-start.17 = (f32[256]{0:T(256)S(1)}, f32[256]{0:T(256)S(1)}, u32[]{:S(2)}, u32[]{:S(2)}) collective-permute-start(f32[256]{0:T(256)S(1)} %add.130), channel_id=1, source_target_pairs={{0,2},{1,3},{2,0},{3,1},{4,6},{5,7},{6,4},{7,5},{8,10},{9,11},{10,... | collective-permute-start | bytes 3080 | tf_op jit(solution)/shard_map/ppermute | solution.py:16
  171.1 3.6 %collective-permute-start.18 = (f32[256]{0:T(256)S(1)}, f32[256]{0:T(256)S(1)}, u32[]{:S(2)}, u32[]{:S(2)}) collective-permute-start(f32[256]{0:T(256)S(1)} %add.131), channel_id=1, source_target_pairs={{0,4},{1,5},{2,6},{3,7},{4,0},{5,1},{6,2},{7,3},{8,12},{9,13},{10,... | collective-permute-start | bytes 3080 | tf_op jit(solution)/shard_map/ppermute | solution.py:16
  174.6 4.5 %collective-permute-start.19 = (f32[256]{0:T(256)S(1)}, f32[256]{0:T(256)S(1)}, u32[]{:S(2)}, u32[]{:S(2)}) collective-permute-start(f32[256]{0:T(256)S(1)} %add.132), channel_id=1, source_target_pairs={{0,8},{1,9},{2,10},{3,11},{4,12},{5,13},{6,14},{7,15},{8,0},{9,1},... | collective-permute-start | bytes 3080 | tf_op jit(solution)/shard_map/ppermute | solution.py:16

commit v3 on v2

v3 whole, which is shorter than its diff:
```python
import jax
import jax.numpy as jnp
from jax import lax
from jax.sharding import PartitionSpec as P

SECTORS = 2


def contract_rows(left, right):
    return lax.dot_general(
        left, right, (((0,), (0,)), ((), ())), preferred_element_type=jnp.float32
    )


def exchange(x, distance, devices):
    return lax.ppermute(x, "row", [(i, i ^ distance) for i in range(devices)])


def halving_reduce_scatter(z, devices, order):
    bits = devices.bit_length() - 1
    me = lax.axis_index("row")
    cur = z.reshape((2,) * bits + (z.shape[0] // devices, z.shape[1]))
    left = list(range(bits - 1, -1, -1))
    for bit in order:
        axis = left.index(bit)
        left.remove(bit)
        mine = (me >> bit) & 1
        keep = lax.dynamic_index_in_dim(cur, mine, axis=axis, keepdims=False)
        send = lax.dynamic_index_in_dim(cur, 1 - mine, axis=axis, keepdims=False)
        cur = keep + exchange(send, 1 << bit, devices)
    return cur


def doubling_all_gather(x, devices, order):
    me = lax.axis_index("row")
    cur = x
    done = []
    for bit in order:
        other = exchange(cur, 1 << bit, devices)
        low = (me >> bit) & 1 == 0
        axis = sum(1 for b in done if b > bit)
        done.append(bit)
        cur = jnp.stack(
            [jnp.where(low, cur, other), jnp.where(low, other, cur)], axis=axis
        )
    return cur.reshape((-1, x.shape[-1]))


def doubling_all_reduce(x, devices):
    bits = devices.bit_length() - 1
    for bit in range(bits):
        x = x + exchange(x, 1 << bit, devices)
    return x


def stage_orders(devices):
    bits = list(range(devices.bit_length() - 1))
    if len(bits) < 3:
        return bits, bits
    return bits, [bits[0], bits[2], bits[1]] + bits[3:]


def shards(panels, first_f, first_g, phase, wavenum):
    chan_rows = first_f.shape[0]
    width = first_f.shape[1]
    devices = lax.axis_size("row")
    all_channels = chan_rows * devices
    first_row = lax.axis_index("row") * chan_rows
    order_amp, order_der = stage_orders(devices)
    amp_full = doubling_all_gather(first_f, devices, order_amp[::-1])
    der_full = doubling_all_gather(first_g, devices, order_der[::-1])
    scale = None
    for sector in range(SECTORS):
        solutions = jnp.concatenate([amp_full, der_full], axis=1)
        projected = jnp.dot(panels[sector], solutions, preferred_element_type=jnp.float32)
        if scale is not None:
            projected = projected * jnp.concatenate([scale, scale])[None, :]
        partial = contract_rows(panels[sector + 1], projected.astype(jnp.bfloat16))
        rot_amp = halving_reduce_scatter(partial[:, :width], devices, order_amp)
        rot_der = halving_reduce_scatter(partial[:, width:], devices, order_der)
        angle_rows = lax.dynamic_slice_in_dim(phase[sector], first_row, chan_rows, 0)
        wave_rows = lax.dynamic_slice_in_dim(wavenum[sector], first_row, chan_rows, 0)
        cosine = jnp.cos(angle_rows)[:, None]
        sine = jnp.sin(angle_rows)[:, None]
        wave = wave_rows[:, None]
        new_amp = cosine * rot_amp + sine / wave * rot_der
        new_der = -wave * sine * rot_amp + cosine * rot_der
        if sector + 1 < SECTORS:
            amp_full = doubling_all_gather(new_amp.astype(jnp.bfloat16), devices, order_amp[::-1])
            der_full = doubling_all_gather(new_der.astype(jnp.bfloat16), devices, order_der[::-1])
            amp_wide = amp_full.astype(jnp.float32)
            der_wide = der_full.astype(jnp.float32)
            norm = jnp.sum(amp_wide * amp_wide, axis=0) + jnp.sum(der_wide * der_wide, axis=0)
        else:
            local_norm = jnp.sum(new_amp * new_amp, axis=0) + jnp.sum(new_der * new_der, axis=0)
            norm = doubling_all_reduce(local_norm, devices)
        scale = 1.0 / jnp.sqrt(norm / (2.0 * all_channels) + 1e-06)
    return (new_amp * scale[None, :], new_der * scale[None, :])


def solution(mesh):
    in_specs = (
        P(None, "row", None),
        P("row", "grp"),
        P("row", "grp"),
        P("grp", None),
        P("grp", None),
    )
    out_specs = (P("row", "grp"), P("row", "grp"))
    return jax.shard_map(shards, mesh=mesh, in_specs=in_specs, out_specs=out_specs, check_vma=False)
```

time: 180 us -> 146 us (0.81)
  waiting for transfers between devices: 130 us -> 78.4 us
  starting transfers between devices: 21.5 us -> 33 us
  local copies, waits for them, and re-layouts: 9.7 us -> 14.9 us
    ppermute x20 -> x36, waiting for transfers between devices: 130 us -> 78.4 us  [exchange(): return lax.ppermute(x, 'row', [(i, i ^ distance) for i in range(devices)])]
    ppermute x20 -> x36, starting transfers between devices: 21.5 us -> 33 us  [exchange(): return lax.ppermute(x, 'row', [(i, i ^ distance) for i in range(devices)])]
    slice x1 -> x7, local copies, waits for them, and re-layouts: 0.02 us -> 11.2 us  [the longest x3 5.58 us: shards(): rot_der = halving_reduce_scatter(partial[:, width:], devices, order_der)]
    dot_general x2 -> x0, local copies, waits for them, and re-layouts: 4.75 us -> none  [contract_rows(): lax.dot_general(left, right, (((0,), (0,)), ((), ())), preferred_element_...]
    add x8 -> x12, other arithmetic: 3.72 us -> 3.99 us  [halving_reduce_scatter(): cur = keep + exchange(send, 1 << bit, devices)]
  transfers between devices with their start and end apart: 20 -> 36, of which waited for: 20 -> 27; matrix products, arithmetic and copies ran while one was open for 0% -> 7% of each run, Pallas kernels for 0% -> 0%
where the time goes in v3:
time: 146 us
  waiting for transfers between devices  78.4 us (54%)
  starting transfers between devices  33 us (23%)
  local copies, waits for them, and re-layouts  14.9 us (10%)
  matrix products  10.7 us (7%)
  other arithmetic  7.64 us (5%)
    ppermute x36, waiting for transfers between devices, exchange(): return lax.ppermute(x, 'row', [(i, i ^ distance) for i in range(devices)])  78.4 us
    ppermute x36, starting transfers between devices, exchange(): return lax.ppermute(x, 'row', [(i, i ^ distance) for i in range(devices)])  33 us
    dot_general x2, matrix products, contract_rows(): lax.dot_general(left, right, (((0,), (0,)), ((), ())), preferred_element_...  10.7 us
    slice x3, local copies, waits for them, and re-layouts, shards(): rot_der = halving_reduce_scatter(partial[:, width:], devices, order_der)  5.58 us
    slice x3, local copies, waits for them, and re-layouts, shards(): rot_amp = halving_reduce_scatter(partial[:, :width], devices, order_amp)  5.58 us
    add x12, other arithmetic, halving_reduce_scatter(): cur = keep + exchange(send, 1 << bit, devices)  3.99 us
  transfers between devices with their start and end apart: 36, of which 27 were waited for; matrix products, arithmetic and copies ran while one was open for 7% of the time, Pallas kernels for 0%

profile of v3, /device:TPU:0, one launch (start us, length us, event | category | flops | bytes accessed | tf_op | source)
XLA Modules:
  0.0 145.9 jit_solution(7554438361671553255)
XLA Ops:
  0.6 4.1 %collective-permute-start = (bf16[96,256]{1,0:T(8,128)(2,1)}, bf16[96,256]{1,0:T(8,128)(2,1)S(1)}, u32[]{:S(2)}, u32[]{:S(2)}) collective-permute-start(bf16[96,256]{1,0:T(8,128)(2,1)} %param.6), channel_id=1, source_target_pairs={{0,8},{1,9},{2,10},{3,11},{4,12},{5,13},{6,14},{7,15},{8,0},{9,1},... | collective-permute-start | bytes 147464 | tf_op jit(solution)/shard_map/ppermute | solution.py:16
  4.8 2.7 %collective-permute-done = bf16[96,256]{1,0:T(8,128)(2,1)S(1)} collective-permute-done((bf16[96,256]{1,0:T(8,128)(2,1)}, bf16[96,256]{1,0:T(8,128)(2,1)S(1)}, u32[]{:S(2)}, u32[]{:S(2)}) %collective-permute-start) | collective-permute-done | bytes 49184 | tf_op jit(solution)/shard_map/ppermute | solution.py:16
  7.5 2.5 %collective-permute-done.4 = bf16[96,256]{1,0:T(8,128)(2,1)S(1)} collective-permute-done((bf16[96,256]{1,0:T(8,128)(2,1)}, bf16[96,256]{1,0:T(8,128)(2,1)S(1)}, u32[]{:S(2)}, u32[]{:S(2)}) %collective-permute-start.4) | collective-permute-done | bytes 49184 | tf_op jit(solution)/shard_map/ppermute | solution.py:16
  10.1 0.8 select_bitcast_fusion.29
  10.9 1.6 %collective-permute-start.5 = (bf16[2,96,256]{2,1,0:T(8,128)(2,1)S(1)}, bf16[2,96,256]{2,1,0:T(8,128)(2,1)S(1)}, u32[]{:S(2)}, u32[]{:S(2)}) collective-permute-start(bf16[2,96,256]{2,1,0:T(8,128)(2,1)S(1)} %pad_maximum_fusion.13), channel_id=1, source_target_pairs={{0,2},{1,3},{2,0},{3,1},{4,6},{5,7},{6,4},{7,5},{8,10},{9,11},{10,... | collective-permute-start | bytes 294920 | tf_op jit(solution)/shard_map/ppermute | solution.py:16
  12.5 1.5 %collective-permute-start.1 = (bf16[2,96,256]{2,1,0:T(8,128)(2,1)S(1)}, bf16[2,96,256]{2,1,0:T(8,128)(2,1)S(1)}, u32[]{:S(2)}, u32[]{:S(2)}) collective-permute-start(bf16[2,96,256]{2,1,0:T(8,128)(2,1)S(1)} %pad_maximum_fusion.12), channel_id=1, source_target_pairs={{0,4},{1,5},{2,6},{3,7},{4,0},{5,1},{6,2},{7,3},{8,12},{9,13},{10,... | collective-permute-start | bytes 294920 | tf_op jit(solution)/shard_map/ppermute | solution.py:16
  14.0 1.6 %collective-permute-done.5 = bf16[2,96,256]{2,1,0:T(8,128)(2,1)S(1)} collective-permute-done((bf16[2,96,256]{2,1,0:T(8,128)(2,1)S(1)}, bf16[2,96,256]{2,1,0:T(8,128)(2,1)S(1)}, u32[]{:S(2)}, u32[]{:S(2)}) %collective-permute-start.5) | collective-permute-done | bytes 98336 | tf_op jit(solution)/shard_map/ppermute | solution.py:16
  15.7 1.5 %collective-permute-start.6 = (bf16[2,2,96,256]{3,2,1,0:T(8,128)(2,1)S(1)}, bf16[2,2,96,256]{3,2,1,0:T(8,128)(2,1)S(1)}, u32[]{:S(2)}, u32[]{:S(2)}) collective-permute-start(bf16[2,2,96,256]{3,2,1,0:T(8,128)(2,1)S(1)} %pad_maximum_fusion.9), channel_id=1, source_target_pairs={{0,4},{1,5},{2,6},{3,7},{4,0},{5,1},{6,2},{7,3},{8,12},{9,13},{10,... | collective-permute-start | bytes 589832 | tf_op jit(solution)/shard_map/ppermute | solution.py:16
  17.2 1.1 collective-permute-done.1
  18.3 0.5 collective-permute-start.2
  18.8 2.6 %collective-permute-done.6 = bf16[2,2,96,256]{3,2,1,0:T(8,128)(2,1)S(1)} collective-permute-done((bf16[2,2,96,256]{3,2,1,0:T(8,128)(2,1)S(1)}, bf16[2,2,96,256]{3,2,1,0:T(8,128)(2,1)S(1)}, u32[]{:S(2)}, u32[]{:S(2)}) %collective-permute-start.6) | collective-permute-done | bytes 196640 | tf_op jit(solution)/shard_map/ppermute | solution.py:16
  21.5 2.5 %collective-permute-done.2 = bf16[2,2,96,256]{3,2,0,1:T(8,128)(2,1)S(1)} collective-permute-done((bf16[2,2,96,256]{3,2,0,1:T(8,128)(2,1)S(1)}, bf16[2,2,96,256]{3,2,0,1:T(8,128)(2,1)S(1)}, u32[]{:S(2)}, u32[]{:S(2)}) %collective-permute-start.2) | collective-permute-done | bytes 196640 | tf_op jit(solution)/shard_map/ppermute | solution.py:16
  24.5 1.5 %collective-permute-done.3 = bf16[2,2,2,96,256]{4,3,2,1,0:T(8,128)(2,1)S(1)} collective-permute-done((bf16[2,2,2,96,256]{4,3,2,1,0:T(8,128)(2,1)S(1)}, bf16[2,2,2,96,256]{4,3,2,1,0:T(8,128)(2,1)S(1)}, u32[]{:S(2)}, u32[]{:S(2)}) %collective-permute-start.3) | collective-permute-done | bytes 393248 | tf_op jit(solution)/shard_map/ppermute | solution.py:16
  26.2 5.4 %convolution_bitcast_fusion.1 = f32[1536,512]{0,1:T(8,128)} fusion(bf16[3,512,1536]{2,1,0:T(8,128)(2,1)} %param.5, bf16[1536,256]{1,0:T(8,128)(2,1)S(1)} %bitcast.221, bf16[1536,256]{1,0:T(8,128)(2,1)S(1)} %bitcast.224), kind=kOutput, calls=%fused_computation.1 | convolution fusion | flops 1614020608 | bytes 7864320 | tf_op jit(solution)/shard_map/dot_general | solution.py:10
  31.5 3.2 %fusion.49 = (f32[1536,256]{0,1:T(8,128)S(1)}, f32[1536,256]{0,1:T(8,128)}) fusion(f32[1536,512]{0,1:T(8,128)} %convolution_bitcast_fusion.1), kind=kLoop, calls=%fused_computation.132 | loop fusion | bytes 6291456 | tf_op jit(solution)/shard_map/slice | solution.py:80
  34.8 0.5 copy.37
  35.3 1.0 dynamic-slice_bitcast_fusion.2
  36.4 1.9 %copy.36 = f32[1536,256]{1,0:T(8,128)S(1)} copy(f32[1536,256]{0,1:T(8,128)} %get-tuple-element.9) | data formatting | bytes 3145728 | tf_op jit(solution)/shard_map/slice | solution.py:79
  39.0 1.2 bitcast_add_fusion.2
  40.3 1.3 collective-permute-start.13
  42.0 9.7 %collective-permute-done.13 = f32[2,2,96,256]{3,2,1,0:T(8,128)S(1)} collective-permute-done((f32[2,2,96,256]{3,2,1,0:T(8,128)S(1)}, f32[2,2,96,256]{3,2,1,0:T(8,128)S(1)}, u32[]{:S(2)}, u32[]{:S(2)}) %collective-permute-start.13) | collective-permute-done | bytes 393248 | tf_op jit(solution)/shard_map/ppermute | solution.py:16
  51.8 1.0 bitcast_add_fusion.6
  52.9 0.5 collective-permute-start.14
  53.5 0.9 collective-permute-start.10
  54.4 4.9 %collective-permute-done.14 = f32[2,96,256]{2,1,0:T(8,128)S(1)} collective-permute-done((f32[2,96,256]{2,1,0:T(8,128)S(1)}, f32[2,96,256]{2,1,0:T(8,128)S(1)}, u32[]{:S(2)}, u32[]{:S(2)}) %collective-permute-start.14) | collective-permute-done | bytes 196640 | tf_op jit(solution)/shard_map/ppermute | solution.py:16
  59.4 1.6 %collective-permute-start.15 = (f32[96,256]{1,0:T(8,128)S(1)}, f32[96,256]{1,0:T(8,128)S(1)}, u32[]{:S(2)}, u32[]{:S(2)}) collective-permute-start(f32[96,256]{1,0:T(8,128)S(1)} %dynamic-slice_bitcast_fusion.14), channel_id=1, source_target_pairs={{0,8},{1,9},{2,10},{3,11},{4,12},{5,13},{6,14},{7,15},{8,0},{9,1},... | collective-permute-start | bytes 294920 | tf_op jit(solution)/shard_map/ppermute | solution.py:16
  61.0 1.5 %collective-permute-start.11 = (f32[96,256]{1,0:T(8,128)S(1)}, f32[96,256]{1,0:T(8,128)S(1)}, u32[]{:S(2)}, u32[]{:S(2)}) collective-permute-start(f32[96,256]{1,0:T(8,128)S(1)} %dynamic-slice_bitcast_fusion.15), channel_id=1, source_target_pairs={{0,8},{1,9},{2,10},{3,11},{4,12},{5,13},{6,14},{7,15},{8,0},{9,1},... | collective-permute-start | bytes 294920 | tf_op jit(solution)/shard_map/ppermute | solution.py:16
  62.5 0.8 cosine_bitcast_fusion
  63.3 5.7 %collective-permute-done.15 = f32[96,256]{1,0:T(8,128)S(1)} collective-permute-done((f32[96,256]{1,0:T(8,128)S(1)}, f32[96,256]{1,0:T(8,128)S(1)}, u32[]{:S(2)}, u32[]{:S(2)}) %collective-permute-start.15) | collective-permute-done | bytes 98336 | tf_op jit(solution)/shard_map/ppermute | solution.py:16
  68.9 1.1 collective-permute-done.11
  70.2 2.9 %collective-permute-start.20 = (bf16[96,256]{1,0:T(8,128)(2,1)S(1)}, bf16[96,256]{1,0:T(8,128)(2,1)S(1)}, u32[]{:S(2)}, u32[]{:S(2)}) collective-permute-start(bf16[96,256]{1,0:T(8,128)(2,1)S(1)} %get-tuple-element.21), channel_id=1, source_target_pairs={{0,8},{1,9},{2,10},{3,11},{4,12},{5,13},{6,14},{7,15},{8,0},{9,1},... | collective-permute-start | bytes 147464 | tf_op jit(solution)/shard_map/ppermute | solution.py:16
  73.1 2.2 %collective-permute-done.16 = bf16[96,256]{1,0:T(8,128)(2,1)S(1)} collective-permute-done((bf16[96,256]{1,0:T(8,128)(2,1)S(1)}, bf16[96,256]{1,0:T(8,128)(2,1)S(1)}, u32[]{:S(2)}, u32[]{:S(2)}) %collective-permute-start.16) | collective-permute-done | bytes 49184 | tf_op jit(solution)/shard_map/ppermute | solution.py:16
  75.4 1.0 collective-permute-done.20
  76.5 0.6 collective-permute-start.21
  77.1 2.9 %collective-permute-done.17 = bf16[2,96,256]{2,1,0:T(8,128)(2,1)S(1)} collective-permute-done((bf16[2,96,256]{2,1,0:T(8,128)(2,1)S(1)}, bf16[2,96,256]{2,1,0:T(8,128)(2,1)S(1)}, u32[]{:S(2)}, u32[]{:S(2)}) %collective-permute-start.17) | collective-permute-done | bytes 98336 | tf_op jit(solution)/shard_map/ppermute | solution.py:16
  80.0 1.3 collective-permute-start.18
  81.3 0.8 collective-permute-done.21
  82.2 1.7 %collective-permute-start.22 = (bf16[2,2,96,256]{3,2,1,0:T(8,128)(2,1)S(1)}, bf16[2,2,96,256]{3,2,1,0:T(8,128)(2,1)S(1)}, u32[]{:S(2)}, u32[]{:S(2)}) collective-permute-start(bf16[2,2,96,256]{3,2,1,0:T(8,128)(2,1)S(1)} %pad_maximum_fusion.11), channel_id=1, source_target_pairs={{0,4},{1,5},{2,6},{3,7},{4,0},{5,1},{6,2},{7,3},{8,12},{9,13},{10,... | collective-permute-start | bytes 589832 | tf_op jit(solution)/shard_map/ppermute | solution.py:16
  83.9 1.9 %collective-permute-done.18 = bf16[2,2,96,256]{3,2,0,1:T(8,128)(2,1)S(1)} collective-permute-done((bf16[2,2,96,256]{3,2,0,1:T(8,128)(2,1)S(1)}, bf16[2,2,96,256]{3,2,0,1:T(8,128)(2,1)S(1)}, u32[]{:S(2)}, u32[]{:S(2)}) %collective-permute-start.18) | collective-permute-done | bytes 196640 | tf_op jit(solution)/shard_map/ppermute | solution.py:16
  85.9 2.0 %collective-permute-done.22 = bf16[2,2,96,256]{3,2,1,0:T(8,128)(2,1)S(1)} collective-permute-done((bf16[2,2,96,256]{3,2,1,0:T(8,128)(2,1)S(1)}, bf16[2,2,96,256]{3,2,1,0:T(8,128)(2,1)S(1)}, u32[]{:S(2)}, u32[]{:S(2)}) %collective-permute-start.22) | collective-permute-done | bytes 196640 | tf_op jit(solution)/shard_map/ppermute | solution.py:16
  88.5 1.3 collective-permute-done.23
  90.3 5.4 %convolution_bitcast_fusion = f32[1536,512]{0,1:T(8,128)} fusion(bf16[3,512,1536]{2,1,0:T(8,128)(2,1)} %param.5, bf16[1536,256]{1,0:T(8,128)(2,1)S(1)} %bitcast.223, bf16[1536,256]{1,0:T(8,128)(2,1)S(1)} %bitcast.222, f32[512]{0:T(512)S(1)} %pad_maximum_fusion.16), kind=kOutput, calls=%fused_computation | convolution fusion | flops 1614282752 | bytes 7866368 | tf_op jit(solution)/shard_map/dot_general | solution.py:10
  95.7 3.2 %fusion.48 = (f32[1536,256]{0,1:T(8,128)S(1)}, f32[1536,256]{0,1:T(8,128)}) fusion(f32[1536,512]{0,1:T(8,128)} %convolution_bitcast_fusion), kind=kLoop, calls=%fused_computation.131 | loop fusion | bytes 6291456 | tf_op jit(solution)/shard_map/slice | solution.py:79
  98.9 0.5 copy.45
  99.4 1.0 dynamic-slice_bitcast_fusion.1
  100.5 1.9 %copy.46 = f32[1536,256]{1,0:T(8,128)S(1)} copy(f32[1536,256]{0,1:T(8,128)} %get-tuple-element.7) | data formatting | bytes 3145728 | tf_op jit(solution)/shard_map/slice | solution.py:80
  103.0 1.2 bitcast_add_fusion.1
  104.3 0.7 collective-permute-start.25
  105.1 1.9 %collective-permute-start.29 = (f32[2,2,96,256]{3,2,1,0:T(8,128)S(1)}, f32[2,2,96,256]{3,2,1,0:T(8,128)S(1)}, u32[]{:S(2)}, u32[]{:S(2)}) collective-permute-start(f32[2,2,96,256]{3,2,1,0:T(8,128)S(1)} %dynamic-slice_bitcast_fusion.4), channel_id=1, source_target_pairs={{0,4},{1,5},{2,6},{3,7},{4,0},{5,1},{6,2},{7,3},{8,12},{9,13},{10,... | collective-permute-start | bytes 1179656 | tf_op jit(solution)/shard_map/ppermute | solution.py:16
  107.2 8.4 %collective-permute-done.25 = f32[2,2,96,256]{3,2,1,0:T(8,128)S(1)} collective-permute-done((f32[2,2,96,256]{3,2,1,0:T(8,128)S(1)}, f32[2,2,96,256]{3,2,1,0:T(8,128)S(1)}, u32[]{:S(2)}, u32[]{:S(2)}) %collective-permute-start.25) | collective-permute-done | bytes 393248 | tf_op jit(solution)/shard_map/ppermute | solution.py:16
  115.6 1.7 %collective-permute-start.26 = (f32[2,96,256]{2,1,0:T(8,128)S(1)}, f32[2,96,256]{2,1,0:T(8,128)S(1)}, u32[]{:S(2)}, u32[]{:S(2)}) collective-permute-start(f32[2,96,256]{2,1,0:T(8,128)S(1)} %dynamic-slice_bitcast_fusion.9), channel_id=1, source_target_pairs={{0,4},{1,5},{2,6},{3,7},{4,0},{5,1},{6,2},{7,3},{8,12},{9,13},{10,... | collective-permute-start | bytes 589832 | tf_op jit(solution)/shard_map/ppermute | solution.py:16
  117.3 0.9 collective-permute-start.30
  118.3 3.5 %collective-permute-done.26 = f32[2,96,256]{2,1,0:T(8,128)S(1)} collective-permute-done((f32[2,96,256]{2,1,0:T(8,128)S(1)}, f32[2,96,256]{2,1,0:T(8,128)S(1)}, u32[]{:S(2)}, u32[]{:S(2)}) %collective-permute-start.26) | collective-permute-done | bytes 196640 | tf_op jit(solution)/shard_map/ppermute | solution.py:16
  121.8 2.1 %collective-permute-start.27 = (f32[96,256]{1,0:T(8,128)S(1)}, f32[96,256]{1,0:T(8,128)S(1)}, u32[]{:S(2)}, u32[]{:S(2)}) collective-permute-start(f32[96,256]{1,0:T(8,128)S(1)} %dynamic-slice_bitcast_fusion.13), channel_id=1, source_target_pairs={{0,8},{1,9},{2,10},{3,11},{4,12},{5,13},{6,14},{7,15},{8,0},{9,1},... | collective-permute-start | bytes 294920 | tf_op jit(solution)/shard_map/ppermute | solution.py:16
  123.9 1.0 collective-permute-start.31
  125.1 6.1 %collective-permute-done.27 = f32[96,256]{1,0:T(8,128)S(1)} collective-permute-done((f32[96,256]{1,0:T(8,128)S(1)}, f32[96,256]{1,0:T(8,128)S(1)}, u32[]{:S(2)}, u32[]{:S(2)}) %collective-permute-start.27) | collective-permute-done | bytes 98336 | tf_op jit(solution)/shard_map/ppermute | solution.py:16
  131.1 1.1 collective-permute-done.31
  132.4 1.1 collective-permute-done.32
  133.5 0.8 collective-permute-start.33
  134.4 2.7 %collective-permute-done.33 = f32[256]{0:T(256)S(1)} collective-permute-done((f32[256]{0:T(256)S(1)}, f32[256]{0:T(256)S(1)}, u32[]{:S(2)}, u32[]{:S(2)}) %collective-permute-start.33) | collective-permute-done | bytes 1056 | tf_op jit(solution)/shard_map/ppermute | solution.py:16
  137.1 3.6 %collective-permute-done.34 = f32[256]{0:T(256)S(1)} collective-permute-done((f32[256]{0:T(256)S(1)}, f32[256]{0:T(256)S(1)}, u32[]{:S(2)}, u32[]{:S(2)}) %collective-permute-start.34) | collective-permute-done | bytes 1056 | tf_op jit(solution)/shard_map/ppermute | solution.py:16
  140.7 0.6 collective-permute-start.35
  141.3 3.9 %collective-permute-done.35 = f32[256]{0:T(256)S(1)} collective-permute-done((f32[256]{0:T(256)S(1)}, f32[256]{0:T(256)S(1)}, u32[]{:S(2)}, u32[]{:S(2)}) %collective-permute-start.35) | collective-permute-done | bytes 1056 | tf_op jit(solution)/shard_map/ppermute | solution.py:16
  145.2 0.7 broadcast_multiply_fusion
  (104 shorter events, 5.5 us)
Async XLA Ops:
  0.6 6.9 %collective-permute-start = (bf16[96,256]{1,0:T(8,128)(2,1)}, bf16[96,256]{1,0:T(8,128)(2,1)S(1)}, u32[]{:S(2)}, u32[]{:S(2)}) collective-permute-start(bf16[96,256]{1,0:T(8,128)(2,1)} %param.6), channel_id=1, source_target_pairs={{0,8},{1,9},{2,10},{3,11},{4,12},{5,13},{6,14},{7,15},{8,0},{9,1},... | collective-permute-start | bytes 147464 | tf_op jit(solution)/shard_map/ppermute | solution.py:16
  4.7 5.3 %collective-permute-start.4 = (bf16[96,256]{1,0:T(8,128)(2,1)}, bf16[96,256]{1,0:T(8,128)(2,1)S(1)}, u32[]{:S(2)}, u32[]{:S(2)}) collective-permute-start(bf16[96,256]{1,0:T(8,128)(2,1)} %param.7), channel_id=1, source_target_pairs={{0,8},{1,9},{2,10},{3,11},{4,12},{5,13},{6,14},{7,15},{8,0},{9,1},... | collective-permute-start | bytes 147464 | tf_op jit(solution)/shard_map/ppermute | solution.py:16
  10.9 4.7 %collective-permute-start.5 = (bf16[2,96,256]{2,1,0:T(8,128)(2,1)S(1)}, bf16[2,96,256]{2,1,0:T(8,128)(2,1)S(1)}, u32[]{:S(2)}, u32[]{:S(2)}) collective-permute-start(bf16[2,96,256]{2,1,0:T(8,128)(2,1)S(1)} %pad_maximum_fusion.13), channel_id=1, source_target_pairs={{0,2},{1,3},{2,0},{3,1},{4,6},{5,7},{6,4},{7,5},{8,10},{9,11},{10,... | collective-permute-start | bytes 294920 | tf_op jit(solution)/shard_map/ppermute | solution.py:16
  12.5 5.7 %collective-permute-start.1 = (bf16[2,96,256]{2,1,0:T(8,128)(2,1)S(1)}, bf16[2,96,256]{2,1,0:T(8,128)(2,1)S(1)}, u32[]{:S(2)}, u32[]{:S(2)}) collective-permute-start(bf16[2,96,256]{2,1,0:T(8,128)(2,1)S(1)} %pad_maximum_fusion.12), channel_id=1, source_target_pairs={{0,4},{1,5},{2,6},{3,7},{4,0},{5,1},{6,2},{7,3},{8,12},{9,13},{10,... | collective-permute-start | bytes 294920 | tf_op jit(solution)/shard_map/ppermute | solution.py:16
  15.7 5.7 %collective-permute-start.6 = (bf16[2,2,96,256]{3,2,1,0:T(8,128)(2,1)S(1)}, bf16[2,2,96,256]{3,2,1,0:T(8,128)(2,1)S(1)}, u32[]{:S(2)}, u32[]{:S(2)}) collective-permute-start(bf16[2,2,96,256]{3,2,1,0:T(8,128)(2,1)S(1)} %pad_maximum_fusion.9), channel_id=1, source_target_pairs={{0,4},{1,5},{2,6},{3,7},{4,0},{5,1},{6,2},{7,3},{8,12},{9,13},{10,... | collective-permute-start | bytes 589832 | tf_op jit(solution)/shard_map/ppermute | solution.py:16
  18.3 5.7 %collective-permute-start.2 = (bf16[2,2,96,256]{3,2,0,1:T(8,128)(2,1)S(1)}, bf16[2,2,96,256]{3,2,0,1:T(8,128)(2,1)S(1)}, u32[]{:S(2)}, u32[]{:S(2)}) collective-permute-start(bf16[2,2,96,256]{3,2,0,1:T(8,128)(2,1)S(1)} %pad_maximum_fusion.8), channel_id=1, source_target_pairs={{0,2},{1,3},{2,0},{3,1},{4,6},{5,7},{6,4},{7,5},{8,10},{9,11},{10,... | collective-permute-start | bytes 589832 | tf_op jit(solution)/shard_map/ppermute | solution.py:16
  21.5 2.8 %collective-permute-start.7 = (bf16[2,2,2,96,256]{4,3,2,0,1:T(8,128)(2,1)S(1)}, bf16[2,2,2,96,256]{4,3,2,0,1:T(8,128)(2,1)S(1)}, u32[]{:S(2)}, u32[]{:S(2)}) collective-permute-start(bf16[2,2,2,96,256]{4,3,2,0,1:T(8,128)(2,1)S(1)} %pad_maximum_fusion.5), channel_id=1, source_target_pairs={{0,1},{1,0},{2,3},{3,2},{4,5},{5,4},{6,7},{7,6},{8,9},{9,8},{10,11... | collective-permute-start | bytes 1179656 | tf_op jit(solution)/shard_map/ppermute | solution.py:16
  24.2 1.8 %collective-permute-start.3 = (bf16[2,2,2,96,256]{4,3,2,1,0:T(8,128)(2,1)S(1)}, bf16[2,2,2,96,256]{4,3,2,1,0:T(8,128)(2,1)S(1)}, u32[]{:S(2)}, u32[]{:S(2)}) collective-permute-start(bf16[2,2,2,96,256]{4,3,2,1,0:T(8,128)(2,1)S(1)} %copy.47), channel_id=1, source_target_pairs={{0,1},{1,0},{2,3},{3,2},{4,5},{5,4},{6,7},{7,6},{8,9},{9,8},{10,11... | collective-permute-start | bytes 1179656 | tf_op jit(solution)/shard_map/ppermute | solution.py:16
  36.2 2.8 %collective-permute-start.12 = (f32[2,2,2,96,256]{4,3,2,1,0:T(8,128)}, f32[2,2,2,96,256]{4,3,2,1,0:T(8,128)}, u32[]{:S(2)}, u32[]{:S(2)}) collective-permute-start(f32[2,2,2,96,256]{4,3,2,1,0:T(8,128)} %dynamic-slice_bitcast_fusion.2), channel_id=1, source_target_pairs={{0,1},{1,0},{2,3},{3,2},{4,5},{5,4},{6,7},{7,6},{8,9},{9,8},{10,11... | collective-permute-start | bytes 2359304 | tf_op jit(solution)/shard_map/ppermute | solution.py:16
  38.3 0.7 copy-start.1
  38.3 0.7 copy-start.2
  38.4 3.3 %collective-permute-start.8 = (f32[2,2,2,96,256]{4,3,2,1,0:T(8,128)S(1)}, f32[2,2,2,96,256]{4,3,2,1,0:T(8,128)S(1)}, u32[]{:S(2)}, u32[]{:S(2)}) collective-permute-start(f32[2,2,2,96,256]{4,3,2,1,0:T(8,128)S(1)} %dynamic-slice_bitcast_fusion.3), channel_id=1, source_target_pairs={{0,1},{1,0},{2,3},{3,2},{4,5},{5,4},{6,7},{7,6},{8,9},{9,8},{10,11... | collective-permute-start | bytes 2359304 | tf_op jit(solution)/shard_map/ppermute | solution.py:16
  39.0 2.9 %copy-start.3 = (f32[1,1536]{1,0:T(1,128)}, f32[1,1536]{1,0:T(1,128)S(1)}, u32[]{:S(2)}) copy-start(f32[1,1536]{1,0:T(1,128)S(1)} %get-tuple-element.49) | copy-start | bytes 18436
  40.3 1.5 %copy-start = (f32[2,2,2,96,256]{4,3,2,1,0:T(8,128)}, f32[2,2,2,96,256]{4,3,2,1,0:T(8,128)S(1)}, u32[]{:S(2)}) copy-start(f32[2,2,2,96,256]{4,3,2,1,0:T(8,128)S(1)} %bitcast_add_fusion.2) | copy-start | bytes 2359300
  40.3 11.5 %collective-permute-start.13 = (f32[2,2,96,256]{3,2,1,0:T(8,128)S(1)}, f32[2,2,96,256]{3,2,1,0:T(8,128)S(1)}, u32[]{:S(2)}, u32[]{:S(2)}) collective-permute-start(f32[2,2,96,256]{3,2,1,0:T(8,128)S(1)} %dynamic-slice_bitcast_fusion.6), channel_id=1, source_target_pairs={{0,4},{1,5},{2,6},{3,7},{4,0},{5,1},{6,2},{7,3},{8,12},{9,13},{10,... | collective-permute-start | bytes 1179656 | tf_op jit(solution)/shard_map/ppermute | solution.py:16
  41.8 11.5 %collective-permute-start.9 = (f32[2,2,96,256]{3,2,1,0:T(8,128)S(1)}, f32[2,2,96,256]{3,2,1,0:T(8,128)S(1)}, u32[]{:S(2)}, u32[]{:S(2)}) collective-permute-start(f32[2,2,96,256]{3,2,1,0:T(8,128)S(1)} %dynamic-slice_bitcast_fusion.7), channel_id=1, source_target_pairs={{0,2},{1,3},{2,0},{3,1},{4,6},{5,7},{6,4},{7,5},{8,10},{9,11},{10,... | collective-permute-start | bytes 1179656 | tf_op jit(solution)/shard_map/ppermute | solution.py:16
  52.9 6.4 %collective-permute-start.14 = (f32[2,96,256]{2,1,0:T(8,128)S(1)}, f32[2,96,256]{2,1,0:T(8,128)S(1)}, u32[]{:S(2)}, u32[]{:S(2)}) collective-permute-start(f32[2,96,256]{2,1,0:T(8,128)S(1)} %dynamic-slice_bitcast_fusion.10), channel_id=1, source_target_pairs={{0,2},{1,3},{2,0},{3,1},{4,6},{5,7},{6,4},{7,5},{8,10},{9,11},{10,... | collective-permute-start | bytes 589832 | tf_op jit(solution)/shard_map/ppermute | solution.py:16
  53.5 7.4 %collective-permute-start.10 = (f32[2,96,256]{2,1,0:T(8,128)S(1)}, f32[2,96,256]{2,1,0:T(8,128)S(1)}, u32[]{:S(2)}, u32[]{:S(2)}) collective-permute-start(f32[2,96,256]{2,1,0:T(8,128)S(1)} %dynamic-slice_bitcast_fusion.11), channel_id=1, source_target_pairs={{0,4},{1,5},{2,6},{3,7},{4,0},{5,1},{6,2},{7,3},{8,12},{9,13},{10,... | collective-permute-start | bytes 589832 | tf_op jit(solution)/shard_map/ppermute | solution.py:16
  59.4 9.6 %collective-permute-start.15 = (f32[96,256]{1,0:T(8,128)S(1)}, f32[96,256]{1,0:T(8,128)S(1)}, u32[]{:S(2)}, u32[]{:S(2)}) collective-permute-start(f32[96,256]{1,0:T(8,128)S(1)} %dynamic-slice_bitcast_fusion.14), channel_id=1, source_target_pairs={{0,8},{1,9},{2,10},{3,11},{4,12},{5,13},{6,14},{7,15},{8,0},{9,1},... | collective-permute-start | bytes 294920 | tf_op jit(solution)/shard_map/ppermute | solution.py:16
  61.0 9.0 %collective-permute-start.11 = (f32[96,256]{1,0:T(8,128)S(1)}, f32[96,256]{1,0:T(8,128)S(1)}, u32[]{:S(2)}, u32[]{:S(2)}) collective-permute-start(f32[96,256]{1,0:T(8,128)S(1)} %dynamic-slice_bitcast_fusion.15), channel_id=1, source_target_pairs={{0,8},{1,9},{2,10},{3,11},{4,12},{5,13},{6,14},{7,15},{8,0},{9,1},... | collective-permute-start | bytes 294920 | tf_op jit(solution)/shard_map/ppermute | solution.py:16
  70.1 5.2 %collective-permute-start.16 = (bf16[96,256]{1,0:T(8,128)(2,1)S(1)}, bf16[96,256]{1,0:T(8,128)(2,1)S(1)}, u32[]{:S(2)}, u32[]{:S(2)}) collective-permute-start(bf16[96,256]{1,0:T(8,128)(2,1)S(1)} %get-tuple-element.20), channel_id=1, source_target_pairs={{0,8},{1,9},{2,10},{3,11},{4,12},{5,13},{6,14},{7,15},{8,0},{9,1},... | collective-permute-start | bytes 147464 | tf_op jit(solution)/shard_map/ppermute | solution.py:16
  70.2 6.3 %collective-permute-start.20 = (bf16[96,256]{1,0:T(8,128)(2,1)S(1)}, bf16[96,256]{1,0:T(8,128)(2,1)S(1)}, u32[]{:S(2)}, u32[]{:S(2)}) collective-permute-start(bf16[96,256]{1,0:T(8,128)(2,1)S(1)} %get-tuple-element.21), channel_id=1, source_target_pairs={{0,8},{1,9},{2,10},{3,11},{4,12},{5,13},{6,14},{7,15},{8,0},{9,1},... | collective-permute-start | bytes 147464 | tf_op jit(solution)/shard_map/ppermute | solution.py:16
  75.3 4.7 %collective-permute-start.17 = (bf16[2,96,256]{2,1,0:T(8,128)(2,1)S(1)}, bf16[2,96,256]{2,1,0:T(8,128)(2,1)S(1)}, u32[]{:S(2)}, u32[]{:S(2)}) collective-permute-start(bf16[2,96,256]{2,1,0:T(8,128)(2,1)S(1)} %pad_maximum_fusion.14), channel_id=1, source_target_pairs={{0,4},{1,5},{2,6},{3,7},{4,0},{5,1},{6,2},{7,3},{8,12},{9,13},{10,... | collective-permute-start | bytes 294920 | tf_op jit(solution)/shard_map/ppermute | solution.py:16
  76.5 5.7 %collective-permute-start.21 = (bf16[2,96,256]{2,1,0:T(8,128)(2,1)S(1)}, bf16[2,96,256]{2,1,0:T(8,128)(2,1)S(1)}, u32[]{:S(2)}, u32[]{:S(2)}) collective-permute-start(bf16[2,96,256]{2,1,0:T(8,128)(2,1)S(1)} %pad_maximum_fusion.15), channel_id=1, source_target_pairs={{0,2},{1,3},{2,0},{3,1},{4,6},{5,7},{6,4},{7,5},{8,10},{9,11},{10,... | collective-permute-start | bytes 294920 | tf_op jit(solution)/shard_map/ppermute | solution.py:16
  80.0 5.7 %collective-permute-start.18 = (bf16[2,2,96,256]{3,2,0,1:T(8,128)(2,1)S(1)}, bf16[2,2,96,256]{3,2,0,1:T(8,128)(2,1)S(1)}, u32[]{:S(2)}, u32[]{:S(2)}) collective-permute-start(bf16[2,2,96,256]{3,2,0,1:T(8,128)(2,1)S(1)} %pad_maximum_fusion.10), channel_id=1, source_target_pairs={{0,2},{1,3},{2,0},{3,1},{4,6},{5,7},{6,4},{7,5},{8,10},{9,11},{10,... | collective-permute-start | bytes 589832 | tf_op jit(solution)/shard_map/ppermute | solution.py:16
  82.2 5.7 %collective-permute-start.22 = (bf16[2,2,96,256]{3,2,1,0:T(8,128)(2,1)S(1)}, bf16[2,2,96,256]{3,2,1,0:T(8,128)(2,1)S(1)}, u32[]{:S(2)}, u32[]{:S(2)}) collective-permute-start(bf16[2,2,96,256]{3,2,1,0:T(8,128)(2,1)S(1)} %pad_maximum_fusion.11), channel_id=1, source_target_pairs={{0,4},{1,5},{2,6},{3,7},{4,0},{5,1},{6,2},{7,3},{8,12},{9,13},{10,... | collective-permute-start | bytes 589832 | tf_op jit(solution)/shard_map/ppermute | solution.py:16
  85.9 2.2 %collective-permute-start.19 = (bf16[2,2,2,96,256]{4,3,0,1,2:T(8,128)(2,1)S(1)}, bf16[2,2,2,96,256]{4,3,0,1,2:T(8,128)(2,1)S(1)}, u32[]{:S(2)}, u32[]{:S(2)}) collective-permute-start(bf16[2,2,2,96,256]{4,3,0,1,2:T(8,128)(2,1)S(1)} %pad_maximum_fusion.6), channel_id=1, source_target_pairs={{0,1},{1,0},{2,3},{3,2},{4,5},{5,4},{6,7},{7,6},{8,9},{9,8},{10,11... | collective-permute-start | bytes 1179656 | tf_op jit(solution)/shard_map/ppermute | solution.py:16
  88.0 1.8 %collective-permute-start.23 = (bf16[2,2,2,96,256]{4,3,2,1,0:T(8,128)(2,1)S(1)}, bf16[2,2,2,96,256]{4,3,2,1,0:T(8,128)(2,1)S(1)}, u32[]{:S(2)}, u32[]{:S(2)}) collective-permute-start(bf16[2,2,2,96,256]{4,3,2,1,0:T(8,128)(2,1)S(1)} %pad_maximum_fusion.7), channel_id=1, source_target_pairs={{0,1},{1,0},{2,3},{3,2},{4,5},{5,4},{6,7},{7,6},{8,9},{9,8},{10,11... | collective-permute-start | bytes 1179656 | tf_op jit(solution)/shard_map/ppermute | solution.py:16
  100.4 2.6 %collective-permute-start.24 = (f32[2,2,2,96,256]{4,3,2,1,0:T(8,128)}, f32[2,2,2,96,256]{4,3,2,1,0:T(8,128)}, u32[]{:S(2)}, u32[]{:S(2)}) collective-permute-start(f32[2,2,2,96,256]{4,3,2,1,0:T(8,128)} %dynamic-slice_bitcast_fusion.1), channel_id=1, source_target_pairs={{0,1},{1,0},{2,3},{3,2},{4,5},{5,4},{6,7},{7,6},{8,9},{9,8},{10,11... | collective-permute-start | bytes 2359304 | tf_op jit(solution)/shard_map/ppermute | solution.py:16
  102.5 2.5 %collective-permute-start.28 = (f32[2,2,2,96,256]{4,3,2,1,0:T(8,128)S(1)}, f32[2,2,2,96,256]{4,3,2,1,0:T(8,128)S(1)}, u32[]{:S(2)}, u32[]{:S(2)}) collective-permute-start(f32[2,2,2,96,256]{4,3,2,1,0:T(8,128)S(1)} %dynamic-slice_bitcast_fusion), channel_id=1, source_target_pairs={{0,1},{1,0},{2,3},{3,2},{4,5},{5,4},{6,7},{7,6},{8,9},{9,8},{10,11... | collective-permute-start | bytes 2359304 | tf_op jit(solution)/shard_map/ppermute | solution.py:16
  104.3 11.2 %collective-permute-start.25 = (f32[2,2,96,256]{3,2,1,0:T(8,128)S(1)}, f32[2,2,96,256]{3,2,1,0:T(8,128)S(1)}, u32[]{:S(2)}, u32[]{:S(2)}) collective-permute-start(f32[2,2,96,256]{3,2,1,0:T(8,128)S(1)} %dynamic-slice_bitcast_fusion.5), channel_id=1, source_target_pairs={{0,2},{1,3},{2,0},{3,1},{4,6},{5,7},{6,4},{7,5},{8,10},{9,11},{10,... | collective-permute-start | bytes 1179656 | tf_op jit(solution)/shard_map/ppermute | solution.py:16
  105.1 12.1 %collective-permute-start.29 = (f32[2,2,96,256]{3,2,1,0:T(8,128)S(1)}, f32[2,2,96,256]{3,2,1,0:T(8,128)S(1)}, u32[]{:S(2)}, u32[]{:S(2)}) collective-permute-start(f32[2,2,96,256]{3,2,1,0:T(8,128)S(1)} %dynamic-slice_bitcast_fusion.4), channel_id=1, source_target_pairs={{0,4},{1,5},{2,6},{3,7},{4,0},{5,1},{6,2},{7,3},{8,12},{9,13},{10,... | collective-permute-start | bytes 1179656 | tf_op jit(solution)/shard_map/ppermute | solution.py:16
  115.6 6.2 %collective-permute-start.26 = (f32[2,96,256]{2,1,0:T(8,128)S(1)}, f32[2,96,256]{2,1,0:T(8,128)S(1)}, u32[]{:S(2)}, u32[]{:S(2)}) collective-permute-start(f32[2,96,256]{2,1,0:T(8,128)S(1)} %dynamic-slice_bitcast_fusion.9), channel_id=1, source_target_pairs={{0,4},{1,5},{2,6},{3,7},{4,0},{5,1},{6,2},{7,3},{8,12},{9,13},{10,... | collective-permute-start | bytes 589832 | tf_op jit(solution)/shard_map/ppermute | solution.py:16
  117.3 6.5 %collective-permute-start.30 = (f32[2,96,256]{2,1,0:T(8,128)S(1)}, f32[2,96,256]{2,1,0:T(8,128)S(1)}, u32[]{:S(2)}, u32[]{:S(2)}) collective-permute-start(f32[2,96,256]{2,1,0:T(8,128)S(1)} %dynamic-slice_bitcast_fusion.8), channel_id=1, source_target_pairs={{0,2},{1,3},{2,0},{3,1},{4,6},{5,7},{6,4},{7,5},{8,10},{9,11},{10,... | collective-permute-start | bytes 589832 | tf_op jit(solution)/shard_map/ppermute | solution.py:16
  121.8 9.3 %collective-permute-start.27 = (f32[96,256]{1,0:T(8,128)S(1)}, f32[96,256]{1,0:T(8,128)S(1)}, u32[]{:S(2)}, u32[]{:S(2)}) collective-permute-start(f32[96,256]{1,0:T(8,128)S(1)} %dynamic-slice_bitcast_fusion.13), channel_id=1, source_target_pairs={{0,8},{1,9},{2,10},{3,11},{4,12},{5,13},{6,14},{7,15},{8,0},{9,1},... | collective-permute-start | bytes 294920 | tf_op jit(solution)/shard_map/ppermute | solution.py:16
  123.9 8.3 %collective-permute-start.31 = (f32[96,256]{1,0:T(8,128)S(1)}, f32[96,256]{1,0:T(8,128)S(1)}, u32[]{:S(2)}, u32[]{:S(2)}) collective-permute-start(f32[96,256]{1,0:T(8,128)S(1)} %dynamic-slice_bitcast_fusion.12), channel_id=1, source_target_pairs={{0,8},{1,9},{2,10},{3,11},{4,12},{5,13},{6,14},{7,15},{8,0},{9,1},... | collective-permute-start | bytes 294920 | tf_op jit(solution)/shard_map/ppermute | solution.py:16
  132.3 1.2 collective-permute-start.32
  133.5 3.6 %collective-permute-start.33 = (f32[256]{0:T(256)S(1)}, f32[256]{0:T(256)S(1)}, u32[]{:S(2)}, u32[]{:S(2)}) collective-permute-start(f32[256]{0:T(256)S(1)} %add.179), channel_id=1, source_target_pairs={{0,2},{1,3},{2,0},{3,1},{4,6},{5,7},{6,4},{7,5},{8,10},{9,11},{10,... | collective-permute-start | bytes 3080 | tf_op jit(solution)/shard_map/ppermute | solution.py:16
  137.1 3.6 %collective-permute-start.34 = (f32[256]{0:T(256)S(1)}, f32[256]{0:T(256)S(1)}, u32[]{:S(2)}, u32[]{:S(2)}) collective-permute-start(f32[256]{0:T(256)S(1)} %add.180), channel_id=1, source_target_pairs={{0,4},{1,5},{2,6},{3,7},{4,0},{5,1},{6,2},{7,3},{8,12},{9,13},{10,... | collective-permute-start | bytes 3080 | tf_op jit(solution)/shard_map/ppermute | solution.py:16
  140.7 4.5 %collective-permute-start.35 = (f32[256]{0:T(256)S(1)}, f32[256]{0:T(256)S(1)}, u32[]{:S(2)}, u32[]{:S(2)}) collective-permute-start(f32[256]{0:T(256)S(1)} %add.181), channel_id=1, source_target_pairs={{0,8},{1,9},{2,10},{3,11},{4,12},{5,13},{6,14},{7,15},{8,0},{9,1},... | collective-permute-start | bytes 3080 | tf_op jit(solution)/shard_map/ppermute | solution.py:16

commit v4 on v3

--- a/solution.py
+++ b/solution.py
@@ -71,13 +71,14 @@
     der_full = doubling_all_gather(first_g, devices, order_der[::-1])
     scale = None
     for sector in range(SECTORS):
-        solutions = jnp.concatenate([amp_full, der_full], axis=1)
-        projected = jnp.dot(panels[sector], solutions, preferred_element_type=jnp.float32)
-        if scale is not None:
-            projected = projected * jnp.concatenate([scale, scale])[None, :]
-        partial = contract_rows(panels[sector + 1], projected.astype(jnp.bfloat16))
-        rot_amp = halving_reduce_scatter(partial[:, :width], devices, order_amp)
-        rot_der = halving_reduce_scatter(partial[:, width:], devices, order_der)
+        halves = []
+        for gathered in (amp_full, der_full):
+            projected = jnp.dot(panels[sector], gathered, preferred_element_type=jnp.float32)
+            if scale is not None:
+                projected = projected * scale[None, :]
+            halves.append(contract_rows(panels[sector + 1], projected.astype(jnp.bfloat16)))
+        rot_amp = halving_reduce_scatter(halves[0], devices, order_amp)
+        rot_der = halving_reduce_scatter(halves[1], devices, order_der)
         angle_rows = lax.dynamic_slice_in_dim(phase[sector], first_row, chan_rows, 0)
         wave_rows = lax.dynamic_slice_in_dim(wavenum[sector], first_row, chan_rows, 0)
         cosine = jnp.cos(angle_rows)[:, None]

time: 146 us -> 146 us (level)
  waiting for transfers between devices: 78.4 us -> 69.8 us
  starting transfers between devices: 33 us -> 38.4 us
  matrix products: 10.7 us -> 15.4 us
  local copies, waits for them, and re-layouts: 14.9 us -> 10.9 us
  other arithmetic: 7.64 us -> 9.4 us
    slice x6 -> x0, local copies, waits for them, and re-layouts: 11.2 us -> none  [the longest x3 5.58 us: shards(): rot_der = halving_reduce_scatter(partial[:, width:], devices, order_der)]
    ppermute x36, waiting for transfers between devices: 78.4 us -> 69.8 us  [exchange(): return lax.ppermute(x, 'row', [(i, i ^ distance) for i in range(devices)])]
    dot_general x0 -> x4, local copies, waits for them, and re-layouts: none -> 6.08 us  [contract_rows(): lax.dot_general(left, right, (((0,), (0,)), ((), ())), preferred_element_...]
    ppermute x36, starting transfers between devices: 33 us -> 38.4 us  [exchange(): return lax.ppermute(x, 'row', [(i, i ^ distance) for i in range(devices)])]
    dot_general x2 -> x4, matrix products: 10.7 us -> 15.4 us  [contract_rows(): lax.dot_general(left, right, (((0,), (0,)), ((), ())), preferred_element_...]
    another operation x31 -> x32, other arithmetic: 1.98 us -> 3.75 us  [doubling_all_gather(): jnp.stack([jnp.where(low, cur, other), jnp.where(low, other, cur)], axis=...]
  transfers between devices with their start and end apart: 36 -> 36, of which waited for: 27 -> 23; matrix products, arithmetic and copies ran while one was open for 7% -> 18% of each run, Pallas kernels for 0% -> 0%
where the time goes in v4:
time: 146 us; the launch traced here: 145 us
  waiting for transfers between devices  69.8 us (48%)
  starting transfers between devices  38.4 us (26%)
  matrix products  15.4 us (11%)
  local copies, waits for them, and re-layouts  10.9 us (7%)
  other arithmetic  9.4 us (6%)
    ppermute x36, waiting for transfers between devices, exchange(): return lax.ppermute(x, 'row', [(i, i ^ distance) for i in range(devices)])  69.8 us
    ppermute x36, starting transfers between devices, exchange(): return lax.ppermute(x, 'row', [(i, i ^ distance) for i in range(devices)])  38.4 us
    dot_general x4, matrix products, contract_rows(): lax.dot_general(left, right, (((0,), (0,)), ((), ())), preferred_element_...  15.4 us
    dot_general x4, local copies, waits for them, and re-layouts, contract_rows(): lax.dot_general(left, right, (((0,), (0,)), ((), ())), preferred_element_...  6.08 us
    add x12, other arithmetic, halving_reduce_scatter(): cur = keep + exchange(send, 1 << bit, devices)  3.99 us
    another operation x32, other arithmetic, doubling_all_gather(): jnp.stack([jnp.where(low, cur, other), jnp.where(low, other, cur)], axis=...  3.75 us
  transfers between devices with their start and end apart: 36, of which 23 were waited for; matrix products, arithmetic and copies ran while one was open for 18% of the time, Pallas kernels for 0%

profile of v4, /device:TPU:0, one launch (start us, length us, event | category | flops | bytes accessed | tf_op | source)
XLA Modules:
  0.0 145.2 jit_solution(3730282601905878638)
XLA Ops:
  0.6 4.1 %collective-permute-start.8 = (bf16[96,256]{1,0:T(8,128)(2,1)}, bf16[96,256]{1,0:T(8,128)(2,1)S(1)}, u32[]{:S(2)}, u32[]{:S(2)}) collective-permute-start(bf16[96,256]{1,0:T(8,128)(2,1)} %param.7), channel_id=1, source_target_pairs={{0,8},{1,9},{2,10},{3,11},{4,12},{5,13},{6,14},{7,15},{8,0},{9,1},... | collective-permute-start | bytes 147464 | tf_op jit(solution)/shard_map/ppermute | solution.py:16
  4.8 2.7 %collective-permute-done.8 = bf16[96,256]{1,0:T(8,128)(2,1)S(1)} collective-permute-done((bf16[96,256]{1,0:T(8,128)(2,1)}, bf16[96,256]{1,0:T(8,128)(2,1)S(1)}, u32[]{:S(2)}, u32[]{:S(2)}) %collective-permute-start.8) | collective-permute-done | bytes 49184 | tf_op jit(solution)/shard_map/ppermute | solution.py:16
  7.5 0.8 select_bitcast_fusion.29
  8.4 1.8 %collective-permute-start.9 = (bf16[2,96,256]{2,1,0:T(8,128)(2,1)S(1)}, bf16[2,96,256]{2,1,0:T(8,128)(2,1)S(1)}, u32[]{:S(2)}, u32[]{:S(2)}) collective-permute-start(bf16[2,96,256]{2,1,0:T(8,128)(2,1)S(1)} %pad_maximum_fusion.13), channel_id=1, source_target_pairs={{0,2},{1,3},{2,0},{3,1},{4,6},{5,7},{6,4},{7,5},{8,10},{9,11},{10,... | collective-permute-start | bytes 294920 | tf_op jit(solution)/shard_map/ppermute | solution.py:16
  10.2 0.8 select_bitcast_fusion.31
  11.0 2.0 %collective-permute-start.1 = (bf16[2,96,256]{2,1,0:T(8,128)(2,1)S(1)}, bf16[2,96,256]{2,1,0:T(8,128)(2,1)S(1)}, u32[]{:S(2)}, u32[]{:S(2)}) collective-permute-start(bf16[2,96,256]{2,1,0:T(8,128)(2,1)S(1)} %pad_maximum_fusion.12), channel_id=1, source_target_pairs={{0,4},{1,5},{2,6},{3,7},{4,0},{5,1},{6,2},{7,3},{8,12},{9,13},{10,... | collective-permute-start | bytes 294920 | tf_op jit(solution)/shard_map/ppermute | solution.py:16
  13.1 2.2 %collective-permute-start.10 = (bf16[2,2,96,256]{3,2,1,0:T(8,128)(2,1)S(1)}, bf16[2,2,96,256]{3,2,1,0:T(8,128)(2,1)S(1)}, u32[]{:S(2)}, u32[]{:S(2)}) collective-permute-start(bf16[2,2,96,256]{3,2,1,0:T(8,128)(2,1)S(1)} %pad_maximum_fusion.9), channel_id=1, source_target_pairs={{0,4},{1,5},{2,6},{3,7},{4,0},{5,1},{6,2},{7,3},{8,12},{9,13},{10,... | collective-permute-start | bytes 589832 | tf_op jit(solution)/shard_map/ppermute | solution.py:16
  15.3 1.0 collective-permute-done.1
  16.4 1.5 %collective-permute-start.2 = (bf16[2,2,96,256]{3,2,0,1:T(8,128)(2,1)S(1)}, bf16[2,2,96,256]{3,2,0,1:T(8,128)(2,1)S(1)}, u32[]{:S(2)}, u32[]{:S(2)}) collective-permute-start(bf16[2,2,96,256]{3,2,0,1:T(8,128)(2,1)S(1)} %pad_maximum_fusion.8), channel_id=1, source_target_pairs={{0,2},{1,3},{2,0},{3,1},{4,6},{5,7},{6,4},{7,5},{8,10},{9,11},{10,... | collective-permute-start | bytes 589832 | tf_op jit(solution)/shard_map/ppermute | solution.py:16
  17.9 2.0 %collective-permute-done.10 = bf16[2,2,96,256]{3,2,1,0:T(8,128)(2,1)S(1)} collective-permute-done((bf16[2,2,96,256]{3,2,1,0:T(8,128)(2,1)S(1)}, bf16[2,2,96,256]{3,2,1,0:T(8,128)(2,1)S(1)}, u32[]{:S(2)}, u32[]{:S(2)}) %collective-permute-start.10) | collective-permute-done | bytes 196640 | tf_op jit(solution)/shard_map/ppermute | solution.py:16
  20.1 2.0 %collective-permute-done.2 = bf16[2,2,96,256]{3,2,0,1:T(8,128)(2,1)S(1)} collective-permute-done((bf16[2,2,96,256]{3,2,0,1:T(8,128)(2,1)S(1)}, bf16[2,2,96,256]{3,2,0,1:T(8,128)(2,1)S(1)}, u32[]{:S(2)}, u32[]{:S(2)}) %collective-permute-start.2) | collective-permute-done | bytes 196640 | tf_op jit(solution)/shard_map/ppermute | solution.py:16
  22.2 0.8 copy.47
  23.2 3.0 %convolution_bitcast_fusion.2 = f32[1536,256]{0,1:T(8,128)S(1)} fusion(bf16[1536,256]{1,0:T(8,128)(2,1)S(1)} %bitcast.250, bf16[3,512,1536]{2,1,0:T(8,128)(2,1)} %param.5), kind=kOutput, calls=%fused_computation.2 | convolution fusion | flops 805437440 | bytes 5505024 | tf_op jit(solution)/shard_map/dot_general | solution.py:10
  26.6 1.0 dynamic-slice_bitcast_fusion.2
  27.6 0.5 collective-permute-start.12
  28.1 1.2 select_bitcast_fusion.7
  29.4 4.2 %convolution_bitcast_fusion.3 = f32[1536,256]{0,1:T(8,128)} fusion(bf16[1536,256]{1,0:T(8,128)(2,1)S(1)} %bitcast.248, bf16[3,512,1536]{2,1,0:T(8,128)(2,1)} %param.5), kind=kOutput, calls=%fused_computation.3 | convolution fusion | flops 805437440 | bytes 5505024 | tf_op jit(solution)/shard_map/dot_general | solution.py:10
  33.5 1.9 %copy.32 = f32[1536,256]{1,0:T(8,128)S(1)} copy(f32[1536,256]{0,1:T(8,128)} %convolution_bitcast_fusion.3) | data formatting | bytes 3145728 | tf_op jit(solution)/shard_map/dot_general | solution.py:10
  35.6 0.5 copy-done.1
  36.2 1.2 bitcast_add_fusion.2
  37.5 2.3 %collective-permute-start.13 = (f32[2,2,96,256]{3,2,1,0:T(8,128)S(1)}, f32[2,2,96,256]{3,2,1,0:T(8,128)S(1)}, u32[]{:S(2)}, u32[]{:S(2)}) collective-permute-start(f32[2,2,96,256]{3,2,1,0:T(8,128)S(1)} %dynamic-slice_bitcast_fusion.6), channel_id=1, source_target_pairs={{0,4},{1,5},{2,6},{3,7},{4,0},{5,1},{6,2},{7,3},{8,12},{9,13},{10,... | collective-permute-start | bytes 1179656 | tf_op jit(solution)/shard_map/ppermute | solution.py:16
  40.4 8.6 %collective-permute-done.13 = f32[2,2,96,256]{3,2,1,0:T(8,128)S(1)} collective-permute-done((f32[2,2,96,256]{3,2,1,0:T(8,128)S(1)}, f32[2,2,96,256]{3,2,1,0:T(8,128)S(1)}, u32[]{:S(2)}, u32[]{:S(2)}) %collective-permute-start.13) | collective-permute-done | bytes 393248 | tf_op jit(solution)/shard_map/ppermute | solution.py:16
  49.1 1.0 bitcast_add_fusion.6
  50.2 1.0 collective-permute-start.14
  51.2 1.2 collective-permute-start.6
  52.4 4.1 %collective-permute-done.14 = f32[2,96,256]{2,1,0:T(8,128)S(1)} collective-permute-done((f32[2,96,256]{2,1,0:T(8,128)S(1)}, f32[2,96,256]{2,1,0:T(8,128)S(1)}, u32[]{:S(2)}, u32[]{:S(2)}) %collective-permute-start.14) | collective-permute-done | bytes 196640 | tf_op jit(solution)/shard_map/ppermute | solution.py:16
  56.6 3.3 %collective-permute-start.15 = (f32[96,256]{1,0:T(8,128)S(1)}, f32[96,256]{1,0:T(8,128)S(1)}, u32[]{:S(2)}, u32[]{:S(2)}) collective-permute-start(f32[96,256]{1,0:T(8,128)S(1)} %dynamic-slice_bitcast_fusion.14), channel_id=1, source_target_pairs={{0,8},{1,9},{2,10},{3,11},{4,12},{5,13},{6,14},{7,15},{8,0},{9,1},... | collective-permute-start | bytes 294920 | tf_op jit(solution)/shard_map/ppermute | solution.py:16
  60.1 0.8 cosine_bitcast_fusion
  60.9 4.4 %collective-permute-done.15 = f32[96,256]{1,0:T(8,128)S(1)} collective-permute-done((f32[96,256]{1,0:T(8,128)S(1)}, f32[96,256]{1,0:T(8,128)S(1)}, u32[]{:S(2)}, u32[]{:S(2)}) %collective-permute-start.15) | collective-permute-done | bytes 98336 | tf_op jit(solution)/shard_map/ppermute | solution.py:16
  65.3 2.5 %collective-permute-done.7 = f32[96,256]{1,0:T(8,128)S(1)} collective-permute-done((f32[96,256]{1,0:T(8,128)S(1)}, f32[96,256]{1,0:T(8,128)S(1)}, u32[]{:S(2)}, u32[]{:S(2)}) %collective-permute-start.7) | collective-permute-done | bytes 98336 | tf_op jit(solution)/shard_map/ppermute | solution.py:16
  68.0 2.9 %collective-permute-start.20 = (bf16[96,256]{1,0:T(8,128)(2,1)S(1)}, bf16[96,256]{1,0:T(8,128)(2,1)S(1)}, u32[]{:S(2)}, u32[]{:S(2)}) collective-permute-start(bf16[96,256]{1,0:T(8,128)(2,1)S(1)} %get-tuple-element.17), channel_id=1, source_target_pairs={{0,8},{1,9},{2,10},{3,11},{4,12},{5,13},{6,14},{7,15},{8,0},{9,1},... | collective-permute-start | bytes 147464 | tf_op jit(solution)/shard_map/ppermute | solution.py:16
  70.9 2.6 %collective-permute-done.16 = bf16[96,256]{1,0:T(8,128)(2,1)S(1)} collective-permute-done((bf16[96,256]{1,0:T(8,128)(2,1)S(1)}, bf16[96,256]{1,0:T(8,128)(2,1)S(1)}, u32[]{:S(2)}, u32[]{:S(2)}) %collective-permute-start.16) | collective-permute-done | bytes 49184 | tf_op jit(solution)/shard_map/ppermute | solution.py:16
  73.9 0.7 collective-permute-done.20
  74.7 0.7 collective-permute-start.21
  75.3 2.8 %collective-permute-done.17 = bf16[2,96,256]{2,1,0:T(8,128)(2,1)S(1)} collective-permute-done((bf16[2,96,256]{2,1,0:T(8,128)(2,1)S(1)}, bf16[2,96,256]{2,1,0:T(8,128)(2,1)S(1)}, u32[]{:S(2)}, u32[]{:S(2)}) %collective-permute-start.17) | collective-permute-done | bytes 98336 | tf_op jit(solution)/shard_map/ppermute | solution.py:16
  78.2 0.8 collective-permute-start.18
  79.0 1.3 collective-permute-done.21
  80.4 1.8 %collective-permute-start.22 = (bf16[2,2,96,256]{3,2,1,0:T(8,128)(2,1)S(1)}, bf16[2,2,96,256]{3,2,1,0:T(8,128)(2,1)S(1)}, u32[]{:S(2)}, u32[]{:S(2)}) collective-permute-start(bf16[2,2,96,256]{3,2,1,0:T(8,128)(2,1)S(1)} %pad_maximum_fusion.11), channel_id=1, source_target_pairs={{0,4},{1,5},{2,6},{3,7},{4,0},{5,1},{6,2},{7,3},{8,12},{9,13},{10,... | collective-permute-start | bytes 589832 | tf_op jit(solution)/shard_map/ppermute | solution.py:16
  82.2 1.8 %collective-permute-done.18 = bf16[2,2,96,256]{3,2,0,1:T(8,128)(2,1)S(1)} collective-permute-done((bf16[2,2,96,256]{3,2,0,1:T(8,128)(2,1)S(1)}, bf16[2,2,96,256]{3,2,0,1:T(8,128)(2,1)S(1)}, u32[]{:S(2)}, u32[]{:S(2)}) %collective-permute-start.18) | collective-permute-done | bytes 196640 | tf_op jit(solution)/shard_map/ppermute | solution.py:16
  84.1 2.0 %collective-permute-done.22 = bf16[2,2,96,256]{3,2,1,0:T(8,128)(2,1)S(1)} collective-permute-done((bf16[2,2,96,256]{3,2,1,0:T(8,128)(2,1)S(1)}, bf16[2,2,96,256]{3,2,1,0:T(8,128)(2,1)S(1)}, u32[]{:S(2)}, u32[]{:S(2)}) %collective-permute-start.22) | collective-permute-done | bytes 196640 | tf_op jit(solution)/shard_map/ppermute | solution.py:16
  86.7 1.3 collective-permute-done.23
  88.5 4.2 %convolution_bitcast_fusion.1 = f32[1536,256]{0,1:T(8,128)} fusion(bf16[3,512,1536]{2,1,0:T(8,128)(2,1)} %param.5, bf16[1536,256]{1,0:T(8,128)(2,1)S(1)} %bitcast.247, f32[256]{0:T(256)S(1)} %add_rsqrt_fusion.1), kind=kOutput, calls=%fused_computation.1 | convolution fusion | flops 805568512 | bytes 5506048 | tf_op jit(solution)/shard_map/dot_general | solution.py:10
  92.6 1.9 %copy.44 = f32[1536,256]{1,0:T(8,128)S(1)} copy(f32[1536,256]{0,1:T(8,128)} %convolution_bitcast_fusion.1) | data formatting | bytes 3145728 | tf_op jit(solution)/shard_map/dot_general | solution.py:10
  94.5 1.0 dynamic-slice_bitcast_fusion.1
  95.7 4.2 %convolution_bitcast_fusion = f32[1536,256]{0,1:T(8,128)} fusion(bf16[3,512,1536]{2,1,0:T(8,128)(2,1)} %param.5, bf16[1536,256]{1,0:T(8,128)(2,1)S(1)} %bitcast.249, f32[256]{0:T(256)S(1)} %add_rsqrt_fusion.1), kind=kOutput, calls=%fused_computation | convolution fusion | flops 805568512 | bytes 5506048 | tf_op jit(solution)/shard_map/dot_general | solution.py:10
  99.8 1.9 %copy.46 = f32[1536,256]{1,0:T(8,128)S(1)} copy(f32[1536,256]{0,1:T(8,128)} %convolution_bitcast_fusion) | data formatting | bytes 3145728 | tf_op jit(solution)/shard_map/dot_general | solution.py:10
  102.2 1.2 bitcast_add_fusion.1
  103.5 0.7 collective-permute-start.25
  104.4 1.9 %collective-permute-start.29 = (f32[2,2,96,256]{3,2,1,0:T(8,128)S(1)}, f32[2,2,96,256]{3,2,1,0:T(8,128)S(1)}, u32[]{:S(2)}, u32[]{:S(2)}) collective-permute-start(f32[2,2,96,256]{3,2,1,0:T(8,128)S(1)} %dynamic-slice_bitcast_fusion.4), channel_id=1, source_target_pairs={{0,4},{1,5},{2,6},{3,7},{4,0},{5,1},{6,2},{7,3},{8,12},{9,13},{10,... | collective-permute-start | bytes 1179656 | tf_op jit(solution)/shard_map/ppermute | solution.py:16
  106.4 8.3 %collective-permute-done.25 = f32[2,2,96,256]{3,2,1,0:T(8,128)S(1)} collective-permute-done((f32[2,2,96,256]{3,2,1,0:T(8,128)S(1)}, f32[2,2,96,256]{3,2,1,0:T(8,128)S(1)}, u32[]{:S(2)}, u32[]{:S(2)}) %collective-permute-start.25) | collective-permute-done | bytes 393248 | tf_op jit(solution)/shard_map/ppermute | solution.py:16
  114.8 1.8 %collective-permute-start.26 = (f32[2,96,256]{2,1,0:T(8,128)S(1)}, f32[2,96,256]{2,1,0:T(8,128)S(1)}, u32[]{:S(2)}, u32[]{:S(2)}) collective-permute-start(f32[2,96,256]{2,1,0:T(8,128)S(1)} %dynamic-slice_bitcast_fusion.9), channel_id=1, source_target_pairs={{0,4},{1,5},{2,6},{3,7},{4,0},{5,1},{6,2},{7,3},{8,12},{9,13},{10,... | collective-permute-start | bytes 589832 | tf_op jit(solution)/shard_map/ppermute | solution.py:16
  116.7 0.8 collective-permute-start.30
  117.6 3.5 %collective-permute-done.26 = f32[2,96,256]{2,1,0:T(8,128)S(1)} collective-permute-done((f32[2,96,256]{2,1,0:T(8,128)S(1)}, f32[2,96,256]{2,1,0:T(8,128)S(1)}, u32[]{:S(2)}, u32[]{:S(2)}) %collective-permute-start.26) | collective-permute-done | bytes 196640 | tf_op jit(solution)/shard_map/ppermute | solution.py:16
  121.1 2.2 %collective-permute-start.27 = (f32[96,256]{1,0:T(8,128)S(1)}, f32[96,256]{1,0:T(8,128)S(1)}, u32[]{:S(2)}, u32[]{:S(2)}) collective-permute-start(f32[96,256]{1,0:T(8,128)S(1)} %dynamic-slice_bitcast_fusion.13), channel_id=1, source_target_pairs={{0,8},{1,9},{2,10},{3,11},{4,12},{5,13},{6,14},{7,15},{8,0},{9,1},... | collective-permute-start | bytes 294920 | tf_op jit(solution)/shard_map/ppermute | solution.py:16
  123.4 1.2 collective-permute-start.31
  124.7 5.8 %collective-permute-done.27 = f32[96,256]{1,0:T(8,128)S(1)} collective-permute-done((f32[96,256]{1,0:T(8,128)S(1)}, f32[96,256]{1,0:T(8,128)S(1)}, u32[]{:S(2)}, u32[]{:S(2)}) %collective-permute-start.27) | collective-permute-done | bytes 98336 | tf_op jit(solution)/shard_map/ppermute | solution.py:16
  130.5 1.1 collective-permute-done.31
  131.8 1.1 collective-permute-done.32
  132.9 0.8 collective-permute-start.33
  133.7 2.7 %collective-permute-done.33 = f32[256]{0:T(256)S(1)} collective-permute-done((f32[256]{0:T(256)S(1)}, f32[256]{0:T(256)S(1)}, u32[]{:S(2)}, u32[]{:S(2)}) %collective-permute-start.33) | collective-permute-done | bytes 1056 | tf_op jit(solution)/shard_map/ppermute | solution.py:16
  136.5 3.6 %collective-permute-done.34 = f32[256]{0:T(256)S(1)} collective-permute-done((f32[256]{0:T(256)S(1)}, f32[256]{0:T(256)S(1)}, u32[]{:S(2)}, u32[]{:S(2)}) %collective-permute-start.34) | collective-permute-done | bytes 1056 | tf_op jit(solution)/shard_map/ppermute | solution.py:16
  140.0 0.7 collective-permute-start.35
  140.8 3.7 %collective-permute-done.35 = f32[256]{0:T(256)S(1)} collective-permute-done((f32[256]{0:T(256)S(1)}, f32[256]{0:T(256)S(1)}, u32[]{:S(2)}, u32[]{:S(2)}) %collective-permute-start.35) | collective-permute-done | bytes 1056 | tf_op jit(solution)/shard_map/ppermute | solution.py:16
  144.5 0.7 broadcast_multiply_fusion
  (104 shorter events, 5.7 us)
Async XLA Ops:
  0.6 6.9 %collective-permute-start.8 = (bf16[96,256]{1,0:T(8,128)(2,1)}, bf16[96,256]{1,0:T(8,128)(2,1)S(1)}, u32[]{:S(2)}, u32[]{:S(2)}) collective-permute-start(bf16[96,256]{1,0:T(8,128)(2,1)} %param.7), channel_id=1, source_target_pairs={{0,8},{1,9},{2,10},{3,11},{4,12},{5,13},{6,14},{7,15},{8,0},{9,1},... | collective-permute-start | bytes 147464 | tf_op jit(solution)/shard_map/ppermute | solution.py:16
  4.7 5.4 %collective-permute-start = (bf16[96,256]{1,0:T(8,128)(2,1)}, bf16[96,256]{1,0:T(8,128)(2,1)S(1)}, u32[]{:S(2)}, u32[]{:S(2)}) collective-permute-start(bf16[96,256]{1,0:T(8,128)(2,1)} %param.6), channel_id=1, source_target_pairs={{0,8},{1,9},{2,10},{3,11},{4,12},{5,13},{6,14},{7,15},{8,0},{9,1},... | collective-permute-start | bytes 147464 | tf_op jit(solution)/shard_map/ppermute | solution.py:16
  8.4 4.7 %collective-permute-start.9 = (bf16[2,96,256]{2,1,0:T(8,128)(2,1)S(1)}, bf16[2,96,256]{2,1,0:T(8,128)(2,1)S(1)}, u32[]{:S(2)}, u32[]{:S(2)}) collective-permute-start(bf16[2,96,256]{2,1,0:T(8,128)(2,1)S(1)} %pad_maximum_fusion.13), channel_id=1, source_target_pairs={{0,2},{1,3},{2,0},{3,1},{4,6},{5,7},{6,4},{7,5},{8,10},{9,11},{10,... | collective-permute-start | bytes 294920 | tf_op jit(solution)/shard_map/ppermute | solution.py:16
  11.0 5.3 %collective-permute-start.1 = (bf16[2,96,256]{2,1,0:T(8,128)(2,1)S(1)}, bf16[2,96,256]{2,1,0:T(8,128)(2,1)S(1)}, u32[]{:S(2)}, u32[]{:S(2)}) collective-permute-start(bf16[2,96,256]{2,1,0:T(8,128)(2,1)S(1)} %pad_maximum_fusion.12), channel_id=1, source_target_pairs={{0,4},{1,5},{2,6},{3,7},{4,0},{5,1},{6,2},{7,3},{8,12},{9,13},{10,... | collective-permute-start | bytes 294920 | tf_op jit(solution)/shard_map/ppermute | solution.py:16
  13.1 6.8 %collective-permute-start.10 = (bf16[2,2,96,256]{3,2,1,0:T(8,128)(2,1)S(1)}, bf16[2,2,96,256]{3,2,1,0:T(8,128)(2,1)S(1)}, u32[]{:S(2)}, u32[]{:S(2)}) collective-permute-start(bf16[2,2,96,256]{3,2,1,0:T(8,128)(2,1)S(1)} %pad_maximum_fusion.9), channel_id=1, source_target_pairs={{0,4},{1,5},{2,6},{3,7},{4,0},{5,1},{6,2},{7,3},{8,12},{9,13},{10,... | collective-permute-start | bytes 589832 | tf_op jit(solution)/shard_map/ppermute | solution.py:16
  16.4 5.7 %collective-permute-start.2 = (bf16[2,2,96,256]{3,2,0,1:T(8,128)(2,1)S(1)}, bf16[2,2,96,256]{3,2,0,1:T(8,128)(2,1)S(1)}, u32[]{:S(2)}, u32[]{:S(2)}) collective-permute-start(bf16[2,2,96,256]{3,2,0,1:T(8,128)(2,1)S(1)} %pad_maximum_fusion.8), channel_id=1, source_target_pairs={{0,2},{1,3},{2,0},{3,1},{4,6},{5,7},{6,4},{7,5},{8,10},{9,11},{10,... | collective-permute-start | bytes 589832 | tf_op jit(solution)/shard_map/ppermute | solution.py:16
  20.0 3.0 %collective-permute-start.11 = (bf16[2,2,2,96,256]{4,3,2,0,1:T(8,128)(2,1)S(1)}, bf16[2,2,2,96,256]{4,3,2,0,1:T(8,128)(2,1)S(1)}, u32[]{:S(2)}, u32[]{:S(2)}) collective-permute-start(bf16[2,2,2,96,256]{4,3,2,0,1:T(8,128)(2,1)S(1)} %pad_maximum_fusion.5), channel_id=1, source_target_pairs={{0,1},{1,0},{2,3},{3,2},{4,5},{5,4},{6,7},{7,6},{8,9},{9,8},{10,11... | collective-permute-start | bytes 1179656 | tf_op jit(solution)/shard_map/ppermute | solution.py:16
  23.0 5.2 %collective-permute-start.3 = (bf16[2,2,2,96,256]{4,3,2,1,0:T(8,128)(2,1)}, bf16[2,2,2,96,256]{4,3,2,1,0:T(8,128)(2,1)}, u32[]{:S(2)}, u32[]{:S(2)}) collective-permute-start(bf16[2,2,2,96,256]{4,3,2,1,0:T(8,128)(2,1)} %copy.47), channel_id=1, source_target_pairs={{0,1},{1,0},{2,3},{3,2},{4,5},{5,4},{6,7},{7,6},{8,9},{9,8},{10,11... | collective-permute-start | bytes 1179656 | tf_op jit(solution)/shard_map/ppermute | solution.py:16
  27.6 8.6 %collective-permute-start.12 = (f32[2,2,2,96,256]{4,3,2,1,0:T(8,128)}, f32[2,2,2,96,256]{4,3,2,1,0:T(8,128)}, u32[]{:S(2)}, u32[]{:S(2)}) collective-permute-start(f32[2,2,2,96,256]{4,3,2,1,0:T(8,128)} %dynamic-slice_bitcast_fusion.2), channel_id=1, source_target_pairs={{0,1},{1,0},{2,3},{3,2},{4,5},{5,4},{6,7},{7,6},{8,9},{9,8},{10,11... | collective-permute-start | bytes 2359304 | tf_op jit(solution)/shard_map/ppermute | solution.py:16
  35.4 0.7 copy-start.1
  35.4 0.7 copy-start.2
  35.5 4.3 %collective-permute-start.4 = (f32[2,2,2,96,256]{4,3,2,1,0:T(8,128)S(1)}, f32[2,2,2,96,256]{4,3,2,1,0:T(8,128)S(1)}, u32[]{:S(2)}, u32[]{:S(2)}) collective-permute-start(f32[2,2,2,96,256]{4,3,2,1,0:T(8,128)S(1)} %dynamic-slice_bitcast_fusion.3), channel_id=1, source_target_pairs={{0,1},{1,0},{2,3},{3,2},{4,5},{5,4},{6,7},{7,6},{8,9},{9,8},{10,11... | collective-permute-start | bytes 2359304 | tf_op jit(solution)/shard_map/ppermute | solution.py:16
  36.2 4.2 %copy-start.3 = (f32[1,1536]{1,0:T(1,128)}, f32[1,1536]{1,0:T(1,128)S(1)}, u32[]{:S(2)}) copy-start(f32[1,1536]{1,0:T(1,128)S(1)} %get-tuple-element.45) | copy-start | bytes 18436
  37.4 2.5 %copy-start = (f32[2,2,2,96,256]{4,3,2,1,0:T(8,128)}, f32[2,2,2,96,256]{4,3,2,1,0:T(8,128)S(1)}, u32[]{:S(2)}) copy-start(f32[2,2,2,96,256]{4,3,2,1,0:T(8,128)S(1)} %bitcast_add_fusion.2) | copy-start | bytes 2359300
  37.5 11.6 %collective-permute-start.13 = (f32[2,2,96,256]{3,2,1,0:T(8,128)S(1)}, f32[2,2,96,256]{3,2,1,0:T(8,128)S(1)}, u32[]{:S(2)}, u32[]{:S(2)}) collective-permute-start(f32[2,2,96,256]{3,2,1,0:T(8,128)S(1)} %dynamic-slice_bitcast_fusion.6), channel_id=1, source_target_pairs={{0,4},{1,5},{2,6},{3,7},{4,0},{5,1},{6,2},{7,3},{8,12},{9,13},{10,... | collective-permute-start | bytes 1179656 | tf_op jit(solution)/shard_map/ppermute | solution.py:16
  39.9 11.2 %collective-permute-start.5 = (f32[2,2,96,256]{3,2,1,0:T(8,128)S(1)}, f32[2,2,96,256]{3,2,1,0:T(8,128)S(1)}, u32[]{:S(2)}, u32[]{:S(2)}) collective-permute-start(f32[2,2,96,256]{3,2,1,0:T(8,128)S(1)} %dynamic-slice_bitcast_fusion.7), channel_id=1, source_target_pairs={{0,2},{1,3},{2,0},{3,1},{4,6},{5,7},{6,4},{7,5},{8,10},{9,11},{10,... | collective-permute-start | bytes 1179656 | tf_op jit(solution)/shard_map/ppermute | solution.py:16
  50.2 6.4 %collective-permute-start.14 = (f32[2,96,256]{2,1,0:T(8,128)S(1)}, f32[2,96,256]{2,1,0:T(8,128)S(1)}, u32[]{:S(2)}, u32[]{:S(2)}) collective-permute-start(f32[2,96,256]{2,1,0:T(8,128)S(1)} %dynamic-slice_bitcast_fusion.10), channel_id=1, source_target_pairs={{0,2},{1,3},{2,0},{3,1},{4,6},{5,7},{6,4},{7,5},{8,10},{9,11},{10,... | collective-permute-start | bytes 589832 | tf_op jit(solution)/shard_map/ppermute | solution.py:16
  51.2 8.7 %collective-permute-start.6 = (f32[2,96,256]{2,1,0:T(8,128)S(1)}, f32[2,96,256]{2,1,0:T(8,128)S(1)}, u32[]{:S(2)}, u32[]{:S(2)}) collective-permute-start(f32[2,96,256]{2,1,0:T(8,128)S(1)} %dynamic-slice_bitcast_fusion.11), channel_id=1, source_target_pairs={{0,4},{1,5},{2,6},{3,7},{4,0},{5,1},{6,2},{7,3},{8,12},{9,13},{10,... | collective-permute-start | bytes 589832 | tf_op jit(solution)/shard_map/ppermute | solution.py:16
  56.6 8.7 %collective-permute-start.15 = (f32[96,256]{1,0:T(8,128)S(1)}, f32[96,256]{1,0:T(8,128)S(1)}, u32[]{:S(2)}, u32[]{:S(2)}) collective-permute-start(f32[96,256]{1,0:T(8,128)S(1)} %dynamic-slice_bitcast_fusion.14), channel_id=1, source_target_pairs={{0,8},{1,9},{2,10},{3,11},{4,12},{5,13},{6,14},{7,15},{8,0},{9,1},... | collective-permute-start | bytes 294920 | tf_op jit(solution)/shard_map/ppermute | solution.py:16
  60.0 7.8 %collective-permute-start.7 = (f32[96,256]{1,0:T(8,128)S(1)}, f32[96,256]{1,0:T(8,128)S(1)}, u32[]{:S(2)}, u32[]{:S(2)}) collective-permute-start(f32[96,256]{1,0:T(8,128)S(1)} %dynamic-slice_bitcast_fusion.15), channel_id=1, source_target_pairs={{0,8},{1,9},{2,10},{3,11},{4,12},{5,13},{6,14},{7,15},{8,0},{9,1},... | collective-permute-start | bytes 294920 | tf_op jit(solution)/shard_map/ppermute | solution.py:16
  67.9 5.6 %collective-permute-start.16 = (bf16[96,256]{1,0:T(8,128)(2,1)S(1)}, bf16[96,256]{1,0:T(8,128)(2,1)S(1)}, u32[]{:S(2)}, u32[]{:S(2)}) collective-permute-start(bf16[96,256]{1,0:T(8,128)(2,1)S(1)} %get-tuple-element.16), channel_id=1, source_target_pairs={{0,8},{1,9},{2,10},{3,11},{4,12},{5,13},{6,14},{7,15},{8,0},{9,1},... | collective-permute-start | bytes 147464 | tf_op jit(solution)/shard_map/ppermute | solution.py:16
  68.0 6.7 %collective-permute-start.20 = (bf16[96,256]{1,0:T(8,128)(2,1)S(1)}, bf16[96,256]{1,0:T(8,128)(2,1)S(1)}, u32[]{:S(2)}, u32[]{:S(2)}) collective-permute-start(bf16[96,256]{1,0:T(8,128)(2,1)S(1)} %get-tuple-element.17), channel_id=1, source_target_pairs={{0,8},{1,9},{2,10},{3,11},{4,12},{5,13},{6,14},{7,15},{8,0},{9,1},... | collective-permute-start | bytes 147464 | tf_op jit(solution)/shard_map/ppermute | solution.py:16
  73.5 4.7 %collective-permute-start.17 = (bf16[2,96,256]{2,1,0:T(8,128)(2,1)S(1)}, bf16[2,96,256]{2,1,0:T(8,128)(2,1)S(1)}, u32[]{:S(2)}, u32[]{:S(2)}) collective-permute-start(bf16[2,96,256]{2,1,0:T(8,128)(2,1)S(1)} %pad_maximum_fusion.14), channel_id=1, source_target_pairs={{0,4},{1,5},{2,6},{3,7},{4,0},{5,1},{6,2},{7,3},{8,12},{9,13},{10,... | collective-permute-start | bytes 294920 | tf_op jit(solution)/shard_map/ppermute | solution.py:16
  74.7 5.7 %collective-permute-start.21 = (bf16[2,96,256]{2,1,0:T(8,128)(2,1)S(1)}, bf16[2,96,256]{2,1,0:T(8,128)(2,1)S(1)}, u32[]{:S(2)}, u32[]{:S(2)}) collective-permute-start(bf16[2,96,256]{2,1,0:T(8,128)(2,1)S(1)} %pad_maximum_fusion.15), channel_id=1, source_target_pairs={{0,2},{1,3},{2,0},{3,1},{4,6},{5,7},{6,4},{7,5},{8,10},{9,11},{10,... | collective-permute-start | bytes 294920 | tf_op jit(solution)/shard_map/ppermute | solution.py:16
  78.2 5.7 %collective-permute-start.18 = (bf16[2,2,96,256]{3,2,0,1:T(8,128)(2,1)S(1)}, bf16[2,2,96,256]{3,2,0,1:T(8,128)(2,1)S(1)}, u32[]{:S(2)}, u32[]{:S(2)}) collective-permute-start(bf16[2,2,96,256]{3,2,0,1:T(8,128)(2,1)S(1)} %pad_maximum_fusion.10), channel_id=1, source_target_pairs={{0,2},{1,3},{2,0},{3,1},{4,6},{5,7},{6,4},{7,5},{8,10},{9,11},{10,... | collective-permute-start | bytes 589832 | tf_op jit(solution)/shard_map/ppermute | solution.py:16
  80.4 5.7 %collective-permute-start.22 = (bf16[2,2,96,256]{3,2,1,0:T(8,128)(2,1)S(1)}, bf16[2,2,96,256]{3,2,1,0:T(8,128)(2,1)S(1)}, u32[]{:S(2)}, u32[]{:S(2)}) collective-permute-start(bf16[2,2,96,256]{3,2,1,0:T(8,128)(2,1)S(1)} %pad_maximum_fusion.11), channel_id=1, source_target_pairs={{0,4},{1,5},{2,6},{3,7},{4,0},{5,1},{6,2},{7,3},{8,12},{9,13},{10,... | collective-permute-start | bytes 589832 | tf_op jit(solution)/shard_map/ppermute | solution.py:16
  84.1 2.2 %collective-permute-start.19 = (bf16[2,2,2,96,256]{4,3,0,1,2:T(8,128)(2,1)S(1)}, bf16[2,2,2,96,256]{4,3,0,1,2:T(8,128)(2,1)S(1)}, u32[]{:S(2)}, u32[]{:S(2)}) collective-permute-start(bf16[2,2,2,96,256]{4,3,0,1,2:T(8,128)(2,1)S(1)} %pad_maximum_fusion.6), channel_id=1, source_target_pairs={{0,1},{1,0},{2,3},{3,2},{4,5},{5,4},{6,7},{7,6},{8,9},{9,8},{10,11... | collective-permute-start | bytes 1179656 | tf_op jit(solution)/shard_map/ppermute | solution.py:16
  86.2 1.8 %collective-permute-start.23 = (bf16[2,2,2,96,256]{4,3,2,1,0:T(8,128)(2,1)S(1)}, bf16[2,2,2,96,256]{4,3,2,1,0:T(8,128)(2,1)S(1)}, u32[]{:S(2)}, u32[]{:S(2)}) collective-permute-start(bf16[2,2,2,96,256]{4,3,2,1,0:T(8,128)(2,1)S(1)} %pad_maximum_fusion.7), channel_id=1, source_target_pairs={{0,1},{1,0},{2,3},{3,2},{4,5},{5,4},{6,7},{7,6},{8,9},{9,8},{10,11... | collective-permute-start | bytes 1179656 | tf_op jit(solution)/shard_map/ppermute | solution.py:16
  95.5 6.8 %collective-permute-start.24 = (f32[2,2,2,96,256]{4,3,2,1,0:T(8,128)}, f32[2,2,2,96,256]{4,3,2,1,0:T(8,128)}, u32[]{:S(2)}, u32[]{:S(2)}) collective-permute-start(f32[2,2,2,96,256]{4,3,2,1,0:T(8,128)} %dynamic-slice_bitcast_fusion.1), channel_id=1, source_target_pairs={{0,1},{1,0},{2,3},{3,2},{4,5},{5,4},{6,7},{7,6},{8,9},{9,8},{10,11... | collective-permute-start | bytes 2359304 | tf_op jit(solution)/shard_map/ppermute | solution.py:16
  101.8 2.4 %collective-permute-start.28 = (f32[2,2,2,96,256]{4,3,2,1,0:T(8,128)S(1)}, f32[2,2,2,96,256]{4,3,2,1,0:T(8,128)S(1)}, u32[]{:S(2)}, u32[]{:S(2)}) collective-permute-start(f32[2,2,2,96,256]{4,3,2,1,0:T(8,128)S(1)} %dynamic-slice_bitcast_fusion), channel_id=1, source_target_pairs={{0,1},{1,0},{2,3},{3,2},{4,5},{5,4},{6,7},{7,6},{8,9},{9,8},{10,11... | collective-permute-start | bytes 2359304 | tf_op jit(solution)/shard_map/ppermute | solution.py:16
  103.5 11.2 %collective-permute-start.25 = (f32[2,2,96,256]{3,2,1,0:T(8,128)S(1)}, f32[2,2,96,256]{3,2,1,0:T(8,128)S(1)}, u32[]{:S(2)}, u32[]{:S(2)}) collective-permute-start(f32[2,2,96,256]{3,2,1,0:T(8,128)S(1)} %dynamic-slice_bitcast_fusion.5), channel_id=1, source_target_pairs={{0,2},{1,3},{2,0},{3,1},{4,6},{5,7},{6,4},{7,5},{8,10},{9,11},{10,... | collective-permute-start | bytes 1179656 | tf_op jit(solution)/shard_map/ppermute | solution.py:16
  104.4 12.3 %collective-permute-start.29 = (f32[2,2,96,256]{3,2,1,0:T(8,128)S(1)}, f32[2,2,96,256]{3,2,1,0:T(8,128)S(1)}, u32[]{:S(2)}, u32[]{:S(2)}) collective-permute-start(f32[2,2,96,256]{3,2,1,0:T(8,128)S(1)} %dynamic-slice_bitcast_fusion.4), channel_id=1, source_target_pairs={{0,4},{1,5},{2,6},{3,7},{4,0},{5,1},{6,2},{7,3},{8,12},{9,13},{10,... | collective-permute-start | bytes 1179656 | tf_op jit(solution)/shard_map/ppermute | solution.py:16
  114.8 6.2 %collective-permute-start.26 = (f32[2,96,256]{2,1,0:T(8,128)S(1)}, f32[2,96,256]{2,1,0:T(8,128)S(1)}, u32[]{:S(2)}, u32[]{:S(2)}) collective-permute-start(f32[2,96,256]{2,1,0:T(8,128)S(1)} %dynamic-slice_bitcast_fusion.9), channel_id=1, source_target_pairs={{0,4},{1,5},{2,6},{3,7},{4,0},{5,1},{6,2},{7,3},{8,12},{9,13},{10,... | collective-permute-start | bytes 589832 | tf_op jit(solution)/shard_map/ppermute | solution.py:16
  116.7 6.6 %collective-permute-start.30 = (f32[2,96,256]{2,1,0:T(8,128)S(1)}, f32[2,96,256]{2,1,0:T(8,128)S(1)}, u32[]{:S(2)}, u32[]{:S(2)}) collective-permute-start(f32[2,96,256]{2,1,0:T(8,128)S(1)} %dynamic-slice_bitcast_fusion.8), channel_id=1, source_target_pairs={{0,2},{1,3},{2,0},{3,1},{4,6},{5,7},{6,4},{7,5},{8,10},{9,11},{10,... | collective-permute-start | bytes 589832 | tf_op jit(solution)/shard_map/ppermute | solution.py:16
  121.1 9.4 %collective-permute-start.27 = (f32[96,256]{1,0:T(8,128)S(1)}, f32[96,256]{1,0:T(8,128)S(1)}, u32[]{:S(2)}, u32[]{:S(2)}) collective-permute-start(f32[96,256]{1,0:T(8,128)S(1)} %dynamic-slice_bitcast_fusion.13), channel_id=1, source_target_pairs={{0,8},{1,9},{2,10},{3,11},{4,12},{5,13},{6,14},{7,15},{8,0},{9,1},... | collective-permute-start | bytes 294920 | tf_op jit(solution)/shard_map/ppermute | solution.py:16
  123.4 8.2 %collective-permute-start.31 = (f32[96,256]{1,0:T(8,128)S(1)}, f32[96,256]{1,0:T(8,128)S(1)}, u32[]{:S(2)}, u32[]{:S(2)}) collective-permute-start(f32[96,256]{1,0:T(8,128)S(1)} %dynamic-slice_bitcast_fusion.12), channel_id=1, source_target_pairs={{0,8},{1,9},{2,10},{3,11},{4,12},{5,13},{6,14},{7,15},{8,0},{9,1},... | collective-permute-start | bytes 294920 | tf_op jit(solution)/shard_map/ppermute | solution.py:16
  131.7 1.2 collective-permute-start.32
  132.9 3.6 %collective-permute-start.33 = (f32[256]{0:T(256)S(1)}, f32[256]{0:T(256)S(1)}, u32[]{:S(2)}, u32[]{:S(2)}) collective-permute-start(f32[256]{0:T(256)S(1)} %add.187), channel_id=1, source_target_pairs={{0,2},{1,3},{2,0},{3,1},{4,6},{5,7},{6,4},{7,5},{8,10},{9,11},{10,... | collective-permute-start | bytes 3080 | tf_op jit(solution)/shard_map/ppermute | solution.py:16
  136.5 3.6 %collective-permute-start.34 = (f32[256]{0:T(256)S(1)}, f32[256]{0:T(256)S(1)}, u32[]{:S(2)}, u32[]{:S(2)}) collective-permute-start(f32[256]{0:T(256)S(1)} %add.188), channel_id=1, source_target_pairs={{0,4},{1,5},{2,6},{3,7},{4,0},{5,1},{6,2},{7,3},{8,12},{9,13},{10,... | collective-permute-start | bytes 3080 | tf_op jit(solution)/shard_map/ppermute | solution.py:16
  140.0 4.5 %collective-permute-start.35 = (f32[256]{0:T(256)S(1)}, f32[256]{0:T(256)S(1)}, u32[]{:S(2)}, u32[]{:S(2)}) collective-permute-start(f32[256]{0:T(256)S(1)} %add.189), channel_id=1, source_target_pairs={{0,8},{1,9},{2,10},{3,11},{4,12},{5,13},{6,14},{7,15},{8,0},{9,1},... | collective-permute-start | bytes 3080 | tf_op jit(solution)/shard_map/ppermute | solution.py:16

commit v5 on v4

--- a/solution.py
+++ b/solution.py
@@ -47,6 +47,11 @@
 
 
 def doubling_all_reduce(x, devices):
+    if devices <= 16:
+        total = x
+        for shift in range(1, devices):
+            total = total + exchange(x, shift, devices)
+        return total
     bits = devices.bit_length() - 1
     for bit in range(bits):
         x = x + exchange(x, 1 << bit, devices)

time: 146 us -> 157 us (1.075)
  starting transfers between devices: 38.4 us -> 57.3 us
  waiting for transfers between devices: 69.8 us -> 62.2 us
    ppermute x36 -> x47, starting transfers between devices: 38.4 us -> 57.3 us  [exchange(): return lax.ppermute(x, 'row', [(i, i ^ distance) for i in range(devices)])]
    ppermute x36 -> x47, waiting for transfers between devices: 69.8 us -> 62.2 us  [exchange(): return lax.ppermute(x, 'row', [(i, i ^ distance) for i in range(devices)])]
  transfers between devices with their start and end apart: 36 -> 47, of which waited for: 23 -> 21; matrix products, arithmetic and copies ran while one was open for 18% -> 17% of each run, Pallas kernels for 0% -> 0%
where the time goes in v5:
time: 157 us; the launch traced here: 156 us
  waiting for transfers between devices  62.2 us (40%)
  starting transfers between devices  57.3 us (36%)
  matrix products  15.4 us (10%)
  local copies, waits for them, and re-layouts  10.9 us (7%)
  other arithmetic  9.4 us (6%)
    ppermute x47, waiting for transfers between devices, exchange(): return lax.ppermute(x, 'row', [(i, i ^ distance) for i in range(devices)])  62.2 us
    ppermute x47, starting transfers between devices, exchange(): return lax.ppermute(x, 'row', [(i, i ^ distance) for i in range(devices)])  57.3 us
    dot_general x4, matrix products, contract_rows(): lax.dot_general(left, right, (((0,), (0,)), ((), ())), preferred_element_...  15.4 us
    dot_general x4, local copies, waits for them, and re-layouts, contract_rows(): lax.dot_general(left, right, (((0,), (0,)), ((), ())), preferred_element_...  6.08 us
    add x12, other arithmetic, halving_reduce_scatter(): cur = keep + exchange(send, 1 << bit, devices)  3.99 us
    another operation x32, other arithmetic, doubling_all_gather(): jnp.stack([jnp.where(low, cur, other), jnp.where(low, other, cur)], axis=...  3.75 us
  transfers between devices with their start and end apart: 47, of which 21 were waited for; matrix products, arithmetic and copies ran while one was open for 17% of the time, Pallas kernels for 0%

profile of v5, /device:TPU:0, one launch (start us, length us, event | category | flops | bytes accessed | tf_op | source)
XLA Modules:
  0.0 156.4 jit_solution(5739015072060993713)
XLA Ops:
  0.6 4.1 %collective-permute-start.8 = (bf16[96,256]{1,0:T(8,128)(2,1)}, bf16[96,256]{1,0:T(8,128)(2,1)S(1)}, u32[]{:S(2)}, u32[]{:S(2)}) collective-permute-start(bf16[96,256]{1,0:T(8,128)(2,1)} %param.7), channel_id=1, source_target_pairs={{0,8},{1,9},{2,10},{3,11},{4,12},{5,13},{6,14},{7,15},{8,0},{9,1},... | collective-permute-start | bytes 147464 | tf_op jit(solution)/shard_map/ppermute | solution.py:16
  4.8 2.7 %collective-permute-done.8 = bf16[96,256]{1,0:T(8,128)(2,1)S(1)} collective-permute-done((bf16[96,256]{1,0:T(8,128)(2,1)}, bf16[96,256]{1,0:T(8,128)(2,1)S(1)}, u32[]{:S(2)}, u32[]{:S(2)}) %collective-permute-start.8) | collective-permute-done | bytes 49184 | tf_op jit(solution)/shard_map/ppermute | solution.py:16
  7.5 0.8 select_bitcast_fusion.29
  8.4 1.8 %collective-permute-start.9 = (bf16[2,96,256]{2,1,0:T(8,128)(2,1)S(1)}, bf16[2,96,256]{2,1,0:T(8,128)(2,1)S(1)}, u32[]{:S(2)}, u32[]{:S(2)}) collective-permute-start(bf16[2,96,256]{2,1,0:T(8,128)(2,1)S(1)} %pad_maximum_fusion.13), channel_id=1, source_target_pairs={{0,2},{1,3},{2,0},{3,1},{4,6},{5,7},{6,4},{7,5},{8,10},{9,11},{10,... | collective-permute-start | bytes 294920 | tf_op jit(solution)/shard_map/ppermute | solution.py:16
  10.2 0.8 select_bitcast_fusion.31
  11.0 2.0 %collective-permute-start.1 = (bf16[2,96,256]{2,1,0:T(8,128)(2,1)S(1)}, bf16[2,96,256]{2,1,0:T(8,128)(2,1)S(1)}, u32[]{:S(2)}, u32[]{:S(2)}) collective-permute-start(bf16[2,96,256]{2,1,0:T(8,128)(2,1)S(1)} %pad_maximum_fusion.12), channel_id=1, source_target_pairs={{0,4},{1,5},{2,6},{3,7},{4,0},{5,1},{6,2},{7,3},{8,12},{9,13},{10,... | collective-permute-start | bytes 294920 | tf_op jit(solution)/shard_map/ppermute | solution.py:16
  13.1 2.2 %collective-permute-start.10 = (bf16[2,2,96,256]{3,2,1,0:T(8,128)(2,1)S(1)}, bf16[2,2,96,256]{3,2,1,0:T(8,128)(2,1)S(1)}, u32[]{:S(2)}, u32[]{:S(2)}) collective-permute-start(bf16[2,2,96,256]{3,2,1,0:T(8,128)(2,1)S(1)} %pad_maximum_fusion.9), channel_id=1, source_target_pairs={{0,4},{1,5},{2,6},{3,7},{4,0},{5,1},{6,2},{7,3},{8,12},{9,13},{10,... | collective-permute-start | bytes 589832 | tf_op jit(solution)/shard_map/ppermute | solution.py:16
  15.3 1.0 collective-permute-done.1
  16.4 1.5 collective-permute-start.2
  17.9 2.0 %collective-permute-done.10 = bf16[2,2,96,256]{3,2,1,0:T(8,128)(2,1)S(1)} collective-permute-done((bf16[2,2,96,256]{3,2,1,0:T(8,128)(2,1)S(1)}, bf16[2,2,96,256]{3,2,1,0:T(8,128)(2,1)S(1)}, u32[]{:S(2)}, u32[]{:S(2)}) %collective-permute-start.10) | collective-permute-done | bytes 196640 | tf_op jit(solution)/shard_map/ppermute | solution.py:16
  20.1 2.0 %collective-permute-done.2 = bf16[2,2,96,256]{3,2,0,1:T(8,128)(2,1)S(1)} collective-permute-done((bf16[2,2,96,256]{3,2,0,1:T(8,128)(2,1)S(1)}, bf16[2,2,96,256]{3,2,0,1:T(8,128)(2,1)S(1)}, u32[]{:S(2)}, u32[]{:S(2)}) %collective-permute-start.2) | collective-permute-done | bytes 196640 | tf_op jit(solution)/shard_map/ppermute | solution.py:16
  23.2 3.0 %convolution_bitcast_fusion.2 = f32[1536,256]{0,1:T(8,128)S(1)} fusion(bf16[1536,256]{1,0:T(8,128)(2,1)S(1)} %bitcast.250, bf16[3,512,1536]{2,1,0:T(8,128)(2,1)} %param.5), kind=kOutput, calls=%fused_computation.2 | convolution fusion | flops 805437440 | bytes 5505024 | tf_op jit(solution)/shard_map/dot_general | solution.py:10
  26.6 1.0 dynamic-slice_bitcast_fusion.2
  28.1 1.2 select_bitcast_fusion.7
  29.4 4.2 %convolution_bitcast_fusion.3 = f32[1536,256]{0,1:T(8,128)} fusion(bf16[1536,256]{1,0:T(8,128)(2,1)S(1)} %bitcast.248, bf16[3,512,1536]{2,1,0:T(8,128)(2,1)} %param.5), kind=kOutput, calls=%fused_computation.3 | convolution fusion | flops 805437440 | bytes 5505024 | tf_op jit(solution)/shard_map/dot_general | solution.py:10
  33.5 1.9 %copy.32 = f32[1536,256]{1,0:T(8,128)S(1)} copy(f32[1536,256]{0,1:T(8,128)} %convolution_bitcast_fusion.3) | data formatting | bytes 3145728 | tf_op jit(solution)/shard_map/dot_general | solution.py:10
  36.2 1.2 bitcast_add_fusion.2
  37.5 2.3 %collective-permute-start.13 = (f32[2,2,96,256]{3,2,1,0:T(8,128)S(1)}, f32[2,2,96,256]{3,2,1,0:T(8,128)S(1)}, u32[]{:S(2)}, u32[]{:S(2)}) collective-permute-start(f32[2,2,96,256]{3,2,1,0:T(8,128)S(1)} %dynamic-slice_bitcast_fusion.6), channel_id=1, source_target_pairs={{0,4},{1,5},{2,6},{3,7},{4,0},{5,1},{6,2},{7,3},{8,12},{9,13},{10,... | collective-permute-start | bytes 1179656 | tf_op jit(solution)/shard_map/ppermute | solution.py:16
  40.4 8.6 %collective-permute-done.13 = f32[2,2,96,256]{3,2,1,0:T(8,128)S(1)} collective-permute-done((f32[2,2,96,256]{3,2,1,0:T(8,128)S(1)}, f32[2,2,96,256]{3,2,1,0:T(8,128)S(1)}, u32[]{:S(2)}, u32[]{:S(2)}) %collective-permute-start.13) | collective-permute-done | bytes 393248 | tf_op jit(solution)/shard_map/ppermute | solution.py:16
  49.1 1.0 bitcast_add_fusion.6
  50.2 1.0 collective-permute-start.14
  51.2 1.2 collective-permute-start.6
  52.4 4.1 %collective-permute-done.14 = f32[2,96,256]{2,1,0:T(8,128)S(1)} collective-permute-done((f32[2,96,256]{2,1,0:T(8,128)S(1)}, f32[2,96,256]{2,1,0:T(8,128)S(1)}, u32[]{:S(2)}, u32[]{:S(2)}) %collective-permute-start.14) | collective-permute-done | bytes 196640 | tf_op jit(solution)/shard_map/ppermute | solution.py:16
  56.6 3.3 %collective-permute-start.15 = (f32[96,256]{1,0:T(8,128)S(1)}, f32[96,256]{1,0:T(8,128)S(1)}, u32[]{:S(2)}, u32[]{:S(2)}) collective-permute-start(f32[96,256]{1,0:T(8,128)S(1)} %dynamic-slice_bitcast_fusion.14), channel_id=1, source_target_pairs={{0,8},{1,9},{2,10},{3,11},{4,12},{5,13},{6,14},{7,15},{8,0},{9,1},... | collective-permute-start | bytes 294920 | tf_op jit(solution)/shard_map/ppermute | solution.py:16
  60.1 0.8 cosine_bitcast_fusion
  60.9 4.4 %collective-permute-done.15 = f32[96,256]{1,0:T(8,128)S(1)} collective-permute-done((f32[96,256]{1,0:T(8,128)S(1)}, f32[96,256]{1,0:T(8,128)S(1)}, u32[]{:S(2)}, u32[]{:S(2)}) %collective-permute-start.15) | collective-permute-done | bytes 98336 | tf_op jit(solution)/shard_map/ppermute | solution.py:16
  65.3 2.5 %collective-permute-done.7 = f32[96,256]{1,0:T(8,128)S(1)} collective-permute-done((f32[96,256]{1,0:T(8,128)S(1)}, f32[96,256]{1,0:T(8,128)S(1)}, u32[]{:S(2)}, u32[]{:S(2)}) %collective-permute-start.7) | collective-permute-done | bytes 98336 | tf_op jit(solution)/shard_map/ppermute | solution.py:16
  67.9 2.9 %collective-permute-start.20 = (bf16[96,256]{1,0:T(8,128)(2,1)S(1)}, bf16[96,256]{1,0:T(8,128)(2,1)S(1)}, u32[]{:S(2)}, u32[]{:S(2)}) collective-permute-start(bf16[96,256]{1,0:T(8,128)(2,1)S(1)} %get-tuple-element.17), channel_id=1, source_target_pairs={{0,8},{1,9},{2,10},{3,11},{4,12},{5,13},{6,14},{7,15},{8,0},{9,1},... | collective-permute-start | bytes 147464 | tf_op jit(solution)/shard_map/ppermute | solution.py:16
  70.9 2.6 %collective-permute-done.16 = bf16[96,256]{1,0:T(8,128)(2,1)S(1)} collective-permute-done((bf16[96,256]{1,0:T(8,128)(2,1)S(1)}, bf16[96,256]{1,0:T(8,128)(2,1)S(1)}, u32[]{:S(2)}, u32[]{:S(2)}) %collective-permute-start.16) | collective-permute-done | bytes 49184 | tf_op jit(solution)/shard_map/ppermute | solution.py:16
  75.4 2.8 %collective-permute-done.17 = bf16[2,96,256]{2,1,0:T(8,128)(2,1)S(1)} collective-permute-done((bf16[2,96,256]{2,1,0:T(8,128)(2,1)S(1)}, bf16[2,96,256]{2,1,0:T(8,128)(2,1)S(1)}, u32[]{:S(2)}, u32[]{:S(2)}) %collective-permute-start.17) | collective-permute-done | bytes 98336 | tf_op jit(solution)/shard_map/ppermute | solution.py:16
  79.0 1.3 collective-permute-done.21
  80.4 1.8 %collective-permute-start.22 = (bf16[2,2,96,256]{3,2,1,0:T(8,128)(2,1)S(1)}, bf16[2,2,96,256]{3,2,1,0:T(8,128)(2,1)S(1)}, u32[]{:S(2)}, u32[]{:S(2)}) collective-permute-start(bf16[2,2,96,256]{3,2,1,0:T(8,128)(2,1)S(1)} %pad_maximum_fusion.11), channel_id=1, source_target_pairs={{0,4},{1,5},{2,6},{3,7},{4,0},{5,1},{6,2},{7,3},{8,12},{9,13},{10,... | collective-permute-start | bytes 589832 | tf_op jit(solution)/shard_map/ppermute | solution.py:16
  82.2 1.8 %collective-permute-done.18 = bf16[2,2,96,256]{3,2,0,1:T(8,128)(2,1)S(1)} collective-permute-done((bf16[2,2,96,256]{3,2,0,1:T(8,128)(2,1)S(1)}, bf16[2,2,96,256]{3,2,0,1:T(8,128)(2,1)S(1)}, u32[]{:S(2)}, u32[]{:S(2)}) %collective-permute-start.18) | collective-permute-done | bytes 196640 | tf_op jit(solution)/shard_map/ppermute | solution.py:16
  84.1 2.0 %collective-permute-done.22 = bf16[2,2,96,256]{3,2,1,0:T(8,128)(2,1)S(1)} collective-permute-done((bf16[2,2,96,256]{3,2,1,0:T(8,128)(2,1)S(1)}, bf16[2,2,96,256]{3,2,1,0:T(8,128)(2,1)S(1)}, u32[]{:S(2)}, u32[]{:S(2)}) %collective-permute-start.22) | collective-permute-done | bytes 196640 | tf_op jit(solution)/shard_map/ppermute | solution.py:16
  86.7 1.3 collective-permute-done.23
  88.4 4.2 %convolution_bitcast_fusion.1 = f32[1536,256]{0,1:T(8,128)} fusion(bf16[3,512,1536]{2,1,0:T(8,128)(2,1)} %param.5, bf16[1536,256]{1,0:T(8,128)(2,1)S(1)} %bitcast.247, f32[256]{0:T(256)S(1)} %add_rsqrt_fusion.1), kind=kOutput, calls=%fused_computation.1 | convolution fusion | flops 805568512 | bytes 5506048 | tf_op jit(solution)/shard_map/dot_general | solution.py:10
  92.6 1.9 %copy.44 = f32[1536,256]{1,0:T(8,128)S(1)} copy(f32[1536,256]{0,1:T(8,128)} %convolution_bitcast_fusion.1) | data formatting | bytes 3145728 | tf_op jit(solution)/shard_map/dot_general | solution.py:10
  94.5 1.0 dynamic-slice_bitcast_fusion.1
  95.7 4.2 %convolution_bitcast_fusion = f32[1536,256]{0,1:T(8,128)} fusion(bf16[3,512,1536]{2,1,0:T(8,128)(2,1)} %param.5, bf16[1536,256]{1,0:T(8,128)(2,1)S(1)} %bitcast.249, f32[256]{0:T(256)S(1)} %add_rsqrt_fusion.1), kind=kOutput, calls=%fused_computation | convolution fusion | flops 805568512 | bytes 5506048 | tf_op jit(solution)/shard_map/dot_general | solution.py:10
  99.8 1.9 %copy.46 = f32[1536,256]{1,0:T(8,128)S(1)} copy(f32[1536,256]{0,1:T(8,128)} %convolution_bitcast_fusion) | data formatting | bytes 3145728 | tf_op jit(solution)/shard_map/dot_general | solution.py:10
  102.2 1.2 bitcast_add_fusion.1
  103.5 0.8 collective-permute-start.25
  104.4 1.8 %collective-permute-start.29 = (f32[2,2,96,256]{3,2,1,0:T(8,128)S(1)}, f32[2,2,96,256]{3,2,1,0:T(8,128)S(1)}, u32[]{:S(2)}, u32[]{:S(2)}) collective-permute-start(f32[2,2,96,256]{3,2,1,0:T(8,128)S(1)} %dynamic-slice_bitcast_fusion.4), channel_id=1, source_target_pairs={{0,4},{1,5},{2,6},{3,7},{4,0},{5,1},{6,2},{7,3},{8,12},{9,13},{10,... | collective-permute-start | bytes 1179656 | tf_op jit(solution)/shard_map/ppermute | solution.py:16
  106.4 8.3 %collective-permute-done.25 = f32[2,2,96,256]{3,2,1,0:T(8,128)S(1)} collective-permute-done((f32[2,2,96,256]{3,2,1,0:T(8,128)S(1)}, f32[2,2,96,256]{3,2,1,0:T(8,128)S(1)}, u32[]{:S(2)}, u32[]{:S(2)}) %collective-permute-start.25) | collective-permute-done | bytes 393248 | tf_op jit(solution)/shard_map/ppermute | solution.py:16
  114.8 1.8 %collective-permute-start.26 = (f32[2,96,256]{2,1,0:T(8,128)S(1)}, f32[2,96,256]{2,1,0:T(8,128)S(1)}, u32[]{:S(2)}, u32[]{:S(2)}) collective-permute-start(f32[2,96,256]{2,1,0:T(8,128)S(1)} %dynamic-slice_bitcast_fusion.9), channel_id=1, source_target_pairs={{0,4},{1,5},{2,6},{3,7},{4,0},{5,1},{6,2},{7,3},{8,12},{9,13},{10,... | collective-permute-start | bytes 589832 | tf_op jit(solution)/shard_map/ppermute | solution.py:16
  116.7 0.8 collective-permute-start.30
  117.5 3.5 %collective-permute-done.26 = f32[2,96,256]{2,1,0:T(8,128)S(1)} collective-permute-done((f32[2,96,256]{2,1,0:T(8,128)S(1)}, f32[2,96,256]{2,1,0:T(8,128)S(1)}, u32[]{:S(2)}, u32[]{:S(2)}) %collective-permute-start.26) | collective-permute-done | bytes 196640 | tf_op jit(solution)/shard_map/ppermute | solution.py:16
  121.1 2.2 %collective-permute-start.27 = (f32[96,256]{1,0:T(8,128)S(1)}, f32[96,256]{1,0:T(8,128)S(1)}, u32[]{:S(2)}, u32[]{:S(2)}) collective-permute-start(f32[96,256]{1,0:T(8,128)S(1)} %dynamic-slice_bitcast_fusion.13), channel_id=1, source_target_pairs={{0,8},{1,9},{2,10},{3,11},{4,12},{5,13},{6,14},{7,15},{8,0},{9,1},... | collective-permute-start | bytes 294920 | tf_op jit(solution)/shard_map/ppermute | solution.py:16
  123.4 1.1 collective-permute-start.31
  124.6 5.9 %collective-permute-done.27 = f32[96,256]{1,0:T(8,128)S(1)} collective-permute-done((f32[96,256]{1,0:T(8,128)S(1)}, f32[96,256]{1,0:T(8,128)S(1)}, u32[]{:S(2)}, u32[]{:S(2)}) %collective-permute-start.27) | collective-permute-done | bytes 98336 | tf_op jit(solution)/shard_map/ppermute | solution.py:16
  130.5 1.1 collective-permute-done.31
  131.8 0.8 collective-permute-start.33
  132.6 1.1 collective-permute-start.34
  133.6 1.7 %collective-permute-start.36 = (f32[256]{0:T(256)S(1)}, f32[256]{0:T(256)S(1)}, u32[]{:S(2)}, u32[]{:S(2)}) collective-permute-start(f32[256]{0:T(256)S(1)} %add.219), channel_id=1, source_target_pairs={{0,5},{1,4},{2,7},{3,6},{4,1},{5,0},{6,3},{7,2},{8,13},{9,12},{10,... | collective-permute-start | bytes 3080 | tf_op jit(solution)/shard_map/ppermute | solution.py:16
  135.9 2.2 %collective-permute-start.38 = (f32[256]{0:T(256)S(1)}, f32[256]{0:T(256)S(1)}, u32[]{:S(2)}, u32[]{:S(2)}) collective-permute-start(f32[256]{0:T(256)S(1)} %add.219), channel_id=1, source_target_pairs={{0,7},{1,6},{2,5},{3,4},{4,3},{5,2},{6,1},{7,0},{8,15},{9,14},{10,... | collective-permute-start | bytes 3080 | tf_op jit(solution)/shard_map/ppermute | solution.py:16
  138.7 1.9 %collective-permute-start.40 = (f32[256]{0:T(256)S(1)}, f32[256]{0:T(256)S(1)}, u32[]{:S(2)}, u32[]{:S(2)}) collective-permute-start(f32[256]{0:T(256)S(1)} %add.219), channel_id=1, source_target_pairs={{0,9},{1,8},{2,11},{3,10},{4,13},{5,12},{6,15},{7,14},{8,1},{9,0},... | collective-permute-start | bytes 3080 | tf_op jit(solution)/shard_map/ppermute | solution.py:16
  140.6 1.2 collective-permute-start.41
  141.8 2.4 %collective-permute-start.42 = (f32[256]{0:T(256)S(1)}, f32[256]{0:T(256)S(1)}, u32[]{:S(2)}, u32[]{:S(2)}) collective-permute-start(f32[256]{0:T(256)S(1)} %add.219), channel_id=1, source_target_pairs={{0,11},{1,10},{2,9},{3,8},{4,15},{5,14},{6,13},{7,12},{8,3},{9,2},... | collective-permute-start | bytes 3080 | tf_op jit(solution)/shard_map/ppermute | solution.py:16
  144.3 2.1 %collective-permute-start.43 = (f32[256]{0:T(256)S(1)}, f32[256]{0:T(256)S(1)}, u32[]{:S(2)}, u32[]{:S(2)}) collective-permute-start(f32[256]{0:T(256)S(1)} %add.219), channel_id=1, source_target_pairs={{0,12},{1,13},{2,14},{3,15},{4,8},{5,9},{6,10},{7,11},{8,4},{9,5},... | collective-permute-start | bytes 3080 | tf_op jit(solution)/shard_map/ppermute | solution.py:16
  146.4 1.4 collective-permute-start.44
  147.7 2.3 %collective-permute-start.45 = (f32[256]{0:T(256)S(1)}, f32[256]{0:T(256)S(1)}, u32[]{:S(2)}, u32[]{:S(2)}) collective-permute-start(f32[256]{0:T(256)S(1)} %add.219), channel_id=1, source_target_pairs={{0,14},{1,15},{2,12},{3,13},{4,10},{5,11},{6,8},{7,9},{8,6},{9,7},... | collective-permute-start | bytes 3080 | tf_op jit(solution)/shard_map/ppermute | solution.py:16
  150.0 2.2 %collective-permute-start.46 = (f32[256]{0:T(256)S(1)}, f32[256]{0:T(256)S(1)}, u32[]{:S(2)}, u32[]{:S(2)}) collective-permute-start(f32[256]{0:T(256)S(1)} %add.219), channel_id=1, source_target_pairs={{0,15},{1,14},{2,13},{3,12},{4,11},{5,10},{6,9},{7,8},{8,7},{9,6},... | collective-permute-start | bytes 3080 | tf_op jit(solution)/shard_map/ppermute | solution.py:16
  152.3 1.7 %collective-permute-done.45 = f32[256]{0:T(256)S(1)} collective-permute-done((f32[256]{0:T(256)S(1)}, f32[256]{0:T(256)S(1)}, u32[]{:S(2)}, u32[]{:S(2)}) %collective-permute-start.45) | collective-permute-done | bytes 1056 | tf_op jit(solution)/shard_map/ppermute | solution.py:16
  154.0 1.7 %collective-permute-done.46 = f32[256]{0:T(256)S(1)} collective-permute-done((f32[256]{0:T(256)S(1)}, f32[256]{0:T(256)S(1)}, u32[]{:S(2)}, u32[]{:S(2)}) %collective-permute-start.46) | collective-permute-done | bytes 1056 | tf_op jit(solution)/shard_map/ppermute | solution.py:16
  (123 shorter events, 11.7 us)
Async XLA Ops:
  0.6 6.9 %collective-permute-start.8 = (bf16[96,256]{1,0:T(8,128)(2,1)}, bf16[96,256]{1,0:T(8,128)(2,1)S(1)}, u32[]{:S(2)}, u32[]{:S(2)}) collective-permute-start(bf16[96,256]{1,0:T(8,128)(2,1)} %param.7), channel_id=1, source_target_pairs={{0,8},{1,9},{2,10},{3,11},{4,12},{5,13},{6,14},{7,15},{8,0},{9,1},... | collective-permute-start | bytes 147464 | tf_op jit(solution)/shard_map/ppermute | solution.py:16
  4.7 5.4 %collective-permute-start = (bf16[96,256]{1,0:T(8,128)(2,1)}, bf16[96,256]{1,0:T(8,128)(2,1)S(1)}, u32[]{:S(2)}, u32[]{:S(2)}) collective-permute-start(bf16[96,256]{1,0:T(8,128)(2,1)} %param.6), channel_id=1, source_target_pairs={{0,8},{1,9},{2,10},{3,11},{4,12},{5,13},{6,14},{7,15},{8,0},{9,1},... | collective-permute-start | bytes 147464 | tf_op jit(solution)/shard_map/ppermute | solution.py:16
  8.4 4.7 %collective-permute-start.9 = (bf16[2,96,256]{2,1,0:T(8,128)(2,1)S(1)}, bf16[2,96,256]{2,1,0:T(8,128)(2,1)S(1)}, u32[]{:S(2)}, u32[]{:S(2)}) collective-permute-start(bf16[2,96,256]{2,1,0:T(8,128)(2,1)S(1)} %pad_maximum_fusion.13), channel_id=1, source_target_pairs={{0,2},{1,3},{2,0},{3,1},{4,6},{5,7},{6,4},{7,5},{8,10},{9,11},{10,... | collective-permute-start | bytes 294920 | tf_op jit(solution)/shard_map/ppermute | solution.py:16
  11.0 5.3 %collective-permute-start.1 = (bf16[2,96,256]{2,1,0:T(8,128)(2,1)S(1)}, bf16[2,96,256]{2,1,0:T(8,128)(2,1)S(1)}, u32[]{:S(2)}, u32[]{:S(2)}) collective-permute-start(bf16[2,96,256]{2,1,0:T(8,128)(2,1)S(1)} %pad_maximum_fusion.12), channel_id=1, source_target_pairs={{0,4},{1,5},{2,6},{3,7},{4,0},{5,1},{6,2},{7,3},{8,12},{9,13},{10,... | collective-permute-start | bytes 294920 | tf_op jit(solution)/shard_map/ppermute | solution.py:16
  13.1 6.8 %collective-permute-start.10 = (bf16[2,2,96,256]{3,2,1,0:T(8,128)(2,1)S(1)}, bf16[2,2,96,256]{3,2,1,0:T(8,128)(2,1)S(1)}, u32[]{:S(2)}, u32[]{:S(2)}) collective-permute-start(bf16[2,2,96,256]{3,2,1,0:T(8,128)(2,1)S(1)} %pad_maximum_fusion.9), channel_id=1, source_target_pairs={{0,4},{1,5},{2,6},{3,7},{4,0},{5,1},{6,2},{7,3},{8,12},{9,13},{10,... | collective-permute-start | bytes 589832 | tf_op jit(solution)/shard_map/ppermute | solution.py:16
  16.4 5.7 %collective-permute-start.2 = (bf16[2,2,96,256]{3,2,0,1:T(8,128)(2,1)S(1)}, bf16[2,2,96,256]{3,2,0,1:T(8,128)(2,1)S(1)}, u32[]{:S(2)}, u32[]{:S(2)}) collective-permute-start(bf16[2,2,96,256]{3,2,0,1:T(8,128)(2,1)S(1)} %pad_maximum_fusion.8), channel_id=1, source_target_pairs={{0,2},{1,3},{2,0},{3,1},{4,6},{5,7},{6,4},{7,5},{8,10},{9,11},{10,... | collective-permute-start | bytes 589832 | tf_op jit(solution)/shard_map/ppermute | solution.py:16
  20.0 3.0 %collective-permute-start.11 = (bf16[2,2,2,96,256]{4,3,2,0,1:T(8,128)(2,1)S(1)}, bf16[2,2,2,96,256]{4,3,2,0,1:T(8,128)(2,1)S(1)}, u32[]{:S(2)}, u32[]{:S(2)}) collective-permute-start(bf16[2,2,2,96,256]{4,3,2,0,1:T(8,128)(2,1)S(1)} %pad_maximum_fusion.5), channel_id=1, source_target_pairs={{0,1},{1,0},{2,3},{3,2},{4,5},{5,4},{6,7},{7,6},{8,9},{9,8},{10,11... | collective-permute-start | bytes 1179656 | tf_op jit(solution)/shard_map/ppermute | solution.py:16
  23.0 5.1 %collective-permute-start.3 = (bf16[2,2,2,96,256]{4,3,2,1,0:T(8,128)(2,1)}, bf16[2,2,2,96,256]{4,3,2,1,0:T(8,128)(2,1)}, u32[]{:S(2)}, u32[]{:S(2)}) collective-permute-start(bf16[2,2,2,96,256]{4,3,2,1,0:T(8,128)(2,1)} %copy.47), channel_id=1, source_target_pairs={{0,1},{1,0},{2,3},{3,2},{4,5},{5,4},{6,7},{7,6},{8,9},{9,8},{10,11... | collective-permute-start | bytes 1179656 | tf_op jit(solution)/shard_map/ppermute | solution.py:16
  27.6 8.6 %collective-permute-start.12 = (f32[2,2,2,96,256]{4,3,2,1,0:T(8,128)}, f32[2,2,2,96,256]{4,3,2,1,0:T(8,128)}, u32[]{:S(2)}, u32[]{:S(2)}) collective-permute-start(f32[2,2,2,96,256]{4,3,2,1,0:T(8,128)} %dynamic-slice_bitcast_fusion.2), channel_id=1, source_target_pairs={{0,1},{1,0},{2,3},{3,2},{4,5},{5,4},{6,7},{7,6},{8,9},{9,8},{10,11... | collective-permute-start | bytes 2359304 | tf_op jit(solution)/shard_map/ppermute | solution.py:16
  35.4 0.7 copy-start.1
  35.4 0.7 copy-start.2
  35.5 4.3 %collective-permute-start.4 = (f32[2,2,2,96,256]{4,3,2,1,0:T(8,128)S(1)}, f32[2,2,2,96,256]{4,3,2,1,0:T(8,128)S(1)}, u32[]{:S(2)}, u32[]{:S(2)}) collective-permute-start(f32[2,2,2,96,256]{4,3,2,1,0:T(8,128)S(1)} %dynamic-slice_bitcast_fusion.3), channel_id=1, source_target_pairs={{0,1},{1,0},{2,3},{3,2},{4,5},{5,4},{6,7},{7,6},{8,9},{9,8},{10,11... | collective-permute-start | bytes 2359304 | tf_op jit(solution)/shard_map/ppermute | solution.py:16
  36.1 4.2 %copy-start.3 = (f32[1,1536]{1,0:T(1,128)}, f32[1,1536]{1,0:T(1,128)S(1)}, u32[]{:S(2)}) copy-start(f32[1,1536]{1,0:T(1,128)S(1)} %get-tuple-element.45) | copy-start | bytes 18436
  37.4 2.5 %copy-start = (f32[2,2,2,96,256]{4,3,2,1,0:T(8,128)}, f32[2,2,2,96,256]{4,3,2,1,0:T(8,128)S(1)}, u32[]{:S(2)}) copy-start(f32[2,2,2,96,256]{4,3,2,1,0:T(8,128)S(1)} %bitcast_add_fusion.2) | copy-start | bytes 2359300
  37.5 11.6 %collective-permute-start.13 = (f32[2,2,96,256]{3,2,1,0:T(8,128)S(1)}, f32[2,2,96,256]{3,2,1,0:T(8,128)S(1)}, u32[]{:S(2)}, u32[]{:S(2)}) collective-permute-start(f32[2,2,96,256]{3,2,1,0:T(8,128)S(1)} %dynamic-slice_bitcast_fusion.6), channel_id=1, source_target_pairs={{0,4},{1,5},{2,6},{3,7},{4,0},{5,1},{6,2},{7,3},{8,12},{9,13},{10,... | collective-permute-start | bytes 1179656 | tf_op jit(solution)/shard_map/ppermute | solution.py:16
  39.9 11.2 %collective-permute-start.5 = (f32[2,2,96,256]{3,2,1,0:T(8,128)S(1)}, f32[2,2,96,256]{3,2,1,0:T(8,128)S(1)}, u32[]{:S(2)}, u32[]{:S(2)}) collective-permute-start(f32[2,2,96,256]{3,2,1,0:T(8,128)S(1)} %dynamic-slice_bitcast_fusion.7), channel_id=1, source_target_pairs={{0,2},{1,3},{2,0},{3,1},{4,6},{5,7},{6,4},{7,5},{8,10},{9,11},{10,... | collective-permute-start | bytes 1179656 | tf_op jit(solution)/shard_map/ppermute | solution.py:16
  50.2 6.4 %collective-permute-start.14 = (f32[2,96,256]{2,1,0:T(8,128)S(1)}, f32[2,96,256]{2,1,0:T(8,128)S(1)}, u32[]{:S(2)}, u32[]{:S(2)}) collective-permute-start(f32[2,96,256]{2,1,0:T(8,128)S(1)} %dynamic-slice_bitcast_fusion.10), channel_id=1, source_target_pairs={{0,2},{1,3},{2,0},{3,1},{4,6},{5,7},{6,4},{7,5},{8,10},{9,11},{10,... | collective-permute-start | bytes 589832 | tf_op jit(solution)/shard_map/ppermute | solution.py:16
  51.2 8.7 %collective-permute-start.6 = (f32[2,96,256]{2,1,0:T(8,128)S(1)}, f32[2,96,256]{2,1,0:T(8,128)S(1)}, u32[]{:S(2)}, u32[]{:S(2)}) collective-permute-start(f32[2,96,256]{2,1,0:T(8,128)S(1)} %dynamic-slice_bitcast_fusion.11), channel_id=1, source_target_pairs={{0,4},{1,5},{2,6},{3,7},{4,0},{5,1},{6,2},{7,3},{8,12},{9,13},{10,... | collective-permute-start | bytes 589832 | tf_op jit(solution)/shard_map/ppermute | solution.py:16
  56.6 8.7 %collective-permute-start.15 = (f32[96,256]{1,0:T(8,128)S(1)}, f32[96,256]{1,0:T(8,128)S(1)}, u32[]{:S(2)}, u32[]{:S(2)}) collective-permute-start(f32[96,256]{1,0:T(8,128)S(1)} %dynamic-slice_bitcast_fusion.14), channel_id=1, source_target_pairs={{0,8},{1,9},{2,10},{3,11},{4,12},{5,13},{6,14},{7,15},{8,0},{9,1},... | collective-permute-start | bytes 294920 | tf_op jit(solution)/shard_map/ppermute | solution.py:16
  59.9 7.8 %collective-permute-start.7 = (f32[96,256]{1,0:T(8,128)S(1)}, f32[96,256]{1,0:T(8,128)S(1)}, u32[]{:S(2)}, u32[]{:S(2)}) collective-permute-start(f32[96,256]{1,0:T(8,128)S(1)} %dynamic-slice_bitcast_fusion.15), channel_id=1, source_target_pairs={{0,8},{1,9},{2,10},{3,11},{4,12},{5,13},{6,14},{7,15},{8,0},{9,1},... | collective-permute-start | bytes 294920 | tf_op jit(solution)/shard_map/ppermute | solution.py:16
  67.9 5.6 %collective-permute-start.16 = (bf16[96,256]{1,0:T(8,128)(2,1)S(1)}, bf16[96,256]{1,0:T(8,128)(2,1)S(1)}, u32[]{:S(2)}, u32[]{:S(2)}) collective-permute-start(bf16[96,256]{1,0:T(8,128)(2,1)S(1)} %get-tuple-element.16), channel_id=1, source_target_pairs={{0,8},{1,9},{2,10},{3,11},{4,12},{5,13},{6,14},{7,15},{8,0},{9,1},... | collective-permute-start | bytes 147464 | tf_op jit(solution)/shard_map/ppermute | solution.py:16
  67.9 6.7 %collective-permute-start.20 = (bf16[96,256]{1,0:T(8,128)(2,1)S(1)}, bf16[96,256]{1,0:T(8,128)(2,1)S(1)}, u32[]{:S(2)}, u32[]{:S(2)}) collective-permute-start(bf16[96,256]{1,0:T(8,128)(2,1)S(1)} %get-tuple-element.17), channel_id=1, source_target_pairs={{0,8},{1,9},{2,10},{3,11},{4,12},{5,13},{6,14},{7,15},{8,0},{9,1},... | collective-permute-start | bytes 147464 | tf_op jit(solution)/shard_map/ppermute | solution.py:16
  73.5 4.7 %collective-permute-start.17 = (bf16[2,96,256]{2,1,0:T(8,128)(2,1)S(1)}, bf16[2,96,256]{2,1,0:T(8,128)(2,1)S(1)}, u32[]{:S(2)}, u32[]{:S(2)}) collective-permute-start(bf16[2,96,256]{2,1,0:T(8,128)(2,1)S(1)} %pad_maximum_fusion.14), channel_id=1, source_target_pairs={{0,4},{1,5},{2,6},{3,7},{4,0},{5,1},{6,2},{7,3},{8,12},{9,13},{10,... | collective-permute-start | bytes 294920 | tf_op jit(solution)/shard_map/ppermute | solution.py:16
  74.7 5.7 %collective-permute-start.21 = (bf16[2,96,256]{2,1,0:T(8,128)(2,1)S(1)}, bf16[2,96,256]{2,1,0:T(8,128)(2,1)S(1)}, u32[]{:S(2)}, u32[]{:S(2)}) collective-permute-start(bf16[2,96,256]{2,1,0:T(8,128)(2,1)S(1)} %pad_maximum_fusion.15), channel_id=1, source_target_pairs={{0,2},{1,3},{2,0},{3,1},{4,6},{5,7},{6,4},{7,5},{8,10},{9,11},{10,... | collective-permute-start | bytes 294920 | tf_op jit(solution)/shard_map/ppermute | solution.py:16
  78.2 5.7 %collective-permute-start.18 = (bf16[2,2,96,256]{3,2,0,1:T(8,128)(2,1)S(1)}, bf16[2,2,96,256]{3,2,0,1:T(8,128)(2,1)S(1)}, u32[]{:S(2)}, u32[]{:S(2)}) collective-permute-start(bf16[2,2,96,256]{3,2,0,1:T(8,128)(2,1)S(1)} %pad_maximum_fusion.10), channel_id=1, source_target_pairs={{0,2},{1,3},{2,0},{3,1},{4,6},{5,7},{6,4},{7,5},{8,10},{9,11},{10,... | collective-permute-start | bytes 589832 | tf_op jit(solution)/shard_map/ppermute | solution.py:16
  80.4 5.7 %collective-permute-start.22 = (bf16[2,2,96,256]{3,2,1,0:T(8,128)(2,1)S(1)}, bf16[2,2,96,256]{3,2,1,0:T(8,128)(2,1)S(1)}, u32[]{:S(2)}, u32[]{:S(2)}) collective-permute-start(bf16[2,2,96,256]{3,2,1,0:T(8,128)(2,1)S(1)} %pad_maximum_fusion.11), channel_id=1, source_target_pairs={{0,4},{1,5},{2,6},{3,7},{4,0},{5,1},{6,2},{7,3},{8,12},{9,13},{10,... | collective-permute-start | bytes 589832 | tf_op jit(solution)/shard_map/ppermute | solution.py:16
  84.0 2.2 %collective-permute-start.19 = (bf16[2,2,2,96,256]{4,3,0,1,2:T(8,128)(2,1)S(1)}, bf16[2,2,2,96,256]{4,3,0,1,2:T(8,128)(2,1)S(1)}, u32[]{:S(2)}, u32[]{:S(2)}) collective-permute-start(bf16[2,2,2,96,256]{4,3,0,1,2:T(8,128)(2,1)S(1)} %pad_maximum_fusion.6), channel_id=1, source_target_pairs={{0,1},{1,0},{2,3},{3,2},{4,5},{5,4},{6,7},{7,6},{8,9},{9,8},{10,11... | collective-permute-start | bytes 1179656 | tf_op jit(solution)/shard_map/ppermute | solution.py:16
  86.2 1.8 %collective-permute-start.23 = (bf16[2,2,2,96,256]{4,3,2,1,0:T(8,128)(2,1)S(1)}, bf16[2,2,2,96,256]{4,3,2,1,0:T(8,128)(2,1)S(1)}, u32[]{:S(2)}, u32[]{:S(2)}) collective-permute-start(bf16[2,2,2,96,256]{4,3,2,1,0:T(8,128)(2,1)S(1)} %pad_maximum_fusion.7), channel_id=1, source_target_pairs={{0,1},{1,0},{2,3},{3,2},{4,5},{5,4},{6,7},{7,6},{8,9},{9,8},{10,11... | collective-permute-start | bytes 1179656 | tf_op jit(solution)/shard_map/ppermute | solution.py:16
  95.5 6.8 %collective-permute-start.24 = (f32[2,2,2,96,256]{4,3,2,1,0:T(8,128)}, f32[2,2,2,96,256]{4,3,2,1,0:T(8,128)}, u32[]{:S(2)}, u32[]{:S(2)}) collective-permute-start(f32[2,2,2,96,256]{4,3,2,1,0:T(8,128)} %dynamic-slice_bitcast_fusion.1), channel_id=1, source_target_pairs={{0,1},{1,0},{2,3},{3,2},{4,5},{5,4},{6,7},{7,6},{8,9},{9,8},{10,11... | collective-permute-start | bytes 2359304 | tf_op jit(solution)/shard_map/ppermute | solution.py:16
  101.8 2.5 %collective-permute-start.28 = (f32[2,2,2,96,256]{4,3,2,1,0:T(8,128)S(1)}, f32[2,2,2,96,256]{4,3,2,1,0:T(8,128)S(1)}, u32[]{:S(2)}, u32[]{:S(2)}) collective-permute-start(f32[2,2,2,96,256]{4,3,2,1,0:T(8,128)S(1)} %dynamic-slice_bitcast_fusion), channel_id=1, source_target_pairs={{0,1},{1,0},{2,3},{3,2},{4,5},{5,4},{6,7},{7,6},{8,9},{9,8},{10,11... | collective-permute-start | bytes 2359304 | tf_op jit(solution)/shard_map/ppermute | solution.py:16
  103.5 11.2 %collective-permute-start.25 = (f32[2,2,96,256]{3,2,1,0:T(8,128)S(1)}, f32[2,2,96,256]{3,2,1,0:T(8,128)S(1)}, u32[]{:S(2)}, u32[]{:S(2)}) collective-permute-start(f32[2,2,96,256]{3,2,1,0:T(8,128)S(1)} %dynamic-slice_bitcast_fusion.5), channel_id=1, source_target_pairs={{0,2},{1,3},{2,0},{3,1},{4,6},{5,7},{6,4},{7,5},{8,10},{9,11},{10,... | collective-permute-start | bytes 1179656 | tf_op jit(solution)/shard_map/ppermute | solution.py:16
  104.4 12.2 %collective-permute-start.29 = (f32[2,2,96,256]{3,2,1,0:T(8,128)S(1)}, f32[2,2,96,256]{3,2,1,0:T(8,128)S(1)}, u32[]{:S(2)}, u32[]{:S(2)}) collective-permute-start(f32[2,2,96,256]{3,2,1,0:T(8,128)S(1)} %dynamic-slice_bitcast_fusion.4), channel_id=1, source_target_pairs={{0,4},{1,5},{2,6},{3,7},{4,0},{5,1},{6,2},{7,3},{8,12},{9,13},{10,... | collective-permute-start | bytes 1179656 | tf_op jit(solution)/shard_map/ppermute | solution.py:16
  114.8 6.2 %collective-permute-start.26 = (f32[2,96,256]{2,1,0:T(8,128)S(1)}, f32[2,96,256]{2,1,0:T(8,128)S(1)}, u32[]{:S(2)}, u32[]{:S(2)}) collective-permute-start(f32[2,96,256]{2,1,0:T(8,128)S(1)} %dynamic-slice_bitcast_fusion.9), channel_id=1, source_target_pairs={{0,4},{1,5},{2,6},{3,7},{4,0},{5,1},{6,2},{7,3},{8,12},{9,13},{10,... | collective-permute-start | bytes 589832 | tf_op jit(solution)/shard_map/ppermute | solution.py:16
  116.7 6.6 %collective-permute-start.30 = (f32[2,96,256]{2,1,0:T(8,128)S(1)}, f32[2,96,256]{2,1,0:T(8,128)S(1)}, u32[]{:S(2)}, u32[]{:S(2)}) collective-permute-start(f32[2,96,256]{2,1,0:T(8,128)S(1)} %dynamic-slice_bitcast_fusion.8), channel_id=1, source_target_pairs={{0,2},{1,3},{2,0},{3,1},{4,6},{5,7},{6,4},{7,5},{8,10},{9,11},{10,... | collective-permute-start | bytes 589832 | tf_op jit(solution)/shard_map/ppermute | solution.py:16
  121.1 9.4 %collective-permute-start.27 = (f32[96,256]{1,0:T(8,128)S(1)}, f32[96,256]{1,0:T(8,128)S(1)}, u32[]{:S(2)}, u32[]{:S(2)}) collective-permute-start(f32[96,256]{1,0:T(8,128)S(1)} %dynamic-slice_bitcast_fusion.13), channel_id=1, source_target_pairs={{0,8},{1,9},{2,10},{3,11},{4,12},{5,13},{6,14},{7,15},{8,0},{9,1},... | collective-permute-start | bytes 294920 | tf_op jit(solution)/shard_map/ppermute | solution.py:16
  123.4 8.2 %collective-permute-start.31 = (f32[96,256]{1,0:T(8,128)S(1)}, f32[96,256]{1,0:T(8,128)S(1)}, u32[]{:S(2)}, u32[]{:S(2)}) collective-permute-start(f32[96,256]{1,0:T(8,128)S(1)} %dynamic-slice_bitcast_fusion.12), channel_id=1, source_target_pairs={{0,8},{1,9},{2,10},{3,11},{4,12},{5,13},{6,14},{7,15},{8,0},{9,1},... | collective-permute-start | bytes 294920 | tf_op jit(solution)/shard_map/ppermute | solution.py:16
  131.7 3.6 %collective-permute-start.32 = (f32[256]{0:T(256)S(1)}, f32[256]{0:T(256)S(1)}, u32[]{:S(2)}, u32[]{:S(2)}) collective-permute-start(f32[256]{0:T(256)S(1)} %add.219), channel_id=1, source_target_pairs={{0,1},{1,0},{2,3},{3,2},{4,5},{5,4},{6,7},{7,6},{8,9},{9,8},{10,11... | collective-permute-start | bytes 3080 | tf_op jit(solution)/shard_map/ppermute | solution.py:16
  131.8 4.1 %collective-permute-start.33 = (f32[256]{0:T(256)S(1)}, f32[256]{0:T(256)S(1)}, u32[]{:S(2)}, u32[]{:S(2)}) collective-permute-start(f32[256]{0:T(256)S(1)} %add.219), channel_id=1, source_target_pairs={{0,2},{1,3},{2,0},{3,1},{4,6},{5,7},{6,4},{7,5},{8,10},{9,11},{10,... | collective-permute-start | bytes 3080 | tf_op jit(solution)/shard_map/ppermute | solution.py:16
  132.6 5.5 %collective-permute-start.34 = (f32[256]{0:T(256)S(1)}, f32[256]{0:T(256)S(1)}, u32[]{:S(2)}, u32[]{:S(2)}) collective-permute-start(f32[256]{0:T(256)S(1)} %add.219), channel_id=1, source_target_pairs={{0,3},{1,2},{2,1},{3,0},{4,7},{5,6},{6,5},{7,4},{8,11},{9,10},{10,... | collective-permute-start | bytes 3080 | tf_op jit(solution)/shard_map/ppermute | solution.py:16
  133.6 5.1 %collective-permute-start.35 = (f32[256]{0:T(256)S(1)}, f32[256]{0:T(256)S(1)}, u32[]{:S(2)}, u32[]{:S(2)}) collective-permute-start(f32[256]{0:T(256)S(1)} %add.219), channel_id=1, source_target_pairs={{0,4},{1,5},{2,6},{3,7},{4,0},{5,1},{6,2},{7,3},{8,12},{9,13},{10,... | collective-permute-start | bytes 3080 | tf_op jit(solution)/shard_map/ppermute | solution.py:16
  133.6 7.0 %collective-permute-start.36 = (f32[256]{0:T(256)S(1)}, f32[256]{0:T(256)S(1)}, u32[]{:S(2)}, u32[]{:S(2)}) collective-permute-start(f32[256]{0:T(256)S(1)} %add.219), channel_id=1, source_target_pairs={{0,5},{1,4},{2,7},{3,6},{4,1},{5,0},{6,3},{7,2},{8,13},{9,12},{10,... | collective-permute-start | bytes 3080 | tf_op jit(solution)/shard_map/ppermute | solution.py:16
  135.3 6.5 %collective-permute-start.37 = (f32[256]{0:T(256)S(1)}, f32[256]{0:T(256)S(1)}, u32[]{:S(2)}, u32[]{:S(2)}) collective-permute-start(f32[256]{0:T(256)S(1)} %add.219), channel_id=1, source_target_pairs={{0,6},{1,7},{2,4},{3,5},{4,2},{5,3},{6,0},{7,1},{8,14},{9,15},{10,... | collective-permute-start | bytes 3080 | tf_op jit(solution)/shard_map/ppermute | solution.py:16
  135.9 8.4 %collective-permute-start.38 = (f32[256]{0:T(256)S(1)}, f32[256]{0:T(256)S(1)}, u32[]{:S(2)}, u32[]{:S(2)}) collective-permute-start(f32[256]{0:T(256)S(1)} %add.219), channel_id=1, source_target_pairs={{0,7},{1,6},{2,5},{3,4},{4,3},{5,2},{6,1},{7,0},{8,15},{9,14},{10,... | collective-permute-start | bytes 3080 | tf_op jit(solution)/shard_map/ppermute | solution.py:16
  138.1 8.3 %collective-permute-start.39 = (f32[256]{0:T(256)S(1)}, f32[256]{0:T(256)S(1)}, u32[]{:S(2)}, u32[]{:S(2)}) collective-permute-start(f32[256]{0:T(256)S(1)} %add.219), channel_id=1, source_target_pairs={{0,8},{1,9},{2,10},{3,11},{4,12},{5,13},{6,14},{7,15},{8,0},{9,1},... | collective-permute-start | bytes 3080 | tf_op jit(solution)/shard_map/ppermute | solution.py:16
  138.7 9.0 %collective-permute-start.40 = (f32[256]{0:T(256)S(1)}, f32[256]{0:T(256)S(1)}, u32[]{:S(2)}, u32[]{:S(2)}) collective-permute-start(f32[256]{0:T(256)S(1)} %add.219), channel_id=1, source_target_pairs={{0,9},{1,8},{2,11},{3,10},{4,13},{5,12},{6,15},{7,14},{8,1},{9,0},... | collective-permute-start | bytes 3080 | tf_op jit(solution)/shard_map/ppermute | solution.py:16
  140.6 9.4 %collective-permute-start.41 = (f32[256]{0:T(256)S(1)}, f32[256]{0:T(256)S(1)}, u32[]{:S(2)}, u32[]{:S(2)}) collective-permute-start(f32[256]{0:T(256)S(1)} %add.219), channel_id=1, source_target_pairs={{0,10},{1,11},{2,8},{3,9},{4,14},{5,15},{6,12},{7,13},{8,2},{9,3},... | collective-permute-start | bytes 3080 | tf_op jit(solution)/shard_map/ppermute | solution.py:16
  141.8 10.4 %collective-permute-start.42 = (f32[256]{0:T(256)S(1)}, f32[256]{0:T(256)S(1)}, u32[]{:S(2)}, u32[]{:S(2)}) collective-permute-start(f32[256]{0:T(256)S(1)} %add.219), channel_id=1, source_target_pairs={{0,11},{1,10},{2,9},{3,8},{4,15},{5,14},{6,13},{7,12},{8,3},{9,2},... | collective-permute-start | bytes 3080 | tf_op jit(solution)/shard_map/ppermute | solution.py:16
  144.3 8.0 %collective-permute-start.43 = (f32[256]{0:T(256)S(1)}, f32[256]{0:T(256)S(1)}, u32[]{:S(2)}, u32[]{:S(2)}) collective-permute-start(f32[256]{0:T(256)S(1)} %add.219), channel_id=1, source_target_pairs={{0,12},{1,13},{2,14},{3,15},{4,8},{5,9},{6,10},{7,11},{8,4},{9,5},... | collective-permute-start | bytes 3080 | tf_op jit(solution)/shard_map/ppermute | solution.py:16
  146.4 5.9 %collective-permute-start.44 = (f32[256]{0:T(256)S(1)}, f32[256]{0:T(256)S(1)}, u32[]{:S(2)}, u32[]{:S(2)}) collective-permute-start(f32[256]{0:T(256)S(1)} %add.219), channel_id=1, source_target_pairs={{0,13},{1,12},{2,15},{3,14},{4,9},{5,8},{6,11},{7,10},{8,5},{9,4},... | collective-permute-start | bytes 3080 | tf_op jit(solution)/shard_map/ppermute | solution.py:16
  147.7 6.3 %collective-permute-start.45 = (f32[256]{0:T(256)S(1)}, f32[256]{0:T(256)S(1)}, u32[]{:S(2)}, u32[]{:S(2)}) collective-permute-start(f32[256]{0:T(256)S(1)} %add.219), channel_id=1, source_target_pairs={{0,14},{1,15},{2,12},{3,13},{4,10},{5,11},{6,8},{7,9},{8,6},{9,7},... | collective-permute-start | bytes 3080 | tf_op jit(solution)/shard_map/ppermute | solution.py:16
  150.0 5.7 %collective-permute-start.46 = (f32[256]{0:T(256)S(1)}, f32[256]{0:T(256)S(1)}, u32[]{:S(2)}, u32[]{:S(2)}) collective-permute-start(f32[256]{0:T(256)S(1)} %add.219), channel_id=1, source_target_pairs={{0,15},{1,14},{2,13},{3,12},{4,11},{5,10},{6,9},{7,8},{8,7},{9,6},... | collective-permute-start | bytes 3080 | tf_op jit(solution)/shard_map/ppermute | solution.py:16

commit v6 on v4

--- a/solution.py
+++ b/solution.py
@@ -27,7 +27,10 @@
         mine = (me >> bit) & 1
         keep = lax.dynamic_index_in_dim(cur, mine, axis=axis, keepdims=False)
         send = lax.dynamic_index_in_dim(cur, 1 - mine, axis=axis, keepdims=False)
-        cur = keep + exchange(send, 1 << bit, devices)
+        if bit == 0:
+            cur = keep + exchange(send, 1 << bit, devices)
+        else:
+            cur = keep + exchange(send.astype(jnp.bfloat16), 1 << bit, devices).astype(jnp.float32)
     return cur
 
 

time: 146 us -> 129 us (0.88)
  waiting for transfers between devices: 69.8 us -> 57.2 us
  starting transfers between devices: 38.4 us -> 35.7 us
    ppermute x36, waiting for transfers between devices: 69.8 us -> 57.2 us  [exchange(): return lax.ppermute(x, 'row', [(i, i ^ distance) for i in range(devices)])]
    ppermute x36, starting transfers between devices: 38.4 us -> 35.7 us  [exchange(): return lax.ppermute(x, 'row', [(i, i ^ distance) for i in range(devices)])]
    add x12 -> x4, other arithmetic: 3.99 us -> 1.57 us  [halving_reduce_scatter(): cur = keep + exchange(send, 1 << bit, devices)]
    another operation x32, other arithmetic: 3.75 us -> 5.4 us  [doubling_all_gather(): jnp.stack([jnp.where(low, cur, other), jnp.where(low, other, cur)], axis=...]
    dynamic_slice x0 -> x3, local copies, waits for them, and re-layouts: none -> 1.63 us  [the longest x1 1.48 us: halving_reduce_scatter(): keep = lax.dynamic_index_in_dim(cur, mine, axis=axis, keepdims=False)]
  transfers between devices with their start and end apart: 36 -> 36, of which waited for: 23 -> 28; matrix products, arithmetic and copies ran while one was open for 18% -> 13% of each run, Pallas kernels for 0% -> 0%
where the time goes in v6:
time: 129 us
  waiting for transfers between devices  57.2 us (44%)
  starting transfers between devices  35.7 us (28%)
  matrix products  15.6 us (12%)
  local copies, waits for them, and re-layouts  10.1 us (8%)
  other arithmetic  8.85 us (7%)
    ppermute x36, waiting for transfers between devices, exchange(): return lax.ppermute(x, 'row', [(i, i ^ distance) for i in range(devices)])  57.2 us
    ppermute x36, starting transfers between devices, exchange(): return lax.ppermute(x, 'row', [(i, i ^ distance) for i in range(devices)])  35.7 us
    dot_general x4, matrix products, contract_rows(): lax.dot_general(left, right, (((0,), (0,)), ((), ())), preferred_element_...  15.6 us
    dot_general x4, local copies, waits for them, and re-layouts, contract_rows(): lax.dot_general(left, right, (((0,), (0,)), ((), ())), preferred_element_...  6.08 us
    another operation x32, other arithmetic, doubling_all_gather(): jnp.stack([jnp.where(low, cur, other), jnp.where(low, other, cur)], axis=...  5.4 us
  transfers between devices with their start and end apart: 36, of which 28 were waited for; matrix products, arithmetic and copies ran while one was open for 13% of the time, Pallas kernels for 0%

profile of v6, /device:TPU:0, one launch (start us, length us, event | category | flops | bytes accessed | tf_op | source)
XLA Modules:
  0.0 128.7 jit_solution(11011825045850057271)
XLA Ops:
  0.6 4.1 %collective-permute-start = (bf16[96,256]{1,0:T(8,128)(2,1)}, bf16[96,256]{1,0:T(8,128)(2,1)S(1)}, u32[]{:S(2)}, u32[]{:S(2)}) collective-permute-start(bf16[96,256]{1,0:T(8,128)(2,1)} %param.6), channel_id=1, source_target_pairs={{0,8},{1,9},{2,10},{3,11},{4,12},{5,13},{6,14},{7,15},{8,0},{9,1},... | collective-permute-start | bytes 147464 | tf_op jit(solution)/shard_map/ppermute | solution.py:16
  4.8 2.7 %collective-permute-done = bf16[96,256]{1,0:T(8,128)(2,1)S(1)} collective-permute-done((bf16[96,256]{1,0:T(8,128)(2,1)}, bf16[96,256]{1,0:T(8,128)(2,1)S(1)}, u32[]{:S(2)}, u32[]{:S(2)}) %collective-permute-start) | collective-permute-done | bytes 49184 | tf_op jit(solution)/shard_map/ppermute | solution.py:16
  7.5 0.8 select_bitcast_fusion.31
  8.4 2.2 %collective-permute-start.1 = (bf16[2,96,256]{2,1,0:T(8,128)(2,1)S(1)}, bf16[2,96,256]{2,1,0:T(8,128)(2,1)S(1)}, u32[]{:S(2)}, u32[]{:S(2)}) collective-permute-start(bf16[2,96,256]{2,1,0:T(8,128)(2,1)S(1)} %pad_maximum_fusion.12), channel_id=1, source_target_pairs={{0,4},{1,5},{2,6},{3,7},{4,0},{5,1},{6,2},{7,3},{8,12},{9,13},{10,... | collective-permute-start | bytes 294920 | tf_op jit(solution)/shard_map/ppermute | solution.py:16
  10.6 0.8 select_bitcast_fusion.29
  11.4 1.6 %collective-permute-start.9 = (bf16[2,96,256]{2,1,0:T(8,128)(2,1)S(1)}, bf16[2,96,256]{2,1,0:T(8,128)(2,1)S(1)}, u32[]{:S(2)}, u32[]{:S(2)}) collective-permute-start(bf16[2,96,256]{2,1,0:T(8,128)(2,1)S(1)} %pad_maximum_fusion.13), channel_id=1, source_target_pairs={{0,2},{1,3},{2,0},{3,1},{4,6},{5,7},{6,4},{7,5},{8,10},{9,11},{10,... | collective-permute-start | bytes 294920 | tf_op jit(solution)/shard_map/ppermute | solution.py:16
  13.5 1.6 %collective-permute-start.2 = (bf16[2,2,96,256]{3,2,0,1:T(8,128)(2,1)S(1)}, bf16[2,2,96,256]{3,2,0,1:T(8,128)(2,1)S(1)}, u32[]{:S(2)}, u32[]{:S(2)}) collective-permute-start(bf16[2,2,96,256]{3,2,0,1:T(8,128)(2,1)S(1)} %pad_maximum_fusion.8), channel_id=1, source_target_pairs={{0,2},{1,3},{2,0},{3,1},{4,6},{5,7},{6,4},{7,5},{8,10},{9,11},{10,... | collective-permute-start | bytes 589832 | tf_op jit(solution)/shard_map/ppermute | solution.py:16
  15.1 1.6 %collective-permute-done.9 = bf16[2,96,256]{2,1,0:T(8,128)(2,1)S(1)} collective-permute-done((bf16[2,96,256]{2,1,0:T(8,128)(2,1)S(1)}, bf16[2,96,256]{2,1,0:T(8,128)(2,1)S(1)}, u32[]{:S(2)}, u32[]{:S(2)}) %collective-permute-start.9) | collective-permute-done | bytes 98336 | tf_op jit(solution)/shard_map/ppermute | solution.py:16
  16.8 0.7 collective-permute-start.10
  17.5 2.8 %collective-permute-done.2 = bf16[2,2,96,256]{3,2,0,1:T(8,128)(2,1)S(1)} collective-permute-done((bf16[2,2,96,256]{3,2,0,1:T(8,128)(2,1)S(1)}, bf16[2,2,96,256]{3,2,0,1:T(8,128)(2,1)S(1)}, u32[]{:S(2)}, u32[]{:S(2)}) %collective-permute-start.2) | collective-permute-done | bytes 196640 | tf_op jit(solution)/shard_map/ppermute | solution.py:16
  20.5 2.0 %collective-permute-done.10 = bf16[2,2,96,256]{3,2,1,0:T(8,128)(2,1)S(1)} collective-permute-done((bf16[2,2,96,256]{3,2,1,0:T(8,128)(2,1)S(1)}, bf16[2,2,96,256]{3,2,1,0:T(8,128)(2,1)S(1)}, u32[]{:S(2)}, u32[]{:S(2)}) %collective-permute-start.10) | collective-permute-done | bytes 196640 | tf_op jit(solution)/shard_map/ppermute | solution.py:16
  22.6 0.8 pad_maximum_fusion.5
  23.5 1.0 pad_maximum_fusion
  24.5 3.2 %convolution_bitcast_fusion.3 = f32[1536,256]{0,1:T(8,128)S(1)} fusion(bf16[1536,256]{1,0:T(8,128)(2,1)} %bitcast.249, bf16[3,512,1536]{2,1,0:T(8,128)(2,1)} %param.5), kind=kOutput, calls=%fused_computation.3 | convolution fusion | flops 805437440 | bytes 5505024 | tf_op jit(solution)/shard_map/dot_general | solution.py:10
  28.2 1.1 select_bitcast_fusion.5
  29.4 4.1 %convolution_bitcast_fusion.2 = f32[1536,256]{0,1:T(8,128)} fusion(bf16[1536,256]{1,0:T(8,128)(2,1)S(1)} %bitcast.251, bf16[3,512,1536]{2,1,0:T(8,128)(2,1)} %param.5), kind=kOutput, calls=%fused_computation.2 | convolution fusion | flops 805437440 | bytes 5505024 | tf_op jit(solution)/shard_map/dot_general | solution.py:10
  33.5 1.9 %copy.51 = f32[1536,256]{1,0:T(8,128)S(1)} copy(f32[1536,256]{0,1:T(8,128)} %convolution_bitcast_fusion.2) | data formatting | bytes 3145728 | tf_op jit(solution)/shard_map/dot_general | solution.py:10
  35.4 1.5 %constant_dynamic-slice_fusion.2 = (f32[2,2,2,1,96,256]{5,4,3,2,1,0:T(8,128)}, f32[2,2,2,1,96,256]{5,4,3,2,1,0:T(8,128)S(1)}, f32[2,2,2,1,96,256]{5,4,3,2,1,0:T(8,128)}, f32[2,2,2,1,96,256]{5,4,3,2,1,0:T(8,128)}) fusion(f32[2,2,2,2,96,256]{5,4,3,2,1,0:T(8,128)S(1)} %bitcast.245, s32[]{:T(128)S(6)} %select_n.220, s32[]{:T(128)S(6)} %select_n.221, ...), kind=kLoop, calls=%fused_computation.137 | loop fusion | bytes 6291464 | tf_op jit(solution)/shard_map/jit(dynamic_index_in_dim)/dynamic_slice | solution.py:28
  37.0 0.6 collective-permute-start.12
  38.1 0.6 collective-permute-start.4
  38.8 0.6 collective-permute-done.12
  39.6 0.7 collective-permute-start.13
  40.7 1.7 %collective-permute-start.5 = (bf16[2,2,96,256]{3,2,0,1:T(8,128)(2,1)S(1)}, bf16[2,2,96,256]{3,2,0,1:T(8,128)(2,1)S(1)}, u32[]{:S(2)}, u32[]{:S(2)}) collective-permute-start(bf16[2,2,96,256]{3,2,0,1:T(8,128)(2,1)S(1)} %fusion.50), channel_id=1, source_target_pairs={{0,2},{1,3},{2,0},{3,1},{4,6},{5,7},{6,4},{7,5},{8,10},{9,11},{10,... | collective-permute-start | bytes 589832 | tf_op jit(solution)/shard_map/ppermute | solution.py:16
  42.4 4.5 %collective-permute-done.13 = bf16[2,2,96,256]{3,2,0,1:T(8,128)(2,1)S(1)} collective-permute-done((bf16[2,2,96,256]{3,2,0,1:T(8,128)(2,1)S(1)}, bf16[2,2,96,256]{3,2,0,1:T(8,128)(2,1)S(1)}, u32[]{:S(2)}, u32[]{:S(2)}) %collective-permute-start.13) | collective-permute-done | bytes 196640 | tf_op jit(solution)/shard_map/ppermute | solution.py:16
  47.0 1.6 %collective-permute-start.14 = (bf16[2,96,256]{2,1,0:T(8,128)(2,1)S(1)}, bf16[2,96,256]{2,1,0:T(8,128)(2,1)S(1)}, u32[]{:S(2)}, u32[]{:S(2)}) collective-permute-start(bf16[2,96,256]{2,1,0:T(8,128)(2,1)S(1)} %fusion.55), channel_id=1, source_target_pairs={{0,2},{1,3},{2,0},{3,1},{4,6},{5,7},{6,4},{7,5},{8,10},{9,11},{10,... | collective-permute-start | bytes 294920 | tf_op jit(solution)/shard_map/ppermute | solution.py:16
  48.7 0.6 collective-permute-start.6
  49.3 2.3 %collective-permute-done.14 = bf16[2,96,256]{2,1,0:T(8,128)(2,1)S(1)} collective-permute-done((bf16[2,96,256]{2,1,0:T(8,128)(2,1)S(1)}, bf16[2,96,256]{2,1,0:T(8,128)(2,1)S(1)}, u32[]{:S(2)}, u32[]{:S(2)}) %collective-permute-start.14) | collective-permute-done | bytes 98336 | tf_op jit(solution)/shard_map/ppermute | solution.py:16
  51.7 3.3 %collective-permute-start.15 = (bf16[96,256]{1,0:T(8,128)(2,1)S(1)}, bf16[96,256]{1,0:T(8,128)(2,1)S(1)}, u32[]{:S(2)}, u32[]{:S(2)}) collective-permute-start(bf16[96,256]{1,0:T(8,128)(2,1)S(1)} %fusion.59), channel_id=1, source_target_pairs={{0,8},{1,9},{2,10},{3,11},{4,12},{5,13},{6,14},{7,15},{8,0},{9,1},... | collective-permute-start | bytes 147464 | tf_op jit(solution)/shard_map/ppermute | solution.py:16
  55.1 1.6 %collective-permute-start.7 = (bf16[96,256]{1,0:T(8,128)(2,1)S(1)}, bf16[96,256]{1,0:T(8,128)(2,1)S(1)}, u32[]{:S(2)}, u32[]{:S(2)}) collective-permute-start(bf16[96,256]{1,0:T(8,128)(2,1)S(1)} %fusion.58), channel_id=1, source_target_pairs={{0,8},{1,9},{2,10},{3,11},{4,12},{5,13},{6,14},{7,15},{8,0},{9,1},... | collective-permute-start | bytes 147464 | tf_op jit(solution)/shard_map/ppermute | solution.py:16
  56.8 1.6 %collective-permute-done.15 = bf16[96,256]{1,0:T(8,128)(2,1)S(1)} collective-permute-done((bf16[96,256]{1,0:T(8,128)(2,1)S(1)}, bf16[96,256]{1,0:T(8,128)(2,1)S(1)}, u32[]{:S(2)}, u32[]{:S(2)}) %collective-permute-start.15) | collective-permute-done | bytes 49184 | tf_op jit(solution)/shard_map/ppermute | solution.py:16
  58.4 2.0 %collective-permute-done.7 = bf16[96,256]{1,0:T(8,128)(2,1)S(1)} collective-permute-done((bf16[96,256]{1,0:T(8,128)(2,1)S(1)}, bf16[96,256]{1,0:T(8,128)(2,1)S(1)}, u32[]{:S(2)}, u32[]{:S(2)}) %collective-permute-start.7) | collective-permute-done | bytes 49184 | tf_op jit(solution)/shard_map/ppermute | solution.py:16
  60.5 1.4 %collective-permute-start.16 = (bf16[96,256]{1,0:T(8,128)(2,1)S(1)}, bf16[96,256]{1,0:T(8,128)(2,1)S(1)}, u32[]{:S(2)}, u32[]{:S(2)}) collective-permute-start(bf16[96,256]{1,0:T(8,128)(2,1)S(1)} %get-tuple-element.22), channel_id=1, source_target_pairs={{0,8},{1,9},{2,10},{3,11},{4,12},{5,13},{6,14},{7,15},{8,0},{9,1},... | collective-permute-start | bytes 147464 | tf_op jit(solution)/shard_map/ppermute | solution.py:16
  61.9 1.6 %collective-permute-start.20 = (bf16[96,256]{1,0:T(8,128)(2,1)S(1)}, bf16[96,256]{1,0:T(8,128)(2,1)S(1)}, u32[]{:S(2)}, u32[]{:S(2)}) collective-permute-start(bf16[96,256]{1,0:T(8,128)(2,1)S(1)} %get-tuple-element.23), channel_id=1, source_target_pairs={{0,8},{1,9},{2,10},{3,11},{4,12},{5,13},{6,14},{7,15},{8,0},{9,1},... | collective-permute-start | bytes 147464 | tf_op jit(solution)/shard_map/ppermute | solution.py:16
  63.5 2.1 %collective-permute-done.16 = bf16[96,256]{1,0:T(8,128)(2,1)S(1)} collective-permute-done((bf16[96,256]{1,0:T(8,128)(2,1)S(1)}, bf16[96,256]{1,0:T(8,128)(2,1)S(1)}, u32[]{:S(2)}, u32[]{:S(2)}) %collective-permute-start.16) | collective-permute-done | bytes 49184 | tf_op jit(solution)/shard_map/ppermute | solution.py:16
  65.7 1.5 %collective-permute-done.20 = bf16[96,256]{1,0:T(8,128)(2,1)S(1)} collective-permute-done((bf16[96,256]{1,0:T(8,128)(2,1)S(1)}, bf16[96,256]{1,0:T(8,128)(2,1)S(1)}, u32[]{:S(2)}, u32[]{:S(2)}) %collective-permute-start.20) | collective-permute-done | bytes 49184 | tf_op jit(solution)/shard_map/ppermute | solution.py:16
  67.3 1.6 %collective-permute-start.21 = (bf16[2,96,256]{2,1,0:T(8,128)(2,1)S(1)}, bf16[2,96,256]{2,1,0:T(8,128)(2,1)S(1)}, u32[]{:S(2)}, u32[]{:S(2)}) collective-permute-start(bf16[2,96,256]{2,1,0:T(8,128)(2,1)S(1)} %pad_maximum_fusion.15), channel_id=1, source_target_pairs={{0,2},{1,3},{2,0},{3,1},{4,6},{5,7},{6,4},{7,5},{8,10},{9,11},{10,... | collective-permute-start | bytes 294920 | tf_op jit(solution)/shard_map/ppermute | solution.py:16
  68.8 1.4 %collective-permute-done.17 = bf16[2,96,256]{2,1,0:T(8,128)(2,1)S(1)} collective-permute-done((bf16[2,96,256]{2,1,0:T(8,128)(2,1)S(1)}, bf16[2,96,256]{2,1,0:T(8,128)(2,1)S(1)}, u32[]{:S(2)}, u32[]{:S(2)}) %collective-permute-start.17) | collective-permute-done | bytes 98336 | tf_op jit(solution)/shard_map/ppermute | solution.py:16
  70.3 1.8 %collective-permute-start.18 = (bf16[2,2,96,256]{3,2,0,1:T(8,128)(2,1)S(1)}, bf16[2,2,96,256]{3,2,0,1:T(8,128)(2,1)S(1)}, u32[]{:S(2)}, u32[]{:S(2)}) collective-permute-start(bf16[2,2,96,256]{3,2,0,1:T(8,128)(2,1)S(1)} %pad_maximum_fusion.10), channel_id=1, source_target_pairs={{0,2},{1,3},{2,0},{3,1},{4,6},{5,7},{6,4},{7,5},{8,10},{9,11},{10,... | collective-permute-start | bytes 589832 | tf_op jit(solution)/shard_map/ppermute | solution.py:16
  72.2 0.8 collective-permute-done.21
  73.1 3.0 %collective-permute-done.18 = bf16[2,2,96,256]{3,2,0,1:T(8,128)(2,1)S(1)} collective-permute-done((bf16[2,2,96,256]{3,2,0,1:T(8,128)(2,1)S(1)}, bf16[2,2,96,256]{3,2,0,1:T(8,128)(2,1)S(1)}, u32[]{:S(2)}, u32[]{:S(2)}) %collective-permute-start.18) | collective-permute-done | bytes 196640 | tf_op jit(solution)/shard_map/ppermute | solution.py:16
  76.2 2.5 %collective-permute-done.22 = bf16[2,2,96,256]{3,2,1,0:T(8,128)(2,1)S(1)} collective-permute-done((bf16[2,2,96,256]{3,2,1,0:T(8,128)(2,1)S(1)}, bf16[2,2,96,256]{3,2,1,0:T(8,128)(2,1)S(1)}, u32[]{:S(2)}, u32[]{:S(2)}) %collective-permute-start.22) | collective-permute-done | bytes 196640 | tf_op jit(solution)/shard_map/ppermute | solution.py:16
  79.3 1.3 %collective-permute-done.23 = bf16[2,2,2,96,256]{4,3,2,1,0:T(8,128)(2,1)S(1)} collective-permute-done((bf16[2,2,2,96,256]{4,3,2,1,0:T(8,128)(2,1)S(1)}, bf16[2,2,2,96,256]{4,3,2,1,0:T(8,128)(2,1)S(1)}, u32[]{:S(2)}, u32[]{:S(2)}) %collective-permute-start.23) | collective-permute-done | bytes 393248 | tf_op jit(solution)/shard_map/ppermute | solution.py:16
  81.1 4.1 %convolution_bitcast_fusion.1 = f32[1536,256]{0,1:T(8,128)} fusion(bf16[3,512,1536]{2,1,0:T(8,128)(2,1)} %param.5, bf16[1536,256]{1,0:T(8,128)(2,1)S(1)} %bitcast.248, f32[256]{0:T(256)S(1)} %add_rsqrt_fusion.1), kind=kOutput, calls=%fused_computation.1 | convolution fusion | flops 805568512 | bytes 5506048 | tf_op jit(solution)/shard_map/dot_general | solution.py:10
  85.2 1.9 %copy.60 = f32[1536,256]{1,0:T(8,128)S(1)} copy(f32[1536,256]{0,1:T(8,128)} %convolution_bitcast_fusion.1) | data formatting | bytes 3145728 | tf_op jit(solution)/shard_map/dot_general | solution.py:10
  87.1 1.0 dynamic-slice_bitcast_fusion.2
  88.3 4.2 %convolution_bitcast_fusion = f32[1536,256]{0,1:T(8,128)} fusion(bf16[3,512,1536]{2,1,0:T(8,128)(2,1)} %param.5, bf16[1536,256]{1,0:T(8,128)(2,1)S(1)} %bitcast.250, f32[256]{0:T(256)S(1)} %add_rsqrt_fusion.1), kind=kOutput, calls=%fused_computation | convolution fusion | flops 805568512 | bytes 5506048 | tf_op jit(solution)/shard_map/dot_general | solution.py:10
  92.4 1.9 %copy.62 = f32[1536,256]{1,0:T(8,128)S(1)} copy(f32[1536,256]{0,1:T(8,128)} %convolution_bitcast_fusion) | data formatting | bytes 3145728 | tf_op jit(solution)/shard_map/dot_general | solution.py:10
  95.1 1.2 bitcast_add_fusion
  96.4 1.4 %collective-permute-start.25 = (bf16[2,2,96,256]{3,2,1,0:T(8,128)(2,1)S(1)}, bf16[2,2,96,256]{3,2,1,0:T(8,128)(2,1)S(1)}, u32[]{:S(2)}, u32[]{:S(2)}) collective-permute-start(bf16[2,2,96,256]{3,2,1,0:T(8,128)(2,1)S(1)} %fusion.52), channel_id=1, source_target_pairs={{0,2},{1,3},{2,0},{3,1},{4,6},{5,7},{6,4},{7,5},{8,10},{9,11},{10,... | collective-permute-start | bytes 589832 | tf_op jit(solution)/shard_map/ppermute | solution.py:16
  98.2 5.2 %collective-permute-done.25 = bf16[2,2,96,256]{3,2,1,0:T(8,128)(2,1)S(1)} collective-permute-done((bf16[2,2,96,256]{3,2,1,0:T(8,128)(2,1)S(1)}, bf16[2,2,96,256]{3,2,1,0:T(8,128)(2,1)S(1)}, u32[]{:S(2)}, u32[]{:S(2)}) %collective-permute-start.25) | collective-permute-done | bytes 196640 | tf_op jit(solution)/shard_map/ppermute | solution.py:16
  103.5 1.1 collective-permute-done.29
  104.7 1.0 collective-permute-start.30
  105.7 2.4 %collective-permute-done.26 = bf16[2,96,256]{2,1,0:T(8,128)(2,1)S(1)} collective-permute-done((bf16[2,96,256]{2,1,0:T(8,128)(2,1)S(1)}, bf16[2,96,256]{2,1,0:T(8,128)(2,1)S(1)}, u32[]{:S(2)}, u32[]{:S(2)}) %collective-permute-start.26) | collective-permute-done | bytes 98336 | tf_op jit(solution)/shard_map/ppermute | solution.py:16
  108.5 0.9 collective-permute-done.30
  109.4 1.9 %collective-permute-start.31 = (bf16[96,256]{1,0:T(8,128)(2,1)S(1)}, bf16[96,256]{1,0:T(8,128)(2,1)S(1)}, u32[]{:S(2)}, u32[]{:S(2)}) collective-permute-start(bf16[96,256]{1,0:T(8,128)(2,1)S(1)} %fusion.61), channel_id=1, source_target_pairs={{0,8},{1,9},{2,10},{3,11},{4,12},{5,13},{6,14},{7,15},{8,0},{9,1},... | collective-permute-start | bytes 147464 | tf_op jit(solution)/shard_map/ppermute | solution.py:16
  111.4 1.8 %collective-permute-done.27 = bf16[96,256]{1,0:T(8,128)(2,1)S(1)} collective-permute-done((bf16[96,256]{1,0:T(8,128)(2,1)S(1)}, bf16[96,256]{1,0:T(8,128)(2,1)S(1)}, u32[]{:S(2)}, u32[]{:S(2)}) %collective-permute-start.27) | collective-permute-done | bytes 49184 | tf_op jit(solution)/shard_map/ppermute | solution.py:16
  113.2 1.8 %collective-permute-done.31 = bf16[96,256]{1,0:T(8,128)(2,1)S(1)} collective-permute-done((bf16[96,256]{1,0:T(8,128)(2,1)S(1)}, bf16[96,256]{1,0:T(8,128)(2,1)S(1)}, u32[]{:S(2)}, u32[]{:S(2)}) %collective-permute-start.31) | collective-permute-done | bytes 49184 | tf_op jit(solution)/shard_map/ppermute | solution.py:16
  115.2 1.1 collective-permute-done.32
  116.8 3.1 %collective-permute-done.33 = f32[256]{0:T(256)S(1)} collective-permute-done((f32[256]{0:T(256)S(1)}, f32[256]{0:T(256)S(1)}, u32[]{:S(2)}, u32[]{:S(2)}) %collective-permute-start.33) | collective-permute-done | bytes 1056 | tf_op jit(solution)/shard_map/ppermute | solution.py:16
  119.9 0.5 collective-permute-start.34
  120.4 3.1 %collective-permute-done.34 = f32[256]{0:T(256)S(1)} collective-permute-done((f32[256]{0:T(256)S(1)}, f32[256]{0:T(256)S(1)}, u32[]{:S(2)}, u32[]{:S(2)}) %collective-permute-start.34) | collective-permute-done | bytes 1056 | tf_op jit(solution)/shard_map/ppermute | solution.py:16
  123.5 1.3 collective-permute-start.35
  124.8 3.2 %collective-permute-done.35 = f32[256]{0:T(256)S(1)} collective-permute-done((f32[256]{0:T(256)S(1)}, f32[256]{0:T(256)S(1)}, u32[]{:S(2)}, u32[]{:S(2)}) %collective-permute-start.35) | collective-permute-done | bytes 1056 | tf_op jit(solution)/shard_map/ppermute | solution.py:16
  128.0 0.7 broadcast_multiply_fusion
  (108 shorter events, 7.4 us)
Async XLA Ops:
  0.6 6.9 %collective-permute-start = (bf16[96,256]{1,0:T(8,128)(2,1)}, bf16[96,256]{1,0:T(8,128)(2,1)S(1)}, u32[]{:S(2)}, u32[]{:S(2)}) collective-permute-start(bf16[96,256]{1,0:T(8,128)(2,1)} %param.6), channel_id=1, source_target_pairs={{0,8},{1,9},{2,10},{3,11},{4,12},{5,13},{6,14},{7,15},{8,0},{9,1},... | collective-permute-start | bytes 147464 | tf_op jit(solution)/shard_map/ppermute | solution.py:16
  4.7 5.9 %collective-permute-start.8 = (bf16[96,256]{1,0:T(8,128)(2,1)}, bf16[96,256]{1,0:T(8,128)(2,1)S(1)}, u32[]{:S(2)}, u32[]{:S(2)}) collective-permute-start(bf16[96,256]{1,0:T(8,128)(2,1)} %param.7), channel_id=1, source_target_pairs={{0,8},{1,9},{2,10},{3,11},{4,12},{5,13},{6,14},{7,15},{8,0},{9,1},... | collective-permute-start | bytes 147464 | tf_op jit(solution)/shard_map/ppermute | solution.py:16
  8.4 5.1 %collective-permute-start.1 = (bf16[2,96,256]{2,1,0:T(8,128)(2,1)S(1)}, bf16[2,96,256]{2,1,0:T(8,128)(2,1)S(1)}, u32[]{:S(2)}, u32[]{:S(2)}) collective-permute-start(bf16[2,96,256]{2,1,0:T(8,128)(2,1)S(1)} %pad_maximum_fusion.12), channel_id=1, source_target_pairs={{0,4},{1,5},{2,6},{3,7},{4,0},{5,1},{6,2},{7,3},{8,12},{9,13},{10,... | collective-permute-start | bytes 294920 | tf_op jit(solution)/shard_map/ppermute | solution.py:16
  11.4 5.3 %collective-permute-start.9 = (bf16[2,96,256]{2,1,0:T(8,128)(2,1)S(1)}, bf16[2,96,256]{2,1,0:T(8,128)(2,1)S(1)}, u32[]{:S(2)}, u32[]{:S(2)}) collective-permute-start(bf16[2,96,256]{2,1,0:T(8,128)(2,1)S(1)} %pad_maximum_fusion.13), channel_id=1, source_target_pairs={{0,2},{1,3},{2,0},{3,1},{4,6},{5,7},{6,4},{7,5},{8,10},{9,11},{10,... | collective-permute-start | bytes 294920 | tf_op jit(solution)/shard_map/ppermute | solution.py:16
  13.5 6.8 %collective-permute-start.2 = (bf16[2,2,96,256]{3,2,0,1:T(8,128)(2,1)S(1)}, bf16[2,2,96,256]{3,2,0,1:T(8,128)(2,1)S(1)}, u32[]{:S(2)}, u32[]{:S(2)}) collective-permute-start(bf16[2,2,96,256]{3,2,0,1:T(8,128)(2,1)S(1)} %pad_maximum_fusion.8), channel_id=1, source_target_pairs={{0,2},{1,3},{2,0},{3,1},{4,6},{5,7},{6,4},{7,5},{8,10},{9,11},{10,... | collective-permute-start | bytes 589832 | tf_op jit(solution)/shard_map/ppermute | solution.py:16
  16.8 5.7 %collective-permute-start.10 = (bf16[2,2,96,256]{3,2,1,0:T(8,128)(2,1)S(1)}, bf16[2,2,96,256]{3,2,1,0:T(8,128)(2,1)S(1)}, u32[]{:S(2)}, u32[]{:S(2)}) collective-permute-start(bf16[2,2,96,256]{3,2,1,0:T(8,128)(2,1)S(1)} %pad_maximum_fusion.9), channel_id=1, source_target_pairs={{0,4},{1,5},{2,6},{3,7},{4,0},{5,1},{6,2},{7,3},{8,12},{9,13},{10,... | collective-permute-start | bytes 589832 | tf_op jit(solution)/shard_map/ppermute | solution.py:16
  20.5 2.9 %collective-permute-start.3 = (bf16[2,2,2,96,256]{4,3,2,1,0:T(8,128)(2,1)S(1)}, bf16[2,2,2,96,256]{4,3,2,1,0:T(8,128)(2,1)S(1)}, u32[]{:S(2)}, u32[]{:S(2)}) collective-permute-start(bf16[2,2,2,96,256]{4,3,2,1,0:T(8,128)(2,1)S(1)} %copy.65), channel_id=1, source_target_pairs={{0,1},{1,0},{2,3},{3,2},{4,5},{5,4},{6,7},{7,6},{8,9},{9,8},{10,11... | collective-permute-start | bytes 1179656 | tf_op jit(solution)/shard_map/ppermute | solution.py:16
  23.3 4.8 %collective-permute-start.11 = (bf16[2,2,2,96,256]{4,3,2,0,1:T(8,128)(2,1)}, bf16[2,2,2,96,256]{4,3,2,0,1:T(8,128)(2,1)}, u32[]{:S(2)}, u32[]{:S(2)}) collective-permute-start(bf16[2,2,2,96,256]{4,3,2,0,1:T(8,128)(2,1)} %pad_maximum_fusion.5), channel_id=1, source_target_pairs={{0,1},{1,0},{2,3},{3,2},{4,5},{5,4},{6,7},{7,6},{8,9},{9,8},{10,11... | collective-permute-start | bytes 1179656 | tf_op jit(solution)/shard_map/ppermute | solution.py:16
  36.9 1.1 copy-start
  36.9 1.8 %copy-start.3 = (f32[2,1536]{1,0:T(2,128)S(1)}, f32[2,1536]{1,0:T(2,128)}, u32[]{:S(2)}) copy-start(f32[2,1536]{1,0:T(2,128)} %param.8) | copy-start | bytes 36868
  36.9 1.8 %copy-start.4 = (f32[2,1536]{1,0:T(2,128)S(1)}, f32[2,1536]{1,0:T(2,128)}, u32[]{:S(2)}) copy-start(f32[2,1536]{1,0:T(2,128)} %param.9) | copy-start | bytes 36868
  36.9 2.6 %copy-start.2 = (f32[2,2,2,1,96,256]{5,4,3,2,1,0:T(8,128)S(1)}, f32[2,2,2,1,96,256]{5,4,3,2,1,0:T(8,128)}, u32[]{:S(2)}) copy-start(f32[2,2,2,1,96,256]{5,4,3,2,1,0:T(8,128)} %get-tuple-element.8) | copy-start | bytes 2359300
  37.0 2.5 %collective-permute-start.12 = (f32[2,2,2,96,256]{4,3,0,2,1:T(8,128)S(1)}, f32[2,2,2,96,256]{4,3,0,2,1:T(8,128)S(1)}, u32[]{:S(2)}, u32[]{:S(2)}) collective-permute-start(f32[2,2,2,96,256]{4,3,0,2,1:T(8,128)S(1)} %bitcast.246), channel_id=1, source_target_pairs={{0,1},{1,0},{2,3},{3,2},{4,5},{5,4},{6,7},{7,6},{8,9},{9,8},{10,11... | collective-permute-start | bytes 2359304 | tf_op jit(solution)/shard_map/ppermute | solution.py:16
  38.1 2.5 %copy-start.1 = (f32[2,2,2,1,96,256]{5,4,3,2,1,0:T(8,128)S(1)}, f32[2,2,2,1,96,256]{5,4,3,2,1,0:T(8,128)}, u32[]{:S(2)}) copy-start(f32[2,2,2,1,96,256]{5,4,3,2,1,0:T(8,128)} %get-tuple-element.59) | copy-start | bytes 2359300
  38.1 2.5 %collective-permute-start.4 = (f32[2,2,2,96,256]{4,3,0,1,2:T(8,128)S(1)}, f32[2,2,2,96,256]{4,3,0,1,2:T(8,128)S(1)}, u32[]{:S(2)}, u32[]{:S(2)}) collective-permute-start(f32[2,2,2,96,256]{4,3,0,1,2:T(8,128)S(1)} %bitcast.247), channel_id=1, source_target_pairs={{0,1},{1,0},{2,3},{3,2},{4,5},{5,4},{6,7},{7,6},{8,9},{9,8},{10,11... | collective-permute-start | bytes 2359304 | tf_op jit(solution)/shard_map/ppermute | solution.py:16
  39.6 7.2 %collective-permute-start.13 = (bf16[2,2,96,256]{3,2,0,1:T(8,128)(2,1)S(1)}, bf16[2,2,96,256]{3,2,0,1:T(8,128)(2,1)S(1)}, u32[]{:S(2)}, u32[]{:S(2)}) collective-permute-start(bf16[2,2,96,256]{3,2,0,1:T(8,128)(2,1)S(1)} %fusion.51), channel_id=1, source_target_pairs={{0,4},{1,5},{2,6},{3,7},{4,0},{5,1},{6,2},{7,3},{8,12},{9,13},{10,... | collective-permute-start | bytes 589832 | tf_op jit(solution)/shard_map/ppermute | solution.py:16
  40.7 7.9 %collective-permute-start.5 = (bf16[2,2,96,256]{3,2,0,1:T(8,128)(2,1)S(1)}, bf16[2,2,96,256]{3,2,0,1:T(8,128)(2,1)S(1)}, u32[]{:S(2)}, u32[]{:S(2)}) collective-permute-start(bf16[2,2,96,256]{3,2,0,1:T(8,128)(2,1)S(1)} %fusion.50), channel_id=1, source_target_pairs={{0,2},{1,3},{2,0},{3,1},{4,6},{5,7},{6,4},{7,5},{8,10},{9,11},{10,... | collective-permute-start | bytes 589832 | tf_op jit(solution)/shard_map/ppermute | solution.py:16
  47.0 4.7 %collective-permute-start.14 = (bf16[2,96,256]{2,1,0:T(8,128)(2,1)S(1)}, bf16[2,96,256]{2,1,0:T(8,128)(2,1)S(1)}, u32[]{:S(2)}, u32[]{:S(2)}) collective-permute-start(bf16[2,96,256]{2,1,0:T(8,128)(2,1)S(1)} %fusion.55), channel_id=1, source_target_pairs={{0,2},{1,3},{2,0},{3,1},{4,6},{5,7},{6,4},{7,5},{8,10},{9,11},{10,... | collective-permute-start | bytes 294920 | tf_op jit(solution)/shard_map/ppermute | solution.py:16
  48.7 6.4 %collective-permute-start.6 = (bf16[2,96,256]{2,1,0:T(8,128)(2,1)S(1)}, bf16[2,96,256]{2,1,0:T(8,128)(2,1)S(1)}, u32[]{:S(2)}, u32[]{:S(2)}) collective-permute-start(bf16[2,96,256]{2,1,0:T(8,128)(2,1)S(1)} %fusion.54), channel_id=1, source_target_pairs={{0,4},{1,5},{2,6},{3,7},{4,0},{5,1},{6,2},{7,3},{8,12},{9,13},{10,... | collective-permute-start | bytes 294920 | tf_op jit(solution)/shard_map/ppermute | solution.py:16
  51.7 6.7 %collective-permute-start.15 = (bf16[96,256]{1,0:T(8,128)(2,1)S(1)}, bf16[96,256]{1,0:T(8,128)(2,1)S(1)}, u32[]{:S(2)}, u32[]{:S(2)}) collective-permute-start(bf16[96,256]{1,0:T(8,128)(2,1)S(1)} %fusion.59), channel_id=1, source_target_pairs={{0,8},{1,9},{2,10},{3,11},{4,12},{5,13},{6,14},{7,15},{8,0},{9,1},... | collective-permute-start | bytes 147464 | tf_op jit(solution)/shard_map/ppermute | solution.py:16
  55.1 5.3 %collective-permute-start.7 = (bf16[96,256]{1,0:T(8,128)(2,1)S(1)}, bf16[96,256]{1,0:T(8,128)(2,1)S(1)}, u32[]{:S(2)}, u32[]{:S(2)}) collective-permute-start(bf16[96,256]{1,0:T(8,128)(2,1)S(1)} %fusion.58), channel_id=1, source_target_pairs={{0,8},{1,9},{2,10},{3,11},{4,12},{5,13},{6,14},{7,15},{8,0},{9,1},... | collective-permute-start | bytes 147464 | tf_op jit(solution)/shard_map/ppermute | solution.py:16
  60.5 5.1 %collective-permute-start.16 = (bf16[96,256]{1,0:T(8,128)(2,1)S(1)}, bf16[96,256]{1,0:T(8,128)(2,1)S(1)}, u32[]{:S(2)}, u32[]{:S(2)}) collective-permute-start(bf16[96,256]{1,0:T(8,128)(2,1)S(1)} %get-tuple-element.22), channel_id=1, source_target_pairs={{0,8},{1,9},{2,10},{3,11},{4,12},{5,13},{6,14},{7,15},{8,0},{9,1},... | collective-permute-start | bytes 147464 | tf_op jit(solution)/shard_map/ppermute | solution.py:16
  61.9 5.4 %collective-permute-start.20 = (bf16[96,256]{1,0:T(8,128)(2,1)S(1)}, bf16[96,256]{1,0:T(8,128)(2,1)S(1)}, u32[]{:S(2)}, u32[]{:S(2)}) collective-permute-start(bf16[96,256]{1,0:T(8,128)(2,1)S(1)} %get-tuple-element.23), channel_id=1, source_target_pairs={{0,8},{1,9},{2,10},{3,11},{4,12},{5,13},{6,14},{7,15},{8,0},{9,1},... | collective-permute-start | bytes 147464 | tf_op jit(solution)/shard_map/ppermute | solution.py:16
  65.6 4.7 %collective-permute-start.17 = (bf16[2,96,256]{2,1,0:T(8,128)(2,1)S(1)}, bf16[2,96,256]{2,1,0:T(8,128)(2,1)S(1)}, u32[]{:S(2)}, u32[]{:S(2)}) collective-permute-start(bf16[2,96,256]{2,1,0:T(8,128)(2,1)S(1)} %pad_maximum_fusion.14), channel_id=1, source_target_pairs={{0,4},{1,5},{2,6},{3,7},{4,0},{5,1},{6,2},{7,3},{8,12},{9,13},{10,... | collective-permute-start | bytes 294920 | tf_op jit(solution)/shard_map/ppermute | solution.py:16
  67.3 5.7 %collective-permute-start.21 = (bf16[2,96,256]{2,1,0:T(8,128)(2,1)S(1)}, bf16[2,96,256]{2,1,0:T(8,128)(2,1)S(1)}, u32[]{:S(2)}, u32[]{:S(2)}) collective-permute-start(bf16[2,96,256]{2,1,0:T(8,128)(2,1)S(1)} %pad_maximum_fusion.15), channel_id=1, source_target_pairs={{0,2},{1,3},{2,0},{3,1},{4,6},{5,7},{6,4},{7,5},{8,10},{9,11},{10,... | collective-permute-start | bytes 294920 | tf_op jit(solution)/shard_map/ppermute | solution.py:16
  70.3 5.7 %collective-permute-start.18 = (bf16[2,2,96,256]{3,2,0,1:T(8,128)(2,1)S(1)}, bf16[2,2,96,256]{3,2,0,1:T(8,128)(2,1)S(1)}, u32[]{:S(2)}, u32[]{:S(2)}) collective-permute-start(bf16[2,2,96,256]{3,2,0,1:T(8,128)(2,1)S(1)} %pad_maximum_fusion.10), channel_id=1, source_target_pairs={{0,2},{1,3},{2,0},{3,1},{4,6},{5,7},{6,4},{7,5},{8,10},{9,11},{10,... | collective-permute-start | bytes 589832 | tf_op jit(solution)/shard_map/ppermute | solution.py:16
  73.0 5.7 %collective-permute-start.22 = (bf16[2,2,96,256]{3,2,1,0:T(8,128)(2,1)S(1)}, bf16[2,2,96,256]{3,2,1,0:T(8,128)(2,1)S(1)}, u32[]{:S(2)}, u32[]{:S(2)}) collective-permute-start(bf16[2,2,96,256]{3,2,1,0:T(8,128)(2,1)S(1)} %pad_maximum_fusion.11), channel_id=1, source_target_pairs={{0,4},{1,5},{2,6},{3,7},{4,0},{5,1},{6,2},{7,3},{8,12},{9,13},{10,... | collective-permute-start | bytes 589832 | tf_op jit(solution)/shard_map/ppermute | solution.py:16
  76.2 2.7 %collective-permute-start.19 = (bf16[2,2,2,96,256]{4,3,0,1,2:T(8,128)(2,1)S(1)}, bf16[2,2,2,96,256]{4,3,0,1,2:T(8,128)(2,1)S(1)}, u32[]{:S(2)}, u32[]{:S(2)}) collective-permute-start(bf16[2,2,2,96,256]{4,3,0,1,2:T(8,128)(2,1)S(1)} %pad_maximum_fusion.6), channel_id=1, source_target_pairs={{0,1},{1,0},{2,3},{3,2},{4,5},{5,4},{6,7},{7,6},{8,9},{9,8},{10,11... | collective-permute-start | bytes 1179656 | tf_op jit(solution)/shard_map/ppermute | solution.py:16
  78.8 1.8 %collective-permute-start.23 = (bf16[2,2,2,96,256]{4,3,2,1,0:T(8,128)(2,1)S(1)}, bf16[2,2,2,96,256]{4,3,2,1,0:T(8,128)(2,1)S(1)}, u32[]{:S(2)}, u32[]{:S(2)}) collective-permute-start(bf16[2,2,2,96,256]{4,3,2,1,0:T(8,128)(2,1)S(1)} %pad_maximum_fusion.7), channel_id=1, source_target_pairs={{0,1},{1,0},{2,3},{3,2},{4,5},{5,4},{6,7},{7,6},{8,9},{9,8},{10,11... | collective-permute-start | bytes 1179656 | tf_op jit(solution)/shard_map/ppermute | solution.py:16
  88.1 7.0 %collective-permute-start.24 = (f32[2,2,2,96,256]{4,3,2,1,0:T(8,128)}, f32[2,2,2,96,256]{4,3,2,1,0:T(8,128)}, u32[]{:S(2)}, u32[]{:S(2)}) collective-permute-start(f32[2,2,2,96,256]{4,3,2,1,0:T(8,128)} %dynamic-slice_bitcast_fusion.2), channel_id=1, source_target_pairs={{0,1},{1,0},{2,3},{3,2},{4,5},{5,4},{6,7},{7,6},{8,9},{9,8},{10,11... | collective-permute-start | bytes 2359304 | tf_op jit(solution)/shard_map/ppermute | solution.py:16
  94.5 3.2 %collective-permute-start.28 = (f32[2,2,2,96,256]{4,3,0,2,1:T(8,128)S(1)}, f32[2,2,2,96,256]{4,3,0,2,1:T(8,128)S(1)}, u32[]{:S(2)}, u32[]{:S(2)}) collective-permute-start(f32[2,2,2,96,256]{4,3,0,2,1:T(8,128)S(1)} %copy.63), channel_id=1, source_target_pairs={{0,1},{1,0},{2,3},{3,2},{4,5},{5,4},{6,7},{7,6},{8,9},{9,8},{10,11... | collective-permute-start | bytes 2359304 | tf_op jit(solution)/shard_map/ppermute | solution.py:16
  96.4 7.0 %collective-permute-start.25 = (bf16[2,2,96,256]{3,2,1,0:T(8,128)(2,1)S(1)}, bf16[2,2,96,256]{3,2,1,0:T(8,128)(2,1)S(1)}, u32[]{:S(2)}, u32[]{:S(2)}) collective-permute-start(bf16[2,2,96,256]{3,2,1,0:T(8,128)(2,1)S(1)} %fusion.52), channel_id=1, source_target_pairs={{0,2},{1,3},{2,0},{3,1},{4,6},{5,7},{6,4},{7,5},{8,10},{9,11},{10,... | collective-permute-start | bytes 589832 | tf_op jit(solution)/shard_map/ppermute | solution.py:16
  97.9 6.7 %collective-permute-start.29 = (bf16[2,2,96,256]{3,2,0,1:T(8,128)(2,1)S(1)}, bf16[2,2,96,256]{3,2,0,1:T(8,128)(2,1)S(1)}, u32[]{:S(2)}, u32[]{:S(2)}) collective-permute-start(bf16[2,2,96,256]{3,2,0,1:T(8,128)(2,1)S(1)} %fusion.53), channel_id=1, source_target_pairs={{0,4},{1,5},{2,6},{3,7},{4,0},{5,1},{6,2},{7,3},{8,12},{9,13},{10,... | collective-permute-start | bytes 589832 | tf_op jit(solution)/shard_map/ppermute | solution.py:16
  103.5 4.7 %collective-permute-start.26 = (bf16[2,96,256]{2,1,0:T(8,128)(2,1)S(1)}, bf16[2,96,256]{2,1,0:T(8,128)(2,1)S(1)}, u32[]{:S(2)}, u32[]{:S(2)}) collective-permute-start(bf16[2,96,256]{2,1,0:T(8,128)(2,1)S(1)} %fusion.56), channel_id=1, source_target_pairs={{0,4},{1,5},{2,6},{3,7},{4,0},{5,1},{6,2},{7,3},{8,12},{9,13},{10,... | collective-permute-start | bytes 294920 | tf_op jit(solution)/shard_map/ppermute | solution.py:16
  104.7 4.7 %collective-permute-start.30 = (bf16[2,96,256]{2,1,0:T(8,128)(2,1)S(1)}, bf16[2,96,256]{2,1,0:T(8,128)(2,1)S(1)}, u32[]{:S(2)}, u32[]{:S(2)}) collective-permute-start(bf16[2,96,256]{2,1,0:T(8,128)(2,1)S(1)} %fusion.57), channel_id=1, source_target_pairs={{0,2},{1,3},{2,0},{3,1},{4,6},{5,7},{6,4},{7,5},{8,10},{9,11},{10,... | collective-permute-start | bytes 294920 | tf_op jit(solution)/shard_map/ppermute | solution.py:16
  108.2 5.1 %collective-permute-start.27 = (bf16[96,256]{1,0:T(8,128)(2,1)S(1)}, bf16[96,256]{1,0:T(8,128)(2,1)S(1)}, u32[]{:S(2)}, u32[]{:S(2)}) collective-permute-start(bf16[96,256]{1,0:T(8,128)(2,1)S(1)} %fusion.60), channel_id=1, source_target_pairs={{0,8},{1,9},{2,10},{3,11},{4,12},{5,13},{6,14},{7,15},{8,0},{9,1},... | collective-permute-start | bytes 147464 | tf_op jit(solution)/shard_map/ppermute | solution.py:16
  109.4 5.6 %collective-permute-start.31 = (bf16[96,256]{1,0:T(8,128)(2,1)S(1)}, bf16[96,256]{1,0:T(8,128)(2,1)S(1)}, u32[]{:S(2)}, u32[]{:S(2)}) collective-permute-start(bf16[96,256]{1,0:T(8,128)(2,1)S(1)} %fusion.61), channel_id=1, source_target_pairs={{0,8},{1,9},{2,10},{3,11},{4,12},{5,13},{6,14},{7,15},{8,0},{9,1},... | collective-permute-start | bytes 147464 | tf_op jit(solution)/shard_map/ppermute | solution.py:16
  115.1 1.2 collective-permute-start.32
  116.3 3.6 %collective-permute-start.33 = (f32[256]{0:T(256)S(1)}, f32[256]{0:T(256)S(1)}, u32[]{:S(2)}, u32[]{:S(2)}) collective-permute-start(f32[256]{0:T(256)S(1)} %add.187), channel_id=1, source_target_pairs={{0,2},{1,3},{2,0},{3,1},{4,6},{5,7},{6,4},{7,5},{8,10},{9,11},{10,... | collective-permute-start | bytes 3080 | tf_op jit(solution)/shard_map/ppermute | solution.py:16
  119.9 3.6 %collective-permute-start.34 = (f32[256]{0:T(256)S(1)}, f32[256]{0:T(256)S(1)}, u32[]{:S(2)}, u32[]{:S(2)}) collective-permute-start(f32[256]{0:T(256)S(1)} %add.188), channel_id=1, source_target_pairs={{0,4},{1,5},{2,6},{3,7},{4,0},{5,1},{6,2},{7,3},{8,12},{9,13},{10,... | collective-permute-start | bytes 3080 | tf_op jit(solution)/shard_map/ppermute | solution.py:16
  123.5 4.5 %collective-permute-start.35 = (f32[256]{0:T(256)S(1)}, f32[256]{0:T(256)S(1)}, u32[]{:S(2)}, u32[]{:S(2)}) collective-permute-start(f32[256]{0:T(256)S(1)} %add.189), channel_id=1, source_target_pairs={{0,8},{1,9},{2,10},{3,11},{4,12},{5,13},{6,14},{7,15},{8,0},{9,1},... | collective-permute-start | bytes 3080 | tf_op jit(solution)/shard_map/ppermute | solution.py:16

commit v7 on v6

--- a/solution.py
+++ b/solution.py
@@ -1,15 +1,39 @@
+import functools
+
 import jax
 import jax.numpy as jnp
 from jax import lax
+from jax.experimental import pallas as pl
+from jax.experimental.pallas import tpu as pltpu
 from jax.sharding import PartitionSpec as P
 
 SECTORS = 2
 
 
-def contract_rows(left, right):
-    return lax.dot_general(
-        left, right, (((0,), (0,)), ((), ())), preferred_element_type=jnp.float32
+def rotate_kernel(sector, panels_ref, state_ref, scale_ref, out_ref):
+    projected = jnp.dot(panels_ref[sector], state_ref[...], preferred_element_type=jnp.float32)
+    projected = (projected * scale_ref[...]).astype(jnp.bfloat16)
+    out_ref[...] = lax.dot_general(
+        panels_ref[sector + 1], projected, (((0,), (0,)), ((), ())),
+        preferred_element_type=jnp.float32,
     )
+
+
+def rotate_local(panels, state, scale, sector):
+    points, channels = panels.shape[1], panels.shape[2]
+    width = state.shape[1]
+    vmem = pl.BlockSpec(memory_space=pltpu.VMEM)
+    return pl.pallas_call(
+        functools.partial(rotate_kernel, sector),
+        out_shape=jax.ShapeDtypeStruct((channels, width), jnp.float32),
+        in_specs=[vmem, vmem, vmem],
+        out_specs=vmem,
+        cost_estimate=pl.CostEstimate(
+            flops=4 * points * channels * width,
+            transcendentals=0,
+            bytes_accessed=2 * (panels.size + state.size) + 4 * channels * width,
+        ),
+    )(panels, state, scale[None, :])
 
 
 def exchange(x, distance, devices):
@@ -74,12 +98,9 @@
     der_full = doubling_all_gather(first_g, devices, order_der[::-1])
     scale = None
     for sector in range(SECTORS):
-        halves = []
-        for gathered in (amp_full, der_full):
-            projected = jnp.dot(panels[sector], gathered, preferred_element_type=jnp.float32)
-            if scale is not None:
-                projected = projected * scale[None, :]
-            halves.append(contract_rows(panels[sector + 1], projected.astype(jnp.bfloat16)))
+        if scale is None:
+            scale = jnp.ones((width,), jnp.float32)
+        halves = [rotate_local(panels, gathered, scale, sector) for gathered in (amp_full, der_full)]
         rot_amp = halving_reduce_scatter(halves[0], devices, order_amp)
         rot_der = halving_reduce_scatter(halves[1], devices, order_der)
         angle_rows = lax.dynamic_slice_in_dim(phase[sector], first_row, chan_rows, 0)

time: 129 us -> 134 us (1.039)
  Pallas kernels: 0 us -> 22.4 us
  matrix products: 15.6 us -> 0 us
  other arithmetic: 8.85 us -> 5.54 us
    pallas_call x0 -> x4, Pallas kernels: none -> 22.4 us  [rotate_local(): pl.pallas_call(functools.partial(rotate_kernel, sector), out_shape=jax.Sh...]
    dot_general x4 -> x0, matrix products: 15.6 us -> none  [contract_rows(): lax.dot_general(left, right, (((0,), (0,)), ((), ())), preferred_element_...]
    dot_general x4 -> x0, local copies, waits for them, and re-layouts: 6.08 us -> none  [contract_rows(): lax.dot_general(left, right, (((0,), (0,)), ((), ())), preferred_element_...]
    another operation x4, local copies, waits for them, and re-layouts: 0.18 us -> 3.75 us  [doubling_all_gather(): jnp.stack([jnp.where(low, cur, other), jnp.where(low, other, cur)], axis=...]
    dynamic_slice x1 -> x3, local copies, waits for them, and re-layouts: 1.48 us -> 4.69 us  [halving_reduce_scatter(): keep = lax.dynamic_index_in_dim(cur, mine, axis=axis, keepdims=False)]
    another operation x32, other arithmetic: 5.4 us -> 2.66 us  [doubling_all_gather(): jnp.stack([jnp.where(low, cur, other), jnp.where(low, other, cur)], axis=...]
  transfers between devices with their start and end apart: 36 -> 36, of which waited for: 28 -> 29; matrix products, arithmetic and copies ran while one was open for 13% -> 5% of each run, Pallas kernels for 0% -> 4%
where the time goes in v7:
time: 134 us; the launch traced here: 133 us
  waiting for transfers between devices  57.9 us (43%)
  starting transfers between devices  36.3 us (27%)
  Pallas kernels  22.4 us (17%)
  local copies, waits for them, and re-layouts  9.93 us (7%)
  other arithmetic  5.54 us (4%)
    ppermute x36, waiting for transfers between devices, exchange(): return lax.ppermute(x, 'row', [(i, i ^ distance) for i in range(devices)])  57.9 us
    ppermute x36, starting transfers between devices, exchange(): return lax.ppermute(x, 'row', [(i, i ^ distance) for i in range(devices)])  36.3 us
    pallas_call x4, Pallas kernels, rotate_local(): pl.pallas_call(functools.partial(rotate_kernel, sector), out_shape=jax.Sh...  22.4 us
    dynamic_slice x3, local copies, waits for them, and re-layouts, halving_reduce_scatter(): keep = lax.dynamic_index_in_dim(cur, mine, axis=axis, keepdims=False)  4.69 us
    another operation x4, local copies, waits for them, and re-layouts, doubling_all_gather(): jnp.stack([jnp.where(low, cur, other), jnp.where(low, other, cur)], axis=...  3.75 us
  transfers between devices with their start and end apart: 36, of which 29 were waited for; matrix products, arithmetic and copies ran while one was open for 5% of the time, Pallas kernels for 4%

profile of v7, /device:TPU:0, one launch (start us, length us, event | category | flops | bytes accessed | tf_op | source)
XLA Modules:
  0.0 133.3 jit_solution(3196595886690367129)
XLA Ops:
  0.6 4.1 %collective-permute-start = (bf16[96,256]{1,0:T(8,128)(2,1)}, bf16[96,256]{1,0:T(8,128)(2,1)S(1)}, u32[]{:S(2)}, u32[]{:S(2)}) collective-permute-start(bf16[96,256]{1,0:T(8,128)(2,1)} %param.6), channel_id=1, source_target_pairs={{0,8},{1,9},{2,10},{3,11},{4,12},{5,13},{6,14},{7,15},{8,0},{9,1},... | collective-permute-start | bytes 147464 | tf_op jit(solution)/shard_map/ppermute | solution.py:40
  4.8 2.7 %collective-permute-done = bf16[96,256]{1,0:T(8,128)(2,1)S(1)} collective-permute-done((bf16[96,256]{1,0:T(8,128)(2,1)}, bf16[96,256]{1,0:T(8,128)(2,1)S(1)}, u32[]{:S(2)}, u32[]{:S(2)}) %collective-permute-start) | collective-permute-done | bytes 49184 | tf_op jit(solution)/shard_map/ppermute | solution.py:40
  7.5 0.8 select_bitcast_fusion.31
  8.4 2.2 %collective-permute-start.1 = (bf16[2,96,256]{2,1,0:T(8,128)(2,1)S(1)}, bf16[2,96,256]{2,1,0:T(8,128)(2,1)S(1)}, u32[]{:S(2)}, u32[]{:S(2)}) collective-permute-start(bf16[2,96,256]{2,1,0:T(8,128)(2,1)S(1)} %pad_maximum_fusion.12), channel_id=1, source_target_pairs={{0,4},{1,5},{2,6},{3,7},{4,0},{5,1},{6,2},{7,3},{8,12},{9,13},{10,... | collective-permute-start | bytes 294920 | tf_op jit(solution)/shard_map/ppermute | solution.py:40
  10.6 0.8 select_bitcast_fusion.29
  11.4 1.6 %collective-permute-start.9 = (bf16[2,96,256]{2,1,0:T(8,128)(2,1)S(1)}, bf16[2,96,256]{2,1,0:T(8,128)(2,1)S(1)}, u32[]{:S(2)}, u32[]{:S(2)}) collective-permute-start(bf16[2,96,256]{2,1,0:T(8,128)(2,1)S(1)} %pad_maximum_fusion.13), channel_id=1, source_target_pairs={{0,2},{1,3},{2,0},{3,1},{4,6},{5,7},{6,4},{7,5},{8,10},{9,11},{10,... | collective-permute-start | bytes 294920 | tf_op jit(solution)/shard_map/ppermute | solution.py:40
  13.5 1.6 %collective-permute-start.2 = (bf16[2,2,96,256]{3,2,0,1:T(8,128)(2,1)S(1)}, bf16[2,2,96,256]{3,2,0,1:T(8,128)(2,1)S(1)}, u32[]{:S(2)}, u32[]{:S(2)}) collective-permute-start(bf16[2,2,96,256]{3,2,0,1:T(8,128)(2,1)S(1)} %pad_maximum_fusion.8), channel_id=1, source_target_pairs={{0,2},{1,3},{2,0},{3,1},{4,6},{5,7},{6,4},{7,5},{8,10},{9,11},{10,... | collective-permute-start | bytes 589832 | tf_op jit(solution)/shard_map/ppermute | solution.py:40
  15.1 1.6 %collective-permute-done.9 = bf16[2,96,256]{2,1,0:T(8,128)(2,1)S(1)} collective-permute-done((bf16[2,96,256]{2,1,0:T(8,128)(2,1)S(1)}, bf16[2,96,256]{2,1,0:T(8,128)(2,1)S(1)}, u32[]{:S(2)}, u32[]{:S(2)}) %collective-permute-start.9) | collective-permute-done | bytes 98336 | tf_op jit(solution)/shard_map/ppermute | solution.py:40
  16.8 0.7 collective-permute-start.10
  17.5 2.8 %collective-permute-done.2 = bf16[2,2,96,256]{3,2,0,1:T(8,128)(2,1)S(1)} collective-permute-done((bf16[2,2,96,256]{3,2,0,1:T(8,128)(2,1)S(1)}, bf16[2,2,96,256]{3,2,0,1:T(8,128)(2,1)S(1)}, u32[]{:S(2)}, u32[]{:S(2)}) %collective-permute-start.2) | collective-permute-done | bytes 196640 | tf_op jit(solution)/shard_map/ppermute | solution.py:40
  20.5 2.0 %collective-permute-done.10 = bf16[2,2,96,256]{3,2,0,1:T(8,128)(2,1)S(1)} collective-permute-done((bf16[2,2,96,256]{3,2,0,1:T(8,128)(2,1)S(1)}, bf16[2,2,96,256]{3,2,0,1:T(8,128)(2,1)S(1)}, u32[]{:S(2)}, u32[]{:S(2)}) %collective-permute-start.10) | collective-permute-done | bytes 196640 | tf_op jit(solution)/shard_map/ppermute | solution.py:40
  22.9 0.9 copy.9
  23.9 0.6 collective-permute-done.11
  24.6 0.9 copy.12
  25.5 0.6 broadcast_7_scale_ref.2.scale_ref
  26.0 5.6 %shard_map.69 = f32[1536,256]{1,0:T(8,128)} custom-call(bf16[3,512,1536]{2,1,0:T(8,128)(2,1)} %panels_ref.7, bf16[1536,256]{1,0:T(8,128)(2,1)} %bitcast.190, f32[1,256]{1,0:T(1,128)} %broadcast_7_scale_ref.2.scale_ref), custom_call_target="tpu_custom_call" | custom-call | flops 805306368 | bytes 7077888 | tf_op jit(solution)/shard_map/pallas_call | solution.py:26
  31.6 1.5 %constant_dynamic-slice_fusion.6 = (f32[2,2,2,1,96,256]{5,4,3,2,1,0:T(8,128)S(1)}, f32[2,2,2,1,96,256]{5,4,3,2,1,0:T(8,128)S(1)}) fusion(f32[2,2,2,2,96,256]{5,4,3,2,1,0:T(8,128)} %bitcast.184, s32[]{:T(128)S(6)} %select_n.220, s32[]{:T(128)S(6)} %select_n.221), kind=kLoop, calls=%fused_computation.108 | loop fusion | bytes 3145736 | tf_op jit(solution)/shard_map/jit(dynamic_index_in_dim)/dynamic_slice | solution.py:52
  33.4 5.6 %shard_map.68 = f32[1536,256]{1,0:T(8,128)} custom-call(bf16[3,512,1536]{2,1,0:T(8,128)(2,1)} %panels_ref.7, bf16[1536,256]{1,0:T(8,128)(2,1)} %bitcast.187, f32[1,256]{1,0:T(1,128)} %broadcast_7_scale_ref.2.scale_ref), custom_call_target="tpu_custom_call" | custom-call | flops 805306368 | bytes 7077888 | tf_op jit(solution)/shard_map/pallas_call | solution.py:26
  39.0 1.5 %constant_dynamic-slice_fusion.9 = (f32[2,2,2,1,96,256]{5,4,3,2,1,0:T(8,128)S(1)}, f32[2,2,2,1,96,256]{5,4,3,2,1,0:T(8,128)S(1)}) fusion(f32[2,2,2,2,96,256]{5,4,3,2,1,0:T(8,128)} %bitcast.183, s32[]{:T(128)S(6)} %select_n.220, s32[]{:T(128)S(6)} %select_n.221), kind=kLoop, calls=%fused_computation.111 | loop fusion | bytes 3145736 | tf_op jit(solution)/shard_map/jit(dynamic_index_in_dim)/dynamic_slice | solution.py:52
  41.5 0.7 collective-permute-start.13
  42.2 0.7 collective-permute-done.4
  43.1 1.7 %collective-permute-start.5 = (bf16[2,2,96,256]{3,2,0,1:T(8,128)(2,1)S(1)}, bf16[2,2,96,256]{3,2,0,1:T(8,128)(2,1)S(1)}, u32[]{:S(2)}, u32[]{:S(2)}) collective-permute-start(bf16[2,2,96,256]{3,2,0,1:T(8,128)(2,1)S(1)} %fusion), channel_id=1, source_target_pairs={{0,2},{1,3},{2,0},{3,1},{4,6},{5,7},{6,4},{7,5},{8,10},{9,11},{10,... | collective-permute-start | bytes 589832 | tf_op jit(solution)/shard_map/ppermute | solution.py:40
  44.8 4.0 %collective-permute-done.13 = bf16[2,2,96,256]{3,2,0,1:T(8,128)(2,1)S(1)} collective-permute-done((bf16[2,2,96,256]{3,2,0,1:T(8,128)(2,1)S(1)}, bf16[2,2,96,256]{3,2,0,1:T(8,128)(2,1)S(1)}, u32[]{:S(2)}, u32[]{:S(2)}) %collective-permute-start.13) | collective-permute-done | bytes 196640 | tf_op jit(solution)/shard_map/ppermute | solution.py:40
  48.8 1.7 %collective-permute-start.14 = (bf16[2,96,256]{2,1,0:T(8,128)(2,1)S(1)}, bf16[2,96,256]{2,1,0:T(8,128)(2,1)S(1)}, u32[]{:S(2)}, u32[]{:S(2)}) collective-permute-start(bf16[2,96,256]{2,1,0:T(8,128)(2,1)S(1)} %fusion.5), channel_id=1, source_target_pairs={{0,2},{1,3},{2,0},{3,1},{4,6},{5,7},{6,4},{7,5},{8,10},{9,11},{10,... | collective-permute-start | bytes 294920 | tf_op jit(solution)/shard_map/ppermute | solution.py:40
  50.6 0.6 collective-permute-start.6
  51.2 2.3 %collective-permute-done.14 = bf16[2,96,256]{2,1,0:T(8,128)(2,1)S(1)} collective-permute-done((bf16[2,96,256]{2,1,0:T(8,128)(2,1)S(1)}, bf16[2,96,256]{2,1,0:T(8,128)(2,1)S(1)}, u32[]{:S(2)}, u32[]{:S(2)}) %collective-permute-start.14) | collective-permute-done | bytes 98336 | tf_op jit(solution)/shard_map/ppermute | solution.py:40
  53.6 3.3 %collective-permute-start.15 = (bf16[96,256]{1,0:T(8,128)(2,1)S(1)}, bf16[96,256]{1,0:T(8,128)(2,1)S(1)}, u32[]{:S(2)}, u32[]{:S(2)}) collective-permute-start(bf16[96,256]{1,0:T(8,128)(2,1)S(1)} %fusion.9), channel_id=1, source_target_pairs={{0,8},{1,9},{2,10},{3,11},{4,12},{5,13},{6,14},{7,15},{8,0},{9,1},... | collective-permute-start | bytes 147464 | tf_op jit(solution)/shard_map/ppermute | solution.py:40
  57.0 1.7 %collective-permute-start.7 = (bf16[96,256]{1,0:T(8,128)(2,1)S(1)}, bf16[96,256]{1,0:T(8,128)(2,1)S(1)}, u32[]{:S(2)}, u32[]{:S(2)}) collective-permute-start(bf16[96,256]{1,0:T(8,128)(2,1)S(1)} %fusion.8), channel_id=1, source_target_pairs={{0,8},{1,9},{2,10},{3,11},{4,12},{5,13},{6,14},{7,15},{8,0},{9,1},... | collective-permute-start | bytes 147464 | tf_op jit(solution)/shard_map/ppermute | solution.py:40
  58.8 1.5 %collective-permute-done.15 = bf16[96,256]{1,0:T(8,128)(2,1)S(1)} collective-permute-done((bf16[96,256]{1,0:T(8,128)(2,1)S(1)}, bf16[96,256]{1,0:T(8,128)(2,1)S(1)}, u32[]{:S(2)}, u32[]{:S(2)}) %collective-permute-start.15) | collective-permute-done | bytes 49184 | tf_op jit(solution)/shard_map/ppermute | solution.py:40
  60.3 2.0 %collective-permute-done.7 = bf16[96,256]{1,0:T(8,128)(2,1)S(1)} collective-permute-done((bf16[96,256]{1,0:T(8,128)(2,1)S(1)}, bf16[96,256]{1,0:T(8,128)(2,1)S(1)}, u32[]{:S(2)}, u32[]{:S(2)}) %collective-permute-start.7) | collective-permute-done | bytes 49184 | tf_op jit(solution)/shard_map/ppermute | solution.py:40
  62.4 1.5 %collective-permute-start.16 = (bf16[96,256]{1,0:T(8,128)(2,1)S(1)}, bf16[96,256]{1,0:T(8,128)(2,1)S(1)}, u32[]{:S(2)}, u32[]{:S(2)}) collective-permute-start(bf16[96,256]{1,0:T(8,128)(2,1)S(1)} %get-tuple-element.24), channel_id=1, source_target_pairs={{0,8},{1,9},{2,10},{3,11},{4,12},{5,13},{6,14},{7,15},{8,0},{9,1},... | collective-permute-start | bytes 147464 | tf_op jit(solution)/shard_map/ppermute | solution.py:40
  63.8 1.5 %collective-permute-start.20 = (bf16[96,256]{1,0:T(8,128)(2,1)S(1)}, bf16[96,256]{1,0:T(8,128)(2,1)S(1)}, u32[]{:S(2)}, u32[]{:S(2)}) collective-permute-start(bf16[96,256]{1,0:T(8,128)(2,1)S(1)} %get-tuple-element.25), channel_id=1, source_target_pairs={{0,8},{1,9},{2,10},{3,11},{4,12},{5,13},{6,14},{7,15},{8,0},{9,1},... | collective-permute-start | bytes 147464 | tf_op jit(solution)/shard_map/ppermute | solution.py:40
  65.4 2.1 %collective-permute-done.16 = bf16[96,256]{1,0:T(8,128)(2,1)S(1)} collective-permute-done((bf16[96,256]{1,0:T(8,128)(2,1)S(1)}, bf16[96,256]{1,0:T(8,128)(2,1)S(1)}, u32[]{:S(2)}, u32[]{:S(2)}) %collective-permute-start.16) | collective-permute-done | bytes 49184 | tf_op jit(solution)/shard_map/ppermute | solution.py:40
  67.6 1.6 %collective-permute-done.20 = bf16[96,256]{1,0:T(8,128)(2,1)S(1)} collective-permute-done((bf16[96,256]{1,0:T(8,128)(2,1)S(1)}, bf16[96,256]{1,0:T(8,128)(2,1)S(1)}, u32[]{:S(2)}, u32[]{:S(2)}) %collective-permute-start.20) | collective-permute-done | bytes 49184 | tf_op jit(solution)/shard_map/ppermute | solution.py:40
  69.2 1.6 %collective-permute-start.21 = (bf16[2,96,256]{2,1,0:T(8,128)(2,1)S(1)}, bf16[2,96,256]{2,1,0:T(8,128)(2,1)S(1)}, u32[]{:S(2)}, u32[]{:S(2)}) collective-permute-start(bf16[2,96,256]{2,1,0:T(8,128)(2,1)S(1)} %pad_maximum_fusion.15), channel_id=1, source_target_pairs={{0,2},{1,3},{2,0},{3,1},{4,6},{5,7},{6,4},{7,5},{8,10},{9,11},{10,... | collective-permute-start | bytes 294920 | tf_op jit(solution)/shard_map/ppermute | solution.py:40
  70.8 1.4 %collective-permute-done.17 = bf16[2,96,256]{2,1,0:T(8,128)(2,1)S(1)} collective-permute-done((bf16[2,96,256]{2,1,0:T(8,128)(2,1)S(1)}, bf16[2,96,256]{2,1,0:T(8,128)(2,1)S(1)}, u32[]{:S(2)}, u32[]{:S(2)}) %collective-permute-start.17) | collective-permute-done | bytes 98336 | tf_op jit(solution)/shard_map/ppermute | solution.py:40
  72.2 1.8 %collective-permute-start.18 = (bf16[2,2,96,256]{3,2,0,1:T(8,128)(2,1)S(1)}, bf16[2,2,96,256]{3,2,0,1:T(8,128)(2,1)S(1)}, u32[]{:S(2)}, u32[]{:S(2)}) collective-permute-start(bf16[2,2,96,256]{3,2,0,1:T(8,128)(2,1)S(1)} %pad_maximum_fusion.10), channel_id=1, source_target_pairs={{0,2},{1,3},{2,0},{3,1},{4,6},{5,7},{6,4},{7,5},{8,10},{9,11},{10,... | collective-permute-start | bytes 589832 | tf_op jit(solution)/shard_map/ppermute | solution.py:40
  74.0 0.9 collective-permute-done.21
  75.1 2.8 %collective-permute-done.18 = bf16[2,2,96,256]{3,2,0,1:T(8,128)(2,1)S(1)} collective-permute-done((bf16[2,2,96,256]{3,2,0,1:T(8,128)(2,1)S(1)}, bf16[2,2,96,256]{3,2,0,1:T(8,128)(2,1)S(1)}, u32[]{:S(2)}, u32[]{:S(2)}) %collective-permute-start.18) | collective-permute-done | bytes 196640 | tf_op jit(solution)/shard_map/ppermute | solution.py:40
  78.1 2.5 %collective-permute-done.22 = bf16[2,2,96,256]{3,2,0,1:T(8,128)(2,1)S(1)} collective-permute-done((bf16[2,2,96,256]{3,2,0,1:T(8,128)(2,1)S(1)}, bf16[2,2,96,256]{3,2,0,1:T(8,128)(2,1)S(1)}, u32[]{:S(2)}, u32[]{:S(2)}) %collective-permute-start.22) | collective-permute-done | bytes 196640 | tf_op jit(solution)/shard_map/ppermute | solution.py:40
  81.2 1.3 collective-permute-done.23
  82.9 0.9 copy.17
  83.8 0.9 copy.20
  84.8 0.6 add_rsqrt_fusion.1
  85.3 5.6 %shard_map.71 = f32[1536,256]{1,0:T(8,128)} custom-call(bf16[3,512,1536]{2,1,0:T(8,128)(2,1)} %panels_ref.7, bf16[1536,256]{1,0:T(8,128)(2,1)} %bitcast.189, f32[1,256]{1,0:T(1,128)} %bitcast.195), custom_call_target="tpu_custom_call" | custom-call | flops 805306368 | bytes 7077888 | tf_op jit(solution)/shard_map/pallas_call | solution.py:26
  90.9 5.7 %shard_map.70 = f32[1536,256]{1,0:T(8,128)} custom-call(bf16[3,512,1536]{2,1,0:T(8,128)(2,1)} %panels_ref.7, bf16[1536,256]{1,0:T(8,128)(2,1)} %bitcast.188, f32[1,256]{1,0:T(1,128)} %bitcast.196), custom_call_target="tpu_custom_call" | custom-call | flops 805306368 | bytes 7077888 | tf_op jit(solution)/shard_map/pallas_call | solution.py:26
  96.6 1.7 %constant_dynamic-slice_fusion.1 = (f32[2,2,2,1,96,256]{5,4,3,2,1,0:T(8,128)S(1)}, f32[2,2,2,1,96,256]{5,4,3,2,1,0:T(8,128)S(1)}, f32[2,2,2,1,96,256]{5,4,3,2,1,0:T(8,128)S(1)}, f32[2,2,2,1,96,256]{5,4,3,2,1,0:T(8,128)S(1)}) fusion(f32[2,2,2,2,96,256]{5,4,3,2,1,0:T(8,128)S(1)} %bitcast.185, s32[]{:T(128)S(6)} %select_n.220, s32[]{:T(128)S(6)} %select_n.221, ...), kind=kLoop, calls=%fused_computation.103 | loop fusion | bytes 6291464 | tf_op jit(solution)/shard_map/jit(dynamic_index_in_dim)/dynamic_slice | solution.py:52
  99.1 1.5 %collective-permute-done.24 = f32[2,2,2,96,256]{4,3,0,1,2:T(8,128)S(1)} collective-permute-done((f32[2,2,2,96,256]{4,3,0,1,2:T(8,128)S(1)}, f32[2,2,2,96,256]{4,3,0,1,2:T(8,128)S(1)}, u32[]{:S(2)}, u32[]{:S(2)}) %collective-permute-start.24) | collective-permute-done | bytes 786464 | tf_op jit(solution)/shard_map/ppermute | solution.py:40
  100.8 1.6 %collective-permute-start.25 = (bf16[2,2,96,256]{3,2,0,1:T(8,128)(2,1)S(1)}, bf16[2,2,96,256]{3,2,0,1:T(8,128)(2,1)S(1)}, u32[]{:S(2)}, u32[]{:S(2)}) collective-permute-start(bf16[2,2,96,256]{3,2,0,1:T(8,128)(2,1)S(1)} %fusion.2), channel_id=1, source_target_pairs={{0,2},{1,3},{2,0},{3,1},{4,6},{5,7},{6,4},{7,5},{8,10},{9,11},{10,... | collective-permute-start | bytes 589832 | tf_op jit(solution)/shard_map/ppermute | solution.py:40
  102.8 5.0 %collective-permute-done.25 = bf16[2,2,96,256]{3,2,0,1:T(8,128)(2,1)S(1)} collective-permute-done((bf16[2,2,96,256]{3,2,0,1:T(8,128)(2,1)S(1)}, bf16[2,2,96,256]{3,2,0,1:T(8,128)(2,1)S(1)}, u32[]{:S(2)}, u32[]{:S(2)}) %collective-permute-start.25) | collective-permute-done | bytes 196640 | tf_op jit(solution)/shard_map/ppermute | solution.py:40
  108.1 1.1 collective-permute-done.29
  109.3 1.3 collective-permute-start.30
  110.6 2.0 %collective-permute-done.26 = bf16[2,96,256]{2,1,0:T(8,128)(2,1)S(1)} collective-permute-done((bf16[2,96,256]{2,1,0:T(8,128)(2,1)S(1)}, bf16[2,96,256]{2,1,0:T(8,128)(2,1)S(1)}, u32[]{:S(2)}, u32[]{:S(2)}) %collective-permute-start.26) | collective-permute-done | bytes 98336 | tf_op jit(solution)/shard_map/ppermute | solution.py:40
  112.6 1.1 collective-permute-start.27
  114.1 1.7 %collective-permute-start.31 = (bf16[96,256]{1,0:T(8,128)(2,1)S(1)}, bf16[96,256]{1,0:T(8,128)(2,1)S(1)}, u32[]{:S(2)}, u32[]{:S(2)}) collective-permute-start(bf16[96,256]{1,0:T(8,128)(2,1)S(1)} %fusion.11), channel_id=1, source_target_pairs={{0,8},{1,9},{2,10},{3,11},{4,12},{5,13},{6,14},{7,15},{8,0},{9,1},... | collective-permute-start | bytes 147464 | tf_op jit(solution)/shard_map/ppermute | solution.py:40
  115.8 2.0 %collective-permute-done.27 = bf16[96,256]{1,0:T(8,128)(2,1)S(1)} collective-permute-done((bf16[96,256]{1,0:T(8,128)(2,1)S(1)}, bf16[96,256]{1,0:T(8,128)(2,1)S(1)}, u32[]{:S(2)}, u32[]{:S(2)}) %collective-permute-start.27) | collective-permute-done | bytes 49184 | tf_op jit(solution)/shard_map/ppermute | solution.py:40
  117.9 1.8 %collective-permute-done.31 = bf16[96,256]{1,0:T(8,128)(2,1)S(1)} collective-permute-done((bf16[96,256]{1,0:T(8,128)(2,1)S(1)}, bf16[96,256]{1,0:T(8,128)(2,1)S(1)}, u32[]{:S(2)}, u32[]{:S(2)}) %collective-permute-start.31) | collective-permute-done | bytes 49184 | tf_op jit(solution)/shard_map/ppermute | solution.py:40
  119.9 1.1 collective-permute-done.32
  121.0 0.7 collective-permute-start.33
  121.7 2.9 %collective-permute-done.33 = f32[256]{0:T(256)S(1)} collective-permute-done((f32[256]{0:T(256)S(1)}, f32[256]{0:T(256)S(1)}, u32[]{:S(2)}, u32[]{:S(2)}) %collective-permute-start.33) | collective-permute-done | bytes 1056 | tf_op jit(solution)/shard_map/ppermute | solution.py:40
  124.8 3.3 %collective-permute-done.34 = f32[256]{0:T(256)S(1)} collective-permute-done((f32[256]{0:T(256)S(1)}, f32[256]{0:T(256)S(1)}, u32[]{:S(2)}, u32[]{:S(2)}) %collective-permute-start.34) | collective-permute-done | bytes 1056 | tf_op jit(solution)/shard_map/ppermute | solution.py:40
  128.1 1.1 collective-permute-start.35
  129.2 3.4 %collective-permute-done.35 = f32[256]{0:T(256)S(1)} collective-permute-done((f32[256]{0:T(256)S(1)}, f32[256]{0:T(256)S(1)}, u32[]{:S(2)}, u32[]{:S(2)}) %collective-permute-start.35) | collective-permute-done | bytes 1056 | tf_op jit(solution)/shard_map/ppermute | solution.py:40
  132.6 0.7 broadcast_multiply_fusion
  (103 shorter events, 7.3 us)
Async XLA Ops:
  0.6 6.9 %collective-permute-start = (bf16[96,256]{1,0:T(8,128)(2,1)}, bf16[96,256]{1,0:T(8,128)(2,1)S(1)}, u32[]{:S(2)}, u32[]{:S(2)}) collective-permute-start(bf16[96,256]{1,0:T(8,128)(2,1)} %param.6), channel_id=1, source_target_pairs={{0,8},{1,9},{2,10},{3,11},{4,12},{5,13},{6,14},{7,15},{8,0},{9,1},... | collective-permute-start | bytes 147464 | tf_op jit(solution)/shard_map/ppermute | solution.py:40
  4.7 5.9 %collective-permute-start.8 = (bf16[96,256]{1,0:T(8,128)(2,1)}, bf16[96,256]{1,0:T(8,128)(2,1)S(1)}, u32[]{:S(2)}, u32[]{:S(2)}) collective-permute-start(bf16[96,256]{1,0:T(8,128)(2,1)} %param.7), channel_id=1, source_target_pairs={{0,8},{1,9},{2,10},{3,11},{4,12},{5,13},{6,14},{7,15},{8,0},{9,1},... | collective-permute-start | bytes 147464 | tf_op jit(solution)/shard_map/ppermute | solution.py:40
  8.4 5.1 %collective-permute-start.1 = (bf16[2,96,256]{2,1,0:T(8,128)(2,1)S(1)}, bf16[2,96,256]{2,1,0:T(8,128)(2,1)S(1)}, u32[]{:S(2)}, u32[]{:S(2)}) collective-permute-start(bf16[2,96,256]{2,1,0:T(8,128)(2,1)S(1)} %pad_maximum_fusion.12), channel_id=1, source_target_pairs={{0,4},{1,5},{2,6},{3,7},{4,0},{5,1},{6,2},{7,3},{8,12},{9,13},{10,... | collective-permute-start | bytes 294920 | tf_op jit(solution)/shard_map/ppermute | solution.py:40
  11.4 5.3 %collective-permute-start.9 = (bf16[2,96,256]{2,1,0:T(8,128)(2,1)S(1)}, bf16[2,96,256]{2,1,0:T(8,128)(2,1)S(1)}, u32[]{:S(2)}, u32[]{:S(2)}) collective-permute-start(bf16[2,96,256]{2,1,0:T(8,128)(2,1)S(1)} %pad_maximum_fusion.13), channel_id=1, source_target_pairs={{0,2},{1,3},{2,0},{3,1},{4,6},{5,7},{6,4},{7,5},{8,10},{9,11},{10,... | collective-permute-start | bytes 294920 | tf_op jit(solution)/shard_map/ppermute | solution.py:40
  13.5 6.8 %collective-permute-start.2 = (bf16[2,2,96,256]{3,2,0,1:T(8,128)(2,1)S(1)}, bf16[2,2,96,256]{3,2,0,1:T(8,128)(2,1)S(1)}, u32[]{:S(2)}, u32[]{:S(2)}) collective-permute-start(bf16[2,2,96,256]{3,2,0,1:T(8,128)(2,1)S(1)} %pad_maximum_fusion.8), channel_id=1, source_target_pairs={{0,2},{1,3},{2,0},{3,1},{4,6},{5,7},{6,4},{7,5},{8,10},{9,11},{10,... | collective-permute-start | bytes 589832 | tf_op jit(solution)/shard_map/ppermute | solution.py:40
  16.8 5.9 %copy-start.1 = (f32[2,1536]{1,0:T(2,128)S(1)}, f32[2,1536]{1,0:T(2,128)}, u32[]{:S(2)}) copy-start(f32[2,1536]{1,0:T(2,128)} %param.8) | copy-start | bytes 36868
  16.8 5.7 %collective-permute-start.10 = (bf16[2,2,96,256]{3,2,0,1:T(8,128)(2,1)S(1)}, bf16[2,2,96,256]{3,2,0,1:T(8,128)(2,1)S(1)}, u32[]{:S(2)}, u32[]{:S(2)}) collective-permute-start(bf16[2,2,96,256]{3,2,0,1:T(8,128)(2,1)S(1)} %pad_maximum_fusion.9), channel_id=1, source_target_pairs={{0,4},{1,5},{2,6},{3,7},{4,0},{5,1},{6,2},{7,3},{8,12},{9,13},{10,... | collective-permute-start | bytes 589832 | tf_op jit(solution)/shard_map/ppermute | solution.py:40
  20.4 2.3 %collective-permute-start.3 = (bf16[2,2,2,96,256]{4,3,0,1,2:T(8,128)(2,1)S(1)}, bf16[2,2,2,96,256]{4,3,0,1,2:T(8,128)(2,1)S(1)}, u32[]{:S(2)}, u32[]{:S(2)}) collective-permute-start(bf16[2,2,2,96,256]{4,3,0,1,2:T(8,128)(2,1)S(1)} %pad_maximum_fusion.4), channel_id=1, source_target_pairs={{0,1},{1,0},{2,3},{3,2},{4,5},{5,4},{6,7},{7,6},{8,9},{9,8},{10,11... | collective-permute-start | bytes 1179656 | tf_op jit(solution)/shard_map/ppermute | solution.py:40
  22.6 1.8 %collective-permute-start.11 = (bf16[2,2,2,96,256]{4,3,0,2,1:T(8,128)(2,1)S(1)}, bf16[2,2,2,96,256]{4,3,0,2,1:T(8,128)(2,1)S(1)}, u32[]{:S(2)}, u32[]{:S(2)}) collective-permute-start(bf16[2,2,2,96,256]{4,3,0,2,1:T(8,128)(2,1)S(1)} %pad_maximum_fusion.5), channel_id=1, source_target_pairs={{0,1},{1,0},{2,3},{3,2},{4,5},{5,4},{6,7},{7,6},{8,9},{9,8},{10,11... | collective-permute-start | bytes 1179656 | tf_op jit(solution)/shard_map/ppermute | solution.py:40
  33.2 8.2 %collective-permute-start.12 = (f32[2,2,2,96,256]{4,3,0,2,1:T(8,128)S(1)}, f32[2,2,2,96,256]{4,3,0,2,1:T(8,128)S(1)}, u32[]{:S(2)}, u32[]{:S(2)}) collective-permute-start(f32[2,2,2,96,256]{4,3,0,2,1:T(8,128)S(1)} %bitcast.191), channel_id=1, source_target_pairs={{0,1},{1,0},{2,3},{3,2},{4,5},{5,4},{6,7},{7,6},{8,9},{9,8},{10,11... | collective-permute-start | bytes 2359304 | tf_op jit(solution)/shard_map/ppermute | solution.py:40
  40.5 0.7 copy-start.2
  40.6 2.4 %collective-permute-start.4 = (f32[2,2,2,96,256]{4,3,0,1,2:T(8,128)S(1)}, f32[2,2,2,96,256]{4,3,0,1,2:T(8,128)S(1)}, u32[]{:S(2)}, u32[]{:S(2)}) collective-permute-start(f32[2,2,2,96,256]{4,3,0,1,2:T(8,128)S(1)} %bitcast.192), channel_id=1, source_target_pairs={{0,1},{1,0},{2,3},{3,2},{4,5},{5,4},{6,7},{7,6},{8,9},{9,8},{10,11... | collective-permute-start | bytes 2359304 | tf_op jit(solution)/shard_map/ppermute | solution.py:40
  41.5 7.2 %collective-permute-start.13 = (bf16[2,2,96,256]{3,2,0,1:T(8,128)(2,1)S(1)}, bf16[2,2,96,256]{3,2,0,1:T(8,128)(2,1)S(1)}, u32[]{:S(2)}, u32[]{:S(2)}) collective-permute-start(bf16[2,2,96,256]{3,2,0,1:T(8,128)(2,1)S(1)} %fusion.1), channel_id=1, source_target_pairs={{0,4},{1,5},{2,6},{3,7},{4,0},{5,1},{6,2},{7,3},{8,12},{9,13},{10,... | collective-permute-start | bytes 589832 | tf_op jit(solution)/shard_map/ppermute | solution.py:40
  43.1 7.4 %collective-permute-start.5 = (bf16[2,2,96,256]{3,2,0,1:T(8,128)(2,1)S(1)}, bf16[2,2,96,256]{3,2,0,1:T(8,128)(2,1)S(1)}, u32[]{:S(2)}, u32[]{:S(2)}) collective-permute-start(bf16[2,2,96,256]{3,2,0,1:T(8,128)(2,1)S(1)} %fusion), channel_id=1, source_target_pairs={{0,2},{1,3},{2,0},{3,1},{4,6},{5,7},{6,4},{7,5},{8,10},{9,11},{10,... | collective-permute-start | bytes 589832 | tf_op jit(solution)/shard_map/ppermute | solution.py:40
  48.8 4.7 %collective-permute-start.14 = (bf16[2,96,256]{2,1,0:T(8,128)(2,1)S(1)}, bf16[2,96,256]{2,1,0:T(8,128)(2,1)S(1)}, u32[]{:S(2)}, u32[]{:S(2)}) collective-permute-start(bf16[2,96,256]{2,1,0:T(8,128)(2,1)S(1)} %fusion.5), channel_id=1, source_target_pairs={{0,2},{1,3},{2,0},{3,1},{4,6},{5,7},{6,4},{7,5},{8,10},{9,11},{10,... | collective-permute-start | bytes 294920 | tf_op jit(solution)/shard_map/ppermute | solution.py:40
  50.6 6.3 %collective-permute-start.6 = (bf16[2,96,256]{2,1,0:T(8,128)(2,1)S(1)}, bf16[2,96,256]{2,1,0:T(8,128)(2,1)S(1)}, u32[]{:S(2)}, u32[]{:S(2)}) collective-permute-start(bf16[2,96,256]{2,1,0:T(8,128)(2,1)S(1)} %fusion.4), channel_id=1, source_target_pairs={{0,4},{1,5},{2,6},{3,7},{4,0},{5,1},{6,2},{7,3},{8,12},{9,13},{10,... | collective-permute-start | bytes 294920 | tf_op jit(solution)/shard_map/ppermute | solution.py:40
  53.6 6.7 %collective-permute-start.15 = (bf16[96,256]{1,0:T(8,128)(2,1)S(1)}, bf16[96,256]{1,0:T(8,128)(2,1)S(1)}, u32[]{:S(2)}, u32[]{:S(2)}) collective-permute-start(bf16[96,256]{1,0:T(8,128)(2,1)S(1)} %fusion.9), channel_id=1, source_target_pairs={{0,8},{1,9},{2,10},{3,11},{4,12},{5,13},{6,14},{7,15},{8,0},{9,1},... | collective-permute-start | bytes 147464 | tf_op jit(solution)/shard_map/ppermute | solution.py:40
  57.0 5.3 %collective-permute-start.7 = (bf16[96,256]{1,0:T(8,128)(2,1)S(1)}, bf16[96,256]{1,0:T(8,128)(2,1)S(1)}, u32[]{:S(2)}, u32[]{:S(2)}) collective-permute-start(bf16[96,256]{1,0:T(8,128)(2,1)S(1)} %fusion.8), channel_id=1, source_target_pairs={{0,8},{1,9},{2,10},{3,11},{4,12},{5,13},{6,14},{7,15},{8,0},{9,1},... | collective-permute-start | bytes 147464 | tf_op jit(solution)/shard_map/ppermute | solution.py:40
  62.4 5.1 %collective-permute-start.16 = (bf16[96,256]{1,0:T(8,128)(2,1)S(1)}, bf16[96,256]{1,0:T(8,128)(2,1)S(1)}, u32[]{:S(2)}, u32[]{:S(2)}) collective-permute-start(bf16[96,256]{1,0:T(8,128)(2,1)S(1)} %get-tuple-element.24), channel_id=1, source_target_pairs={{0,8},{1,9},{2,10},{3,11},{4,12},{5,13},{6,14},{7,15},{8,0},{9,1},... | collective-permute-start | bytes 147464 | tf_op jit(solution)/shard_map/ppermute | solution.py:40
  63.8 5.3 %collective-permute-start.20 = (bf16[96,256]{1,0:T(8,128)(2,1)S(1)}, bf16[96,256]{1,0:T(8,128)(2,1)S(1)}, u32[]{:S(2)}, u32[]{:S(2)}) collective-permute-start(bf16[96,256]{1,0:T(8,128)(2,1)S(1)} %get-tuple-element.25), channel_id=1, source_target_pairs={{0,8},{1,9},{2,10},{3,11},{4,12},{5,13},{6,14},{7,15},{8,0},{9,1},... | collective-permute-start | bytes 147464 | tf_op jit(solution)/shard_map/ppermute | solution.py:40
  67.5 4.7 %collective-permute-start.17 = (bf16[2,96,256]{2,1,0:T(8,128)(2,1)S(1)}, bf16[2,96,256]{2,1,0:T(8,128)(2,1)S(1)}, u32[]{:S(2)}, u32[]{:S(2)}) collective-permute-start(bf16[2,96,256]{2,1,0:T(8,128)(2,1)S(1)} %pad_maximum_fusion.14), channel_id=1, source_target_pairs={{0,4},{1,5},{2,6},{3,7},{4,0},{5,1},{6,2},{7,3},{8,12},{9,13},{10,... | collective-permute-start | bytes 294920 | tf_op jit(solution)/shard_map/ppermute | solution.py:40
  69.2 5.6 %collective-permute-start.21 = (bf16[2,96,256]{2,1,0:T(8,128)(2,1)S(1)}, bf16[2,96,256]{2,1,0:T(8,128)(2,1)S(1)}, u32[]{:S(2)}, u32[]{:S(2)}) collective-permute-start(bf16[2,96,256]{2,1,0:T(8,128)(2,1)S(1)} %pad_maximum_fusion.15), channel_id=1, source_target_pairs={{0,2},{1,3},{2,0},{3,1},{4,6},{5,7},{6,4},{7,5},{8,10},{9,11},{10,... | collective-permute-start | bytes 294920 | tf_op jit(solution)/shard_map/ppermute | solution.py:40
  72.2 5.7 %collective-permute-start.18 = (bf16[2,2,96,256]{3,2,0,1:T(8,128)(2,1)S(1)}, bf16[2,2,96,256]{3,2,0,1:T(8,128)(2,1)S(1)}, u32[]{:S(2)}, u32[]{:S(2)}) collective-permute-start(bf16[2,2,96,256]{3,2,0,1:T(8,128)(2,1)S(1)} %pad_maximum_fusion.10), channel_id=1, source_target_pairs={{0,2},{1,3},{2,0},{3,1},{4,6},{5,7},{6,4},{7,5},{8,10},{9,11},{10,... | collective-permute-start | bytes 589832 | tf_op jit(solution)/shard_map/ppermute | solution.py:40
  74.9 5.7 %collective-permute-start.22 = (bf16[2,2,96,256]{3,2,0,1:T(8,128)(2,1)S(1)}, bf16[2,2,96,256]{3,2,0,1:T(8,128)(2,1)S(1)}, u32[]{:S(2)}, u32[]{:S(2)}) collective-permute-start(bf16[2,2,96,256]{3,2,0,1:T(8,128)(2,1)S(1)} %pad_maximum_fusion.11), channel_id=1, source_target_pairs={{0,4},{1,5},{2,6},{3,7},{4,0},{5,1},{6,2},{7,3},{8,12},{9,13},{10,... | collective-permute-start | bytes 589832 | tf_op jit(solution)/shard_map/ppermute | solution.py:40
  78.0 2.7 %collective-permute-start.19 = (bf16[2,2,2,96,256]{4,3,0,1,2:T(8,128)(2,1)S(1)}, bf16[2,2,2,96,256]{4,3,0,1,2:T(8,128)(2,1)S(1)}, u32[]{:S(2)}, u32[]{:S(2)}) collective-permute-start(bf16[2,2,2,96,256]{4,3,0,1,2:T(8,128)(2,1)S(1)} %pad_maximum_fusion.6), channel_id=1, source_target_pairs={{0,1},{1,0},{2,3},{3,2},{4,5},{5,4},{6,7},{7,6},{8,9},{9,8},{10,11... | collective-permute-start | bytes 1179656 | tf_op jit(solution)/shard_map/ppermute | solution.py:40
  80.7 1.8 %collective-permute-start.23 = (bf16[2,2,2,96,256]{4,3,0,2,1:T(8,128)(2,1)S(1)}, bf16[2,2,2,96,256]{4,3,0,2,1:T(8,128)(2,1)S(1)}, u32[]{:S(2)}, u32[]{:S(2)}) collective-permute-start(bf16[2,2,2,96,256]{4,3,0,2,1:T(8,128)(2,1)S(1)} %pad_maximum_fusion.7), channel_id=1, source_target_pairs={{0,1},{1,0},{2,3},{3,2},{4,5},{5,4},{6,7},{7,6},{8,9},{9,8},{10,11... | collective-permute-start | bytes 1179656 | tf_op jit(solution)/shard_map/ppermute | solution.py:40
  90.9 5.7 %copy-start = (f32[1536,256]{1,0:T(8,128)S(1)}, f32[1536,256]{1,0:T(8,128)}, u32[]{:S(2)}) copy-start(f32[1536,256]{1,0:T(8,128)} %shard_map.71) | copy-start | bytes 4718596
  98.3 2.4 %collective-permute-start.24 = (f32[2,2,2,96,256]{4,3,0,1,2:T(8,128)S(1)}, f32[2,2,2,96,256]{4,3,0,1,2:T(8,128)S(1)}, u32[]{:S(2)}, u32[]{:S(2)}) collective-permute-start(f32[2,2,2,96,256]{4,3,0,1,2:T(8,128)S(1)} %bitcast.194), channel_id=1, source_target_pairs={{0,1},{1,0},{2,3},{3,2},{4,5},{5,4},{6,7},{7,6},{8,9},{9,8},{10,11... | collective-permute-start | bytes 2359304 | tf_op jit(solution)/shard_map/ppermute | solution.py:40
  98.6 3.8 %collective-permute-start.28 = (f32[2,2,2,96,256]{4,3,0,2,1:T(8,128)S(1)}, f32[2,2,2,96,256]{4,3,0,2,1:T(8,128)S(1)}, u32[]{:S(2)}, u32[]{:S(2)}) collective-permute-start(f32[2,2,2,96,256]{4,3,0,2,1:T(8,128)S(1)} %bitcast.193), channel_id=1, source_target_pairs={{0,1},{1,0},{2,3},{3,2},{4,5},{5,4},{6,7},{7,6},{8,9},{9,8},{10,11... | collective-permute-start | bytes 2359304 | tf_op jit(solution)/shard_map/ppermute | solution.py:40
  100.8 7.0 %collective-permute-start.25 = (bf16[2,2,96,256]{3,2,0,1:T(8,128)(2,1)S(1)}, bf16[2,2,96,256]{3,2,0,1:T(8,128)(2,1)S(1)}, u32[]{:S(2)}, u32[]{:S(2)}) collective-permute-start(bf16[2,2,96,256]{3,2,0,1:T(8,128)(2,1)S(1)} %fusion.2), channel_id=1, source_target_pairs={{0,2},{1,3},{2,0},{3,1},{4,6},{5,7},{6,4},{7,5},{8,10},{9,11},{10,... | collective-permute-start | bytes 589832 | tf_op jit(solution)/shard_map/ppermute | solution.py:40
  102.5 6.7 %collective-permute-start.29 = (bf16[2,2,96,256]{3,2,0,1:T(8,128)(2,1)S(1)}, bf16[2,2,96,256]{3,2,0,1:T(8,128)(2,1)S(1)}, u32[]{:S(2)}, u32[]{:S(2)}) collective-permute-start(bf16[2,2,96,256]{3,2,0,1:T(8,128)(2,1)S(1)} %fusion.3), channel_id=1, source_target_pairs={{0,4},{1,5},{2,6},{3,7},{4,0},{5,1},{6,2},{7,3},{8,12},{9,13},{10,... | collective-permute-start | bytes 589832 | tf_op jit(solution)/shard_map/ppermute | solution.py:40
  107.9 4.7 %collective-permute-start.26 = (bf16[2,96,256]{2,1,0:T(8,128)(2,1)S(1)}, bf16[2,96,256]{2,1,0:T(8,128)(2,1)S(1)}, u32[]{:S(2)}, u32[]{:S(2)}) collective-permute-start(bf16[2,96,256]{2,1,0:T(8,128)(2,1)S(1)} %fusion.6), channel_id=1, source_target_pairs={{0,4},{1,5},{2,6},{3,7},{4,0},{5,1},{6,2},{7,3},{8,12},{9,13},{10,... | collective-permute-start | bytes 294920 | tf_op jit(solution)/shard_map/ppermute | solution.py:40
  109.3 4.7 %collective-permute-start.30 = (bf16[2,96,256]{2,1,0:T(8,128)(2,1)S(1)}, bf16[2,96,256]{2,1,0:T(8,128)(2,1)S(1)}, u32[]{:S(2)}, u32[]{:S(2)}) collective-permute-start(bf16[2,96,256]{2,1,0:T(8,128)(2,1)S(1)} %fusion.7), channel_id=1, source_target_pairs={{0,2},{1,3},{2,0},{3,1},{4,6},{5,7},{6,4},{7,5},{8,10},{9,11},{10,... | collective-permute-start | bytes 294920 | tf_op jit(solution)/shard_map/ppermute | solution.py:40
  112.6 5.2 %collective-permute-start.27 = (bf16[96,256]{1,0:T(8,128)(2,1)S(1)}, bf16[96,256]{1,0:T(8,128)(2,1)S(1)}, u32[]{:S(2)}, u32[]{:S(2)}) collective-permute-start(bf16[96,256]{1,0:T(8,128)(2,1)S(1)} %fusion.10), channel_id=1, source_target_pairs={{0,8},{1,9},{2,10},{3,11},{4,12},{5,13},{6,14},{7,15},{8,0},{9,1},... | collective-permute-start | bytes 147464 | tf_op jit(solution)/shard_map/ppermute | solution.py:40
  114.1 5.6 %collective-permute-start.31 = (bf16[96,256]{1,0:T(8,128)(2,1)S(1)}, bf16[96,256]{1,0:T(8,128)(2,1)S(1)}, u32[]{:S(2)}, u32[]{:S(2)}) collective-permute-start(bf16[96,256]{1,0:T(8,128)(2,1)S(1)} %fusion.11), channel_id=1, source_target_pairs={{0,8},{1,9},{2,10},{3,11},{4,12},{5,13},{6,14},{7,15},{8,0},{9,1},... | collective-permute-start | bytes 147464 | tf_op jit(solution)/shard_map/ppermute | solution.py:40
  119.8 1.2 collective-permute-start.32
  121.0 3.6 %collective-permute-start.33 = (f32[256]{0:T(256)S(1)}, f32[256]{0:T(256)S(1)}, u32[]{:S(2)}, u32[]{:S(2)}) collective-permute-start(f32[256]{0:T(256)S(1)} %add.195), channel_id=1, source_target_pairs={{0,2},{1,3},{2,0},{3,1},{4,6},{5,7},{6,4},{7,5},{8,10},{9,11},{10,... | collective-permute-start | bytes 3080 | tf_op jit(solution)/shard_map/ppermute | solution.py:40
  124.6 3.6 %collective-permute-start.34 = (f32[256]{0:T(256)S(1)}, f32[256]{0:T(256)S(1)}, u32[]{:S(2)}, u32[]{:S(2)}) collective-permute-start(f32[256]{0:T(256)S(1)} %add.196), channel_id=1, source_target_pairs={{0,4},{1,5},{2,6},{3,7},{4,0},{5,1},{6,2},{7,3},{8,12},{9,13},{10,... | collective-permute-start | bytes 3080 | tf_op jit(solution)/shard_map/ppermute | solution.py:40
  128.1 4.5 %collective-permute-start.35 = (f32[256]{0:T(256)S(1)}, f32[256]{0:T(256)S(1)}, u32[]{:S(2)}, u32[]{:S(2)}) collective-permute-start(f32[256]{0:T(256)S(1)} %add.197), channel_id=1, source_target_pairs={{0,8},{1,9},{2,10},{3,11},{4,12},{5,13},{6,14},{7,15},{8,0},{9,1},... | collective-permute-start | bytes 3080 | tf_op jit(solution)/shard_map/ppermute | solution.py:40

commit v8 on v4

--- a/solution.py
+++ b/solution.py
@@ -16,34 +16,56 @@
     return lax.ppermute(x, "row", [(i, i ^ distance) for i in range(devices)])
 
 
-def halving_reduce_scatter(z, devices, order):
+def halving_reduce_scatter(parts, devices, orders):
     bits = devices.bit_length() - 1
     me = lax.axis_index("row")
-    cur = z.reshape((2,) * bits + (z.shape[0] // devices, z.shape[1]))
-    left = list(range(bits - 1, -1, -1))
-    for bit in order:
-        axis = left.index(bit)
-        left.remove(bit)
-        mine = (me >> bit) & 1
-        keep = lax.dynamic_index_in_dim(cur, mine, axis=axis, keepdims=False)
-        send = lax.dynamic_index_in_dim(cur, 1 - mine, axis=axis, keepdims=False)
-        cur = keep + exchange(send, 1 << bit, devices)
-    return cur
+    curs = [z.reshape((2,) * bits + (z.shape[0] // devices, z.shape[1])) for z in parts]
+    lefts = [list(range(bits - 1, -1, -1)) for _ in parts]
+    for step in range(bits):
+        keeps, sends = [], []
+        for i, cur in enumerate(curs):
+            bit = orders[i][step]
+            axis = lefts[i].index(bit)
+            lefts[i].remove(bit)
+            mine = (me >> bit) & 1
+            keeps.append(lax.dynamic_index_in_dim(cur, mine, axis=axis, keepdims=False))
+            send = lax.dynamic_index_in_dim(cur, 1 - mine, axis=axis, keepdims=False)
+            if bit != 0:
+                send = send.astype(jnp.bfloat16)
+            sends.append(send)
+        received = grouped_exchange(sends, [order[step] for order in orders], devices)
+        curs = [keep + got.astype(jnp.float32) for keep, got in zip(keeps, received)]
+    return curs
 
 
-def doubling_all_gather(x, devices, order):
+def grouped_exchange(sends, bits, devices):
+    received = [None] * len(sends)
+    for bit in sorted(set(bits)):
+        members = [i for i, b in enumerate(bits) if b == bit]
+        if len(members) == 1:
+            received[members[0]] = exchange(sends[members[0]], 1 << bit, devices)
+        else:
+            got = exchange(jnp.stack([sends[i] for i in members]), 1 << bit, devices)
+            for j, i in enumerate(members):
+                received[i] = got[j]
+    return received
+
+
+def doubling_all_gather(parts, devices, orders):
     me = lax.axis_index("row")
-    cur = x
-    done = []
-    for bit in order:
-        other = exchange(cur, 1 << bit, devices)
-        low = (me >> bit) & 1 == 0
-        axis = sum(1 for b in done if b > bit)
-        done.append(bit)
-        cur = jnp.stack(
-            [jnp.where(low, cur, other), jnp.where(low, other, cur)], axis=axis
-        )
-    return cur.reshape((-1, x.shape[-1]))
+    curs = list(parts)
+    dones = [[] for _ in parts]
+    for step in range(len(orders[0])):
+        bits = [order[step] for order in orders]
+        others = grouped_exchange(curs, bits, devices)
+        for i, bit in enumerate(bits):
+            low = (me >> bit) & 1 == 0
+            axis = sum(1 for b in dones[i] if b > bit)
+            dones[i].append(bit)
+            curs[i] = jnp.stack(
+                [jnp.where(low, curs[i], others[i]), jnp.where(low, others[i], curs[i])], axis=axis
+            )
+    return [cur.reshape((-1, part.shape[-1])) for cur, part in zip(curs, parts)]
 
 
 def doubling_all_reduce(x, devices):
@@ -67,8 +89,8 @@
     all_channels = chan_rows * devices
     first_row = lax.axis_index("row") * chan_rows
     order_amp, order_der = stage_orders(devices)
-    amp_full = doubling_all_gather(first_f, devices, order_amp[::-1])
-    der_full = doubling_all_gather(first_g, devices, order_der[::-1])
+    gather_orders = [order_amp[::-1], order_der[::-1]]
+    amp_full, der_full = doubling_all_gather([first_f, first_g], devices, gather_orders)
     scale = None
     for sector in range(SECTORS):
         halves = []
@@ -77,8 +99,7 @@
             if scale is not None:
                 projected = projected * scale[None, :]
             halves.append(contract_rows(panels[sector + 1], projected.astype(jnp.bfloat16)))
-        rot_amp = halving_reduce_scatter(halves[0], devices, order_amp)
-        rot_der = halving_reduce_scatter(halves[1], devices, order_der)
+        rot_amp, rot_der = halving_reduce_scatter(halves, devices, [order_amp, order_der])
         angle_rows = lax.dynamic_slice_in_dim(phase[sector], first_row, chan_rows, 0)
         wave_rows = lax.dynamic_slice_in_dim(wavenum[sector], first_row, chan_rows, 0)
         cosine = jnp.cos(angle_rows)[:, None]
@@ -87,8 +108,9 @@
         new_amp = cosine * rot_amp + sine / wave * rot_der
         new_der = -wave * sine * rot_amp + cosine * rot_der
         if sector + 1 < SECTORS:
-            amp_full = doubling_all_gather(new_amp.astype(jnp.bfloat16), devices, order_amp[::-1])
-            der_full = doubling_all_gather(new_der.astype(jnp.bfloat16), devices, order_der[::-1])
+            amp_full, der_full = doubling_all_gather(
+                [new_amp.astype(jnp.bfloat16), new_der.astype(jnp.bfloat16)], devices, gather_orders
+            )
             amp_wide = amp_full.astype(jnp.float32)
             der_wide = der_full.astype(jnp.float32)
             norm = jnp.sum(amp_wide * amp_wide, axis=0) + jnp.sum(der_wide * der_wide, axis=0)

time: 146 us -> 138 us (0.945)
  starting transfers between devices: 38.4 us -> 34.7 us
  other arithmetic: 9.4 us -> 7.09 us
  waiting for transfers between devices: 69.8 us -> 67.9 us
    ppermute x36 -> x28, starting transfers between devices: 38.4 us -> 34.7 us  [exchange(): return lax.ppermute(x, 'row', [(i, i ^ distance) for i in range(devices)])]
    squeeze x16 -> x1, local copies, waits for them, and re-layouts: 2.43 us -> 0.14 us  [halving_reduce_scatter(): keeps.append(lax.dynamic_index_in_dim(cur, mine, axis=axis, keepdims=False))]
    add x12 -> x11, other arithmetic: 3.99 us -> 2.02 us  [halving_reduce_scatter(): keep + got.astype(jnp.float32)]
    ppermute x36 -> x28, waiting for transfers between devices: 69.8 us -> 67.9 us  [exchange(): return lax.ppermute(x, 'row', [(i, i ^ distance) for i in range(devices)])]
  transfers between devices with their start and end apart: 36 -> 28, of which waited for: 23 -> 27; matrix products, arithmetic and copies ran while one was open for 18% -> 1% of each run, Pallas kernels for 0% -> 0%
where the time goes in v8:
time: 138 us; the launch traced here: 137 us
  waiting for transfers between devices  67.9 us (49%)
  starting transfers between devices  34.7 us (25%)
  matrix products  15.6 us (11%)
  local copies, waits for them, and re-layouts  10.8 us (8%)
  other arithmetic  7.09 us (5%)
    ppermute x28, waiting for transfers between devices, exchange(): return lax.ppermute(x, 'row', [(i, i ^ distance) for i in range(devices)])  67.9 us
    ppermute x28, starting transfers between devices, exchange(): return lax.ppermute(x, 'row', [(i, i ^ distance) for i in range(devices)])  34.7 us
    dot_general x4, matrix products, contract_rows(): lax.dot_general(left, right, (((0,), (0,)), ((), ())), preferred_element_...  15.6 us
    dot_general x4, local copies, waits for them, and re-layouts, contract_rows(): lax.dot_general(left, right, (((0,), (0,)), ((), ())), preferred_element_...  6.08 us
  transfers between devices with their start and end apart: 28, of which 27 were waited for; matrix products, arithmetic and copies ran while one was open for 1% of the time, Pallas kernels for 0%

profile of v8, /device:TPU:0, one launch (start us, length us, event | category | flops | bytes accessed | tf_op | source)
XLA Modules:
  0.0 137.4 jit_solution(14566351969585564034)
XLA Ops:
  0.6 0.8 pad_maximum_fusion.16
  1.5 4.1 %collective-permute-start = (bf16[2,96,256]{2,1,0:T(8,128)(2,1)S(1)}, bf16[2,96,256]{2,1,0:T(8,128)(2,1)S(1)}, u32[]{:S(2)}, u32[]{:S(2)}) collective-permute-start(bf16[2,96,256]{2,1,0:T(8,128)(2,1)S(1)} %pad_maximum_fusion.16), channel_id=1, source_target_pairs={{0,8},{1,9},{2,10},{3,11},{4,12},{5,13},{6,14},{7,15},{8,0},{9,1},... | collective-permute-start | bytes 294920 | tf_op jit(solution)/shard_map/ppermute | solution.py:16
  5.6 4.9 %collective-permute-done = bf16[2,96,256]{2,1,0:T(8,128)(2,1)S(1)} collective-permute-done((bf16[2,96,256]{2,1,0:T(8,128)(2,1)S(1)}, bf16[2,96,256]{2,1,0:T(8,128)(2,1)S(1)}, u32[]{:S(2)}, u32[]{:S(2)}) %collective-permute-start) | collective-permute-done | bytes 98336 | tf_op jit(solution)/shard_map/ppermute | solution.py:16
  10.5 0.8 select_bitcast_fusion.11
  11.3 1.6 %collective-permute-start.3 = (bf16[2,96,256]{2,1,0:T(8,128)(2,1)S(1)}, bf16[2,96,256]{2,1,0:T(8,128)(2,1)S(1)}, u32[]{:S(2)}, u32[]{:S(2)}) collective-permute-start(bf16[2,96,256]{2,1,0:T(8,128)(2,1)S(1)} %pad_maximum_fusion.18), channel_id=1, source_target_pairs={{0,2},{1,3},{2,0},{3,1},{4,6},{5,7},{6,4},{7,5},{8,10},{9,11},{10,... | collective-permute-start | bytes 294920 | tf_op jit(solution)/shard_map/ppermute | solution.py:16
  13.0 0.7 collective-permute-start.1
  13.7 2.3 %collective-permute-done.3 = bf16[2,96,256]{2,1,0:T(8,128)(2,1)S(1)} collective-permute-done((bf16[2,96,256]{2,1,0:T(8,128)(2,1)S(1)}, bf16[2,96,256]{2,1,0:T(8,128)(2,1)S(1)}, u32[]{:S(2)}, u32[]{:S(2)}) %collective-permute-start.3) | collective-permute-done | bytes 98336 | tf_op jit(solution)/shard_map/ppermute | solution.py:16
  16.0 1.6 %collective-permute-done.1 = bf16[2,96,256]{2,1,0:T(8,128)(2,1)S(1)} collective-permute-done((bf16[2,96,256]{2,1,0:T(8,128)(2,1)S(1)}, bf16[2,96,256]{2,1,0:T(8,128)(2,1)S(1)}, u32[]{:S(2)}, u32[]{:S(2)}) %collective-permute-start.1) | collective-permute-done | bytes 98336 | tf_op jit(solution)/shard_map/ppermute | solution.py:16
  17.7 0.5 collective-permute-start.2
  18.3 0.8 collective-permute-start.4
  19.1 4.4 %collective-permute-done.2 = bf16[2,2,96,256]{3,2,0,1:T(8,128)(2,1)S(1)} collective-permute-done((bf16[2,2,96,256]{3,2,0,1:T(8,128)(2,1)S(1)}, bf16[2,2,96,256]{3,2,0,1:T(8,128)(2,1)S(1)}, u32[]{:S(2)}, u32[]{:S(2)}) %collective-permute-start.2) | collective-permute-done | bytes 196640 | tf_op jit(solution)/shard_map/ppermute | solution.py:16
  23.6 0.4 collective-permute-done.4
  24.4 2.3 %collective-permute-done.5 = bf16[2,2,2,2,96,256]{5,4,3,2,1,0:T(8,128)(2,1)S(1)} collective-permute-done((bf16[2,2,2,2,96,256]{5,4,3,2,1,0:T(8,128)(2,1)S(1)}, bf16[2,2,2,2,96,256]{5,4,3,2,1,0:T(8,128)(2,1)S(1)}, u32[]{:S(2)}, u32[]{:S(2)}) %collective-permute-start.5) | collective-permute-done | bytes 786464 | tf_op jit(solution)/shard_map/ppermute | solution.py:16
  27.0 4.2 %convolution_bitcast_fusion.2 = f32[1536,256]{0,1:T(8,128)} fusion(bf16[1536,256]{1,0:T(8,128)(2,1)S(1)} %bitcast.286, bf16[3,512,1536]{2,1,0:T(8,128)(2,1)} %param.5), kind=kOutput, calls=%fused_computation.2 | convolution fusion | flops 805437440 | bytes 5505024 | tf_op jit(solution)/shard_map/dot_general | solution.py:10
  31.1 1.9 %copy.68 = f32[1536,256]{1,0:T(8,128)S(1)} copy(f32[1536,256]{0,1:T(8,128)} %convolution_bitcast_fusion.2) | data formatting | bytes 3145728 | tf_op jit(solution)/shard_map/dot_general | solution.py:10
  33.1 1.0 copy.109
  34.4 4.1 %convolution_bitcast_fusion.3 = f32[1536,256]{0,1:T(8,128)} fusion(bf16[1536,256]{1,0:T(8,128)(2,1)S(1)} %bitcast.285, bf16[3,512,1536]{2,1,0:T(8,128)(2,1)} %param.5), kind=kOutput, calls=%fused_computation.3 | convolution fusion | flops 805437440 | bytes 5505024 | tf_op jit(solution)/shard_map/dot_general | solution.py:10
  38.5 1.9 %copy.61 = f32[1536,256]{1,0:T(8,128)S(1)} copy(f32[1536,256]{0,1:T(8,128)} %convolution_bitcast_fusion.3) | data formatting | bytes 3145728 | tf_op jit(solution)/shard_map/dot_general | solution.py:10
  40.6 1.1 copy-done
  42.0 0.4 copy-done.1
  42.4 3.0 %collective-permute-done.6 = f32[2,2,2,2,96,256]{5,4,1,3,2,0:T(8,128)} collective-permute-done((f32[2,2,2,2,96,256]{5,4,1,3,2,0:T(8,128)S(1)}, f32[2,2,2,2,96,256]{5,4,1,3,2,0:T(8,128)}, u32[]{:S(2)}, u32[]{:S(2)}) %collective-permute-start.6) | collective-permute-done | bytes 1572896 | tf_op jit(solution)/shard_map/ppermute | solution.py:16
  45.4 1.6 %fusion.49 = (f32[2,2,2,96,256]{4,3,0,2,1:T(8,128)S(1)}, f32[2,2,2,96,256]{4,3,0,2,1:T(8,128)S(1)}) fusion(f32[2,2,2,2,96,256]{5,4,1,3,2,0:T(8,128)} %collective-permute-done.6, f32[2,2,2,1,96,256]{5,4,3,2,1,0:T(8,128)S(1)} %get-tuple-element.10, f32[2,2,2,1,96,256]{5,4,3,2,1,0:T(8,128)S(1)} %get-tuple-element.12), kind=kLoop, calls=%fused_computation.40 | loop fusion | flops 393216 | bytes 4718592 | tf_op jit(solution)/shard_map/add | solution.py:37
  47.0 1.6 %collective-permute-start.7 = (bf16[2,2,96,256]{3,2,0,1:T(8,128)(2,1)S(1)}, bf16[2,2,96,256]{3,2,0,1:T(8,128)(2,1)S(1)}, u32[]{:S(2)}, u32[]{:S(2)}) collective-permute-start(bf16[2,2,96,256]{3,2,0,1:T(8,128)(2,1)S(1)} %fusion.53), channel_id=1, source_target_pairs={{0,2},{1,3},{2,0},{3,1},{4,6},{5,7},{6,4},{7,5},{8,10},{9,11},{10,... | collective-permute-start | bytes 589832 | tf_op jit(solution)/shard_map/ppermute | solution.py:16
  48.8 0.7 collective-permute-start.9
  49.6 4.5 %collective-permute-done.7 = bf16[2,2,96,256]{3,2,0,1:T(8,128)(2,1)S(1)} collective-permute-done((bf16[2,2,96,256]{3,2,0,1:T(8,128)(2,1)S(1)}, bf16[2,2,96,256]{3,2,0,1:T(8,128)(2,1)S(1)}, u32[]{:S(2)}, u32[]{:S(2)}) %collective-permute-start.7) | collective-permute-done | bytes 196640 | tf_op jit(solution)/shard_map/ppermute | solution.py:16
  54.1 0.8 collective-permute-start.8
  54.9 0.7 collective-permute-done.9
  55.6 0.9 collective-permute-start.10
  56.6 2.2 %collective-permute-done.8 = bf16[2,96,256]{2,1,0:T(8,128)(2,1)S(1)} collective-permute-done((bf16[2,96,256]{2,1,0:T(8,128)(2,1)S(1)}, bf16[2,96,256]{2,1,0:T(8,128)(2,1)S(1)}, u32[]{:S(2)}, u32[]{:S(2)}) %collective-permute-start.8) | collective-permute-done | bytes 98336 | tf_op jit(solution)/shard_map/ppermute | solution.py:16
  58.8 1.5 %collective-permute-done.10 = bf16[2,96,256]{2,1,0:T(8,128)(2,1)S(1)} collective-permute-done((bf16[2,96,256]{2,1,0:T(8,128)(2,1)S(1)}, bf16[2,96,256]{2,1,0:T(8,128)(2,1)S(1)}, u32[]{:S(2)}, u32[]{:S(2)}) %collective-permute-start.10) | collective-permute-done | bytes 98336 | tf_op jit(solution)/shard_map/ppermute | solution.py:16
  60.4 2.8 %collective-permute-start.11 = (bf16[2,96,256]{2,1,0:T(8,128)(2,1)S(1)}, bf16[2,96,256]{2,1,0:T(8,128)(2,1)S(1)}, u32[]{:S(2)}, u32[]{:S(2)}) collective-permute-start(bf16[2,96,256]{2,1,0:T(8,128)(2,1)S(1)} %pad_maximum_fusion.19), channel_id=1, source_target_pairs={{0,8},{1,9},{2,10},{3,11},{4,12},{5,13},{6,14},{7,15},{8,0},{9,1},... | collective-permute-start | bytes 294920 | tf_op jit(solution)/shard_map/ppermute | solution.py:16
  63.3 3.7 %collective-permute-done.11 = bf16[2,96,256]{2,1,0:T(8,128)(2,1)S(1)} collective-permute-done((bf16[2,96,256]{2,1,0:T(8,128)(2,1)S(1)}, bf16[2,96,256]{2,1,0:T(8,128)(2,1)S(1)}, u32[]{:S(2)}, u32[]{:S(2)}) %collective-permute-start.11) | collective-permute-done | bytes 98336 | tf_op jit(solution)/shard_map/ppermute | solution.py:16
  67.2 1.9 %collective-permute-start.12 = (bf16[2,96,256]{2,1,0:T(8,128)(2,1)S(1)}, bf16[2,96,256]{2,1,0:T(8,128)(2,1)S(1)}, u32[]{:S(2)}, u32[]{:S(2)}) collective-permute-start(bf16[2,96,256]{2,1,0:T(8,128)(2,1)S(1)} %pad_maximum_fusion.20), channel_id=1, source_target_pairs={{0,8},{1,9},{2,10},{3,11},{4,12},{5,13},{6,14},{7,15},{8,0},{9,1},... | collective-permute-start | bytes 294920 | tf_op jit(solution)/shard_map/ppermute | solution.py:16
  69.0 3.8 %collective-permute-done.12 = bf16[2,96,256]{2,1,0:T(8,128)(2,1)S(1)} collective-permute-done((bf16[2,96,256]{2,1,0:T(8,128)(2,1)S(1)}, bf16[2,96,256]{2,1,0:T(8,128)(2,1)S(1)}, u32[]{:S(2)}, u32[]{:S(2)}) %collective-permute-start.12) | collective-permute-done | bytes 98336 | tf_op jit(solution)/shard_map/ppermute | solution.py:16
  72.8 3.2 %collective-permute-start.13 = (bf16[2,96,256]{2,1,0:T(8,128)(2,1)S(1)}, bf16[2,96,256]{2,1,0:T(8,128)(2,1)S(1)}, u32[]{:S(2)}, u32[]{:S(2)}) collective-permute-start(bf16[2,96,256]{2,1,0:T(8,128)(2,1)S(1)} %pad_maximum_fusion.21), channel_id=1, source_target_pairs={{0,4},{1,5},{2,6},{3,7},{4,0},{5,1},{6,2},{7,3},{8,12},{9,13},{10,... | collective-permute-start | bytes 294920 | tf_op jit(solution)/shard_map/ppermute | solution.py:16
  76.1 3.5 %collective-permute-done.13 = bf16[2,96,256]{2,1,0:T(8,128)(2,1)S(1)} collective-permute-done((bf16[2,96,256]{2,1,0:T(8,128)(2,1)S(1)}, bf16[2,96,256]{2,1,0:T(8,128)(2,1)S(1)}, u32[]{:S(2)}, u32[]{:S(2)}) %collective-permute-start.13) | collective-permute-done | bytes 98336 | tf_op jit(solution)/shard_map/ppermute | solution.py:16
  79.7 0.8 collective-permute-start.14
  80.7 0.7 collective-permute-start.16
  81.5 3.9 %collective-permute-done.14 = bf16[2,2,96,256]{3,2,0,1:T(8,128)(2,1)S(1)} collective-permute-done((bf16[2,2,96,256]{3,2,0,1:T(8,128)(2,1)S(1)}, bf16[2,2,96,256]{3,2,0,1:T(8,128)(2,1)S(1)}, u32[]{:S(2)}, u32[]{:S(2)}) %collective-permute-start.14) | collective-permute-done | bytes 196640 | tf_op jit(solution)/shard_map/ppermute | solution.py:16
  85.5 1.0 collective-permute-done.16
  86.7 2.3 %collective-permute-done.17 = bf16[2,2,2,2,96,256]{5,4,1,2,3,0:T(8,128)(2,1)S(1)} collective-permute-done((bf16[2,2,2,2,96,256]{5,4,1,2,3,0:T(8,128)(2,1)S(1)}, bf16[2,2,2,2,96,256]{5,4,1,2,3,0:T(8,128)(2,1)S(1)}, u32[]{:S(2)}, u32[]{:S(2)}) %collective-permute-start.17) | collective-permute-done | bytes 786464 | tf_op jit(solution)/shard_map/ppermute | solution.py:16
  89.7 0.9 copy.77
  90.7 3.0 %convolution_bitcast_fusion.1 = f32[1536,256]{0,1:T(8,128)S(1)} fusion(bf16[3,512,1536]{2,1,0:T(8,128)(2,1)} %param.5, bf16[1536,256]{1,0:T(8,128)(2,1)S(1)} %bitcast.284, f32[256]{0:T(256)S(1)} %add_rsqrt_fusion.1), kind=kOutput, calls=%fused_computation.1 | convolution fusion | flops 805568512 | bytes 5506048 | tf_op jit(solution)/shard_map/dot_general | solution.py:10
  93.7 0.5 copy.76
  94.2 4.4 %convolution_bitcast_fusion = f32[1536,256]{0,1:T(8,128)} fusion(bf16[3,512,1536]{2,1,0:T(8,128)(2,1)} %param.5, bf16[1536,256]{1,0:T(8,128)(2,1)} %bitcast.283, f32[256]{0:T(256)S(1)} %add_rsqrt_fusion.1), kind=kOutput, calls=%fused_computation | convolution fusion | flops 805568512 | bytes 5506048 | tf_op jit(solution)/shard_map/dot_general | solution.py:10
  98.6 1.9 %copy.78 = f32[1536,256]{1,0:T(8,128)S(1)} copy(f32[1536,256]{0,1:T(8,128)} %convolution_bitcast_fusion) | data formatting | bytes 3145728 | tf_op jit(solution)/shard_map/dot_general | solution.py:10
  101.3 3.2 %collective-permute-done.18 = f32[2,2,2,2,96,256]{5,4,1,3,2,0:T(8,128)S(1)} collective-permute-done((f32[2,2,2,2,96,256]{5,4,1,3,2,0:T(8,128)S(1)}, f32[2,2,2,2,96,256]{5,4,1,3,2,0:T(8,128)S(1)}, u32[]{:S(2)}, u32[]{:S(2)}) %collective-permute-start.18) | collective-permute-done | bytes 1572896 | tf_op jit(solution)/shard_map/ppermute | solution.py:16
  104.6 1.2 collective-permute-start.19
  105.9 1.7 %collective-permute-start.21 = (bf16[2,2,96,256]{3,2,0,1:T(8,128)(2,1)S(1)}, bf16[2,2,96,256]{3,2,0,1:T(8,128)(2,1)S(1)}, u32[]{:S(2)}, u32[]{:S(2)}) collective-permute-start(bf16[2,2,96,256]{3,2,0,1:T(8,128)(2,1)S(1)} %fusion.56), channel_id=1, source_target_pairs={{0,4},{1,5},{2,6},{3,7},{4,0},{5,1},{6,2},{7,3},{8,12},{9,13},{10,... | collective-permute-start | bytes 589832 | tf_op jit(solution)/shard_map/ppermute | solution.py:16
  107.5 4.1 %collective-permute-done.19 = bf16[2,2,96,256]{3,2,1,0:T(8,128)(2,1)S(1)} collective-permute-done((bf16[2,2,96,256]{3,2,1,0:T(8,128)(2,1)S(1)}, bf16[2,2,96,256]{3,2,1,0:T(8,128)(2,1)S(1)}, u32[]{:S(2)}, u32[]{:S(2)}) %collective-permute-start.19) | collective-permute-done | bytes 196640 | tf_op jit(solution)/shard_map/ppermute | solution.py:16
  111.6 1.0 collective-permute-start.20
  112.7 1.8 %collective-permute-start.22 = (bf16[2,96,256]{2,1,0:T(8,128)(2,1)S(1)}, bf16[2,96,256]{2,1,0:T(8,128)(2,1)S(1)}, u32[]{:S(2)}, u32[]{:S(2)}) collective-permute-start(bf16[2,96,256]{2,1,0:T(8,128)(2,1)S(1)} %fusion.60), channel_id=1, source_target_pairs={{0,2},{1,3},{2,0},{3,1},{4,6},{5,7},{6,4},{7,5},{8,10},{9,11},{10,... | collective-permute-start | bytes 294920 | tf_op jit(solution)/shard_map/ppermute | solution.py:16
  114.5 1.8 %collective-permute-done.20 = bf16[2,96,256]{2,1,0:T(8,128)(2,1)S(1)} collective-permute-done((bf16[2,96,256]{2,1,0:T(8,128)(2,1)S(1)}, bf16[2,96,256]{2,1,0:T(8,128)(2,1)S(1)}, u32[]{:S(2)}, u32[]{:S(2)}) %collective-permute-start.20) | collective-permute-done | bytes 98336 | tf_op jit(solution)/shard_map/ppermute | solution.py:16
  116.4 1.0 collective-permute-done.22
  117.5 1.9 %collective-permute-start.23 = (bf16[2,96,256]{2,1,0:T(8,128)(2,1)S(1)}, bf16[2,96,256]{2,1,0:T(8,128)(2,1)S(1)}, u32[]{:S(2)}, u32[]{:S(2)}) collective-permute-start(bf16[2,96,256]{2,1,0:T(8,128)(2,1)S(1)} %pad_maximum_fusion.23), channel_id=1, source_target_pairs={{0,8},{1,9},{2,10},{3,11},{4,12},{5,13},{6,14},{7,15},{8,0},{9,1},... | collective-permute-start | bytes 294920 | tf_op jit(solution)/shard_map/ppermute | solution.py:16
  119.5 3.6 %collective-permute-done.23 = bf16[2,96,256]{2,1,0:T(8,128)(2,1)S(1)} collective-permute-done((bf16[2,96,256]{2,1,0:T(8,128)(2,1)S(1)}, bf16[2,96,256]{2,1,0:T(8,128)(2,1)S(1)}, u32[]{:S(2)}, u32[]{:S(2)}) %collective-permute-start.23) | collective-permute-done | bytes 98336 | tf_op jit(solution)/shard_map/ppermute | solution.py:16
  123.3 1.1 collective-permute-done.24
  124.4 2.6 %collective-permute-start.25 = (f32[256]{0:T(256)S(1)}, f32[256]{0:T(256)S(1)}, u32[]{:S(2)}, u32[]{:S(2)}) collective-permute-start(f32[256]{0:T(256)S(1)} %add.213), channel_id=1, source_target_pairs={{0,2},{1,3},{2,0},{3,1},{4,6},{5,7},{6,4},{7,5},{8,10},{9,11},{10,... | collective-permute-start | bytes 3080 | tf_op jit(solution)/shard_map/ppermute | solution.py:16
  127.1 1.5 %collective-permute-done.25 = f32[256]{0:T(256)S(1)} collective-permute-done((f32[256]{0:T(256)S(1)}, f32[256]{0:T(256)S(1)}, u32[]{:S(2)}, u32[]{:S(2)}) %collective-permute-start.25) | collective-permute-done | bytes 1056 | tf_op jit(solution)/shard_map/ppermute | solution.py:16
  128.6 1.0 collective-permute-start.26
  129.6 2.6 %collective-permute-done.26 = f32[256]{0:T(256)S(1)} collective-permute-done((f32[256]{0:T(256)S(1)}, f32[256]{0:T(256)S(1)}, u32[]{:S(2)}, u32[]{:S(2)}) %collective-permute-start.26) | collective-permute-done | bytes 1056 | tf_op jit(solution)/shard_map/ppermute | solution.py:16
  132.2 1.6 %collective-permute-start.27 = (f32[256]{0:T(256)S(1)}, f32[256]{0:T(256)S(1)}, u32[]{:S(2)}, u32[]{:S(2)}) collective-permute-start(f32[256]{0:T(256)S(1)} %add.215), channel_id=1, source_target_pairs={{0,8},{1,9},{2,10},{3,11},{4,12},{5,13},{6,14},{7,15},{8,0},{9,1},... | collective-permute-start | bytes 3080 | tf_op jit(solution)/shard_map/ppermute | solution.py:16
  133.8 2.9 %collective-permute-done.27 = f32[256]{0:T(256)S(1)} collective-permute-done((f32[256]{0:T(256)S(1)}, f32[256]{0:T(256)S(1)}, u32[]{:S(2)}, u32[]{:S(2)}) %collective-permute-start.27) | collective-permute-done | bytes 1056 | tf_op jit(solution)/shard_map/ppermute | solution.py:16
  136.7 0.7 broadcast_multiply_fusion
  (93 shorter events, 5.4 us)
Async XLA Ops:
  1.5 9.0 %collective-permute-start = (bf16[2,96,256]{2,1,0:T(8,128)(2,1)S(1)}, bf16[2,96,256]{2,1,0:T(8,128)(2,1)S(1)}, u32[]{:S(2)}, u32[]{:S(2)}) collective-permute-start(bf16[2,96,256]{2,1,0:T(8,128)(2,1)S(1)} %pad_maximum_fusion.16), channel_id=1, source_target_pairs={{0,8},{1,9},{2,10},{3,11},{4,12},{5,13},{6,14},{7,15},{8,0},{9,1},... | collective-permute-start | bytes 294920 | tf_op jit(solution)/shard_map/ppermute | solution.py:16
  11.3 4.7 %collective-permute-start.3 = (bf16[2,96,256]{2,1,0:T(8,128)(2,1)S(1)}, bf16[2,96,256]{2,1,0:T(8,128)(2,1)S(1)}, u32[]{:S(2)}, u32[]{:S(2)}) collective-permute-start(bf16[2,96,256]{2,1,0:T(8,128)(2,1)S(1)} %pad_maximum_fusion.18), channel_id=1, source_target_pairs={{0,2},{1,3},{2,0},{3,1},{4,6},{5,7},{6,4},{7,5},{8,10},{9,11},{10,... | collective-permute-start | bytes 294920 | tf_op jit(solution)/shard_map/ppermute | solution.py:16
  13.0 4.7 %collective-permute-start.1 = (bf16[2,96,256]{2,1,0:T(8,128)(2,1)S(1)}, bf16[2,96,256]{2,1,0:T(8,128)(2,1)S(1)}, u32[]{:S(2)}, u32[]{:S(2)}) collective-permute-start(bf16[2,96,256]{2,1,0:T(8,128)(2,1)S(1)} %pad_maximum_fusion.17), channel_id=1, source_target_pairs={{0,4},{1,5},{2,6},{3,7},{4,0},{5,1},{6,2},{7,3},{8,12},{9,13},{10,... | collective-permute-start | bytes 294920 | tf_op jit(solution)/shard_map/ppermute | solution.py:16
  17.7 5.7 %collective-permute-start.2 = (bf16[2,2,96,256]{3,2,0,1:T(8,128)(2,1)S(1)}, bf16[2,2,96,256]{3,2,0,1:T(8,128)(2,1)S(1)}, u32[]{:S(2)}, u32[]{:S(2)}) collective-permute-start(bf16[2,2,96,256]{3,2,0,1:T(8,128)(2,1)S(1)} %pad_maximum_fusion.12), channel_id=1, source_target_pairs={{0,2},{1,3},{2,0},{3,1},{4,6},{5,7},{6,4},{7,5},{8,10},{9,11},{10,... | collective-permute-start | bytes 589832 | tf_op jit(solution)/shard_map/ppermute | solution.py:16
  18.3 5.7 %collective-permute-start.4 = (bf16[2,2,96,256]{3,2,0,1:T(8,128)(2,1)S(1)}, bf16[2,2,96,256]{3,2,0,1:T(8,128)(2,1)S(1)}, u32[]{:S(2)}, u32[]{:S(2)}) collective-permute-start(bf16[2,2,96,256]{3,2,0,1:T(8,128)(2,1)S(1)} %pad_maximum_fusion.13), channel_id=1, source_target_pairs={{0,4},{1,5},{2,6},{3,7},{4,0},{5,1},{6,2},{7,3},{8,12},{9,13},{10,... | collective-permute-start | bytes 589832 | tf_op jit(solution)/shard_map/ppermute | solution.py:16
  24.3 2.4 %collective-permute-start.5 = (bf16[2,2,2,2,96,256]{5,4,3,2,1,0:T(8,128)(2,1)S(1)}, bf16[2,2,2,2,96,256]{5,4,3,2,1,0:T(8,128)(2,1)S(1)}, u32[]{:S(2)}, u32[]{:S(2)}) collective-permute-start(bf16[2,2,2,2,96,256]{5,4,3,2,1,0:T(8,128)(2,1)S(1)} %copy.58), channel_id=1, source_target_pairs={{0,1},{1,0},{2,3},{3,2},{4,5},{5,4},{6,7},{7,6},{8,9},{9,8},{10,11... | collective-permute-start | bytes 2359304 | tf_op jit(solution)/shard_map/ppermute | solution.py:16
  40.5 1.1 copy-start
  41.7 0.7 copy-start.1
  41.7 0.7 copy-start.2
  41.8 3.6 %collective-permute-start.6 = (f32[2,2,2,2,96,256]{5,4,1,3,2,0:T(8,128)S(1)}, f32[2,2,2,2,96,256]{5,4,1,3,2,0:T(8,128)}, u32[]{:S(2)}, u32[]{:S(2)}) collective-permute-start(f32[2,2,2,2,96,256]{5,4,1,3,2,0:T(8,128)S(1)} %pad_maximum_fusion), channel_id=1, source_target_pairs={{0,1},{1,0},{2,3},{3,2},{4,5},{5,4},{6,7},{7,6},{8,9},{9,8},{10,11... | collective-permute-start | bytes 4718600 | tf_op jit(solution)/shard_map/ppermute | solution.py:16
  47.0 7.0 %collective-permute-start.7 = (bf16[2,2,96,256]{3,2,0,1:T(8,128)(2,1)S(1)}, bf16[2,2,96,256]{3,2,0,1:T(8,128)(2,1)S(1)}, u32[]{:S(2)}, u32[]{:S(2)}) collective-permute-start(bf16[2,2,96,256]{3,2,0,1:T(8,128)(2,1)S(1)} %fusion.53), channel_id=1, source_target_pairs={{0,2},{1,3},{2,0},{3,1},{4,6},{5,7},{6,4},{7,5},{8,10},{9,11},{10,... | collective-permute-start | bytes 589832 | tf_op jit(solution)/shard_map/ppermute | solution.py:16
  48.8 6.7 %collective-permute-start.9 = (bf16[2,2,96,256]{3,2,0,1:T(8,128)(2,1)S(1)}, bf16[2,2,96,256]{3,2,0,1:T(8,128)(2,1)S(1)}, u32[]{:S(2)}, u32[]{:S(2)}) collective-permute-start(bf16[2,2,96,256]{3,2,0,1:T(8,128)(2,1)S(1)} %fusion.54), channel_id=1, source_target_pairs={{0,4},{1,5},{2,6},{3,7},{4,0},{5,1},{6,2},{7,3},{8,12},{9,13},{10,... | collective-permute-start | bytes 589832 | tf_op jit(solution)/shard_map/ppermute | solution.py:16
  54.1 4.7 %collective-permute-start.8 = (bf16[2,96,256]{2,1,0:T(8,128)(2,1)S(1)}, bf16[2,96,256]{2,1,0:T(8,128)(2,1)S(1)}, u32[]{:S(2)}, u32[]{:S(2)}) collective-permute-start(bf16[2,96,256]{2,1,0:T(8,128)(2,1)S(1)} %fusion.57), channel_id=1, source_target_pairs={{0,4},{1,5},{2,6},{3,7},{4,0},{5,1},{6,2},{7,3},{8,12},{9,13},{10,... | collective-permute-start | bytes 294920 | tf_op jit(solution)/shard_map/ppermute | solution.py:16
  55.6 4.7 %collective-permute-start.10 = (bf16[2,96,256]{2,1,0:T(8,128)(2,1)S(1)}, bf16[2,96,256]{2,1,0:T(8,128)(2,1)S(1)}, u32[]{:S(2)}, u32[]{:S(2)}) collective-permute-start(bf16[2,96,256]{2,1,0:T(8,128)(2,1)S(1)} %fusion.58), channel_id=1, source_target_pairs={{0,2},{1,3},{2,0},{3,1},{4,6},{5,7},{6,4},{7,5},{8,10},{9,11},{10,... | collective-permute-start | bytes 294920 | tf_op jit(solution)/shard_map/ppermute | solution.py:16
  60.4 6.6 %collective-permute-start.11 = (bf16[2,96,256]{2,1,0:T(8,128)(2,1)S(1)}, bf16[2,96,256]{2,1,0:T(8,128)(2,1)S(1)}, u32[]{:S(2)}, u32[]{:S(2)}) collective-permute-start(bf16[2,96,256]{2,1,0:T(8,128)(2,1)S(1)} %pad_maximum_fusion.19), channel_id=1, source_target_pairs={{0,8},{1,9},{2,10},{3,11},{4,12},{5,13},{6,14},{7,15},{8,0},{9,1},... | collective-permute-start | bytes 294920 | tf_op jit(solution)/shard_map/ppermute | solution.py:16
  67.2 5.6 %collective-permute-start.12 = (bf16[2,96,256]{2,1,0:T(8,128)(2,1)S(1)}, bf16[2,96,256]{2,1,0:T(8,128)(2,1)S(1)}, u32[]{:S(2)}, u32[]{:S(2)}) collective-permute-start(bf16[2,96,256]{2,1,0:T(8,128)(2,1)S(1)} %pad_maximum_fusion.20), channel_id=1, source_target_pairs={{0,8},{1,9},{2,10},{3,11},{4,12},{5,13},{6,14},{7,15},{8,0},{9,1},... | collective-permute-start | bytes 294920 | tf_op jit(solution)/shard_map/ppermute | solution.py:16
  72.8 6.8 %collective-permute-start.13 = (bf16[2,96,256]{2,1,0:T(8,128)(2,1)S(1)}, bf16[2,96,256]{2,1,0:T(8,128)(2,1)S(1)}, u32[]{:S(2)}, u32[]{:S(2)}) collective-permute-start(bf16[2,96,256]{2,1,0:T(8,128)(2,1)S(1)} %pad_maximum_fusion.21), channel_id=1, source_target_pairs={{0,4},{1,5},{2,6},{3,7},{4,0},{5,1},{6,2},{7,3},{8,12},{9,13},{10,... | collective-permute-start | bytes 294920 | tf_op jit(solution)/shard_map/ppermute | solution.py:16
  76.0 4.7 %collective-permute-start.15 = (bf16[2,96,256]{2,1,0:T(8,128)(2,1)S(1)}, bf16[2,96,256]{2,1,0:T(8,128)(2,1)S(1)}, u32[]{:S(2)}, u32[]{:S(2)}) collective-permute-start(bf16[2,96,256]{2,1,0:T(8,128)(2,1)S(1)} %pad_maximum_fusion.22), channel_id=1, source_target_pairs={{0,2},{1,3},{2,0},{3,1},{4,6},{5,7},{6,4},{7,5},{8,10},{9,11},{10,... | collective-permute-start | bytes 294920 | tf_op jit(solution)/shard_map/ppermute | solution.py:16
  79.7 5.7 %collective-permute-start.14 = (bf16[2,2,96,256]{3,2,0,1:T(8,128)(2,1)S(1)}, bf16[2,2,96,256]{3,2,0,1:T(8,128)(2,1)S(1)}, u32[]{:S(2)}, u32[]{:S(2)}) collective-permute-start(bf16[2,2,96,256]{3,2,0,1:T(8,128)(2,1)S(1)} %pad_maximum_fusion.14), channel_id=1, source_target_pairs={{0,2},{1,3},{2,0},{3,1},{4,6},{5,7},{6,4},{7,5},{8,10},{9,11},{10,... | collective-permute-start | bytes 589832 | tf_op jit(solution)/shard_map/ppermute | solution.py:16
  80.7 5.7 %collective-permute-start.16 = (bf16[2,2,96,256]{3,2,0,1:T(8,128)(2,1)S(1)}, bf16[2,2,96,256]{3,2,0,1:T(8,128)(2,1)S(1)}, u32[]{:S(2)}, u32[]{:S(2)}) collective-permute-start(bf16[2,2,96,256]{3,2,0,1:T(8,128)(2,1)S(1)} %pad_maximum_fusion.15), channel_id=1, source_target_pairs={{0,4},{1,5},{2,6},{3,7},{4,0},{5,1},{6,2},{7,3},{8,12},{9,13},{10,... | collective-permute-start | bytes 589832 | tf_op jit(solution)/shard_map/ppermute | solution.py:16
  86.6 2.4 %collective-permute-start.17 = (bf16[2,2,2,2,96,256]{5,4,1,2,3,0:T(8,128)(2,1)S(1)}, bf16[2,2,2,2,96,256]{5,4,1,2,3,0:T(8,128)(2,1)S(1)}, u32[]{:S(2)}, u32[]{:S(2)}) collective-permute-start(bf16[2,2,2,2,96,256]{5,4,1,2,3,0:T(8,128)(2,1)S(1)} %pad_maximum_fusion.5), channel_id=1, source_target_pairs={{0,1},{1,0},{2,3},{3,2},{4,5},{5,4},{6,7},{7,6},{8,9},{9,8},{10,11... | collective-permute-start | bytes 2359304 | tf_op jit(solution)/shard_map/ppermute | solution.py:16
  100.9 3.5 %collective-permute-start.18 = (f32[2,2,2,2,96,256]{5,4,1,3,2,0:T(8,128)S(1)}, f32[2,2,2,2,96,256]{5,4,1,3,2,0:T(8,128)S(1)}, u32[]{:S(2)}, u32[]{:S(2)}) collective-permute-start(f32[2,2,2,2,96,256]{5,4,1,3,2,0:T(8,128)S(1)} %copy.84), channel_id=1, source_target_pairs={{0,1},{1,0},{2,3},{3,2},{4,5},{5,4},{6,7},{7,6},{8,9},{9,8},{10,11... | collective-permute-start | bytes 4718600 | tf_op jit(solution)/shard_map/ppermute | solution.py:16
  104.6 7.0 %collective-permute-start.19 = (bf16[2,2,96,256]{3,2,1,0:T(8,128)(2,1)S(1)}, bf16[2,2,96,256]{3,2,1,0:T(8,128)(2,1)S(1)}, u32[]{:S(2)}, u32[]{:S(2)}) collective-permute-start(bf16[2,2,96,256]{3,2,1,0:T(8,128)(2,1)S(1)} %fusion.55), channel_id=1, source_target_pairs={{0,2},{1,3},{2,0},{3,1},{4,6},{5,7},{6,4},{7,5},{8,10},{9,11},{10,... | collective-permute-start | bytes 589832 | tf_op jit(solution)/shard_map/ppermute | solution.py:16
  105.9 6.8 %collective-permute-start.21 = (bf16[2,2,96,256]{3,2,0,1:T(8,128)(2,1)S(1)}, bf16[2,2,96,256]{3,2,0,1:T(8,128)(2,1)S(1)}, u32[]{:S(2)}, u32[]{:S(2)}) collective-permute-start(bf16[2,2,96,256]{3,2,0,1:T(8,128)(2,1)S(1)} %fusion.56), channel_id=1, source_target_pairs={{0,4},{1,5},{2,6},{3,7},{4,0},{5,1},{6,2},{7,3},{8,12},{9,13},{10,... | collective-permute-start | bytes 589832 | tf_op jit(solution)/shard_map/ppermute | solution.py:16
  111.6 4.7 %collective-permute-start.20 = (bf16[2,96,256]{2,1,0:T(8,128)(2,1)S(1)}, bf16[2,96,256]{2,1,0:T(8,128)(2,1)S(1)}, u32[]{:S(2)}, u32[]{:S(2)}) collective-permute-start(bf16[2,96,256]{2,1,0:T(8,128)(2,1)S(1)} %fusion.59), channel_id=1, source_target_pairs={{0,4},{1,5},{2,6},{3,7},{4,0},{5,1},{6,2},{7,3},{8,12},{9,13},{10,... | collective-permute-start | bytes 294920 | tf_op jit(solution)/shard_map/ppermute | solution.py:16
  112.7 4.7 %collective-permute-start.22 = (bf16[2,96,256]{2,1,0:T(8,128)(2,1)S(1)}, bf16[2,96,256]{2,1,0:T(8,128)(2,1)S(1)}, u32[]{:S(2)}, u32[]{:S(2)}) collective-permute-start(bf16[2,96,256]{2,1,0:T(8,128)(2,1)S(1)} %fusion.60), channel_id=1, source_target_pairs={{0,2},{1,3},{2,0},{3,1},{4,6},{5,7},{6,4},{7,5},{8,10},{9,11},{10,... | collective-permute-start | bytes 294920 | tf_op jit(solution)/shard_map/ppermute | solution.py:16
  117.5 5.6 %collective-permute-start.23 = (bf16[2,96,256]{2,1,0:T(8,128)(2,1)S(1)}, bf16[2,96,256]{2,1,0:T(8,128)(2,1)S(1)}, u32[]{:S(2)}, u32[]{:S(2)}) collective-permute-start(bf16[2,96,256]{2,1,0:T(8,128)(2,1)S(1)} %pad_maximum_fusion.23), channel_id=1, source_target_pairs={{0,8},{1,9},{2,10},{3,11},{4,12},{5,13},{6,14},{7,15},{8,0},{9,1},... | collective-permute-start | bytes 294920 | tf_op jit(solution)/shard_map/ppermute | solution.py:16
  123.2 1.2 collective-permute-start.24
  124.4 4.2 %collective-permute-start.25 = (f32[256]{0:T(256)S(1)}, f32[256]{0:T(256)S(1)}, u32[]{:S(2)}, u32[]{:S(2)}) collective-permute-start(f32[256]{0:T(256)S(1)} %add.213), channel_id=1, source_target_pairs={{0,2},{1,3},{2,0},{3,1},{4,6},{5,7},{6,4},{7,5},{8,10},{9,11},{10,... | collective-permute-start | bytes 3080 | tf_op jit(solution)/shard_map/ppermute | solution.py:16
  128.6 3.6 %collective-permute-start.26 = (f32[256]{0:T(256)S(1)}, f32[256]{0:T(256)S(1)}, u32[]{:S(2)}, u32[]{:S(2)}) collective-permute-start(f32[256]{0:T(256)S(1)} %add.214), channel_id=1, source_target_pairs={{0,4},{1,5},{2,6},{3,7},{4,0},{5,1},{6,2},{7,3},{8,12},{9,13},{10,... | collective-permute-start | bytes 3080 | tf_op jit(solution)/shard_map/ppermute | solution.py:16
  132.2 4.5 %collective-permute-start.27 = (f32[256]{0:T(256)S(1)}, f32[256]{0:T(256)S(1)}, u32[]{:S(2)}, u32[]{:S(2)}) collective-permute-start(f32[256]{0:T(256)S(1)} %add.215), channel_id=1, source_target_pairs={{0,8},{1,9},{2,10},{3,11},{4,12},{5,13},{6,14},{7,15},{8,0},{9,1},... | collective-permute-start | bytes 3080 | tf_op jit(solution)/shard_map/ppermute | solution.py:16

commit v9 on v4

--- a/solution.py
+++ b/solution.py
@@ -27,7 +27,7 @@
         mine = (me >> bit) & 1
         keep = lax.dynamic_index_in_dim(cur, mine, axis=axis, keepdims=False)
         send = lax.dynamic_index_in_dim(cur, 1 - mine, axis=axis, keepdims=False)
-        cur = keep + exchange(send, 1 << bit, devices)
+        cur = keep + exchange(send.astype(jnp.bfloat16), 1 << bit, devices).astype(jnp.float32)
     return cur
 
 

time: 146 us -> 125 us (0.86)
  waiting for transfers between devices: 69.8 us -> 47.3 us
  starting transfers between devices: 38.4 us -> 42.7 us
    ppermute x36, waiting for transfers between devices: 69.8 us -> 47.3 us  [exchange(): return lax.ppermute(x, 'row', [(i, i ^ distance) for i in range(devices)])]
    ppermute x36, starting transfers between devices: 38.4 us -> 42.7 us  [exchange(): return lax.ppermute(x, 'row', [(i, i ^ distance) for i in range(devices)])]
    convert_element_type x0 -> x16, local copies, waits for them, and re-layouts: none -> 2.71 us  [halving_reduce_scatter(): send.astype(jnp.bfloat16)]
    squeeze x16 -> x0, local copies, waits for them, and re-layouts: 2.43 us -> none  [halving_reduce_scatter(): send = lax.dynamic_index_in_dim(cur, 1 - mine, axis=axis, keepdims=False)]
    add x12, other arithmetic: 3.99 us -> 1.6 us  [halving_reduce_scatter(): keep + exchange(send.astype(jnp.bfloat16), 1 << bit, devices).astype(jnp....]
  transfers between devices with their start and end apart: 36 -> 36, of which waited for: 23 -> 24; matrix products, arithmetic and copies ran while one was open for 18% -> 22% of each run, Pallas kernels for 0% -> 0%
where the time goes in v9:
time: 125 us
  waiting for transfers between devices  47.3 us (38%)
  starting transfers between devices  42.7 us (34%)
  matrix products  14.5 us (12%)
  local copies, waits for them, and re-layouts  10.7 us (9%)
  other arithmetic  8.3 us (7%)
    ppermute x36, waiting for transfers between devices, exchange(): return lax.ppermute(x, 'row', [(i, i ^ distance) for i in range(devices)])  47.3 us
    ppermute x36, starting transfers between devices, exchange(): return lax.ppermute(x, 'row', [(i, i ^ distance) for i in range(devices)])  42.7 us
    dot_general x4, matrix products, contract_rows(): lax.dot_general(left, right, (((0,), (0,)), ((), ())), preferred_element_...  14.5 us
    dot_general x4, local copies, waits for them, and re-layouts, contract_rows(): lax.dot_general(left, right, (((0,), (0,)), ((), ())), preferred_element_...  4.68 us
    another operation x32, other arithmetic, doubling_all_gather(): jnp.stack([jnp.where(low, cur, other), jnp.where(low, other, cur)], axis=...  3.75 us
    convert_element_type x16, local copies, waits for them, and re-layouts, halving_reduce_scatter(): send.astype(jnp.bfloat16)  2.71 us
  transfers between devices with their start and end apart: 36, of which 24 were waited for; matrix products, arithmetic and copies ran while one was open for 22% of the time, Pallas kernels for 0%

profile of v9, /device:TPU:0, one launch (start us, length us, event | category | flops | bytes accessed | tf_op | source)
XLA Modules:
  0.0 124.7 jit_solution(16916778927533580667)
XLA Ops:
  0.6 4.1 %collective-permute-start.8 = (bf16[96,256]{1,0:T(8,128)(2,1)}, bf16[96,256]{1,0:T(8,128)(2,1)S(1)}, u32[]{:S(2)}, u32[]{:S(2)}) collective-permute-start(bf16[96,256]{1,0:T(8,128)(2,1)} %param.7), channel_id=1, source_target_pairs={{0,8},{1,9},{2,10},{3,11},{4,12},{5,13},{6,14},{7,15},{8,0},{9,1},... | collective-permute-start | bytes 147464 | tf_op jit(solution)/shard_map/ppermute | solution.py:16
  4.8 2.7 %collective-permute-done.8 = bf16[96,256]{1,0:T(8,128)(2,1)S(1)} collective-permute-done((bf16[96,256]{1,0:T(8,128)(2,1)}, bf16[96,256]{1,0:T(8,128)(2,1)S(1)}, u32[]{:S(2)}, u32[]{:S(2)}) %collective-permute-start.8) | collective-permute-done | bytes 49184 | tf_op jit(solution)/shard_map/ppermute | solution.py:16
  7.5 0.8 select_bitcast_fusion.29
  8.4 1.8 %collective-permute-start.9 = (bf16[2,96,256]{2,1,0:T(8,128)(2,1)S(1)}, bf16[2,96,256]{2,1,0:T(8,128)(2,1)S(1)}, u32[]{:S(2)}, u32[]{:S(2)}) collective-permute-start(bf16[2,96,256]{2,1,0:T(8,128)(2,1)S(1)} %pad_maximum_fusion.13), channel_id=1, source_target_pairs={{0,2},{1,3},{2,0},{3,1},{4,6},{5,7},{6,4},{7,5},{8,10},{9,11},{10,... | collective-permute-start | bytes 294920 | tf_op jit(solution)/shard_map/ppermute | solution.py:16
  10.2 0.8 select_bitcast_fusion.31
  11.0 2.0 %collective-permute-start.1 = (bf16[2,96,256]{2,1,0:T(8,128)(2,1)S(1)}, bf16[2,96,256]{2,1,0:T(8,128)(2,1)S(1)}, u32[]{:S(2)}, u32[]{:S(2)}) collective-permute-start(bf16[2,96,256]{2,1,0:T(8,128)(2,1)S(1)} %pad_maximum_fusion.12), channel_id=1, source_target_pairs={{0,4},{1,5},{2,6},{3,7},{4,0},{5,1},{6,2},{7,3},{8,12},{9,13},{10,... | collective-permute-start | bytes 294920 | tf_op jit(solution)/shard_map/ppermute | solution.py:16
  13.1 2.2 %collective-permute-start.10 = (bf16[2,2,96,256]{3,2,1,0:T(8,128)(2,1)S(1)}, bf16[2,2,96,256]{3,2,1,0:T(8,128)(2,1)S(1)}, u32[]{:S(2)}, u32[]{:S(2)}) collective-permute-start(bf16[2,2,96,256]{3,2,1,0:T(8,128)(2,1)S(1)} %pad_maximum_fusion.9), channel_id=1, source_target_pairs={{0,4},{1,5},{2,6},{3,7},{4,0},{5,1},{6,2},{7,3},{8,12},{9,13},{10,... | collective-permute-start | bytes 589832 | tf_op jit(solution)/shard_map/ppermute | solution.py:16
  15.3 1.0 collective-permute-done.1
  16.4 1.5 %collective-permute-start.2 = (bf16[2,2,96,256]{3,2,0,1:T(8,128)(2,1)S(1)}, bf16[2,2,96,256]{3,2,0,1:T(8,128)(2,1)S(1)}, u32[]{:S(2)}, u32[]{:S(2)}) collective-permute-start(bf16[2,2,96,256]{3,2,0,1:T(8,128)(2,1)S(1)} %pad_maximum_fusion.8), channel_id=1, source_target_pairs={{0,2},{1,3},{2,0},{3,1},{4,6},{5,7},{6,4},{7,5},{8,10},{9,11},{10,... | collective-permute-start | bytes 589832 | tf_op jit(solution)/shard_map/ppermute | solution.py:16
  17.9 2.0 %collective-permute-done.10 = bf16[2,2,96,256]{3,2,1,0:T(8,128)(2,1)S(1)} collective-permute-done((bf16[2,2,96,256]{3,2,1,0:T(8,128)(2,1)S(1)}, bf16[2,2,96,256]{3,2,1,0:T(8,128)(2,1)S(1)}, u32[]{:S(2)}, u32[]{:S(2)}) %collective-permute-start.10) | collective-permute-done | bytes 196640 | tf_op jit(solution)/shard_map/ppermute | solution.py:16
  20.1 0.6 fusion.70
  20.7 1.4 %collective-permute-done.2 = bf16[2,2,96,256]{3,2,0,1:T(8,128)(2,1)S(1)} collective-permute-done((bf16[2,2,96,256]{3,2,0,1:T(8,128)(2,1)S(1)}, bf16[2,2,96,256]{3,2,0,1:T(8,128)(2,1)S(1)}, u32[]{:S(2)}, u32[]{:S(2)}) %collective-permute-start.2) | collective-permute-done | bytes 196640 | tf_op jit(solution)/shard_map/ppermute | solution.py:16
  22.2 0.8 copy.43
  23.2 3.0 %convolution_bitcast_fusion.2 = f32[1536,256]{0,1:T(8,128)S(1)} fusion(bf16[1536,256]{1,0:T(8,128)(2,1)S(1)} %bitcast.250, bf16[3,512,1536]{2,1,0:T(8,128)(2,1)} %param.5), kind=kOutput, calls=%fused_computation.2 | convolution fusion | flops 805437440 | bytes 5505024 | tf_op jit(solution)/shard_map/dot_general | solution.py:10
  26.7 0.8 fusion.50
  28.0 1.2 select_bitcast_fusion.7
  29.2 4.2 %convolution_bitcast_fusion.3 = f32[1536,256]{0,1:T(8,128)} fusion(bf16[1536,256]{1,0:T(8,128)(2,1)S(1)} %bitcast.249, bf16[3,512,1536]{2,1,0:T(8,128)(2,1)} %param.5), kind=kOutput, calls=%fused_computation.3 | convolution fusion | flops 805437440 | bytes 5505024 | tf_op jit(solution)/shard_map/dot_general | solution.py:10
  33.4 1.9 %copy.22 = f32[1536,256]{1,0:T(8,128)S(1)} copy(f32[1536,256]{0,1:T(8,128)} %convolution_bitcast_fusion.3) | data formatting | bytes 3145728 | tf_op jit(solution)/shard_map/dot_general | solution.py:10
  35.2 0.8 fusion.49
  36.0 1.4 %bitcast_divide_fusion.1 = (f32[96]{0:T(128)}, f32[96]{0:T(128)}) fusion(f32[1,1536]{1,0:T(1,128)} %get-tuple-element.52, s32[]{:T(128)S(6)} %select_n.207, f32[1,1536]{1,0:T(1,128)} %get-tuple-element.45), kind=kLoop, calls=%fused_computation.155 | loop fusion | flops 288 | bytes 1540 | tf_op jit(solution)/shard_map/div | solution.py:87
  37.6 2.3 %collective-permute-start.13 = (bf16[2,2,96,256]{3,2,0,1:T(8,128)(2,1)S(1)}, bf16[2,2,96,256]{3,2,0,1:T(8,128)(2,1)S(1)}, u32[]{:S(2)}, u32[]{:S(2)}) collective-permute-start(bf16[2,2,96,256]{3,2,0,1:T(8,128)(2,1)S(1)} %fusion.55), channel_id=1, source_target_pairs={{0,4},{1,5},{2,6},{3,7},{4,0},{5,1},{6,2},{7,3},{8,12},{9,13},{10,... | collective-permute-start | bytes 589832 | tf_op jit(solution)/shard_map/ppermute | solution.py:16
  39.9 1.1 bitcast_add_fusion.3
  41.5 4.0 %collective-permute-done.13 = bf16[2,2,96,256]{3,2,0,1:T(8,128)(2,1)S(1)} collective-permute-done((bf16[2,2,96,256]{3,2,0,1:T(8,128)(2,1)S(1)}, bf16[2,2,96,256]{3,2,0,1:T(8,128)(2,1)S(1)}, u32[]{:S(2)}, u32[]{:S(2)}) %collective-permute-start.13) | collective-permute-done | bytes 196640 | tf_op jit(solution)/shard_map/ppermute | solution.py:16
  45.6 1.0 collective-permute-start.14
  46.6 1.6 %collective-permute-done.5 = bf16[2,2,96,256]{3,2,0,1:T(8,128)(2,1)S(1)} collective-permute-done((bf16[2,2,96,256]{3,2,0,1:T(8,128)(2,1)S(1)}, bf16[2,2,96,256]{3,2,0,1:T(8,128)(2,1)S(1)}, u32[]{:S(2)}, u32[]{:S(2)}) %collective-permute-start.5) | collective-permute-done | bytes 196640 | tf_op jit(solution)/shard_map/ppermute | solution.py:16
  48.7 1.6 %collective-permute-done.14 = bf16[2,96,256]{2,1,0:T(8,128)(2,1)S(1)} collective-permute-done((bf16[2,96,256]{2,1,0:T(8,128)(2,1)S(1)}, bf16[2,96,256]{2,1,0:T(8,128)(2,1)S(1)}, u32[]{:S(2)}, u32[]{:S(2)}) %collective-permute-start.14) | collective-permute-done | bytes 98336 | tf_op jit(solution)/shard_map/ppermute | solution.py:16
  50.3 3.3 %collective-permute-start.15 = (bf16[96,256]{1,0:T(8,128)(2,1)S(1)}, bf16[96,256]{1,0:T(8,128)(2,1)S(1)}, u32[]{:S(2)}, u32[]{:S(2)}) collective-permute-start(bf16[96,256]{1,0:T(8,128)(2,1)S(1)} %fusion.63), channel_id=1, source_target_pairs={{0,8},{1,9},{2,10},{3,11},{4,12},{5,13},{6,14},{7,15},{8,0},{9,1},... | collective-permute-start | bytes 147464 | tf_op jit(solution)/shard_map/ppermute | solution.py:16
  53.7 2.8 %collective-permute-start.7 = (bf16[96,256]{1,0:T(8,128)(2,1)S(1)}, bf16[96,256]{1,0:T(8,128)(2,1)S(1)}, u32[]{:S(2)}, u32[]{:S(2)}) collective-permute-start(bf16[96,256]{1,0:T(8,128)(2,1)S(1)} %fusion.62), channel_id=1, source_target_pairs={{0,8},{1,9},{2,10},{3,11},{4,12},{5,13},{6,14},{7,15},{8,0},{9,1},... | collective-permute-start | bytes 147464 | tf_op jit(solution)/shard_map/ppermute | solution.py:16
  56.5 0.8 cosine_bitcast_fusion
  57.3 1.5 %collective-permute-done.7 = bf16[96,256]{1,0:T(8,128)(2,1)S(1)} collective-permute-done((bf16[96,256]{1,0:T(8,128)(2,1)S(1)}, bf16[96,256]{1,0:T(8,128)(2,1)S(1)}, u32[]{:S(2)}, u32[]{:S(2)}) %collective-permute-start.7) | collective-permute-done | bytes 49184 | tf_op jit(solution)/shard_map/ppermute | solution.py:16
  58.9 2.8 %collective-permute-start.16 = (bf16[96,256]{1,0:T(8,128)(2,1)S(1)}, bf16[96,256]{1,0:T(8,128)(2,1)S(1)}, u32[]{:S(2)}, u32[]{:S(2)}) collective-permute-start(bf16[96,256]{1,0:T(8,128)(2,1)S(1)} %get-tuple-element.16), channel_id=1, source_target_pairs={{0,8},{1,9},{2,10},{3,11},{4,12},{5,13},{6,14},{7,15},{8,0},{9,1},... | collective-permute-start | bytes 147464 | tf_op jit(solution)/shard_map/ppermute | solution.py:16
  61.9 2.1 %collective-permute-done.16 = bf16[96,256]{1,0:T(8,128)(2,1)S(1)} collective-permute-done((bf16[96,256]{1,0:T(8,128)(2,1)S(1)}, bf16[96,256]{1,0:T(8,128)(2,1)S(1)}, u32[]{:S(2)}, u32[]{:S(2)}) %collective-permute-start.16) | collective-permute-done | bytes 49184 | tf_op jit(solution)/shard_map/ppermute | solution.py:16
  64.0 1.8 %collective-permute-start.17 = (bf16[2,96,256]{2,1,0:T(8,128)(2,1)S(1)}, bf16[2,96,256]{2,1,0:T(8,128)(2,1)S(1)}, u32[]{:S(2)}, u32[]{:S(2)}) collective-permute-start(bf16[2,96,256]{2,1,0:T(8,128)(2,1)S(1)} %pad_maximum_fusion.14), channel_id=1, source_target_pairs={{0,4},{1,5},{2,6},{3,7},{4,0},{5,1},{6,2},{7,3},{8,12},{9,13},{10,... | collective-permute-start | bytes 294920 | tf_op jit(solution)/shard_map/ppermute | solution.py:16
  65.8 1.2 collective-permute-done.20
  67.0 0.8 collective-permute-start.21
  67.8 0.9 collective-permute-done.17
  69.3 2.6 %collective-permute-done.21 = bf16[2,96,256]{2,1,0:T(8,128)(2,1)S(1)} collective-permute-done((bf16[2,96,256]{2,1,0:T(8,128)(2,1)S(1)}, bf16[2,96,256]{2,1,0:T(8,128)(2,1)S(1)}, u32[]{:S(2)}, u32[]{:S(2)}) %collective-permute-start.21) | collective-permute-done | bytes 98336 | tf_op jit(solution)/shard_map/ppermute | solution.py:16
  71.9 1.3 %collective-permute-start.22 = (bf16[2,2,96,256]{3,2,1,0:T(8,128)(2,1)S(1)}, bf16[2,2,96,256]{3,2,1,0:T(8,128)(2,1)S(1)}, u32[]{:S(2)}, u32[]{:S(2)}) collective-permute-start(bf16[2,2,96,256]{3,2,1,0:T(8,128)(2,1)S(1)} %pad_maximum_fusion.11), channel_id=1, source_target_pairs={{0,4},{1,5},{2,6},{3,7},{4,0},{5,1},{6,2},{7,3},{8,12},{9,13},{10,... | collective-permute-start | bytes 589832 | tf_op jit(solution)/shard_map/ppermute | solution.py:16
  73.2 1.2 collective-permute-done.18
  74.6 3.0 %collective-permute-done.22 = bf16[2,2,96,256]{3,2,1,0:T(8,128)(2,1)S(1)} collective-permute-done((bf16[2,2,96,256]{3,2,1,0:T(8,128)(2,1)S(1)}, bf16[2,2,96,256]{3,2,1,0:T(8,128)(2,1)S(1)}, u32[]{:S(2)}, u32[]{:S(2)}) %collective-permute-start.22) | collective-permute-done | bytes 196640 | tf_op jit(solution)/shard_map/ppermute | solution.py:16
  78.2 1.3 %collective-permute-done.23 = bf16[2,2,2,96,256]{4,3,2,1,0:T(8,128)(2,1)S(1)} collective-permute-done((bf16[2,2,2,96,256]{4,3,2,1,0:T(8,128)(2,1)S(1)}, bf16[2,2,2,96,256]{4,3,2,1,0:T(8,128)(2,1)S(1)}, u32[]{:S(2)}, u32[]{:S(2)}) %collective-permute-start.23) | collective-permute-done | bytes 393248 | tf_op jit(solution)/shard_map/ppermute | solution.py:16
  79.9 0.9 copy.34
  80.9 3.0 %convolution_bitcast_fusion = f32[1536,256]{0,1:T(8,128)S(1)} fusion(bf16[3,512,1536]{2,1,0:T(8,128)(2,1)} %param.5, bf16[1536,256]{1,0:T(8,128)(2,1)S(1)} %bitcast.248, f32[256]{0:T(256)S(1)} %add_rsqrt_fusion.1), kind=kOutput, calls=%fused_computation | convolution fusion | flops 805568512 | bytes 5506048 | tf_op jit(solution)/shard_map/dot_general | solution.py:10
  84.4 0.8 fusion.51
  85.3 4.4 %convolution_bitcast_fusion.1 = f32[1536,256]{0,1:T(8,128)} fusion(bf16[3,512,1536]{2,1,0:T(8,128)(2,1)} %param.5, bf16[1536,256]{1,0:T(8,128)(2,1)} %bitcast.247, f32[256]{0:T(256)} %copy-done.4), kind=kOutput, calls=%fused_computation.1 | convolution fusion | flops 805568512 | bytes 5506048 | tf_op jit(solution)/shard_map/dot_general | solution.py:10
  89.7 1.9 %copy.38 = f32[1536,256]{1,0:T(8,128)S(1)} copy(f32[1536,256]{0,1:T(8,128)} %convolution_bitcast_fusion.1) | data formatting | bytes 3145728 | tf_op jit(solution)/shard_map/dot_general | solution.py:10
  92.4 1.3 %collective-permute-start.29 = (bf16[2,2,96,256]{3,2,0,1:T(8,128)(2,1)S(1)}, bf16[2,2,96,256]{3,2,0,1:T(8,128)(2,1)S(1)}, u32[]{:S(2)}, u32[]{:S(2)}) collective-permute-start(bf16[2,2,96,256]{3,2,0,1:T(8,128)(2,1)S(1)} %fusion.57), channel_id=1, source_target_pairs={{0,4},{1,5},{2,6},{3,7},{4,0},{5,1},{6,2},{7,3},{8,12},{9,13},{10,... | collective-permute-start | bytes 589832 | tf_op jit(solution)/shard_map/ppermute | solution.py:16
  94.3 5.0 %collective-permute-done.29 = bf16[2,2,96,256]{3,2,0,1:T(8,128)(2,1)S(1)} collective-permute-done((bf16[2,2,96,256]{3,2,0,1:T(8,128)(2,1)S(1)}, bf16[2,2,96,256]{3,2,0,1:T(8,128)(2,1)S(1)}, u32[]{:S(2)}, u32[]{:S(2)}) %collective-permute-start.29) | collective-permute-done | bytes 196640 | tf_op jit(solution)/shard_map/ppermute | solution.py:16
  99.4 0.6 collective-permute-start.30
  100.1 0.8 collective-permute-done.25
  100.9 1.3 %collective-permute-start.26 = (bf16[2,96,256]{2,1,0:T(8,128)(2,1)S(1)}, bf16[2,96,256]{2,1,0:T(8,128)(2,1)S(1)}, u32[]{:S(2)}, u32[]{:S(2)}) collective-permute-start(bf16[2,96,256]{2,1,0:T(8,128)(2,1)S(1)} %fusion.60), channel_id=1, source_target_pairs={{0,4},{1,5},{2,6},{3,7},{4,0},{5,1},{6,2},{7,3},{8,12},{9,13},{10,... | collective-permute-start | bytes 294920 | tf_op jit(solution)/shard_map/ppermute | solution.py:16
  102.2 1.9 %collective-permute-done.30 = bf16[2,96,256]{2,1,0:T(8,128)(2,1)S(1)} collective-permute-done((bf16[2,96,256]{2,1,0:T(8,128)(2,1)S(1)}, bf16[2,96,256]{2,1,0:T(8,128)(2,1)S(1)}, u32[]{:S(2)}, u32[]{:S(2)}) %collective-permute-start.30) | collective-permute-done | bytes 98336 | tf_op jit(solution)/shard_map/ppermute | solution.py:16
  104.2 1.8 %collective-permute-start.31 = (bf16[96,256]{1,0:T(8,128)(2,1)S(1)}, bf16[96,256]{1,0:T(8,128)(2,1)S(1)}, u32[]{:S(2)}, u32[]{:S(2)}) collective-permute-start(bf16[96,256]{1,0:T(8,128)(2,1)S(1)} %fusion.65), channel_id=1, source_target_pairs={{0,8},{1,9},{2,10},{3,11},{4,12},{5,13},{6,14},{7,15},{8,0},{9,1},... | collective-permute-start | bytes 147464 | tf_op jit(solution)/shard_map/ppermute | solution.py:16
  106.0 1.8 %collective-permute-start.27 = (bf16[96,256]{1,0:T(8,128)(2,1)S(1)}, bf16[96,256]{1,0:T(8,128)(2,1)S(1)}, u32[]{:S(2)}, u32[]{:S(2)}) collective-permute-start(bf16[96,256]{1,0:T(8,128)(2,1)S(1)} %fusion.64), channel_id=1, source_target_pairs={{0,8},{1,9},{2,10},{3,11},{4,12},{5,13},{6,14},{7,15},{8,0},{9,1},... | collective-permute-start | bytes 147464 | tf_op jit(solution)/shard_map/ppermute | solution.py:16
  108.0 2.2 %collective-permute-done.31 = bf16[96,256]{1,0:T(8,128)(2,1)S(1)} collective-permute-done((bf16[96,256]{1,0:T(8,128)(2,1)S(1)}, bf16[96,256]{1,0:T(8,128)(2,1)S(1)}, u32[]{:S(2)}, u32[]{:S(2)}) %collective-permute-start.31) | collective-permute-done | bytes 49184 | tf_op jit(solution)/shard_map/ppermute | solution.py:16
  110.1 1.0 collective-permute-done.27
  111.3 1.1 collective-permute-done.32
  112.4 1.7 %collective-permute-start.33 = (f32[256]{0:T(256)S(1)}, f32[256]{0:T(256)S(1)}, u32[]{:S(2)}, u32[]{:S(2)}) collective-permute-start(f32[256]{0:T(256)S(1)} %add.187), channel_id=1, source_target_pairs={{0,2},{1,3},{2,0},{3,1},{4,6},{5,7},{6,4},{7,5},{8,10},{9,11},{10,... | collective-permute-start | bytes 3080 | tf_op jit(solution)/shard_map/ppermute | solution.py:16
  114.1 1.9 %collective-permute-done.33 = f32[256]{0:T(256)S(1)} collective-permute-done((f32[256]{0:T(256)S(1)}, f32[256]{0:T(256)S(1)}, u32[]{:S(2)}, u32[]{:S(2)}) %collective-permute-start.33) | collective-permute-done | bytes 1056 | tf_op jit(solution)/shard_map/ppermute | solution.py:16
  116.0 1.1 collective-permute-start.34
  117.1 2.5 %collective-permute-done.34 = f32[256]{0:T(256)S(1)} collective-permute-done((f32[256]{0:T(256)S(1)}, f32[256]{0:T(256)S(1)}, u32[]{:S(2)}, u32[]{:S(2)}) %collective-permute-start.34) | collective-permute-done | bytes 1056 | tf_op jit(solution)/shard_map/ppermute | solution.py:16
  119.6 1.8 %collective-permute-start.35 = (f32[256]{0:T(256)S(1)}, f32[256]{0:T(256)S(1)}, u32[]{:S(2)}, u32[]{:S(2)}) collective-permute-start(f32[256]{0:T(256)S(1)} %add.189), channel_id=1, source_target_pairs={{0,8},{1,9},{2,10},{3,11},{4,12},{5,13},{6,14},{7,15},{8,0},{9,1},... | collective-permute-start | bytes 3080 | tf_op jit(solution)/shard_map/ppermute | solution.py:16
  121.3 2.7 %collective-permute-done.35 = f32[256]{0:T(256)S(1)} collective-permute-done((f32[256]{0:T(256)S(1)}, f32[256]{0:T(256)S(1)}, u32[]{:S(2)}, u32[]{:S(2)}) %collective-permute-start.35) | collective-permute-done | bytes 1056 | tf_op jit(solution)/shard_map/ppermute | solution.py:16
  124.0 0.7 broadcast_multiply_fusion
  (106 shorter events, 7.3 us)
Async XLA Ops:
  0.6 6.9 %collective-permute-start.8 = (bf16[96,256]{1,0:T(8,128)(2,1)}, bf16[96,256]{1,0:T(8,128)(2,1)S(1)}, u32[]{:S(2)}, u32[]{:S(2)}) collective-permute-start(bf16[96,256]{1,0:T(8,128)(2,1)} %param.7), channel_id=1, source_target_pairs={{0,8},{1,9},{2,10},{3,11},{4,12},{5,13},{6,14},{7,15},{8,0},{9,1},... | collective-permute-start | bytes 147464 | tf_op jit(solution)/shard_map/ppermute | solution.py:16
  4.7 5.4 %collective-permute-start = (bf16[96,256]{1,0:T(8,128)(2,1)}, bf16[96,256]{1,0:T(8,128)(2,1)S(1)}, u32[]{:S(2)}, u32[]{:S(2)}) collective-permute-start(bf16[96,256]{1,0:T(8,128)(2,1)} %param.6), channel_id=1, source_target_pairs={{0,8},{1,9},{2,10},{3,11},{4,12},{5,13},{6,14},{7,15},{8,0},{9,1},... | collective-permute-start | bytes 147464 | tf_op jit(solution)/shard_map/ppermute | solution.py:16
  8.4 4.7 %collective-permute-start.9 = (bf16[2,96,256]{2,1,0:T(8,128)(2,1)S(1)}, bf16[2,96,256]{2,1,0:T(8,128)(2,1)S(1)}, u32[]{:S(2)}, u32[]{:S(2)}) collective-permute-start(bf16[2,96,256]{2,1,0:T(8,128)(2,1)S(1)} %pad_maximum_fusion.13), channel_id=1, source_target_pairs={{0,2},{1,3},{2,0},{3,1},{4,6},{5,7},{6,4},{7,5},{8,10},{9,11},{10,... | collective-permute-start | bytes 294920 | tf_op jit(solution)/shard_map/ppermute | solution.py:16
  11.0 9.1 %copy-start = (f32[2,1536]{1,0:T(2,128)S(1)}, f32[2,1536]{1,0:T(2,128)}, u32[]{:S(2)}) copy-start(f32[2,1536]{1,0:T(2,128)} %param.8) | copy-start | bytes 36868
  11.0 9.1 %copy-start.1 = (f32[2,1536]{1,0:T(2,128)S(1)}, f32[2,1536]{1,0:T(2,128)}, u32[]{:S(2)}) copy-start(f32[2,1536]{1,0:T(2,128)} %param.9) | copy-start | bytes 36868
  11.0 5.3 %collective-permute-start.1 = (bf16[2,96,256]{2,1,0:T(8,128)(2,1)S(1)}, bf16[2,96,256]{2,1,0:T(8,128)(2,1)S(1)}, u32[]{:S(2)}, u32[]{:S(2)}) collective-permute-start(bf16[2,96,256]{2,1,0:T(8,128)(2,1)S(1)} %pad_maximum_fusion.12), channel_id=1, source_target_pairs={{0,4},{1,5},{2,6},{3,7},{4,0},{5,1},{6,2},{7,3},{8,12},{9,13},{10,... | collective-permute-start | bytes 294920 | tf_op jit(solution)/shard_map/ppermute | solution.py:16
  13.1 6.8 %collective-permute-start.10 = (bf16[2,2,96,256]{3,2,1,0:T(8,128)(2,1)S(1)}, bf16[2,2,96,256]{3,2,1,0:T(8,128)(2,1)S(1)}, u32[]{:S(2)}, u32[]{:S(2)}) collective-permute-start(bf16[2,2,96,256]{3,2,1,0:T(8,128)(2,1)S(1)} %pad_maximum_fusion.9), channel_id=1, source_target_pairs={{0,4},{1,5},{2,6},{3,7},{4,0},{5,1},{6,2},{7,3},{8,12},{9,13},{10,... | collective-permute-start | bytes 589832 | tf_op jit(solution)/shard_map/ppermute | solution.py:16
  16.4 5.7 %collective-permute-start.2 = (bf16[2,2,96,256]{3,2,0,1:T(8,128)(2,1)S(1)}, bf16[2,2,96,256]{3,2,0,1:T(8,128)(2,1)S(1)}, u32[]{:S(2)}, u32[]{:S(2)}) collective-permute-start(bf16[2,2,96,256]{3,2,0,1:T(8,128)(2,1)S(1)} %pad_maximum_fusion.8), channel_id=1, source_target_pairs={{0,2},{1,3},{2,0},{3,1},{4,6},{5,7},{6,4},{7,5},{8,10},{9,11},{10,... | collective-permute-start | bytes 589832 | tf_op jit(solution)/shard_map/ppermute | solution.py:16
  20.0 3.0 %collective-permute-start.11 = (bf16[2,2,2,96,256]{4,3,2,0,1:T(8,128)(2,1)S(1)}, bf16[2,2,2,96,256]{4,3,2,0,1:T(8,128)(2,1)S(1)}, u32[]{:S(2)}, u32[]{:S(2)}) collective-permute-start(bf16[2,2,2,96,256]{4,3,2,0,1:T(8,128)(2,1)S(1)} %pad_maximum_fusion.5), channel_id=1, source_target_pairs={{0,1},{1,0},{2,3},{3,2},{4,5},{5,4},{6,7},{7,6},{8,9},{9,8},{10,11... | collective-permute-start | bytes 1179656 | tf_op jit(solution)/shard_map/ppermute | solution.py:16
  23.0 5.0 %collective-permute-start.3 = (bf16[2,2,2,96,256]{4,3,2,1,0:T(8,128)(2,1)}, bf16[2,2,2,96,256]{4,3,2,1,0:T(8,128)(2,1)}, u32[]{:S(2)}, u32[]{:S(2)}) collective-permute-start(bf16[2,2,2,96,256]{4,3,2,1,0:T(8,128)(2,1)} %copy.43), channel_id=1, source_target_pairs={{0,1},{1,0},{2,3},{3,2},{4,5},{5,4},{6,7},{7,6},{8,9},{9,8},{10,11... | collective-permute-start | bytes 1179656 | tf_op jit(solution)/shard_map/ppermute | solution.py:16
  27.5 10.0 %collective-permute-start.12 = (bf16[2,2,2,96,256]{4,3,0,2,1:T(8,128)(2,1)}, bf16[2,2,2,96,256]{4,3,0,2,1:T(8,128)(2,1)S(1)}, u32[]{:S(2)}, u32[]{:S(2)}) collective-permute-start(bf16[2,2,2,96,256]{4,3,0,2,1:T(8,128)(2,1)} %fusion.50), channel_id=1, source_target_pairs={{0,1},{1,0},{2,3},{3,2},{4,5},{5,4},{6,7},{7,6},{8,9},{9,8},{10,11... | collective-permute-start | bytes 1179656 | tf_op jit(solution)/shard_map/ppermute | solution.py:16
  36.0 3.9 %collective-permute-start.4 = (bf16[2,2,2,96,256]{4,3,0,1,2:T(8,128)(2,1)}, bf16[2,2,2,96,256]{4,3,0,1,2:T(8,128)(2,1)}, u32[]{:S(2)}, u32[]{:S(2)}) collective-permute-start(bf16[2,2,2,96,256]{4,3,0,1,2:T(8,128)(2,1)} %fusion.49), channel_id=1, source_target_pairs={{0,1},{1,0},{2,3},{3,2},{4,5},{5,4},{6,7},{7,6},{8,9},{9,8},{10,11... | collective-permute-start | bytes 1179656 | tf_op jit(solution)/shard_map/ppermute | solution.py:16
  37.6 7.9 %collective-permute-start.13 = (bf16[2,2,96,256]{3,2,0,1:T(8,128)(2,1)S(1)}, bf16[2,2,96,256]{3,2,0,1:T(8,128)(2,1)S(1)}, u32[]{:S(2)}, u32[]{:S(2)}) collective-permute-start(bf16[2,2,96,256]{3,2,0,1:T(8,128)(2,1)S(1)} %fusion.55), channel_id=1, source_target_pairs={{0,4},{1,5},{2,6},{3,7},{4,0},{5,1},{6,2},{7,3},{8,12},{9,13},{10,... | collective-permute-start | bytes 589832 | tf_op jit(solution)/shard_map/ppermute | solution.py:16
  41.1 17.7 %copy-start.2 = (f32[96]{0:T(128)S(1)}, f32[96]{0:T(128)}, u32[]{:S(2)}) copy-start(f32[96]{0:T(128)} %get-tuple-element.48) | copy-start | bytes 1156
  41.1 17.7 %copy-start.3 = (f32[96]{0:T(128)S(1)}, f32[96]{0:T(128)}, u32[]{:S(2)}) copy-start(f32[96]{0:T(128)} %get-tuple-element.49) | copy-start | bytes 1156
  41.1 7.1 %collective-permute-start.5 = (bf16[2,2,96,256]{3,2,0,1:T(8,128)(2,1)S(1)}, bf16[2,2,96,256]{3,2,0,1:T(8,128)(2,1)S(1)}, u32[]{:S(2)}, u32[]{:S(2)}) collective-permute-start(bf16[2,2,96,256]{3,2,0,1:T(8,128)(2,1)S(1)} %fusion.54), channel_id=1, source_target_pairs={{0,2},{1,3},{2,0},{3,1},{4,6},{5,7},{6,4},{7,5},{8,10},{9,11},{10,... | collective-permute-start | bytes 589832 | tf_op jit(solution)/shard_map/ppermute | solution.py:16
  45.6 4.7 %collective-permute-start.14 = (bf16[2,96,256]{2,1,0:T(8,128)(2,1)S(1)}, bf16[2,96,256]{2,1,0:T(8,128)(2,1)S(1)}, u32[]{:S(2)}, u32[]{:S(2)}) collective-permute-start(bf16[2,96,256]{2,1,0:T(8,128)(2,1)S(1)} %fusion.59), channel_id=1, source_target_pairs={{0,2},{1,3},{2,0},{3,1},{4,6},{5,7},{6,4},{7,5},{8,10},{9,11},{10,... | collective-permute-start | bytes 294920 | tf_op jit(solution)/shard_map/ppermute | solution.py:16
  48.2 5.4 %collective-permute-start.6 = (bf16[2,96,256]{2,1,0:T(8,128)(2,1)S(1)}, bf16[2,96,256]{2,1,0:T(8,128)(2,1)S(1)}, u32[]{:S(2)}, u32[]{:S(2)}) collective-permute-start(bf16[2,96,256]{2,1,0:T(8,128)(2,1)S(1)} %fusion.58), channel_id=1, source_target_pairs={{0,4},{1,5},{2,6},{3,7},{4,0},{5,1},{6,2},{7,3},{8,12},{9,13},{10,... | collective-permute-start | bytes 294920 | tf_op jit(solution)/shard_map/ppermute | solution.py:16
  50.3 7.0 %collective-permute-start.15 = (bf16[96,256]{1,0:T(8,128)(2,1)S(1)}, bf16[96,256]{1,0:T(8,128)(2,1)S(1)}, u32[]{:S(2)}, u32[]{:S(2)}) collective-permute-start(bf16[96,256]{1,0:T(8,128)(2,1)S(1)} %fusion.63), channel_id=1, source_target_pairs={{0,8},{1,9},{2,10},{3,11},{4,12},{5,13},{6,14},{7,15},{8,0},{9,1},... | collective-permute-start | bytes 147464 | tf_op jit(solution)/shard_map/ppermute | solution.py:16
  53.7 5.1 %collective-permute-start.7 = (bf16[96,256]{1,0:T(8,128)(2,1)S(1)}, bf16[96,256]{1,0:T(8,128)(2,1)S(1)}, u32[]{:S(2)}, u32[]{:S(2)}) collective-permute-start(bf16[96,256]{1,0:T(8,128)(2,1)S(1)} %fusion.62), channel_id=1, source_target_pairs={{0,8},{1,9},{2,10},{3,11},{4,12},{5,13},{6,14},{7,15},{8,0},{9,1},... | collective-permute-start | bytes 147464 | tf_op jit(solution)/shard_map/ppermute | solution.py:16
  58.9 5.1 %collective-permute-start.16 = (bf16[96,256]{1,0:T(8,128)(2,1)S(1)}, bf16[96,256]{1,0:T(8,128)(2,1)S(1)}, u32[]{:S(2)}, u32[]{:S(2)}) collective-permute-start(bf16[96,256]{1,0:T(8,128)(2,1)S(1)} %get-tuple-element.16), channel_id=1, source_target_pairs={{0,8},{1,9},{2,10},{3,11},{4,12},{5,13},{6,14},{7,15},{8,0},{9,1},... | collective-permute-start | bytes 147464 | tf_op jit(solution)/shard_map/ppermute | solution.py:16
  61.7 5.3 %collective-permute-start.20 = (bf16[96,256]{1,0:T(8,128)(2,1)S(1)}, bf16[96,256]{1,0:T(8,128)(2,1)S(1)}, u32[]{:S(2)}, u32[]{:S(2)}) collective-permute-start(bf16[96,256]{1,0:T(8,128)(2,1)S(1)} %get-tuple-element.17), channel_id=1, source_target_pairs={{0,8},{1,9},{2,10},{3,11},{4,12},{5,13},{6,14},{7,15},{8,0},{9,1},... | collective-permute-start | bytes 147464 | tf_op jit(solution)/shard_map/ppermute | solution.py:16
  64.0 4.7 %collective-permute-start.17 = (bf16[2,96,256]{2,1,0:T(8,128)(2,1)S(1)}, bf16[2,96,256]{2,1,0:T(8,128)(2,1)S(1)}, u32[]{:S(2)}, u32[]{:S(2)}) collective-permute-start(bf16[2,96,256]{2,1,0:T(8,128)(2,1)S(1)} %pad_maximum_fusion.14), channel_id=1, source_target_pairs={{0,4},{1,5},{2,6},{3,7},{4,0},{5,1},{6,2},{7,3},{8,12},{9,13},{10,... | collective-permute-start | bytes 294920 | tf_op jit(solution)/shard_map/ppermute | solution.py:16
  67.0 4.8 %collective-permute-start.21 = (bf16[2,96,256]{2,1,0:T(8,128)(2,1)S(1)}, bf16[2,96,256]{2,1,0:T(8,128)(2,1)S(1)}, u32[]{:S(2)}, u32[]{:S(2)}) collective-permute-start(bf16[2,96,256]{2,1,0:T(8,128)(2,1)S(1)} %pad_maximum_fusion.15), channel_id=1, source_target_pairs={{0,2},{1,3},{2,0},{3,1},{4,6},{5,7},{6,4},{7,5},{8,10},{9,11},{10,... | collective-permute-start | bytes 294920 | tf_op jit(solution)/shard_map/ppermute | solution.py:16
  68.7 5.7 %collective-permute-start.18 = (bf16[2,2,96,256]{3,2,0,1:T(8,128)(2,1)S(1)}, bf16[2,2,96,256]{3,2,0,1:T(8,128)(2,1)S(1)}, u32[]{:S(2)}, u32[]{:S(2)}) collective-permute-start(bf16[2,2,96,256]{3,2,0,1:T(8,128)(2,1)S(1)} %pad_maximum_fusion.10), channel_id=1, source_target_pairs={{0,2},{1,3},{2,0},{3,1},{4,6},{5,7},{6,4},{7,5},{8,10},{9,11},{10,... | collective-permute-start | bytes 589832 | tf_op jit(solution)/shard_map/ppermute | solution.py:16
  71.9 5.7 %collective-permute-start.22 = (bf16[2,2,96,256]{3,2,1,0:T(8,128)(2,1)S(1)}, bf16[2,2,96,256]{3,2,1,0:T(8,128)(2,1)S(1)}, u32[]{:S(2)}, u32[]{:S(2)}) collective-permute-start(bf16[2,2,96,256]{3,2,1,0:T(8,128)(2,1)S(1)} %pad_maximum_fusion.11), channel_id=1, source_target_pairs={{0,4},{1,5},{2,6},{3,7},{4,0},{5,1},{6,2},{7,3},{8,12},{9,13},{10,... | collective-permute-start | bytes 589832 | tf_op jit(solution)/shard_map/ppermute | solution.py:16
  74.5 3.3 %collective-permute-start.19 = (bf16[2,2,2,96,256]{4,3,0,1,2:T(8,128)(2,1)S(1)}, bf16[2,2,2,96,256]{4,3,0,1,2:T(8,128)(2,1)S(1)}, u32[]{:S(2)}, u32[]{:S(2)}) collective-permute-start(bf16[2,2,2,96,256]{4,3,0,1,2:T(8,128)(2,1)S(1)} %pad_maximum_fusion.6), channel_id=1, source_target_pairs={{0,1},{1,0},{2,3},{3,2},{4,5},{5,4},{6,7},{7,6},{8,9},{9,8},{10,11... | collective-permute-start | bytes 1179656 | tf_op jit(solution)/shard_map/ppermute | solution.py:16
  77.7 1.8 %collective-permute-start.23 = (bf16[2,2,2,96,256]{4,3,2,1,0:T(8,128)(2,1)S(1)}, bf16[2,2,2,96,256]{4,3,2,1,0:T(8,128)(2,1)S(1)}, u32[]{:S(2)}, u32[]{:S(2)}) collective-permute-start(bf16[2,2,2,96,256]{4,3,2,1,0:T(8,128)(2,1)S(1)} %pad_maximum_fusion.7), channel_id=1, source_target_pairs={{0,1},{1,0},{2,3},{3,2},{4,5},{5,4},{6,7},{7,6},{8,9},{9,8},{10,11... | collective-permute-start | bytes 1179656 | tf_op jit(solution)/shard_map/ppermute | solution.py:16
  80.9 3.0 %copy-start.4 = (f32[256]{0:T(256)}, f32[256]{0:T(256)S(1)}, u32[]{:S(2)}) copy-start(f32[256]{0:T(256)S(1)} %add_rsqrt_fusion.1) | copy-start | bytes 3076
  85.2 7.0 %collective-permute-start.28 = (bf16[2,2,2,96,256]{4,3,0,2,1:T(8,128)(2,1)}, bf16[2,2,2,96,256]{4,3,0,2,1:T(8,128)(2,1)S(1)}, u32[]{:S(2)}, u32[]{:S(2)}) collective-permute-start(bf16[2,2,2,96,256]{4,3,0,2,1:T(8,128)(2,1)} %fusion.51), channel_id=1, source_target_pairs={{0,1},{1,0},{2,3},{3,2},{4,5},{5,4},{6,7},{7,6},{8,9},{9,8},{10,11... | collective-permute-start | bytes 1179656 | tf_op jit(solution)/shard_map/ppermute | solution.py:16
  91.6 2.0 %collective-permute-start.24 = (bf16[2,2,2,96,256]{4,3,2,1,0:T(8,128)(2,1)S(1)}, bf16[2,2,2,96,256]{4,3,2,1,0:T(8,128)(2,1)S(1)}, u32[]{:S(2)}, u32[]{:S(2)}) collective-permute-start(bf16[2,2,2,96,256]{4,3,2,1,0:T(8,128)(2,1)S(1)} %fusion.48), channel_id=1, source_target_pairs={{0,1},{1,0},{2,3},{3,2},{4,5},{5,4},{6,7},{7,6},{8,9},{9,8},{10,11... | collective-permute-start | bytes 1179656 | tf_op jit(solution)/shard_map/ppermute | solution.py:16
  92.4 7.0 %collective-permute-start.29 = (bf16[2,2,96,256]{3,2,0,1:T(8,128)(2,1)S(1)}, bf16[2,2,96,256]{3,2,0,1:T(8,128)(2,1)S(1)}, u32[]{:S(2)}, u32[]{:S(2)}) collective-permute-start(bf16[2,2,96,256]{3,2,0,1:T(8,128)(2,1)S(1)} %fusion.57), channel_id=1, source_target_pairs={{0,4},{1,5},{2,6},{3,7},{4,0},{5,1},{6,2},{7,3},{8,12},{9,13},{10,... | collective-permute-start | bytes 589832 | tf_op jit(solution)/shard_map/ppermute | solution.py:16
  93.8 7.0 %collective-permute-start.25 = (bf16[2,2,96,256]{3,2,1,0:T(8,128)(2,1)S(1)}, bf16[2,2,96,256]{3,2,1,0:T(8,128)(2,1)S(1)}, u32[]{:S(2)}, u32[]{:S(2)}) collective-permute-start(bf16[2,2,96,256]{3,2,1,0:T(8,128)(2,1)S(1)} %fusion.56), channel_id=1, source_target_pairs={{0,2},{1,3},{2,0},{3,1},{4,6},{5,7},{6,4},{7,5},{8,10},{9,11},{10,... | collective-permute-start | bytes 589832 | tf_op jit(solution)/shard_map/ppermute | solution.py:16
  99.4 4.7 %collective-permute-start.30 = (bf16[2,96,256]{2,1,0:T(8,128)(2,1)S(1)}, bf16[2,96,256]{2,1,0:T(8,128)(2,1)S(1)}, u32[]{:S(2)}, u32[]{:S(2)}) collective-permute-start(bf16[2,96,256]{2,1,0:T(8,128)(2,1)S(1)} %fusion.61), channel_id=1, source_target_pairs={{0,2},{1,3},{2,0},{3,1},{4,6},{5,7},{6,4},{7,5},{8,10},{9,11},{10,... | collective-permute-start | bytes 294920 | tf_op jit(solution)/shard_map/ppermute | solution.py:16
  100.9 5.0 %collective-permute-start.26 = (bf16[2,96,256]{2,1,0:T(8,128)(2,1)S(1)}, bf16[2,96,256]{2,1,0:T(8,128)(2,1)S(1)}, u32[]{:S(2)}, u32[]{:S(2)}) collective-permute-start(bf16[2,96,256]{2,1,0:T(8,128)(2,1)S(1)} %fusion.60), channel_id=1, source_target_pairs={{0,4},{1,5},{2,6},{3,7},{4,0},{5,1},{6,2},{7,3},{8,12},{9,13},{10,... | collective-permute-start | bytes 294920 | tf_op jit(solution)/shard_map/ppermute | solution.py:16
  104.2 6.0 %collective-permute-start.31 = (bf16[96,256]{1,0:T(8,128)(2,1)S(1)}, bf16[96,256]{1,0:T(8,128)(2,1)S(1)}, u32[]{:S(2)}, u32[]{:S(2)}) collective-permute-start(bf16[96,256]{1,0:T(8,128)(2,1)S(1)} %fusion.65), channel_id=1, source_target_pairs={{0,8},{1,9},{2,10},{3,11},{4,12},{5,13},{6,14},{7,15},{8,0},{9,1},... | collective-permute-start | bytes 147464 | tf_op jit(solution)/shard_map/ppermute | solution.py:16
  106.0 5.1 %collective-permute-start.27 = (bf16[96,256]{1,0:T(8,128)(2,1)S(1)}, bf16[96,256]{1,0:T(8,128)(2,1)S(1)}, u32[]{:S(2)}, u32[]{:S(2)}) collective-permute-start(bf16[96,256]{1,0:T(8,128)(2,1)S(1)} %fusion.64), channel_id=1, source_target_pairs={{0,8},{1,9},{2,10},{3,11},{4,12},{5,13},{6,14},{7,15},{8,0},{9,1},... | collective-permute-start | bytes 147464 | tf_op jit(solution)/shard_map/ppermute | solution.py:16
  111.2 1.2 collective-permute-start.32
  112.4 3.6 %collective-permute-start.33 = (f32[256]{0:T(256)S(1)}, f32[256]{0:T(256)S(1)}, u32[]{:S(2)}, u32[]{:S(2)}) collective-permute-start(f32[256]{0:T(256)S(1)} %add.187), channel_id=1, source_target_pairs={{0,2},{1,3},{2,0},{3,1},{4,6},{5,7},{6,4},{7,5},{8,10},{9,11},{10,... | collective-permute-start | bytes 3080 | tf_op jit(solution)/shard_map/ppermute | solution.py:16
  116.0 3.6 %collective-permute-start.34 = (f32[256]{0:T(256)S(1)}, f32[256]{0:T(256)S(1)}, u32[]{:S(2)}, u32[]{:S(2)}) collective-permute-start(f32[256]{0:T(256)S(1)} %add.188), channel_id=1, source_target_pairs={{0,4},{1,5},{2,6},{3,7},{4,0},{5,1},{6,2},{7,3},{8,12},{9,13},{10,... | collective-permute-start | bytes 3080 | tf_op jit(solution)/shard_map/ppermute | solution.py:16
  119.6 4.5 %collective-permute-start.35 = (f32[256]{0:T(256)S(1)}, f32[256]{0:T(256)S(1)}, u32[]{:S(2)}, u32[]{:S(2)}) collective-permute-start(f32[256]{0:T(256)S(1)} %add.189), channel_id=1, source_target_pairs={{0,8},{1,9},{2,10},{3,11},{4,12},{5,13},{6,14},{7,15},{8,0},{9,1},... | collective-permute-start | bytes 3080 | tf_op jit(solution)/shard_map/ppermute | solution.py:16

commit v10 on v9

--- a/solution.py
+++ b/solution.py
@@ -31,19 +31,22 @@
     return cur
 
 
-def doubling_all_gather(x, devices, order):
+def doubling_all_gather(x, devices, order, carry=None):
     me = lax.axis_index("row")
     cur = x
     done = []
     for bit in order:
         other = exchange(cur, 1 << bit, devices)
+        if carry is not None:
+            other, carry = lax.optimization_barrier((other, carry))
         low = (me >> bit) & 1 == 0
         axis = sum(1 for b in done if b > bit)
         done.append(bit)
         cur = jnp.stack(
             [jnp.where(low, cur, other), jnp.where(low, other, cur)], axis=axis
         )
-    return cur.reshape((-1, x.shape[-1]))
+    result = cur.reshape((-1, x.shape[-1]))
+    return result if carry is None else (result, carry)
 
 
 def doubling_all_reduce(x, devices):
@@ -67,7 +70,17 @@
     all_channels = chan_rows * devices
     first_row = lax.axis_index("row") * chan_rows
     order_amp, order_der = stage_orders(devices)
-    amp_full = doubling_all_gather(first_f, devices, order_amp[::-1])
+    coefficients = []
+    for sector in range(SECTORS):
+        angle_rows = lax.dynamic_slice_in_dim(phase[sector], first_row, chan_rows, 0)
+        wave_rows = lax.dynamic_slice_in_dim(wavenum[sector], first_row, chan_rows, 0)
+        cosine = jnp.cos(angle_rows)[:, None]
+        sine = jnp.sin(angle_rows)[:, None]
+        wave = wave_rows[:, None]
+        coefficients.append((cosine, sine / wave, -wave * sine))
+    amp_full, coefficients = doubling_all_gather(
+        first_f, devices, order_amp[::-1], carry=coefficients
+    )
     der_full = doubling_all_gather(first_g, devices, order_der[::-1])
     scale = None
     for sector in range(SECTORS):
@@ -79,13 +92,9 @@
             halves.append(contract_rows(panels[sector + 1], projected.astype(jnp.bfloat16)))
         rot_amp = halving_reduce_scatter(halves[0], devices, order_amp)
         rot_der = halving_reduce_scatter(halves[1], devices, order_der)
-        angle_rows = lax.dynamic_slice_in_dim(phase[sector], first_row, chan_rows, 0)
-        wave_rows = lax.dynamic_slice_in_dim(wavenum[sector], first_row, chan_rows, 0)
-        cosine = jnp.cos(angle_rows)[:, None]
-        sine = jnp.sin(angle_rows)[:, None]
-        wave = wave_rows[:, None]
-        new_amp = cosine * rot_amp + sine / wave * rot_der
-        new_der = -wave * sine * rot_amp + cosine * rot_der
+        cosine, sine_over_wave, minus_wave_sine = coefficients[sector]
+        new_amp = cosine * rot_amp + sine_over_wave * rot_der
+        new_der = minus_wave_sine * rot_amp + cosine * rot_der
         if sector + 1 < SECTORS:
             amp_full = doubling_all_gather(new_amp.astype(jnp.bfloat16), devices, order_amp[::-1])
             der_full = doubling_all_gather(new_der.astype(jnp.bfloat16), devices, order_der[::-1])

time: 125 us -> 126 us (level)
  waiting for transfers between devices: 47.3 us -> 42.4 us
  starting transfers between devices: 42.7 us -> 46.8 us
    ppermute x36, waiting for transfers between devices: 47.3 us -> 42.4 us  [exchange(): return lax.ppermute(x, 'row', [(i, i ^ distance) for i in range(devices)])]
    ppermute x36, starting transfers between devices: 42.7 us -> 46.8 us  [exchange(): return lax.ppermute(x, 'row', [(i, i ^ distance) for i in range(devices)])]
    dot_general x4, local copies, waits for them, and re-layouts: 4.68 us -> 6.08 us  [contract_rows(): lax.dot_general(left, right, (((0,), (0,)), ((), ())), preferred_element_...]
    div x1 -> x0, other arithmetic: 1.41 us -> none  [shards(): new_amp = cosine * rot_amp + sine / wave * rot_der]
  transfers between devices with their start and end apart: 36 -> 36, of which waited for: 24 -> 24; matrix products, arithmetic and copies ran while one was open for 22% -> 21% of each run, Pallas kernels for 0% -> 0%
where the time goes in v10:
time: 126 us; the launch traced here: 125 us
  starting transfers between devices  46.8 us (37%)
  waiting for transfers between devices  42.4 us (34%)
  matrix products  15.5 us (12%)
  local copies, waits for them, and re-layouts  11.9 us (9%)
  other arithmetic  7.42 us (6%)
    ppermute x36, starting transfers between devices, exchange(): return lax.ppermute(x, 'row', [(i, i ^ distance) for i in range(devices)])  46.8 us
    ppermute x36, waiting for transfers between devices, exchange(): return lax.ppermute(x, 'row', [(i, i ^ distance) for i in range(devices)])  42.4 us
    dot_general x4, matrix products, contract_rows(): lax.dot_general(left, right, (((0,), (0,)), ((), ())), preferred_element_...  15.5 us
    dot_general x4, local copies, waits for them, and re-layouts, contract_rows(): lax.dot_general(left, right, (((0,), (0,)), ((), ())), preferred_element_...  6.08 us
    another operation x32, other arithmetic, doubling_all_gather(): jnp.stack([jnp.where(low, cur, other), jnp.where(low, other, cur)], axis=...  3.75 us
    convert_element_type x16, local copies, waits for them, and re-layouts, halving_reduce_scatter(): send.astype(jnp.bfloat16)  2.69 us
  transfers between devices with their start and end apart: 36, of which 24 were waited for; matrix products, arithmetic and copies ran while one was open for 21% of the time, Pallas kernels for 0%

profile of v10, /device:TPU:0, one launch (start us, length us, event | category | flops | bytes accessed | tf_op | source)
XLA Modules:
  0.0 125.2 jit_solution(5054457224456882011)
XLA Ops:
  0.6 4.1 %collective-permute-start.8 = (bf16[96,256]{1,0:T(8,128)(2,1)}, bf16[96,256]{1,0:T(8,128)(2,1)S(1)}, u32[]{:S(2)}, u32[]{:S(2)}) collective-permute-start(bf16[96,256]{1,0:T(8,128)(2,1)} %param.7), channel_id=1, source_target_pairs={{0,8},{1,9},{2,10},{3,11},{4,12},{5,13},{6,14},{7,15},{8,0},{9,1},... | collective-permute-start | bytes 147464 | tf_op jit(solution)/shard_map/ppermute | solution.py:16
  4.8 0.8 fusion.71
  5.6 0.8 fusion.70
  6.4 0.6 bitcast_multiply_fusion
  7.0 0.6 cosine_bitcast_fusion
  7.7 0.8 select_bitcast_fusion.29
  8.5 1.8 %collective-permute-start.9 = (bf16[2,96,256]{2,1,0:T(8,128)(2,1)S(1)}, bf16[2,96,256]{2,1,0:T(8,128)(2,1)S(1)}, u32[]{:S(2)}, u32[]{:S(2)}) collective-permute-start(bf16[2,96,256]{2,1,0:T(8,128)(2,1)S(1)} %pad_maximum_fusion.13), channel_id=1, source_target_pairs={{0,2},{1,3},{2,0},{3,1},{4,6},{5,7},{6,4},{7,5},{8,10},{9,11},{10,... | collective-permute-start | bytes 294920 | tf_op jit(solution)/shard_map/ppermute | solution.py:16
  10.3 0.8 select_bitcast_fusion.31
  11.2 1.8 %collective-permute-start.1 = (bf16[2,96,256]{2,1,0:T(8,128)(2,1)S(1)}, bf16[2,96,256]{2,1,0:T(8,128)(2,1)S(1)}, u32[]{:S(2)}, u32[]{:S(2)}) collective-permute-start(bf16[2,96,256]{2,1,0:T(8,128)(2,1)S(1)} %pad_maximum_fusion.12), channel_id=1, source_target_pairs={{0,4},{1,5},{2,6},{3,7},{4,0},{5,1},{6,2},{7,3},{8,12},{9,13},{10,... | collective-permute-start | bytes 294920 | tf_op jit(solution)/shard_map/ppermute | solution.py:16
  13.2 2.1 %collective-permute-start.10 = (bf16[2,2,96,256]{3,2,1,0:T(8,128)(2,1)S(1)}, bf16[2,2,96,256]{3,2,1,0:T(8,128)(2,1)S(1)}, u32[]{:S(2)}, u32[]{:S(2)}) collective-permute-start(bf16[2,2,96,256]{3,2,1,0:T(8,128)(2,1)S(1)} %pad_maximum_fusion.9), channel_id=1, source_target_pairs={{0,4},{1,5},{2,6},{3,7},{4,0},{5,1},{6,2},{7,3},{8,12},{9,13},{10,... | collective-permute-start | bytes 589832 | tf_op jit(solution)/shard_map/ppermute | solution.py:16
  15.3 1.3 %collective-permute-done.1 = bf16[2,96,256]{2,1,0:T(8,128)(2,1)S(1)} collective-permute-done((bf16[2,96,256]{2,1,0:T(8,128)(2,1)S(1)}, bf16[2,96,256]{2,1,0:T(8,128)(2,1)S(1)}, u32[]{:S(2)}, u32[]{:S(2)}) %collective-permute-start.1) | collective-permute-done | bytes 98336 | tf_op jit(solution)/shard_map/ppermute | solution.py:16
  16.7 1.2 collective-permute-start.2
  17.9 2.2 %collective-permute-done.10 = bf16[2,2,96,256]{3,2,1,0:T(8,128)(2,1)S(1)} collective-permute-done((bf16[2,2,96,256]{3,2,1,0:T(8,128)(2,1)S(1)}, bf16[2,2,96,256]{3,2,1,0:T(8,128)(2,1)S(1)}, u32[]{:S(2)}, u32[]{:S(2)}) %collective-permute-start.10) | collective-permute-done | bytes 196640 | tf_op jit(solution)/shard_map/ppermute | solution.py:16
  20.2 2.2 %collective-permute-done.2 = bf16[2,2,96,256]{3,2,0,1:T(8,128)(2,1)S(1)} collective-permute-done((bf16[2,2,96,256]{3,2,0,1:T(8,128)(2,1)S(1)}, bf16[2,2,96,256]{3,2,0,1:T(8,128)(2,1)S(1)}, u32[]{:S(2)}, u32[]{:S(2)}) %collective-permute-start.2) | collective-permute-done | bytes 196640 | tf_op jit(solution)/shard_map/ppermute | solution.py:16
  22.5 0.8 copy.43
  23.5 3.0 %convolution_bitcast_fusion.2 = f32[1536,256]{0,1:T(8,128)S(1)} fusion(bf16[1536,256]{1,0:T(8,128)(2,1)S(1)} %bitcast.256, bf16[3,512,1536]{2,1,0:T(8,128)(2,1)} %param.5), kind=kOutput, calls=%fused_computation.2 | convolution fusion | flops 805437440 | bytes 5505024 | tf_op jit(solution)/shard_map/dot_general | solution.py:10
  26.9 0.8 fusion.50
  28.2 1.2 select_bitcast_fusion.7
  29.4 4.2 %convolution_bitcast_fusion.3 = f32[1536,256]{0,1:T(8,128)} fusion(bf16[1536,256]{1,0:T(8,128)(2,1)S(1)} %bitcast.254, bf16[3,512,1536]{2,1,0:T(8,128)(2,1)} %param.5), kind=kOutput, calls=%fused_computation.3 | convolution fusion | flops 805437440 | bytes 5505024 | tf_op jit(solution)/shard_map/dot_general | solution.py:10
  33.6 1.9 %copy.22 = f32[1536,256]{1,0:T(8,128)S(1)} copy(f32[1536,256]{0,1:T(8,128)} %convolution_bitcast_fusion.3) | data formatting | bytes 3145728 | tf_op jit(solution)/shard_map/dot_general | solution.py:10
  35.5 0.8 fusion.49
  36.4 2.0 %collective-permute-start.13 = (bf16[2,2,96,256]{3,2,0,1:T(8,128)(2,1)S(1)}, bf16[2,2,96,256]{3,2,0,1:T(8,128)(2,1)S(1)}, u32[]{:S(2)}, u32[]{:S(2)}) collective-permute-start(bf16[2,2,96,256]{3,2,0,1:T(8,128)(2,1)S(1)} %fusion.55), channel_id=1, source_target_pairs={{0,4},{1,5},{2,6},{3,7},{4,0},{5,1},{6,2},{7,3},{8,12},{9,13},{10,... | collective-permute-start | bytes 589832 | tf_op jit(solution)/shard_map/ppermute | solution.py:16
  38.5 1.1 bitcast_add_fusion.3
  39.6 1.1 collective-permute-start.5
  40.7 3.4 %collective-permute-done.13 = bf16[2,2,96,256]{3,2,0,1:T(8,128)(2,1)S(1)} collective-permute-done((bf16[2,2,96,256]{3,2,0,1:T(8,128)(2,1)S(1)}, bf16[2,2,96,256]{3,2,0,1:T(8,128)(2,1)S(1)}, u32[]{:S(2)}, u32[]{:S(2)}) %collective-permute-start.13) | collective-permute-done | bytes 196640 | tf_op jit(solution)/shard_map/ppermute | solution.py:16
  44.1 1.0 collective-permute-start.14
  45.1 1.6 %collective-permute-done.5 = bf16[2,2,96,256]{3,2,0,1:T(8,128)(2,1)S(1)} collective-permute-done((bf16[2,2,96,256]{3,2,0,1:T(8,128)(2,1)S(1)}, bf16[2,2,96,256]{3,2,0,1:T(8,128)(2,1)S(1)}, u32[]{:S(2)}, u32[]{:S(2)}) %collective-permute-start.5) | collective-permute-done | bytes 196640 | tf_op jit(solution)/shard_map/ppermute | solution.py:16
  46.8 2.0 %collective-permute-start.6 = (bf16[2,96,256]{2,1,0:T(8,128)(2,1)S(1)}, bf16[2,96,256]{2,1,0:T(8,128)(2,1)S(1)}, u32[]{:S(2)}, u32[]{:S(2)}) collective-permute-start(bf16[2,96,256]{2,1,0:T(8,128)(2,1)S(1)} %fusion.58), channel_id=1, source_target_pairs={{0,4},{1,5},{2,6},{3,7},{4,0},{5,1},{6,2},{7,3},{8,12},{9,13},{10,... | collective-permute-start | bytes 294920 | tf_op jit(solution)/shard_map/ppermute | solution.py:16
  48.9 3.3 %collective-permute-start.15 = (bf16[96,256]{1,0:T(8,128)(2,1)S(1)}, bf16[96,256]{1,0:T(8,128)(2,1)S(1)}, u32[]{:S(2)}, u32[]{:S(2)}) collective-permute-start(bf16[96,256]{1,0:T(8,128)(2,1)S(1)} %fusion.63), channel_id=1, source_target_pairs={{0,8},{1,9},{2,10},{3,11},{4,12},{5,13},{6,14},{7,15},{8,0},{9,1},... | collective-permute-start | bytes 147464 | tf_op jit(solution)/shard_map/ppermute | solution.py:16
  52.2 3.0 %collective-permute-start.7 = (bf16[96,256]{1,0:T(8,128)(2,1)S(1)}, bf16[96,256]{1,0:T(8,128)(2,1)S(1)}, u32[]{:S(2)}, u32[]{:S(2)}) collective-permute-start(bf16[96,256]{1,0:T(8,128)(2,1)S(1)} %fusion.62), channel_id=1, source_target_pairs={{0,8},{1,9},{2,10},{3,11},{4,12},{5,13},{6,14},{7,15},{8,0},{9,1},... | collective-permute-start | bytes 147464 | tf_op jit(solution)/shard_map/ppermute | solution.py:16
  55.3 2.1 %collective-permute-done.7 = bf16[96,256]{1,0:T(8,128)(2,1)S(1)} collective-permute-done((bf16[96,256]{1,0:T(8,128)(2,1)S(1)}, bf16[96,256]{1,0:T(8,128)(2,1)S(1)}, u32[]{:S(2)}, u32[]{:S(2)}) %collective-permute-start.7) | collective-permute-done | bytes 49184 | tf_op jit(solution)/shard_map/ppermute | solution.py:16
  57.4 3.0 %collective-permute-start.16 = (bf16[96,256]{1,0:T(8,128)(2,1)S(1)}, bf16[96,256]{1,0:T(8,128)(2,1)S(1)}, u32[]{:S(2)}, u32[]{:S(2)}) collective-permute-start(bf16[96,256]{1,0:T(8,128)(2,1)S(1)} %get-tuple-element.72), channel_id=1, source_target_pairs={{0,8},{1,9},{2,10},{3,11},{4,12},{5,13},{6,14},{7,15},{8,0},{9,1},... | collective-permute-start | bytes 147464 | tf_op jit(solution)/shard_map/ppermute | solution.py:16
  60.5 2.0 %collective-permute-done.16 = bf16[96,256]{1,0:T(8,128)(2,1)S(1)} collective-permute-done((bf16[96,256]{1,0:T(8,128)(2,1)S(1)}, bf16[96,256]{1,0:T(8,128)(2,1)S(1)}, u32[]{:S(2)}, u32[]{:S(2)}) %collective-permute-start.16) | collective-permute-done | bytes 49184 | tf_op jit(solution)/shard_map/ppermute | solution.py:16
  62.6 2.2 %collective-permute-start.17 = (bf16[2,96,256]{2,1,0:T(8,128)(2,1)S(1)}, bf16[2,96,256]{2,1,0:T(8,128)(2,1)S(1)}, u32[]{:S(2)}, u32[]{:S(2)}) collective-permute-start(bf16[2,96,256]{2,1,0:T(8,128)(2,1)S(1)} %pad_maximum_fusion.14), channel_id=1, source_target_pairs={{0,4},{1,5},{2,6},{3,7},{4,0},{5,1},{6,2},{7,3},{8,12},{9,13},{10,... | collective-permute-start | bytes 294920 | tf_op jit(solution)/shard_map/ppermute | solution.py:16
  64.8 0.7 collective-permute-done.20
  66.0 1.4 %collective-permute-done.17 = bf16[2,96,256]{2,1,0:T(8,128)(2,1)S(1)} collective-permute-done((bf16[2,96,256]{2,1,0:T(8,128)(2,1)S(1)}, bf16[2,96,256]{2,1,0:T(8,128)(2,1)S(1)}, u32[]{:S(2)}, u32[]{:S(2)}) %collective-permute-start.17) | collective-permute-done | bytes 98336 | tf_op jit(solution)/shard_map/ppermute | solution.py:16
  67.9 2.3 %collective-permute-done.21 = bf16[2,96,256]{2,1,0:T(8,128)(2,1)S(1)} collective-permute-done((bf16[2,96,256]{2,1,0:T(8,128)(2,1)S(1)}, bf16[2,96,256]{2,1,0:T(8,128)(2,1)S(1)}, u32[]{:S(2)}, u32[]{:S(2)}) %collective-permute-start.21) | collective-permute-done | bytes 98336 | tf_op jit(solution)/shard_map/ppermute | solution.py:16
  70.2 2.0 %collective-permute-start.22 = (bf16[2,2,96,256]{3,2,1,0:T(8,128)(2,1)S(1)}, bf16[2,2,96,256]{3,2,1,0:T(8,128)(2,1)S(1)}, u32[]{:S(2)}, u32[]{:S(2)}) collective-permute-start(bf16[2,2,96,256]{3,2,1,0:T(8,128)(2,1)S(1)} %pad_maximum_fusion.11), channel_id=1, source_target_pairs={{0,4},{1,5},{2,6},{3,7},{4,0},{5,1},{6,2},{7,3},{8,12},{9,13},{10,... | collective-permute-start | bytes 589832 | tf_op jit(solution)/shard_map/ppermute | solution.py:16
  72.2 0.9 collective-permute-done.18
  73.3 2.6 %collective-permute-done.22 = bf16[2,2,96,256]{3,2,1,0:T(8,128)(2,1)S(1)} collective-permute-done((bf16[2,2,96,256]{3,2,1,0:T(8,128)(2,1)S(1)}, bf16[2,2,96,256]{3,2,1,0:T(8,128)(2,1)S(1)}, u32[]{:S(2)}, u32[]{:S(2)}) %collective-permute-start.22) | collective-permute-done | bytes 196640 | tf_op jit(solution)/shard_map/ppermute | solution.py:16
  76.5 1.3 %collective-permute-done.23 = bf16[2,2,2,96,256]{4,3,2,1,0:T(8,128)(2,1)S(1)} collective-permute-done((bf16[2,2,2,96,256]{4,3,2,1,0:T(8,128)(2,1)S(1)}, bf16[2,2,2,96,256]{4,3,2,1,0:T(8,128)(2,1)S(1)}, u32[]{:S(2)}, u32[]{:S(2)}) %collective-permute-start.23) | collective-permute-done | bytes 393248 | tf_op jit(solution)/shard_map/ppermute | solution.py:16
  78.3 4.2 %convolution_bitcast_fusion.1 = f32[1536,256]{0,1:T(8,128)} fusion(bf16[3,512,1536]{2,1,0:T(8,128)(2,1)} %param.5, bf16[1536,256]{1,0:T(8,128)(2,1)S(1)} %bitcast.253, f32[256]{0:T(256)S(1)} %add_rsqrt_fusion.1), kind=kOutput, calls=%fused_computation.1 | convolution fusion | flops 805568512 | bytes 5506048 | tf_op jit(solution)/shard_map/dot_general | solution.py:10
  82.4 1.9 %copy.38 = f32[1536,256]{1,0:T(8,128)S(1)} copy(f32[1536,256]{0,1:T(8,128)} %convolution_bitcast_fusion.1) | data formatting | bytes 3145728 | tf_op jit(solution)/shard_map/dot_general | solution.py:10
  84.3 0.8 fusion.48
  85.3 4.2 %convolution_bitcast_fusion = f32[1536,256]{0,1:T(8,128)} fusion(bf16[3,512,1536]{2,1,0:T(8,128)(2,1)} %param.5, bf16[1536,256]{1,0:T(8,128)(2,1)S(1)} %bitcast.255, f32[256]{0:T(256)S(1)} %add_rsqrt_fusion.1), kind=kOutput, calls=%fused_computation | convolution fusion | flops 805568512 | bytes 5506048 | tf_op jit(solution)/shard_map/dot_general | solution.py:10
  89.5 1.9 %copy.40 = f32[1536,256]{1,0:T(8,128)S(1)} copy(f32[1536,256]{0,1:T(8,128)} %convolution_bitcast_fusion) | data formatting | bytes 3145728 | tf_op jit(solution)/shard_map/dot_general | solution.py:10
  92.0 0.5 collective-permute-start.25
  92.5 0.7 collective-permute-done.28
  93.4 2.0 %collective-permute-start.29 = (bf16[2,2,96,256]{3,2,0,1:T(8,128)(2,1)S(1)}, bf16[2,2,96,256]{3,2,0,1:T(8,128)(2,1)S(1)}, u32[]{:S(2)}, u32[]{:S(2)}) collective-permute-start(bf16[2,2,96,256]{3,2,0,1:T(8,128)(2,1)S(1)} %fusion.57), channel_id=1, source_target_pairs={{0,4},{1,5},{2,6},{3,7},{4,0},{5,1},{6,2},{7,3},{8,12},{9,13},{10,... | collective-permute-start | bytes 589832 | tf_op jit(solution)/shard_map/ppermute | solution.py:16
  95.4 3.6 %collective-permute-done.25 = bf16[2,2,96,256]{3,2,1,0:T(8,128)(2,1)S(1)} collective-permute-done((bf16[2,2,96,256]{3,2,1,0:T(8,128)(2,1)S(1)}, bf16[2,2,96,256]{3,2,1,0:T(8,128)(2,1)S(1)}, u32[]{:S(2)}, u32[]{:S(2)}) %collective-permute-start.25) | collective-permute-done | bytes 196640 | tf_op jit(solution)/shard_map/ppermute | solution.py:16
  99.1 2.0 %collective-permute-start.26 = (bf16[2,96,256]{2,1,0:T(8,128)(2,1)S(1)}, bf16[2,96,256]{2,1,0:T(8,128)(2,1)S(1)}, u32[]{:S(2)}, u32[]{:S(2)}) collective-permute-start(bf16[2,96,256]{2,1,0:T(8,128)(2,1)S(1)} %fusion.60), channel_id=1, source_target_pairs={{0,4},{1,5},{2,6},{3,7},{4,0},{5,1},{6,2},{7,3},{8,12},{9,13},{10,... | collective-permute-start | bytes 294920 | tf_op jit(solution)/shard_map/ppermute | solution.py:16
  101.5 2.2 %collective-permute-done.26 = bf16[2,96,256]{2,1,0:T(8,128)(2,1)S(1)} collective-permute-done((bf16[2,96,256]{2,1,0:T(8,128)(2,1)S(1)}, bf16[2,96,256]{2,1,0:T(8,128)(2,1)S(1)}, u32[]{:S(2)}, u32[]{:S(2)}) %collective-permute-start.26) | collective-permute-done | bytes 98336 | tf_op jit(solution)/shard_map/ppermute | solution.py:16
  103.8 2.6 %collective-permute-start.27 = (bf16[96,256]{1,0:T(8,128)(2,1)S(1)}, bf16[96,256]{1,0:T(8,128)(2,1)S(1)}, u32[]{:S(2)}, u32[]{:S(2)}) collective-permute-start(bf16[96,256]{1,0:T(8,128)(2,1)S(1)} %fusion.64), channel_id=1, source_target_pairs={{0,8},{1,9},{2,10},{3,11},{4,12},{5,13},{6,14},{7,15},{8,0},{9,1},... | collective-permute-start | bytes 147464 | tf_op jit(solution)/shard_map/ppermute | solution.py:16
  106.5 1.8 %collective-permute-start.31 = (bf16[96,256]{1,0:T(8,128)(2,1)S(1)}, bf16[96,256]{1,0:T(8,128)(2,1)S(1)}, u32[]{:S(2)}, u32[]{:S(2)}) collective-permute-start(bf16[96,256]{1,0:T(8,128)(2,1)S(1)} %fusion.65), channel_id=1, source_target_pairs={{0,8},{1,9},{2,10},{3,11},{4,12},{5,13},{6,14},{7,15},{8,0},{9,1},... | collective-permute-start | bytes 147464 | tf_op jit(solution)/shard_map/ppermute | solution.py:16
  108.2 0.7 collective-permute-done.27
  109.0 2.6 %collective-permute-done.31 = bf16[96,256]{1,0:T(8,128)(2,1)S(1)} collective-permute-done((bf16[96,256]{1,0:T(8,128)(2,1)S(1)}, bf16[96,256]{1,0:T(8,128)(2,1)S(1)}, u32[]{:S(2)}, u32[]{:S(2)}) %collective-permute-start.31) | collective-permute-done | bytes 49184 | tf_op jit(solution)/shard_map/ppermute | solution.py:16
  111.8 1.1 collective-permute-done.32
  112.9 0.8 collective-permute-start.33
  113.7 2.8 %collective-permute-done.33 = f32[256]{0:T(256)S(1)} collective-permute-done((f32[256]{0:T(256)S(1)}, f32[256]{0:T(256)S(1)}, u32[]{:S(2)}, u32[]{:S(2)}) %collective-permute-start.33) | collective-permute-done | bytes 1056 | tf_op jit(solution)/shard_map/ppermute | solution.py:16
  116.5 1.7 %collective-permute-start.34 = (f32[256]{0:T(256)S(1)}, f32[256]{0:T(256)S(1)}, u32[]{:S(2)}, u32[]{:S(2)}) collective-permute-start(f32[256]{0:T(256)S(1)} %add.188), channel_id=1, source_target_pairs={{0,4},{1,5},{2,6},{3,7},{4,0},{5,1},{6,2},{7,3},{8,12},{9,13},{10,... | collective-permute-start | bytes 3080 | tf_op jit(solution)/shard_map/ppermute | solution.py:16
  118.1 1.9 %collective-permute-done.34 = f32[256]{0:T(256)S(1)} collective-permute-done((f32[256]{0:T(256)S(1)}, f32[256]{0:T(256)S(1)}, u32[]{:S(2)}, u32[]{:S(2)}) %collective-permute-start.34) | collective-permute-done | bytes 1056 | tf_op jit(solution)/shard_map/ppermute | solution.py:16
  120.0 1.7 %collective-permute-start.35 = (f32[256]{0:T(256)S(1)}, f32[256]{0:T(256)S(1)}, u32[]{:S(2)}, u32[]{:S(2)}) collective-permute-start(f32[256]{0:T(256)S(1)} %add.189), channel_id=1, source_target_pairs={{0,8},{1,9},{2,10},{3,11},{4,12},{5,13},{6,14},{7,15},{8,0},{9,1},... | collective-permute-start | bytes 3080 | tf_op jit(solution)/shard_map/ppermute | solution.py:16
  121.8 2.7 %collective-permute-done.35 = f32[256]{0:T(256)S(1)} collective-permute-done((f32[256]{0:T(256)S(1)}, f32[256]{0:T(256)S(1)}, u32[]{:S(2)}, u32[]{:S(2)}) %collective-permute-start.35) | collective-permute-done | bytes 1056 | tf_op jit(solution)/shard_map/ppermute | solution.py:16
  124.5 0.7 broadcast_multiply_fusion
  (99 shorter events, 6.3 us)
Async XLA Ops:
  0.6 7.0 %collective-permute-start.8 = (bf16[96,256]{1,0:T(8,128)(2,1)}, bf16[96,256]{1,0:T(8,128)(2,1)S(1)}, u32[]{:S(2)}, u32[]{:S(2)}) collective-permute-start(bf16[96,256]{1,0:T(8,128)(2,1)} %param.7), channel_id=1, source_target_pairs={{0,8},{1,9},{2,10},{3,11},{4,12},{5,13},{6,14},{7,15},{8,0},{9,1},... | collective-permute-start | bytes 147464 | tf_op jit(solution)/shard_map/ppermute | solution.py:16
  4.7 5.6 %collective-permute-start = (bf16[96,256]{1,0:T(8,128)(2,1)}, bf16[96,256]{1,0:T(8,128)(2,1)S(1)}, u32[]{:S(2)}, u32[]{:S(2)}) collective-permute-start(bf16[96,256]{1,0:T(8,128)(2,1)} %param.6), channel_id=1, source_target_pairs={{0,8},{1,9},{2,10},{3,11},{4,12},{5,13},{6,14},{7,15},{8,0},{9,1},... | collective-permute-start | bytes 147464 | tf_op jit(solution)/shard_map/ppermute | solution.py:16
  8.5 4.7 %collective-permute-start.9 = (bf16[2,96,256]{2,1,0:T(8,128)(2,1)S(1)}, bf16[2,96,256]{2,1,0:T(8,128)(2,1)S(1)}, u32[]{:S(2)}, u32[]{:S(2)}) collective-permute-start(bf16[2,96,256]{2,1,0:T(8,128)(2,1)S(1)} %pad_maximum_fusion.13), channel_id=1, source_target_pairs={{0,2},{1,3},{2,0},{3,1},{4,6},{5,7},{6,4},{7,5},{8,10},{9,11},{10,... | collective-permute-start | bytes 294920 | tf_op jit(solution)/shard_map/ppermute | solution.py:16
  11.2 5.4 %collective-permute-start.1 = (bf16[2,96,256]{2,1,0:T(8,128)(2,1)S(1)}, bf16[2,96,256]{2,1,0:T(8,128)(2,1)S(1)}, u32[]{:S(2)}, u32[]{:S(2)}) collective-permute-start(bf16[2,96,256]{2,1,0:T(8,128)(2,1)S(1)} %pad_maximum_fusion.12), channel_id=1, source_target_pairs={{0,4},{1,5},{2,6},{3,7},{4,0},{5,1},{6,2},{7,3},{8,12},{9,13},{10,... | collective-permute-start | bytes 294920 | tf_op jit(solution)/shard_map/ppermute | solution.py:16
  13.2 6.8 %collective-permute-start.10 = (bf16[2,2,96,256]{3,2,1,0:T(8,128)(2,1)S(1)}, bf16[2,2,96,256]{3,2,1,0:T(8,128)(2,1)S(1)}, u32[]{:S(2)}, u32[]{:S(2)}) collective-permute-start(bf16[2,2,96,256]{3,2,1,0:T(8,128)(2,1)S(1)} %pad_maximum_fusion.9), channel_id=1, source_target_pairs={{0,4},{1,5},{2,6},{3,7},{4,0},{5,1},{6,2},{7,3},{8,12},{9,13},{10,... | collective-permute-start | bytes 589832 | tf_op jit(solution)/shard_map/ppermute | solution.py:16
  16.7 5.7 %collective-permute-start.2 = (bf16[2,2,96,256]{3,2,0,1:T(8,128)(2,1)S(1)}, bf16[2,2,96,256]{3,2,0,1:T(8,128)(2,1)S(1)}, u32[]{:S(2)}, u32[]{:S(2)}) collective-permute-start(bf16[2,2,96,256]{3,2,0,1:T(8,128)(2,1)S(1)} %pad_maximum_fusion.8), channel_id=1, source_target_pairs={{0,2},{1,3},{2,0},{3,1},{4,6},{5,7},{6,4},{7,5},{8,10},{9,11},{10,... | collective-permute-start | bytes 589832 | tf_op jit(solution)/shard_map/ppermute | solution.py:16
  20.2 3.1 %collective-permute-start.11 = (bf16[2,2,2,96,256]{4,3,2,0,1:T(8,128)(2,1)S(1)}, bf16[2,2,2,96,256]{4,3,2,0,1:T(8,128)(2,1)S(1)}, u32[]{:S(2)}, u32[]{:S(2)}) collective-permute-start(bf16[2,2,2,96,256]{4,3,2,0,1:T(8,128)(2,1)S(1)} %pad_maximum_fusion.5), channel_id=1, source_target_pairs={{0,1},{1,0},{2,3},{3,2},{4,5},{5,4},{6,7},{7,6},{8,9},{9,8},{10,11... | collective-permute-start | bytes 1179656 | tf_op jit(solution)/shard_map/ppermute | solution.py:16
  23.2 5.0 %collective-permute-start.3 = (bf16[2,2,2,96,256]{4,3,2,1,0:T(8,128)(2,1)}, bf16[2,2,2,96,256]{4,3,2,1,0:T(8,128)(2,1)}, u32[]{:S(2)}, u32[]{:S(2)}) collective-permute-start(bf16[2,2,2,96,256]{4,3,2,1,0:T(8,128)(2,1)} %copy.43), channel_id=1, source_target_pairs={{0,1},{1,0},{2,3},{3,2},{4,5},{5,4},{6,7},{7,6},{8,9},{9,8},{10,11... | collective-permute-start | bytes 1179656 | tf_op jit(solution)/shard_map/ppermute | solution.py:16
  27.7 8.6 %collective-permute-start.12 = (bf16[2,2,2,96,256]{4,3,0,2,1:T(8,128)(2,1)}, bf16[2,2,2,96,256]{4,3,0,2,1:T(8,128)(2,1)S(1)}, u32[]{:S(2)}, u32[]{:S(2)}) collective-permute-start(bf16[2,2,2,96,256]{4,3,0,2,1:T(8,128)(2,1)} %fusion.50), channel_id=1, source_target_pairs={{0,1},{1,0},{2,3},{3,2},{4,5},{5,4},{6,7},{7,6},{8,9},{9,8},{10,11... | collective-permute-start | bytes 1179656 | tf_op jit(solution)/shard_map/ppermute | solution.py:16
  36.3 2.2 %collective-permute-start.4 = (bf16[2,2,2,96,256]{4,3,0,1,2:T(8,128)(2,1)}, bf16[2,2,2,96,256]{4,3,0,1,2:T(8,128)(2,1)}, u32[]{:S(2)}, u32[]{:S(2)}) collective-permute-start(bf16[2,2,2,96,256]{4,3,0,1,2:T(8,128)(2,1)} %fusion.49), channel_id=1, source_target_pairs={{0,1},{1,0},{2,3},{3,2},{4,5},{5,4},{6,7},{7,6},{8,9},{9,8},{10,11... | collective-permute-start | bytes 1179656 | tf_op jit(solution)/shard_map/ppermute | solution.py:16
  36.4 7.6 %collective-permute-start.13 = (bf16[2,2,96,256]{3,2,0,1:T(8,128)(2,1)S(1)}, bf16[2,2,96,256]{3,2,0,1:T(8,128)(2,1)S(1)}, u32[]{:S(2)}, u32[]{:S(2)}) collective-permute-start(bf16[2,2,96,256]{3,2,0,1:T(8,128)(2,1)S(1)} %fusion.55), channel_id=1, source_target_pairs={{0,4},{1,5},{2,6},{3,7},{4,0},{5,1},{6,2},{7,3},{8,12},{9,13},{10,... | collective-permute-start | bytes 589832 | tf_op jit(solution)/shard_map/ppermute | solution.py:16
  39.6 7.1 %collective-permute-start.5 = (bf16[2,2,96,256]{3,2,0,1:T(8,128)(2,1)S(1)}, bf16[2,2,96,256]{3,2,0,1:T(8,128)(2,1)S(1)}, u32[]{:S(2)}, u32[]{:S(2)}) collective-permute-start(bf16[2,2,96,256]{3,2,0,1:T(8,128)(2,1)S(1)} %fusion.54), channel_id=1, source_target_pairs={{0,2},{1,3},{2,0},{3,1},{4,6},{5,7},{6,4},{7,5},{8,10},{9,11},{10,... | collective-permute-start | bytes 589832 | tf_op jit(solution)/shard_map/ppermute | solution.py:16
  44.1 4.7 %collective-permute-start.14 = (bf16[2,96,256]{2,1,0:T(8,128)(2,1)S(1)}, bf16[2,96,256]{2,1,0:T(8,128)(2,1)S(1)}, u32[]{:S(2)}, u32[]{:S(2)}) collective-permute-start(bf16[2,96,256]{2,1,0:T(8,128)(2,1)S(1)} %fusion.59), channel_id=1, source_target_pairs={{0,2},{1,3},{2,0},{3,1},{4,6},{5,7},{6,4},{7,5},{8,10},{9,11},{10,... | collective-permute-start | bytes 294920 | tf_op jit(solution)/shard_map/ppermute | solution.py:16
  46.8 5.4 %collective-permute-start.6 = (bf16[2,96,256]{2,1,0:T(8,128)(2,1)S(1)}, bf16[2,96,256]{2,1,0:T(8,128)(2,1)S(1)}, u32[]{:S(2)}, u32[]{:S(2)}) collective-permute-start(bf16[2,96,256]{2,1,0:T(8,128)(2,1)S(1)} %fusion.58), channel_id=1, source_target_pairs={{0,4},{1,5},{2,6},{3,7},{4,0},{5,1},{6,2},{7,3},{8,12},{9,13},{10,... | collective-permute-start | bytes 294920 | tf_op jit(solution)/shard_map/ppermute | solution.py:16
  48.9 6.4 %collective-permute-start.15 = (bf16[96,256]{1,0:T(8,128)(2,1)S(1)}, bf16[96,256]{1,0:T(8,128)(2,1)S(1)}, u32[]{:S(2)}, u32[]{:S(2)}) collective-permute-start(bf16[96,256]{1,0:T(8,128)(2,1)S(1)} %fusion.63), channel_id=1, source_target_pairs={{0,8},{1,9},{2,10},{3,11},{4,12},{5,13},{6,14},{7,15},{8,0},{9,1},... | collective-permute-start | bytes 147464 | tf_op jit(solution)/shard_map/ppermute | solution.py:16
  52.2 5.1 %collective-permute-start.7 = (bf16[96,256]{1,0:T(8,128)(2,1)S(1)}, bf16[96,256]{1,0:T(8,128)(2,1)S(1)}, u32[]{:S(2)}, u32[]{:S(2)}) collective-permute-start(bf16[96,256]{1,0:T(8,128)(2,1)S(1)} %fusion.62), channel_id=1, source_target_pairs={{0,8},{1,9},{2,10},{3,11},{4,12},{5,13},{6,14},{7,15},{8,0},{9,1},... | collective-permute-start | bytes 147464 | tf_op jit(solution)/shard_map/ppermute | solution.py:16
  57.4 5.1 %collective-permute-start.16 = (bf16[96,256]{1,0:T(8,128)(2,1)S(1)}, bf16[96,256]{1,0:T(8,128)(2,1)S(1)}, u32[]{:S(2)}, u32[]{:S(2)}) collective-permute-start(bf16[96,256]{1,0:T(8,128)(2,1)S(1)} %get-tuple-element.72), channel_id=1, source_target_pairs={{0,8},{1,9},{2,10},{3,11},{4,12},{5,13},{6,14},{7,15},{8,0},{9,1},... | collective-permute-start | bytes 147464 | tf_op jit(solution)/shard_map/ppermute | solution.py:16
  60.5 5.0 %collective-permute-start.20 = (bf16[96,256]{1,0:T(8,128)(2,1)S(1)}, bf16[96,256]{1,0:T(8,128)(2,1)S(1)}, u32[]{:S(2)}, u32[]{:S(2)}) collective-permute-start(bf16[96,256]{1,0:T(8,128)(2,1)S(1)} %get-tuple-element.73), channel_id=1, source_target_pairs={{0,8},{1,9},{2,10},{3,11},{4,12},{5,13},{6,14},{7,15},{8,0},{9,1},... | collective-permute-start | bytes 147464 | tf_op jit(solution)/shard_map/ppermute | solution.py:16
  62.6 4.8 %collective-permute-start.17 = (bf16[2,96,256]{2,1,0:T(8,128)(2,1)S(1)}, bf16[2,96,256]{2,1,0:T(8,128)(2,1)S(1)}, u32[]{:S(2)}, u32[]{:S(2)}) collective-permute-start(bf16[2,96,256]{2,1,0:T(8,128)(2,1)S(1)} %pad_maximum_fusion.14), channel_id=1, source_target_pairs={{0,4},{1,5},{2,6},{3,7},{4,0},{5,1},{6,2},{7,3},{8,12},{9,13},{10,... | collective-permute-start | bytes 294920 | tf_op jit(solution)/shard_map/ppermute | solution.py:16
  65.5 4.7 %collective-permute-start.21 = (bf16[2,96,256]{2,1,0:T(8,128)(2,1)S(1)}, bf16[2,96,256]{2,1,0:T(8,128)(2,1)S(1)}, u32[]{:S(2)}, u32[]{:S(2)}) collective-permute-start(bf16[2,96,256]{2,1,0:T(8,128)(2,1)S(1)} %pad_maximum_fusion.15), channel_id=1, source_target_pairs={{0,2},{1,3},{2,0},{3,1},{4,6},{5,7},{6,4},{7,5},{8,10},{9,11},{10,... | collective-permute-start | bytes 294920 | tf_op jit(solution)/shard_map/ppermute | solution.py:16
  67.4 5.7 %collective-permute-start.18 = (bf16[2,2,96,256]{3,2,0,1:T(8,128)(2,1)S(1)}, bf16[2,2,96,256]{3,2,0,1:T(8,128)(2,1)S(1)}, u32[]{:S(2)}, u32[]{:S(2)}) collective-permute-start(bf16[2,2,96,256]{3,2,0,1:T(8,128)(2,1)S(1)} %pad_maximum_fusion.10), channel_id=1, source_target_pairs={{0,2},{1,3},{2,0},{3,1},{4,6},{5,7},{6,4},{7,5},{8,10},{9,11},{10,... | collective-permute-start | bytes 589832 | tf_op jit(solution)/shard_map/ppermute | solution.py:16
  70.2 5.7 %collective-permute-start.22 = (bf16[2,2,96,256]{3,2,1,0:T(8,128)(2,1)S(1)}, bf16[2,2,96,256]{3,2,1,0:T(8,128)(2,1)S(1)}, u32[]{:S(2)}, u32[]{:S(2)}) collective-permute-start(bf16[2,2,96,256]{3,2,1,0:T(8,128)(2,1)S(1)} %pad_maximum_fusion.11), channel_id=1, source_target_pairs={{0,4},{1,5},{2,6},{3,7},{4,0},{5,1},{6,2},{7,3},{8,12},{9,13},{10,... | collective-permute-start | bytes 589832 | tf_op jit(solution)/shard_map/ppermute | solution.py:16
  73.2 2.9 %collective-permute-start.19 = (bf16[2,2,2,96,256]{4,3,0,1,2:T(8,128)(2,1)S(1)}, bf16[2,2,2,96,256]{4,3,0,1,2:T(8,128)(2,1)S(1)}, u32[]{:S(2)}, u32[]{:S(2)}) collective-permute-start(bf16[2,2,2,96,256]{4,3,0,1,2:T(8,128)(2,1)S(1)} %pad_maximum_fusion.6), channel_id=1, source_target_pairs={{0,1},{1,0},{2,3},{3,2},{4,5},{5,4},{6,7},{7,6},{8,9},{9,8},{10,11... | collective-permute-start | bytes 1179656 | tf_op jit(solution)/shard_map/ppermute | solution.py:16
  76.0 1.8 %collective-permute-start.23 = (bf16[2,2,2,96,256]{4,3,2,1,0:T(8,128)(2,1)S(1)}, bf16[2,2,2,96,256]{4,3,2,1,0:T(8,128)(2,1)S(1)}, u32[]{:S(2)}, u32[]{:S(2)}) collective-permute-start(bf16[2,2,2,96,256]{4,3,2,1,0:T(8,128)(2,1)S(1)} %pad_maximum_fusion.7), channel_id=1, source_target_pairs={{0,1},{1,0},{2,3},{3,2},{4,5},{5,4},{6,7},{7,6},{8,9},{9,8},{10,11... | collective-permute-start | bytes 1179656 | tf_op jit(solution)/shard_map/ppermute | solution.py:16
  85.1 6.7 %collective-permute-start.24 = (bf16[2,2,2,96,256]{4,3,2,1,0:T(8,128)(2,1)}, bf16[2,2,2,96,256]{4,3,2,1,0:T(8,128)(2,1)S(1)}, u32[]{:S(2)}, u32[]{:S(2)}) collective-permute-start(bf16[2,2,2,96,256]{4,3,2,1,0:T(8,128)(2,1)} %fusion.48), channel_id=1, source_target_pairs={{0,1},{1,0},{2,3},{3,2},{4,5},{5,4},{6,7},{7,6},{8,9},{9,8},{10,11... | collective-permute-start | bytes 1179656 | tf_op jit(solution)/shard_map/ppermute | solution.py:16
  91.4 1.8 %collective-permute-start.28 = (bf16[2,2,2,96,256]{4,3,0,2,1:T(8,128)(2,1)S(1)}, bf16[2,2,2,96,256]{4,3,0,2,1:T(8,128)(2,1)S(1)}, u32[]{:S(2)}, u32[]{:S(2)}) collective-permute-start(bf16[2,2,2,96,256]{4,3,0,2,1:T(8,128)(2,1)S(1)} %fusion.51), channel_id=1, source_target_pairs={{0,1},{1,0},{2,3},{3,2},{4,5},{5,4},{6,7},{7,6},{8,9},{9,8},{10,11... | collective-permute-start | bytes 1179656 | tf_op jit(solution)/shard_map/ppermute | solution.py:16
  92.0 7.0 %collective-permute-start.25 = (bf16[2,2,96,256]{3,2,1,0:T(8,128)(2,1)S(1)}, bf16[2,2,96,256]{3,2,1,0:T(8,128)(2,1)S(1)}, u32[]{:S(2)}, u32[]{:S(2)}) collective-permute-start(bf16[2,2,96,256]{3,2,1,0:T(8,128)(2,1)S(1)} %fusion.56), channel_id=1, source_target_pairs={{0,2},{1,3},{2,0},{3,1},{4,6},{5,7},{6,4},{7,5},{8,10},{9,11},{10,... | collective-permute-start | bytes 589832 | tf_op jit(solution)/shard_map/ppermute | solution.py:16
  93.3 18.2 %copy-start = (f32[96,1]{0,1:T(1,128)S(1)}, f32[96,1]{0,1:T(1,128)}, u32[]{:S(2)}) copy-start(f32[96,1]{0,1:T(1,128)} %get-tuple-element.56) | copy-start | bytes 1156
  93.4 18.2 %copy-start.1 = (f32[96,1]{0,1:T(1,128)S(1)}, f32[96,1]{0,1:T(1,128)}, u32[]{:S(2)}) copy-start(f32[96,1]{0,1:T(1,128)} %get-tuple-element.51) | copy-start | bytes 1156
  93.4 7.7 %collective-permute-start.29 = (bf16[2,2,96,256]{3,2,0,1:T(8,128)(2,1)S(1)}, bf16[2,2,96,256]{3,2,0,1:T(8,128)(2,1)S(1)}, u32[]{:S(2)}, u32[]{:S(2)}) collective-permute-start(bf16[2,2,96,256]{3,2,0,1:T(8,128)(2,1)S(1)} %fusion.57), channel_id=1, source_target_pairs={{0,4},{1,5},{2,6},{3,7},{4,0},{5,1},{6,2},{7,3},{8,12},{9,13},{10,... | collective-permute-start | bytes 589832 | tf_op jit(solution)/shard_map/ppermute | solution.py:16
  99.1 4.7 %collective-permute-start.26 = (bf16[2,96,256]{2,1,0:T(8,128)(2,1)S(1)}, bf16[2,96,256]{2,1,0:T(8,128)(2,1)S(1)}, u32[]{:S(2)}, u32[]{:S(2)}) collective-permute-start(bf16[2,96,256]{2,1,0:T(8,128)(2,1)S(1)} %fusion.60), channel_id=1, source_target_pairs={{0,4},{1,5},{2,6},{3,7},{4,0},{5,1},{6,2},{7,3},{8,12},{9,13},{10,... | collective-permute-start | bytes 294920 | tf_op jit(solution)/shard_map/ppermute | solution.py:16
  101.2 5.3 %collective-permute-start.30 = (bf16[2,96,256]{2,1,0:T(8,128)(2,1)S(1)}, bf16[2,96,256]{2,1,0:T(8,128)(2,1)S(1)}, u32[]{:S(2)}, u32[]{:S(2)}) collective-permute-start(bf16[2,96,256]{2,1,0:T(8,128)(2,1)S(1)} %fusion.61), channel_id=1, source_target_pairs={{0,2},{1,3},{2,0},{3,1},{4,6},{5,7},{6,4},{7,5},{8,10},{9,11},{10,... | collective-permute-start | bytes 294920 | tf_op jit(solution)/shard_map/ppermute | solution.py:16
  103.8 5.2 %collective-permute-start.27 = (bf16[96,256]{1,0:T(8,128)(2,1)S(1)}, bf16[96,256]{1,0:T(8,128)(2,1)S(1)}, u32[]{:S(2)}, u32[]{:S(2)}) collective-permute-start(bf16[96,256]{1,0:T(8,128)(2,1)S(1)} %fusion.64), channel_id=1, source_target_pairs={{0,8},{1,9},{2,10},{3,11},{4,12},{5,13},{6,14},{7,15},{8,0},{9,1},... | collective-permute-start | bytes 147464 | tf_op jit(solution)/shard_map/ppermute | solution.py:16
  106.5 5.1 %collective-permute-start.31 = (bf16[96,256]{1,0:T(8,128)(2,1)S(1)}, bf16[96,256]{1,0:T(8,128)(2,1)S(1)}, u32[]{:S(2)}, u32[]{:S(2)}) collective-permute-start(bf16[96,256]{1,0:T(8,128)(2,1)S(1)} %fusion.65), channel_id=1, source_target_pairs={{0,8},{1,9},{2,10},{3,11},{4,12},{5,13},{6,14},{7,15},{8,0},{9,1},... | collective-permute-start | bytes 147464 | tf_op jit(solution)/shard_map/ppermute | solution.py:16
  111.7 1.2 collective-permute-start.32
  112.9 3.6 %collective-permute-start.33 = (f32[256]{0:T(256)S(1)}, f32[256]{0:T(256)S(1)}, u32[]{:S(2)}, u32[]{:S(2)}) collective-permute-start(f32[256]{0:T(256)S(1)} %add.187), channel_id=1, source_target_pairs={{0,2},{1,3},{2,0},{3,1},{4,6},{5,7},{6,4},{7,5},{8,10},{9,11},{10,... | collective-permute-start | bytes 3080 | tf_op jit(solution)/shard_map/ppermute | solution.py:16
  116.5 3.6 %collective-permute-start.34 = (f32[256]{0:T(256)S(1)}, f32[256]{0:T(256)S(1)}, u32[]{:S(2)}, u32[]{:S(2)}) collective-permute-start(f32[256]{0:T(256)S(1)} %add.188), channel_id=1, source_target_pairs={{0,4},{1,5},{2,6},{3,7},{4,0},{5,1},{6,2},{7,3},{8,12},{9,13},{10,... | collective-permute-start | bytes 3080 | tf_op jit(solution)/shard_map/ppermute | solution.py:16
  120.0 4.5 %collective-permute-start.35 = (f32[256]{0:T(256)S(1)}, f32[256]{0:T(256)S(1)}, u32[]{:S(2)}, u32[]{:S(2)}) collective-permute-start(f32[256]{0:T(256)S(1)} %add.189), channel_id=1, source_target_pairs={{0,8},{1,9},{2,10},{3,11},{4,12},{5,13},{6,14},{7,15},{8,0},{9,1},... | collective-permute-start | bytes 3080 | tf_op jit(solution)/shard_map/ppermute | solution.py:16

commit v11 on v9

--- a/solution.py
+++ b/solution.py
@@ -48,8 +48,14 @@
 
 def doubling_all_reduce(x, devices):
     bits = devices.bit_length() - 1
-    for bit in range(bits):
-        x = x + exchange(x, 1 << bit, devices)
+    low = 0
+    while low < bits:
+        width = 2 if low + 1 < bits else 1
+        total = x
+        for digit in range(1, 1 << width):
+            total = total + exchange(x, digit << low, devices)
+        x = total
+        low += width
     return x
 
 

time: 125 us -> 122 us (0.976)
  waiting for transfers between devices: 47.3 us -> 42.9 us
  starting transfers between devices: 42.7 us -> 44.4 us
    ppermute x36 -> x38, waiting for transfers between devices: 47.3 us -> 42.9 us  [exchange(): return lax.ppermute(x, 'row', [(i, i ^ distance) for i in range(devices)])]
    ppermute x36 -> x38, starting transfers between devices: 42.7 us -> 44.4 us  [exchange(): return lax.ppermute(x, 'row', [(i, i ^ distance) for i in range(devices)])]
  transfers between devices with their start and end apart: 36 -> 38, of which waited for: 24 -> 24; matrix products, arithmetic and copies ran while one was open for 22% -> 22% of each run, Pallas kernels for 0% -> 0%
where the time goes in v11:
time: 122 us
  starting transfers between devices  44.4 us (36%)
  waiting for transfers between devices  42.9 us (35%)
  matrix products  14.5 us (12%)
  local copies, waits for them, and re-layouts  10.7 us (9%)
  other arithmetic  8.28 us (7%)
  between operations  1.23 us (1%)
    ppermute x38, starting transfers between devices, exchange(): return lax.ppermute(x, 'row', [(i, i ^ distance) for i in range(devices)])  44.4 us
    ppermute x38, waiting for transfers between devices, exchange(): return lax.ppermute(x, 'row', [(i, i ^ distance) for i in range(devices)])  42.9 us
    dot_general x4, matrix products, contract_rows(): lax.dot_general(left, right, (((0,), (0,)), ((), ())), preferred_element_...  14.5 us
    dot_general x4, local copies, waits for them, and re-layouts, contract_rows(): lax.dot_general(left, right, (((0,), (0,)), ((), ())), preferred_element_...  4.68 us
    another operation x32, other arithmetic, doubling_all_gather(): jnp.stack([jnp.where(low, cur, other), jnp.where(low, other, cur)], axis=...  3.75 us
    convert_element_type x16, local copies, waits for them, and re-layouts, halving_reduce_scatter(): send.astype(jnp.bfloat16)  2.71 us
  transfers between devices with their start and end apart: 38, of which 24 were waited for; matrix products, arithmetic and copies ran while one was open for 22% of the time, Pallas kernels for 0%

profile of v11, /device:TPU:0, one launch (start us, length us, event | category | flops | bytes accessed | tf_op | source)
XLA Modules:
  0.0 122.1 jit_solution(5007204408574686954)
XLA Ops:
  0.6 4.1 %collective-permute-start.8 = (bf16[96,256]{1,0:T(8,128)(2,1)}, bf16[96,256]{1,0:T(8,128)(2,1)S(1)}, u32[]{:S(2)}, u32[]{:S(2)}) collective-permute-start(bf16[96,256]{1,0:T(8,128)(2,1)} %param.7), channel_id=1, source_target_pairs={{0,8},{1,9},{2,10},{3,11},{4,12},{5,13},{6,14},{7,15},{8,0},{9,1},... | collective-permute-start | bytes 147464 | tf_op jit(solution)/shard_map/ppermute | solution.py:16
  4.8 2.7 %collective-permute-done.8 = bf16[96,256]{1,0:T(8,128)(2,1)S(1)} collective-permute-done((bf16[96,256]{1,0:T(8,128)(2,1)}, bf16[96,256]{1,0:T(8,128)(2,1)S(1)}, u32[]{:S(2)}, u32[]{:S(2)}) %collective-permute-start.8) | collective-permute-done | bytes 49184 | tf_op jit(solution)/shard_map/ppermute | solution.py:16
  7.5 0.8 select_bitcast_fusion.29
  8.4 1.8 %collective-permute-start.9 = (bf16[2,96,256]{2,1,0:T(8,128)(2,1)S(1)}, bf16[2,96,256]{2,1,0:T(8,128)(2,1)S(1)}, u32[]{:S(2)}, u32[]{:S(2)}) collective-permute-start(bf16[2,96,256]{2,1,0:T(8,128)(2,1)S(1)} %pad_maximum_fusion.13), channel_id=1, source_target_pairs={{0,2},{1,3},{2,0},{3,1},{4,6},{5,7},{6,4},{7,5},{8,10},{9,11},{10,... | collective-permute-start | bytes 294920 | tf_op jit(solution)/shard_map/ppermute | solution.py:16
  10.2 0.8 select_bitcast_fusion.31
  11.0 2.0 %collective-permute-start.1 = (bf16[2,96,256]{2,1,0:T(8,128)(2,1)S(1)}, bf16[2,96,256]{2,1,0:T(8,128)(2,1)S(1)}, u32[]{:S(2)}, u32[]{:S(2)}) collective-permute-start(bf16[2,96,256]{2,1,0:T(8,128)(2,1)S(1)} %pad_maximum_fusion.12), channel_id=1, source_target_pairs={{0,4},{1,5},{2,6},{3,7},{4,0},{5,1},{6,2},{7,3},{8,12},{9,13},{10,... | collective-permute-start | bytes 294920 | tf_op jit(solution)/shard_map/ppermute | solution.py:16
  13.1 2.2 %collective-permute-start.10 = (bf16[2,2,96,256]{3,2,1,0:T(8,128)(2,1)S(1)}, bf16[2,2,96,256]{3,2,1,0:T(8,128)(2,1)S(1)}, u32[]{:S(2)}, u32[]{:S(2)}) collective-permute-start(bf16[2,2,96,256]{3,2,1,0:T(8,128)(2,1)S(1)} %pad_maximum_fusion.9), channel_id=1, source_target_pairs={{0,4},{1,5},{2,6},{3,7},{4,0},{5,1},{6,2},{7,3},{8,12},{9,13},{10,... | collective-permute-start | bytes 589832 | tf_op jit(solution)/shard_map/ppermute | solution.py:16
  15.3 1.0 collective-permute-done.1
  16.4 1.5 %collective-permute-start.2 = (bf16[2,2,96,256]{3,2,0,1:T(8,128)(2,1)S(1)}, bf16[2,2,96,256]{3,2,0,1:T(8,128)(2,1)S(1)}, u32[]{:S(2)}, u32[]{:S(2)}) collective-permute-start(bf16[2,2,96,256]{3,2,0,1:T(8,128)(2,1)S(1)} %pad_maximum_fusion.8), channel_id=1, source_target_pairs={{0,2},{1,3},{2,0},{3,1},{4,6},{5,7},{6,4},{7,5},{8,10},{9,11},{10,... | collective-permute-start | bytes 589832 | tf_op jit(solution)/shard_map/ppermute | solution.py:16
  17.9 2.0 %collective-permute-done.10 = bf16[2,2,96,256]{3,2,1,0:T(8,128)(2,1)S(1)} collective-permute-done((bf16[2,2,96,256]{3,2,1,0:T(8,128)(2,1)S(1)}, bf16[2,2,96,256]{3,2,1,0:T(8,128)(2,1)S(1)}, u32[]{:S(2)}, u32[]{:S(2)}) %collective-permute-start.10) | collective-permute-done | bytes 196640 | tf_op jit(solution)/shard_map/ppermute | solution.py:16
  20.7 1.4 %collective-permute-done.2 = bf16[2,2,96,256]{3,2,0,1:T(8,128)(2,1)S(1)} collective-permute-done((bf16[2,2,96,256]{3,2,0,1:T(8,128)(2,1)S(1)}, bf16[2,2,96,256]{3,2,0,1:T(8,128)(2,1)S(1)}, u32[]{:S(2)}, u32[]{:S(2)}) %collective-permute-start.2) | collective-permute-done | bytes 196640 | tf_op jit(solution)/shard_map/ppermute | solution.py:16
  22.2 0.8 copy.43
  23.2 3.0 %convolution_bitcast_fusion.2 = f32[1536,256]{0,1:T(8,128)S(1)} fusion(bf16[1536,256]{1,0:T(8,128)(2,1)S(1)} %bitcast.250, bf16[3,512,1536]{2,1,0:T(8,128)(2,1)} %param.5), kind=kOutput, calls=%fused_computation.2 | convolution fusion | flops 805437440 | bytes 5505024 | tf_op jit(solution)/shard_map/dot_general | solution.py:10
  26.7 0.8 fusion.50
  28.0 1.2 select_bitcast_fusion.7
  29.2 4.1 %convolution_bitcast_fusion.3 = f32[1536,256]{0,1:T(8,128)} fusion(bf16[1536,256]{1,0:T(8,128)(2,1)S(1)} %bitcast.249, bf16[3,512,1536]{2,1,0:T(8,128)(2,1)} %param.5), kind=kOutput, calls=%fused_computation.3 | convolution fusion | flops 805437440 | bytes 5505024 | tf_op jit(solution)/shard_map/dot_general | solution.py:10
  33.4 1.9 %copy.22 = f32[1536,256]{1,0:T(8,128)S(1)} copy(f32[1536,256]{0,1:T(8,128)} %convolution_bitcast_fusion.3) | data formatting | bytes 3145728 | tf_op jit(solution)/shard_map/dot_general | solution.py:10
  35.2 0.8 fusion.49
  36.0 1.4 %bitcast_divide_fusion.1 = (f32[96]{0:T(128)}, f32[96]{0:T(128)}) fusion(f32[1,1536]{1,0:T(1,128)} %get-tuple-element.52, s32[]{:T(128)S(6)} %select_n.207, f32[1,1536]{1,0:T(1,128)} %get-tuple-element.45), kind=kLoop, calls=%fused_computation.156 | loop fusion | flops 288 | bytes 1540 | tf_op jit(solution)/shard_map/div | solution.py:93
  37.6 2.3 %collective-permute-start.13 = (bf16[2,2,96,256]{3,2,0,1:T(8,128)(2,1)S(1)}, bf16[2,2,96,256]{3,2,0,1:T(8,128)(2,1)S(1)}, u32[]{:S(2)}, u32[]{:S(2)}) collective-permute-start(bf16[2,2,96,256]{3,2,0,1:T(8,128)(2,1)S(1)} %fusion.55), channel_id=1, source_target_pairs={{0,4},{1,5},{2,6},{3,7},{4,0},{5,1},{6,2},{7,3},{8,12},{9,13},{10,... | collective-permute-start | bytes 589832 | tf_op jit(solution)/shard_map/ppermute | solution.py:16
  39.9 1.1 bitcast_add_fusion.3
  41.4 4.0 %collective-permute-done.13 = bf16[2,2,96,256]{3,2,0,1:T(8,128)(2,1)S(1)} collective-permute-done((bf16[2,2,96,256]{3,2,0,1:T(8,128)(2,1)S(1)}, bf16[2,2,96,256]{3,2,0,1:T(8,128)(2,1)S(1)}, u32[]{:S(2)}, u32[]{:S(2)}) %collective-permute-start.13) | collective-permute-done | bytes 196640 | tf_op jit(solution)/shard_map/ppermute | solution.py:16
  45.6 1.0 collective-permute-start.14
  46.5 1.6 %collective-permute-done.5 = bf16[2,2,96,256]{3,2,0,1:T(8,128)(2,1)S(1)} collective-permute-done((bf16[2,2,96,256]{3,2,0,1:T(8,128)(2,1)S(1)}, bf16[2,2,96,256]{3,2,0,1:T(8,128)(2,1)S(1)}, u32[]{:S(2)}, u32[]{:S(2)}) %collective-permute-start.5) | collective-permute-done | bytes 196640 | tf_op jit(solution)/shard_map/ppermute | solution.py:16
  48.7 1.6 %collective-permute-done.14 = bf16[2,96,256]{2,1,0:T(8,128)(2,1)S(1)} collective-permute-done((bf16[2,96,256]{2,1,0:T(8,128)(2,1)S(1)}, bf16[2,96,256]{2,1,0:T(8,128)(2,1)S(1)}, u32[]{:S(2)}, u32[]{:S(2)}) %collective-permute-start.14) | collective-permute-done | bytes 98336 | tf_op jit(solution)/shard_map/ppermute | solution.py:16
  50.3 3.3 %collective-permute-start.15 = (bf16[96,256]{1,0:T(8,128)(2,1)S(1)}, bf16[96,256]{1,0:T(8,128)(2,1)S(1)}, u32[]{:S(2)}, u32[]{:S(2)}) collective-permute-start(bf16[96,256]{1,0:T(8,128)(2,1)S(1)} %fusion.63), channel_id=1, source_target_pairs={{0,8},{1,9},{2,10},{3,11},{4,12},{5,13},{6,14},{7,15},{8,0},{9,1},... | collective-permute-start | bytes 147464 | tf_op jit(solution)/shard_map/ppermute | solution.py:16
  53.7 2.8 %collective-permute-start.7 = (bf16[96,256]{1,0:T(8,128)(2,1)S(1)}, bf16[96,256]{1,0:T(8,128)(2,1)S(1)}, u32[]{:S(2)}, u32[]{:S(2)}) collective-permute-start(bf16[96,256]{1,0:T(8,128)(2,1)S(1)} %fusion.62), channel_id=1, source_target_pairs={{0,8},{1,9},{2,10},{3,11},{4,12},{5,13},{6,14},{7,15},{8,0},{9,1},... | collective-permute-start | bytes 147464 | tf_op jit(solution)/shard_map/ppermute | solution.py:16
  56.5 0.8 cosine_bitcast_fusion
  57.3 1.5 %collective-permute-done.7 = bf16[96,256]{1,0:T(8,128)(2,1)S(1)} collective-permute-done((bf16[96,256]{1,0:T(8,128)(2,1)S(1)}, bf16[96,256]{1,0:T(8,128)(2,1)S(1)}, u32[]{:S(2)}, u32[]{:S(2)}) %collective-permute-start.7) | collective-permute-done | bytes 49184 | tf_op jit(solution)/shard_map/ppermute | solution.py:16
  58.9 2.8 %collective-permute-start.16 = (bf16[96,256]{1,0:T(8,128)(2,1)S(1)}, bf16[96,256]{1,0:T(8,128)(2,1)S(1)}, u32[]{:S(2)}, u32[]{:S(2)}) collective-permute-start(bf16[96,256]{1,0:T(8,128)(2,1)S(1)} %get-tuple-element.16), channel_id=1, source_target_pairs={{0,8},{1,9},{2,10},{3,11},{4,12},{5,13},{6,14},{7,15},{8,0},{9,1},... | collective-permute-start | bytes 147464 | tf_op jit(solution)/shard_map/ppermute | solution.py:16
  61.9 2.1 %collective-permute-done.16 = bf16[96,256]{1,0:T(8,128)(2,1)S(1)} collective-permute-done((bf16[96,256]{1,0:T(8,128)(2,1)S(1)}, bf16[96,256]{1,0:T(8,128)(2,1)S(1)}, u32[]{:S(2)}, u32[]{:S(2)}) %collective-permute-start.16) | collective-permute-done | bytes 49184 | tf_op jit(solution)/shard_map/ppermute | solution.py:16
  64.0 1.8 %collective-permute-start.17 = (bf16[2,96,256]{2,1,0:T(8,128)(2,1)S(1)}, bf16[2,96,256]{2,1,0:T(8,128)(2,1)S(1)}, u32[]{:S(2)}, u32[]{:S(2)}) collective-permute-start(bf16[2,96,256]{2,1,0:T(8,128)(2,1)S(1)} %pad_maximum_fusion.14), channel_id=1, source_target_pairs={{0,4},{1,5},{2,6},{3,7},{4,0},{5,1},{6,2},{7,3},{8,12},{9,13},{10,... | collective-permute-start | bytes 294920 | tf_op jit(solution)/shard_map/ppermute | solution.py:16
  65.7 1.3 %collective-permute-done.20 = bf16[96,256]{1,0:T(8,128)(2,1)S(1)} collective-permute-done((bf16[96,256]{1,0:T(8,128)(2,1)S(1)}, bf16[96,256]{1,0:T(8,128)(2,1)S(1)}, u32[]{:S(2)}, u32[]{:S(2)}) %collective-permute-start.20) | collective-permute-done | bytes 49184 | tf_op jit(solution)/shard_map/ppermute | solution.py:16
  67.0 0.7 collective-permute-start.21
  67.8 0.9 collective-permute-done.17
  69.3 2.6 %collective-permute-done.21 = bf16[2,96,256]{2,1,0:T(8,128)(2,1)S(1)} collective-permute-done((bf16[2,96,256]{2,1,0:T(8,128)(2,1)S(1)}, bf16[2,96,256]{2,1,0:T(8,128)(2,1)S(1)}, u32[]{:S(2)}, u32[]{:S(2)}) %collective-permute-start.21) | collective-permute-done | bytes 98336 | tf_op jit(solution)/shard_map/ppermute | solution.py:16
  71.9 1.3 %collective-permute-start.22 = (bf16[2,2,96,256]{3,2,1,0:T(8,128)(2,1)S(1)}, bf16[2,2,96,256]{3,2,1,0:T(8,128)(2,1)S(1)}, u32[]{:S(2)}, u32[]{:S(2)}) collective-permute-start(bf16[2,2,96,256]{3,2,1,0:T(8,128)(2,1)S(1)} %pad_maximum_fusion.11), channel_id=1, source_target_pairs={{0,4},{1,5},{2,6},{3,7},{4,0},{5,1},{6,2},{7,3},{8,12},{9,13},{10,... | collective-permute-start | bytes 589832 | tf_op jit(solution)/shard_map/ppermute | solution.py:16
  73.2 1.2 collective-permute-done.18
  74.6 3.0 %collective-permute-done.22 = bf16[2,2,96,256]{3,2,1,0:T(8,128)(2,1)S(1)} collective-permute-done((bf16[2,2,96,256]{3,2,1,0:T(8,128)(2,1)S(1)}, bf16[2,2,96,256]{3,2,1,0:T(8,128)(2,1)S(1)}, u32[]{:S(2)}, u32[]{:S(2)}) %collective-permute-start.22) | collective-permute-done | bytes 196640 | tf_op jit(solution)/shard_map/ppermute | solution.py:16
  78.2 1.3 %collective-permute-done.23 = bf16[2,2,2,96,256]{4,3,2,1,0:T(8,128)(2,1)S(1)} collective-permute-done((bf16[2,2,2,96,256]{4,3,2,1,0:T(8,128)(2,1)S(1)}, bf16[2,2,2,96,256]{4,3,2,1,0:T(8,128)(2,1)S(1)}, u32[]{:S(2)}, u32[]{:S(2)}) %collective-permute-start.23) | collective-permute-done | bytes 393248 | tf_op jit(solution)/shard_map/ppermute | solution.py:16
  79.9 0.9 copy.34
  80.9 3.0 %convolution_bitcast_fusion = f32[1536,256]{0,1:T(8,128)S(1)} fusion(bf16[3,512,1536]{2,1,0:T(8,128)(2,1)} %param.5, bf16[1536,256]{1,0:T(8,128)(2,1)S(1)} %bitcast.248, f32[256]{0:T(256)S(1)} %add_rsqrt_fusion.1), kind=kOutput, calls=%fused_computation | convolution fusion | flops 805568512 | bytes 5506048 | tf_op jit(solution)/shard_map/dot_general | solution.py:10
  84.4 0.8 fusion.51
  85.3 4.4 %convolution_bitcast_fusion.1 = f32[1536,256]{0,1:T(8,128)} fusion(bf16[3,512,1536]{2,1,0:T(8,128)(2,1)} %param.5, bf16[1536,256]{1,0:T(8,128)(2,1)} %bitcast.247, f32[256]{0:T(256)} %copy-done.4), kind=kOutput, calls=%fused_computation.1 | convolution fusion | flops 805568512 | bytes 5506048 | tf_op jit(solution)/shard_map/dot_general | solution.py:10
  89.7 1.9 %copy.38 = f32[1536,256]{1,0:T(8,128)S(1)} copy(f32[1536,256]{0,1:T(8,128)} %convolution_bitcast_fusion.1) | data formatting | bytes 3145728 | tf_op jit(solution)/shard_map/dot_general | solution.py:10
  92.3 1.3 %collective-permute-start.29 = (bf16[2,2,96,256]{3,2,0,1:T(8,128)(2,1)S(1)}, bf16[2,2,96,256]{3,2,0,1:T(8,128)(2,1)S(1)}, u32[]{:S(2)}, u32[]{:S(2)}) collective-permute-start(bf16[2,2,96,256]{3,2,0,1:T(8,128)(2,1)S(1)} %fusion.57), channel_id=1, source_target_pairs={{0,4},{1,5},{2,6},{3,7},{4,0},{5,1},{6,2},{7,3},{8,12},{9,13},{10,... | collective-permute-start | bytes 589832 | tf_op jit(solution)/shard_map/ppermute | solution.py:16
  94.3 5.0 %collective-permute-done.29 = bf16[2,2,96,256]{3,2,0,1:T(8,128)(2,1)S(1)} collective-permute-done((bf16[2,2,96,256]{3,2,0,1:T(8,128)(2,1)S(1)}, bf16[2,2,96,256]{3,2,0,1:T(8,128)(2,1)S(1)}, u32[]{:S(2)}, u32[]{:S(2)}) %collective-permute-start.29) | collective-permute-done | bytes 196640 | tf_op jit(solution)/shard_map/ppermute | solution.py:16
  99.4 0.6 collective-permute-start.30
  100.0 0.8 collective-permute-done.25
  100.9 1.3 %collective-permute-start.26 = (bf16[2,96,256]{2,1,0:T(8,128)(2,1)S(1)}, bf16[2,96,256]{2,1,0:T(8,128)(2,1)S(1)}, u32[]{:S(2)}, u32[]{:S(2)}) collective-permute-start(bf16[2,96,256]{2,1,0:T(8,128)(2,1)S(1)} %fusion.60), channel_id=1, source_target_pairs={{0,4},{1,5},{2,6},{3,7},{4,0},{5,1},{6,2},{7,3},{8,12},{9,13},{10,... | collective-permute-start | bytes 294920 | tf_op jit(solution)/shard_map/ppermute | solution.py:16
  102.2 1.9 %collective-permute-done.30 = bf16[2,96,256]{2,1,0:T(8,128)(2,1)S(1)} collective-permute-done((bf16[2,96,256]{2,1,0:T(8,128)(2,1)S(1)}, bf16[2,96,256]{2,1,0:T(8,128)(2,1)S(1)}, u32[]{:S(2)}, u32[]{:S(2)}) %collective-permute-start.30) | collective-permute-done | bytes 98336 | tf_op jit(solution)/shard_map/ppermute | solution.py:16
  104.1 1.8 %collective-permute-start.31 = (bf16[96,256]{1,0:T(8,128)(2,1)S(1)}, bf16[96,256]{1,0:T(8,128)(2,1)S(1)}, u32[]{:S(2)}, u32[]{:S(2)}) collective-permute-start(bf16[96,256]{1,0:T(8,128)(2,1)S(1)} %fusion.65), channel_id=1, source_target_pairs={{0,8},{1,9},{2,10},{3,11},{4,12},{5,13},{6,14},{7,15},{8,0},{9,1},... | collective-permute-start | bytes 147464 | tf_op jit(solution)/shard_map/ppermute | solution.py:16
  106.0 1.8 %collective-permute-start.27 = (bf16[96,256]{1,0:T(8,128)(2,1)S(1)}, bf16[96,256]{1,0:T(8,128)(2,1)S(1)}, u32[]{:S(2)}, u32[]{:S(2)}) collective-permute-start(bf16[96,256]{1,0:T(8,128)(2,1)S(1)} %fusion.64), channel_id=1, source_target_pairs={{0,8},{1,9},{2,10},{3,11},{4,12},{5,13},{6,14},{7,15},{8,0},{9,1},... | collective-permute-start | bytes 147464 | tf_op jit(solution)/shard_map/ppermute | solution.py:16
  107.9 2.2 %collective-permute-done.31 = bf16[96,256]{1,0:T(8,128)(2,1)S(1)} collective-permute-done((bf16[96,256]{1,0:T(8,128)(2,1)S(1)}, bf16[96,256]{1,0:T(8,128)(2,1)S(1)}, u32[]{:S(2)}, u32[]{:S(2)}) %collective-permute-start.31) | collective-permute-done | bytes 49184 | tf_op jit(solution)/shard_map/ppermute | solution.py:16
  110.1 0.9 collective-permute-done.27
  111.2 1.8 %collective-permute-start.33 = (f32[256]{0:T(256)S(1)}, f32[256]{0:T(256)S(1)}, u32[]{:S(2)}, u32[]{:S(2)}) collective-permute-start(f32[256]{0:T(256)S(1)} %add.192), channel_id=1, source_target_pairs={{0,2},{1,3},{2,0},{3,1},{4,6},{5,7},{6,4},{7,5},{8,10},{9,11},{10,... | collective-permute-start | bytes 3080 | tf_op jit(solution)/shard_map/ppermute | solution.py:16
  113.1 1.1 collective-permute-done.34
  114.2 0.7 collective-permute-done.33
  114.9 2.0 %collective-permute-start.37 = (f32[256]{0:T(256)S(1)}, f32[256]{0:T(256)S(1)}, u32[]{:S(2)}, u32[]{:S(2)}) collective-permute-start(f32[256]{0:T(256)S(1)} %add_add_fusion), channel_id=1, source_target_pairs={{0,12},{1,13},{2,14},{3,15},{4,8},{5,9},{6,10},{7,11},{8,4},{9,5},... | collective-permute-start | bytes 3080 | tf_op jit(solution)/shard_map/ppermute | solution.py:16
  116.9 0.6 collective-permute-start.36
  117.5 1.8 %collective-permute-start.35 = (f32[256]{0:T(256)S(1)}, f32[256]{0:T(256)S(1)}, u32[]{:S(2)}, u32[]{:S(2)}) collective-permute-start(f32[256]{0:T(256)S(1)} %add_add_fusion), channel_id=1, source_target_pairs={{0,4},{1,5},{2,6},{3,7},{4,0},{5,1},{6,2},{7,3},{8,12},{9,13},{10,... | collective-permute-start | bytes 3080 | tf_op jit(solution)/shard_map/ppermute | solution.py:16
  119.3 1.0 collective-permute-done.37
  120.3 1.0 collective-permute-done.36
  121.4 0.7 broadcast_multiply_fusion
  (108 shorter events, 8.0 us)
Async XLA Ops:
  0.6 6.9 %collective-permute-start.8 = (bf16[96,256]{1,0:T(8,128)(2,1)}, bf16[96,256]{1,0:T(8,128)(2,1)S(1)}, u32[]{:S(2)}, u32[]{:S(2)}) collective-permute-start(bf16[96,256]{1,0:T(8,128)(2,1)} %param.7), channel_id=1, source_target_pairs={{0,8},{1,9},{2,10},{3,11},{4,12},{5,13},{6,14},{7,15},{8,0},{9,1},... | collective-permute-start | bytes 147464 | tf_op jit(solution)/shard_map/ppermute | solution.py:16
  4.7 5.4 %collective-permute-start = (bf16[96,256]{1,0:T(8,128)(2,1)}, bf16[96,256]{1,0:T(8,128)(2,1)S(1)}, u32[]{:S(2)}, u32[]{:S(2)}) collective-permute-start(bf16[96,256]{1,0:T(8,128)(2,1)} %param.6), channel_id=1, source_target_pairs={{0,8},{1,9},{2,10},{3,11},{4,12},{5,13},{6,14},{7,15},{8,0},{9,1},... | collective-permute-start | bytes 147464 | tf_op jit(solution)/shard_map/ppermute | solution.py:16
  8.4 4.7 %collective-permute-start.9 = (bf16[2,96,256]{2,1,0:T(8,128)(2,1)S(1)}, bf16[2,96,256]{2,1,0:T(8,128)(2,1)S(1)}, u32[]{:S(2)}, u32[]{:S(2)}) collective-permute-start(bf16[2,96,256]{2,1,0:T(8,128)(2,1)S(1)} %pad_maximum_fusion.13), channel_id=1, source_target_pairs={{0,2},{1,3},{2,0},{3,1},{4,6},{5,7},{6,4},{7,5},{8,10},{9,11},{10,... | collective-permute-start | bytes 294920 | tf_op jit(solution)/shard_map/ppermute | solution.py:16
  11.0 9.1 %copy-start = (f32[2,1536]{1,0:T(2,128)S(1)}, f32[2,1536]{1,0:T(2,128)}, u32[]{:S(2)}) copy-start(f32[2,1536]{1,0:T(2,128)} %param.8) | copy-start | bytes 36868
  11.0 9.1 %copy-start.1 = (f32[2,1536]{1,0:T(2,128)S(1)}, f32[2,1536]{1,0:T(2,128)}, u32[]{:S(2)}) copy-start(f32[2,1536]{1,0:T(2,128)} %param.9) | copy-start | bytes 36868
  11.0 5.3 %collective-permute-start.1 = (bf16[2,96,256]{2,1,0:T(8,128)(2,1)S(1)}, bf16[2,96,256]{2,1,0:T(8,128)(2,1)S(1)}, u32[]{:S(2)}, u32[]{:S(2)}) collective-permute-start(bf16[2,96,256]{2,1,0:T(8,128)(2,1)S(1)} %pad_maximum_fusion.12), channel_id=1, source_target_pairs={{0,4},{1,5},{2,6},{3,7},{4,0},{5,1},{6,2},{7,3},{8,12},{9,13},{10,... | collective-permute-start | bytes 294920 | tf_op jit(solution)/shard_map/ppermute | solution.py:16
  13.1 6.8 %collective-permute-start.10 = (bf16[2,2,96,256]{3,2,1,0:T(8,128)(2,1)S(1)}, bf16[2,2,96,256]{3,2,1,0:T(8,128)(2,1)S(1)}, u32[]{:S(2)}, u32[]{:S(2)}) collective-permute-start(bf16[2,2,96,256]{3,2,1,0:T(8,128)(2,1)S(1)} %pad_maximum_fusion.9), channel_id=1, source_target_pairs={{0,4},{1,5},{2,6},{3,7},{4,0},{5,1},{6,2},{7,3},{8,12},{9,13},{10,... | collective-permute-start | bytes 589832 | tf_op jit(solution)/shard_map/ppermute | solution.py:16
  16.4 5.7 %collective-permute-start.2 = (bf16[2,2,96,256]{3,2,0,1:T(8,128)(2,1)S(1)}, bf16[2,2,96,256]{3,2,0,1:T(8,128)(2,1)S(1)}, u32[]{:S(2)}, u32[]{:S(2)}) collective-permute-start(bf16[2,2,96,256]{3,2,0,1:T(8,128)(2,1)S(1)} %pad_maximum_fusion.8), channel_id=1, source_target_pairs={{0,2},{1,3},{2,0},{3,1},{4,6},{5,7},{6,4},{7,5},{8,10},{9,11},{10,... | collective-permute-start | bytes 589832 | tf_op jit(solution)/shard_map/ppermute | solution.py:16
  20.0 3.0 %collective-permute-start.11 = (bf16[2,2,2,96,256]{4,3,2,0,1:T(8,128)(2,1)S(1)}, bf16[2,2,2,96,256]{4,3,2,0,1:T(8,128)(2,1)S(1)}, u32[]{:S(2)}, u32[]{:S(2)}) collective-permute-start(bf16[2,2,2,96,256]{4,3,2,0,1:T(8,128)(2,1)S(1)} %pad_maximum_fusion.5), channel_id=1, source_target_pairs={{0,1},{1,0},{2,3},{3,2},{4,5},{5,4},{6,7},{7,6},{8,9},{9,8},{10,11... | collective-permute-start | bytes 1179656 | tf_op jit(solution)/shard_map/ppermute | solution.py:16
  23.0 5.0 %collective-permute-start.3 = (bf16[2,2,2,96,256]{4,3,2,1,0:T(8,128)(2,1)}, bf16[2,2,2,96,256]{4,3,2,1,0:T(8,128)(2,1)}, u32[]{:S(2)}, u32[]{:S(2)}) collective-permute-start(bf16[2,2,2,96,256]{4,3,2,1,0:T(8,128)(2,1)} %copy.43), channel_id=1, source_target_pairs={{0,1},{1,0},{2,3},{3,2},{4,5},{5,4},{6,7},{7,6},{8,9},{9,8},{10,11... | collective-permute-start | bytes 1179656 | tf_op jit(solution)/shard_map/ppermute | solution.py:16
  27.5 10.0 %collective-permute-start.12 = (bf16[2,2,2,96,256]{4,3,0,2,1:T(8,128)(2,1)}, bf16[2,2,2,96,256]{4,3,0,2,1:T(8,128)(2,1)S(1)}, u32[]{:S(2)}, u32[]{:S(2)}) collective-permute-start(bf16[2,2,2,96,256]{4,3,0,2,1:T(8,128)(2,1)} %fusion.50), channel_id=1, source_target_pairs={{0,1},{1,0},{2,3},{3,2},{4,5},{5,4},{6,7},{7,6},{8,9},{9,8},{10,11... | collective-permute-start | bytes 1179656 | tf_op jit(solution)/shard_map/ppermute | solution.py:16
  36.0 3.9 %collective-permute-start.4 = (bf16[2,2,2,96,256]{4,3,0,1,2:T(8,128)(2,1)}, bf16[2,2,2,96,256]{4,3,0,1,2:T(8,128)(2,1)}, u32[]{:S(2)}, u32[]{:S(2)}) collective-permute-start(bf16[2,2,2,96,256]{4,3,0,1,2:T(8,128)(2,1)} %fusion.49), channel_id=1, source_target_pairs={{0,1},{1,0},{2,3},{3,2},{4,5},{5,4},{6,7},{7,6},{8,9},{9,8},{10,11... | collective-permute-start | bytes 1179656 | tf_op jit(solution)/shard_map/ppermute | solution.py:16
  37.6 7.9 %collective-permute-start.13 = (bf16[2,2,96,256]{3,2,0,1:T(8,128)(2,1)S(1)}, bf16[2,2,96,256]{3,2,0,1:T(8,128)(2,1)S(1)}, u32[]{:S(2)}, u32[]{:S(2)}) collective-permute-start(bf16[2,2,96,256]{3,2,0,1:T(8,128)(2,1)S(1)} %fusion.55), channel_id=1, source_target_pairs={{0,4},{1,5},{2,6},{3,7},{4,0},{5,1},{6,2},{7,3},{8,12},{9,13},{10,... | collective-permute-start | bytes 589832 | tf_op jit(solution)/shard_map/ppermute | solution.py:16
  41.0 17.7 %copy-start.2 = (f32[96]{0:T(128)S(1)}, f32[96]{0:T(128)}, u32[]{:S(2)}) copy-start(f32[96]{0:T(128)} %get-tuple-element.48) | copy-start | bytes 1156
  41.1 17.7 %copy-start.3 = (f32[96]{0:T(128)S(1)}, f32[96]{0:T(128)}, u32[]{:S(2)}) copy-start(f32[96]{0:T(128)} %get-tuple-element.49) | copy-start | bytes 1156
  41.1 7.1 %collective-permute-start.5 = (bf16[2,2,96,256]{3,2,0,1:T(8,128)(2,1)S(1)}, bf16[2,2,96,256]{3,2,0,1:T(8,128)(2,1)S(1)}, u32[]{:S(2)}, u32[]{:S(2)}) collective-permute-start(bf16[2,2,96,256]{3,2,0,1:T(8,128)(2,1)S(1)} %fusion.54), channel_id=1, source_target_pairs={{0,2},{1,3},{2,0},{3,1},{4,6},{5,7},{6,4},{7,5},{8,10},{9,11},{10,... | collective-permute-start | bytes 589832 | tf_op jit(solution)/shard_map/ppermute | solution.py:16
  45.6 4.7 %collective-permute-start.14 = (bf16[2,96,256]{2,1,0:T(8,128)(2,1)S(1)}, bf16[2,96,256]{2,1,0:T(8,128)(2,1)S(1)}, u32[]{:S(2)}, u32[]{:S(2)}) collective-permute-start(bf16[2,96,256]{2,1,0:T(8,128)(2,1)S(1)} %fusion.59), channel_id=1, source_target_pairs={{0,2},{1,3},{2,0},{3,1},{4,6},{5,7},{6,4},{7,5},{8,10},{9,11},{10,... | collective-permute-start | bytes 294920 | tf_op jit(solution)/shard_map/ppermute | solution.py:16
  48.2 5.4 %collective-permute-start.6 = (bf16[2,96,256]{2,1,0:T(8,128)(2,1)S(1)}, bf16[2,96,256]{2,1,0:T(8,128)(2,1)S(1)}, u32[]{:S(2)}, u32[]{:S(2)}) collective-permute-start(bf16[2,96,256]{2,1,0:T(8,128)(2,1)S(1)} %fusion.58), channel_id=1, source_target_pairs={{0,4},{1,5},{2,6},{3,7},{4,0},{5,1},{6,2},{7,3},{8,12},{9,13},{10,... | collective-permute-start | bytes 294920 | tf_op jit(solution)/shard_map/ppermute | solution.py:16
  50.3 7.0 %collective-permute-start.15 = (bf16[96,256]{1,0:T(8,128)(2,1)S(1)}, bf16[96,256]{1,0:T(8,128)(2,1)S(1)}, u32[]{:S(2)}, u32[]{:S(2)}) collective-permute-start(bf16[96,256]{1,0:T(8,128)(2,1)S(1)} %fusion.63), channel_id=1, source_target_pairs={{0,8},{1,9},{2,10},{3,11},{4,12},{5,13},{6,14},{7,15},{8,0},{9,1},... | collective-permute-start | bytes 147464 | tf_op jit(solution)/shard_map/ppermute | solution.py:16
  53.7 5.1 %collective-permute-start.7 = (bf16[96,256]{1,0:T(8,128)(2,1)S(1)}, bf16[96,256]{1,0:T(8,128)(2,1)S(1)}, u32[]{:S(2)}, u32[]{:S(2)}) collective-permute-start(bf16[96,256]{1,0:T(8,128)(2,1)S(1)} %fusion.62), channel_id=1, source_target_pairs={{0,8},{1,9},{2,10},{3,11},{4,12},{5,13},{6,14},{7,15},{8,0},{9,1},... | collective-permute-start | bytes 147464 | tf_op jit(solution)/shard_map/ppermute | solution.py:16
  58.9 5.1 %collective-permute-start.16 = (bf16[96,256]{1,0:T(8,128)(2,1)S(1)}, bf16[96,256]{1,0:T(8,128)(2,1)S(1)}, u32[]{:S(2)}, u32[]{:S(2)}) collective-permute-start(bf16[96,256]{1,0:T(8,128)(2,1)S(1)} %get-tuple-element.16), channel_id=1, source_target_pairs={{0,8},{1,9},{2,10},{3,11},{4,12},{5,13},{6,14},{7,15},{8,0},{9,1},... | collective-permute-start | bytes 147464 | tf_op jit(solution)/shard_map/ppermute | solution.py:16
  61.7 5.3 %collective-permute-start.20 = (bf16[96,256]{1,0:T(8,128)(2,1)S(1)}, bf16[96,256]{1,0:T(8,128)(2,1)S(1)}, u32[]{:S(2)}, u32[]{:S(2)}) collective-permute-start(bf16[96,256]{1,0:T(8,128)(2,1)S(1)} %get-tuple-element.17), channel_id=1, source_target_pairs={{0,8},{1,9},{2,10},{3,11},{4,12},{5,13},{6,14},{7,15},{8,0},{9,1},... | collective-permute-start | bytes 147464 | tf_op jit(solution)/shard_map/ppermute | solution.py:16
  64.0 4.7 %collective-permute-start.17 = (bf16[2,96,256]{2,1,0:T(8,128)(2,1)S(1)}, bf16[2,96,256]{2,1,0:T(8,128)(2,1)S(1)}, u32[]{:S(2)}, u32[]{:S(2)}) collective-permute-start(bf16[2,96,256]{2,1,0:T(8,128)(2,1)S(1)} %pad_maximum_fusion.14), channel_id=1, source_target_pairs={{0,4},{1,5},{2,6},{3,7},{4,0},{5,1},{6,2},{7,3},{8,12},{9,13},{10,... | collective-permute-start | bytes 294920 | tf_op jit(solution)/shard_map/ppermute | solution.py:16
  67.0 4.8 %collective-permute-start.21 = (bf16[2,96,256]{2,1,0:T(8,128)(2,1)S(1)}, bf16[2,96,256]{2,1,0:T(8,128)(2,1)S(1)}, u32[]{:S(2)}, u32[]{:S(2)}) collective-permute-start(bf16[2,96,256]{2,1,0:T(8,128)(2,1)S(1)} %pad_maximum_fusion.15), channel_id=1, source_target_pairs={{0,2},{1,3},{2,0},{3,1},{4,6},{5,7},{6,4},{7,5},{8,10},{9,11},{10,... | collective-permute-start | bytes 294920 | tf_op jit(solution)/shard_map/ppermute | solution.py:16
  68.7 5.7 %collective-permute-start.18 = (bf16[2,2,96,256]{3,2,0,1:T(8,128)(2,1)S(1)}, bf16[2,2,96,256]{3,2,0,1:T(8,128)(2,1)S(1)}, u32[]{:S(2)}, u32[]{:S(2)}) collective-permute-start(bf16[2,2,96,256]{3,2,0,1:T(8,128)(2,1)S(1)} %pad_maximum_fusion.10), channel_id=1, source_target_pairs={{0,2},{1,3},{2,0},{3,1},{4,6},{5,7},{6,4},{7,5},{8,10},{9,11},{10,... | collective-permute-start | bytes 589832 | tf_op jit(solution)/shard_map/ppermute | solution.py:16
  71.9 5.7 %collective-permute-start.22 = (bf16[2,2,96,256]{3,2,1,0:T(8,128)(2,1)S(1)}, bf16[2,2,96,256]{3,2,1,0:T(8,128)(2,1)S(1)}, u32[]{:S(2)}, u32[]{:S(2)}) collective-permute-start(bf16[2,2,96,256]{3,2,1,0:T(8,128)(2,1)S(1)} %pad_maximum_fusion.11), channel_id=1, source_target_pairs={{0,4},{1,5},{2,6},{3,7},{4,0},{5,1},{6,2},{7,3},{8,12},{9,13},{10,... | collective-permute-start | bytes 589832 | tf_op jit(solution)/shard_map/ppermute | solution.py:16
  74.5 3.3 %collective-permute-start.19 = (bf16[2,2,2,96,256]{4,3,0,1,2:T(8,128)(2,1)S(1)}, bf16[2,2,2,96,256]{4,3,0,1,2:T(8,128)(2,1)S(1)}, u32[]{:S(2)}, u32[]{:S(2)}) collective-permute-start(bf16[2,2,2,96,256]{4,3,0,1,2:T(8,128)(2,1)S(1)} %pad_maximum_fusion.6), channel_id=1, source_target_pairs={{0,1},{1,0},{2,3},{3,2},{4,5},{5,4},{6,7},{7,6},{8,9},{9,8},{10,11... | collective-permute-start | bytes 1179656 | tf_op jit(solution)/shard_map/ppermute | solution.py:16
  77.7 1.8 %collective-permute-start.23 = (bf16[2,2,2,96,256]{4,3,2,1,0:T(8,128)(2,1)S(1)}, bf16[2,2,2,96,256]{4,3,2,1,0:T(8,128)(2,1)S(1)}, u32[]{:S(2)}, u32[]{:S(2)}) collective-permute-start(bf16[2,2,2,96,256]{4,3,2,1,0:T(8,128)(2,1)S(1)} %pad_maximum_fusion.7), channel_id=1, source_target_pairs={{0,1},{1,0},{2,3},{3,2},{4,5},{5,4},{6,7},{7,6},{8,9},{9,8},{10,11... | collective-permute-start | bytes 1179656 | tf_op jit(solution)/shard_map/ppermute | solution.py:16
  80.9 3.0 %copy-start.4 = (f32[256]{0:T(256)}, f32[256]{0:T(256)S(1)}, u32[]{:S(2)}) copy-start(f32[256]{0:T(256)S(1)} %add_rsqrt_fusion.1) | copy-start | bytes 3076
  85.2 7.0 %collective-permute-start.28 = (bf16[2,2,2,96,256]{4,3,0,2,1:T(8,128)(2,1)}, bf16[2,2,2,96,256]{4,3,0,2,1:T(8,128)(2,1)S(1)}, u32[]{:S(2)}, u32[]{:S(2)}) collective-permute-start(bf16[2,2,2,96,256]{4,3,0,2,1:T(8,128)(2,1)} %fusion.51), channel_id=1, source_target_pairs={{0,1},{1,0},{2,3},{3,2},{4,5},{5,4},{6,7},{7,6},{8,9},{9,8},{10,11... | collective-permute-start | bytes 1179656 | tf_op jit(solution)/shard_map/ppermute | solution.py:16
  91.6 2.1 %collective-permute-start.24 = (bf16[2,2,2,96,256]{4,3,2,1,0:T(8,128)(2,1)S(1)}, bf16[2,2,2,96,256]{4,3,2,1,0:T(8,128)(2,1)S(1)}, u32[]{:S(2)}, u32[]{:S(2)}) collective-permute-start(bf16[2,2,2,96,256]{4,3,2,1,0:T(8,128)(2,1)S(1)} %fusion.48), channel_id=1, source_target_pairs={{0,1},{1,0},{2,3},{3,2},{4,5},{5,4},{6,7},{7,6},{8,9},{9,8},{10,11... | collective-permute-start | bytes 1179656 | tf_op jit(solution)/shard_map/ppermute | solution.py:16
  92.3 7.0 %collective-permute-start.29 = (bf16[2,2,96,256]{3,2,0,1:T(8,128)(2,1)S(1)}, bf16[2,2,96,256]{3,2,0,1:T(8,128)(2,1)S(1)}, u32[]{:S(2)}, u32[]{:S(2)}) collective-permute-start(bf16[2,2,96,256]{3,2,0,1:T(8,128)(2,1)S(1)} %fusion.57), channel_id=1, source_target_pairs={{0,4},{1,5},{2,6},{3,7},{4,0},{5,1},{6,2},{7,3},{8,12},{9,13},{10,... | collective-permute-start | bytes 589832 | tf_op jit(solution)/shard_map/ppermute | solution.py:16
  93.8 7.0 %collective-permute-start.25 = (bf16[2,2,96,256]{3,2,1,0:T(8,128)(2,1)S(1)}, bf16[2,2,96,256]{3,2,1,0:T(8,128)(2,1)S(1)}, u32[]{:S(2)}, u32[]{:S(2)}) collective-permute-start(bf16[2,2,96,256]{3,2,1,0:T(8,128)(2,1)S(1)} %fusion.56), channel_id=1, source_target_pairs={{0,2},{1,3},{2,0},{3,1},{4,6},{5,7},{6,4},{7,5},{8,10},{9,11},{10,... | collective-permute-start | bytes 589832 | tf_op jit(solution)/shard_map/ppermute | solution.py:16
  99.4 4.7 %collective-permute-start.30 = (bf16[2,96,256]{2,1,0:T(8,128)(2,1)S(1)}, bf16[2,96,256]{2,1,0:T(8,128)(2,1)S(1)}, u32[]{:S(2)}, u32[]{:S(2)}) collective-permute-start(bf16[2,96,256]{2,1,0:T(8,128)(2,1)S(1)} %fusion.61), channel_id=1, source_target_pairs={{0,2},{1,3},{2,0},{3,1},{4,6},{5,7},{6,4},{7,5},{8,10},{9,11},{10,... | collective-permute-start | bytes 294920 | tf_op jit(solution)/shard_map/ppermute | solution.py:16
  100.9 5.0 %collective-permute-start.26 = (bf16[2,96,256]{2,1,0:T(8,128)(2,1)S(1)}, bf16[2,96,256]{2,1,0:T(8,128)(2,1)S(1)}, u32[]{:S(2)}, u32[]{:S(2)}) collective-permute-start(bf16[2,96,256]{2,1,0:T(8,128)(2,1)S(1)} %fusion.60), channel_id=1, source_target_pairs={{0,4},{1,5},{2,6},{3,7},{4,0},{5,1},{6,2},{7,3},{8,12},{9,13},{10,... | collective-permute-start | bytes 294920 | tf_op jit(solution)/shard_map/ppermute | solution.py:16
  104.1 6.0 %collective-permute-start.31 = (bf16[96,256]{1,0:T(8,128)(2,1)S(1)}, bf16[96,256]{1,0:T(8,128)(2,1)S(1)}, u32[]{:S(2)}, u32[]{:S(2)}) collective-permute-start(bf16[96,256]{1,0:T(8,128)(2,1)S(1)} %fusion.65), channel_id=1, source_target_pairs={{0,8},{1,9},{2,10},{3,11},{4,12},{5,13},{6,14},{7,15},{8,0},{9,1},... | collective-permute-start | bytes 147464 | tf_op jit(solution)/shard_map/ppermute | solution.py:16
  106.0 5.1 %collective-permute-start.27 = (bf16[96,256]{1,0:T(8,128)(2,1)S(1)}, bf16[96,256]{1,0:T(8,128)(2,1)S(1)}, u32[]{:S(2)}, u32[]{:S(2)}) collective-permute-start(bf16[96,256]{1,0:T(8,128)(2,1)S(1)} %fusion.64), channel_id=1, source_target_pairs={{0,8},{1,9},{2,10},{3,11},{4,12},{5,13},{6,14},{7,15},{8,0},{9,1},... | collective-permute-start | bytes 147464 | tf_op jit(solution)/shard_map/ppermute | solution.py:16
  111.2 3.1 %collective-permute-start.34 = (f32[256]{0:T(256)S(1)}, f32[256]{0:T(256)S(1)}, u32[]{:S(2)}, u32[]{:S(2)}) collective-permute-start(f32[256]{0:T(256)S(1)} %add.192), channel_id=1, source_target_pairs={{0,3},{1,2},{2,1},{3,0},{4,7},{5,6},{6,5},{7,4},{8,11},{9,10},{10,... | collective-permute-start | bytes 3080 | tf_op jit(solution)/shard_map/ppermute | solution.py:16
  111.2 3.6 %collective-permute-start.33 = (f32[256]{0:T(256)S(1)}, f32[256]{0:T(256)S(1)}, u32[]{:S(2)}, u32[]{:S(2)}) collective-permute-start(f32[256]{0:T(256)S(1)} %add.192), channel_id=1, source_target_pairs={{0,2},{1,3},{2,0},{3,1},{4,6},{5,7},{6,4},{7,5},{8,10},{9,11},{10,... | collective-permute-start | bytes 3080 | tf_op jit(solution)/shard_map/ppermute | solution.py:16
  113.0 1.9 %collective-permute-start.32 = (f32[256]{0:T(256)S(1)}, f32[256]{0:T(256)S(1)}, u32[]{:S(2)}, u32[]{:S(2)}) collective-permute-start(f32[256]{0:T(256)S(1)} %add.192), channel_id=1, source_target_pairs={{0,1},{1,0},{2,3},{3,2},{4,5},{5,4},{6,7},{7,6},{8,9},{9,8},{10,11... | collective-permute-start | bytes 3080 | tf_op jit(solution)/shard_map/ppermute | solution.py:16
  114.9 5.4 %collective-permute-start.37 = (f32[256]{0:T(256)S(1)}, f32[256]{0:T(256)S(1)}, u32[]{:S(2)}, u32[]{:S(2)}) collective-permute-start(f32[256]{0:T(256)S(1)} %add_add_fusion), channel_id=1, source_target_pairs={{0,12},{1,13},{2,14},{3,15},{4,8},{5,9},{6,10},{7,11},{8,4},{9,5},... | collective-permute-start | bytes 3080 | tf_op jit(solution)/shard_map/ppermute | solution.py:16
  116.9 4.5 %collective-permute-start.36 = (f32[256]{0:T(256)S(1)}, f32[256]{0:T(256)S(1)}, u32[]{:S(2)}, u32[]{:S(2)}) collective-permute-start(f32[256]{0:T(256)S(1)} %add_add_fusion), channel_id=1, source_target_pairs={{0,8},{1,9},{2,10},{3,11},{4,12},{5,13},{6,14},{7,15},{8,0},{9,1},... | collective-permute-start | bytes 3080 | tf_op jit(solution)/shard_map/ppermute | solution.py:16
  117.5 3.8 %collective-permute-start.35 = (f32[256]{0:T(256)S(1)}, f32[256]{0:T(256)S(1)}, u32[]{:S(2)}, u32[]{:S(2)}) collective-permute-start(f32[256]{0:T(256)S(1)} %add_add_fusion), channel_id=1, source_target_pairs={{0,4},{1,5},{2,6},{3,7},{4,0},{5,1},{6,2},{7,3},{8,12},{9,13},{10,... | collective-permute-start | bytes 3080 | tf_op jit(solution)/shard_map/ppermute | solution.py:16

commit v12 on v11

--- a/solution.py
+++ b/solution.py
@@ -34,15 +34,23 @@
 def doubling_all_gather(x, devices, order):
     me = lax.axis_index("row")
     cur = x
-    done = []
-    for bit in order:
-        other = exchange(cur, 1 << bit, devices)
-        low = (me >> bit) & 1 == 0
-        axis = sum(1 for b in done if b > bit)
-        done.append(bit)
-        cur = jnp.stack(
-            [jnp.where(low, cur, other), jnp.where(low, other, cur)], axis=axis
+    axes = []
+    for start in range(0, len(order), 2):
+        group = order[start:start + 2]
+        n = len(group)
+        mine = sum(((me >> bit) & 1) << (n - 1 - k) for k, bit in enumerate(group))
+        blocks = [cur]
+        for digit in range(1, 1 << n):
+            xor = sum(((digit >> (n - 1 - k)) & 1) << bit for k, bit in enumerate(group))
+            blocks.append(exchange(cur, xor, devices))
+        slots = [lax.select_n(slot ^ mine, *blocks) for slot in range(1 << n)]
+        lead = len(axes)
+        cur = jnp.stack(slots, axis=lead).reshape(
+            cur.shape[:lead] + (2,) * n + cur.shape[lead:]
         )
+        axes += group
+    perm = sorted(range(len(axes)), key=lambda k: -axes[k])
+    cur = jnp.transpose(cur, perm + [len(axes), len(axes) + 1])
     return cur.reshape((-1, x.shape[-1]))
 
 

time: 122 us -> 131 us (1.074)
  waiting for transfers between devices: 42.9 us -> 51.3 us
  starting transfers between devices: 44.4 us -> 42.8 us
    ppermute x38 -> x46, waiting for transfers between devices: 42.9 us -> 51.3 us  [exchange(): return lax.ppermute(x, 'row', [(i, i ^ distance) for i in range(devices)])]
    another operation x4 -> x2, local copies, waits for them, and re-layouts: 1.82 us -> 0.11 us  [doubling_all_gather(): jnp.stack(slots, axis=lead)]
    ppermute x38 -> x46, starting transfers between devices: 44.4 us -> 42.8 us  [exchange(): return lax.ppermute(x, 'row', [(i, i ^ distance) for i in range(devices)])]
    dot_general x4, local copies, waits for them, and re-layouts: 4.68 us -> 6.08 us  [contract_rows(): lax.dot_general(left, right, (((0,), (0,)), ((), ())), preferred_element_...]
    another operation x32 -> x15, other arithmetic: 3.75 us -> 3.54 us  [doubling_all_gather(): jnp.stack(slots, axis=lead)]
  transfers between devices with their start and end apart: 38 -> 46, of which waited for: 24 -> 25; matrix products, arithmetic and copies ran while one was open for 22% -> 20% of each run, Pallas kernels for 0% -> 0%
where the time goes in v12:
time: 131 us
  waiting for transfers between devices  51.3 us (39%)
  starting transfers between devices  42.8 us (33%)
  matrix products  15.4 us (12%)
  local copies, waits for them, and re-layouts  11.9 us (9%)
  other arithmetic  8.15 us (6%)
    ppermute x46, waiting for transfers between devices, exchange(): return lax.ppermute(x, 'row', [(i, i ^ distance) for i in range(devices)])  51.3 us
    ppermute x46, starting transfers between devices, exchange(): return lax.ppermute(x, 'row', [(i, i ^ distance) for i in range(devices)])  42.8 us
    dot_general x4, matrix products, contract_rows(): lax.dot_general(left, right, (((0,), (0,)), ((), ())), preferred_element_...  15.4 us
    dot_general x4, local copies, waits for them, and re-layouts, contract_rows(): lax.dot_general(left, right, (((0,), (0,)), ((), ())), preferred_element_...  6.08 us
    another operation x15, other arithmetic, doubling_all_gather(): jnp.stack(slots, axis=lead)  3.54 us
    convert_element_type x16, local copies, waits for them, and re-layouts, halving_reduce_scatter(): send.astype(jnp.bfloat16)  2.75 us
  transfers between devices with their start and end apart: 46, of which 25 were waited for; matrix products, arithmetic and copies ran while one was open for 20% of the time, Pallas kernels for 0%

profile of v12, /device:TPU:0, one launch (start us, length us, event | category | flops | bytes accessed | tf_op | source)
XLA Modules:
  0.0 130.8 jit_solution(2202879204527592024)
XLA Ops:
  0.6 3.0 %collective-permute-start.10 = (bf16[96,256]{1,0:T(8,128)(2,1)}, bf16[96,256]{1,0:T(8,128)(2,1)S(1)}, u32[]{:S(2)}, u32[]{:S(2)}) collective-permute-start(bf16[96,256]{1,0:T(8,128)(2,1)} %param.7), channel_id=1, source_target_pairs={{0,2},{1,3},{2,0},{3,1},{4,6},{5,7},{6,4},{7,5},{8,10},{9,11},{10,... | collective-permute-start | bytes 147464 | tf_op jit(solution)/shard_map/ppermute | solution.py:16
  3.7 2.6 %collective-permute-start.11 = (bf16[96,256]{1,0:T(8,128)(2,1)}, bf16[96,256]{1,0:T(8,128)(2,1)S(1)}, u32[]{:S(2)}, u32[]{:S(2)}) collective-permute-start(bf16[96,256]{1,0:T(8,128)(2,1)} %param.7), channel_id=1, source_target_pairs={{0,8},{1,9},{2,10},{3,11},{4,12},{5,13},{6,14},{7,15},{8,0},{9,1},... | collective-permute-start | bytes 147464 | tf_op jit(solution)/shard_map/ppermute | solution.py:16
  6.3 1.9 %collective-permute-start = (bf16[96,256]{1,0:T(8,128)(2,1)}, bf16[96,256]{1,0:T(8,128)(2,1)S(1)}, u32[]{:S(2)}, u32[]{:S(2)}) collective-permute-start(bf16[96,256]{1,0:T(8,128)(2,1)} %param.6), channel_id=1, source_target_pairs={{0,4},{1,5},{2,6},{3,7},{4,0},{5,1},{6,2},{7,3},{8,12},{9,13},{10,... | collective-permute-start | bytes 147464 | tf_op jit(solution)/shard_map/ppermute | solution.py:16
  8.1 2.6 %collective-permute-start.1 = (bf16[96,256]{1,0:T(8,128)(2,1)}, bf16[96,256]{1,0:T(8,128)(2,1)S(1)}, u32[]{:S(2)}, u32[]{:S(2)}) collective-permute-start(bf16[96,256]{1,0:T(8,128)(2,1)} %param.6), channel_id=1, source_target_pairs={{0,8},{1,9},{2,10},{3,11},{4,12},{5,13},{6,14},{7,15},{8,0},{9,1},... | collective-permute-start | bytes 147464 | tf_op jit(solution)/shard_map/ppermute | solution.py:16
  10.7 1.4 %fusion.70 = (f32[1,1536]{1,0:T(1,128)S(1)}, f32[1,1536]{1,0:T(1,128)}, f32[1,1536]{1,0:T(1,128)}, f32[1,1536]{1,0:T(1,128)S(1)}) fusion(f32[2,1536]{1,0:T(2,128)} %param.8, f32[2,1536]{1,0:T(2,128)} %param.9), kind=kLoop, calls=%fused_computation.151 | loop fusion | bytes 49152 | tf_op jit(solution)/shard_map/slice | solution.py:96
  12.1 1.7 %collective-permute-done.12 = bf16[96,256]{1,0:T(8,128)(2,1)S(1)} collective-permute-done((bf16[96,256]{1,0:T(8,128)(2,1)}, bf16[96,256]{1,0:T(8,128)(2,1)S(1)}, u32[]{:S(2)}, u32[]{:S(2)}) %collective-permute-start.12) | collective-permute-done | bytes 49184 | tf_op jit(solution)/shard_map/ppermute | solution.py:16
  13.8 0.8 select_bitcast_fusion.27
  14.9 1.6 %collective-permute-start.15 = (bf16[2,2,96,256]{3,2,1,0:T(8,128)(2,1)S(1)}, bf16[2,2,96,256]{3,2,1,0:T(8,128)(2,1)S(1)}, u32[]{:S(2)}, u32[]{:S(2)}) collective-permute-start(bf16[2,2,96,256]{3,2,1,0:T(8,128)(2,1)S(1)} %bitcast.273), channel_id=1, source_target_pairs={{0,5},{1,4},{2,7},{3,6},{4,1},{5,0},{6,3},{7,2},{8,13},{9,12},{10,... | collective-permute-start | bytes 589832 | tf_op jit(solution)/shard_map/ppermute | solution.py:16
  16.6 1.6 %collective-permute-done.2 = bf16[96,256]{1,0:T(8,128)(2,1)S(1)} collective-permute-done((bf16[96,256]{1,0:T(8,128)(2,1)}, bf16[96,256]{1,0:T(8,128)(2,1)S(1)}, u32[]{:S(2)}, u32[]{:S(2)}) %collective-permute-start.2) | collective-permute-done | bytes 49184 | tf_op jit(solution)/shard_map/ppermute | solution.py:16
  18.2 0.8 select_bitcast_fusion.31
  19.2 1.7 %collective-permute-start.4 = (bf16[2,2,96,256]{3,2,1,0:T(8,128)(2,1)S(1)}, bf16[2,2,96,256]{3,2,1,0:T(8,128)(2,1)}, u32[]{:S(2)}, u32[]{:S(2)}) collective-permute-start(bf16[2,2,96,256]{3,2,1,0:T(8,128)(2,1)S(1)} %bitcast.276), channel_id=1, source_target_pairs={{0,2},{1,3},{2,0},{3,1},{4,6},{5,7},{6,4},{7,5},{8,10},{9,11},{10,... | collective-permute-start | bytes 589832 | tf_op jit(solution)/shard_map/ppermute | solution.py:16
  21.1 1.5 %collective-permute-done.14 = bf16[2,2,96,256]{3,2,1,0:T(8,128)(2,1)S(1)} collective-permute-done((bf16[2,2,96,256]{3,2,1,0:T(8,128)(2,1)S(1)}, bf16[2,2,96,256]{3,2,1,0:T(8,128)(2,1)S(1)}, u32[]{:S(2)}, u32[]{:S(2)}) %collective-permute-start.14) | collective-permute-done | bytes 196640 | tf_op jit(solution)/shard_map/ppermute | solution.py:16
  22.6 3.9 %collective-permute-done.15 = bf16[2,2,96,256]{3,2,1,0:T(8,128)(2,1)S(1)} collective-permute-done((bf16[2,2,96,256]{3,2,1,0:T(8,128)(2,1)S(1)}, bf16[2,2,96,256]{3,2,1,0:T(8,128)(2,1)S(1)}, u32[]{:S(2)}, u32[]{:S(2)}) %collective-permute-start.15) | collective-permute-done | bytes 196640 | tf_op jit(solution)/shard_map/ppermute | solution.py:16
  26.8 3.0 %convolution_bitcast_fusion.2 = f32[1536,256]{0,1:T(8,128)S(1)} fusion(bf16[1536,256]{1,0:T(8,128)(2,1)S(1)} %bitcast.282, bf16[3,512,1536]{2,1,0:T(8,128)(2,1)} %param.5), kind=kOutput, calls=%fused_computation.2 | convolution fusion | flops 805437440 | bytes 5505024 | tf_op jit(solution)/shard_map/dot_general | solution.py:10
  30.2 0.8 fusion.50
  31.4 1.1 select_bitcast_fusion.15
  32.6 4.2 %convolution_bitcast_fusion.3 = f32[1536,256]{0,1:T(8,128)} fusion(bf16[1536,256]{1,0:T(8,128)(2,1)S(1)} %bitcast.280, bf16[3,512,1536]{2,1,0:T(8,128)(2,1)} %param.5), kind=kOutput, calls=%fused_computation.3 | convolution fusion | flops 805437440 | bytes 5505024 | tf_op jit(solution)/shard_map/dot_general | solution.py:10
  36.8 1.9 %copy.30 = f32[1536,256]{1,0:T(8,128)S(1)} copy(f32[1536,256]{0,1:T(8,128)} %convolution_bitcast_fusion.3) | data formatting | bytes 3145728 | tf_op jit(solution)/shard_map/dot_general | solution.py:10
  38.7 0.8 fusion.48
  39.6 1.4 %bitcast_divide_fusion.1 = (f32[96]{0:T(128)}, f32[96]{0:T(128)}) fusion(f32[1,1536]{1,0:T(1,128)} %get-tuple-element.54, s32[]{:T(128)S(6)} %select_n.731, f32[1,1536]{1,0:T(1,128)} %get-tuple-element.47), kind=kLoop, calls=%fused_computation.146 | loop fusion | flops 288 | bytes 1540 | tf_op jit(solution)/shard_map/div | solution.py:101
  41.0 1.1 bitcast_add_fusion.2
  42.4 0.8 collective-permute-start.7
  43.2 6.2 %collective-permute-done.17 = bf16[2,2,96,256]{3,2,0,1:T(8,128)(2,1)S(1)} collective-permute-done((bf16[2,2,96,256]{3,2,0,1:T(8,128)(2,1)S(1)}, bf16[2,2,96,256]{3,2,0,1:T(8,128)(2,1)S(1)}, u32[]{:S(2)}, u32[]{:S(2)}) %collective-permute-start.17) | collective-permute-done | bytes 196640 | tf_op jit(solution)/shard_map/ppermute | solution.py:16
  49.5 0.8 collective-permute-start.18
  50.3 1.2 collective-permute-start.8
  51.5 2.6 %collective-permute-done.18 = bf16[2,96,256]{2,1,0:T(8,128)(2,1)S(1)} collective-permute-done((bf16[2,96,256]{2,1,0:T(8,128)(2,1)S(1)}, bf16[2,96,256]{2,1,0:T(8,128)(2,1)S(1)}, u32[]{:S(2)}, u32[]{:S(2)}) %collective-permute-start.18) | collective-permute-done | bytes 98336 | tf_op jit(solution)/shard_map/ppermute | solution.py:16
  54.2 0.7 collective-permute-start.19
  55.0 2.3 %collective-permute-start.9 = (bf16[96,256]{1,0:T(8,128)(2,1)S(1)}, bf16[96,256]{1,0:T(8,128)(2,1)S(1)}, u32[]{:S(2)}, u32[]{:S(2)}) collective-permute-start(bf16[96,256]{1,0:T(8,128)(2,1)S(1)} %fusion.62), channel_id=1, source_target_pairs={{0,8},{1,9},{2,10},{3,11},{4,12},{5,13},{6,14},{7,15},{8,0},{9,1},... | collective-permute-start | bytes 147464 | tf_op jit(solution)/shard_map/ppermute | solution.py:16
  57.3 0.8 cosine_bitcast_fusion
  58.1 1.4 %collective-permute-done.19 = bf16[96,256]{1,0:T(8,128)(2,1)S(1)} collective-permute-done((bf16[96,256]{1,0:T(8,128)(2,1)S(1)}, bf16[96,256]{1,0:T(8,128)(2,1)S(1)}, u32[]{:S(2)}, u32[]{:S(2)}) %collective-permute-start.19) | collective-permute-done | bytes 49184 | tf_op jit(solution)/shard_map/ppermute | solution.py:16
  60.2 1.6 %collective-permute-start.26 = (bf16[96,256]{1,0:T(8,128)(2,1)S(1)}, bf16[96,256]{1,0:T(8,128)(2,1)S(1)}, u32[]{:S(2)}, u32[]{:S(2)}) collective-permute-start(bf16[96,256]{1,0:T(8,128)(2,1)S(1)} %get-tuple-element.27), channel_id=1, source_target_pairs={{0,2},{1,3},{2,0},{3,1},{4,6},{5,7},{6,4},{7,5},{8,10},{9,11},{10,... | collective-permute-start | bytes 147464 | tf_op jit(solution)/shard_map/ppermute | solution.py:16
  61.8 2.1 %collective-permute-start.27 = (bf16[96,256]{1,0:T(8,128)(2,1)S(1)}, bf16[96,256]{1,0:T(8,128)(2,1)S(1)}, u32[]{:S(2)}, u32[]{:S(2)}) collective-permute-start(bf16[96,256]{1,0:T(8,128)(2,1)S(1)} %get-tuple-element.27), channel_id=1, source_target_pairs={{0,8},{1,9},{2,10},{3,11},{4,12},{5,13},{6,14},{7,15},{8,0},{9,1},... | collective-permute-start | bytes 147464 | tf_op jit(solution)/shard_map/ppermute | solution.py:16
  63.9 0.8 collective-permute-start.28
  64.7 1.6 %collective-permute-start.20 = (bf16[96,256]{1,0:T(8,128)(2,1)S(1)}, bf16[96,256]{1,0:T(8,128)(2,1)S(1)}, u32[]{:S(2)}, u32[]{:S(2)}) collective-permute-start(bf16[96,256]{1,0:T(8,128)(2,1)S(1)} %get-tuple-element.26), channel_id=1, source_target_pairs={{0,4},{1,5},{2,6},{3,7},{4,0},{5,1},{6,2},{7,3},{8,12},{9,13},{10,... | collective-permute-start | bytes 147464 | tf_op jit(solution)/shard_map/ppermute | solution.py:16
  66.3 2.2 %collective-permute-start.21 = (bf16[96,256]{1,0:T(8,128)(2,1)S(1)}, bf16[96,256]{1,0:T(8,128)(2,1)S(1)}, u32[]{:S(2)}, u32[]{:S(2)}) collective-permute-start(bf16[96,256]{1,0:T(8,128)(2,1)S(1)} %get-tuple-element.26), channel_id=1, source_target_pairs={{0,8},{1,9},{2,10},{3,11},{4,12},{5,13},{6,14},{7,15},{8,0},{9,1},... | collective-permute-start | bytes 147464 | tf_op jit(solution)/shard_map/ppermute | solution.py:16
  68.5 0.6 collective-permute-start.22
  69.0 1.7 %collective-permute-done.28 = bf16[96,256]{1,0:T(8,128)(2,1)S(1)} collective-permute-done((bf16[96,256]{1,0:T(8,128)(2,1)S(1)}, bf16[96,256]{1,0:T(8,128)(2,1)S(1)}, u32[]{:S(2)}, u32[]{:S(2)}) %collective-permute-start.28) | collective-permute-done | bytes 49184 | tf_op jit(solution)/shard_map/ppermute | solution.py:16
  71.0 1.8 %collective-permute-start.31 = (bf16[2,2,96,256]{3,2,1,0:T(8,128)(2,1)S(1)}, bf16[2,2,96,256]{3,2,1,0:T(8,128)(2,1)S(1)}, u32[]{:S(2)}, u32[]{:S(2)}) collective-permute-start(bf16[2,2,96,256]{3,2,1,0:T(8,128)(2,1)S(1)} %bitcast.265), channel_id=1, source_target_pairs={{0,5},{1,4},{2,7},{3,6},{4,1},{5,0},{6,3},{7,2},{8,13},{9,12},{10,... | collective-permute-start | bytes 589832 | tf_op jit(solution)/shard_map/ppermute | solution.py:16
  72.8 1.6 %collective-permute-done.22 = bf16[96,256]{1,0:T(8,128)(2,1)S(1)} collective-permute-done((bf16[96,256]{1,0:T(8,128)(2,1)S(1)}, bf16[96,256]{1,0:T(8,128)(2,1)S(1)}, u32[]{:S(2)}, u32[]{:S(2)}) %collective-permute-start.22) | collective-permute-done | bytes 49184 | tf_op jit(solution)/shard_map/ppermute | solution.py:16
  74.9 1.5 %collective-permute-start.25 = (bf16[2,2,96,256]{3,2,1,0:T(8,128)(2,1)S(1)}, bf16[2,2,96,256]{3,2,1,0:T(8,128)(2,1)S(1)}, u32[]{:S(2)}, u32[]{:S(2)}) collective-permute-start(bf16[2,2,96,256]{3,2,1,0:T(8,128)(2,1)S(1)} %bitcast.269), channel_id=1, source_target_pairs={{0,3},{1,2},{2,1},{3,0},{4,7},{5,6},{6,5},{7,4},{8,11},{9,10},{10,... | collective-permute-start | bytes 589832 | tf_op jit(solution)/shard_map/ppermute | solution.py:16
  76.4 2.3 %collective-permute-done.30 = bf16[2,2,96,256]{3,2,1,0:T(8,128)(2,1)S(1)} collective-permute-done((bf16[2,2,96,256]{3,2,1,0:T(8,128)(2,1)S(1)}, bf16[2,2,96,256]{3,2,1,0:T(8,128)(2,1)S(1)}, u32[]{:S(2)}, u32[]{:S(2)}) %collective-permute-start.30) | collective-permute-done | bytes 196640 | tf_op jit(solution)/shard_map/ppermute | solution.py:16
  78.8 3.9 %collective-permute-done.31 = bf16[2,2,96,256]{3,2,1,0:T(8,128)(2,1)S(1)} collective-permute-done((bf16[2,2,96,256]{3,2,1,0:T(8,128)(2,1)S(1)}, bf16[2,2,96,256]{3,2,1,0:T(8,128)(2,1)S(1)}, u32[]{:S(2)}, u32[]{:S(2)}) %collective-permute-start.31) | collective-permute-done | bytes 196640 | tf_op jit(solution)/shard_map/ppermute | solution.py:16
  83.1 2.5 %collective-permute-done.25 = bf16[2,2,96,256]{3,2,1,0:T(8,128)(2,1)S(1)} collective-permute-done((bf16[2,2,96,256]{3,2,1,0:T(8,128)(2,1)S(1)}, bf16[2,2,96,256]{3,2,1,0:T(8,128)(2,1)S(1)}, u32[]{:S(2)}, u32[]{:S(2)}) %collective-permute-start.25) | collective-permute-done | bytes 196640 | tf_op jit(solution)/shard_map/ppermute | solution.py:16
  86.7 4.2 %convolution_bitcast_fusion.1 = f32[1536,256]{0,1:T(8,128)} fusion(bf16[3,512,1536]{2,1,0:T(8,128)(2,1)} %param.5, bf16[1536,256]{1,0:T(8,128)(2,1)S(1)} %bitcast.279, f32[256]{0:T(256)S(1)} %add_rsqrt_fusion.1), kind=kOutput, calls=%fused_computation.1 | convolution fusion | flops 805568512 | bytes 5506048 | tf_op jit(solution)/shard_map/dot_general | solution.py:10
  90.8 1.9 %copy.40 = f32[1536,256]{1,0:T(8,128)S(1)} copy(f32[1536,256]{0,1:T(8,128)} %convolution_bitcast_fusion.1) | data formatting | bytes 3145728 | tf_op jit(solution)/shard_map/dot_general | solution.py:10
  92.7 0.8 fusion.49
  93.8 4.2 %convolution_bitcast_fusion = f32[1536,256]{0,1:T(8,128)} fusion(bf16[3,512,1536]{2,1,0:T(8,128)(2,1)} %param.5, bf16[1536,256]{1,0:T(8,128)(2,1)S(1)} %bitcast.281, f32[256]{0:T(256)} %copy-done.2), kind=kOutput, calls=%fused_computation | convolution fusion | flops 805568512 | bytes 5506048 | tf_op jit(solution)/shard_map/dot_general | solution.py:10
  98.0 1.9 %copy.42 = f32[1536,256]{1,0:T(8,128)S(1)} copy(f32[1536,256]{0,1:T(8,128)} %convolution_bitcast_fusion) | data formatting | bytes 3145728 | tf_op jit(solution)/shard_map/dot_general | solution.py:10
  100.9 0.9 collective-permute-done.36
  101.9 5.7 %collective-permute-done.33 = bf16[2,2,96,256]{3,2,1,0:T(8,128)(2,1)S(1)} collective-permute-done((bf16[2,2,96,256]{3,2,1,0:T(8,128)(2,1)S(1)}, bf16[2,2,96,256]{3,2,1,0:T(8,128)(2,1)S(1)}, u32[]{:S(2)}, u32[]{:S(2)}) %collective-permute-start.33) | collective-permute-done | bytes 196640 | tf_op jit(solution)/shard_map/ppermute | solution.py:16
  107.8 1.2 collective-permute-done.37
  109.1 0.7 collective-permute-start.38
  109.7 2.7 %collective-permute-done.34 = bf16[2,96,256]{2,1,0:T(8,128)(2,1)S(1)} collective-permute-done((bf16[2,96,256]{2,1,0:T(8,128)(2,1)S(1)}, bf16[2,96,256]{2,1,0:T(8,128)(2,1)S(1)}, u32[]{:S(2)}, u32[]{:S(2)}) %collective-permute-start.34) | collective-permute-done | bytes 98336 | tf_op jit(solution)/shard_map/ppermute | solution.py:16
  112.5 1.2 collective-permute-done.38
  113.8 1.8 %collective-permute-start.39 = (bf16[96,256]{1,0:T(8,128)(2,1)S(1)}, bf16[96,256]{1,0:T(8,128)(2,1)S(1)}, u32[]{:S(2)}, u32[]{:S(2)}) collective-permute-start(bf16[96,256]{1,0:T(8,128)(2,1)S(1)} %fusion.65), channel_id=1, source_target_pairs={{0,8},{1,9},{2,10},{3,11},{4,12},{5,13},{6,14},{7,15},{8,0},{9,1},... | collective-permute-start | bytes 147464 | tf_op jit(solution)/shard_map/ppermute | solution.py:16
  115.7 2.1 %collective-permute-done.35 = bf16[96,256]{1,0:T(8,128)(2,1)S(1)} collective-permute-done((bf16[96,256]{1,0:T(8,128)(2,1)S(1)}, bf16[96,256]{1,0:T(8,128)(2,1)S(1)}, u32[]{:S(2)}, u32[]{:S(2)}) %collective-permute-start.35) | collective-permute-done | bytes 49184 | tf_op jit(solution)/shard_map/ppermute | solution.py:16
  117.8 1.6 %collective-permute-done.39 = bf16[96,256]{1,0:T(8,128)(2,1)S(1)} collective-permute-done((bf16[96,256]{1,0:T(8,128)(2,1)S(1)}, bf16[96,256]{1,0:T(8,128)(2,1)S(1)}, u32[]{:S(2)}, u32[]{:S(2)}) %collective-permute-start.39) | collective-permute-done | bytes 49184 | tf_op jit(solution)/shard_map/ppermute | solution.py:16
  119.6 0.7 collective-permute-start.41
  120.3 1.2 collective-permute-start.42
  121.4 1.8 %collective-permute-done.41 = f32[256]{0:T(256)S(1)} collective-permute-done((f32[256]{0:T(256)S(1)}, f32[256]{0:T(256)S(1)}, u32[]{:S(2)}, u32[]{:S(2)}) %collective-permute-start.41) | collective-permute-done | bytes 1056 | tf_op jit(solution)/shard_map/ppermute | solution.py:16
  123.7 1.0 collective-permute-start.44
  124.8 2.9 %collective-permute-start.45 = (f32[256]{0:T(256)S(1)}, f32[256]{0:T(256)S(1)}, u32[]{:S(2)}, u32[]{:S(2)}) collective-permute-start(f32[256]{0:T(256)S(1)} %add_add_fusion), channel_id=1, source_target_pairs={{0,12},{1,13},{2,14},{3,15},{4,8},{5,9},{6,10},{7,11},{8,4},{9,5},... | collective-permute-start | bytes 3080 | tf_op jit(solution)/shard_map/ppermute | solution.py:16
  128.2 1.9 %collective-permute-done.45 = f32[256]{0:T(256)S(1)} collective-permute-done((f32[256]{0:T(256)S(1)}, f32[256]{0:T(256)S(1)}, u32[]{:S(2)}, u32[]{:S(2)}) %collective-permute-start.45) | collective-permute-done | bytes 1056 | tf_op jit(solution)/shard_map/ppermute | solution.py:16
  130.1 0.7 broadcast_multiply_fusion
  (103 shorter events, 8.5 us)
Async XLA Ops:
  0.6 11.5 %collective-permute-start.10 = (bf16[96,256]{1,0:T(8,128)(2,1)}, bf16[96,256]{1,0:T(8,128)(2,1)S(1)}, u32[]{:S(2)}, u32[]{:S(2)}) collective-permute-start(bf16[96,256]{1,0:T(8,128)(2,1)} %param.7), channel_id=1, source_target_pairs={{0,2},{1,3},{2,0},{3,1},{4,6},{5,7},{6,4},{7,5},{8,10},{9,11},{10,... | collective-permute-start | bytes 147464 | tf_op jit(solution)/shard_map/ppermute | solution.py:16
  3.7 8.5 %collective-permute-start.11 = (bf16[96,256]{1,0:T(8,128)(2,1)}, bf16[96,256]{1,0:T(8,128)(2,1)S(1)}, u32[]{:S(2)}, u32[]{:S(2)}) collective-permute-start(bf16[96,256]{1,0:T(8,128)(2,1)} %param.7), channel_id=1, source_target_pairs={{0,8},{1,9},{2,10},{3,11},{4,12},{5,13},{6,14},{7,15},{8,0},{9,1},... | collective-permute-start | bytes 147464 | tf_op jit(solution)/shard_map/ppermute | solution.py:16
  6.3 7.5 %collective-permute-start.12 = (bf16[96,256]{1,0:T(8,128)(2,1)}, bf16[96,256]{1,0:T(8,128)(2,1)S(1)}, u32[]{:S(2)}, u32[]{:S(2)}) collective-permute-start(bf16[96,256]{1,0:T(8,128)(2,1)} %param.7), channel_id=1, source_target_pairs={{0,10},{1,11},{2,8},{3,9},{4,14},{5,15},{6,12},{7,13},{8,2},{9,3},... | collective-permute-start | bytes 147464 | tf_op jit(solution)/shard_map/ppermute | solution.py:16
  6.3 8.7 %collective-permute-start = (bf16[96,256]{1,0:T(8,128)(2,1)}, bf16[96,256]{1,0:T(8,128)(2,1)S(1)}, u32[]{:S(2)}, u32[]{:S(2)}) collective-permute-start(bf16[96,256]{1,0:T(8,128)(2,1)} %param.6), channel_id=1, source_target_pairs={{0,4},{1,5},{2,6},{3,7},{4,0},{5,1},{6,2},{7,3},{8,12},{9,13},{10,... | collective-permute-start | bytes 147464 | tf_op jit(solution)/shard_map/ppermute | solution.py:16
  8.1 8.5 %collective-permute-start.1 = (bf16[96,256]{1,0:T(8,128)(2,1)}, bf16[96,256]{1,0:T(8,128)(2,1)S(1)}, u32[]{:S(2)}, u32[]{:S(2)}) collective-permute-start(bf16[96,256]{1,0:T(8,128)(2,1)} %param.6), channel_id=1, source_target_pairs={{0,8},{1,9},{2,10},{3,11},{4,12},{5,13},{6,14},{7,15},{8,0},{9,1},... | collective-permute-start | bytes 147464 | tf_op jit(solution)/shard_map/ppermute | solution.py:16
  12.1 6.1 %collective-permute-start.2 = (bf16[96,256]{1,0:T(8,128)(2,1)}, bf16[96,256]{1,0:T(8,128)(2,1)S(1)}, u32[]{:S(2)}, u32[]{:S(2)}) collective-permute-start(bf16[96,256]{1,0:T(8,128)(2,1)} %param.6), channel_id=1, source_target_pairs={{0,12},{1,13},{2,14},{3,15},{4,8},{5,9},{6,10},{7,11},{8,4},{9,5},... | collective-permute-start | bytes 147464 | tf_op jit(solution)/shard_map/ppermute | solution.py:16
  14.6 6.2 %collective-permute-start.13 = (bf16[2,2,96,256]{3,2,1,0:T(8,128)(2,1)S(1)}, bf16[2,2,96,256]{3,2,1,0:T(8,128)(2,1)S(1)}, u32[]{:S(2)}, u32[]{:S(2)}) collective-permute-start(bf16[2,2,96,256]{3,2,1,0:T(8,128)(2,1)S(1)} %bitcast.271), channel_id=1, source_target_pairs={{0,1},{1,0},{2,3},{3,2},{4,5},{5,4},{6,7},{7,6},{8,9},{9,8},{10,11... | collective-permute-start | bytes 589832 | tf_op jit(solution)/shard_map/ppermute | solution.py:16
  14.7 7.8 %collective-permute-start.14 = (bf16[2,2,96,256]{3,2,1,0:T(8,128)(2,1)S(1)}, bf16[2,2,96,256]{3,2,1,0:T(8,128)(2,1)S(1)}, u32[]{:S(2)}, u32[]{:S(2)}) collective-permute-start(bf16[2,2,96,256]{3,2,1,0:T(8,128)(2,1)S(1)} %bitcast.272), channel_id=1, source_target_pairs={{0,4},{1,5},{2,6},{3,7},{4,0},{5,1},{6,2},{7,3},{8,12},{9,13},{10,... | collective-permute-start | bytes 589832 | tf_op jit(solution)/shard_map/ppermute | solution.py:16
  14.9 11.5 %collective-permute-start.15 = (bf16[2,2,96,256]{3,2,1,0:T(8,128)(2,1)S(1)}, bf16[2,2,96,256]{3,2,1,0:T(8,128)(2,1)S(1)}, u32[]{:S(2)}, u32[]{:S(2)}) collective-permute-start(bf16[2,2,96,256]{3,2,1,0:T(8,128)(2,1)S(1)} %bitcast.273), channel_id=1, source_target_pairs={{0,5},{1,4},{2,7},{3,6},{4,1},{5,0},{6,3},{7,2},{8,13},{9,12},{10,... | collective-permute-start | bytes 589832 | tf_op jit(solution)/shard_map/ppermute | solution.py:16
  19.1 12.3 %collective-permute-start.3 = (bf16[2,2,96,256]{3,2,1,0:T(8,128)(2,1)S(1)}, bf16[2,2,96,256]{3,2,1,0:T(8,128)(2,1)S(1)}, u32[]{:S(2)}, u32[]{:S(2)}) collective-permute-start(bf16[2,2,96,256]{3,2,1,0:T(8,128)(2,1)S(1)} %bitcast.275), channel_id=1, source_target_pairs={{0,1},{1,0},{2,3},{3,2},{4,5},{5,4},{6,7},{7,6},{8,9},{9,8},{10,11... | collective-permute-start | bytes 589832 | tf_op jit(solution)/shard_map/ppermute | solution.py:16
  19.2 12.2 %collective-permute-start.4 = (bf16[2,2,96,256]{3,2,1,0:T(8,128)(2,1)S(1)}, bf16[2,2,96,256]{3,2,1,0:T(8,128)(2,1)}, u32[]{:S(2)}, u32[]{:S(2)}) collective-permute-start(bf16[2,2,96,256]{3,2,1,0:T(8,128)(2,1)S(1)} %bitcast.276), channel_id=1, source_target_pairs={{0,2},{1,3},{2,0},{3,1},{4,6},{5,7},{6,4},{7,5},{8,10},{9,11},{10,... | collective-permute-start | bytes 589832 | tf_op jit(solution)/shard_map/ppermute | solution.py:16
  20.8 10.5 %collective-permute-start.5 = (bf16[2,2,96,256]{3,2,1,0:T(8,128)(2,1)S(1)}, bf16[2,2,96,256]{3,2,1,0:T(8,128)(2,1)}, u32[]{:S(2)}, u32[]{:S(2)}) collective-permute-start(bf16[2,2,96,256]{3,2,1,0:T(8,128)(2,1)S(1)} %bitcast.277), channel_id=1, source_target_pairs={{0,3},{1,2},{2,1},{3,0},{4,7},{5,6},{6,5},{7,4},{8,11},{9,10},{10,... | collective-permute-start | bytes 589832 | tf_op jit(solution)/shard_map/ppermute | solution.py:16
  31.0 10.0 %collective-permute-start.16 = (bf16[2,2,2,96,256]{4,3,0,2,1:T(8,128)(2,1)}, bf16[2,2,2,96,256]{4,3,0,2,1:T(8,128)(2,1)}, u32[]{:S(2)}, u32[]{:S(2)}) collective-permute-start(bf16[2,2,2,96,256]{4,3,0,2,1:T(8,128)(2,1)} %fusion.50), channel_id=1, source_target_pairs={{0,1},{1,0},{2,3},{3,2},{4,5},{5,4},{6,7},{7,6},{8,9},{9,8},{10,11... | collective-permute-start | bytes 1179656 | tf_op jit(solution)/shard_map/ppermute | solution.py:16
  39.5 2.8 %collective-permute-start.6 = (bf16[2,2,2,96,256]{4,3,2,1,0:T(8,128)(2,1)}, bf16[2,2,2,96,256]{4,3,2,1,0:T(8,128)(2,1)S(1)}, u32[]{:S(2)}, u32[]{:S(2)}) collective-permute-start(bf16[2,2,2,96,256]{4,3,2,1,0:T(8,128)(2,1)} %fusion.48), channel_id=1, source_target_pairs={{0,1},{1,0},{2,3},{3,2},{4,5},{5,4},{6,7},{7,6},{8,9},{9,8},{10,11... | collective-permute-start | bytes 1179656 | tf_op jit(solution)/shard_map/ppermute | solution.py:16
  42.1 7.2 %collective-permute-start.17 = (bf16[2,2,96,256]{3,2,0,1:T(8,128)(2,1)S(1)}, bf16[2,2,96,256]{3,2,0,1:T(8,128)(2,1)S(1)}, u32[]{:S(2)}, u32[]{:S(2)}) collective-permute-start(bf16[2,2,96,256]{3,2,0,1:T(8,128)(2,1)S(1)} %fusion.55), channel_id=1, source_target_pairs={{0,4},{1,5},{2,6},{3,7},{4,0},{5,1},{6,2},{7,3},{8,12},{9,13},{10,... | collective-permute-start | bytes 589832 | tf_op jit(solution)/shard_map/ppermute | solution.py:16
  42.4 17.7 %copy-start = (f32[96]{0:T(128)S(1)}, f32[96]{0:T(128)}, u32[]{:S(2)}) copy-start(f32[96]{0:T(128)} %get-tuple-element.50) | copy-start | bytes 1156
  42.4 17.7 %copy-start.1 = (f32[96]{0:T(128)S(1)}, f32[96]{0:T(128)}, u32[]{:S(2)}) copy-start(f32[96]{0:T(128)} %get-tuple-element.51) | copy-start | bytes 1156
  42.4 7.8 %collective-permute-start.7 = (bf16[2,2,96,256]{3,2,1,0:T(8,128)(2,1)S(1)}, bf16[2,2,96,256]{3,2,1,0:T(8,128)(2,1)S(1)}, u32[]{:S(2)}, u32[]{:S(2)}) collective-permute-start(bf16[2,2,96,256]{3,2,1,0:T(8,128)(2,1)S(1)} %fusion.54), channel_id=1, source_target_pairs={{0,2},{1,3},{2,0},{3,1},{4,6},{5,7},{6,4},{7,5},{8,10},{9,11},{10,... | collective-permute-start | bytes 589832 | tf_op jit(solution)/shard_map/ppermute | solution.py:16
  49.5 4.7 %collective-permute-start.18 = (bf16[2,96,256]{2,1,0:T(8,128)(2,1)S(1)}, bf16[2,96,256]{2,1,0:T(8,128)(2,1)S(1)}, u32[]{:S(2)}, u32[]{:S(2)}) collective-permute-start(bf16[2,96,256]{2,1,0:T(8,128)(2,1)S(1)} %fusion.59), channel_id=1, source_target_pairs={{0,2},{1,3},{2,0},{3,1},{4,6},{5,7},{6,4},{7,5},{8,10},{9,11},{10,... | collective-permute-start | bytes 294920 | tf_op jit(solution)/shard_map/ppermute | solution.py:16
  50.3 4.7 %collective-permute-start.8 = (bf16[2,96,256]{2,1,0:T(8,128)(2,1)S(1)}, bf16[2,96,256]{2,1,0:T(8,128)(2,1)S(1)}, u32[]{:S(2)}, u32[]{:S(2)}) collective-permute-start(bf16[2,96,256]{2,1,0:T(8,128)(2,1)S(1)} %fusion.58), channel_id=1, source_target_pairs={{0,4},{1,5},{2,6},{3,7},{4,0},{5,1},{6,2},{7,3},{8,12},{9,13},{10,... | collective-permute-start | bytes 294920 | tf_op jit(solution)/shard_map/ppermute | solution.py:16
  54.2 5.3 %collective-permute-start.19 = (bf16[96,256]{1,0:T(8,128)(2,1)S(1)}, bf16[96,256]{1,0:T(8,128)(2,1)S(1)}, u32[]{:S(2)}, u32[]{:S(2)}) collective-permute-start(bf16[96,256]{1,0:T(8,128)(2,1)S(1)} %fusion.63), channel_id=1, source_target_pairs={{0,8},{1,9},{2,10},{3,11},{4,12},{5,13},{6,14},{7,15},{8,0},{9,1},... | collective-permute-start | bytes 147464 | tf_op jit(solution)/shard_map/ppermute | solution.py:16
  55.0 5.1 %collective-permute-start.9 = (bf16[96,256]{1,0:T(8,128)(2,1)S(1)}, bf16[96,256]{1,0:T(8,128)(2,1)S(1)}, u32[]{:S(2)}, u32[]{:S(2)}) collective-permute-start(bf16[96,256]{1,0:T(8,128)(2,1)S(1)} %fusion.62), channel_id=1, source_target_pairs={{0,8},{1,9},{2,10},{3,11},{4,12},{5,13},{6,14},{7,15},{8,0},{9,1},... | collective-permute-start | bytes 147464 | tf_op jit(solution)/shard_map/ppermute | solution.py:16
  60.2 8.3 %collective-permute-start.26 = (bf16[96,256]{1,0:T(8,128)(2,1)S(1)}, bf16[96,256]{1,0:T(8,128)(2,1)S(1)}, u32[]{:S(2)}, u32[]{:S(2)}) collective-permute-start(bf16[96,256]{1,0:T(8,128)(2,1)S(1)} %get-tuple-element.27), channel_id=1, source_target_pairs={{0,2},{1,3},{2,0},{3,1},{4,6},{5,7},{6,4},{7,5},{8,10},{9,11},{10,... | collective-permute-start | bytes 147464 | tf_op jit(solution)/shard_map/ppermute | solution.py:16
  61.8 7.3 %collective-permute-start.27 = (bf16[96,256]{1,0:T(8,128)(2,1)S(1)}, bf16[96,256]{1,0:T(8,128)(2,1)S(1)}, u32[]{:S(2)}, u32[]{:S(2)}) collective-permute-start(bf16[96,256]{1,0:T(8,128)(2,1)S(1)} %get-tuple-element.27), channel_id=1, source_target_pairs={{0,8},{1,9},{2,10},{3,11},{4,12},{5,13},{6,14},{7,15},{8,0},{9,1},... | collective-permute-start | bytes 147464 | tf_op jit(solution)/shard_map/ppermute | solution.py:16
  63.9 6.9 %collective-permute-start.28 = (bf16[96,256]{1,0:T(8,128)(2,1)S(1)}, bf16[96,256]{1,0:T(8,128)(2,1)S(1)}, u32[]{:S(2)}, u32[]{:S(2)}) collective-permute-start(bf16[96,256]{1,0:T(8,128)(2,1)S(1)} %get-tuple-element.27), channel_id=1, source_target_pairs={{0,10},{1,11},{2,8},{3,9},{4,14},{5,15},{6,12},{7,13},{8,2},{9,3},... | collective-permute-start | bytes 147464 | tf_op jit(solution)/shard_map/ppermute | solution.py:16
  64.7 6.3 %collective-permute-start.20 = (bf16[96,256]{1,0:T(8,128)(2,1)S(1)}, bf16[96,256]{1,0:T(8,128)(2,1)S(1)}, u32[]{:S(2)}, u32[]{:S(2)}) collective-permute-start(bf16[96,256]{1,0:T(8,128)(2,1)S(1)} %get-tuple-element.26), channel_id=1, source_target_pairs={{0,4},{1,5},{2,6},{3,7},{4,0},{5,1},{6,2},{7,3},{8,12},{9,13},{10,... | collective-permute-start | bytes 147464 | tf_op jit(solution)/shard_map/ppermute | solution.py:16
  66.3 6.5 %collective-permute-start.21 = (bf16[96,256]{1,0:T(8,128)(2,1)S(1)}, bf16[96,256]{1,0:T(8,128)(2,1)S(1)}, u32[]{:S(2)}, u32[]{:S(2)}) collective-permute-start(bf16[96,256]{1,0:T(8,128)(2,1)S(1)} %get-tuple-element.26), channel_id=1, source_target_pairs={{0,8},{1,9},{2,10},{3,11},{4,12},{5,13},{6,14},{7,15},{8,0},{9,1},... | collective-permute-start | bytes 147464 | tf_op jit(solution)/shard_map/ppermute | solution.py:16
  68.5 5.9 %collective-permute-start.22 = (bf16[96,256]{1,0:T(8,128)(2,1)S(1)}, bf16[96,256]{1,0:T(8,128)(2,1)S(1)}, u32[]{:S(2)}, u32[]{:S(2)}) collective-permute-start(bf16[96,256]{1,0:T(8,128)(2,1)S(1)} %get-tuple-element.26), channel_id=1, source_target_pairs={{0,12},{1,13},{2,14},{3,15},{4,8},{5,9},{6,10},{7,11},{8,4},{9,5},... | collective-permute-start | bytes 147464 | tf_op jit(solution)/shard_map/ppermute | solution.py:16
  70.8 4.0 %collective-permute-start.29 = (bf16[2,2,96,256]{3,2,1,0:T(8,128)(2,1)S(1)}, bf16[2,2,96,256]{3,2,1,0:T(8,128)(2,1)S(1)}, u32[]{:S(2)}, u32[]{:S(2)}) collective-permute-start(bf16[2,2,96,256]{3,2,1,0:T(8,128)(2,1)S(1)} %bitcast.263), channel_id=1, source_target_pairs={{0,1},{1,0},{2,3},{3,2},{4,5},{5,4},{6,7},{7,6},{8,9},{9,8},{10,11... | collective-permute-start | bytes 589832 | tf_op jit(solution)/shard_map/ppermute | solution.py:16
  70.9 7.8 %collective-permute-start.30 = (bf16[2,2,96,256]{3,2,1,0:T(8,128)(2,1)S(1)}, bf16[2,2,96,256]{3,2,1,0:T(8,128)(2,1)S(1)}, u32[]{:S(2)}, u32[]{:S(2)}) collective-permute-start(bf16[2,2,96,256]{3,2,1,0:T(8,128)(2,1)S(1)} %bitcast.264), channel_id=1, source_target_pairs={{0,4},{1,5},{2,6},{3,7},{4,0},{5,1},{6,2},{7,3},{8,12},{9,13},{10,... | collective-permute-start | bytes 589832 | tf_op jit(solution)/shard_map/ppermute | solution.py:16
  71.0 11.6 %collective-permute-start.31 = (bf16[2,2,96,256]{3,2,1,0:T(8,128)(2,1)S(1)}, bf16[2,2,96,256]{3,2,1,0:T(8,128)(2,1)S(1)}, u32[]{:S(2)}, u32[]{:S(2)}) collective-permute-start(bf16[2,2,96,256]{3,2,1,0:T(8,128)(2,1)S(1)} %bitcast.265), channel_id=1, source_target_pairs={{0,5},{1,4},{2,7},{3,6},{4,1},{5,0},{6,3},{7,2},{8,13},{9,12},{10,... | collective-permute-start | bytes 589832 | tf_op jit(solution)/shard_map/ppermute | solution.py:16
  74.5 8.7 %collective-permute-start.23 = (bf16[2,2,96,256]{3,2,1,0:T(8,128)(2,1)S(1)}, bf16[2,2,96,256]{3,2,1,0:T(8,128)(2,1)S(1)}, u32[]{:S(2)}, u32[]{:S(2)}) collective-permute-start(bf16[2,2,96,256]{3,2,1,0:T(8,128)(2,1)S(1)} %bitcast.267), channel_id=1, source_target_pairs={{0,1},{1,0},{2,3},{3,2},{4,5},{5,4},{6,7},{7,6},{8,9},{9,8},{10,11... | collective-permute-start | bytes 589832 | tf_op jit(solution)/shard_map/ppermute | solution.py:16
  74.5 8.6 %collective-permute-start.24 = (bf16[2,2,96,256]{3,2,1,0:T(8,128)(2,1)S(1)}, bf16[2,2,96,256]{3,2,1,0:T(8,128)(2,1)S(1)}, u32[]{:S(2)}, u32[]{:S(2)}) collective-permute-start(bf16[2,2,96,256]{3,2,1,0:T(8,128)(2,1)S(1)} %bitcast.268), channel_id=1, source_target_pairs={{0,2},{1,3},{2,0},{3,1},{4,6},{5,7},{6,4},{7,5},{8,10},{9,11},{10,... | collective-permute-start | bytes 589832 | tf_op jit(solution)/shard_map/ppermute | solution.py:16
  74.9 10.8 %collective-permute-start.25 = (bf16[2,2,96,256]{3,2,1,0:T(8,128)(2,1)S(1)}, bf16[2,2,96,256]{3,2,1,0:T(8,128)(2,1)S(1)}, u32[]{:S(2)}, u32[]{:S(2)}) collective-permute-start(bf16[2,2,96,256]{3,2,1,0:T(8,128)(2,1)S(1)} %bitcast.269), channel_id=1, source_target_pairs={{0,3},{1,2},{2,1},{3,0},{4,7},{5,6},{6,5},{7,4},{8,11},{9,10},{10,... | collective-permute-start | bytes 589832 | tf_op jit(solution)/shard_map/ppermute | solution.py:16
  86.1 0.6 copy-start.2
  93.5 6.8 %collective-permute-start.32 = (bf16[2,2,2,96,256]{4,3,2,1,0:T(8,128)(2,1)}, bf16[2,2,2,96,256]{4,3,2,1,0:T(8,128)(2,1)S(1)}, u32[]{:S(2)}, u32[]{:S(2)}) collective-permute-start(bf16[2,2,2,96,256]{4,3,2,1,0:T(8,128)(2,1)} %fusion.49), channel_id=1, source_target_pairs={{0,1},{1,0},{2,3},{3,2},{4,5},{5,4},{6,7},{7,6},{8,9},{9,8},{10,11... | collective-permute-start | bytes 1179656 | tf_op jit(solution)/shard_map/ppermute | solution.py:16
  99.9 1.8 %collective-permute-start.36 = (bf16[2,2,2,96,256]{4,3,0,2,1:T(8,128)(2,1)S(1)}, bf16[2,2,2,96,256]{4,3,0,2,1:T(8,128)(2,1)S(1)}, u32[]{:S(2)}, u32[]{:S(2)}) collective-permute-start(bf16[2,2,2,96,256]{4,3,0,2,1:T(8,128)(2,1)S(1)} %fusion.51), channel_id=1, source_target_pairs={{0,1},{1,0},{2,3},{3,2},{4,5},{5,4},{6,7},{7,6},{8,9},{9,8},{10,11... | collective-permute-start | bytes 1179656 | tf_op jit(solution)/shard_map/ppermute | solution.py:16
  100.5 7.1 %collective-permute-start.33 = (bf16[2,2,96,256]{3,2,1,0:T(8,128)(2,1)S(1)}, bf16[2,2,96,256]{3,2,1,0:T(8,128)(2,1)S(1)}, u32[]{:S(2)}, u32[]{:S(2)}) collective-permute-start(bf16[2,2,96,256]{3,2,1,0:T(8,128)(2,1)S(1)} %fusion.56), channel_id=1, source_target_pairs={{0,2},{1,3},{2,0},{3,1},{4,6},{5,7},{6,4},{7,5},{8,10},{9,11},{10,... | collective-permute-start | bytes 589832 | tf_op jit(solution)/shard_map/ppermute | solution.py:16
  101.9 7.1 %collective-permute-start.37 = (bf16[2,2,96,256]{3,2,0,1:T(8,128)(2,1)S(1)}, bf16[2,2,96,256]{3,2,0,1:T(8,128)(2,1)S(1)}, u32[]{:S(2)}, u32[]{:S(2)}) collective-permute-start(bf16[2,2,96,256]{3,2,0,1:T(8,128)(2,1)S(1)} %fusion.57), channel_id=1, source_target_pairs={{0,4},{1,5},{2,6},{3,7},{4,0},{5,1},{6,2},{7,3},{8,12},{9,13},{10,... | collective-permute-start | bytes 589832 | tf_op jit(solution)/shard_map/ppermute | solution.py:16
  107.7 4.7 %collective-permute-start.34 = (bf16[2,96,256]{2,1,0:T(8,128)(2,1)S(1)}, bf16[2,96,256]{2,1,0:T(8,128)(2,1)S(1)}, u32[]{:S(2)}, u32[]{:S(2)}) collective-permute-start(bf16[2,96,256]{2,1,0:T(8,128)(2,1)S(1)} %fusion.60), channel_id=1, source_target_pairs={{0,4},{1,5},{2,6},{3,7},{4,0},{5,1},{6,2},{7,3},{8,12},{9,13},{10,... | collective-permute-start | bytes 294920 | tf_op jit(solution)/shard_map/ppermute | solution.py:16
  109.1 4.7 %collective-permute-start.38 = (bf16[2,96,256]{2,1,0:T(8,128)(2,1)S(1)}, bf16[2,96,256]{2,1,0:T(8,128)(2,1)S(1)}, u32[]{:S(2)}, u32[]{:S(2)}) collective-permute-start(bf16[2,96,256]{2,1,0:T(8,128)(2,1)S(1)} %fusion.61), channel_id=1, source_target_pairs={{0,2},{1,3},{2,0},{3,1},{4,6},{5,7},{6,4},{7,5},{8,10},{9,11},{10,... | collective-permute-start | bytes 294920 | tf_op jit(solution)/shard_map/ppermute | solution.py:16
  112.5 5.3 %collective-permute-start.35 = (bf16[96,256]{1,0:T(8,128)(2,1)S(1)}, bf16[96,256]{1,0:T(8,128)(2,1)S(1)}, u32[]{:S(2)}, u32[]{:S(2)}) collective-permute-start(bf16[96,256]{1,0:T(8,128)(2,1)S(1)} %fusion.64), channel_id=1, source_target_pairs={{0,8},{1,9},{2,10},{3,11},{4,12},{5,13},{6,14},{7,15},{8,0},{9,1},... | collective-permute-start | bytes 147464 | tf_op jit(solution)/shard_map/ppermute | solution.py:16
  113.8 5.6 %collective-permute-start.39 = (bf16[96,256]{1,0:T(8,128)(2,1)S(1)}, bf16[96,256]{1,0:T(8,128)(2,1)S(1)}, u32[]{:S(2)}, u32[]{:S(2)}) collective-permute-start(bf16[96,256]{1,0:T(8,128)(2,1)S(1)} %fusion.65), channel_id=1, source_target_pairs={{0,8},{1,9},{2,10},{3,11},{4,12},{5,13},{6,14},{7,15},{8,0},{9,1},... | collective-permute-start | bytes 147464 | tf_op jit(solution)/shard_map/ppermute | solution.py:16
  119.5 1.9 %collective-permute-start.40 = (f32[256]{0:T(256)S(1)}, f32[256]{0:T(256)S(1)}, u32[]{:S(2)}, u32[]{:S(2)}) collective-permute-start(f32[256]{0:T(256)S(1)} %add.212), channel_id=1, source_target_pairs={{0,1},{1,0},{2,3},{3,2},{4,5},{5,4},{6,7},{7,6},{8,9},{9,8},{10,11... | collective-permute-start | bytes 3080 | tf_op jit(solution)/shard_map/ppermute | solution.py:16
  119.6 3.6 %collective-permute-start.41 = (f32[256]{0:T(256)S(1)}, f32[256]{0:T(256)S(1)}, u32[]{:S(2)}, u32[]{:S(2)}) collective-permute-start(f32[256]{0:T(256)S(1)} %add.212), channel_id=1, source_target_pairs={{0,2},{1,3},{2,0},{3,1},{4,6},{5,7},{6,4},{7,5},{8,10},{9,11},{10,... | collective-permute-start | bytes 3080 | tf_op jit(solution)/shard_map/ppermute | solution.py:16
  120.3 3.0 %collective-permute-start.42 = (f32[256]{0:T(256)S(1)}, f32[256]{0:T(256)S(1)}, u32[]{:S(2)}, u32[]{:S(2)}) collective-permute-start(f32[256]{0:T(256)S(1)} %add.212), channel_id=1, source_target_pairs={{0,3},{1,2},{2,1},{3,0},{4,7},{5,6},{6,5},{7,4},{8,11},{9,10},{10,... | collective-permute-start | bytes 3080 | tf_op jit(solution)/shard_map/ppermute | solution.py:16
  123.3 4.4 %collective-permute-start.43 = (f32[256]{0:T(256)S(1)}, f32[256]{0:T(256)S(1)}, u32[]{:S(2)}, u32[]{:S(2)}) collective-permute-start(f32[256]{0:T(256)S(1)} %add_add_fusion), channel_id=1, source_target_pairs={{0,4},{1,5},{2,6},{3,7},{4,0},{5,1},{6,2},{7,3},{8,12},{9,13},{10,... | collective-permute-start | bytes 3080 | tf_op jit(solution)/shard_map/ppermute | solution.py:16
  123.7 4.5 %collective-permute-start.44 = (f32[256]{0:T(256)S(1)}, f32[256]{0:T(256)S(1)}, u32[]{:S(2)}, u32[]{:S(2)}) collective-permute-start(f32[256]{0:T(256)S(1)} %add_add_fusion), channel_id=1, source_target_pairs={{0,8},{1,9},{2,10},{3,11},{4,12},{5,13},{6,14},{7,15},{8,0},{9,1},... | collective-permute-start | bytes 3080 | tf_op jit(solution)/shard_map/ppermute | solution.py:16
  124.8 5.4 %collective-permute-start.45 = (f32[256]{0:T(256)S(1)}, f32[256]{0:T(256)S(1)}, u32[]{:S(2)}, u32[]{:S(2)}) collective-permute-start(f32[256]{0:T(256)S(1)} %add_add_fusion), channel_id=1, source_target_pairs={{0,12},{1,13},{2,14},{3,15},{4,8},{5,9},{6,10},{7,11},{8,4},{9,5},... | collective-permute-start | bytes 3080 | tf_op jit(solution)/shard_map/ppermute | solution.py:16

commit v13 on v11

--- a/solution.py
+++ b/solution.py
@@ -31,19 +31,29 @@
     return cur
 
 
-def doubling_all_gather(x, devices, order):
+def doubling_all_gather(parts, devices, orders):
     me = lax.axis_index("row")
-    cur = x
-    done = []
-    for bit in order:
-        other = exchange(cur, 1 << bit, devices)
-        low = (me >> bit) & 1 == 0
-        axis = sum(1 for b in done if b > bit)
-        done.append(bit)
-        cur = jnp.stack(
-            [jnp.where(low, cur, other), jnp.where(low, other, cur)], axis=axis
-        )
-    return cur.reshape((-1, x.shape[-1]))
+    curs = list(parts)
+    dones = [[] for _ in parts]
+    for step in range(len(orders[0])):
+        bits = [order[step] for order in orders]
+        others = [None] * len(curs)
+        for bit in sorted(set(bits)):
+            members = [i for i, b in enumerate(bits) if b == bit]
+            if len(members) == 1:
+                others[members[0]] = exchange(curs[members[0]], 1 << bit, devices)
+            else:
+                got = exchange(jnp.stack([curs[i] for i in members]), 1 << bit, devices)
+                for j, i in enumerate(members):
+                    others[i] = got[j]
+        for i, bit in enumerate(bits):
+            low = (me >> bit) & 1 == 0
+            axis = sum(1 for b in dones[i] if b > bit)
+            dones[i].append(bit)
+            curs[i] = jnp.stack(
+                [jnp.where(low, curs[i], others[i]), jnp.where(low, others[i], curs[i])], axis=axis
+            )
+    return [cur.reshape((-1, part.shape[-1])) for cur, part in zip(curs, parts)]
 
 
 def doubling_all_reduce(x, devices):
@@ -73,8 +83,8 @@
     all_channels = chan_rows * devices
     first_row = lax.axis_index("row") * chan_rows
     order_amp, order_der = stage_orders(devices)
-    amp_full = doubling_all_gather(first_f, devices, order_amp[::-1])
-    der_full = doubling_all_gather(first_g, devices, order_der[::-1])
+    gather_orders = [order_amp[::-1], order_der[::-1]]
+    amp_full, der_full = doubling_all_gather([first_f, first_g], devices, gather_orders)
     scale = None
     for sector in range(SECTORS):
         halves = []
@@ -93,8 +103,9 @@
         new_amp = cosine * rot_amp + sine / wave * rot_der
         new_der = -wave * sine * rot_amp + cosine * rot_der
         if sector + 1 < SECTORS:
-            amp_full = doubling_all_gather(new_amp.astype(jnp.bfloat16), devices, order_amp[::-1])
-            der_full = doubling_all_gather(new_der.astype(jnp.bfloat16), devices, order_der[::-1])
+            amp_full, der_full = doubling_all_gather(
+                [new_amp.astype(jnp.bfloat16), new_der.astype(jnp.bfloat16)], devices, gather_orders
+            )
             amp_wide = amp_full.astype(jnp.float32)
             der_wide = der_full.astype(jnp.float32)
             norm = jnp.sum(amp_wide * amp_wide, axis=0) + jnp.sum(der_wide * der_wide, axis=0)

time: 122 us -> 129 us (1.057)
  waiting for transfers between devices: 42.9 us -> 48.3 us
    ppermute x38 -> x34, waiting for transfers between devices: 42.9 us -> 48.3 us  [exchange(): return lax.ppermute(x, 'row', [(i, i ^ distance) for i in range(devices)])]
    select_n x0 -> x4, other arithmetic: none -> 1.42 us  [doubling_all_gather(): jnp.where(low, curs[i], others[i])]
    another operation x32 -> x29, other arithmetic: 3.75 us -> 2.7 us  [the longest x22 1.61 us: doubling_all_gather(): jnp.stack([jnp.where(low, curs[i], others[i]), jnp.where(low, others[i],...]
    ppermute x38 -> x34, starting transfers between devices: 44.4 us -> 44.7 us  [exchange(): return lax.ppermute(x, 'row', [(i, i ^ distance) for i in range(devices)])]
  transfers between devices with their start and end apart: 38 -> 34, of which waited for: 24 -> 24; matrix products, arithmetic and copies ran while one was open for 22% -> 15% of each run, Pallas kernels for 0% -> 0%
where the time goes in v13:
time: 129 us; the launch traced here: 128 us
  waiting for transfers between devices  48.3 us (37%)
  starting transfers between devices  44.7 us (35%)
  matrix products  14.5 us (11%)
  local copies, waits for them, and re-layouts  11.1 us (9%)
  other arithmetic  8.62 us (7%)
    ppermute x34, waiting for transfers between devices, exchange(): return lax.ppermute(x, 'row', [(i, i ^ distance) for i in range(devices)])  48.3 us
    ppermute x34, starting transfers between devices, exchange(): return lax.ppermute(x, 'row', [(i, i ^ distance) for i in range(devices)])  44.7 us
    dot_general x4, matrix products, contract_rows(): lax.dot_general(left, right, (((0,), (0,)), ((), ())), preferred_element_...  14.5 us
    dot_general x4, local copies, waits for them, and re-layouts, contract_rows(): lax.dot_general(left, right, (((0,), (0,)), ((), ())), preferred_element_...  4.68 us
    convert_element_type x16, local copies, waits for them, and re-layouts, halving_reduce_scatter(): send.astype(jnp.bfloat16)  2.71 us
  transfers between devices with their start and end apart: 34, of which 24 were waited for; matrix products, arithmetic and copies ran while one was open for 15% of the time, Pallas kernels for 0%

profile of v13, /device:TPU:0, one launch (start us, length us, event | category | flops | bytes accessed | tf_op | source)
XLA Modules:
  0.0 128.5 jit_solution(14812271681952824443)
XLA Ops:
  0.6 0.8 pad_maximum_fusion.14
  1.5 4.1 %collective-permute-start = (bf16[2,96,256]{2,1,0:T(8,128)(2,1)S(1)}, bf16[2,96,256]{2,1,0:T(8,128)(2,1)S(1)}, u32[]{:S(2)}, u32[]{:S(2)}) collective-permute-start(bf16[2,96,256]{2,1,0:T(8,128)(2,1)S(1)} %pad_maximum_fusion.14), channel_id=1, source_target_pairs={{0,8},{1,9},{2,10},{3,11},{4,12},{5,13},{6,14},{7,15},{8,0},{9,1},... | collective-permute-start | bytes 294920 | tf_op jit(solution)/shard_map/ppermute | solution.py:16
  5.6 4.9 %collective-permute-done = bf16[2,96,256]{2,1,0:T(8,128)(2,1)S(1)} collective-permute-done((bf16[2,96,256]{2,1,0:T(8,128)(2,1)S(1)}, bf16[2,96,256]{2,1,0:T(8,128)(2,1)S(1)}, u32[]{:S(2)}, u32[]{:S(2)}) %collective-permute-start) | collective-permute-done | bytes 98336 | tf_op jit(solution)/shard_map/ppermute | solution.py:16
  10.5 0.8 select_bitcast_fusion.15
  11.3 1.6 %collective-permute-start.3 = (bf16[2,96,256]{2,1,0:T(8,128)(2,1)S(1)}, bf16[2,96,256]{2,1,0:T(8,128)(2,1)S(1)}, u32[]{:S(2)}, u32[]{:S(2)}) collective-permute-start(bf16[2,96,256]{2,1,0:T(8,128)(2,1)S(1)} %pad_maximum_fusion.16), channel_id=1, source_target_pairs={{0,2},{1,3},{2,0},{3,1},{4,6},{5,7},{6,4},{7,5},{8,10},{9,11},{10,... | collective-permute-start | bytes 294920 | tf_op jit(solution)/shard_map/ppermute | solution.py:16
  13.0 0.7 collective-permute-start.1
  13.7 2.3 %collective-permute-done.3 = bf16[2,96,256]{2,1,0:T(8,128)(2,1)S(1)} collective-permute-done((bf16[2,96,256]{2,1,0:T(8,128)(2,1)S(1)}, bf16[2,96,256]{2,1,0:T(8,128)(2,1)S(1)}, u32[]{:S(2)}, u32[]{:S(2)}) %collective-permute-start.3) | collective-permute-done | bytes 98336 | tf_op jit(solution)/shard_map/ppermute | solution.py:16
  16.0 1.6 %collective-permute-done.1 = bf16[2,96,256]{2,1,0:T(8,128)(2,1)S(1)} collective-permute-done((bf16[2,96,256]{2,1,0:T(8,128)(2,1)S(1)}, bf16[2,96,256]{2,1,0:T(8,128)(2,1)S(1)}, u32[]{:S(2)}, u32[]{:S(2)}) %collective-permute-start.1) | collective-permute-done | bytes 98336 | tf_op jit(solution)/shard_map/ppermute | solution.py:16
  17.7 0.5 collective-permute-start.2
  18.3 0.8 collective-permute-start.4
  19.1 4.4 %collective-permute-done.2 = bf16[2,2,96,256]{3,2,0,1:T(8,128)(2,1)S(1)} collective-permute-done((bf16[2,2,96,256]{3,2,0,1:T(8,128)(2,1)S(1)}, bf16[2,2,96,256]{3,2,0,1:T(8,128)(2,1)S(1)}, u32[]{:S(2)}, u32[]{:S(2)}) %collective-permute-start.2) | collective-permute-done | bytes 196640 | tf_op jit(solution)/shard_map/ppermute | solution.py:16
  24.9 0.6 fusion.86
  25.5 1.2 collective-permute-done.5
  26.9 0.6 copy-done
  27.6 3.0 %convolution_bitcast_fusion.2 = f32[1536,256]{0,1:T(8,128)S(1)} fusion(bf16[1536,256]{1,0:T(8,128)(2,1)S(1)} %bitcast.310, bf16[3,512,1536]{2,1,0:T(8,128)(2,1)} %param.5), kind=kOutput, calls=%fused_computation.2 | convolution fusion | flops 805437440 | bytes 5505024 | tf_op jit(solution)/shard_map/dot_general | solution.py:10
  31.1 0.8 fusion.50
  32.0 1.2 broadcast_select_fusion.3
  33.3 4.1 %convolution_bitcast_fusion.3 = f32[1536,256]{0,1:T(8,128)} fusion(bf16[1536,256]{1,0:T(8,128)(2,1)S(1)} %bitcast.309, bf16[3,512,1536]{2,1,0:T(8,128)(2,1)} %param.5), kind=kOutput, calls=%fused_computation.3 | convolution fusion | flops 805437440 | bytes 5505024 | tf_op jit(solution)/shard_map/dot_general | solution.py:10
  37.4 1.9 %copy.33 = f32[1536,256]{1,0:T(8,128)S(1)} copy(f32[1536,256]{0,1:T(8,128)} %convolution_bitcast_fusion.3) | data formatting | bytes 3145728 | tf_op jit(solution)/shard_map/dot_general | solution.py:10
  39.3 0.8 fusion.49
  40.4 1.4 %bitcast_divide_fusion.1 = (f32[96]{0:T(128)}, f32[96]{0:T(128)}) fusion(f32[1,1536]{1,0:T(1,128)} %get-tuple-element.66, s32[]{:T(128)S(6)} %select_n.263, f32[1,1536]{1,0:T(1,128)} %get-tuple-element.57), kind=kLoop, calls=%fused_computation.188 | loop fusion | flops 288 | bytes 1540 | tf_op jit(solution)/shard_map/div | solution.py:103
  41.8 1.1 bitcast_add_fusion.2
  42.9 0.8 collective-permute-start.11
  43.9 1.6 %collective-permute-start.7 = (bf16[2,2,96,256]{3,2,0,1:T(8,128)(2,1)S(1)}, bf16[2,2,96,256]{3,2,0,1:T(8,128)(2,1)S(1)}, u32[]{:S(2)}, u32[]{:S(2)}) collective-permute-start(bf16[2,2,96,256]{3,2,0,1:T(8,128)(2,1)S(1)} %fusion.54), channel_id=1, source_target_pairs={{0,2},{1,3},{2,0},{3,1},{4,6},{5,7},{6,4},{7,5},{8,10},{9,11},{10,... | collective-permute-start | bytes 589832 | tf_op jit(solution)/shard_map/ppermute | solution.py:16
  45.5 4.5 %collective-permute-done.11 = bf16[2,2,96,256]{3,2,0,1:T(8,128)(2,1)S(1)} collective-permute-done((bf16[2,2,96,256]{3,2,0,1:T(8,128)(2,1)S(1)}, bf16[2,2,96,256]{3,2,0,1:T(8,128)(2,1)S(1)}, u32[]{:S(2)}, u32[]{:S(2)}) %collective-permute-start.11) | collective-permute-done | bytes 196640 | tf_op jit(solution)/shard_map/ppermute | solution.py:16
  50.0 1.6 %collective-permute-start.12 = (bf16[2,96,256]{2,1,0:T(8,128)(2,1)S(1)}, bf16[2,96,256]{2,1,0:T(8,128)(2,1)S(1)}, u32[]{:S(2)}, u32[]{:S(2)}) collective-permute-start(bf16[2,96,256]{2,1,0:T(8,128)(2,1)S(1)} %fusion.59), channel_id=1, source_target_pairs={{0,2},{1,3},{2,0},{3,1},{4,6},{5,7},{6,4},{7,5},{8,10},{9,11},{10,... | collective-permute-start | bytes 294920 | tf_op jit(solution)/shard_map/ppermute | solution.py:16
  51.7 0.7 collective-permute-start.8
  52.5 2.2 %collective-permute-done.12 = bf16[2,96,256]{2,1,0:T(8,128)(2,1)S(1)} collective-permute-done((bf16[2,96,256]{2,1,0:T(8,128)(2,1)S(1)}, bf16[2,96,256]{2,1,0:T(8,128)(2,1)S(1)}, u32[]{:S(2)}, u32[]{:S(2)}) %collective-permute-start.12) | collective-permute-done | bytes 98336 | tf_op jit(solution)/shard_map/ppermute | solution.py:16
  54.7 2.4 %collective-permute-start.13 = (bf16[96,256]{1,0:T(8,128)(2,1)S(1)}, bf16[96,256]{1,0:T(8,128)(2,1)S(1)}, u32[]{:S(2)}, u32[]{:S(2)}) collective-permute-start(bf16[96,256]{1,0:T(8,128)(2,1)S(1)} %fusion.77), channel_id=1, source_target_pairs={{0,8},{1,9},{2,10},{3,11},{4,12},{5,13},{6,14},{7,15},{8,0},{9,1},... | collective-permute-start | bytes 147464 | tf_op jit(solution)/shard_map/ppermute | solution.py:16
  57.2 2.2 %collective-permute-start.9 = (bf16[96,256]{1,0:T(8,128)(2,1)S(1)}, bf16[96,256]{1,0:T(8,128)(2,1)S(1)}, u32[]{:S(2)}, u32[]{:S(2)}) collective-permute-start(bf16[96,256]{1,0:T(8,128)(2,1)S(1)} %fusion.76), channel_id=1, source_target_pairs={{0,8},{1,9},{2,10},{3,11},{4,12},{5,13},{6,14},{7,15},{8,0},{9,1},... | collective-permute-start | bytes 147464 | tf_op jit(solution)/shard_map/ppermute | solution.py:16
  59.4 0.8 cosine_bitcast_fusion
  60.2 2.1 %collective-permute-done.9 = bf16[96,256]{1,0:T(8,128)(2,1)S(1)} collective-permute-done((bf16[96,256]{1,0:T(8,128)(2,1)S(1)}, bf16[96,256]{1,0:T(8,128)(2,1)S(1)}, u32[]{:S(2)}, u32[]{:S(2)}) %collective-permute-start.9) | collective-permute-done | bytes 49184 | tf_op jit(solution)/shard_map/ppermute | solution.py:16
  62.4 2.3 %collective-permute-start.14 = (bf16[2,96,256]{2,1,0:T(8,128)(2,1)S(1)}, bf16[2,96,256]{2,1,0:T(8,128)(2,1)S(1)}, u32[]{:S(2)}, u32[]{:S(2)}) collective-permute-start(bf16[2,96,256]{2,1,0:T(8,128)(2,1)S(1)} %pad_maximum_fusion.17), channel_id=1, source_target_pairs={{0,8},{1,9},{2,10},{3,11},{4,12},{5,13},{6,14},{7,15},{8,0},{9,1},... | collective-permute-start | bytes 294920 | tf_op jit(solution)/shard_map/ppermute | solution.py:16
  64.7 3.4 %collective-permute-done.14 = bf16[2,96,256]{2,1,0:T(8,128)(2,1)S(1)} collective-permute-done((bf16[2,96,256]{2,1,0:T(8,128)(2,1)S(1)}, bf16[2,96,256]{2,1,0:T(8,128)(2,1)S(1)}, u32[]{:S(2)}, u32[]{:S(2)}) %collective-permute-start.14) | collective-permute-done | bytes 98336 | tf_op jit(solution)/shard_map/ppermute | solution.py:16
  68.2 2.5 %collective-permute-start.15 = (bf16[2,96,256]{2,1,0:T(8,128)(2,1)S(1)}, bf16[2,96,256]{2,1,0:T(8,128)(2,1)S(1)}, u32[]{:S(2)}, u32[]{:S(2)}) collective-permute-start(bf16[2,96,256]{2,1,0:T(8,128)(2,1)S(1)} %pad_maximum_fusion.18), channel_id=1, source_target_pairs={{0,4},{1,5},{2,6},{3,7},{4,0},{5,1},{6,2},{7,3},{8,12},{9,13},{10,... | collective-permute-start | bytes 294920 | tf_op jit(solution)/shard_map/ppermute | solution.py:16
  70.7 1.9 %collective-permute-start.17 = (bf16[2,96,256]{2,1,0:T(8,128)(2,1)S(1)}, bf16[2,96,256]{2,1,0:T(8,128)(2,1)S(1)}, u32[]{:S(2)}, u32[]{:S(2)}) collective-permute-start(bf16[2,96,256]{2,1,0:T(8,128)(2,1)S(1)} %pad_maximum_fusion.19), channel_id=1, source_target_pairs={{0,2},{1,3},{2,0},{3,1},{4,6},{5,7},{6,4},{7,5},{8,10},{9,11},{10,... | collective-permute-start | bytes 294920 | tf_op jit(solution)/shard_map/ppermute | solution.py:16
  72.5 1.1 collective-permute-done.15
  73.7 2.5 %collective-permute-start.16 = (bf16[2,2,96,256]{3,2,0,1:T(8,128)(2,1)S(1)}, bf16[2,2,96,256]{3,2,0,1:T(8,128)(2,1)S(1)}, u32[]{:S(2)}, u32[]{:S(2)}) collective-permute-start(bf16[2,2,96,256]{3,2,0,1:T(8,128)(2,1)S(1)} %pad_maximum_fusion.12), channel_id=1, source_target_pairs={{0,2},{1,3},{2,0},{3,1},{4,6},{5,7},{6,4},{7,5},{8,10},{9,11},{10,... | collective-permute-start | bytes 589832 | tf_op jit(solution)/shard_map/ppermute | solution.py:16
  76.2 2.2 %collective-permute-start.18 = (bf16[2,2,96,256]{3,2,0,1:T(8,128)(2,1)S(1)}, bf16[2,2,96,256]{3,2,0,1:T(8,128)(2,1)S(1)}, u32[]{:S(2)}, u32[]{:S(2)}) collective-permute-start(bf16[2,2,96,256]{3,2,0,1:T(8,128)(2,1)S(1)} %pad_maximum_fusion.13), channel_id=1, source_target_pairs={{0,4},{1,5},{2,6},{3,7},{4,0},{5,1},{6,2},{7,3},{8,12},{9,13},{10,... | collective-permute-start | bytes 589832 | tf_op jit(solution)/shard_map/ppermute | solution.py:16
  78.3 1.4 %collective-permute-done.16 = bf16[2,2,96,256]{3,2,0,1:T(8,128)(2,1)S(1)} collective-permute-done((bf16[2,2,96,256]{3,2,0,1:T(8,128)(2,1)S(1)}, bf16[2,2,96,256]{3,2,0,1:T(8,128)(2,1)S(1)}, u32[]{:S(2)}, u32[]{:S(2)}) %collective-permute-start.16) | collective-permute-done | bytes 196640 | tf_op jit(solution)/shard_map/ppermute | solution.py:16
  79.9 2.1 %collective-permute-done.18 = bf16[2,2,96,256]{3,2,0,1:T(8,128)(2,1)S(1)} collective-permute-done((bf16[2,2,96,256]{3,2,0,1:T(8,128)(2,1)S(1)}, bf16[2,2,96,256]{3,2,0,1:T(8,128)(2,1)S(1)}, u32[]{:S(2)}, u32[]{:S(2)}) %collective-permute-start.18) | collective-permute-done | bytes 196640 | tf_op jit(solution)/shard_map/ppermute | solution.py:16
  82.2 2.3 %collective-permute-done.19 = bf16[2,2,2,2,96,256]{5,4,1,2,3,0:T(8,128)(2,1)S(1)} collective-permute-done((bf16[2,2,2,2,96,256]{5,4,1,2,3,0:T(8,128)(2,1)S(1)}, bf16[2,2,2,2,96,256]{5,4,1,2,3,0:T(8,128)(2,1)S(1)}, u32[]{:S(2)}, u32[]{:S(2)}) %collective-permute-start.19) | collective-permute-done | bytes 786464 | tf_op jit(solution)/shard_map/ppermute | solution.py:16
  85.2 0.9 copy.49
  86.3 3.0 %convolution_bitcast_fusion.1 = f32[1536,256]{0,1:T(8,128)S(1)} fusion(bf16[3,512,1536]{2,1,0:T(8,128)(2,1)} %param.5, bf16[1536,256]{1,0:T(8,128)(2,1)S(1)} %bitcast.308, f32[256]{0:T(256)S(1)} %add_rsqrt_fusion.1), kind=kOutput, calls=%fused_computation.1 | convolution fusion | flops 805568512 | bytes 5506048 | tf_op jit(solution)/shard_map/dot_general | solution.py:10
  89.7 0.8 fusion.48
  90.7 4.4 %convolution_bitcast_fusion = f32[1536,256]{0,1:T(8,128)} fusion(bf16[3,512,1536]{2,1,0:T(8,128)(2,1)} %param.5, bf16[1536,256]{1,0:T(8,128)(2,1)} %bitcast.307, f32[256]{0:T(256)} %copy-done.5), kind=kOutput, calls=%fused_computation | convolution fusion | flops 805568512 | bytes 5506048 | tf_op jit(solution)/shard_map/dot_general | solution.py:10
  95.1 1.9 %copy.50 = f32[1536,256]{1,0:T(8,128)S(1)} copy(f32[1536,256]{0,1:T(8,128)} %convolution_bitcast_fusion) | data formatting | bytes 3145728 | tf_op jit(solution)/shard_map/dot_general | solution.py:10
  97.7 1.0 collective-permute-start.21
  98.9 2.1 %collective-permute-start.25 = (bf16[2,2,96,256]{3,2,0,1:T(8,128)(2,1)S(1)}, bf16[2,2,96,256]{3,2,0,1:T(8,128)(2,1)S(1)}, u32[]{:S(2)}, u32[]{:S(2)}) collective-permute-start(bf16[2,2,96,256]{3,2,0,1:T(8,128)(2,1)S(1)} %fusion.57), channel_id=1, source_target_pairs={{0,4},{1,5},{2,6},{3,7},{4,0},{5,1},{6,2},{7,3},{8,12},{9,13},{10,... | collective-permute-start | bytes 589832 | tf_op jit(solution)/shard_map/ppermute | solution.py:16
  101.0 3.7 %collective-permute-done.21 = bf16[2,2,96,256]{3,2,1,0:T(8,128)(2,1)S(1)} collective-permute-done((bf16[2,2,96,256]{3,2,1,0:T(8,128)(2,1)S(1)}, bf16[2,2,96,256]{3,2,1,0:T(8,128)(2,1)S(1)}, u32[]{:S(2)}, u32[]{:S(2)}) %collective-permute-start.21) | collective-permute-done | bytes 196640 | tf_op jit(solution)/shard_map/ppermute | solution.py:16
  104.8 2.1 %collective-permute-start.22 = (bf16[2,96,256]{2,1,0:T(8,128)(2,1)S(1)}, bf16[2,96,256]{2,1,0:T(8,128)(2,1)S(1)}, u32[]{:S(2)}, u32[]{:S(2)}) collective-permute-start(bf16[2,96,256]{2,1,0:T(8,128)(2,1)S(1)} %fusion.60), channel_id=1, source_target_pairs={{0,4},{1,5},{2,6},{3,7},{4,0},{5,1},{6,2},{7,3},{8,12},{9,13},{10,... | collective-permute-start | bytes 294920 | tf_op jit(solution)/shard_map/ppermute | solution.py:16
  107.3 2.2 %collective-permute-done.22 = bf16[2,96,256]{2,1,0:T(8,128)(2,1)S(1)} collective-permute-done((bf16[2,96,256]{2,1,0:T(8,128)(2,1)S(1)}, bf16[2,96,256]{2,1,0:T(8,128)(2,1)S(1)}, u32[]{:S(2)}, u32[]{:S(2)}) %collective-permute-start.22) | collective-permute-done | bytes 98336 | tf_op jit(solution)/shard_map/ppermute | solution.py:16
  109.5 1.9 %collective-permute-start.23 = (bf16[96,256]{1,0:T(8,128)(2,1)S(1)}, bf16[96,256]{1,0:T(8,128)(2,1)S(1)}, u32[]{:S(2)}, u32[]{:S(2)}) collective-permute-start(bf16[96,256]{1,0:T(8,128)(2,1)S(1)} %fusion.78), channel_id=1, source_target_pairs={{0,8},{1,9},{2,10},{3,11},{4,12},{5,13},{6,14},{7,15},{8,0},{9,1},... | collective-permute-start | bytes 147464 | tf_op jit(solution)/shard_map/ppermute | solution.py:16
  111.7 1.3 collective-permute-start.27
  113.0 1.5 %collective-permute-done.23 = bf16[96,256]{1,0:T(8,128)(2,1)S(1)} collective-permute-done((bf16[96,256]{1,0:T(8,128)(2,1)S(1)}, bf16[96,256]{1,0:T(8,128)(2,1)S(1)}, u32[]{:S(2)}, u32[]{:S(2)}) %collective-permute-start.23) | collective-permute-done | bytes 49184 | tf_op jit(solution)/shard_map/ppermute | solution.py:16
  114.6 2.1 %collective-permute-done.27 = bf16[96,256]{1,0:T(8,128)(2,1)S(1)} collective-permute-done((bf16[96,256]{1,0:T(8,128)(2,1)S(1)}, bf16[96,256]{1,0:T(8,128)(2,1)S(1)}, u32[]{:S(2)}, u32[]{:S(2)}) %collective-permute-start.27) | collective-permute-done | bytes 49184 | tf_op jit(solution)/shard_map/ppermute | solution.py:16
  117.4 1.4 %collective-permute-start.28 = (f32[256]{0:T(256)S(1)}, f32[256]{0:T(256)S(1)}, u32[]{:S(2)}, u32[]{:S(2)}) collective-permute-start(f32[256]{0:T(256)S(1)} %add.192), channel_id=1, source_target_pairs={{0,1},{1,0},{2,3},{3,2},{4,5},{5,4},{6,7},{7,6},{8,9},{9,8},{10,11... | collective-permute-start | bytes 3080 | tf_op jit(solution)/shard_map/ppermute | solution.py:16
  118.8 1.1 collective-permute-done.30
  119.9 0.7 collective-permute-done.29
  120.6 2.7 %collective-permute-start.33 = (f32[256]{0:T(256)S(1)}, f32[256]{0:T(256)S(1)}, u32[]{:S(2)}, u32[]{:S(2)}) collective-permute-start(f32[256]{0:T(256)S(1)} %add_add_fusion), channel_id=1, source_target_pairs={{0,12},{1,13},{2,14},{3,15},{4,8},{5,9},{6,10},{7,11},{8,4},{9,5},... | collective-permute-start | bytes 3080 | tf_op jit(solution)/shard_map/ppermute | solution.py:16
  123.4 1.6 %collective-permute-start.31 = (f32[256]{0:T(256)S(1)}, f32[256]{0:T(256)S(1)}, u32[]{:S(2)}, u32[]{:S(2)}) collective-permute-start(f32[256]{0:T(256)S(1)} %add_add_fusion), channel_id=1, source_target_pairs={{0,4},{1,5},{2,6},{3,7},{4,0},{5,1},{6,2},{7,3},{8,12},{9,13},{10,... | collective-permute-start | bytes 3080 | tf_op jit(solution)/shard_map/ppermute | solution.py:16
  125.0 1.0 collective-permute-done.33
  126.0 1.7 %collective-permute-done.32 = f32[256]{0:T(256)S(1)} collective-permute-done((f32[256]{0:T(256)S(1)}, f32[256]{0:T(256)S(1)}, u32[]{:S(2)}, u32[]{:S(2)}) %collective-permute-start.32) | collective-permute-done | bytes 1056 | tf_op jit(solution)/shard_map/ppermute | solution.py:16
  127.8 0.7 broadcast_multiply_fusion
  (103 shorter events, 7.6 us)
Async XLA Ops:
  1.5 9.0 %collective-permute-start = (bf16[2,96,256]{2,1,0:T(8,128)(2,1)S(1)}, bf16[2,96,256]{2,1,0:T(8,128)(2,1)S(1)}, u32[]{:S(2)}, u32[]{:S(2)}) collective-permute-start(bf16[2,96,256]{2,1,0:T(8,128)(2,1)S(1)} %pad_maximum_fusion.14), channel_id=1, source_target_pairs={{0,8},{1,9},{2,10},{3,11},{4,12},{5,13},{6,14},{7,15},{8,0},{9,1},... | collective-permute-start | bytes 294920 | tf_op jit(solution)/shard_map/ppermute | solution.py:16
  11.3 4.7 %collective-permute-start.3 = (bf16[2,96,256]{2,1,0:T(8,128)(2,1)S(1)}, bf16[2,96,256]{2,1,0:T(8,128)(2,1)S(1)}, u32[]{:S(2)}, u32[]{:S(2)}) collective-permute-start(bf16[2,96,256]{2,1,0:T(8,128)(2,1)S(1)} %pad_maximum_fusion.16), channel_id=1, source_target_pairs={{0,2},{1,3},{2,0},{3,1},{4,6},{5,7},{6,4},{7,5},{8,10},{9,11},{10,... | collective-permute-start | bytes 294920 | tf_op jit(solution)/shard_map/ppermute | solution.py:16
  13.0 4.7 %collective-permute-start.1 = (bf16[2,96,256]{2,1,0:T(8,128)(2,1)S(1)}, bf16[2,96,256]{2,1,0:T(8,128)(2,1)S(1)}, u32[]{:S(2)}, u32[]{:S(2)}) collective-permute-start(bf16[2,96,256]{2,1,0:T(8,128)(2,1)S(1)} %pad_maximum_fusion.15), channel_id=1, source_target_pairs={{0,4},{1,5},{2,6},{3,7},{4,0},{5,1},{6,2},{7,3},{8,12},{9,13},{10,... | collective-permute-start | bytes 294920 | tf_op jit(solution)/shard_map/ppermute | solution.py:16
  17.7 5.7 %collective-permute-start.2 = (bf16[2,2,96,256]{3,2,0,1:T(8,128)(2,1)S(1)}, bf16[2,2,96,256]{3,2,0,1:T(8,128)(2,1)S(1)}, u32[]{:S(2)}, u32[]{:S(2)}) collective-permute-start(bf16[2,2,96,256]{3,2,0,1:T(8,128)(2,1)S(1)} %pad_maximum_fusion.10), channel_id=1, source_target_pairs={{0,2},{1,3},{2,0},{3,1},{4,6},{5,7},{6,4},{7,5},{8,10},{9,11},{10,... | collective-permute-start | bytes 589832 | tf_op jit(solution)/shard_map/ppermute | solution.py:16
  18.3 5.7 %collective-permute-start.4 = (bf16[2,2,96,256]{3,2,0,1:T(8,128)(2,1)S(1)}, bf16[2,2,96,256]{3,2,0,1:T(8,128)(2,1)S(1)}, u32[]{:S(2)}, u32[]{:S(2)}) collective-permute-start(bf16[2,2,96,256]{3,2,0,1:T(8,128)(2,1)S(1)} %pad_maximum_fusion.11), channel_id=1, source_target_pairs={{0,4},{1,5},{2,6},{3,7},{4,0},{5,1},{6,2},{7,3},{8,12},{9,13},{10,... | collective-permute-start | bytes 589832 | tf_op jit(solution)/shard_map/ppermute | solution.py:16
  24.1 0.7 copy-start.1
  24.2 0.7 copy-start.2
  24.3 2.4 %collective-permute-start.5 = (bf16[2,2,2,2,96,256]{5,4,3,2,1,0:T(8,128)(2,1)S(1)}, bf16[2,2,2,2,96,256]{5,4,3,2,1,0:T(8,128)(2,1)S(1)}, u32[]{:S(2)}, u32[]{:S(2)}) collective-permute-start(bf16[2,2,2,2,96,256]{5,4,3,2,1,0:T(8,128)(2,1)S(1)} %copy.30), channel_id=1, source_target_pairs={{0,1},{1,0},{2,3},{3,2},{4,5},{5,4},{6,7},{7,6},{8,9},{9,8},{10,11... | collective-permute-start | bytes 2359304 | tf_op jit(solution)/shard_map/ppermute | solution.py:16
  26.7 0.9 copy-start
  31.9 9.9 %collective-permute-start.10 = (bf16[2,2,2,96,256]{4,3,0,2,1:T(8,128)(2,1)}, bf16[2,2,2,96,256]{4,3,0,2,1:T(8,128)(2,1)}, u32[]{:S(2)}, u32[]{:S(2)}) collective-permute-start(bf16[2,2,2,96,256]{4,3,0,2,1:T(8,128)(2,1)} %fusion.50), channel_id=1, source_target_pairs={{0,1},{1,0},{2,3},{3,2},{4,5},{5,4},{6,7},{7,6},{8,9},{9,8},{10,11... | collective-permute-start | bytes 1179656 | tf_op jit(solution)/shard_map/ppermute | solution.py:16
  40.1 3.7 %collective-permute-start.6 = (bf16[2,2,2,96,256]{4,3,0,1,2:T(8,128)(2,1)}, bf16[2,2,2,96,256]{4,3,0,1,2:T(8,128)(2,1)S(1)}, u32[]{:S(2)}, u32[]{:S(2)}) collective-permute-start(bf16[2,2,2,96,256]{4,3,0,1,2:T(8,128)(2,1)} %fusion.49), channel_id=1, source_target_pairs={{0,1},{1,0},{2,3},{3,2},{4,5},{5,4},{6,7},{7,6},{8,9},{9,8},{10,11... | collective-permute-start | bytes 1179656 | tf_op jit(solution)/shard_map/ppermute | solution.py:16
  42.9 7.0 %collective-permute-start.11 = (bf16[2,2,96,256]{3,2,0,1:T(8,128)(2,1)S(1)}, bf16[2,2,96,256]{3,2,0,1:T(8,128)(2,1)S(1)}, u32[]{:S(2)}, u32[]{:S(2)}) collective-permute-start(bf16[2,2,96,256]{3,2,0,1:T(8,128)(2,1)S(1)} %fusion.55), channel_id=1, source_target_pairs={{0,4},{1,5},{2,6},{3,7},{4,0},{5,1},{6,2},{7,3},{8,12},{9,13},{10,... | collective-permute-start | bytes 589832 | tf_op jit(solution)/shard_map/ppermute | solution.py:16
  43.9 18.4 %copy-start.3 = (f32[96]{0:T(128)S(1)}, f32[96]{0:T(128)}, u32[]{:S(2)}) copy-start(f32[96]{0:T(128)} %get-tuple-element.60) | copy-start | bytes 1156
  43.9 18.4 %copy-start.4 = (f32[96]{0:T(128)S(1)}, f32[96]{0:T(128)}, u32[]{:S(2)}) copy-start(f32[96]{0:T(128)} %get-tuple-element.61) | copy-start | bytes 1156
  43.9 7.8 %collective-permute-start.7 = (bf16[2,2,96,256]{3,2,0,1:T(8,128)(2,1)S(1)}, bf16[2,2,96,256]{3,2,0,1:T(8,128)(2,1)S(1)}, u32[]{:S(2)}, u32[]{:S(2)}) collective-permute-start(bf16[2,2,96,256]{3,2,0,1:T(8,128)(2,1)S(1)} %fusion.54), channel_id=1, source_target_pairs={{0,2},{1,3},{2,0},{3,1},{4,6},{5,7},{6,4},{7,5},{8,10},{9,11},{10,... | collective-permute-start | bytes 589832 | tf_op jit(solution)/shard_map/ppermute | solution.py:16
  50.0 4.7 %collective-permute-start.12 = (bf16[2,96,256]{2,1,0:T(8,128)(2,1)S(1)}, bf16[2,96,256]{2,1,0:T(8,128)(2,1)S(1)}, u32[]{:S(2)}, u32[]{:S(2)}) collective-permute-start(bf16[2,96,256]{2,1,0:T(8,128)(2,1)S(1)} %fusion.59), channel_id=1, source_target_pairs={{0,2},{1,3},{2,0},{3,1},{4,6},{5,7},{6,4},{7,5},{8,10},{9,11},{10,... | collective-permute-start | bytes 294920 | tf_op jit(solution)/shard_map/ppermute | solution.py:16
  51.7 5.5 %collective-permute-start.8 = (bf16[2,96,256]{2,1,0:T(8,128)(2,1)S(1)}, bf16[2,96,256]{2,1,0:T(8,128)(2,1)S(1)}, u32[]{:S(2)}, u32[]{:S(2)}) collective-permute-start(bf16[2,96,256]{2,1,0:T(8,128)(2,1)S(1)} %fusion.58), channel_id=1, source_target_pairs={{0,4},{1,5},{2,6},{3,7},{4,0},{5,1},{6,2},{7,3},{8,12},{9,13},{10,... | collective-permute-start | bytes 294920 | tf_op jit(solution)/shard_map/ppermute | solution.py:16
  54.7 5.4 %collective-permute-start.13 = (bf16[96,256]{1,0:T(8,128)(2,1)S(1)}, bf16[96,256]{1,0:T(8,128)(2,1)S(1)}, u32[]{:S(2)}, u32[]{:S(2)}) collective-permute-start(bf16[96,256]{1,0:T(8,128)(2,1)S(1)} %fusion.77), channel_id=1, source_target_pairs={{0,8},{1,9},{2,10},{3,11},{4,12},{5,13},{6,14},{7,15},{8,0},{9,1},... | collective-permute-start | bytes 147464 | tf_op jit(solution)/shard_map/ppermute | solution.py:16
  57.2 5.1 %collective-permute-start.9 = (bf16[96,256]{1,0:T(8,128)(2,1)S(1)}, bf16[96,256]{1,0:T(8,128)(2,1)S(1)}, u32[]{:S(2)}, u32[]{:S(2)}) collective-permute-start(bf16[96,256]{1,0:T(8,128)(2,1)S(1)} %fusion.76), channel_id=1, source_target_pairs={{0,8},{1,9},{2,10},{3,11},{4,12},{5,13},{6,14},{7,15},{8,0},{9,1},... | collective-permute-start | bytes 147464 | tf_op jit(solution)/shard_map/ppermute | solution.py:16
  62.4 5.7 %collective-permute-start.14 = (bf16[2,96,256]{2,1,0:T(8,128)(2,1)S(1)}, bf16[2,96,256]{2,1,0:T(8,128)(2,1)S(1)}, u32[]{:S(2)}, u32[]{:S(2)}) collective-permute-start(bf16[2,96,256]{2,1,0:T(8,128)(2,1)S(1)} %pad_maximum_fusion.17), channel_id=1, source_target_pairs={{0,8},{1,9},{2,10},{3,11},{4,12},{5,13},{6,14},{7,15},{8,0},{9,1},... | collective-permute-start | bytes 294920 | tf_op jit(solution)/shard_map/ppermute | solution.py:16
  68.2 5.4 %collective-permute-start.15 = (bf16[2,96,256]{2,1,0:T(8,128)(2,1)S(1)}, bf16[2,96,256]{2,1,0:T(8,128)(2,1)S(1)}, u32[]{:S(2)}, u32[]{:S(2)}) collective-permute-start(bf16[2,96,256]{2,1,0:T(8,128)(2,1)S(1)} %pad_maximum_fusion.18), channel_id=1, source_target_pairs={{0,4},{1,5},{2,6},{3,7},{4,0},{5,1},{6,2},{7,3},{8,12},{9,13},{10,... | collective-permute-start | bytes 294920 | tf_op jit(solution)/shard_map/ppermute | solution.py:16
  70.7 5.5 %collective-permute-start.17 = (bf16[2,96,256]{2,1,0:T(8,128)(2,1)S(1)}, bf16[2,96,256]{2,1,0:T(8,128)(2,1)S(1)}, u32[]{:S(2)}, u32[]{:S(2)}) collective-permute-start(bf16[2,96,256]{2,1,0:T(8,128)(2,1)S(1)} %pad_maximum_fusion.19), channel_id=1, source_target_pairs={{0,2},{1,3},{2,0},{3,1},{4,6},{5,7},{6,4},{7,5},{8,10},{9,11},{10,... | collective-permute-start | bytes 294920 | tf_op jit(solution)/shard_map/ppermute | solution.py:16
  73.7 6.1 %collective-permute-start.16 = (bf16[2,2,96,256]{3,2,0,1:T(8,128)(2,1)S(1)}, bf16[2,2,96,256]{3,2,0,1:T(8,128)(2,1)S(1)}, u32[]{:S(2)}, u32[]{:S(2)}) collective-permute-start(bf16[2,2,96,256]{3,2,0,1:T(8,128)(2,1)S(1)} %pad_maximum_fusion.12), channel_id=1, source_target_pairs={{0,2},{1,3},{2,0},{3,1},{4,6},{5,7},{6,4},{7,5},{8,10},{9,11},{10,... | collective-permute-start | bytes 589832 | tf_op jit(solution)/shard_map/ppermute | solution.py:16
  76.2 5.8 %collective-permute-start.18 = (bf16[2,2,96,256]{3,2,0,1:T(8,128)(2,1)S(1)}, bf16[2,2,96,256]{3,2,0,1:T(8,128)(2,1)S(1)}, u32[]{:S(2)}, u32[]{:S(2)}) collective-permute-start(bf16[2,2,96,256]{3,2,0,1:T(8,128)(2,1)S(1)} %pad_maximum_fusion.13), channel_id=1, source_target_pairs={{0,4},{1,5},{2,6},{3,7},{4,0},{5,1},{6,2},{7,3},{8,12},{9,13},{10,... | collective-permute-start | bytes 589832 | tf_op jit(solution)/shard_map/ppermute | solution.py:16
  82.1 2.4 %collective-permute-start.19 = (bf16[2,2,2,2,96,256]{5,4,1,2,3,0:T(8,128)(2,1)S(1)}, bf16[2,2,2,2,96,256]{5,4,1,2,3,0:T(8,128)(2,1)S(1)}, u32[]{:S(2)}, u32[]{:S(2)}) collective-permute-start(bf16[2,2,2,2,96,256]{5,4,1,2,3,0:T(8,128)(2,1)S(1)} %pad_maximum_fusion.3), channel_id=1, source_target_pairs={{0,1},{1,0},{2,3},{3,2},{4,5},{5,4},{6,7},{7,6},{8,9},{9,8},{10,11... | collective-permute-start | bytes 2359304 | tf_op jit(solution)/shard_map/ppermute | solution.py:16
  86.2 3.0 %copy-start.5 = (f32[256]{0:T(256)}, f32[256]{0:T(256)S(1)}, u32[]{:S(2)}) copy-start(f32[256]{0:T(256)S(1)} %add_rsqrt_fusion.1) | copy-start | bytes 3076
  90.5 7.0 %collective-permute-start.20 = (bf16[2,2,2,96,256]{4,3,2,1,0:T(8,128)(2,1)}, bf16[2,2,2,96,256]{4,3,2,1,0:T(8,128)(2,1)S(1)}, u32[]{:S(2)}, u32[]{:S(2)}) collective-permute-start(bf16[2,2,2,96,256]{4,3,2,1,0:T(8,128)(2,1)} %fusion.48), channel_id=1, source_target_pairs={{0,1},{1,0},{2,3},{3,2},{4,5},{5,4},{6,7},{7,6},{8,9},{9,8},{10,11... | collective-permute-start | bytes 1179656 | tf_op jit(solution)/shard_map/ppermute | solution.py:16
  97.0 1.8 %collective-permute-start.24 = (bf16[2,2,2,96,256]{4,3,0,2,1:T(8,128)(2,1)S(1)}, bf16[2,2,2,96,256]{4,3,0,2,1:T(8,128)(2,1)S(1)}, u32[]{:S(2)}, u32[]{:S(2)}) collective-permute-start(bf16[2,2,2,96,256]{4,3,0,2,1:T(8,128)(2,1)S(1)} %fusion.51), channel_id=1, source_target_pairs={{0,1},{1,0},{2,3},{3,2},{4,5},{5,4},{6,7},{7,6},{8,9},{9,8},{10,11... | collective-permute-start | bytes 1179656 | tf_op jit(solution)/shard_map/ppermute | solution.py:16
  97.7 7.0 %collective-permute-start.21 = (bf16[2,2,96,256]{3,2,1,0:T(8,128)(2,1)S(1)}, bf16[2,2,96,256]{3,2,1,0:T(8,128)(2,1)S(1)}, u32[]{:S(2)}, u32[]{:S(2)}) collective-permute-start(bf16[2,2,96,256]{3,2,1,0:T(8,128)(2,1)S(1)} %fusion.56), channel_id=1, source_target_pairs={{0,2},{1,3},{2,0},{3,1},{4,6},{5,7},{6,4},{7,5},{8,10},{9,11},{10,... | collective-permute-start | bytes 589832 | tf_op jit(solution)/shard_map/ppermute | solution.py:16
  98.9 7.9 %collective-permute-start.25 = (bf16[2,2,96,256]{3,2,0,1:T(8,128)(2,1)S(1)}, bf16[2,2,96,256]{3,2,0,1:T(8,128)(2,1)S(1)}, u32[]{:S(2)}, u32[]{:S(2)}) collective-permute-start(bf16[2,2,96,256]{3,2,0,1:T(8,128)(2,1)S(1)} %fusion.57), channel_id=1, source_target_pairs={{0,4},{1,5},{2,6},{3,7},{4,0},{5,1},{6,2},{7,3},{8,12},{9,13},{10,... | collective-permute-start | bytes 589832 | tf_op jit(solution)/shard_map/ppermute | solution.py:16
  104.8 4.7 %collective-permute-start.22 = (bf16[2,96,256]{2,1,0:T(8,128)(2,1)S(1)}, bf16[2,96,256]{2,1,0:T(8,128)(2,1)S(1)}, u32[]{:S(2)}, u32[]{:S(2)}) collective-permute-start(bf16[2,96,256]{2,1,0:T(8,128)(2,1)S(1)} %fusion.60), channel_id=1, source_target_pairs={{0,4},{1,5},{2,6},{3,7},{4,0},{5,1},{6,2},{7,3},{8,12},{9,13},{10,... | collective-permute-start | bytes 294920 | tf_op jit(solution)/shard_map/ppermute | solution.py:16
  106.9 4.7 %collective-permute-start.26 = (bf16[2,96,256]{2,1,0:T(8,128)(2,1)S(1)}, bf16[2,96,256]{2,1,0:T(8,128)(2,1)S(1)}, u32[]{:S(2)}, u32[]{:S(2)}) collective-permute-start(bf16[2,96,256]{2,1,0:T(8,128)(2,1)S(1)} %fusion.61), channel_id=1, source_target_pairs={{0,2},{1,3},{2,0},{3,1},{4,6},{5,7},{6,4},{7,5},{8,10},{9,11},{10,... | collective-permute-start | bytes 294920 | tf_op jit(solution)/shard_map/ppermute | solution.py:16
  109.5 5.1 %collective-permute-start.23 = (bf16[96,256]{1,0:T(8,128)(2,1)S(1)}, bf16[96,256]{1,0:T(8,128)(2,1)S(1)}, u32[]{:S(2)}, u32[]{:S(2)}) collective-permute-start(bf16[96,256]{1,0:T(8,128)(2,1)S(1)} %fusion.78), channel_id=1, source_target_pairs={{0,8},{1,9},{2,10},{3,11},{4,12},{5,13},{6,14},{7,15},{8,0},{9,1},... | collective-permute-start | bytes 147464 | tf_op jit(solution)/shard_map/ppermute | solution.py:16
  111.7 5.1 %collective-permute-start.27 = (bf16[96,256]{1,0:T(8,128)(2,1)S(1)}, bf16[96,256]{1,0:T(8,128)(2,1)S(1)}, u32[]{:S(2)}, u32[]{:S(2)}) collective-permute-start(bf16[96,256]{1,0:T(8,128)(2,1)S(1)} %fusion.79), channel_id=1, source_target_pairs={{0,8},{1,9},{2,10},{3,11},{4,12},{5,13},{6,14},{7,15},{8,0},{9,1},... | collective-permute-start | bytes 147464 | tf_op jit(solution)/shard_map/ppermute | solution.py:16
  116.9 3.1 %collective-permute-start.30 = (f32[256]{0:T(256)S(1)}, f32[256]{0:T(256)S(1)}, u32[]{:S(2)}, u32[]{:S(2)}) collective-permute-start(f32[256]{0:T(256)S(1)} %add.192), channel_id=1, source_target_pairs={{0,3},{1,2},{2,1},{3,0},{4,7},{5,6},{6,5},{7,4},{8,11},{9,10},{10,... | collective-permute-start | bytes 3080 | tf_op jit(solution)/shard_map/ppermute | solution.py:16
  116.9 3.6 %collective-permute-start.29 = (f32[256]{0:T(256)S(1)}, f32[256]{0:T(256)S(1)}, u32[]{:S(2)}, u32[]{:S(2)}) collective-permute-start(f32[256]{0:T(256)S(1)} %add.192), channel_id=1, source_target_pairs={{0,2},{1,3},{2,0},{3,1},{4,6},{5,7},{6,4},{7,5},{8,10},{9,11},{10,... | collective-permute-start | bytes 3080 | tf_op jit(solution)/shard_map/ppermute | solution.py:16
  117.4 3.2 %collective-permute-start.28 = (f32[256]{0:T(256)S(1)}, f32[256]{0:T(256)S(1)}, u32[]{:S(2)}, u32[]{:S(2)}) collective-permute-start(f32[256]{0:T(256)S(1)} %add.192), channel_id=1, source_target_pairs={{0,1},{1,0},{2,3},{3,2},{4,5},{5,4},{6,7},{7,6},{8,9},{9,8},{10,11... | collective-permute-start | bytes 3080 | tf_op jit(solution)/shard_map/ppermute | solution.py:16
  120.6 5.4 %collective-permute-start.33 = (f32[256]{0:T(256)S(1)}, f32[256]{0:T(256)S(1)}, u32[]{:S(2)}, u32[]{:S(2)}) collective-permute-start(f32[256]{0:T(256)S(1)} %add_add_fusion), channel_id=1, source_target_pairs={{0,12},{1,13},{2,14},{3,15},{4,8},{5,9},{6,10},{7,11},{8,4},{9,5},... | collective-permute-start | bytes 3080 | tf_op jit(solution)/shard_map/ppermute | solution.py:16
  123.3 4.5 %collective-permute-start.32 = (f32[256]{0:T(256)S(1)}, f32[256]{0:T(256)S(1)}, u32[]{:S(2)}, u32[]{:S(2)}) collective-permute-start(f32[256]{0:T(256)S(1)} %add_add_fusion), channel_id=1, source_target_pairs={{0,8},{1,9},{2,10},{3,11},{4,12},{5,13},{6,14},{7,15},{8,0},{9,1},... | collective-permute-start | bytes 3080 | tf_op jit(solution)/shard_map/ppermute | solution.py:16
  123.4 4.3 %collective-permute-start.31 = (f32[256]{0:T(256)S(1)}, f32[256]{0:T(256)S(1)}, u32[]{:S(2)}, u32[]{:S(2)}) collective-permute-start(f32[256]{0:T(256)S(1)} %add_add_fusion), channel_id=1, source_target_pairs={{0,4},{1,5},{2,6},{3,7},{4,0},{5,1},{6,2},{7,3},{8,12},{9,13},{10,... | collective-permute-start | bytes 3080 | tf_op jit(solution)/shard_map/ppermute | solution.py:16

commit v14 on v11

--- a/solution.py
+++ b/solution.py
@@ -27,7 +27,9 @@
         mine = (me >> bit) & 1
         keep = lax.dynamic_index_in_dim(cur, mine, axis=axis, keepdims=False)
         send = lax.dynamic_index_in_dim(cur, 1 - mine, axis=axis, keepdims=False)
-        cur = keep + exchange(send.astype(jnp.bfloat16), 1 << bit, devices).astype(jnp.float32)
+        cur = keep.astype(jnp.float32) + exchange(
+            send.astype(jnp.bfloat16), 1 << bit, devices
+        ).astype(jnp.float32)
     return cur
 
 
@@ -82,7 +84,9 @@
             projected = jnp.dot(panels[sector], gathered, preferred_element_type=jnp.float32)
             if scale is not None:
                 projected = projected * scale[None, :]
-            halves.append(contract_rows(panels[sector + 1], projected.astype(jnp.bfloat16)))
+            halves.append(
+                contract_rows(panels[sector + 1], projected.astype(jnp.bfloat16)).astype(jnp.bfloat16)
+            )
         rot_amp = halving_reduce_scatter(halves[0], devices, order_amp)
         rot_der = halving_reduce_scatter(halves[1], devices, order_der)
         angle_rows = lax.dynamic_slice_in_dim(phase[sector], first_row, chan_rows, 0)

time: 122 us -> 111 us (0.910)
  waiting for transfers between devices: 42.9 us -> 53.1 us
  local copies, waits for them, and re-layouts: 10.7 us -> 2.09 us
  starting transfers between devices: 44.4 us -> 37 us
  other arithmetic: 8.28 us -> 4.98 us
  matrix products: 14.5 us -> 11.9 us
    ppermute x38, waiting for transfers between devices: 42.9 us -> 53.1 us  [exchange(): return lax.ppermute(x, 'row', [(i, i ^ distance) for i in range(devices)])]
    ppermute x38, starting transfers between devices: 44.4 us -> 37 us  [exchange(): return lax.ppermute(x, 'row', [(i, i ^ distance) for i in range(devices)])]
    dot_general x4 -> x0, local copies, waits for them, and re-layouts: 4.68 us -> none  [contract_rows(): lax.dot_general(left, right, (((0,), (0,)), ((), ())), preferred_element_...]
    dot_general x4, matrix products: 14.5 us -> 11.9 us  [contract_rows(): lax.dot_general(left, right, (((0,), (0,)), ((), ())), preferred_element_...]
    convert_element_type x16 -> x12, local copies, waits for them, and re-layouts: 2.71 us -> 0.27 us  [halving_reduce_scatter(): send.astype(jnp.bfloat16)]
    another operation x4, local copies, waits for them, and re-layouts: 1.82 us -> 0.19 us  [doubling_all_gather(): jnp.stack([jnp.where(low, cur, other), jnp.where(low, other, cur)], axis=...]
    div x1, other arithmetic: 1.39 us -> 0.11 us  [shards(): new_amp = cosine * rot_amp + sine / wave * rot_der]
  transfers between devices with their start and end apart: 38 -> 38, of which waited for: 24 -> 30; matrix products, arithmetic and copies ran while one was open for 22% -> 10% of each run, Pallas kernels for 0% -> 0%
where the time goes in v14:
time: 111 us; the launch traced here: 110 us
  waiting for transfers between devices  53.1 us (48%)
  starting transfers between devices  37 us (33%)
  matrix products  11.9 us (11%)
  other arithmetic  4.98 us (4%)
  local copies, waits for them, and re-layouts  2.09 us (2%)
  between operations  1.32 us (1%)
    ppermute x38, waiting for transfers between devices, exchange(): return lax.ppermute(x, 'row', [(i, i ^ distance) for i in range(devices)])  53.1 us
    ppermute x38, starting transfers between devices, exchange(): return lax.ppermute(x, 'row', [(i, i ^ distance) for i in range(devices)])  37 us
    dot_general x4, matrix products, contract_rows(): lax.dot_general(left, right, (((0,), (0,)), ((), ())), preferred_element_...  11.9 us
    another operation x32, other arithmetic, doubling_all_gather(): jnp.stack([jnp.where(low, cur, other), jnp.where(low, other, cur)], axis=...  2.76 us
  transfers between devices with their start and end apart: 38, of which 30 were waited for; matrix products, arithmetic and copies ran while one was open for 10% of the time, Pallas kernels for 0%

profile of v14, /device:TPU:0, one launch (start us, length us, event | category | flops | bytes accessed | tf_op | source)
XLA Modules:
  0.0 110.4 jit_solution(7441981214950601693)
XLA Ops:
  0.6 4.1 %collective-permute-start = (bf16[96,256]{1,0:T(8,128)(2,1)}, bf16[96,256]{1,0:T(8,128)(2,1)S(1)}, u32[]{:S(2)}, u32[]{:S(2)}) collective-permute-start(bf16[96,256]{1,0:T(8,128)(2,1)} %param.6), channel_id=1, source_target_pairs={{0,8},{1,9},{2,10},{3,11},{4,12},{5,13},{6,14},{7,15},{8,0},{9,1},... | collective-permute-start | bytes 147464 | tf_op jit(solution)/shard_map/ppermute | solution.py:16
  4.8 2.7 %collective-permute-done = bf16[96,256]{1,0:T(8,128)(2,1)S(1)} collective-permute-done((bf16[96,256]{1,0:T(8,128)(2,1)}, bf16[96,256]{1,0:T(8,128)(2,1)S(1)}, u32[]{:S(2)}, u32[]{:S(2)}) %collective-permute-start) | collective-permute-done | bytes 49184 | tf_op jit(solution)/shard_map/ppermute | solution.py:16
  7.5 0.8 select_bitcast_fusion.31
  8.4 2.2 %collective-permute-start.1 = (bf16[2,96,256]{2,1,0:T(8,128)(2,1)S(1)}, bf16[2,96,256]{2,1,0:T(8,128)(2,1)S(1)}, u32[]{:S(2)}, u32[]{:S(2)}) collective-permute-start(bf16[2,96,256]{2,1,0:T(8,128)(2,1)S(1)} %pad_maximum_fusion.12), channel_id=1, source_target_pairs={{0,4},{1,5},{2,6},{3,7},{4,0},{5,1},{6,2},{7,3},{8,12},{9,13},{10,... | collective-permute-start | bytes 294920 | tf_op jit(solution)/shard_map/ppermute | solution.py:16
  10.6 0.8 select_bitcast_fusion.29
  11.4 1.6 %collective-permute-start.9 = (bf16[2,96,256]{2,1,0:T(8,128)(2,1)S(1)}, bf16[2,96,256]{2,1,0:T(8,128)(2,1)S(1)}, u32[]{:S(2)}, u32[]{:S(2)}) collective-permute-start(bf16[2,96,256]{2,1,0:T(8,128)(2,1)S(1)} %pad_maximum_fusion.13), channel_id=1, source_target_pairs={{0,2},{1,3},{2,0},{3,1},{4,6},{5,7},{6,4},{7,5},{8,10},{9,11},{10,... | collective-permute-start | bytes 294920 | tf_op jit(solution)/shard_map/ppermute | solution.py:16
  13.0 0.5 collective-permute-done.1
  13.5 1.6 %collective-permute-start.2 = (bf16[2,2,96,256]{3,2,0,1:T(8,128)(2,1)S(1)}, bf16[2,2,96,256]{3,2,0,1:T(8,128)(2,1)S(1)}, u32[]{:S(2)}, u32[]{:S(2)}) collective-permute-start(bf16[2,2,96,256]{3,2,0,1:T(8,128)(2,1)S(1)} %pad_maximum_fusion.8), channel_id=1, source_target_pairs={{0,2},{1,3},{2,0},{3,1},{4,6},{5,7},{6,4},{7,5},{8,10},{9,11},{10,... | collective-permute-start | bytes 589832 | tf_op jit(solution)/shard_map/ppermute | solution.py:16
  15.1 1.6 %collective-permute-done.9 = bf16[2,96,256]{2,1,0:T(8,128)(2,1)S(1)} collective-permute-done((bf16[2,96,256]{2,1,0:T(8,128)(2,1)S(1)}, bf16[2,96,256]{2,1,0:T(8,128)(2,1)S(1)}, u32[]{:S(2)}, u32[]{:S(2)}) %collective-permute-start.9) | collective-permute-done | bytes 98336 | tf_op jit(solution)/shard_map/ppermute | solution.py:16
  16.8 0.7 collective-permute-start.10
  17.5 2.8 %collective-permute-done.2 = bf16[2,2,96,256]{3,2,0,1:T(8,128)(2,1)S(1)} collective-permute-done((bf16[2,2,96,256]{3,2,0,1:T(8,128)(2,1)S(1)}, bf16[2,2,96,256]{3,2,0,1:T(8,128)(2,1)S(1)}, u32[]{:S(2)}, u32[]{:S(2)}) %collective-permute-start.2) | collective-permute-done | bytes 196640 | tf_op jit(solution)/shard_map/ppermute | solution.py:16
  20.5 2.0 %collective-permute-done.10 = bf16[2,2,96,256]{3,2,1,0:T(8,128)(2,1)S(1)} collective-permute-done((bf16[2,2,96,256]{3,2,1,0:T(8,128)(2,1)S(1)}, bf16[2,2,96,256]{3,2,1,0:T(8,128)(2,1)S(1)}, u32[]{:S(2)}, u32[]{:S(2)}) %collective-permute-start.10) | collective-permute-done | bytes 196640 | tf_op jit(solution)/shard_map/ppermute | solution.py:16
  23.0 3.0 %fusion = bf16[1536,256]{0,1:T(8,128)(2,1)S(1)} fusion(bf16[1536,256]{1,0:T(8,128)(2,1)S(1)} %bitcast.259, bf16[3,512,1536]{2,1,0:T(8,128)(2,1)} %param.5), kind=kOutput, calls=%fused_computation.4 | convolution fusion | flops 805830656 | bytes 4718592 | tf_op jit(solution)/shard_map/dot_general | solution.py:10
  25.9 0.3 copy.22
  26.4 3.0 %fusion.1 = bf16[1536,256]{0,1:T(8,128)(2,1)S(1)} fusion(bf16[1536,256]{1,0:T(8,128)(2,1)S(1)} %bitcast.260, bf16[3,512,1536]{2,1,0:T(8,128)(2,1)} %param.5), kind=kOutput, calls=%fused_computation.5 | convolution fusion | flops 805830656 | bytes 4718592 | tf_op jit(solution)/shard_map/dot_general | solution.py:10
  29.9 0.5 collective-permute-start.4
  30.5 0.5 collective-permute-start.12
  31.1 0.6 collective-permute-done.4
  31.9 1.7 %collective-permute-start.5 = (bf16[2,2,96,256]{3,2,0,1:T(8,128)(2,1)S(1)}, bf16[2,2,96,256]{3,2,0,1:T(8,128)(2,1)S(1)}, u32[]{:S(2)}, u32[]{:S(2)}) collective-permute-start(bf16[2,2,96,256]{3,2,0,1:T(8,128)(2,1)S(1)} %fusion.54), channel_id=1, source_target_pairs={{0,2},{1,3},{2,0},{3,1},{4,6},{5,7},{6,4},{7,5},{8,10},{9,11},{10,... | collective-permute-start | bytes 589832 | tf_op jit(solution)/shard_map/ppermute | solution.py:16
  33.7 0.6 collective-permute-start.13
  34.3 4.8 %collective-permute-done.5 = bf16[2,2,96,256]{3,2,0,1:T(8,128)(2,1)S(1)} collective-permute-done((bf16[2,2,96,256]{3,2,0,1:T(8,128)(2,1)S(1)}, bf16[2,2,96,256]{3,2,0,1:T(8,128)(2,1)S(1)}, u32[]{:S(2)}, u32[]{:S(2)}) %collective-permute-start.5) | collective-permute-done | bytes 196640 | tf_op jit(solution)/shard_map/ppermute | solution.py:16
  39.2 0.7 collective-permute-start.6
  39.9 0.7 collective-permute-done.13
  40.7 0.9 collective-permute-start.14
  41.6 2.3 %collective-permute-done.6 = bf16[2,96,256]{2,1,0:T(8,128)(2,1)S(1)} collective-permute-done((bf16[2,96,256]{2,1,0:T(8,128)(2,1)S(1)}, bf16[2,96,256]{2,1,0:T(8,128)(2,1)S(1)}, u32[]{:S(2)}, u32[]{:S(2)}) %collective-permute-start.6) | collective-permute-done | bytes 98336 | tf_op jit(solution)/shard_map/ppermute | solution.py:16
  43.9 3.7 %collective-permute-start.7 = (bf16[96,256]{1,0:T(8,128)(2,1)S(1)}, bf16[96,256]{1,0:T(8,128)(2,1)S(1)}, u32[]{:S(2)}, u32[]{:S(2)}) collective-permute-start(bf16[96,256]{1,0:T(8,128)(2,1)S(1)} %fusion.62), channel_id=1, source_target_pairs={{0,8},{1,9},{2,10},{3,11},{4,12},{5,13},{6,14},{7,15},{8,0},{9,1},... | collective-permute-start | bytes 147464 | tf_op jit(solution)/shard_map/ppermute | solution.py:16
  47.7 1.0 collective-permute-start.15
  48.8 1.8 %collective-permute-done.7 = bf16[96,256]{1,0:T(8,128)(2,1)S(1)} collective-permute-done((bf16[96,256]{1,0:T(8,128)(2,1)S(1)}, bf16[96,256]{1,0:T(8,128)(2,1)S(1)}, u32[]{:S(2)}, u32[]{:S(2)}) %collective-permute-start.7) | collective-permute-done | bytes 49184 | tf_op jit(solution)/shard_map/ppermute | solution.py:16
  50.6 2.1 %collective-permute-done.15 = bf16[96,256]{1,0:T(8,128)(2,1)S(1)} collective-permute-done((bf16[96,256]{1,0:T(8,128)(2,1)S(1)}, bf16[96,256]{1,0:T(8,128)(2,1)S(1)}, u32[]{:S(2)}, u32[]{:S(2)}) %collective-permute-start.15) | collective-permute-done | bytes 49184 | tf_op jit(solution)/shard_map/ppermute | solution.py:16
  52.9 1.0 collective-permute-start.16
  53.9 2.0 %collective-permute-start.20 = (bf16[96,256]{1,0:T(8,128)(2,1)S(1)}, bf16[96,256]{1,0:T(8,128)(2,1)S(1)}, u32[]{:S(2)}, u32[]{:S(2)}) collective-permute-start(bf16[96,256]{1,0:T(8,128)(2,1)S(1)} %get-tuple-element.23), channel_id=1, source_target_pairs={{0,8},{1,9},{2,10},{3,11},{4,12},{5,13},{6,14},{7,15},{8,0},{9,1},... | collective-permute-start | bytes 147464 | tf_op jit(solution)/shard_map/ppermute | solution.py:16
  55.9 2.1 %collective-permute-done.16 = bf16[96,256]{1,0:T(8,128)(2,1)S(1)} collective-permute-done((bf16[96,256]{1,0:T(8,128)(2,1)S(1)}, bf16[96,256]{1,0:T(8,128)(2,1)S(1)}, u32[]{:S(2)}, u32[]{:S(2)}) %collective-permute-start.16) | collective-permute-done | bytes 49184 | tf_op jit(solution)/shard_map/ppermute | solution.py:16
  58.0 1.4 %collective-permute-done.20 = bf16[96,256]{1,0:T(8,128)(2,1)S(1)} collective-permute-done((bf16[96,256]{1,0:T(8,128)(2,1)S(1)}, bf16[96,256]{1,0:T(8,128)(2,1)S(1)}, u32[]{:S(2)}, u32[]{:S(2)}) %collective-permute-start.20) | collective-permute-done | bytes 49184 | tf_op jit(solution)/shard_map/ppermute | solution.py:16
  59.5 0.7 collective-permute-start.21
  60.2 2.5 %collective-permute-done.17 = bf16[2,96,256]{2,1,0:T(8,128)(2,1)S(1)} collective-permute-done((bf16[2,96,256]{2,1,0:T(8,128)(2,1)S(1)}, bf16[2,96,256]{2,1,0:T(8,128)(2,1)S(1)}, u32[]{:S(2)}, u32[]{:S(2)}) %collective-permute-start.17) | collective-permute-done | bytes 98336 | tf_op jit(solution)/shard_map/ppermute | solution.py:16
  62.7 1.8 %collective-permute-start.18 = (bf16[2,2,96,256]{3,2,0,1:T(8,128)(2,1)S(1)}, bf16[2,2,96,256]{3,2,0,1:T(8,128)(2,1)S(1)}, u32[]{:S(2)}, u32[]{:S(2)}) collective-permute-start(bf16[2,2,96,256]{3,2,0,1:T(8,128)(2,1)S(1)} %pad_maximum_fusion.10), channel_id=1, source_target_pairs={{0,2},{1,3},{2,0},{3,1},{4,6},{5,7},{6,4},{7,5},{8,10},{9,11},{10,... | collective-permute-start | bytes 589832 | tf_op jit(solution)/shard_map/ppermute | solution.py:16
  64.5 0.8 collective-permute-done.21
  65.4 3.1 %collective-permute-done.18 = bf16[2,2,96,256]{3,2,0,1:T(8,128)(2,1)S(1)} collective-permute-done((bf16[2,2,96,256]{3,2,0,1:T(8,128)(2,1)S(1)}, bf16[2,2,96,256]{3,2,0,1:T(8,128)(2,1)S(1)}, u32[]{:S(2)}, u32[]{:S(2)}) %collective-permute-start.18) | collective-permute-done | bytes 196640 | tf_op jit(solution)/shard_map/ppermute | solution.py:16
  68.6 2.4 %collective-permute-done.22 = bf16[2,2,96,256]{3,2,1,0:T(8,128)(2,1)S(1)} collective-permute-done((bf16[2,2,96,256]{3,2,1,0:T(8,128)(2,1)S(1)}, bf16[2,2,96,256]{3,2,1,0:T(8,128)(2,1)S(1)}, u32[]{:S(2)}, u32[]{:S(2)}) %collective-permute-start.22) | collective-permute-done | bytes 196640 | tf_op jit(solution)/shard_map/ppermute | solution.py:16
  71.6 1.3 %collective-permute-done.23 = bf16[2,2,2,96,256]{4,3,2,1,0:T(8,128)(2,1)S(1)} collective-permute-done((bf16[2,2,2,96,256]{4,3,2,1,0:T(8,128)(2,1)S(1)}, bf16[2,2,2,96,256]{4,3,2,1,0:T(8,128)(2,1)S(1)}, u32[]{:S(2)}, u32[]{:S(2)}) %collective-permute-start.23) | collective-permute-done | bytes 393248 | tf_op jit(solution)/shard_map/ppermute | solution.py:16
  73.4 3.0 %fusion.3 = bf16[1536,256]{0,1:T(8,128)(2,1)S(1)} fusion(bf16[3,512,1536]{2,1,0:T(8,128)(2,1)} %param.5, bf16[1536,256]{1,0:T(8,128)(2,1)S(1)} %bitcast.258, f32[256]{0:T(256)S(1)} %add_rsqrt_fusion.1), kind=kOutput, calls=%fused_computation.7 | convolution fusion | flops 805961728 | bytes 4719616 | tf_op jit(solution)/shard_map/dot_general | solution.py:10
  77.0 3.0 %fusion.2 = bf16[1536,256]{0,1:T(8,128)(2,1)S(1)} fusion(bf16[3,512,1536]{2,1,0:T(8,128)(2,1)} %param.5, bf16[1536,256]{1,0:T(8,128)(2,1)S(1)} %bitcast.257, f32[256]{0:T(256)} %copy-done.2), kind=kOutput, calls=%fused_computation.6 | convolution fusion | flops 805961728 | bytes 4719616 | tf_op jit(solution)/shard_map/dot_general | solution.py:10
  80.3 0.4 collective-permute-start.24
  81.1 1.0 collective-permute-done.24
  82.2 0.7 collective-permute-start.25
  82.9 5.1 %collective-permute-done.29 = bf16[2,2,96,256]{3,2,0,1:T(8,128)(2,1)S(1)} collective-permute-done((bf16[2,2,96,256]{3,2,0,1:T(8,128)(2,1)S(1)}, bf16[2,2,96,256]{3,2,0,1:T(8,128)(2,1)S(1)}, u32[]{:S(2)}, u32[]{:S(2)}) %collective-permute-start.29) | collective-permute-done | bytes 196640 | tf_op jit(solution)/shard_map/ppermute | solution.py:16
  88.1 0.7 collective-permute-start.30
  88.8 0.7 collective-permute-done.25
  89.6 0.5 collective-permute-start.26
  90.1 2.7 %collective-permute-done.30 = bf16[2,96,256]{2,1,0:T(8,128)(2,1)S(1)} collective-permute-done((bf16[2,96,256]{2,1,0:T(8,128)(2,1)S(1)}, bf16[2,96,256]{2,1,0:T(8,128)(2,1)S(1)}, u32[]{:S(2)}, u32[]{:S(2)}) %collective-permute-start.30) | collective-permute-done | bytes 98336 | tf_op jit(solution)/shard_map/ppermute | solution.py:16
  92.8 0.7 collective-permute-start.31
  93.5 0.8 collective-permute-done.26
  94.3 1.6 %collective-permute-start.27 = (bf16[96,256]{1,0:T(8,128)(2,1)S(1)}, bf16[96,256]{1,0:T(8,128)(2,1)S(1)}, u32[]{:S(2)}, u32[]{:S(2)}) collective-permute-start(bf16[96,256]{1,0:T(8,128)(2,1)S(1)} %fusion.64), channel_id=1, source_target_pairs={{0,8},{1,9},{2,10},{3,11},{4,12},{5,13},{6,14},{7,15},{8,0},{9,1},... | collective-permute-start | bytes 147464 | tf_op jit(solution)/shard_map/ppermute | solution.py:16
  96.0 2.3 %collective-permute-done.31 = bf16[96,256]{1,0:T(8,128)(2,1)S(1)} collective-permute-done((bf16[96,256]{1,0:T(8,128)(2,1)S(1)}, bf16[96,256]{1,0:T(8,128)(2,1)S(1)}, u32[]{:S(2)}, u32[]{:S(2)}) %collective-permute-start.31) | collective-permute-done | bytes 49184 | tf_op jit(solution)/shard_map/ppermute | solution.py:16
  98.3 1.5 %collective-permute-done.27 = bf16[96,256]{1,0:T(8,128)(2,1)S(1)} collective-permute-done((bf16[96,256]{1,0:T(8,128)(2,1)S(1)}, bf16[96,256]{1,0:T(8,128)(2,1)S(1)}, u32[]{:S(2)}, u32[]{:S(2)}) %collective-permute-start.27) | collective-permute-done | bytes 49184 | tf_op jit(solution)/shard_map/ppermute | solution.py:16
  100.3 1.6 %collective-permute-start.32 = (f32[256]{0:T(256)S(1)}, f32[256]{0:T(256)S(1)}, u32[]{:S(2)}, u32[]{:S(2)}) collective-permute-start(f32[256]{0:T(256)S(1)} %add.192), channel_id=1, source_target_pairs={{0,1},{1,0},{2,3},{3,2},{4,5},{5,4},{6,7},{7,6},{8,9},{9,8},{10,11... | collective-permute-start | bytes 3080 | tf_op jit(solution)/shard_map/ppermute | solution.py:16
  101.9 1.1 %collective-permute-done.34 = f32[256]{0:T(256)S(1)} collective-permute-done((f32[256]{0:T(256)S(1)}, f32[256]{0:T(256)S(1)}, u32[]{:S(2)}, u32[]{:S(2)}) %collective-permute-start.34) | collective-permute-done | bytes 1056 | tf_op jit(solution)/shard_map/ppermute | solution.py:16
  103.1 0.7 collective-permute-done.33
  103.7 1.3 %collective-permute-start.37 = (f32[256]{0:T(256)S(1)}, f32[256]{0:T(256)S(1)}, u32[]{:S(2)}, u32[]{:S(2)}) collective-permute-start(f32[256]{0:T(256)S(1)} %add_add_fusion), channel_id=1, source_target_pairs={{0,12},{1,13},{2,14},{3,15},{4,8},{5,9},{6,10},{7,11},{8,4},{9,5},... | collective-permute-start | bytes 3080 | tf_op jit(solution)/shard_map/ppermute | solution.py:16
  105.0 0.8 collective-permute-start.36
  105.8 2.4 %collective-permute-start.35 = (f32[256]{0:T(256)S(1)}, f32[256]{0:T(256)S(1)}, u32[]{:S(2)}, u32[]{:S(2)}) collective-permute-start(f32[256]{0:T(256)S(1)} %add_add_fusion), channel_id=1, source_target_pairs={{0,4},{1,5},{2,6},{3,7},{4,0},{5,1},{6,2},{7,3},{8,12},{9,13},{10,... | collective-permute-start | bytes 3080 | tf_op jit(solution)/shard_map/ppermute | solution.py:16
  108.2 1.0 collective-permute-done.37
  109.2 0.3 collective-permute-done.36
  109.7 0.7 broadcast_multiply_fusion
  (106 shorter events, 5.8 us)
Async XLA Ops:
  0.6 6.9 %collective-permute-start = (bf16[96,256]{1,0:T(8,128)(2,1)}, bf16[96,256]{1,0:T(8,128)(2,1)S(1)}, u32[]{:S(2)}, u32[]{:S(2)}) collective-permute-start(bf16[96,256]{1,0:T(8,128)(2,1)} %param.6), channel_id=1, source_target_pairs={{0,8},{1,9},{2,10},{3,11},{4,12},{5,13},{6,14},{7,15},{8,0},{9,1},... | collective-permute-start | bytes 147464 | tf_op jit(solution)/shard_map/ppermute | solution.py:16
  4.7 5.9 %collective-permute-start.8 = (bf16[96,256]{1,0:T(8,128)(2,1)}, bf16[96,256]{1,0:T(8,128)(2,1)S(1)}, u32[]{:S(2)}, u32[]{:S(2)}) collective-permute-start(bf16[96,256]{1,0:T(8,128)(2,1)} %param.7), channel_id=1, source_target_pairs={{0,8},{1,9},{2,10},{3,11},{4,12},{5,13},{6,14},{7,15},{8,0},{9,1},... | collective-permute-start | bytes 147464 | tf_op jit(solution)/shard_map/ppermute | solution.py:16
  8.4 5.1 %collective-permute-start.1 = (bf16[2,96,256]{2,1,0:T(8,128)(2,1)S(1)}, bf16[2,96,256]{2,1,0:T(8,128)(2,1)S(1)}, u32[]{:S(2)}, u32[]{:S(2)}) collective-permute-start(bf16[2,96,256]{2,1,0:T(8,128)(2,1)S(1)} %pad_maximum_fusion.12), channel_id=1, source_target_pairs={{0,4},{1,5},{2,6},{3,7},{4,0},{5,1},{6,2},{7,3},{8,12},{9,13},{10,... | collective-permute-start | bytes 294920 | tf_op jit(solution)/shard_map/ppermute | solution.py:16
  11.4 5.3 %collective-permute-start.9 = (bf16[2,96,256]{2,1,0:T(8,128)(2,1)S(1)}, bf16[2,96,256]{2,1,0:T(8,128)(2,1)S(1)}, u32[]{:S(2)}, u32[]{:S(2)}) collective-permute-start(bf16[2,96,256]{2,1,0:T(8,128)(2,1)S(1)} %pad_maximum_fusion.13), channel_id=1, source_target_pairs={{0,2},{1,3},{2,0},{3,1},{4,6},{5,7},{6,4},{7,5},{8,10},{9,11},{10,... | collective-permute-start | bytes 294920 | tf_op jit(solution)/shard_map/ppermute | solution.py:16
  13.5 6.8 %collective-permute-start.2 = (bf16[2,2,96,256]{3,2,0,1:T(8,128)(2,1)S(1)}, bf16[2,2,96,256]{3,2,0,1:T(8,128)(2,1)S(1)}, u32[]{:S(2)}, u32[]{:S(2)}) collective-permute-start(bf16[2,2,96,256]{3,2,0,1:T(8,128)(2,1)S(1)} %pad_maximum_fusion.8), channel_id=1, source_target_pairs={{0,2},{1,3},{2,0},{3,1},{4,6},{5,7},{6,4},{7,5},{8,10},{9,11},{10,... | collective-permute-start | bytes 589832 | tf_op jit(solution)/shard_map/ppermute | solution.py:16
  16.8 5.7 %collective-permute-start.10 = (bf16[2,2,96,256]{3,2,1,0:T(8,128)(2,1)S(1)}, bf16[2,2,96,256]{3,2,1,0:T(8,128)(2,1)S(1)}, u32[]{:S(2)}, u32[]{:S(2)}) collective-permute-start(bf16[2,2,96,256]{3,2,1,0:T(8,128)(2,1)S(1)} %pad_maximum_fusion.9), channel_id=1, source_target_pairs={{0,4},{1,5},{2,6},{3,7},{4,0},{5,1},{6,2},{7,3},{8,12},{9,13},{10,... | collective-permute-start | bytes 589832 | tf_op jit(solution)/shard_map/ppermute | solution.py:16
  20.5 2.2 %collective-permute-start.3 = (bf16[2,2,2,96,256]{4,3,2,1,0:T(8,128)(2,1)S(1)}, bf16[2,2,2,96,256]{4,3,2,1,0:T(8,128)(2,1)S(1)}, u32[]{:S(2)}, u32[]{:S(2)}) collective-permute-start(bf16[2,2,2,96,256]{4,3,2,1,0:T(8,128)(2,1)S(1)} %copy.43), channel_id=1, source_target_pairs={{0,1},{1,0},{2,3},{3,2},{4,5},{5,4},{6,7},{7,6},{8,9},{9,8},{10,11... | collective-permute-start | bytes 1179656 | tf_op jit(solution)/shard_map/ppermute | solution.py:16
  22.6 3.6 %collective-permute-start.11 = (bf16[2,2,2,96,256]{4,3,2,0,1:T(8,128)(2,1)S(1)}, bf16[2,2,2,96,256]{4,3,2,0,1:T(8,128)(2,1)S(1)}, u32[]{:S(2)}, u32[]{:S(2)}) collective-permute-start(bf16[2,2,2,96,256]{4,3,2,0,1:T(8,128)(2,1)S(1)} %pad_maximum_fusion.5), channel_id=1, source_target_pairs={{0,1},{1,0},{2,3},{3,2},{4,5},{5,4},{6,7},{7,6},{8,9},{9,8},{10,11... | collective-permute-start | bytes 1179656 | tf_op jit(solution)/shard_map/ppermute | solution.py:16
  29.7 0.7 copy-start
  29.7 0.7 copy-start.1
  29.9 1.9 %collective-permute-start.4 = (bf16[2,2,2,96,256]{4,3,0,1,2:T(8,128)(2,1)S(1)}, bf16[2,2,2,96,256]{4,3,0,1,2:T(8,128)(2,1)S(1)}, u32[]{:S(2)}, u32[]{:S(2)}) collective-permute-start(bf16[2,2,2,96,256]{4,3,0,1,2:T(8,128)(2,1)S(1)} %bitcast.262), channel_id=1, source_target_pairs={{0,1},{1,0},{2,3},{3,2},{4,5},{5,4},{6,7},{7,6},{8,9},{9,8},{10,11... | collective-permute-start | bytes 1179656 | tf_op jit(solution)/shard_map/ppermute | solution.py:16
  30.5 3.1 %collective-permute-start.12 = (bf16[2,2,2,96,256]{4,3,0,2,1:T(8,128)(2,1)S(1)}, bf16[2,2,2,96,256]{4,3,0,2,1:T(8,128)(2,1)S(1)}, u32[]{:S(2)}, u32[]{:S(2)}) collective-permute-start(bf16[2,2,2,96,256]{4,3,0,2,1:T(8,128)(2,1)S(1)} %bitcast.261), channel_id=1, source_target_pairs={{0,1},{1,0},{2,3},{3,2},{4,5},{5,4},{6,7},{7,6},{8,9},{9,8},{10,11... | collective-permute-start | bytes 1179656 | tf_op jit(solution)/shard_map/ppermute | solution.py:16
  31.9 7.2 %collective-permute-start.5 = (bf16[2,2,96,256]{3,2,0,1:T(8,128)(2,1)S(1)}, bf16[2,2,96,256]{3,2,0,1:T(8,128)(2,1)S(1)}, u32[]{:S(2)}, u32[]{:S(2)}) collective-permute-start(bf16[2,2,96,256]{3,2,0,1:T(8,128)(2,1)S(1)} %fusion.54), channel_id=1, source_target_pairs={{0,2},{1,3},{2,0},{3,1},{4,6},{5,7},{6,4},{7,5},{8,10},{9,11},{10,... | collective-permute-start | bytes 589832 | tf_op jit(solution)/shard_map/ppermute | solution.py:16
  33.7 7.0 %collective-permute-start.13 = (bf16[2,2,96,256]{3,2,0,1:T(8,128)(2,1)S(1)}, bf16[2,2,96,256]{3,2,0,1:T(8,128)(2,1)S(1)}, u32[]{:S(2)}, u32[]{:S(2)}) collective-permute-start(bf16[2,2,96,256]{3,2,0,1:T(8,128)(2,1)S(1)} %fusion.55), channel_id=1, source_target_pairs={{0,4},{1,5},{2,6},{3,7},{4,0},{5,1},{6,2},{7,3},{8,12},{9,13},{10,... | collective-permute-start | bytes 589832 | tf_op jit(solution)/shard_map/ppermute | solution.py:16
  39.2 4.7 %collective-permute-start.6 = (bf16[2,96,256]{2,1,0:T(8,128)(2,1)S(1)}, bf16[2,96,256]{2,1,0:T(8,128)(2,1)S(1)}, u32[]{:S(2)}, u32[]{:S(2)}) collective-permute-start(bf16[2,96,256]{2,1,0:T(8,128)(2,1)S(1)} %fusion.58), channel_id=1, source_target_pairs={{0,4},{1,5},{2,6},{3,7},{4,0},{5,1},{6,2},{7,3},{8,12},{9,13},{10,... | collective-permute-start | bytes 294920 | tf_op jit(solution)/shard_map/ppermute | solution.py:16
  40.7 7.0 %collective-permute-start.14 = (bf16[2,96,256]{2,1,0:T(8,128)(2,1)S(1)}, bf16[2,96,256]{2,1,0:T(8,128)(2,1)S(1)}, u32[]{:S(2)}, u32[]{:S(2)}) collective-permute-start(bf16[2,96,256]{2,1,0:T(8,128)(2,1)S(1)} %fusion.59), channel_id=1, source_target_pairs={{0,2},{1,3},{2,0},{3,1},{4,6},{5,7},{6,4},{7,5},{8,10},{9,11},{10,... | collective-permute-start | bytes 294920 | tf_op jit(solution)/shard_map/ppermute | solution.py:16
  43.9 6.7 %collective-permute-start.7 = (bf16[96,256]{1,0:T(8,128)(2,1)S(1)}, bf16[96,256]{1,0:T(8,128)(2,1)S(1)}, u32[]{:S(2)}, u32[]{:S(2)}) collective-permute-start(bf16[96,256]{1,0:T(8,128)(2,1)S(1)} %fusion.62), channel_id=1, source_target_pairs={{0,8},{1,9},{2,10},{3,11},{4,12},{5,13},{6,14},{7,15},{8,0},{9,1},... | collective-permute-start | bytes 147464 | tf_op jit(solution)/shard_map/ppermute | solution.py:16
  47.7 5.1 %collective-permute-start.15 = (bf16[96,256]{1,0:T(8,128)(2,1)S(1)}, bf16[96,256]{1,0:T(8,128)(2,1)S(1)}, u32[]{:S(2)}, u32[]{:S(2)}) collective-permute-start(bf16[96,256]{1,0:T(8,128)(2,1)S(1)} %fusion.63), channel_id=1, source_target_pairs={{0,8},{1,9},{2,10},{3,11},{4,12},{5,13},{6,14},{7,15},{8,0},{9,1},... | collective-permute-start | bytes 147464 | tf_op jit(solution)/shard_map/ppermute | solution.py:16
  52.9 5.1 %collective-permute-start.16 = (bf16[96,256]{1,0:T(8,128)(2,1)S(1)}, bf16[96,256]{1,0:T(8,128)(2,1)S(1)}, u32[]{:S(2)}, u32[]{:S(2)}) collective-permute-start(bf16[96,256]{1,0:T(8,128)(2,1)S(1)} %get-tuple-element.22), channel_id=1, source_target_pairs={{0,8},{1,9},{2,10},{3,11},{4,12},{5,13},{6,14},{7,15},{8,0},{9,1},... | collective-permute-start | bytes 147464 | tf_op jit(solution)/shard_map/ppermute | solution.py:16
  53.9 5.6 %collective-permute-start.20 = (bf16[96,256]{1,0:T(8,128)(2,1)S(1)}, bf16[96,256]{1,0:T(8,128)(2,1)S(1)}, u32[]{:S(2)}, u32[]{:S(2)}) collective-permute-start(bf16[96,256]{1,0:T(8,128)(2,1)S(1)} %get-tuple-element.23), channel_id=1, source_target_pairs={{0,8},{1,9},{2,10},{3,11},{4,12},{5,13},{6,14},{7,15},{8,0},{9,1},... | collective-permute-start | bytes 147464 | tf_op jit(solution)/shard_map/ppermute | solution.py:16
  58.0 4.7 %collective-permute-start.17 = (bf16[2,96,256]{2,1,0:T(8,128)(2,1)S(1)}, bf16[2,96,256]{2,1,0:T(8,128)(2,1)S(1)}, u32[]{:S(2)}, u32[]{:S(2)}) collective-permute-start(bf16[2,96,256]{2,1,0:T(8,128)(2,1)S(1)} %pad_maximum_fusion.14), channel_id=1, source_target_pairs={{0,4},{1,5},{2,6},{3,7},{4,0},{5,1},{6,2},{7,3},{8,12},{9,13},{10,... | collective-permute-start | bytes 294920 | tf_op jit(solution)/shard_map/ppermute | solution.py:16
  59.5 5.7 %collective-permute-start.21 = (bf16[2,96,256]{2,1,0:T(8,128)(2,1)S(1)}, bf16[2,96,256]{2,1,0:T(8,128)(2,1)S(1)}, u32[]{:S(2)}, u32[]{:S(2)}) collective-permute-start(bf16[2,96,256]{2,1,0:T(8,128)(2,1)S(1)} %pad_maximum_fusion.15), channel_id=1, source_target_pairs={{0,2},{1,3},{2,0},{3,1},{4,6},{5,7},{6,4},{7,5},{8,10},{9,11},{10,... | collective-permute-start | bytes 294920 | tf_op jit(solution)/shard_map/ppermute | solution.py:16
  62.7 5.7 %collective-permute-start.18 = (bf16[2,2,96,256]{3,2,0,1:T(8,128)(2,1)S(1)}, bf16[2,2,96,256]{3,2,0,1:T(8,128)(2,1)S(1)}, u32[]{:S(2)}, u32[]{:S(2)}) collective-permute-start(bf16[2,2,96,256]{3,2,0,1:T(8,128)(2,1)S(1)} %pad_maximum_fusion.10), channel_id=1, source_target_pairs={{0,2},{1,3},{2,0},{3,1},{4,6},{5,7},{6,4},{7,5},{8,10},{9,11},{10,... | collective-permute-start | bytes 589832 | tf_op jit(solution)/shard_map/ppermute | solution.py:16
  65.3 5.7 %collective-permute-start.22 = (bf16[2,2,96,256]{3,2,1,0:T(8,128)(2,1)S(1)}, bf16[2,2,96,256]{3,2,1,0:T(8,128)(2,1)S(1)}, u32[]{:S(2)}, u32[]{:S(2)}) collective-permute-start(bf16[2,2,96,256]{3,2,1,0:T(8,128)(2,1)S(1)} %pad_maximum_fusion.11), channel_id=1, source_target_pairs={{0,4},{1,5},{2,6},{3,7},{4,0},{5,1},{6,2},{7,3},{8,12},{9,13},{10,... | collective-permute-start | bytes 589832 | tf_op jit(solution)/shard_map/ppermute | solution.py:16
  68.5 2.7 %collective-permute-start.19 = (bf16[2,2,2,96,256]{4,3,0,1,2:T(8,128)(2,1)S(1)}, bf16[2,2,2,96,256]{4,3,0,1,2:T(8,128)(2,1)S(1)}, u32[]{:S(2)}, u32[]{:S(2)}) collective-permute-start(bf16[2,2,2,96,256]{4,3,0,1,2:T(8,128)(2,1)S(1)} %pad_maximum_fusion.6), channel_id=1, source_target_pairs={{0,1},{1,0},{2,3},{3,2},{4,5},{5,4},{6,7},{7,6},{8,9},{9,8},{10,11... | collective-permute-start | bytes 1179656 | tf_op jit(solution)/shard_map/ppermute | solution.py:16
  71.1 1.8 %collective-permute-start.23 = (bf16[2,2,2,96,256]{4,3,2,1,0:T(8,128)(2,1)S(1)}, bf16[2,2,2,96,256]{4,3,2,1,0:T(8,128)(2,1)S(1)}, u32[]{:S(2)}, u32[]{:S(2)}) collective-permute-start(bf16[2,2,2,96,256]{4,3,2,1,0:T(8,128)(2,1)S(1)} %pad_maximum_fusion.7), channel_id=1, source_target_pairs={{0,1},{1,0},{2,3},{3,2},{4,5},{5,4},{6,7},{7,6},{8,9},{9,8},{10,11... | collective-permute-start | bytes 1179656 | tf_op jit(solution)/shard_map/ppermute | solution.py:16
  73.4 3.3 %copy-start.2 = (f32[256]{0:T(256)}, f32[256]{0:T(256)S(1)}, u32[]{:S(2)}) copy-start(f32[256]{0:T(256)S(1)} %add_rsqrt_fusion.1) | copy-start | bytes 3076
  76.8 4.1 %collective-permute-start.28 = (bf16[2,2,2,96,256]{4,3,0,2,1:T(8,128)(2,1)S(1)}, bf16[2,2,2,96,256]{4,3,0,2,1:T(8,128)(2,1)S(1)}, u32[]{:S(2)}, u32[]{:S(2)}) collective-permute-start(bf16[2,2,2,96,256]{4,3,0,2,1:T(8,128)(2,1)S(1)} %bitcast.263), channel_id=1, source_target_pairs={{0,1},{1,0},{2,3},{3,2},{4,5},{5,4},{6,7},{7,6},{8,9},{9,8},{10,11... | collective-permute-start | bytes 1179656 | tf_op jit(solution)/shard_map/ppermute | solution.py:16
  80.3 1.8 %collective-permute-start.24 = (bf16[2,2,2,96,256]{4,3,2,1,0:T(8,128)(2,1)S(1)}, bf16[2,2,2,96,256]{4,3,2,1,0:T(8,128)(2,1)S(1)}, u32[]{:S(2)}, u32[]{:S(2)}) collective-permute-start(bf16[2,2,2,96,256]{4,3,2,1,0:T(8,128)(2,1)S(1)} %dynamic-slice_bitcast_fusion), channel_id=1, source_target_pairs={{0,1},{1,0},{2,3},{3,2},{4,5},{5,4},{6,7},{7,6},{8,9},{9,8},{10,11... | collective-permute-start | bytes 1179656 | tf_op jit(solution)/shard_map/ppermute | solution.py:16
  81.0 7.0 %collective-permute-start.29 = (bf16[2,2,96,256]{3,2,0,1:T(8,128)(2,1)S(1)}, bf16[2,2,96,256]{3,2,0,1:T(8,128)(2,1)S(1)}, u32[]{:S(2)}, u32[]{:S(2)}) collective-permute-start(bf16[2,2,96,256]{3,2,0,1:T(8,128)(2,1)S(1)} %fusion.57), channel_id=1, source_target_pairs={{0,4},{1,5},{2,6},{3,7},{4,0},{5,1},{6,2},{7,3},{8,12},{9,13},{10,... | collective-permute-start | bytes 589832 | tf_op jit(solution)/shard_map/ppermute | solution.py:16
  82.2 7.2 %collective-permute-start.25 = (bf16[2,2,96,256]{3,2,1,0:T(8,128)(2,1)S(1)}, bf16[2,2,96,256]{3,2,1,0:T(8,128)(2,1)S(1)}, u32[]{:S(2)}, u32[]{:S(2)}) collective-permute-start(bf16[2,2,96,256]{3,2,1,0:T(8,128)(2,1)S(1)} %fusion.56), channel_id=1, source_target_pairs={{0,2},{1,3},{2,0},{3,1},{4,6},{5,7},{6,4},{7,5},{8,10},{9,11},{10,... | collective-permute-start | bytes 589832 | tf_op jit(solution)/shard_map/ppermute | solution.py:16
  88.1 4.7 %collective-permute-start.30 = (bf16[2,96,256]{2,1,0:T(8,128)(2,1)S(1)}, bf16[2,96,256]{2,1,0:T(8,128)(2,1)S(1)}, u32[]{:S(2)}, u32[]{:S(2)}) collective-permute-start(bf16[2,96,256]{2,1,0:T(8,128)(2,1)S(1)} %fusion.61), channel_id=1, source_target_pairs={{0,2},{1,3},{2,0},{3,1},{4,6},{5,7},{6,4},{7,5},{8,10},{9,11},{10,... | collective-permute-start | bytes 294920 | tf_op jit(solution)/shard_map/ppermute | solution.py:16
  89.6 4.7 %collective-permute-start.26 = (bf16[2,96,256]{2,1,0:T(8,128)(2,1)S(1)}, bf16[2,96,256]{2,1,0:T(8,128)(2,1)S(1)}, u32[]{:S(2)}, u32[]{:S(2)}) collective-permute-start(bf16[2,96,256]{2,1,0:T(8,128)(2,1)S(1)} %fusion.60), channel_id=1, source_target_pairs={{0,4},{1,5},{2,6},{3,7},{4,0},{5,1},{6,2},{7,3},{8,12},{9,13},{10,... | collective-permute-start | bytes 294920 | tf_op jit(solution)/shard_map/ppermute | solution.py:16
  92.8 5.5 %collective-permute-start.31 = (bf16[96,256]{1,0:T(8,128)(2,1)S(1)}, bf16[96,256]{1,0:T(8,128)(2,1)S(1)}, u32[]{:S(2)}, u32[]{:S(2)}) collective-permute-start(bf16[96,256]{1,0:T(8,128)(2,1)S(1)} %fusion.65), channel_id=1, source_target_pairs={{0,8},{1,9},{2,10},{3,11},{4,12},{5,13},{6,14},{7,15},{8,0},{9,1},... | collective-permute-start | bytes 147464 | tf_op jit(solution)/shard_map/ppermute | solution.py:16
  94.3 5.6 %collective-permute-start.27 = (bf16[96,256]{1,0:T(8,128)(2,1)S(1)}, bf16[96,256]{1,0:T(8,128)(2,1)S(1)}, u32[]{:S(2)}, u32[]{:S(2)}) collective-permute-start(bf16[96,256]{1,0:T(8,128)(2,1)S(1)} %fusion.64), channel_id=1, source_target_pairs={{0,8},{1,9},{2,10},{3,11},{4,12},{5,13},{6,14},{7,15},{8,0},{9,1},... | collective-permute-start | bytes 147464 | tf_op jit(solution)/shard_map/ppermute | solution.py:16
  100.0 3.1 %collective-permute-start.34 = (f32[256]{0:T(256)S(1)}, f32[256]{0:T(256)S(1)}, u32[]{:S(2)}, u32[]{:S(2)}) collective-permute-start(f32[256]{0:T(256)S(1)} %add.192), channel_id=1, source_target_pairs={{0,3},{1,2},{2,1},{3,0},{4,7},{5,6},{6,5},{7,4},{8,11},{9,10},{10,... | collective-permute-start | bytes 3080 | tf_op jit(solution)/shard_map/ppermute | solution.py:16
  100.1 3.6 %collective-permute-start.33 = (f32[256]{0:T(256)S(1)}, f32[256]{0:T(256)S(1)}, u32[]{:S(2)}, u32[]{:S(2)}) collective-permute-start(f32[256]{0:T(256)S(1)} %add.192), channel_id=1, source_target_pairs={{0,2},{1,3},{2,0},{3,1},{4,6},{5,7},{6,4},{7,5},{8,10},{9,11},{10,... | collective-permute-start | bytes 3080 | tf_op jit(solution)/shard_map/ppermute | solution.py:16
  100.3 3.4 %collective-permute-start.32 = (f32[256]{0:T(256)S(1)}, f32[256]{0:T(256)S(1)}, u32[]{:S(2)}, u32[]{:S(2)}) collective-permute-start(f32[256]{0:T(256)S(1)} %add.192), channel_id=1, source_target_pairs={{0,1},{1,0},{2,3},{3,2},{4,5},{5,4},{6,7},{7,6},{8,9},{9,8},{10,11... | collective-permute-start | bytes 3080 | tf_op jit(solution)/shard_map/ppermute | solution.py:16
  103.7 5.4 %collective-permute-start.37 = (f32[256]{0:T(256)S(1)}, f32[256]{0:T(256)S(1)}, u32[]{:S(2)}, u32[]{:S(2)}) collective-permute-start(f32[256]{0:T(256)S(1)} %add_add_fusion), channel_id=1, source_target_pairs={{0,12},{1,13},{2,14},{3,15},{4,8},{5,9},{6,10},{7,11},{8,4},{9,5},... | collective-permute-start | bytes 3080 | tf_op jit(solution)/shard_map/ppermute | solution.py:16
  105.0 4.5 %collective-permute-start.36 = (f32[256]{0:T(256)S(1)}, f32[256]{0:T(256)S(1)}, u32[]{:S(2)}, u32[]{:S(2)}) collective-permute-start(f32[256]{0:T(256)S(1)} %add_add_fusion), channel_id=1, source_target_pairs={{0,8},{1,9},{2,10},{3,11},{4,12},{5,13},{6,14},{7,15},{8,0},{9,1},... | collective-permute-start | bytes 3080 | tf_op jit(solution)/shard_map/ppermute | solution.py:16
  105.8 3.9 %collective-permute-start.35 = (f32[256]{0:T(256)S(1)}, f32[256]{0:T(256)S(1)}, u32[]{:S(2)}, u32[]{:S(2)}) collective-permute-start(f32[256]{0:T(256)S(1)} %add_add_fusion), channel_id=1, source_target_pairs={{0,4},{1,5},{2,6},{3,7},{4,0},{5,1},{6,2},{7,3},{8,12},{9,13},{10,... | collective-permute-start | bytes 3080 | tf_op jit(solution)/shard_map/ppermute | solution.py:16

commit v15 on v14

--- a/solution.py
+++ b/solution.py
@@ -30,6 +30,8 @@
         cur = keep.astype(jnp.float32) + exchange(
             send.astype(jnp.bfloat16), 1 << bit, devices
         ).astype(jnp.float32)
+        if bit != order[-1]:
+            cur = cur.astype(jnp.bfloat16)
     return cur
 
 

time: 111 us -> 111 us (level)
  transfers between devices with their start and end apart: 38 -> 38, of which waited for: 30 -> 29; matrix products, arithmetic and copies ran while one was open for 10% -> 10% of each run, Pallas kernels for 0% -> 0%
where the time goes in v15:
time: 111 us; the launch traced here: 110 us
  waiting for transfers between devices  52.8 us (48%)
  starting transfers between devices  37.2 us (34%)
  matrix products  11.9 us (11%)
  other arithmetic  5.29 us (5%)
  local copies, waits for them, and re-layouts  2.03 us (2%)
  between operations  1.29 us (1%)
    ppermute x38, waiting for transfers between devices, exchange(): return lax.ppermute(x, 'row', [(i, i ^ distance) for i in range(devices)])  52.8 us
    ppermute x38, starting transfers between devices, exchange(): return lax.ppermute(x, 'row', [(i, i ^ distance) for i in range(devices)])  37.2 us
    dot_general x4, matrix products, contract_rows(): lax.dot_general(left, right, (((0,), (0,)), ((), ())), preferred_element_...  11.9 us
    another operation x32, other arithmetic, doubling_all_gather(): jnp.stack([jnp.where(low, cur, other), jnp.where(low, other, cur)], axis=...  2.76 us
  transfers between devices with their start and end apart: 38, of which 29 were waited for; matrix products, arithmetic and copies ran while one was open for 10% of the time, Pallas kernels for 0%

profile of v15, /device:TPU:0, one launch (start us, length us, event | category | flops | bytes accessed | tf_op | source)
XLA Modules:
  0.0 110.4 jit_solution(13975706377322072092)
XLA Ops:
  0.6 4.1 %collective-permute-start = (bf16[96,256]{1,0:T(8,128)(2,1)}, bf16[96,256]{1,0:T(8,128)(2,1)S(1)}, u32[]{:S(2)}, u32[]{:S(2)}) collective-permute-start(bf16[96,256]{1,0:T(8,128)(2,1)} %param.6), channel_id=1, source_target_pairs={{0,8},{1,9},{2,10},{3,11},{4,12},{5,13},{6,14},{7,15},{8,0},{9,1},... | collective-permute-start | bytes 147464 | tf_op jit(solution)/shard_map/ppermute | solution.py:16
  4.8 2.7 %collective-permute-done = bf16[96,256]{1,0:T(8,128)(2,1)S(1)} collective-permute-done((bf16[96,256]{1,0:T(8,128)(2,1)}, bf16[96,256]{1,0:T(8,128)(2,1)S(1)}, u32[]{:S(2)}, u32[]{:S(2)}) %collective-permute-start) | collective-permute-done | bytes 49184 | tf_op jit(solution)/shard_map/ppermute | solution.py:16
  7.5 0.8 select_bitcast_fusion.31
  8.4 2.2 %collective-permute-start.1 = (bf16[2,96,256]{2,1,0:T(8,128)(2,1)S(1)}, bf16[2,96,256]{2,1,0:T(8,128)(2,1)S(1)}, u32[]{:S(2)}, u32[]{:S(2)}) collective-permute-start(bf16[2,96,256]{2,1,0:T(8,128)(2,1)S(1)} %pad_maximum_fusion.12), channel_id=1, source_target_pairs={{0,4},{1,5},{2,6},{3,7},{4,0},{5,1},{6,2},{7,3},{8,12},{9,13},{10,... | collective-permute-start | bytes 294920 | tf_op jit(solution)/shard_map/ppermute | solution.py:16
  10.6 0.8 select_bitcast_fusion.29
  11.4 1.6 %collective-permute-start.9 = (bf16[2,96,256]{2,1,0:T(8,128)(2,1)S(1)}, bf16[2,96,256]{2,1,0:T(8,128)(2,1)S(1)}, u32[]{:S(2)}, u32[]{:S(2)}) collective-permute-start(bf16[2,96,256]{2,1,0:T(8,128)(2,1)S(1)} %pad_maximum_fusion.13), channel_id=1, source_target_pairs={{0,2},{1,3},{2,0},{3,1},{4,6},{5,7},{6,4},{7,5},{8,10},{9,11},{10,... | collective-permute-start | bytes 294920 | tf_op jit(solution)/shard_map/ppermute | solution.py:16
  13.0 0.5 collective-permute-done.1
  13.5 1.6 %collective-permute-start.2 = (bf16[2,2,96,256]{3,2,0,1:T(8,128)(2,1)S(1)}, bf16[2,2,96,256]{3,2,0,1:T(8,128)(2,1)S(1)}, u32[]{:S(2)}, u32[]{:S(2)}) collective-permute-start(bf16[2,2,96,256]{3,2,0,1:T(8,128)(2,1)S(1)} %pad_maximum_fusion.8), channel_id=1, source_target_pairs={{0,2},{1,3},{2,0},{3,1},{4,6},{5,7},{6,4},{7,5},{8,10},{9,11},{10,... | collective-permute-start | bytes 589832 | tf_op jit(solution)/shard_map/ppermute | solution.py:16
  15.1 1.6 %collective-permute-done.9 = bf16[2,96,256]{2,1,0:T(8,128)(2,1)S(1)} collective-permute-done((bf16[2,96,256]{2,1,0:T(8,128)(2,1)S(1)}, bf16[2,96,256]{2,1,0:T(8,128)(2,1)S(1)}, u32[]{:S(2)}, u32[]{:S(2)}) %collective-permute-start.9) | collective-permute-done | bytes 98336 | tf_op jit(solution)/shard_map/ppermute | solution.py:16
  16.8 0.7 collective-permute-start.10
  17.5 2.8 %collective-permute-done.2 = bf16[2,2,96,256]{3,2,0,1:T(8,128)(2,1)S(1)} collective-permute-done((bf16[2,2,96,256]{3,2,0,1:T(8,128)(2,1)S(1)}, bf16[2,2,96,256]{3,2,0,1:T(8,128)(2,1)S(1)}, u32[]{:S(2)}, u32[]{:S(2)}) %collective-permute-start.2) | collective-permute-done | bytes 196640 | tf_op jit(solution)/shard_map/ppermute | solution.py:16
  20.5 2.0 %collective-permute-done.10 = bf16[2,2,96,256]{3,2,1,0:T(8,128)(2,1)S(1)} collective-permute-done((bf16[2,2,96,256]{3,2,1,0:T(8,128)(2,1)S(1)}, bf16[2,2,96,256]{3,2,1,0:T(8,128)(2,1)S(1)}, u32[]{:S(2)}, u32[]{:S(2)}) %collective-permute-start.10) | collective-permute-done | bytes 196640 | tf_op jit(solution)/shard_map/ppermute | solution.py:16
  23.0 3.0 %fusion = bf16[1536,256]{0,1:T(8,128)(2,1)S(1)} fusion(bf16[1536,256]{1,0:T(8,128)(2,1)S(1)} %bitcast.271, bf16[3,512,1536]{2,1,0:T(8,128)(2,1)} %param.5), kind=kOutput, calls=%fused_computation.4 | convolution fusion | flops 805830656 | bytes 4718592 | tf_op jit(solution)/shard_map/dot_general | solution.py:10
  26.4 3.0 %fusion.1 = bf16[1536,256]{0,1:T(8,128)(2,1)S(1)} fusion(bf16[1536,256]{1,0:T(8,128)(2,1)S(1)} %bitcast.272, bf16[3,512,1536]{2,1,0:T(8,128)(2,1)} %param.5), kind=kOutput, calls=%fused_computation.5 | convolution fusion | flops 805830656 | bytes 4718592 | tf_op jit(solution)/shard_map/dot_general | solution.py:10
  29.9 0.5 collective-permute-start.4
  30.5 0.5 collective-permute-start.12
  31.1 0.6 collective-permute-done.4
  31.9 1.7 %collective-permute-start.5 = (bf16[2,2,96,256]{3,2,0,1:T(8,128)(2,1)S(1)}, bf16[2,2,96,256]{3,2,0,1:T(8,128)(2,1)S(1)}, u32[]{:S(2)}, u32[]{:S(2)}) collective-permute-start(bf16[2,2,96,256]{3,2,0,1:T(8,128)(2,1)S(1)} %dynamic-slice_bitcast_fusion.4), channel_id=1, source_target_pairs={{0,2},{1,3},{2,0},{3,1},{4,6},{5,7},{6,4},{7,5},{8,10},{9,11},{10,... | collective-permute-start | bytes 589832 | tf_op jit(solution)/shard_map/ppermute | solution.py:16
  33.7 0.6 collective-permute-start.13
  34.3 4.8 %collective-permute-done.5 = bf16[2,2,96,256]{3,2,0,1:T(8,128)(2,1)S(1)} collective-permute-done((bf16[2,2,96,256]{3,2,0,1:T(8,128)(2,1)S(1)}, bf16[2,2,96,256]{3,2,0,1:T(8,128)(2,1)S(1)}, u32[]{:S(2)}, u32[]{:S(2)}) %collective-permute-start.5) | collective-permute-done | bytes 196640 | tf_op jit(solution)/shard_map/ppermute | solution.py:16
  39.2 0.7 collective-permute-start.6
  39.9 0.7 collective-permute-done.13
  40.7 0.9 collective-permute-start.14
  41.6 2.3 %collective-permute-done.6 = bf16[2,96,256]{2,1,0:T(8,128)(2,1)S(1)} collective-permute-done((bf16[2,96,256]{2,1,0:T(8,128)(2,1)S(1)}, bf16[2,96,256]{2,1,0:T(8,128)(2,1)S(1)}, u32[]{:S(2)}, u32[]{:S(2)}) %collective-permute-start.6) | collective-permute-done | bytes 98336 | tf_op jit(solution)/shard_map/ppermute | solution.py:16
  44.0 3.7 %collective-permute-start.7 = (bf16[96,256]{1,0:T(8,128)(2,1)S(1)}, bf16[96,256]{1,0:T(8,128)(2,1)S(1)}, u32[]{:S(2)}, u32[]{:S(2)}) collective-permute-start(bf16[96,256]{1,0:T(8,128)(2,1)S(1)} %dynamic-slice_bitcast_fusion.12), channel_id=1, source_target_pairs={{0,8},{1,9},{2,10},{3,11},{4,12},{5,13},{6,14},{7,15},{8,0},{9,1},... | collective-permute-start | bytes 147464 | tf_op jit(solution)/shard_map/ppermute | solution.py:16
  47.7 1.0 collective-permute-start.15
  48.9 1.8 %collective-permute-done.7 = bf16[96,256]{1,0:T(8,128)(2,1)S(1)} collective-permute-done((bf16[96,256]{1,0:T(8,128)(2,1)S(1)}, bf16[96,256]{1,0:T(8,128)(2,1)S(1)}, u32[]{:S(2)}, u32[]{:S(2)}) %collective-permute-start.7) | collective-permute-done | bytes 49184 | tf_op jit(solution)/shard_map/ppermute | solution.py:16
  50.7 2.1 %collective-permute-done.15 = bf16[96,256]{1,0:T(8,128)(2,1)S(1)} collective-permute-done((bf16[96,256]{1,0:T(8,128)(2,1)S(1)}, bf16[96,256]{1,0:T(8,128)(2,1)S(1)}, u32[]{:S(2)}, u32[]{:S(2)}) %collective-permute-start.15) | collective-permute-done | bytes 49184 | tf_op jit(solution)/shard_map/ppermute | solution.py:16
  52.9 1.0 collective-permute-start.16
  53.9 2.0 %collective-permute-start.20 = (bf16[96,256]{1,0:T(8,128)(2,1)S(1)}, bf16[96,256]{1,0:T(8,128)(2,1)S(1)}, u32[]{:S(2)}, u32[]{:S(2)}) collective-permute-start(bf16[96,256]{1,0:T(8,128)(2,1)S(1)} %get-tuple-element.29), channel_id=1, source_target_pairs={{0,8},{1,9},{2,10},{3,11},{4,12},{5,13},{6,14},{7,15},{8,0},{9,1},... | collective-permute-start | bytes 147464 | tf_op jit(solution)/shard_map/ppermute | solution.py:16
  55.9 2.1 %collective-permute-done.16 = bf16[96,256]{1,0:T(8,128)(2,1)S(1)} collective-permute-done((bf16[96,256]{1,0:T(8,128)(2,1)S(1)}, bf16[96,256]{1,0:T(8,128)(2,1)S(1)}, u32[]{:S(2)}, u32[]{:S(2)}) %collective-permute-start.16) | collective-permute-done | bytes 49184 | tf_op jit(solution)/shard_map/ppermute | solution.py:16
  58.1 1.5 %collective-permute-done.20 = bf16[96,256]{1,0:T(8,128)(2,1)S(1)} collective-permute-done((bf16[96,256]{1,0:T(8,128)(2,1)S(1)}, bf16[96,256]{1,0:T(8,128)(2,1)S(1)}, u32[]{:S(2)}, u32[]{:S(2)}) %collective-permute-start.20) | collective-permute-done | bytes 49184 | tf_op jit(solution)/shard_map/ppermute | solution.py:16
  59.6 0.6 collective-permute-start.21
  60.2 2.5 %collective-permute-done.17 = bf16[2,96,256]{2,1,0:T(8,128)(2,1)S(1)} collective-permute-done((bf16[2,96,256]{2,1,0:T(8,128)(2,1)S(1)}, bf16[2,96,256]{2,1,0:T(8,128)(2,1)S(1)}, u32[]{:S(2)}, u32[]{:S(2)}) %collective-permute-start.17) | collective-permute-done | bytes 98336 | tf_op jit(solution)/shard_map/ppermute | solution.py:16
  62.7 1.8 %collective-permute-start.18 = (bf16[2,2,96,256]{3,2,0,1:T(8,128)(2,1)S(1)}, bf16[2,2,96,256]{3,2,0,1:T(8,128)(2,1)S(1)}, u32[]{:S(2)}, u32[]{:S(2)}) collective-permute-start(bf16[2,2,96,256]{3,2,0,1:T(8,128)(2,1)S(1)} %pad_maximum_fusion.10), channel_id=1, source_target_pairs={{0,2},{1,3},{2,0},{3,1},{4,6},{5,7},{6,4},{7,5},{8,10},{9,11},{10,... | collective-permute-start | bytes 589832 | tf_op jit(solution)/shard_map/ppermute | solution.py:16
  64.5 0.8 collective-permute-done.21
  65.4 3.0 %collective-permute-done.18 = bf16[2,2,96,256]{3,2,0,1:T(8,128)(2,1)S(1)} collective-permute-done((bf16[2,2,96,256]{3,2,0,1:T(8,128)(2,1)S(1)}, bf16[2,2,96,256]{3,2,0,1:T(8,128)(2,1)S(1)}, u32[]{:S(2)}, u32[]{:S(2)}) %collective-permute-start.18) | collective-permute-done | bytes 196640 | tf_op jit(solution)/shard_map/ppermute | solution.py:16
  68.6 2.4 %collective-permute-done.22 = bf16[2,2,96,256]{3,2,1,0:T(8,128)(2,1)S(1)} collective-permute-done((bf16[2,2,96,256]{3,2,1,0:T(8,128)(2,1)S(1)}, bf16[2,2,96,256]{3,2,1,0:T(8,128)(2,1)S(1)}, u32[]{:S(2)}, u32[]{:S(2)}) %collective-permute-start.22) | collective-permute-done | bytes 196640 | tf_op jit(solution)/shard_map/ppermute | solution.py:16
  71.6 1.3 %collective-permute-done.23 = bf16[2,2,2,96,256]{4,3,2,1,0:T(8,128)(2,1)S(1)} collective-permute-done((bf16[2,2,2,96,256]{4,3,2,1,0:T(8,128)(2,1)S(1)}, bf16[2,2,2,96,256]{4,3,2,1,0:T(8,128)(2,1)S(1)}, u32[]{:S(2)}, u32[]{:S(2)}) %collective-permute-start.23) | collective-permute-done | bytes 393248 | tf_op jit(solution)/shard_map/ppermute | solution.py:16
  73.5 3.0 %fusion.3 = bf16[1536,256]{0,1:T(8,128)(2,1)S(1)} fusion(bf16[3,512,1536]{2,1,0:T(8,128)(2,1)} %param.5, bf16[1536,256]{1,0:T(8,128)(2,1)S(1)} %bitcast.270, f32[256]{0:T(256)S(1)} %add_rsqrt_fusion.1), kind=kOutput, calls=%fused_computation.7 | convolution fusion | flops 805961728 | bytes 4719616 | tf_op jit(solution)/shard_map/dot_general | solution.py:10
  77.0 3.0 %fusion.2 = bf16[1536,256]{0,1:T(8,128)(2,1)S(1)} fusion(bf16[3,512,1536]{2,1,0:T(8,128)(2,1)} %param.5, bf16[1536,256]{1,0:T(8,128)(2,1)S(1)} %bitcast.269, f32[256]{0:T(256)} %copy-done.2), kind=kOutput, calls=%fused_computation.6 | convolution fusion | flops 805961728 | bytes 4719616 | tf_op jit(solution)/shard_map/dot_general | solution.py:10
  80.4 0.4 collective-permute-start.24
  81.1 1.0 collective-permute-done.24
  82.3 0.7 collective-permute-start.25
  83.0 5.1 %collective-permute-done.29 = bf16[2,2,96,256]{3,2,0,1:T(8,128)(2,1)S(1)} collective-permute-done((bf16[2,2,96,256]{3,2,0,1:T(8,128)(2,1)S(1)}, bf16[2,2,96,256]{3,2,0,1:T(8,128)(2,1)S(1)}, u32[]{:S(2)}, u32[]{:S(2)}) %collective-permute-start.29) | collective-permute-done | bytes 196640 | tf_op jit(solution)/shard_map/ppermute | solution.py:16
  88.2 0.6 collective-permute-start.30
  88.8 0.7 collective-permute-done.25
  89.6 0.6 collective-permute-start.26
  90.2 2.7 %collective-permute-done.30 = bf16[2,96,256]{2,1,0:T(8,128)(2,1)S(1)} collective-permute-done((bf16[2,96,256]{2,1,0:T(8,128)(2,1)S(1)}, bf16[2,96,256]{2,1,0:T(8,128)(2,1)S(1)}, u32[]{:S(2)}, u32[]{:S(2)}) %collective-permute-start.30) | collective-permute-done | bytes 98336 | tf_op jit(solution)/shard_map/ppermute | solution.py:16
  92.9 0.7 collective-permute-start.31
  93.6 0.7 collective-permute-done.26
  94.4 1.7 %collective-permute-start.27 = (bf16[96,256]{1,0:T(8,128)(2,1)S(1)}, bf16[96,256]{1,0:T(8,128)(2,1)S(1)}, u32[]{:S(2)}, u32[]{:S(2)}) collective-permute-start(bf16[96,256]{1,0:T(8,128)(2,1)S(1)} %dynamic-slice_bitcast_fusion.10), channel_id=1, source_target_pairs={{0,8},{1,9},{2,10},{3,11},{4,12},{5,13},{6,14},{7,15},{8,0},{9,1},... | collective-permute-start | bytes 147464 | tf_op jit(solution)/shard_map/ppermute | solution.py:16
  96.1 2.3 %collective-permute-done.31 = bf16[96,256]{1,0:T(8,128)(2,1)S(1)} collective-permute-done((bf16[96,256]{1,0:T(8,128)(2,1)S(1)}, bf16[96,256]{1,0:T(8,128)(2,1)S(1)}, u32[]{:S(2)}, u32[]{:S(2)}) %collective-permute-start.31) | collective-permute-done | bytes 49184 | tf_op jit(solution)/shard_map/ppermute | solution.py:16
  98.4 1.0 collective-permute-done.27
  99.6 1.3 %collective-permute-start.33 = (f32[256]{0:T(256)S(1)}, f32[256]{0:T(256)S(1)}, u32[]{:S(2)}, u32[]{:S(2)}) collective-permute-start(f32[256]{0:T(256)S(1)} %add.192), channel_id=1, source_target_pairs={{0,2},{1,3},{2,0},{3,1},{4,6},{5,7},{6,4},{7,5},{8,10},{9,11},{10,... | collective-permute-start | bytes 3080 | tf_op jit(solution)/shard_map/ppermute | solution.py:16
  101.0 0.5 collective-permute-start.32
  101.5 1.1 %collective-permute-done.34 = f32[256]{0:T(256)S(1)} collective-permute-done((f32[256]{0:T(256)S(1)}, f32[256]{0:T(256)S(1)}, u32[]{:S(2)}, u32[]{:S(2)}) %collective-permute-start.34) | collective-permute-done | bytes 1056 | tf_op jit(solution)/shard_map/ppermute | solution.py:16
  102.6 0.7 collective-permute-done.33
  103.3 1.9 %collective-permute-start.37 = (f32[256]{0:T(256)S(1)}, f32[256]{0:T(256)S(1)}, u32[]{:S(2)}, u32[]{:S(2)}) collective-permute-start(f32[256]{0:T(256)S(1)} %add_add_fusion), channel_id=1, source_target_pairs={{0,12},{1,13},{2,14},{3,15},{4,8},{5,9},{6,10},{7,11},{8,4},{9,5},... | collective-permute-start | bytes 3080 | tf_op jit(solution)/shard_map/ppermute | solution.py:16
  105.2 0.7 collective-permute-start.36
  105.9 1.8 %collective-permute-start.35 = (f32[256]{0:T(256)S(1)}, f32[256]{0:T(256)S(1)}, u32[]{:S(2)}, u32[]{:S(2)}) collective-permute-start(f32[256]{0:T(256)S(1)} %add_add_fusion), channel_id=1, source_target_pairs={{0,4},{1,5},{2,6},{3,7},{4,0},{5,1},{6,2},{7,3},{8,12},{9,13},{10,... | collective-permute-start | bytes 3080 | tf_op jit(solution)/shard_map/ppermute | solution.py:16
  107.7 1.0 collective-permute-done.37
  108.7 0.9 collective-permute-done.36
  109.7 0.8 broadcast_multiply_fusion
  (106 shorter events, 5.8 us)
Async XLA Ops:
  0.6 6.9 %collective-permute-start = (bf16[96,256]{1,0:T(8,128)(2,1)}, bf16[96,256]{1,0:T(8,128)(2,1)S(1)}, u32[]{:S(2)}, u32[]{:S(2)}) collective-permute-start(bf16[96,256]{1,0:T(8,128)(2,1)} %param.6), channel_id=1, source_target_pairs={{0,8},{1,9},{2,10},{3,11},{4,12},{5,13},{6,14},{7,15},{8,0},{9,1},... | collective-permute-start | bytes 147464 | tf_op jit(solution)/shard_map/ppermute | solution.py:16
  4.7 5.9 %collective-permute-start.8 = (bf16[96,256]{1,0:T(8,128)(2,1)}, bf16[96,256]{1,0:T(8,128)(2,1)S(1)}, u32[]{:S(2)}, u32[]{:S(2)}) collective-permute-start(bf16[96,256]{1,0:T(8,128)(2,1)} %param.7), channel_id=1, source_target_pairs={{0,8},{1,9},{2,10},{3,11},{4,12},{5,13},{6,14},{7,15},{8,0},{9,1},... | collective-permute-start | bytes 147464 | tf_op jit(solution)/shard_map/ppermute | solution.py:16
  8.4 5.1 %collective-permute-start.1 = (bf16[2,96,256]{2,1,0:T(8,128)(2,1)S(1)}, bf16[2,96,256]{2,1,0:T(8,128)(2,1)S(1)}, u32[]{:S(2)}, u32[]{:S(2)}) collective-permute-start(bf16[2,96,256]{2,1,0:T(8,128)(2,1)S(1)} %pad_maximum_fusion.12), channel_id=1, source_target_pairs={{0,4},{1,5},{2,6},{3,7},{4,0},{5,1},{6,2},{7,3},{8,12},{9,13},{10,... | collective-permute-start | bytes 294920 | tf_op jit(solution)/shard_map/ppermute | solution.py:16
  11.4 5.3 %collective-permute-start.9 = (bf16[2,96,256]{2,1,0:T(8,128)(2,1)S(1)}, bf16[2,96,256]{2,1,0:T(8,128)(2,1)S(1)}, u32[]{:S(2)}, u32[]{:S(2)}) collective-permute-start(bf16[2,96,256]{2,1,0:T(8,128)(2,1)S(1)} %pad_maximum_fusion.13), channel_id=1, source_target_pairs={{0,2},{1,3},{2,0},{3,1},{4,6},{5,7},{6,4},{7,5},{8,10},{9,11},{10,... | collective-permute-start | bytes 294920 | tf_op jit(solution)/shard_map/ppermute | solution.py:16
  13.5 6.8 %collective-permute-start.2 = (bf16[2,2,96,256]{3,2,0,1:T(8,128)(2,1)S(1)}, bf16[2,2,96,256]{3,2,0,1:T(8,128)(2,1)S(1)}, u32[]{:S(2)}, u32[]{:S(2)}) collective-permute-start(bf16[2,2,96,256]{3,2,0,1:T(8,128)(2,1)S(1)} %pad_maximum_fusion.8), channel_id=1, source_target_pairs={{0,2},{1,3},{2,0},{3,1},{4,6},{5,7},{6,4},{7,5},{8,10},{9,11},{10,... | collective-permute-start | bytes 589832 | tf_op jit(solution)/shard_map/ppermute | solution.py:16
  16.8 5.7 %collective-permute-start.10 = (bf16[2,2,96,256]{3,2,1,0:T(8,128)(2,1)S(1)}, bf16[2,2,96,256]{3,2,1,0:T(8,128)(2,1)S(1)}, u32[]{:S(2)}, u32[]{:S(2)}) collective-permute-start(bf16[2,2,96,256]{3,2,1,0:T(8,128)(2,1)S(1)} %pad_maximum_fusion.9), channel_id=1, source_target_pairs={{0,4},{1,5},{2,6},{3,7},{4,0},{5,1},{6,2},{7,3},{8,12},{9,13},{10,... | collective-permute-start | bytes 589832 | tf_op jit(solution)/shard_map/ppermute | solution.py:16
  20.5 2.2 %collective-permute-start.3 = (bf16[2,2,2,96,256]{4,3,2,1,0:T(8,128)(2,1)S(1)}, bf16[2,2,2,96,256]{4,3,2,1,0:T(8,128)(2,1)S(1)}, u32[]{:S(2)}, u32[]{:S(2)}) collective-permute-start(bf16[2,2,2,96,256]{4,3,2,1,0:T(8,128)(2,1)S(1)} %copy.43), channel_id=1, source_target_pairs={{0,1},{1,0},{2,3},{3,2},{4,5},{5,4},{6,7},{7,6},{8,9},{9,8},{10,11... | collective-permute-start | bytes 1179656 | tf_op jit(solution)/shard_map/ppermute | solution.py:16
  22.6 3.6 %collective-permute-start.11 = (bf16[2,2,2,96,256]{4,3,2,0,1:T(8,128)(2,1)S(1)}, bf16[2,2,2,96,256]{4,3,2,0,1:T(8,128)(2,1)S(1)}, u32[]{:S(2)}, u32[]{:S(2)}) collective-permute-start(bf16[2,2,2,96,256]{4,3,2,0,1:T(8,128)(2,1)S(1)} %pad_maximum_fusion.5), channel_id=1, source_target_pairs={{0,1},{1,0},{2,3},{3,2},{4,5},{5,4},{6,7},{7,6},{8,9},{9,8},{10,11... | collective-permute-start | bytes 1179656 | tf_op jit(solution)/shard_map/ppermute | solution.py:16
  29.7 0.7 copy-start
  29.7 0.7 copy-start.1
  29.9 1.9 %collective-permute-start.4 = (bf16[2,2,2,96,256]{4,3,0,1,2:T(8,128)(2,1)S(1)}, bf16[2,2,2,96,256]{4,3,0,1,2:T(8,128)(2,1)S(1)}, u32[]{:S(2)}, u32[]{:S(2)}) collective-permute-start(bf16[2,2,2,96,256]{4,3,0,1,2:T(8,128)(2,1)S(1)} %bitcast.274), channel_id=1, source_target_pairs={{0,1},{1,0},{2,3},{3,2},{4,5},{5,4},{6,7},{7,6},{8,9},{9,8},{10,11... | collective-permute-start | bytes 1179656 | tf_op jit(solution)/shard_map/ppermute | solution.py:16
  30.5 3.1 %collective-permute-start.12 = (bf16[2,2,2,96,256]{4,3,0,2,1:T(8,128)(2,1)S(1)}, bf16[2,2,2,96,256]{4,3,0,2,1:T(8,128)(2,1)S(1)}, u32[]{:S(2)}, u32[]{:S(2)}) collective-permute-start(bf16[2,2,2,96,256]{4,3,0,2,1:T(8,128)(2,1)S(1)} %bitcast.273), channel_id=1, source_target_pairs={{0,1},{1,0},{2,3},{3,2},{4,5},{5,4},{6,7},{7,6},{8,9},{9,8},{10,11... | collective-permute-start | bytes 1179656 | tf_op jit(solution)/shard_map/ppermute | solution.py:16
  31.9 7.2 %collective-permute-start.5 = (bf16[2,2,96,256]{3,2,0,1:T(8,128)(2,1)S(1)}, bf16[2,2,96,256]{3,2,0,1:T(8,128)(2,1)S(1)}, u32[]{:S(2)}, u32[]{:S(2)}) collective-permute-start(bf16[2,2,96,256]{3,2,0,1:T(8,128)(2,1)S(1)} %dynamic-slice_bitcast_fusion.4), channel_id=1, source_target_pairs={{0,2},{1,3},{2,0},{3,1},{4,6},{5,7},{6,4},{7,5},{8,10},{9,11},{10,... | collective-permute-start | bytes 589832 | tf_op jit(solution)/shard_map/ppermute | solution.py:16
  33.7 7.0 %collective-permute-start.13 = (bf16[2,2,96,256]{3,2,0,1:T(8,128)(2,1)S(1)}, bf16[2,2,96,256]{3,2,0,1:T(8,128)(2,1)S(1)}, u32[]{:S(2)}, u32[]{:S(2)}) collective-permute-start(bf16[2,2,96,256]{3,2,0,1:T(8,128)(2,1)S(1)} %dynamic-slice_bitcast_fusion.3), channel_id=1, source_target_pairs={{0,4},{1,5},{2,6},{3,7},{4,0},{5,1},{6,2},{7,3},{8,12},{9,13},{10,... | collective-permute-start | bytes 589832 | tf_op jit(solution)/shard_map/ppermute | solution.py:16
  39.2 4.7 %collective-permute-start.6 = (bf16[2,96,256]{2,1,0:T(8,128)(2,1)S(1)}, bf16[2,96,256]{2,1,0:T(8,128)(2,1)S(1)}, u32[]{:S(2)}, u32[]{:S(2)}) collective-permute-start(bf16[2,96,256]{2,1,0:T(8,128)(2,1)S(1)} %dynamic-slice_bitcast_fusion.8), channel_id=1, source_target_pairs={{0,4},{1,5},{2,6},{3,7},{4,0},{5,1},{6,2},{7,3},{8,12},{9,13},{10,... | collective-permute-start | bytes 294920 | tf_op jit(solution)/shard_map/ppermute | solution.py:16
  40.7 7.0 %collective-permute-start.14 = (bf16[2,96,256]{2,1,0:T(8,128)(2,1)S(1)}, bf16[2,96,256]{2,1,0:T(8,128)(2,1)S(1)}, u32[]{:S(2)}, u32[]{:S(2)}) collective-permute-start(bf16[2,96,256]{2,1,0:T(8,128)(2,1)S(1)} %dynamic-slice_bitcast_fusion.7), channel_id=1, source_target_pairs={{0,2},{1,3},{2,0},{3,1},{4,6},{5,7},{6,4},{7,5},{8,10},{9,11},{10,... | collective-permute-start | bytes 294920 | tf_op jit(solution)/shard_map/ppermute | solution.py:16
  44.0 6.7 %collective-permute-start.7 = (bf16[96,256]{1,0:T(8,128)(2,1)S(1)}, bf16[96,256]{1,0:T(8,128)(2,1)S(1)}, u32[]{:S(2)}, u32[]{:S(2)}) collective-permute-start(bf16[96,256]{1,0:T(8,128)(2,1)S(1)} %dynamic-slice_bitcast_fusion.12), channel_id=1, source_target_pairs={{0,8},{1,9},{2,10},{3,11},{4,12},{5,13},{6,14},{7,15},{8,0},{9,1},... | collective-permute-start | bytes 147464 | tf_op jit(solution)/shard_map/ppermute | solution.py:16
  47.7 5.1 %collective-permute-start.15 = (bf16[96,256]{1,0:T(8,128)(2,1)S(1)}, bf16[96,256]{1,0:T(8,128)(2,1)S(1)}, u32[]{:S(2)}, u32[]{:S(2)}) collective-permute-start(bf16[96,256]{1,0:T(8,128)(2,1)S(1)} %dynamic-slice_bitcast_fusion.11), channel_id=1, source_target_pairs={{0,8},{1,9},{2,10},{3,11},{4,12},{5,13},{6,14},{7,15},{8,0},{9,1},... | collective-permute-start | bytes 147464 | tf_op jit(solution)/shard_map/ppermute | solution.py:16
  52.9 5.1 %collective-permute-start.16 = (bf16[96,256]{1,0:T(8,128)(2,1)S(1)}, bf16[96,256]{1,0:T(8,128)(2,1)S(1)}, u32[]{:S(2)}, u32[]{:S(2)}) collective-permute-start(bf16[96,256]{1,0:T(8,128)(2,1)S(1)} %get-tuple-element.28), channel_id=1, source_target_pairs={{0,8},{1,9},{2,10},{3,11},{4,12},{5,13},{6,14},{7,15},{8,0},{9,1},... | collective-permute-start | bytes 147464 | tf_op jit(solution)/shard_map/ppermute | solution.py:16
  53.9 5.6 %collective-permute-start.20 = (bf16[96,256]{1,0:T(8,128)(2,1)S(1)}, bf16[96,256]{1,0:T(8,128)(2,1)S(1)}, u32[]{:S(2)}, u32[]{:S(2)}) collective-permute-start(bf16[96,256]{1,0:T(8,128)(2,1)S(1)} %get-tuple-element.29), channel_id=1, source_target_pairs={{0,8},{1,9},{2,10},{3,11},{4,12},{5,13},{6,14},{7,15},{8,0},{9,1},... | collective-permute-start | bytes 147464 | tf_op jit(solution)/shard_map/ppermute | solution.py:16
  58.0 4.7 %collective-permute-start.17 = (bf16[2,96,256]{2,1,0:T(8,128)(2,1)S(1)}, bf16[2,96,256]{2,1,0:T(8,128)(2,1)S(1)}, u32[]{:S(2)}, u32[]{:S(2)}) collective-permute-start(bf16[2,96,256]{2,1,0:T(8,128)(2,1)S(1)} %pad_maximum_fusion.14), channel_id=1, source_target_pairs={{0,4},{1,5},{2,6},{3,7},{4,0},{5,1},{6,2},{7,3},{8,12},{9,13},{10,... | collective-permute-start | bytes 294920 | tf_op jit(solution)/shard_map/ppermute | solution.py:16
  59.6 5.7 %collective-permute-start.21 = (bf16[2,96,256]{2,1,0:T(8,128)(2,1)S(1)}, bf16[2,96,256]{2,1,0:T(8,128)(2,1)S(1)}, u32[]{:S(2)}, u32[]{:S(2)}) collective-permute-start(bf16[2,96,256]{2,1,0:T(8,128)(2,1)S(1)} %pad_maximum_fusion.15), channel_id=1, source_target_pairs={{0,2},{1,3},{2,0},{3,1},{4,6},{5,7},{6,4},{7,5},{8,10},{9,11},{10,... | collective-permute-start | bytes 294920 | tf_op jit(solution)/shard_map/ppermute | solution.py:16
  62.7 5.7 %collective-permute-start.18 = (bf16[2,2,96,256]{3,2,0,1:T(8,128)(2,1)S(1)}, bf16[2,2,96,256]{3,2,0,1:T(8,128)(2,1)S(1)}, u32[]{:S(2)}, u32[]{:S(2)}) collective-permute-start(bf16[2,2,96,256]{3,2,0,1:T(8,128)(2,1)S(1)} %pad_maximum_fusion.10), channel_id=1, source_target_pairs={{0,2},{1,3},{2,0},{3,1},{4,6},{5,7},{6,4},{7,5},{8,10},{9,11},{10,... | collective-permute-start | bytes 589832 | tf_op jit(solution)/shard_map/ppermute | solution.py:16
  65.3 5.7 %collective-permute-start.22 = (bf16[2,2,96,256]{3,2,1,0:T(8,128)(2,1)S(1)}, bf16[2,2,96,256]{3,2,1,0:T(8,128)(2,1)S(1)}, u32[]{:S(2)}, u32[]{:S(2)}) collective-permute-start(bf16[2,2,96,256]{3,2,1,0:T(8,128)(2,1)S(1)} %pad_maximum_fusion.11), channel_id=1, source_target_pairs={{0,4},{1,5},{2,6},{3,7},{4,0},{5,1},{6,2},{7,3},{8,12},{9,13},{10,... | collective-permute-start | bytes 589832 | tf_op jit(solution)/shard_map/ppermute | solution.py:16
  68.5 2.7 %collective-permute-start.19 = (bf16[2,2,2,96,256]{4,3,0,1,2:T(8,128)(2,1)S(1)}, bf16[2,2,2,96,256]{4,3,0,1,2:T(8,128)(2,1)S(1)}, u32[]{:S(2)}, u32[]{:S(2)}) collective-permute-start(bf16[2,2,2,96,256]{4,3,0,1,2:T(8,128)(2,1)S(1)} %pad_maximum_fusion.6), channel_id=1, source_target_pairs={{0,1},{1,0},{2,3},{3,2},{4,5},{5,4},{6,7},{7,6},{8,9},{9,8},{10,11... | collective-permute-start | bytes 1179656 | tf_op jit(solution)/shard_map/ppermute | solution.py:16
  71.2 1.8 %collective-permute-start.23 = (bf16[2,2,2,96,256]{4,3,2,1,0:T(8,128)(2,1)S(1)}, bf16[2,2,2,96,256]{4,3,2,1,0:T(8,128)(2,1)S(1)}, u32[]{:S(2)}, u32[]{:S(2)}) collective-permute-start(bf16[2,2,2,96,256]{4,3,2,1,0:T(8,128)(2,1)S(1)} %pad_maximum_fusion.7), channel_id=1, source_target_pairs={{0,1},{1,0},{2,3},{3,2},{4,5},{5,4},{6,7},{7,6},{8,9},{9,8},{10,11... | collective-permute-start | bytes 1179656 | tf_op jit(solution)/shard_map/ppermute | solution.py:16
  73.5 3.3 %copy-start.2 = (f32[256]{0:T(256)}, f32[256]{0:T(256)S(1)}, u32[]{:S(2)}) copy-start(f32[256]{0:T(256)S(1)} %add_rsqrt_fusion.1) | copy-start | bytes 3076
  76.8 4.1 %collective-permute-start.28 = (bf16[2,2,2,96,256]{4,3,0,2,1:T(8,128)(2,1)S(1)}, bf16[2,2,2,96,256]{4,3,0,2,1:T(8,128)(2,1)S(1)}, u32[]{:S(2)}, u32[]{:S(2)}) collective-permute-start(bf16[2,2,2,96,256]{4,3,0,2,1:T(8,128)(2,1)S(1)} %bitcast.275), channel_id=1, source_target_pairs={{0,1},{1,0},{2,3},{3,2},{4,5},{5,4},{6,7},{7,6},{8,9},{9,8},{10,11... | collective-permute-start | bytes 1179656 | tf_op jit(solution)/shard_map/ppermute | solution.py:16
  80.4 1.8 %collective-permute-start.24 = (bf16[2,2,2,96,256]{4,3,2,1,0:T(8,128)(2,1)S(1)}, bf16[2,2,2,96,256]{4,3,2,1,0:T(8,128)(2,1)S(1)}, u32[]{:S(2)}, u32[]{:S(2)}) collective-permute-start(bf16[2,2,2,96,256]{4,3,2,1,0:T(8,128)(2,1)S(1)} %dynamic-slice_bitcast_fusion), channel_id=1, source_target_pairs={{0,1},{1,0},{2,3},{3,2},{4,5},{5,4},{6,7},{7,6},{8,9},{9,8},{10,11... | collective-permute-start | bytes 1179656 | tf_op jit(solution)/shard_map/ppermute | solution.py:16
  81.0 7.0 %collective-permute-start.29 = (bf16[2,2,96,256]{3,2,0,1:T(8,128)(2,1)S(1)}, bf16[2,2,96,256]{3,2,0,1:T(8,128)(2,1)S(1)}, u32[]{:S(2)}, u32[]{:S(2)}) collective-permute-start(bf16[2,2,96,256]{3,2,0,1:T(8,128)(2,1)S(1)} %dynamic-slice_bitcast_fusion.1), channel_id=1, source_target_pairs={{0,4},{1,5},{2,6},{3,7},{4,0},{5,1},{6,2},{7,3},{8,12},{9,13},{10,... | collective-permute-start | bytes 589832 | tf_op jit(solution)/shard_map/ppermute | solution.py:16
  82.3 7.2 %collective-permute-start.25 = (bf16[2,2,96,256]{3,2,1,0:T(8,128)(2,1)S(1)}, bf16[2,2,96,256]{3,2,1,0:T(8,128)(2,1)S(1)}, u32[]{:S(2)}, u32[]{:S(2)}) collective-permute-start(bf16[2,2,96,256]{3,2,1,0:T(8,128)(2,1)S(1)} %dynamic-slice_bitcast_fusion.2), channel_id=1, source_target_pairs={{0,2},{1,3},{2,0},{3,1},{4,6},{5,7},{6,4},{7,5},{8,10},{9,11},{10,... | collective-permute-start | bytes 589832 | tf_op jit(solution)/shard_map/ppermute | solution.py:16
  88.2 4.7 %collective-permute-start.30 = (bf16[2,96,256]{2,1,0:T(8,128)(2,1)S(1)}, bf16[2,96,256]{2,1,0:T(8,128)(2,1)S(1)}, u32[]{:S(2)}, u32[]{:S(2)}) collective-permute-start(bf16[2,96,256]{2,1,0:T(8,128)(2,1)S(1)} %dynamic-slice_bitcast_fusion.5), channel_id=1, source_target_pairs={{0,2},{1,3},{2,0},{3,1},{4,6},{5,7},{6,4},{7,5},{8,10},{9,11},{10,... | collective-permute-start | bytes 294920 | tf_op jit(solution)/shard_map/ppermute | solution.py:16
  89.6 4.7 %collective-permute-start.26 = (bf16[2,96,256]{2,1,0:T(8,128)(2,1)S(1)}, bf16[2,96,256]{2,1,0:T(8,128)(2,1)S(1)}, u32[]{:S(2)}, u32[]{:S(2)}) collective-permute-start(bf16[2,96,256]{2,1,0:T(8,128)(2,1)S(1)} %dynamic-slice_bitcast_fusion.6), channel_id=1, source_target_pairs={{0,4},{1,5},{2,6},{3,7},{4,0},{5,1},{6,2},{7,3},{8,12},{9,13},{10,... | collective-permute-start | bytes 294920 | tf_op jit(solution)/shard_map/ppermute | solution.py:16
  92.9 5.5 %collective-permute-start.31 = (bf16[96,256]{1,0:T(8,128)(2,1)S(1)}, bf16[96,256]{1,0:T(8,128)(2,1)S(1)}, u32[]{:S(2)}, u32[]{:S(2)}) collective-permute-start(bf16[96,256]{1,0:T(8,128)(2,1)S(1)} %dynamic-slice_bitcast_fusion.9), channel_id=1, source_target_pairs={{0,8},{1,9},{2,10},{3,11},{4,12},{5,13},{6,14},{7,15},{8,0},{9,1},... | collective-permute-start | bytes 147464 | tf_op jit(solution)/shard_map/ppermute | solution.py:16
  94.4 5.1 %collective-permute-start.27 = (bf16[96,256]{1,0:T(8,128)(2,1)S(1)}, bf16[96,256]{1,0:T(8,128)(2,1)S(1)}, u32[]{:S(2)}, u32[]{:S(2)}) collective-permute-start(bf16[96,256]{1,0:T(8,128)(2,1)S(1)} %dynamic-slice_bitcast_fusion.10), channel_id=1, source_target_pairs={{0,8},{1,9},{2,10},{3,11},{4,12},{5,13},{6,14},{7,15},{8,0},{9,1},... | collective-permute-start | bytes 147464 | tf_op jit(solution)/shard_map/ppermute | solution.py:16
  99.6 3.1 %collective-permute-start.34 = (f32[256]{0:T(256)S(1)}, f32[256]{0:T(256)S(1)}, u32[]{:S(2)}, u32[]{:S(2)}) collective-permute-start(f32[256]{0:T(256)S(1)} %add.192), channel_id=1, source_target_pairs={{0,3},{1,2},{2,1},{3,0},{4,7},{5,6},{6,5},{7,4},{8,11},{9,10},{10,... | collective-permute-start | bytes 3080 | tf_op jit(solution)/shard_map/ppermute | solution.py:16
  99.6 3.6 %collective-permute-start.33 = (f32[256]{0:T(256)S(1)}, f32[256]{0:T(256)S(1)}, u32[]{:S(2)}, u32[]{:S(2)}) collective-permute-start(f32[256]{0:T(256)S(1)} %add.192), channel_id=1, source_target_pairs={{0,2},{1,3},{2,0},{3,1},{4,6},{5,7},{6,4},{7,5},{8,10},{9,11},{10,... | collective-permute-start | bytes 3080 | tf_op jit(solution)/shard_map/ppermute | solution.py:16
  101.0 2.3 %collective-permute-start.32 = (f32[256]{0:T(256)S(1)}, f32[256]{0:T(256)S(1)}, u32[]{:S(2)}, u32[]{:S(2)}) collective-permute-start(f32[256]{0:T(256)S(1)} %add.192), channel_id=1, source_target_pairs={{0,1},{1,0},{2,3},{3,2},{4,5},{5,4},{6,7},{7,6},{8,9},{9,8},{10,11... | collective-permute-start | bytes 3080 | tf_op jit(solution)/shard_map/ppermute | solution.py:16
  103.3 5.4 %collective-permute-start.37 = (f32[256]{0:T(256)S(1)}, f32[256]{0:T(256)S(1)}, u32[]{:S(2)}, u32[]{:S(2)}) collective-permute-start(f32[256]{0:T(256)S(1)} %add_add_fusion), channel_id=1, source_target_pairs={{0,12},{1,13},{2,14},{3,15},{4,8},{5,9},{6,10},{7,11},{8,4},{9,5},... | collective-permute-start | bytes 3080 | tf_op jit(solution)/shard_map/ppermute | solution.py:16
  105.2 4.5 %collective-permute-start.36 = (f32[256]{0:T(256)S(1)}, f32[256]{0:T(256)S(1)}, u32[]{:S(2)}, u32[]{:S(2)}) collective-permute-start(f32[256]{0:T(256)S(1)} %add_add_fusion), channel_id=1, source_target_pairs={{0,8},{1,9},{2,10},{3,11},{4,12},{5,13},{6,14},{7,15},{8,0},{9,1},... | collective-permute-start | bytes 3080 | tf_op jit(solution)/shard_map/ppermute | solution.py:16
  105.9 3.8 %collective-permute-start.35 = (f32[256]{0:T(256)S(1)}, f32[256]{0:T(256)S(1)}, u32[]{:S(2)}, u32[]{:S(2)}) collective-permute-start(f32[256]{0:T(256)S(1)} %add_add_fusion), channel_id=1, source_target_pairs={{0,4},{1,5},{2,6},{3,7},{4,0},{5,1},{6,2},{7,3},{8,12},{9,13},{10,... | collective-permute-start | bytes 3080 | tf_op jit(solution)/shard_map/ppermute | solution.py:16

commit v16 on v14

--- a/solution.py
+++ b/solution.py
@@ -75,8 +75,11 @@
     all_channels = chan_rows * devices
     first_row = lax.axis_index("row") * chan_rows
     order_amp, order_der = stage_orders(devices)
+    gather_order_der = order_der[::-1]
+    if len(gather_order_der) >= 4:
+        gather_order_der = [gather_order_der[1], gather_order_der[0]] + gather_order_der[2:]
     amp_full = doubling_all_gather(first_f, devices, order_amp[::-1])
-    der_full = doubling_all_gather(first_g, devices, order_der[::-1])
+    der_full = doubling_all_gather(first_g, devices, gather_order_der)
     scale = None
     for sector in range(SECTORS):
         halves = []
@@ -98,7 +101,7 @@
         new_der = -wave * sine * rot_amp + cosine * rot_der
         if sector + 1 < SECTORS:
             amp_full = doubling_all_gather(new_amp.astype(jnp.bfloat16), devices, order_amp[::-1])
-            der_full = doubling_all_gather(new_der.astype(jnp.bfloat16), devices, order_der[::-1])
+            der_full = doubling_all_gather(new_der.astype(jnp.bfloat16), devices, gather_order_der)
             amp_wide = amp_full.astype(jnp.float32)
             der_wide = der_full.astype(jnp.float32)
             norm = jnp.sum(amp_wide * amp_wide, axis=0) + jnp.sum(der_wide * der_wide, axis=0)

time: 111 us -> 111 us (level)
  starting transfers between devices: 37 us -> 46.6 us
  waiting for transfers between devices: 53.1 us -> 44 us
    ppermute x38, starting transfers between devices: 37 us -> 46.6 us  [exchange(): return lax.ppermute(x, 'row', [(i, i ^ distance) for i in range(devices)])]
    ppermute x38, waiting for transfers between devices: 53.1 us -> 44 us  [exchange(): return lax.ppermute(x, 'row', [(i, i ^ distance) for i in range(devices)])]
  transfers between devices with their start and end apart: 38 -> 38, of which waited for: 30 -> 25; matrix products, arithmetic and copies ran while one was open for 10% -> 10% of each run, Pallas kernels for 0% -> 0%
where the time goes in v16:
time: 111 us
  starting transfers between devices  46.6 us (42%)
  waiting for transfers between devices  44 us (40%)
  matrix products  11.9 us (11%)
  other arithmetic  4.98 us (4%)
  local copies, waits for them, and re-layouts  2.09 us (2%)
  between operations  1.33 us (1%)
    ppermute x38, starting transfers between devices, exchange(): return lax.ppermute(x, 'row', [(i, i ^ distance) for i in range(devices)])  46.6 us
    ppermute x38, waiting for transfers between devices, exchange(): return lax.ppermute(x, 'row', [(i, i ^ distance) for i in range(devices)])  44 us
    dot_general x4, matrix products, contract_rows(): lax.dot_general(left, right, (((0,), (0,)), ((), ())), preferred_element_...  11.9 us
    another operation x32, other arithmetic, doubling_all_gather(): jnp.stack([jnp.where(low, cur, other), jnp.where(low, other, cur)], axis=...  2.76 us
  transfers between devices with their start and end apart: 38, of which 25 were waited for; matrix products, arithmetic and copies ran while one was open for 10% of the time, Pallas kernels for 0%

profile of v16, /device:TPU:0, one launch (start us, length us, event | category | flops | bytes accessed | tf_op | source)
XLA Modules:
  0.0 110.9 jit_solution(15105929887323058275)
XLA Ops:
  0.6 4.1 %collective-permute-start = (bf16[96,256]{1,0:T(8,128)(2,1)}, bf16[96,256]{1,0:T(8,128)(2,1)S(1)}, u32[]{:S(2)}, u32[]{:S(2)}) collective-permute-start(bf16[96,256]{1,0:T(8,128)(2,1)} %param.6), channel_id=1, source_target_pairs={{0,8},{1,9},{2,10},{3,11},{4,12},{5,13},{6,14},{7,15},{8,0},{9,1},... | collective-permute-start | bytes 147464 | tf_op jit(solution)/shard_map/ppermute | solution.py:16
  4.7 1.5 %collective-permute-start.8 = (bf16[96,256]{1,0:T(8,128)(2,1)}, bf16[96,256]{1,0:T(8,128)(2,1)S(1)}, u32[]{:S(2)}, u32[]{:S(2)}) collective-permute-start(bf16[96,256]{1,0:T(8,128)(2,1)} %param.7), channel_id=1, source_target_pairs={{0,2},{1,3},{2,0},{3,1},{4,6},{5,7},{6,4},{7,5},{8,10},{9,11},{10,... | collective-permute-start | bytes 147464 | tf_op jit(solution)/shard_map/ppermute | solution.py:16
  6.3 1.3 %collective-permute-done = bf16[96,256]{1,0:T(8,128)(2,1)S(1)} collective-permute-done((bf16[96,256]{1,0:T(8,128)(2,1)}, bf16[96,256]{1,0:T(8,128)(2,1)S(1)}, u32[]{:S(2)}, u32[]{:S(2)}) %collective-permute-start) | collective-permute-done | bytes 49184 | tf_op jit(solution)/shard_map/ppermute | solution.py:16
  7.5 0.8 select_bitcast_fusion.31
  8.4 1.4 %collective-permute-start.1 = (bf16[2,96,256]{2,1,0:T(8,128)(2,1)S(1)}, bf16[2,96,256]{2,1,0:T(8,128)(2,1)S(1)}, u32[]{:S(2)}, u32[]{:S(2)}) collective-permute-start(bf16[2,96,256]{2,1,0:T(8,128)(2,1)S(1)} %pad_maximum_fusion.12), channel_id=1, source_target_pairs={{0,4},{1,5},{2,6},{3,7},{4,0},{5,1},{6,2},{7,3},{8,12},{9,13},{10,... | collective-permute-start | bytes 294920 | tf_op jit(solution)/shard_map/ppermute | solution.py:16
  9.8 0.8 select_bitcast_fusion.29
  10.7 3.1 %collective-permute-start.9 = (bf16[2,96,256]{2,1,0:T(8,128)(2,1)S(1)}, bf16[2,96,256]{2,1,0:T(8,128)(2,1)S(1)}, u32[]{:S(2)}, u32[]{:S(2)}) collective-permute-start(bf16[2,96,256]{2,1,0:T(8,128)(2,1)S(1)} %pad_maximum_fusion.13), channel_id=1, source_target_pairs={{0,8},{1,9},{2,10},{3,11},{4,12},{5,13},{6,14},{7,15},{8,0},{9,1},... | collective-permute-start | bytes 294920 | tf_op jit(solution)/shard_map/ppermute | solution.py:16
  13.8 1.6 %collective-permute-start.2 = (bf16[2,2,96,256]{3,2,0,1:T(8,128)(2,1)S(1)}, bf16[2,2,96,256]{3,2,0,1:T(8,128)(2,1)S(1)}, u32[]{:S(2)}, u32[]{:S(2)}) collective-permute-start(bf16[2,2,96,256]{3,2,0,1:T(8,128)(2,1)S(1)} %pad_maximum_fusion.8), channel_id=1, source_target_pairs={{0,2},{1,3},{2,0},{3,1},{4,6},{5,7},{6,4},{7,5},{8,10},{9,11},{10,... | collective-permute-start | bytes 589832 | tf_op jit(solution)/shard_map/ppermute | solution.py:16
  15.4 2.0 %collective-permute-done.9 = bf16[2,96,256]{2,1,0:T(8,128)(2,1)S(1)} collective-permute-done((bf16[2,96,256]{2,1,0:T(8,128)(2,1)S(1)}, bf16[2,96,256]{2,1,0:T(8,128)(2,1)S(1)}, u32[]{:S(2)}, u32[]{:S(2)}) %collective-permute-start.9) | collective-permute-done | bytes 98336 | tf_op jit(solution)/shard_map/ppermute | solution.py:16
  17.5 2.0 %collective-permute-done.2 = bf16[2,2,96,256]{3,2,0,1:T(8,128)(2,1)S(1)} collective-permute-done((bf16[2,2,96,256]{3,2,0,1:T(8,128)(2,1)S(1)}, bf16[2,2,96,256]{3,2,0,1:T(8,128)(2,1)S(1)}, u32[]{:S(2)}, u32[]{:S(2)}) %collective-permute-start.2) | collective-permute-done | bytes 196640 | tf_op jit(solution)/shard_map/ppermute | solution.py:16
  19.7 3.4 %collective-permute-done.10 = bf16[2,2,96,256]{3,2,1,0:T(8,128)(2,1)S(1)} collective-permute-done((bf16[2,2,96,256]{3,2,1,0:T(8,128)(2,1)S(1)}, bf16[2,2,96,256]{3,2,1,0:T(8,128)(2,1)S(1)}, u32[]{:S(2)}, u32[]{:S(2)}) %collective-permute-start.10) | collective-permute-done | bytes 196640 | tf_op jit(solution)/shard_map/ppermute | solution.py:16
  23.6 3.0 %fusion = bf16[1536,256]{0,1:T(8,128)(2,1)S(1)} fusion(bf16[1536,256]{1,0:T(8,128)(2,1)S(1)} %bitcast.253, bf16[3,512,1536]{2,1,0:T(8,128)(2,1)} %param.5), kind=kOutput, calls=%fused_computation.4 | convolution fusion | flops 805830656 | bytes 4718592 | tf_op jit(solution)/shard_map/dot_general | solution.py:10
  26.6 0.3 copy.22
  27.0 3.0 %fusion.1 = bf16[1536,256]{0,1:T(8,128)(2,1)S(1)} fusion(bf16[1536,256]{1,0:T(8,128)(2,1)S(1)} %bitcast.254, bf16[3,512,1536]{2,1,0:T(8,128)(2,1)} %param.5), kind=kOutput, calls=%fused_computation.5 | convolution fusion | flops 805830656 | bytes 4718592 | tf_op jit(solution)/shard_map/dot_general | solution.py:10
  30.0 0.3 copy.28
  30.5 0.6 collective-permute-start.4
  31.1 0.5 collective-permute-start.12
  31.8 0.6 collective-permute-done.4
  32.5 1.6 %collective-permute-start.5 = (bf16[2,2,96,256]{3,2,0,1:T(8,128)(2,1)S(1)}, bf16[2,2,96,256]{3,2,0,1:T(8,128)(2,1)S(1)}, u32[]{:S(2)}, u32[]{:S(2)}) collective-permute-start(bf16[2,2,96,256]{3,2,0,1:T(8,128)(2,1)S(1)} %fusion.54), channel_id=1, source_target_pairs={{0,2},{1,3},{2,0},{3,1},{4,6},{5,7},{6,4},{7,5},{8,10},{9,11},{10,... | collective-permute-start | bytes 589832 | tf_op jit(solution)/shard_map/ppermute | solution.py:16
  34.3 5.4 %collective-permute-done.5 = bf16[2,2,96,256]{3,2,0,1:T(8,128)(2,1)S(1)} collective-permute-done((bf16[2,2,96,256]{3,2,0,1:T(8,128)(2,1)S(1)}, bf16[2,2,96,256]{3,2,0,1:T(8,128)(2,1)S(1)}, u32[]{:S(2)}, u32[]{:S(2)}) %collective-permute-start.5) | collective-permute-done | bytes 196640 | tf_op jit(solution)/shard_map/ppermute | solution.py:16
  39.9 1.3 %collective-permute-done.13 = bf16[2,2,96,256]{3,2,0,1:T(8,128)(2,1)S(1)} collective-permute-done((bf16[2,2,96,256]{3,2,0,1:T(8,128)(2,1)S(1)}, bf16[2,2,96,256]{3,2,0,1:T(8,128)(2,1)S(1)}, u32[]{:S(2)}, u32[]{:S(2)}) %collective-permute-start.13) | collective-permute-done | bytes 196640 | tf_op jit(solution)/shard_map/ppermute | solution.py:16
  41.3 0.8 collective-permute-start.14
  42.0 2.5 %collective-permute-done.6 = bf16[2,96,256]{2,1,0:T(8,128)(2,1)S(1)} collective-permute-done((bf16[2,96,256]{2,1,0:T(8,128)(2,1)S(1)}, bf16[2,96,256]{2,1,0:T(8,128)(2,1)S(1)}, u32[]{:S(2)}, u32[]{:S(2)}) %collective-permute-start.6) | collective-permute-done | bytes 98336 | tf_op jit(solution)/shard_map/ppermute | solution.py:16
  44.6 2.7 %collective-permute-start.7 = (bf16[96,256]{1,0:T(8,128)(2,1)S(1)}, bf16[96,256]{1,0:T(8,128)(2,1)S(1)}, u32[]{:S(2)}, u32[]{:S(2)}) collective-permute-start(bf16[96,256]{1,0:T(8,128)(2,1)S(1)} %fusion.62), channel_id=1, source_target_pairs={{0,8},{1,9},{2,10},{3,11},{4,12},{5,13},{6,14},{7,15},{8,0},{9,1},... | collective-permute-start | bytes 147464 | tf_op jit(solution)/shard_map/ppermute | solution.py:16
  47.4 1.2 %collective-permute-start.15 = (bf16[96,256]{1,0:T(8,128)(2,1)S(1)}, bf16[96,256]{1,0:T(8,128)(2,1)S(1)}, u32[]{:S(2)}, u32[]{:S(2)}) collective-permute-start(bf16[96,256]{1,0:T(8,128)(2,1)S(1)} %fusion.63), channel_id=1, source_target_pairs={{0,8},{1,9},{2,10},{3,11},{4,12},{5,13},{6,14},{7,15},{8,0},{9,1},... | collective-permute-start | bytes 147464 | tf_op jit(solution)/shard_map/ppermute | solution.py:16
  48.7 2.0 %collective-permute-done.7 = bf16[96,256]{1,0:T(8,128)(2,1)S(1)} collective-permute-done((bf16[96,256]{1,0:T(8,128)(2,1)S(1)}, bf16[96,256]{1,0:T(8,128)(2,1)S(1)}, u32[]{:S(2)}, u32[]{:S(2)}) %collective-permute-start.7) | collective-permute-done | bytes 49184 | tf_op jit(solution)/shard_map/ppermute | solution.py:16
  50.6 1.8 %collective-permute-done.15 = bf16[96,256]{1,0:T(8,128)(2,1)S(1)} collective-permute-done((bf16[96,256]{1,0:T(8,128)(2,1)S(1)}, bf16[96,256]{1,0:T(8,128)(2,1)S(1)}, u32[]{:S(2)}, u32[]{:S(2)}) %collective-permute-start.15) | collective-permute-done | bytes 49184 | tf_op jit(solution)/shard_map/ppermute | solution.py:16
  52.5 1.2 %collective-permute-start.16 = (bf16[96,256]{1,0:T(8,128)(2,1)S(1)}, bf16[96,256]{1,0:T(8,128)(2,1)S(1)}, u32[]{:S(2)}, u32[]{:S(2)}) collective-permute-start(bf16[96,256]{1,0:T(8,128)(2,1)S(1)} %get-tuple-element.22), channel_id=1, source_target_pairs={{0,8},{1,9},{2,10},{3,11},{4,12},{5,13},{6,14},{7,15},{8,0},{9,1},... | collective-permute-start | bytes 147464 | tf_op jit(solution)/shard_map/ppermute | solution.py:16
  53.7 0.9 collective-permute-start.20
  54.6 3.0 %collective-permute-done.16 = bf16[96,256]{1,0:T(8,128)(2,1)S(1)} collective-permute-done((bf16[96,256]{1,0:T(8,128)(2,1)S(1)}, bf16[96,256]{1,0:T(8,128)(2,1)S(1)}, u32[]{:S(2)}, u32[]{:S(2)}) %collective-permute-start.16) | collective-permute-done | bytes 49184 | tf_op jit(solution)/shard_map/ppermute | solution.py:16
  57.8 1.9 %collective-permute-start.21 = (bf16[2,96,256]{2,1,0:T(8,128)(2,1)S(1)}, bf16[2,96,256]{2,1,0:T(8,128)(2,1)S(1)}, u32[]{:S(2)}, u32[]{:S(2)}) collective-permute-start(bf16[2,96,256]{2,1,0:T(8,128)(2,1)S(1)} %pad_maximum_fusion.15), channel_id=1, source_target_pairs={{0,8},{1,9},{2,10},{3,11},{4,12},{5,13},{6,14},{7,15},{8,0},{9,1},... | collective-permute-start | bytes 294920 | tf_op jit(solution)/shard_map/ppermute | solution.py:16
  59.8 2.5 %collective-permute-done.17 = bf16[2,96,256]{2,1,0:T(8,128)(2,1)S(1)} collective-permute-done((bf16[2,96,256]{2,1,0:T(8,128)(2,1)S(1)}, bf16[2,96,256]{2,1,0:T(8,128)(2,1)S(1)}, u32[]{:S(2)}, u32[]{:S(2)}) %collective-permute-start.17) | collective-permute-done | bytes 98336 | tf_op jit(solution)/shard_map/ppermute | solution.py:16
  62.4 1.6 %collective-permute-start.18 = (bf16[2,2,96,256]{3,2,0,1:T(8,128)(2,1)S(1)}, bf16[2,2,96,256]{3,2,0,1:T(8,128)(2,1)S(1)}, u32[]{:S(2)}, u32[]{:S(2)}) collective-permute-start(bf16[2,2,96,256]{3,2,0,1:T(8,128)(2,1)S(1)} %pad_maximum_fusion.10), channel_id=1, source_target_pairs={{0,2},{1,3},{2,0},{3,1},{4,6},{5,7},{6,4},{7,5},{8,10},{9,11},{10,... | collective-permute-start | bytes 589832 | tf_op jit(solution)/shard_map/ppermute | solution.py:16
  64.0 2.5 %collective-permute-start.22 = (bf16[2,2,96,256]{3,2,1,0:T(8,128)(2,1)S(1)}, bf16[2,2,96,256]{3,2,1,0:T(8,128)(2,1)S(1)}, u32[]{:S(2)}, u32[]{:S(2)}) collective-permute-start(bf16[2,2,96,256]{3,2,1,0:T(8,128)(2,1)S(1)} %pad_maximum_fusion.11), channel_id=1, source_target_pairs={{0,4},{1,5},{2,6},{3,7},{4,0},{5,1},{6,2},{7,3},{8,12},{9,13},{10,... | collective-permute-start | bytes 589832 | tf_op jit(solution)/shard_map/ppermute | solution.py:16
  66.5 1.6 %collective-permute-done.18 = bf16[2,2,96,256]{3,2,0,1:T(8,128)(2,1)S(1)} collective-permute-done((bf16[2,2,96,256]{3,2,0,1:T(8,128)(2,1)S(1)}, bf16[2,2,96,256]{3,2,0,1:T(8,128)(2,1)S(1)}, u32[]{:S(2)}, u32[]{:S(2)}) %collective-permute-start.18) | collective-permute-done | bytes 196640 | tf_op jit(solution)/shard_map/ppermute | solution.py:16
  68.3 1.9 %collective-permute-done.22 = bf16[2,2,96,256]{3,2,1,0:T(8,128)(2,1)S(1)} collective-permute-done((bf16[2,2,96,256]{3,2,1,0:T(8,128)(2,1)S(1)}, bf16[2,2,96,256]{3,2,1,0:T(8,128)(2,1)S(1)}, u32[]{:S(2)}, u32[]{:S(2)}) %collective-permute-start.22) | collective-permute-done | bytes 196640 | tf_op jit(solution)/shard_map/ppermute | solution.py:16
  70.4 0.2 multiply_reduce_fusion.1
  70.7 1.3 %collective-permute-done.23 = bf16[2,2,2,96,256]{4,3,2,1,0:T(8,128)(2,1)S(1)} collective-permute-done((bf16[2,2,2,96,256]{4,3,2,1,0:T(8,128)(2,1)S(1)}, bf16[2,2,2,96,256]{4,3,2,1,0:T(8,128)(2,1)S(1)}, u32[]{:S(2)}, u32[]{:S(2)}) %collective-permute-start.23) | collective-permute-done | bytes 393248 | tf_op jit(solution)/shard_map/ppermute | solution.py:16
  72.1 0.2 multiply_reduce_fusion
  72.5 3.0 %fusion.3 = bf16[1536,256]{0,1:T(8,128)(2,1)S(1)} fusion(bf16[3,512,1536]{2,1,0:T(8,128)(2,1)} %param.5, bf16[1536,256]{1,0:T(8,128)(2,1)S(1)} %bitcast.252, f32[256]{0:T(256)S(1)} %add_rsqrt_fusion.1), kind=kOutput, calls=%fused_computation.7 | convolution fusion | flops 805961728 | bytes 4719616 | tf_op jit(solution)/shard_map/dot_general | solution.py:10
  75.5 0.3 copy.37
  76.1 3.0 %fusion.2 = bf16[1536,256]{0,1:T(8,128)(2,1)S(1)} fusion(bf16[3,512,1536]{2,1,0:T(8,128)(2,1)} %param.5, bf16[1536,256]{1,0:T(8,128)(2,1)S(1)} %bitcast.251, f32[256]{0:T(256)} %copy-done.2), kind=kOutput, calls=%fused_computation.6 | convolution fusion | flops 805961728 | bytes 4719616 | tf_op jit(solution)/shard_map/dot_general | solution.py:10
  79.1 0.3 copy.35
  79.4 0.4 collective-permute-start.24
  80.1 2.1 %collective-permute-start.29 = (bf16[2,2,96,256]{3,2,0,1:T(8,128)(2,1)S(1)}, bf16[2,2,96,256]{3,2,0,1:T(8,128)(2,1)S(1)}, u32[]{:S(2)}, u32[]{:S(2)}) collective-permute-start(bf16[2,2,96,256]{3,2,0,1:T(8,128)(2,1)S(1)} %fusion.57), channel_id=1, source_target_pairs={{0,4},{1,5},{2,6},{3,7},{4,0},{5,1},{6,2},{7,3},{8,12},{9,13},{10,... | collective-permute-start | bytes 589832 | tf_op jit(solution)/shard_map/ppermute | solution.py:16
  82.3 1.6 %collective-permute-start.25 = (bf16[2,2,96,256]{3,2,1,0:T(8,128)(2,1)S(1)}, bf16[2,2,96,256]{3,2,1,0:T(8,128)(2,1)S(1)}, u32[]{:S(2)}, u32[]{:S(2)}) collective-permute-start(bf16[2,2,96,256]{3,2,1,0:T(8,128)(2,1)S(1)} %fusion.56), channel_id=1, source_target_pairs={{0,2},{1,3},{2,0},{3,1},{4,6},{5,7},{6,4},{7,5},{8,10},{9,11},{10,... | collective-permute-start | bytes 589832 | tf_op jit(solution)/shard_map/ppermute | solution.py:16
  84.0 3.4 %collective-permute-done.29 = bf16[2,2,96,256]{3,2,0,1:T(8,128)(2,1)S(1)} collective-permute-done((bf16[2,2,96,256]{3,2,0,1:T(8,128)(2,1)S(1)}, bf16[2,2,96,256]{3,2,0,1:T(8,128)(2,1)S(1)}, u32[]{:S(2)}, u32[]{:S(2)}) %collective-permute-start.29) | collective-permute-done | bytes 196640 | tf_op jit(solution)/shard_map/ppermute | solution.py:16
  87.5 1.6 %collective-permute-start.30 = (bf16[2,96,256]{2,1,0:T(8,128)(2,1)S(1)}, bf16[2,96,256]{2,1,0:T(8,128)(2,1)S(1)}, u32[]{:S(2)}, u32[]{:S(2)}) collective-permute-start(bf16[2,96,256]{2,1,0:T(8,128)(2,1)S(1)} %fusion.61), channel_id=1, source_target_pairs={{0,2},{1,3},{2,0},{3,1},{4,6},{5,7},{6,4},{7,5},{8,10},{9,11},{10,... | collective-permute-start | bytes 294920 | tf_op jit(solution)/shard_map/ppermute | solution.py:16
  89.2 1.8 %collective-permute-start.26 = (bf16[2,96,256]{2,1,0:T(8,128)(2,1)S(1)}, bf16[2,96,256]{2,1,0:T(8,128)(2,1)S(1)}, u32[]{:S(2)}, u32[]{:S(2)}) collective-permute-start(bf16[2,96,256]{2,1,0:T(8,128)(2,1)S(1)} %fusion.60), channel_id=1, source_target_pairs={{0,4},{1,5},{2,6},{3,7},{4,0},{5,1},{6,2},{7,3},{8,12},{9,13},{10,... | collective-permute-start | bytes 294920 | tf_op jit(solution)/shard_map/ppermute | solution.py:16
  91.0 1.2 %collective-permute-done.30 = bf16[2,96,256]{2,1,0:T(8,128)(2,1)S(1)} collective-permute-done((bf16[2,96,256]{2,1,0:T(8,128)(2,1)S(1)}, bf16[2,96,256]{2,1,0:T(8,128)(2,1)S(1)}, u32[]{:S(2)}, u32[]{:S(2)}) %collective-permute-start.30) | collective-permute-done | bytes 98336 | tf_op jit(solution)/shard_map/ppermute | solution.py:16
  92.2 1.8 %collective-permute-start.31 = (bf16[96,256]{1,0:T(8,128)(2,1)S(1)}, bf16[96,256]{1,0:T(8,128)(2,1)S(1)}, u32[]{:S(2)}, u32[]{:S(2)}) collective-permute-start(bf16[96,256]{1,0:T(8,128)(2,1)S(1)} %fusion.65), channel_id=1, source_target_pairs={{0,8},{1,9},{2,10},{3,11},{4,12},{5,13},{6,14},{7,15},{8,0},{9,1},... | collective-permute-start | bytes 147464 | tf_op jit(solution)/shard_map/ppermute | solution.py:16
  94.1 2.6 %collective-permute-start.27 = (bf16[96,256]{1,0:T(8,128)(2,1)S(1)}, bf16[96,256]{1,0:T(8,128)(2,1)S(1)}, u32[]{:S(2)}, u32[]{:S(2)}) collective-permute-start(bf16[96,256]{1,0:T(8,128)(2,1)S(1)} %fusion.64), channel_id=1, source_target_pairs={{0,8},{1,9},{2,10},{3,11},{4,12},{5,13},{6,14},{7,15},{8,0},{9,1},... | collective-permute-start | bytes 147464 | tf_op jit(solution)/shard_map/ppermute | solution.py:16
  96.7 1.0 collective-permute-done.31
  97.8 1.3 %collective-permute-done.27 = bf16[96,256]{1,0:T(8,128)(2,1)S(1)} collective-permute-done((bf16[96,256]{1,0:T(8,128)(2,1)S(1)}, bf16[96,256]{1,0:T(8,128)(2,1)S(1)}, u32[]{:S(2)}, u32[]{:S(2)}) %collective-permute-start.27) | collective-permute-done | bytes 49184 | tf_op jit(solution)/shard_map/ppermute | solution.py:16
  99.3 2.1 %collective-permute-start.33 = (f32[256]{0:T(256)S(1)}, f32[256]{0:T(256)S(1)}, u32[]{:S(2)}, u32[]{:S(2)}) collective-permute-start(f32[256]{0:T(256)S(1)} %add.192), channel_id=1, source_target_pairs={{0,2},{1,3},{2,0},{3,1},{4,6},{5,7},{6,4},{7,5},{8,10},{9,11},{10,... | collective-permute-start | bytes 3080 | tf_op jit(solution)/shard_map/ppermute | solution.py:16
  101.5 0.8 collective-permute-done.34
  102.3 0.7 collective-permute-done.33
  103.0 2.4 %collective-permute-start.37 = (f32[256]{0:T(256)S(1)}, f32[256]{0:T(256)S(1)}, u32[]{:S(2)}, u32[]{:S(2)}) collective-permute-start(f32[256]{0:T(256)S(1)} %add_add_fusion), channel_id=1, source_target_pairs={{0,12},{1,13},{2,14},{3,15},{4,8},{5,9},{6,10},{7,11},{8,4},{9,5},... | collective-permute-start | bytes 3080 | tf_op jit(solution)/shard_map/ppermute | solution.py:16
  105.4 1.2 %collective-permute-start.36 = (f32[256]{0:T(256)S(1)}, f32[256]{0:T(256)S(1)}, u32[]{:S(2)}, u32[]{:S(2)}) collective-permute-start(f32[256]{0:T(256)S(1)} %add_add_fusion), channel_id=1, source_target_pairs={{0,8},{1,9},{2,10},{3,11},{4,12},{5,13},{6,14},{7,15},{8,0},{9,1},... | collective-permute-start | bytes 3080 | tf_op jit(solution)/shard_map/ppermute | solution.py:16
  106.6 0.8 collective-permute-start.35
  107.4 1.0 collective-permute-done.37
  108.4 1.4 %collective-permute-done.36 = f32[256]{0:T(256)S(1)} collective-permute-done((f32[256]{0:T(256)S(1)}, f32[256]{0:T(256)S(1)}, u32[]{:S(2)}, u32[]{:S(2)}) %collective-permute-start.36) | collective-permute-done | bytes 1056 | tf_op jit(solution)/shard_map/ppermute | solution.py:16
  109.9 0.3 collective-permute-done.35
  110.2 0.7 broadcast_multiply_fusion
  (106 shorter events, 4.2 us)
Async XLA Ops:
  0.6 6.9 %collective-permute-start = (bf16[96,256]{1,0:T(8,128)(2,1)}, bf16[96,256]{1,0:T(8,128)(2,1)S(1)}, u32[]{:S(2)}, u32[]{:S(2)}) collective-permute-start(bf16[96,256]{1,0:T(8,128)(2,1)} %param.6), channel_id=1, source_target_pairs={{0,8},{1,9},{2,10},{3,11},{4,12},{5,13},{6,14},{7,15},{8,0},{9,1},... | collective-permute-start | bytes 147464 | tf_op jit(solution)/shard_map/ppermute | solution.py:16
  4.7 5.1 %collective-permute-start.8 = (bf16[96,256]{1,0:T(8,128)(2,1)}, bf16[96,256]{1,0:T(8,128)(2,1)S(1)}, u32[]{:S(2)}, u32[]{:S(2)}) collective-permute-start(bf16[96,256]{1,0:T(8,128)(2,1)} %param.7), channel_id=1, source_target_pairs={{0,2},{1,3},{2,0},{3,1},{4,6},{5,7},{6,4},{7,5},{8,10},{9,11},{10,... | collective-permute-start | bytes 147464 | tf_op jit(solution)/shard_map/ppermute | solution.py:16
  8.4 5.4 %collective-permute-start.1 = (bf16[2,96,256]{2,1,0:T(8,128)(2,1)S(1)}, bf16[2,96,256]{2,1,0:T(8,128)(2,1)S(1)}, u32[]{:S(2)}, u32[]{:S(2)}) collective-permute-start(bf16[2,96,256]{2,1,0:T(8,128)(2,1)S(1)} %pad_maximum_fusion.12), channel_id=1, source_target_pairs={{0,4},{1,5},{2,6},{3,7},{4,0},{5,1},{6,2},{7,3},{8,12},{9,13},{10,... | collective-permute-start | bytes 294920 | tf_op jit(solution)/shard_map/ppermute | solution.py:16
  10.7 6.7 %collective-permute-start.9 = (bf16[2,96,256]{2,1,0:T(8,128)(2,1)S(1)}, bf16[2,96,256]{2,1,0:T(8,128)(2,1)S(1)}, u32[]{:S(2)}, u32[]{:S(2)}) collective-permute-start(bf16[2,96,256]{2,1,0:T(8,128)(2,1)S(1)} %pad_maximum_fusion.13), channel_id=1, source_target_pairs={{0,8},{1,9},{2,10},{3,11},{4,12},{5,13},{6,14},{7,15},{8,0},{9,1},... | collective-permute-start | bytes 294920 | tf_op jit(solution)/shard_map/ppermute | solution.py:16
  13.8 5.7 %collective-permute-start.2 = (bf16[2,2,96,256]{3,2,0,1:T(8,128)(2,1)S(1)}, bf16[2,2,96,256]{3,2,0,1:T(8,128)(2,1)S(1)}, u32[]{:S(2)}, u32[]{:S(2)}) collective-permute-start(bf16[2,2,96,256]{3,2,0,1:T(8,128)(2,1)S(1)} %pad_maximum_fusion.8), channel_id=1, source_target_pairs={{0,2},{1,3},{2,0},{3,1},{4,6},{5,7},{6,4},{7,5},{8,10},{9,11},{10,... | collective-permute-start | bytes 589832 | tf_op jit(solution)/shard_map/ppermute | solution.py:16
  17.4 5.7 %collective-permute-start.10 = (bf16[2,2,96,256]{3,2,1,0:T(8,128)(2,1)S(1)}, bf16[2,2,96,256]{3,2,1,0:T(8,128)(2,1)S(1)}, u32[]{:S(2)}, u32[]{:S(2)}) collective-permute-start(bf16[2,2,96,256]{3,2,1,0:T(8,128)(2,1)S(1)} %pad_maximum_fusion.9), channel_id=1, source_target_pairs={{0,4},{1,5},{2,6},{3,7},{4,0},{5,1},{6,2},{7,3},{8,12},{9,13},{10,... | collective-permute-start | bytes 589832 | tf_op jit(solution)/shard_map/ppermute | solution.py:16
  19.6 3.7 %collective-permute-start.3 = (bf16[2,2,2,96,256]{4,3,2,1,0:T(8,128)(2,1)S(1)}, bf16[2,2,2,96,256]{4,3,2,1,0:T(8,128)(2,1)S(1)}, u32[]{:S(2)}, u32[]{:S(2)}) collective-permute-start(bf16[2,2,2,96,256]{4,3,2,1,0:T(8,128)(2,1)S(1)} %copy.40), channel_id=1, source_target_pairs={{0,1},{1,0},{2,3},{3,2},{4,5},{5,4},{6,7},{7,6},{8,9},{9,8},{10,11... | collective-permute-start | bytes 1179656 | tf_op jit(solution)/shard_map/ppermute | solution.py:16
  23.2 3.6 %collective-permute-start.11 = (bf16[2,2,2,96,256]{4,3,2,0,1:T(8,128)(2,1)S(1)}, bf16[2,2,2,96,256]{4,3,2,0,1:T(8,128)(2,1)S(1)}, u32[]{:S(2)}, u32[]{:S(2)}) collective-permute-start(bf16[2,2,2,96,256]{4,3,2,0,1:T(8,128)(2,1)S(1)} %pad_maximum_fusion.5), channel_id=1, source_target_pairs={{0,1},{1,0},{2,3},{3,2},{4,5},{5,4},{6,7},{7,6},{8,9},{9,8},{10,11... | collective-permute-start | bytes 1179656 | tf_op jit(solution)/shard_map/ppermute | solution.py:16
  30.3 0.7 copy-start
  30.3 0.7 copy-start.1
  30.5 1.9 %collective-permute-start.4 = (bf16[2,2,2,96,256]{4,3,0,1,2:T(8,128)(2,1)S(1)}, bf16[2,2,2,96,256]{4,3,0,1,2:T(8,128)(2,1)S(1)}, u32[]{:S(2)}, u32[]{:S(2)}) collective-permute-start(bf16[2,2,2,96,256]{4,3,0,1,2:T(8,128)(2,1)S(1)} %bitcast.256), channel_id=1, source_target_pairs={{0,1},{1,0},{2,3},{3,2},{4,5},{5,4},{6,7},{7,6},{8,9},{9,8},{10,11... | collective-permute-start | bytes 1179656 | tf_op jit(solution)/shard_map/ppermute | solution.py:16
  31.1 3.0 %collective-permute-start.12 = (bf16[2,2,2,96,256]{4,3,0,2,1:T(8,128)(2,1)S(1)}, bf16[2,2,2,96,256]{4,3,0,2,1:T(8,128)(2,1)S(1)}, u32[]{:S(2)}, u32[]{:S(2)}) collective-permute-start(bf16[2,2,2,96,256]{4,3,0,2,1:T(8,128)(2,1)S(1)} %bitcast.255), channel_id=1, source_target_pairs={{0,1},{1,0},{2,3},{3,2},{4,5},{5,4},{6,7},{7,6},{8,9},{9,8},{10,11... | collective-permute-start | bytes 1179656 | tf_op jit(solution)/shard_map/ppermute | solution.py:16
  32.5 7.2 %collective-permute-start.5 = (bf16[2,2,96,256]{3,2,0,1:T(8,128)(2,1)S(1)}, bf16[2,2,96,256]{3,2,0,1:T(8,128)(2,1)S(1)}, u32[]{:S(2)}, u32[]{:S(2)}) collective-permute-start(bf16[2,2,96,256]{3,2,0,1:T(8,128)(2,1)S(1)} %fusion.54), channel_id=1, source_target_pairs={{0,2},{1,3},{2,0},{3,1},{4,6},{5,7},{6,4},{7,5},{8,10},{9,11},{10,... | collective-permute-start | bytes 589832 | tf_op jit(solution)/shard_map/ppermute | solution.py:16
  34.2 7.0 %collective-permute-start.13 = (bf16[2,2,96,256]{3,2,0,1:T(8,128)(2,1)S(1)}, bf16[2,2,96,256]{3,2,0,1:T(8,128)(2,1)S(1)}, u32[]{:S(2)}, u32[]{:S(2)}) collective-permute-start(bf16[2,2,96,256]{3,2,0,1:T(8,128)(2,1)S(1)} %fusion.55), channel_id=1, source_target_pairs={{0,4},{1,5},{2,6},{3,7},{4,0},{5,1},{6,2},{7,3},{8,12},{9,13},{10,... | collective-permute-start | bytes 589832 | tf_op jit(solution)/shard_map/ppermute | solution.py:16
  39.8 4.7 %collective-permute-start.6 = (bf16[2,96,256]{2,1,0:T(8,128)(2,1)S(1)}, bf16[2,96,256]{2,1,0:T(8,128)(2,1)S(1)}, u32[]{:S(2)}, u32[]{:S(2)}) collective-permute-start(bf16[2,96,256]{2,1,0:T(8,128)(2,1)S(1)} %fusion.58), channel_id=1, source_target_pairs={{0,4},{1,5},{2,6},{3,7},{4,0},{5,1},{6,2},{7,3},{8,12},{9,13},{10,... | collective-permute-start | bytes 294920 | tf_op jit(solution)/shard_map/ppermute | solution.py:16
  41.3 6.1 %collective-permute-start.14 = (bf16[2,96,256]{2,1,0:T(8,128)(2,1)S(1)}, bf16[2,96,256]{2,1,0:T(8,128)(2,1)S(1)}, u32[]{:S(2)}, u32[]{:S(2)}) collective-permute-start(bf16[2,96,256]{2,1,0:T(8,128)(2,1)S(1)} %fusion.59), channel_id=1, source_target_pairs={{0,2},{1,3},{2,0},{3,1},{4,6},{5,7},{6,4},{7,5},{8,10},{9,11},{10,... | collective-permute-start | bytes 294920 | tf_op jit(solution)/shard_map/ppermute | solution.py:16
  44.6 6.1 %collective-permute-start.7 = (bf16[96,256]{1,0:T(8,128)(2,1)S(1)}, bf16[96,256]{1,0:T(8,128)(2,1)S(1)}, u32[]{:S(2)}, u32[]{:S(2)}) collective-permute-start(bf16[96,256]{1,0:T(8,128)(2,1)S(1)} %fusion.62), channel_id=1, source_target_pairs={{0,8},{1,9},{2,10},{3,11},{4,12},{5,13},{6,14},{7,15},{8,0},{9,1},... | collective-permute-start | bytes 147464 | tf_op jit(solution)/shard_map/ppermute | solution.py:16
  47.4 5.1 %collective-permute-start.15 = (bf16[96,256]{1,0:T(8,128)(2,1)S(1)}, bf16[96,256]{1,0:T(8,128)(2,1)S(1)}, u32[]{:S(2)}, u32[]{:S(2)}) collective-permute-start(bf16[96,256]{1,0:T(8,128)(2,1)S(1)} %fusion.63), channel_id=1, source_target_pairs={{0,8},{1,9},{2,10},{3,11},{4,12},{5,13},{6,14},{7,15},{8,0},{9,1},... | collective-permute-start | bytes 147464 | tf_op jit(solution)/shard_map/ppermute | solution.py:16
  52.5 5.1 %collective-permute-start.16 = (bf16[96,256]{1,0:T(8,128)(2,1)S(1)}, bf16[96,256]{1,0:T(8,128)(2,1)S(1)}, u32[]{:S(2)}, u32[]{:S(2)}) collective-permute-start(bf16[96,256]{1,0:T(8,128)(2,1)S(1)} %get-tuple-element.22), channel_id=1, source_target_pairs={{0,8},{1,9},{2,10},{3,11},{4,12},{5,13},{6,14},{7,15},{8,0},{9,1},... | collective-permute-start | bytes 147464 | tf_op jit(solution)/shard_map/ppermute | solution.py:16
  53.7 4.1 %collective-permute-start.20 = (bf16[96,256]{1,0:T(8,128)(2,1)S(1)}, bf16[96,256]{1,0:T(8,128)(2,1)S(1)}, u32[]{:S(2)}, u32[]{:S(2)}) collective-permute-start(bf16[96,256]{1,0:T(8,128)(2,1)S(1)} %get-tuple-element.23), channel_id=1, source_target_pairs={{0,2},{1,3},{2,0},{3,1},{4,6},{5,7},{6,4},{7,5},{8,10},{9,11},{10,... | collective-permute-start | bytes 147464 | tf_op jit(solution)/shard_map/ppermute | solution.py:16
  57.6 4.7 %collective-permute-start.17 = (bf16[2,96,256]{2,1,0:T(8,128)(2,1)S(1)}, bf16[2,96,256]{2,1,0:T(8,128)(2,1)S(1)}, u32[]{:S(2)}, u32[]{:S(2)}) collective-permute-start(bf16[2,96,256]{2,1,0:T(8,128)(2,1)S(1)} %pad_maximum_fusion.14), channel_id=1, source_target_pairs={{0,4},{1,5},{2,6},{3,7},{4,0},{5,1},{6,2},{7,3},{8,12},{9,13},{10,... | collective-permute-start | bytes 294920 | tf_op jit(solution)/shard_map/ppermute | solution.py:16
  57.8 6.1 %collective-permute-start.21 = (bf16[2,96,256]{2,1,0:T(8,128)(2,1)S(1)}, bf16[2,96,256]{2,1,0:T(8,128)(2,1)S(1)}, u32[]{:S(2)}, u32[]{:S(2)}) collective-permute-start(bf16[2,96,256]{2,1,0:T(8,128)(2,1)S(1)} %pad_maximum_fusion.15), channel_id=1, source_target_pairs={{0,8},{1,9},{2,10},{3,11},{4,12},{5,13},{6,14},{7,15},{8,0},{9,1},... | collective-permute-start | bytes 294920 | tf_op jit(solution)/shard_map/ppermute | solution.py:16
  62.4 5.7 %collective-permute-start.18 = (bf16[2,2,96,256]{3,2,0,1:T(8,128)(2,1)S(1)}, bf16[2,2,96,256]{3,2,0,1:T(8,128)(2,1)S(1)}, u32[]{:S(2)}, u32[]{:S(2)}) collective-permute-start(bf16[2,2,96,256]{3,2,0,1:T(8,128)(2,1)S(1)} %pad_maximum_fusion.10), channel_id=1, source_target_pairs={{0,2},{1,3},{2,0},{3,1},{4,6},{5,7},{6,4},{7,5},{8,10},{9,11},{10,... | collective-permute-start | bytes 589832 | tf_op jit(solution)/shard_map/ppermute | solution.py:16
  64.0 6.1 %collective-permute-start.22 = (bf16[2,2,96,256]{3,2,1,0:T(8,128)(2,1)S(1)}, bf16[2,2,96,256]{3,2,1,0:T(8,128)(2,1)S(1)}, u32[]{:S(2)}, u32[]{:S(2)}) collective-permute-start(bf16[2,2,96,256]{3,2,1,0:T(8,128)(2,1)S(1)} %pad_maximum_fusion.11), channel_id=1, source_target_pairs={{0,4},{1,5},{2,6},{3,7},{4,0},{5,1},{6,2},{7,3},{8,12},{9,13},{10,... | collective-permute-start | bytes 589832 | tf_op jit(solution)/shard_map/ppermute | solution.py:16
  68.2 2.1 %collective-permute-start.19 = (bf16[2,2,2,96,256]{4,3,0,1,2:T(8,128)(2,1)S(1)}, bf16[2,2,2,96,256]{4,3,0,1,2:T(8,128)(2,1)S(1)}, u32[]{:S(2)}, u32[]{:S(2)}) collective-permute-start(bf16[2,2,2,96,256]{4,3,0,1,2:T(8,128)(2,1)S(1)} %pad_maximum_fusion.6), channel_id=1, source_target_pairs={{0,1},{1,0},{2,3},{3,2},{4,5},{5,4},{6,7},{7,6},{8,9},{9,8},{10,11... | collective-permute-start | bytes 1179656 | tf_op jit(solution)/shard_map/ppermute | solution.py:16
  70.2 1.8 %collective-permute-start.23 = (bf16[2,2,2,96,256]{4,3,2,1,0:T(8,128)(2,1)S(1)}, bf16[2,2,2,96,256]{4,3,2,1,0:T(8,128)(2,1)S(1)}, u32[]{:S(2)}, u32[]{:S(2)}) collective-permute-start(bf16[2,2,2,96,256]{4,3,2,1,0:T(8,128)(2,1)S(1)} %pad_maximum_fusion.7), channel_id=1, source_target_pairs={{0,1},{1,0},{2,3},{3,2},{4,5},{5,4},{6,7},{7,6},{8,9},{9,8},{10,11... | collective-permute-start | bytes 1179656 | tf_op jit(solution)/shard_map/ppermute | solution.py:16
  72.5 3.3 %copy-start.2 = (f32[256]{0:T(256)}, f32[256]{0:T(256)S(1)}, u32[]{:S(2)}) copy-start(f32[256]{0:T(256)S(1)} %add_rsqrt_fusion.1) | copy-start | bytes 3076
  75.9 4.1 %collective-permute-start.28 = (bf16[2,2,2,96,256]{4,3,0,2,1:T(8,128)(2,1)S(1)}, bf16[2,2,2,96,256]{4,3,0,2,1:T(8,128)(2,1)S(1)}, u32[]{:S(2)}, u32[]{:S(2)}) collective-permute-start(bf16[2,2,2,96,256]{4,3,0,2,1:T(8,128)(2,1)S(1)} %bitcast.257), channel_id=1, source_target_pairs={{0,1},{1,0},{2,3},{3,2},{4,5},{5,4},{6,7},{7,6},{8,9},{9,8},{10,11... | collective-permute-start | bytes 1179656 | tf_op jit(solution)/shard_map/ppermute | solution.py:16
  79.4 2.8 %collective-permute-start.24 = (bf16[2,2,2,96,256]{4,3,2,1,0:T(8,128)(2,1)S(1)}, bf16[2,2,2,96,256]{4,3,2,1,0:T(8,128)(2,1)S(1)}, u32[]{:S(2)}, u32[]{:S(2)}) collective-permute-start(bf16[2,2,2,96,256]{4,3,2,1,0:T(8,128)(2,1)S(1)} %dynamic-slice_bitcast_fusion), channel_id=1, source_target_pairs={{0,1},{1,0},{2,3},{3,2},{4,5},{5,4},{6,7},{7,6},{8,9},{9,8},{10,11... | collective-permute-start | bytes 1179656 | tf_op jit(solution)/shard_map/ppermute | solution.py:16
  80.1 7.3 %collective-permute-start.29 = (bf16[2,2,96,256]{3,2,0,1:T(8,128)(2,1)S(1)}, bf16[2,2,96,256]{3,2,0,1:T(8,128)(2,1)S(1)}, u32[]{:S(2)}, u32[]{:S(2)}) collective-permute-start(bf16[2,2,96,256]{3,2,0,1:T(8,128)(2,1)S(1)} %fusion.57), channel_id=1, source_target_pairs={{0,4},{1,5},{2,6},{3,7},{4,0},{5,1},{6,2},{7,3},{8,12},{9,13},{10,... | collective-permute-start | bytes 589832 | tf_op jit(solution)/shard_map/ppermute | solution.py:16
  82.3 6.8 %collective-permute-start.25 = (bf16[2,2,96,256]{3,2,1,0:T(8,128)(2,1)S(1)}, bf16[2,2,96,256]{3,2,1,0:T(8,128)(2,1)S(1)}, u32[]{:S(2)}, u32[]{:S(2)}) collective-permute-start(bf16[2,2,96,256]{3,2,1,0:T(8,128)(2,1)S(1)} %fusion.56), channel_id=1, source_target_pairs={{0,2},{1,3},{2,0},{3,1},{4,6},{5,7},{6,4},{7,5},{8,10},{9,11},{10,... | collective-permute-start | bytes 589832 | tf_op jit(solution)/shard_map/ppermute | solution.py:16
  87.5 4.7 %collective-permute-start.30 = (bf16[2,96,256]{2,1,0:T(8,128)(2,1)S(1)}, bf16[2,96,256]{2,1,0:T(8,128)(2,1)S(1)}, u32[]{:S(2)}, u32[]{:S(2)}) collective-permute-start(bf16[2,96,256]{2,1,0:T(8,128)(2,1)S(1)} %fusion.61), channel_id=1, source_target_pairs={{0,2},{1,3},{2,0},{3,1},{4,6},{5,7},{6,4},{7,5},{8,10},{9,11},{10,... | collective-permute-start | bytes 294920 | tf_op jit(solution)/shard_map/ppermute | solution.py:16
  89.2 4.8 %collective-permute-start.26 = (bf16[2,96,256]{2,1,0:T(8,128)(2,1)S(1)}, bf16[2,96,256]{2,1,0:T(8,128)(2,1)S(1)}, u32[]{:S(2)}, u32[]{:S(2)}) collective-permute-start(bf16[2,96,256]{2,1,0:T(8,128)(2,1)S(1)} %fusion.60), channel_id=1, source_target_pairs={{0,4},{1,5},{2,6},{3,7},{4,0},{5,1},{6,2},{7,3},{8,12},{9,13},{10,... | collective-permute-start | bytes 294920 | tf_op jit(solution)/shard_map/ppermute | solution.py:16
  92.2 5.6 %collective-permute-start.31 = (bf16[96,256]{1,0:T(8,128)(2,1)S(1)}, bf16[96,256]{1,0:T(8,128)(2,1)S(1)}, u32[]{:S(2)}, u32[]{:S(2)}) collective-permute-start(bf16[96,256]{1,0:T(8,128)(2,1)S(1)} %fusion.65), channel_id=1, source_target_pairs={{0,8},{1,9},{2,10},{3,11},{4,12},{5,13},{6,14},{7,15},{8,0},{9,1},... | collective-permute-start | bytes 147464 | tf_op jit(solution)/shard_map/ppermute | solution.py:16
  94.1 5.1 %collective-permute-start.27 = (bf16[96,256]{1,0:T(8,128)(2,1)S(1)}, bf16[96,256]{1,0:T(8,128)(2,1)S(1)}, u32[]{:S(2)}, u32[]{:S(2)}) collective-permute-start(bf16[96,256]{1,0:T(8,128)(2,1)S(1)} %fusion.64), channel_id=1, source_target_pairs={{0,8},{1,9},{2,10},{3,11},{4,12},{5,13},{6,14},{7,15},{8,0},{9,1},... | collective-permute-start | bytes 147464 | tf_op jit(solution)/shard_map/ppermute | solution.py:16
  99.3 3.1 %collective-permute-start.34 = (f32[256]{0:T(256)S(1)}, f32[256]{0:T(256)S(1)}, u32[]{:S(2)}, u32[]{:S(2)}) collective-permute-start(f32[256]{0:T(256)S(1)} %add.192), channel_id=1, source_target_pairs={{0,3},{1,2},{2,1},{3,0},{4,7},{5,6},{6,5},{7,4},{8,11},{9,10},{10,... | collective-permute-start | bytes 3080 | tf_op jit(solution)/shard_map/ppermute | solution.py:16
  99.3 3.6 %collective-permute-start.33 = (f32[256]{0:T(256)S(1)}, f32[256]{0:T(256)S(1)}, u32[]{:S(2)}, u32[]{:S(2)}) collective-permute-start(f32[256]{0:T(256)S(1)} %add.192), channel_id=1, source_target_pairs={{0,2},{1,3},{2,0},{3,1},{4,6},{5,7},{6,4},{7,5},{8,10},{9,11},{10,... | collective-permute-start | bytes 3080 | tf_op jit(solution)/shard_map/ppermute | solution.py:16
  101.4 1.6 %collective-permute-start.32 = (f32[256]{0:T(256)S(1)}, f32[256]{0:T(256)S(1)}, u32[]{:S(2)}, u32[]{:S(2)}) collective-permute-start(f32[256]{0:T(256)S(1)} %add.192), channel_id=1, source_target_pairs={{0,1},{1,0},{2,3},{3,2},{4,5},{5,4},{6,7},{7,6},{8,9},{9,8},{10,11... | collective-permute-start | bytes 3080 | tf_op jit(solution)/shard_map/ppermute | solution.py:16
  103.0 5.4 %collective-permute-start.37 = (f32[256]{0:T(256)S(1)}, f32[256]{0:T(256)S(1)}, u32[]{:S(2)}, u32[]{:S(2)}) collective-permute-start(f32[256]{0:T(256)S(1)} %add_add_fusion), channel_id=1, source_target_pairs={{0,12},{1,13},{2,14},{3,15},{4,8},{5,9},{6,10},{7,11},{8,4},{9,5},... | collective-permute-start | bytes 3080 | tf_op jit(solution)/shard_map/ppermute | solution.py:16
  105.4 4.5 %collective-permute-start.36 = (f32[256]{0:T(256)S(1)}, f32[256]{0:T(256)S(1)}, u32[]{:S(2)}, u32[]{:S(2)}) collective-permute-start(f32[256]{0:T(256)S(1)} %add_add_fusion), channel_id=1, source_target_pairs={{0,8},{1,9},{2,10},{3,11},{4,12},{5,13},{6,14},{7,15},{8,0},{9,1},... | collective-permute-start | bytes 3080 | tf_op jit(solution)/shard_map/ppermute | solution.py:16
  106.6 3.6 %collective-permute-start.35 = (f32[256]{0:T(256)S(1)}, f32[256]{0:T(256)S(1)}, u32[]{:S(2)}, u32[]{:S(2)}) collective-permute-start(f32[256]{0:T(256)S(1)} %add_add_fusion), channel_id=1, source_target_pairs={{0,4},{1,5},{2,6},{3,7},{4,0},{5,1},{6,2},{7,3},{8,12},{9,13},{10,... | collective-permute-start | bytes 3080 | tf_op jit(solution)/shard_map/ppermute | solution.py:16

commit v17 on v14

--- a/solution.py
+++ b/solution.py
@@ -82,13 +82,14 @@
         halves = []
         for gathered in (amp_full, der_full):
             projected = jnp.dot(panels[sector], gathered, preferred_element_type=jnp.float32)
-            if scale is not None:
-                projected = projected * scale[None, :]
             halves.append(
                 contract_rows(panels[sector + 1], projected.astype(jnp.bfloat16)).astype(jnp.bfloat16)
             )
         rot_amp = halving_reduce_scatter(halves[0], devices, order_amp)
         rot_der = halving_reduce_scatter(halves[1], devices, order_der)
+        if scale is not None:
+            rot_amp = rot_amp * scale[None, :]
+            rot_der = rot_der * scale[None, :]
         angle_rows = lax.dynamic_slice_in_dim(phase[sector], first_row, chan_rows, 0)
         wave_rows = lax.dynamic_slice_in_dim(wavenum[sector], first_row, chan_rows, 0)
         cosine = jnp.cos(angle_rows)[:, None]

time: 111 us -> 115 us (1.036)
  starting transfers between devices: 37 us -> 39.7 us
  waiting for transfers between devices: 53.1 us -> 50.9 us
  local copies, waits for them, and re-layouts: 2.09 us -> 3.96 us
    ppermute x38, starting transfers between devices: 37 us -> 39.7 us  [exchange(): return lax.ppermute(x, 'row', [(i, i ^ distance) for i in range(devices)])]
    ppermute x38, waiting for transfers between devices: 53.1 us -> 50.9 us  [exchange(): return lax.ppermute(x, 'row', [(i, i ^ distance) for i in range(devices)])]
  transfers between devices with their start and end apart: 38 -> 38, of which waited for: 30 -> 26; matrix products, arithmetic and copies ran while one was open for 10% -> 16% of each run, Pallas kernels for 0% -> 0%
where the time goes in v17:
time: 115 us
  waiting for transfers between devices  50.9 us (44%)
  starting transfers between devices  39.7 us (35%)
  matrix products  12.8 us (11%)
  other arithmetic  5.97 us (5%)
  local copies, waits for them, and re-layouts  3.96 us (3%)
  between operations  1.27 us (1%)
    ppermute x38, waiting for transfers between devices, exchange(): return lax.ppermute(x, 'row', [(i, i ^ distance) for i in range(devices)])  50.9 us
    ppermute x38, starting transfers between devices, exchange(): return lax.ppermute(x, 'row', [(i, i ^ distance) for i in range(devices)])  39.7 us
    dot_general x4, matrix products, contract_rows(): lax.dot_general(left, right, (((0,), (0,)), ((), ())), preferred_element_...  12.8 us
    another operation x32, other arithmetic, doubling_all_gather(): jnp.stack([jnp.where(low, cur, other), jnp.where(low, other, cur)], axis=...  2.77 us
  transfers between devices with their start and end apart: 38, of which 26 were waited for; matrix products, arithmetic and copies ran while one was open for 16% of the time, Pallas kernels for 0%

profile of v17, /device:TPU:0, one launch (start us, length us, event | category | flops | bytes accessed | tf_op | source)
XLA Modules:
  0.0 114.6 jit_solution(3341079319887563246)
XLA Ops:
  0.6 4.1 %collective-permute-start = (bf16[96,256]{1,0:T(8,128)(2,1)}, bf16[96,256]{1,0:T(8,128)(2,1)S(1)}, u32[]{:S(2)}, u32[]{:S(2)}) collective-permute-start(bf16[96,256]{1,0:T(8,128)(2,1)} %param.6), channel_id=1, source_target_pairs={{0,8},{1,9},{2,10},{3,11},{4,12},{5,13},{6,14},{7,15},{8,0},{9,1},... | collective-permute-start | bytes 147464 | tf_op jit(solution)/shard_map/ppermute | solution.py:16
  4.8 2.7 %collective-permute-done = bf16[96,256]{1,0:T(8,128)(2,1)S(1)} collective-permute-done((bf16[96,256]{1,0:T(8,128)(2,1)}, bf16[96,256]{1,0:T(8,128)(2,1)S(1)}, u32[]{:S(2)}, u32[]{:S(2)}) %collective-permute-start) | collective-permute-done | bytes 49184 | tf_op jit(solution)/shard_map/ppermute | solution.py:16
  7.5 0.8 select_bitcast_fusion.31
  8.4 2.2 %collective-permute-start.1 = (bf16[2,96,256]{2,1,0:T(8,128)(2,1)S(1)}, bf16[2,96,256]{2,1,0:T(8,128)(2,1)S(1)}, u32[]{:S(2)}, u32[]{:S(2)}) collective-permute-start(bf16[2,96,256]{2,1,0:T(8,128)(2,1)S(1)} %pad_maximum_fusion.12), channel_id=1, source_target_pairs={{0,4},{1,5},{2,6},{3,7},{4,0},{5,1},{6,2},{7,3},{8,12},{9,13},{10,... | collective-permute-start | bytes 294920 | tf_op jit(solution)/shard_map/ppermute | solution.py:16
  10.6 0.8 select_bitcast_fusion.29
  11.4 1.6 %collective-permute-start.9 = (bf16[2,96,256]{2,1,0:T(8,128)(2,1)S(1)}, bf16[2,96,256]{2,1,0:T(8,128)(2,1)S(1)}, u32[]{:S(2)}, u32[]{:S(2)}) collective-permute-start(bf16[2,96,256]{2,1,0:T(8,128)(2,1)S(1)} %pad_maximum_fusion.13), channel_id=1, source_target_pairs={{0,2},{1,3},{2,0},{3,1},{4,6},{5,7},{6,4},{7,5},{8,10},{9,11},{10,... | collective-permute-start | bytes 294920 | tf_op jit(solution)/shard_map/ppermute | solution.py:16
  13.0 0.5 collective-permute-done.1
  13.5 1.6 %collective-permute-start.2 = (bf16[2,2,96,256]{3,2,0,1:T(8,128)(2,1)S(1)}, bf16[2,2,96,256]{3,2,0,1:T(8,128)(2,1)S(1)}, u32[]{:S(2)}, u32[]{:S(2)}) collective-permute-start(bf16[2,2,96,256]{3,2,0,1:T(8,128)(2,1)S(1)} %pad_maximum_fusion.8), channel_id=1, source_target_pairs={{0,2},{1,3},{2,0},{3,1},{4,6},{5,7},{6,4},{7,5},{8,10},{9,11},{10,... | collective-permute-start | bytes 589832 | tf_op jit(solution)/shard_map/ppermute | solution.py:16
  15.1 1.6 %collective-permute-done.9 = bf16[2,96,256]{2,1,0:T(8,128)(2,1)S(1)} collective-permute-done((bf16[2,96,256]{2,1,0:T(8,128)(2,1)S(1)}, bf16[2,96,256]{2,1,0:T(8,128)(2,1)S(1)}, u32[]{:S(2)}, u32[]{:S(2)}) %collective-permute-start.9) | collective-permute-done | bytes 98336 | tf_op jit(solution)/shard_map/ppermute | solution.py:16
  16.8 0.7 collective-permute-start.10
  17.5 2.8 %collective-permute-done.2 = bf16[2,2,96,256]{3,2,0,1:T(8,128)(2,1)S(1)} collective-permute-done((bf16[2,2,96,256]{3,2,0,1:T(8,128)(2,1)S(1)}, bf16[2,2,96,256]{3,2,0,1:T(8,128)(2,1)S(1)}, u32[]{:S(2)}, u32[]{:S(2)}) %collective-permute-start.2) | collective-permute-done | bytes 196640 | tf_op jit(solution)/shard_map/ppermute | solution.py:16
  20.5 2.0 %collective-permute-done.10 = bf16[2,2,96,256]{3,2,1,0:T(8,128)(2,1)S(1)} collective-permute-done((bf16[2,2,96,256]{3,2,1,0:T(8,128)(2,1)S(1)}, bf16[2,2,96,256]{3,2,1,0:T(8,128)(2,1)S(1)}, u32[]{:S(2)}, u32[]{:S(2)}) %collective-permute-start.10) | collective-permute-done | bytes 196640 | tf_op jit(solution)/shard_map/ppermute | solution.py:16
  23.0 3.0 %fusion = bf16[1536,256]{0,1:T(8,128)(2,1)S(1)} fusion(bf16[1536,256]{1,0:T(8,128)(2,1)S(1)} %bitcast.257, bf16[3,512,1536]{2,1,0:T(8,128)(2,1)} %param.5), kind=kOutput, calls=%fused_computation.4 | convolution fusion | flops 805830656 | bytes 4718592 | tf_op jit(solution)/shard_map/dot_general | solution.py:10
  26.4 3.0 %fusion.1 = bf16[1536,256]{0,1:T(8,128)(2,1)S(1)} fusion(bf16[1536,256]{1,0:T(8,128)(2,1)S(1)} %bitcast.258, bf16[3,512,1536]{2,1,0:T(8,128)(2,1)} %param.5), kind=kOutput, calls=%fused_computation.5 | convolution fusion | flops 805830656 | bytes 4718592 | tf_op jit(solution)/shard_map/dot_general | solution.py:10
  29.9 0.5 collective-permute-start.12
  30.5 0.5 collective-permute-start.4
  31.1 0.6 collective-permute-done.12
  31.9 0.7 collective-permute-start.13
  32.7 1.6 %collective-permute-start.5 = (bf16[2,2,96,256]{3,2,0,1:T(8,128)(2,1)S(1)}, bf16[2,2,96,256]{3,2,0,1:T(8,128)(2,1)S(1)}, u32[]{:S(2)}, u32[]{:S(2)}) collective-permute-start(bf16[2,2,96,256]{3,2,0,1:T(8,128)(2,1)S(1)} %fusion.46), channel_id=1, source_target_pairs={{0,2},{1,3},{2,0},{3,1},{4,6},{5,7},{6,4},{7,5},{8,10},{9,11},{10,... | collective-permute-start | bytes 589832 | tf_op jit(solution)/shard_map/ppermute | solution.py:16
  34.3 4.8 %collective-permute-done.13 = bf16[2,2,96,256]{3,2,0,1:T(8,128)(2,1)S(1)} collective-permute-done((bf16[2,2,96,256]{3,2,0,1:T(8,128)(2,1)S(1)}, bf16[2,2,96,256]{3,2,0,1:T(8,128)(2,1)S(1)}, u32[]{:S(2)}, u32[]{:S(2)}) %collective-permute-start.13) | collective-permute-done | bytes 196640 | tf_op jit(solution)/shard_map/ppermute | solution.py:16
  39.2 1.7 %collective-permute-start.14 = (bf16[2,96,256]{2,1,0:T(8,128)(2,1)S(1)}, bf16[2,96,256]{2,1,0:T(8,128)(2,1)S(1)}, u32[]{:S(2)}, u32[]{:S(2)}) collective-permute-start(bf16[2,96,256]{2,1,0:T(8,128)(2,1)S(1)} %fusion.51), channel_id=1, source_target_pairs={{0,2},{1,3},{2,0},{3,1},{4,6},{5,7},{6,4},{7,5},{8,10},{9,11},{10,... | collective-permute-start | bytes 294920 | tf_op jit(solution)/shard_map/ppermute | solution.py:16
  40.9 0.6 collective-permute-start.6
  41.6 2.3 %collective-permute-done.14 = bf16[2,96,256]{2,1,0:T(8,128)(2,1)S(1)} collective-permute-done((bf16[2,96,256]{2,1,0:T(8,128)(2,1)S(1)}, bf16[2,96,256]{2,1,0:T(8,128)(2,1)S(1)}, u32[]{:S(2)}, u32[]{:S(2)}) %collective-permute-start.14) | collective-permute-done | bytes 98336 | tf_op jit(solution)/shard_map/ppermute | solution.py:16
  43.9 3.3 %collective-permute-start.15 = (bf16[96,256]{1,0:T(8,128)(2,1)S(1)}, bf16[96,256]{1,0:T(8,128)(2,1)S(1)}, u32[]{:S(2)}, u32[]{:S(2)}) collective-permute-start(bf16[96,256]{1,0:T(8,128)(2,1)S(1)} %fusion.57), channel_id=1, source_target_pairs={{0,8},{1,9},{2,10},{3,11},{4,12},{5,13},{6,14},{7,15},{8,0},{9,1},... | collective-permute-start | bytes 147464 | tf_op jit(solution)/shard_map/ppermute | solution.py:16
  47.3 1.6 %collective-permute-start.7 = (bf16[96,256]{1,0:T(8,128)(2,1)S(1)}, bf16[96,256]{1,0:T(8,128)(2,1)S(1)}, u32[]{:S(2)}, u32[]{:S(2)}) collective-permute-start(bf16[96,256]{1,0:T(8,128)(2,1)S(1)} %fusion.56), channel_id=1, source_target_pairs={{0,8},{1,9},{2,10},{3,11},{4,12},{5,13},{6,14},{7,15},{8,0},{9,1},... | collective-permute-start | bytes 147464 | tf_op jit(solution)/shard_map/ppermute | solution.py:16
  49.0 1.6 %collective-permute-done.15 = bf16[96,256]{1,0:T(8,128)(2,1)S(1)} collective-permute-done((bf16[96,256]{1,0:T(8,128)(2,1)S(1)}, bf16[96,256]{1,0:T(8,128)(2,1)S(1)}, u32[]{:S(2)}, u32[]{:S(2)}) %collective-permute-start.15) | collective-permute-done | bytes 49184 | tf_op jit(solution)/shard_map/ppermute | solution.py:16
  50.6 2.0 %collective-permute-done.7 = bf16[96,256]{1,0:T(8,128)(2,1)S(1)} collective-permute-done((bf16[96,256]{1,0:T(8,128)(2,1)S(1)}, bf16[96,256]{1,0:T(8,128)(2,1)S(1)}, u32[]{:S(2)}, u32[]{:S(2)}) %collective-permute-start.7) | collective-permute-done | bytes 49184 | tf_op jit(solution)/shard_map/ppermute | solution.py:16
  52.7 1.4 %collective-permute-start.16 = (bf16[96,256]{1,0:T(8,128)(2,1)S(1)}, bf16[96,256]{1,0:T(8,128)(2,1)S(1)}, u32[]{:S(2)}, u32[]{:S(2)}) collective-permute-start(bf16[96,256]{1,0:T(8,128)(2,1)S(1)} %get-tuple-element.22), channel_id=1, source_target_pairs={{0,8},{1,9},{2,10},{3,11},{4,12},{5,13},{6,14},{7,15},{8,0},{9,1},... | collective-permute-start | bytes 147464 | tf_op jit(solution)/shard_map/ppermute | solution.py:16
  54.2 1.7 %collective-permute-start.24 = (bf16[96,256]{1,0:T(8,128)(2,1)S(1)}, bf16[96,256]{1,0:T(8,128)(2,1)S(1)}, u32[]{:S(2)}, u32[]{:S(2)}) collective-permute-start(bf16[96,256]{1,0:T(8,128)(2,1)S(1)} %get-tuple-element.23), channel_id=1, source_target_pairs={{0,8},{1,9},{2,10},{3,11},{4,12},{5,13},{6,14},{7,15},{8,0},{9,1},... | collective-permute-start | bytes 147464 | tf_op jit(solution)/shard_map/ppermute | solution.py:16
  55.9 1.9 %collective-permute-done.16 = bf16[96,256]{1,0:T(8,128)(2,1)S(1)} collective-permute-done((bf16[96,256]{1,0:T(8,128)(2,1)S(1)}, bf16[96,256]{1,0:T(8,128)(2,1)S(1)}, u32[]{:S(2)}, u32[]{:S(2)}) %collective-permute-start.16) | collective-permute-done | bytes 49184 | tf_op jit(solution)/shard_map/ppermute | solution.py:16
  58.0 1.6 %collective-permute-done.24 = bf16[96,256]{1,0:T(8,128)(2,1)S(1)} collective-permute-done((bf16[96,256]{1,0:T(8,128)(2,1)S(1)}, bf16[96,256]{1,0:T(8,128)(2,1)S(1)}, u32[]{:S(2)}, u32[]{:S(2)}) %collective-permute-start.24) | collective-permute-done | bytes 49184 | tf_op jit(solution)/shard_map/ppermute | solution.py:16
  59.6 1.4 %collective-permute-start.25 = (bf16[2,96,256]{2,1,0:T(8,128)(2,1)S(1)}, bf16[2,96,256]{2,1,0:T(8,128)(2,1)S(1)}, u32[]{:S(2)}, u32[]{:S(2)}) collective-permute-start(bf16[2,96,256]{2,1,0:T(8,128)(2,1)S(1)} %pad_maximum_fusion.15), channel_id=1, source_target_pairs={{0,2},{1,3},{2,0},{3,1},{4,6},{5,7},{6,4},{7,5},{8,10},{9,11},{10,... | collective-permute-start | bytes 294920 | tf_op jit(solution)/shard_map/ppermute | solution.py:16
  61.0 1.5 %collective-permute-done.17 = bf16[2,96,256]{2,1,0:T(8,128)(2,1)S(1)} collective-permute-done((bf16[2,96,256]{2,1,0:T(8,128)(2,1)S(1)}, bf16[2,96,256]{2,1,0:T(8,128)(2,1)S(1)}, u32[]{:S(2)}, u32[]{:S(2)}) %collective-permute-start.17) | collective-permute-done | bytes 98336 | tf_op jit(solution)/shard_map/ppermute | solution.py:16
  62.6 2.0 %collective-permute-start.18 = (bf16[2,2,96,256]{3,2,0,1:T(8,128)(2,1)S(1)}, bf16[2,2,96,256]{3,2,0,1:T(8,128)(2,1)S(1)}, u32[]{:S(2)}, u32[]{:S(2)}) collective-permute-start(bf16[2,2,96,256]{3,2,0,1:T(8,128)(2,1)S(1)} %pad_maximum_fusion.10), channel_id=1, source_target_pairs={{0,2},{1,3},{2,0},{3,1},{4,6},{5,7},{6,4},{7,5},{8,10},{9,11},{10,... | collective-permute-start | bytes 589832 | tf_op jit(solution)/shard_map/ppermute | solution.py:16
  64.6 0.5 collective-permute-done.25
  65.1 0.3 collective-permute-start.26
  65.4 2.9 %collective-permute-done.18 = bf16[2,2,96,256]{3,2,0,1:T(8,128)(2,1)S(1)} collective-permute-done((bf16[2,2,96,256]{3,2,0,1:T(8,128)(2,1)S(1)}, bf16[2,2,96,256]{3,2,0,1:T(8,128)(2,1)S(1)}, u32[]{:S(2)}, u32[]{:S(2)}) %collective-permute-start.18) | collective-permute-done | bytes 196640 | tf_op jit(solution)/shard_map/ppermute | solution.py:16
  68.6 2.2 %collective-permute-done.26 = bf16[2,2,96,256]{3,2,1,0:T(8,128)(2,1)S(1)} collective-permute-done((bf16[2,2,96,256]{3,2,1,0:T(8,128)(2,1)S(1)}, bf16[2,2,96,256]{3,2,1,0:T(8,128)(2,1)S(1)}, u32[]{:S(2)}, u32[]{:S(2)}) %collective-permute-start.26) | collective-permute-done | bytes 196640 | tf_op jit(solution)/shard_map/ppermute | solution.py:16
  71.2 3.0 %fusion.2 = bf16[1536,256]{0,1:T(8,128)(2,1)S(1)} fusion(bf16[3,512,1536]{2,1,0:T(8,128)(2,1)} %param.5, bf16[1536,256]{1,0:T(8,128)(2,1)S(1)} %bitcast.259), kind=kOutput, calls=%fused_computation.6 | convolution fusion | flops 805830656 | bytes 4718592 | tf_op jit(solution)/shard_map/dot_general | solution.py:10
  74.5 0.8 dynamic-slice_bitcast_fusion
  75.3 0.5 collective-permute-start.20
  75.9 3.9 %fusion.3 = bf16[1536,256]{0,1:T(8,128)(2,1)} fusion(bf16[3,512,1536]{2,1,0:T(8,128)(2,1)} %param.5, bf16[1536,256]{1,0:T(8,128)(2,1)S(1)} %bitcast.260), kind=kOutput, calls=%fused_computation.7 | convolution fusion | flops 805830656 | bytes 4718592 | tf_op jit(solution)/shard_map/dot_general | solution.py:10
  79.8 1.4 %copy.40 = bf16[1536,256]{1,0:T(8,128)(2,1)S(1)} copy(bf16[1536,256]{0,1:T(8,128)(2,1)} %fusion.3) | data formatting | bytes 1572864 | tf_op jit(solution)/shard_map/convert_element_type | solution.py:86
  81.9 1.1 convert_add_fusion.1
  83.0 1.7 %collective-permute-start.21 = (bf16[2,2,96,256]{3,2,1,0:T(8,128)(2,1)S(1)}, bf16[2,2,96,256]{3,2,1,0:T(8,128)(2,1)S(1)}, u32[]{:S(2)}, u32[]{:S(2)}) collective-permute-start(bf16[2,2,96,256]{3,2,1,0:T(8,128)(2,1)S(1)} %fusion.48), channel_id=1, source_target_pairs={{0,2},{1,3},{2,0},{3,1},{4,6},{5,7},{6,4},{7,5},{8,10},{9,11},{10,... | collective-permute-start | bytes 589832 | tf_op jit(solution)/shard_map/ppermute | solution.py:16
  85.0 5.4 %collective-permute-done.21 = bf16[2,2,96,256]{3,2,1,0:T(8,128)(2,1)S(1)} collective-permute-done((bf16[2,2,96,256]{3,2,1,0:T(8,128)(2,1)S(1)}, bf16[2,2,96,256]{3,2,1,0:T(8,128)(2,1)S(1)}, u32[]{:S(2)}, u32[]{:S(2)}) %collective-permute-start.21) | collective-permute-done | bytes 196640 | tf_op jit(solution)/shard_map/ppermute | solution.py:16
  90.5 0.3 collective-permute-start.22
  90.8 1.2 %collective-permute-done.29 = bf16[2,2,96,256]{3,2,0,1:T(8,128)(2,1)S(1)} collective-permute-done((bf16[2,2,96,256]{3,2,0,1:T(8,128)(2,1)S(1)}, bf16[2,2,96,256]{3,2,0,1:T(8,128)(2,1)S(1)}, u32[]{:S(2)}, u32[]{:S(2)}) %collective-permute-start.29) | collective-permute-done | bytes 196640 | tf_op jit(solution)/shard_map/ppermute | solution.py:16
  92.0 0.4 collective-permute-start.30
  92.5 2.7 %collective-permute-done.22 = bf16[2,96,256]{2,1,0:T(8,128)(2,1)S(1)} collective-permute-done((bf16[2,96,256]{2,1,0:T(8,128)(2,1)S(1)}, bf16[2,96,256]{2,1,0:T(8,128)(2,1)S(1)}, u32[]{:S(2)}, u32[]{:S(2)}) %collective-permute-start.22) | collective-permute-done | bytes 98336 | tf_op jit(solution)/shard_map/ppermute | solution.py:16
  95.2 0.7 collective-permute-start.23
  95.9 0.8 collective-permute-done.30
  96.8 1.5 %collective-permute-start.31 = (bf16[96,256]{1,0:T(8,128)(2,1)S(1)}, bf16[96,256]{1,0:T(8,128)(2,1)S(1)}, u32[]{:S(2)}, u32[]{:S(2)}) collective-permute-start(bf16[96,256]{1,0:T(8,128)(2,1)S(1)} %fusion.59), channel_id=1, source_target_pairs={{0,8},{1,9},{2,10},{3,11},{4,12},{5,13},{6,14},{7,15},{8,0},{9,1},... | collective-permute-start | bytes 147464 | tf_op jit(solution)/shard_map/ppermute | solution.py:16
  98.3 2.7 %collective-permute-done.23 = bf16[96,256]{1,0:T(8,128)(2,1)S(1)} collective-permute-done((bf16[96,256]{1,0:T(8,128)(2,1)S(1)}, bf16[96,256]{1,0:T(8,128)(2,1)S(1)}, u32[]{:S(2)}, u32[]{:S(2)}) %collective-permute-start.23) | collective-permute-done | bytes 49184 | tf_op jit(solution)/shard_map/ppermute | solution.py:16
  101.0 0.8 collective-permute-done.31
  102.0 0.9 collective-permute-start.33
  102.9 1.0 collective-permute-start.34
  103.9 1.8 %collective-permute-done.33 = f32[256]{0:T(256)S(1)} collective-permute-done((f32[256]{0:T(256)S(1)}, f32[256]{0:T(256)S(1)}, u32[]{:S(2)}, u32[]{:S(2)}) %collective-permute-start.33) | collective-permute-done | bytes 1056 | tf_op jit(solution)/shard_map/ppermute | solution.py:16
  105.9 1.5 %collective-permute-start.35 = (f32[256]{0:T(256)S(1)}, f32[256]{0:T(256)S(1)}, u32[]{:S(2)}, u32[]{:S(2)}) collective-permute-start(f32[256]{0:T(256)S(1)} %add_add_fusion), channel_id=1, source_target_pairs={{0,4},{1,5},{2,6},{3,7},{4,0},{5,1},{6,2},{7,3},{8,12},{9,13},{10,... | collective-permute-start | bytes 3080 | tf_op jit(solution)/shard_map/ppermute | solution.py:16
  107.5 1.1 collective-permute-start.36
  108.6 1.7 %collective-permute-start.37 = (f32[256]{0:T(256)S(1)}, f32[256]{0:T(256)S(1)}, u32[]{:S(2)}, u32[]{:S(2)}) collective-permute-start(f32[256]{0:T(256)S(1)} %add_add_fusion), channel_id=1, source_target_pairs={{0,12},{1,13},{2,14},{3,15},{4,8},{5,9},{6,10},{7,11},{8,4},{9,5},... | collective-permute-start | bytes 3080 | tf_op jit(solution)/shard_map/ppermute | solution.py:16
  110.3 1.6 %collective-permute-done.36 = f32[256]{0:T(256)S(1)} collective-permute-done((f32[256]{0:T(256)S(1)}, f32[256]{0:T(256)S(1)}, u32[]{:S(2)}, u32[]{:S(2)}) %collective-permute-start.36) | collective-permute-done | bytes 1056 | tf_op jit(solution)/shard_map/ppermute | solution.py:16
  111.9 2.0 %collective-permute-done.37 = f32[256]{0:T(256)S(1)} collective-permute-done((f32[256]{0:T(256)S(1)}, f32[256]{0:T(256)S(1)}, u32[]{:S(2)}, u32[]{:S(2)}) %collective-permute-start.37) | collective-permute-done | bytes 1056 | tf_op jit(solution)/shard_map/ppermute | solution.py:16
  114.0 0.7 broadcast_multiply_fusion
  (104 shorter events, 5.4 us)
Async XLA Ops:
  0.6 6.9 %collective-permute-start = (bf16[96,256]{1,0:T(8,128)(2,1)}, bf16[96,256]{1,0:T(8,128)(2,1)S(1)}, u32[]{:S(2)}, u32[]{:S(2)}) collective-permute-start(bf16[96,256]{1,0:T(8,128)(2,1)} %param.6), channel_id=1, source_target_pairs={{0,8},{1,9},{2,10},{3,11},{4,12},{5,13},{6,14},{7,15},{8,0},{9,1},... | collective-permute-start | bytes 147464 | tf_op jit(solution)/shard_map/ppermute | solution.py:16
  4.7 5.9 %collective-permute-start.8 = (bf16[96,256]{1,0:T(8,128)(2,1)}, bf16[96,256]{1,0:T(8,128)(2,1)S(1)}, u32[]{:S(2)}, u32[]{:S(2)}) collective-permute-start(bf16[96,256]{1,0:T(8,128)(2,1)} %param.7), channel_id=1, source_target_pairs={{0,8},{1,9},{2,10},{3,11},{4,12},{5,13},{6,14},{7,15},{8,0},{9,1},... | collective-permute-start | bytes 147464 | tf_op jit(solution)/shard_map/ppermute | solution.py:16
  8.4 5.1 %collective-permute-start.1 = (bf16[2,96,256]{2,1,0:T(8,128)(2,1)S(1)}, bf16[2,96,256]{2,1,0:T(8,128)(2,1)S(1)}, u32[]{:S(2)}, u32[]{:S(2)}) collective-permute-start(bf16[2,96,256]{2,1,0:T(8,128)(2,1)S(1)} %pad_maximum_fusion.12), channel_id=1, source_target_pairs={{0,4},{1,5},{2,6},{3,7},{4,0},{5,1},{6,2},{7,3},{8,12},{9,13},{10,... | collective-permute-start | bytes 294920 | tf_op jit(solution)/shard_map/ppermute | solution.py:16
  11.4 5.3 %collective-permute-start.9 = (bf16[2,96,256]{2,1,0:T(8,128)(2,1)S(1)}, bf16[2,96,256]{2,1,0:T(8,128)(2,1)S(1)}, u32[]{:S(2)}, u32[]{:S(2)}) collective-permute-start(bf16[2,96,256]{2,1,0:T(8,128)(2,1)S(1)} %pad_maximum_fusion.13), channel_id=1, source_target_pairs={{0,2},{1,3},{2,0},{3,1},{4,6},{5,7},{6,4},{7,5},{8,10},{9,11},{10,... | collective-permute-start | bytes 294920 | tf_op jit(solution)/shard_map/ppermute | solution.py:16
  13.5 6.8 %collective-permute-start.2 = (bf16[2,2,96,256]{3,2,0,1:T(8,128)(2,1)S(1)}, bf16[2,2,96,256]{3,2,0,1:T(8,128)(2,1)S(1)}, u32[]{:S(2)}, u32[]{:S(2)}) collective-permute-start(bf16[2,2,96,256]{3,2,0,1:T(8,128)(2,1)S(1)} %pad_maximum_fusion.8), channel_id=1, source_target_pairs={{0,2},{1,3},{2,0},{3,1},{4,6},{5,7},{6,4},{7,5},{8,10},{9,11},{10,... | collective-permute-start | bytes 589832 | tf_op jit(solution)/shard_map/ppermute | solution.py:16
  16.8 5.7 %collective-permute-start.10 = (bf16[2,2,96,256]{3,2,1,0:T(8,128)(2,1)S(1)}, bf16[2,2,96,256]{3,2,1,0:T(8,128)(2,1)S(1)}, u32[]{:S(2)}, u32[]{:S(2)}) collective-permute-start(bf16[2,2,96,256]{3,2,1,0:T(8,128)(2,1)S(1)} %pad_maximum_fusion.9), channel_id=1, source_target_pairs={{0,4},{1,5},{2,6},{3,7},{4,0},{5,1},{6,2},{7,3},{8,12},{9,13},{10,... | collective-permute-start | bytes 589832 | tf_op jit(solution)/shard_map/ppermute | solution.py:16
  20.5 2.2 %collective-permute-start.3 = (bf16[2,2,2,96,256]{4,3,2,1,0:T(8,128)(2,1)S(1)}, bf16[2,2,2,96,256]{4,3,2,1,0:T(8,128)(2,1)S(1)}, u32[]{:S(2)}, u32[]{:S(2)}) collective-permute-start(bf16[2,2,2,96,256]{4,3,2,1,0:T(8,128)(2,1)S(1)} %copy.43), channel_id=1, source_target_pairs={{0,1},{1,0},{2,3},{3,2},{4,5},{5,4},{6,7},{7,6},{8,9},{9,8},{10,11... | collective-permute-start | bytes 1179656 | tf_op jit(solution)/shard_map/ppermute | solution.py:16
  22.6 3.6 %collective-permute-start.11 = (bf16[2,2,2,96,256]{4,3,2,0,1:T(8,128)(2,1)S(1)}, bf16[2,2,2,96,256]{4,3,2,0,1:T(8,128)(2,1)S(1)}, u32[]{:S(2)}, u32[]{:S(2)}) collective-permute-start(bf16[2,2,2,96,256]{4,3,2,0,1:T(8,128)(2,1)S(1)} %pad_maximum_fusion.5), channel_id=1, source_target_pairs={{0,1},{1,0},{2,3},{3,2},{4,5},{5,4},{6,7},{7,6},{8,9},{9,8},{10,11... | collective-permute-start | bytes 1179656 | tf_op jit(solution)/shard_map/ppermute | solution.py:16
  29.7 0.7 copy-start
  29.7 0.7 copy-start.1
  29.9 1.9 %collective-permute-start.12 = (bf16[2,2,2,96,256]{4,3,0,2,1:T(8,128)(2,1)S(1)}, bf16[2,2,2,96,256]{4,3,0,2,1:T(8,128)(2,1)S(1)}, u32[]{:S(2)}, u32[]{:S(2)}) collective-permute-start(bf16[2,2,2,96,256]{4,3,0,2,1:T(8,128)(2,1)S(1)} %bitcast.262), channel_id=1, source_target_pairs={{0,1},{1,0},{2,3},{3,2},{4,5},{5,4},{6,7},{7,6},{8,9},{9,8},{10,11... | collective-permute-start | bytes 1179656 | tf_op jit(solution)/shard_map/ppermute | solution.py:16
  30.5 2.1 %collective-permute-start.4 = (bf16[2,2,2,96,256]{4,3,0,1,2:T(8,128)(2,1)S(1)}, bf16[2,2,2,96,256]{4,3,0,1,2:T(8,128)(2,1)S(1)}, u32[]{:S(2)}, u32[]{:S(2)}) collective-permute-start(bf16[2,2,2,96,256]{4,3,0,1,2:T(8,128)(2,1)S(1)} %bitcast.261), channel_id=1, source_target_pairs={{0,1},{1,0},{2,3},{3,2},{4,5},{5,4},{6,7},{7,6},{8,9},{9,8},{10,11... | collective-permute-start | bytes 1179656 | tf_op jit(solution)/shard_map/ppermute | solution.py:16
  31.9 7.2 %collective-permute-start.13 = (bf16[2,2,96,256]{3,2,0,1:T(8,128)(2,1)S(1)}, bf16[2,2,96,256]{3,2,0,1:T(8,128)(2,1)S(1)}, u32[]{:S(2)}, u32[]{:S(2)}) collective-permute-start(bf16[2,2,96,256]{3,2,0,1:T(8,128)(2,1)S(1)} %fusion.47), channel_id=1, source_target_pairs={{0,4},{1,5},{2,6},{3,7},{4,0},{5,1},{6,2},{7,3},{8,12},{9,13},{10,... | collective-permute-start | bytes 589832 | tf_op jit(solution)/shard_map/ppermute | solution.py:16
  32.7 8.1 %collective-permute-start.5 = (bf16[2,2,96,256]{3,2,0,1:T(8,128)(2,1)S(1)}, bf16[2,2,96,256]{3,2,0,1:T(8,128)(2,1)S(1)}, u32[]{:S(2)}, u32[]{:S(2)}) collective-permute-start(bf16[2,2,96,256]{3,2,0,1:T(8,128)(2,1)S(1)} %fusion.46), channel_id=1, source_target_pairs={{0,2},{1,3},{2,0},{3,1},{4,6},{5,7},{6,4},{7,5},{8,10},{9,11},{10,... | collective-permute-start | bytes 589832 | tf_op jit(solution)/shard_map/ppermute | solution.py:16
  39.2 4.7 %collective-permute-start.14 = (bf16[2,96,256]{2,1,0:T(8,128)(2,1)S(1)}, bf16[2,96,256]{2,1,0:T(8,128)(2,1)S(1)}, u32[]{:S(2)}, u32[]{:S(2)}) collective-permute-start(bf16[2,96,256]{2,1,0:T(8,128)(2,1)S(1)} %fusion.51), channel_id=1, source_target_pairs={{0,2},{1,3},{2,0},{3,1},{4,6},{5,7},{6,4},{7,5},{8,10},{9,11},{10,... | collective-permute-start | bytes 294920 | tf_op jit(solution)/shard_map/ppermute | solution.py:16
  40.9 6.3 %collective-permute-start.6 = (bf16[2,96,256]{2,1,0:T(8,128)(2,1)S(1)}, bf16[2,96,256]{2,1,0:T(8,128)(2,1)S(1)}, u32[]{:S(2)}, u32[]{:S(2)}) collective-permute-start(bf16[2,96,256]{2,1,0:T(8,128)(2,1)S(1)} %fusion.50), channel_id=1, source_target_pairs={{0,4},{1,5},{2,6},{3,7},{4,0},{5,1},{6,2},{7,3},{8,12},{9,13},{10,... | collective-permute-start | bytes 294920 | tf_op jit(solution)/shard_map/ppermute | solution.py:16
  43.9 6.7 %collective-permute-start.15 = (bf16[96,256]{1,0:T(8,128)(2,1)S(1)}, bf16[96,256]{1,0:T(8,128)(2,1)S(1)}, u32[]{:S(2)}, u32[]{:S(2)}) collective-permute-start(bf16[96,256]{1,0:T(8,128)(2,1)S(1)} %fusion.57), channel_id=1, source_target_pairs={{0,8},{1,9},{2,10},{3,11},{4,12},{5,13},{6,14},{7,15},{8,0},{9,1},... | collective-permute-start | bytes 147464 | tf_op jit(solution)/shard_map/ppermute | solution.py:16
  47.3 5.3 %collective-permute-start.7 = (bf16[96,256]{1,0:T(8,128)(2,1)S(1)}, bf16[96,256]{1,0:T(8,128)(2,1)S(1)}, u32[]{:S(2)}, u32[]{:S(2)}) collective-permute-start(bf16[96,256]{1,0:T(8,128)(2,1)S(1)} %fusion.56), channel_id=1, source_target_pairs={{0,8},{1,9},{2,10},{3,11},{4,12},{5,13},{6,14},{7,15},{8,0},{9,1},... | collective-permute-start | bytes 147464 | tf_op jit(solution)/shard_map/ppermute | solution.py:16
  52.7 5.1 %collective-permute-start.16 = (bf16[96,256]{1,0:T(8,128)(2,1)S(1)}, bf16[96,256]{1,0:T(8,128)(2,1)S(1)}, u32[]{:S(2)}, u32[]{:S(2)}) collective-permute-start(bf16[96,256]{1,0:T(8,128)(2,1)S(1)} %get-tuple-element.22), channel_id=1, source_target_pairs={{0,8},{1,9},{2,10},{3,11},{4,12},{5,13},{6,14},{7,15},{8,0},{9,1},... | collective-permute-start | bytes 147464 | tf_op jit(solution)/shard_map/ppermute | solution.py:16
  54.2 5.4 %collective-permute-start.24 = (bf16[96,256]{1,0:T(8,128)(2,1)S(1)}, bf16[96,256]{1,0:T(8,128)(2,1)S(1)}, u32[]{:S(2)}, u32[]{:S(2)}) collective-permute-start(bf16[96,256]{1,0:T(8,128)(2,1)S(1)} %get-tuple-element.23), channel_id=1, source_target_pairs={{0,8},{1,9},{2,10},{3,11},{4,12},{5,13},{6,14},{7,15},{8,0},{9,1},... | collective-permute-start | bytes 147464 | tf_op jit(solution)/shard_map/ppermute | solution.py:16
  57.8 4.7 %collective-permute-start.17 = (bf16[2,96,256]{2,1,0:T(8,128)(2,1)S(1)}, bf16[2,96,256]{2,1,0:T(8,128)(2,1)S(1)}, u32[]{:S(2)}, u32[]{:S(2)}) collective-permute-start(bf16[2,96,256]{2,1,0:T(8,128)(2,1)S(1)} %pad_maximum_fusion.14), channel_id=1, source_target_pairs={{0,4},{1,5},{2,6},{3,7},{4,0},{5,1},{6,2},{7,3},{8,12},{9,13},{10,... | collective-permute-start | bytes 294920 | tf_op jit(solution)/shard_map/ppermute | solution.py:16
  59.6 5.4 %collective-permute-start.25 = (bf16[2,96,256]{2,1,0:T(8,128)(2,1)S(1)}, bf16[2,96,256]{2,1,0:T(8,128)(2,1)S(1)}, u32[]{:S(2)}, u32[]{:S(2)}) collective-permute-start(bf16[2,96,256]{2,1,0:T(8,128)(2,1)S(1)} %pad_maximum_fusion.15), channel_id=1, source_target_pairs={{0,2},{1,3},{2,0},{3,1},{4,6},{5,7},{6,4},{7,5},{8,10},{9,11},{10,... | collective-permute-start | bytes 294920 | tf_op jit(solution)/shard_map/ppermute | solution.py:16
  62.6 5.7 %collective-permute-start.18 = (bf16[2,2,96,256]{3,2,0,1:T(8,128)(2,1)S(1)}, bf16[2,2,96,256]{3,2,0,1:T(8,128)(2,1)S(1)}, u32[]{:S(2)}, u32[]{:S(2)}) collective-permute-start(bf16[2,2,96,256]{3,2,0,1:T(8,128)(2,1)S(1)} %pad_maximum_fusion.10), channel_id=1, source_target_pairs={{0,2},{1,3},{2,0},{3,1},{4,6},{5,7},{6,4},{7,5},{8,10},{9,11},{10,... | collective-permute-start | bytes 589832 | tf_op jit(solution)/shard_map/ppermute | solution.py:16
  65.1 5.7 %collective-permute-start.26 = (bf16[2,2,96,256]{3,2,1,0:T(8,128)(2,1)S(1)}, bf16[2,2,96,256]{3,2,1,0:T(8,128)(2,1)S(1)}, u32[]{:S(2)}, u32[]{:S(2)}) collective-permute-start(bf16[2,2,96,256]{3,2,1,0:T(8,128)(2,1)S(1)} %pad_maximum_fusion.11), channel_id=1, source_target_pairs={{0,4},{1,5},{2,6},{3,7},{4,0},{5,1},{6,2},{7,3},{8,12},{9,13},{10,... | collective-permute-start | bytes 589832 | tf_op jit(solution)/shard_map/ppermute | solution.py:16
  68.4 2.6 %collective-permute-start.19 = (bf16[2,2,2,96,256]{4,3,0,1,2:T(8,128)(2,1)S(1)}, bf16[2,2,2,96,256]{4,3,0,1,2:T(8,128)(2,1)S(1)}, u32[]{:S(2)}, u32[]{:S(2)}) collective-permute-start(bf16[2,2,2,96,256]{4,3,0,1,2:T(8,128)(2,1)S(1)} %pad_maximum_fusion.6), channel_id=1, source_target_pairs={{0,1},{1,0},{2,3},{3,2},{4,5},{5,4},{6,7},{7,6},{8,9},{9,8},{10,11... | collective-permute-start | bytes 1179656 | tf_op jit(solution)/shard_map/ppermute | solution.py:16
  70.9 4.8 %collective-permute-start.27 = (bf16[2,2,2,96,256]{4,3,2,1,0:T(8,128)(2,1)S(1)}, bf16[2,2,2,96,256]{4,3,2,1,0:T(8,128)(2,1)S(1)}, u32[]{:S(2)}, u32[]{:S(2)}) collective-permute-start(bf16[2,2,2,96,256]{4,3,2,1,0:T(8,128)(2,1)S(1)} %pad_maximum_fusion.7), channel_id=1, source_target_pairs={{0,1},{1,0},{2,3},{3,2},{4,5},{5,4},{6,7},{7,6},{8,9},{9,8},{10,11... | collective-permute-start | bytes 1179656 | tf_op jit(solution)/shard_map/ppermute | solution.py:16
  75.3 6.7 %collective-permute-start.20 = (bf16[2,2,2,96,256]{4,3,2,1,0:T(8,128)(2,1)}, bf16[2,2,2,96,256]{4,3,2,1,0:T(8,128)(2,1)}, u32[]{:S(2)}, u32[]{:S(2)}) collective-permute-start(bf16[2,2,2,96,256]{4,3,2,1,0:T(8,128)(2,1)} %dynamic-slice_bitcast_fusion), channel_id=1, source_target_pairs={{0,1},{1,0},{2,3},{3,2},{4,5},{5,4},{6,7},{7,6},{8,9},{9,8},{10,11... | collective-permute-start | bytes 1179656 | tf_op jit(solution)/shard_map/ppermute | solution.py:16
  81.3 3.4 %collective-permute-start.28 = (bf16[2,2,2,96,256]{4,3,0,2,1:T(8,128)(2,1)S(1)}, bf16[2,2,2,96,256]{4,3,0,2,1:T(8,128)(2,1)S(1)}, u32[]{:S(2)}, u32[]{:S(2)}) collective-permute-start(bf16[2,2,2,96,256]{4,3,0,2,1:T(8,128)(2,1)S(1)} %bitcast.263), channel_id=1, source_target_pairs={{0,1},{1,0},{2,3},{3,2},{4,5},{5,4},{6,7},{7,6},{8,9},{9,8},{10,11... | collective-permute-start | bytes 1179656 | tf_op jit(solution)/shard_map/ppermute | solution.py:16
  83.0 7.4 %collective-permute-start.21 = (bf16[2,2,96,256]{3,2,1,0:T(8,128)(2,1)S(1)}, bf16[2,2,96,256]{3,2,1,0:T(8,128)(2,1)S(1)}, u32[]{:S(2)}, u32[]{:S(2)}) collective-permute-start(bf16[2,2,96,256]{3,2,1,0:T(8,128)(2,1)S(1)} %fusion.48), channel_id=1, source_target_pairs={{0,2},{1,3},{2,0},{3,1},{4,6},{5,7},{6,4},{7,5},{8,10},{9,11},{10,... | collective-permute-start | bytes 589832 | tf_op jit(solution)/shard_map/ppermute | solution.py:16
  84.9 7.1 %collective-permute-start.29 = (bf16[2,2,96,256]{3,2,0,1:T(8,128)(2,1)S(1)}, bf16[2,2,96,256]{3,2,0,1:T(8,128)(2,1)S(1)}, u32[]{:S(2)}, u32[]{:S(2)}) collective-permute-start(bf16[2,2,96,256]{3,2,0,1:T(8,128)(2,1)S(1)} %fusion.49), channel_id=1, source_target_pairs={{0,4},{1,5},{2,6},{3,7},{4,0},{5,1},{6,2},{7,3},{8,12},{9,13},{10,... | collective-permute-start | bytes 589832 | tf_op jit(solution)/shard_map/ppermute | solution.py:16
  90.5 4.7 %collective-permute-start.22 = (bf16[2,96,256]{2,1,0:T(8,128)(2,1)S(1)}, bf16[2,96,256]{2,1,0:T(8,128)(2,1)S(1)}, u32[]{:S(2)}, u32[]{:S(2)}) collective-permute-start(bf16[2,96,256]{2,1,0:T(8,128)(2,1)S(1)} %fusion.52), channel_id=1, source_target_pairs={{0,4},{1,5},{2,6},{3,7},{4,0},{5,1},{6,2},{7,3},{8,12},{9,13},{10,... | collective-permute-start | bytes 294920 | tf_op jit(solution)/shard_map/ppermute | solution.py:16
  92.0 4.7 %collective-permute-start.30 = (bf16[2,96,256]{2,1,0:T(8,128)(2,1)S(1)}, bf16[2,96,256]{2,1,0:T(8,128)(2,1)S(1)}, u32[]{:S(2)}, u32[]{:S(2)}) collective-permute-start(bf16[2,96,256]{2,1,0:T(8,128)(2,1)S(1)} %fusion.53), channel_id=1, source_target_pairs={{0,2},{1,3},{2,0},{3,1},{4,6},{5,7},{6,4},{7,5},{8,10},{9,11},{10,... | collective-permute-start | bytes 294920 | tf_op jit(solution)/shard_map/ppermute | solution.py:16
  95.2 5.8 %collective-permute-start.23 = (bf16[96,256]{1,0:T(8,128)(2,1)S(1)}, bf16[96,256]{1,0:T(8,128)(2,1)S(1)}, u32[]{:S(2)}, u32[]{:S(2)}) collective-permute-start(bf16[96,256]{1,0:T(8,128)(2,1)S(1)} %fusion.58), channel_id=1, source_target_pairs={{0,8},{1,9},{2,10},{3,11},{4,12},{5,13},{6,14},{7,15},{8,0},{9,1},... | collective-permute-start | bytes 147464 | tf_op jit(solution)/shard_map/ppermute | solution.py:16
  96.8 5.1 %collective-permute-start.31 = (bf16[96,256]{1,0:T(8,128)(2,1)S(1)}, bf16[96,256]{1,0:T(8,128)(2,1)S(1)}, u32[]{:S(2)}, u32[]{:S(2)}) collective-permute-start(bf16[96,256]{1,0:T(8,128)(2,1)S(1)} %fusion.59), channel_id=1, source_target_pairs={{0,8},{1,9},{2,10},{3,11},{4,12},{5,13},{6,14},{7,15},{8,0},{9,1},... | collective-permute-start | bytes 147464 | tf_op jit(solution)/shard_map/ppermute | solution.py:16
  101.9 1.9 %collective-permute-start.32 = (f32[256]{0:T(256)S(1)}, f32[256]{0:T(256)S(1)}, u32[]{:S(2)}, u32[]{:S(2)}) collective-permute-start(f32[256]{0:T(256)S(1)} %add.192), channel_id=1, source_target_pairs={{0,1},{1,0},{2,3},{3,2},{4,5},{5,4},{6,7},{7,6},{8,9},{9,8},{10,11... | collective-permute-start | bytes 3080 | tf_op jit(solution)/shard_map/ppermute | solution.py:16
  102.0 3.6 %collective-permute-start.33 = (f32[256]{0:T(256)S(1)}, f32[256]{0:T(256)S(1)}, u32[]{:S(2)}, u32[]{:S(2)}) collective-permute-start(f32[256]{0:T(256)S(1)} %add.192), channel_id=1, source_target_pairs={{0,2},{1,3},{2,0},{3,1},{4,6},{5,7},{6,4},{7,5},{8,10},{9,11},{10,... | collective-permute-start | bytes 3080 | tf_op jit(solution)/shard_map/ppermute | solution.py:16
  102.9 3.0 %collective-permute-start.34 = (f32[256]{0:T(256)S(1)}, f32[256]{0:T(256)S(1)}, u32[]{:S(2)}, u32[]{:S(2)}) collective-permute-start(f32[256]{0:T(256)S(1)} %add.192), channel_id=1, source_target_pairs={{0,3},{1,2},{2,1},{3,0},{4,7},{5,6},{6,5},{7,4},{8,11},{9,10},{10,... | collective-permute-start | bytes 3080 | tf_op jit(solution)/shard_map/ppermute | solution.py:16
  105.9 4.4 %collective-permute-start.35 = (f32[256]{0:T(256)S(1)}, f32[256]{0:T(256)S(1)}, u32[]{:S(2)}, u32[]{:S(2)}) collective-permute-start(f32[256]{0:T(256)S(1)} %add_add_fusion), channel_id=1, source_target_pairs={{0,4},{1,5},{2,6},{3,7},{4,0},{5,1},{6,2},{7,3},{8,12},{9,13},{10,... | collective-permute-start | bytes 3080 | tf_op jit(solution)/shard_map/ppermute | solution.py:16
  107.5 4.5 %collective-permute-start.36 = (f32[256]{0:T(256)S(1)}, f32[256]{0:T(256)S(1)}, u32[]{:S(2)}, u32[]{:S(2)}) collective-permute-start(f32[256]{0:T(256)S(1)} %add_add_fusion), channel_id=1, source_target_pairs={{0,8},{1,9},{2,10},{3,11},{4,12},{5,13},{6,14},{7,15},{8,0},{9,1},... | collective-permute-start | bytes 3080 | tf_op jit(solution)/shard_map/ppermute | solution.py:16
  108.6 5.4 %collective-permute-start.37 = (f32[256]{0:T(256)S(1)}, f32[256]{0:T(256)S(1)}, u32[]{:S(2)}, u32[]{:S(2)}) collective-permute-start(f32[256]{0:T(256)S(1)} %add_add_fusion), channel_id=1, source_target_pairs={{0,12},{1,13},{2,14},{3,15},{4,8},{5,9},{6,10},{7,11},{8,4},{9,5},... | collective-permute-start | bytes 3080 | tf_op jit(solution)/shard_map/ppermute | solution.py:16

commit v18 on v14

--- a/solution.py
+++ b/solution.py
@@ -16,12 +16,16 @@
     return lax.ppermute(x, "row", [(i, i ^ distance) for i in range(devices)])
 
 
-def halving_reduce_scatter(z, devices, order):
+def halving_reduce_scatter(z, devices, order, keep_pair=False):
     bits = devices.bit_length() - 1
     me = lax.axis_index("row")
     cur = z.reshape((2,) * bits + (z.shape[0] // devices, z.shape[1]))
     left = list(range(bits - 1, -1, -1))
     for bit in order:
+        if keep_pair and bit == order[-1]:
+            return cur.astype(jnp.float32) + exchange(
+                cur.astype(jnp.bfloat16), 1 << bit, devices
+            ).astype(jnp.float32)
         axis = left.index(bit)
         left.remove(bit)
         mine = (me >> bit) & 1
@@ -33,10 +37,10 @@
     return cur
 
 
-def doubling_all_gather(x, devices, order):
+def doubling_all_gather(x, devices, order, done=()):
     me = lax.axis_index("row")
     cur = x
-    done = []
+    done = list(done)
     for bit in order:
         other = exchange(cur, 1 << bit, devices)
         low = (me >> bit) & 1 == 0
@@ -87,18 +91,33 @@
             halves.append(
                 contract_rows(panels[sector + 1], projected.astype(jnp.bfloat16)).astype(jnp.bfloat16)
             )
-        rot_amp = halving_reduce_scatter(halves[0], devices, order_amp)
-        rot_der = halving_reduce_scatter(halves[1], devices, order_der)
-        angle_rows = lax.dynamic_slice_in_dim(phase[sector], first_row, chan_rows, 0)
-        wave_rows = lax.dynamic_slice_in_dim(wavenum[sector], first_row, chan_rows, 0)
-        cosine = jnp.cos(angle_rows)[:, None]
-        sine = jnp.sin(angle_rows)[:, None]
-        wave = wave_rows[:, None]
+        last = sector + 1 == SECTORS
+        rot_amp = halving_reduce_scatter(halves[0], devices, order_amp, keep_pair=not last)
+        rot_der = halving_reduce_scatter(halves[1], devices, order_der, keep_pair=not last)
+        if last:
+            blocks = [first_row]
+        else:
+            pair_bit = order_amp[-1]
+            base = lax.axis_index("row") & ~(1 << pair_bit)
+            blocks = [base * chan_rows, (base | (1 << pair_bit)) * chan_rows]
+        angle_rows = jnp.stack(
+            [lax.dynamic_slice_in_dim(phase[sector], b, chan_rows, 0) for b in blocks]
+        ).reshape(rot_amp.shape[:-1] + (1,))
+        wave_rows = jnp.stack(
+            [lax.dynamic_slice_in_dim(wavenum[sector], b, chan_rows, 0) for b in blocks]
+        ).reshape(rot_amp.shape[:-1] + (1,))
+        cosine = jnp.cos(angle_rows)
+        sine = jnp.sin(angle_rows)
+        wave = wave_rows
         new_amp = cosine * rot_amp + sine / wave * rot_der
         new_der = -wave * sine * rot_amp + cosine * rot_der
         if sector + 1 < SECTORS:
-            amp_full = doubling_all_gather(new_amp.astype(jnp.bfloat16), devices, order_amp[::-1])
-            der_full = doubling_all_gather(new_der.astype(jnp.bfloat16), devices, order_der[::-1])
+            amp_full = doubling_all_gather(
+                new_amp.astype(jnp.bfloat16), devices, order_amp[::-1][1:], done=order_amp[-1:]
+            )
+            der_full = doubling_all_gather(
+                new_der.astype(jnp.bfloat16), devices, order_der[::-1][1:], done=order_der[-1:]
+            )
             amp_wide = amp_full.astype(jnp.float32)
             der_wide = der_full.astype(jnp.float32)
             norm = jnp.sum(amp_wide * amp_wide, axis=0) + jnp.sum(der_wide * der_wide, axis=0)

time: 111 us -> 109 us (0.982)
  waiting for transfers between devices: 53.1 us -> 43.6 us
  starting transfers between devices: 37 us -> 43.4 us
    ppermute x38 -> x36, waiting for transfers between devices: 53.1 us -> 43.6 us  [exchange(): return lax.ppermute(x, 'row', [(i, i ^ distance) for i in range(devices)])]
    ppermute x38 -> x36, starting transfers between devices: 37 us -> 43.4 us  [exchange(): return lax.ppermute(x, 'row', [(i, i ^ distance) for i in range(devices)])]
    another operation x32 -> x28, other arithmetic: 2.76 us -> 2.71 us  [doubling_all_gather(): jnp.stack([jnp.where(low, cur, other), jnp.where(low, other, cur)], axis=...]
  transfers between devices with their start and end apart: 38 -> 36, of which waited for: 30 -> 24; matrix products, arithmetic and copies ran while one was open for 10% -> 11% of each run, Pallas kernels for 0% -> 0%
where the time goes in v18:
time: 109 us; the launch traced here: 108 us
  waiting for transfers between devices  43.6 us (40%)
  starting transfers between devices  43.4 us (40%)
  matrix products  11.9 us (11%)
  other arithmetic  5.59 us (5%)
  local copies, waits for them, and re-layouts  2.61 us (2%)
  between operations  1.24 us (1%)
    ppermute x36, waiting for transfers between devices, exchange(): return lax.ppermute(x, 'row', [(i, i ^ distance) for i in range(devices)])  43.6 us
    ppermute x36, starting transfers between devices, exchange(): return lax.ppermute(x, 'row', [(i, i ^ distance) for i in range(devices)])  43.4 us
    dot_general x4, matrix products, contract_rows(): lax.dot_general(left, right, (((0,), (0,)), ((), ())), preferred_element_...  11.9 us
    another operation x28, other arithmetic, doubling_all_gather(): jnp.stack([jnp.where(low, cur, other), jnp.where(low, other, cur)], axis=...  2.71 us
  transfers between devices with their start and end apart: 36, of which 24 were waited for; matrix products, arithmetic and copies ran while one was open for 11% of the time, Pallas kernels for 0%

profile of v18, /device:TPU:0, one launch (start us, length us, event | category | flops | bytes accessed | tf_op | source)
XLA Modules:
  0.0 108.3 jit_solution(9918199389835476727)
XLA Ops:
  0.6 4.1 %collective-permute-start = (bf16[96,256]{1,0:T(8,128)(2,1)}, bf16[96,256]{1,0:T(8,128)(2,1)S(1)}, u32[]{:S(2)}, u32[]{:S(2)}) collective-permute-start(bf16[96,256]{1,0:T(8,128)(2,1)} %param.6), channel_id=1, source_target_pairs={{0,8},{1,9},{2,10},{3,11},{4,12},{5,13},{6,14},{7,15},{8,0},{9,1},... | collective-permute-start | bytes 147464 | tf_op jit(solution)/shard_map/ppermute | solution.py:16
  4.8 2.7 %collective-permute-done = bf16[96,256]{1,0:T(8,128)(2,1)S(1)} collective-permute-done((bf16[96,256]{1,0:T(8,128)(2,1)}, bf16[96,256]{1,0:T(8,128)(2,1)S(1)}, u32[]{:S(2)}, u32[]{:S(2)}) %collective-permute-start) | collective-permute-done | bytes 49184 | tf_op jit(solution)/shard_map/ppermute | solution.py:16
  7.5 0.8 select_bitcast_fusion.27
  8.4 2.2 %collective-permute-start.1 = (bf16[2,96,256]{2,1,0:T(8,128)(2,1)S(1)}, bf16[2,96,256]{2,1,0:T(8,128)(2,1)S(1)}, u32[]{:S(2)}, u32[]{:S(2)}) collective-permute-start(bf16[2,96,256]{2,1,0:T(8,128)(2,1)S(1)} %pad_maximum_fusion.12), channel_id=1, source_target_pairs={{0,4},{1,5},{2,6},{3,7},{4,0},{5,1},{6,2},{7,3},{8,12},{9,13},{10,... | collective-permute-start | bytes 294920 | tf_op jit(solution)/shard_map/ppermute | solution.py:16
  10.6 0.8 select_bitcast_fusion.25
  11.4 1.6 %collective-permute-start.9 = (bf16[2,96,256]{2,1,0:T(8,128)(2,1)S(1)}, bf16[2,96,256]{2,1,0:T(8,128)(2,1)S(1)}, u32[]{:S(2)}, u32[]{:S(2)}) collective-permute-start(bf16[2,96,256]{2,1,0:T(8,128)(2,1)S(1)} %pad_maximum_fusion.13), channel_id=1, source_target_pairs={{0,2},{1,3},{2,0},{3,1},{4,6},{5,7},{6,4},{7,5},{8,10},{9,11},{10,... | collective-permute-start | bytes 294920 | tf_op jit(solution)/shard_map/ppermute | solution.py:16
  13.0 0.5 collective-permute-done.1
  13.6 1.6 %collective-permute-start.2 = (bf16[2,2,96,256]{3,2,0,1:T(8,128)(2,1)S(1)}, bf16[2,2,96,256]{3,2,0,1:T(8,128)(2,1)S(1)}, u32[]{:S(2)}, u32[]{:S(2)}) collective-permute-start(bf16[2,2,96,256]{3,2,0,1:T(8,128)(2,1)S(1)} %pad_maximum_fusion.8), channel_id=1, source_target_pairs={{0,2},{1,3},{2,0},{3,1},{4,6},{5,7},{6,4},{7,5},{8,10},{9,11},{10,... | collective-permute-start | bytes 589832 | tf_op jit(solution)/shard_map/ppermute | solution.py:16
  15.1 1.6 %collective-permute-done.9 = bf16[2,96,256]{2,1,0:T(8,128)(2,1)S(1)} collective-permute-done((bf16[2,96,256]{2,1,0:T(8,128)(2,1)S(1)}, bf16[2,96,256]{2,1,0:T(8,128)(2,1)S(1)}, u32[]{:S(2)}, u32[]{:S(2)}) %collective-permute-start.9) | collective-permute-done | bytes 98336 | tf_op jit(solution)/shard_map/ppermute | solution.py:16
  16.8 0.7 collective-permute-start.10
  17.5 2.9 %collective-permute-done.2 = bf16[2,2,96,256]{3,2,0,1:T(8,128)(2,1)S(1)} collective-permute-done((bf16[2,2,96,256]{3,2,0,1:T(8,128)(2,1)S(1)}, bf16[2,2,96,256]{3,2,0,1:T(8,128)(2,1)S(1)}, u32[]{:S(2)}, u32[]{:S(2)}) %collective-permute-start.2) | collective-permute-done | bytes 196640 | tf_op jit(solution)/shard_map/ppermute | solution.py:16
  20.6 1.9 %collective-permute-done.10 = bf16[2,2,96,256]{3,2,1,0:T(8,128)(2,1)S(1)} collective-permute-done((bf16[2,2,96,256]{3,2,1,0:T(8,128)(2,1)S(1)}, bf16[2,2,96,256]{3,2,1,0:T(8,128)(2,1)S(1)}, u32[]{:S(2)}, u32[]{:S(2)}) %collective-permute-start.10) | collective-permute-done | bytes 196640 | tf_op jit(solution)/shard_map/ppermute | solution.py:16
  22.9 3.0 %fusion = bf16[1536,256]{0,1:T(8,128)(2,1)S(1)} fusion(bf16[1536,256]{1,0:T(8,128)(2,1)S(1)} %bitcast.236, bf16[3,512,1536]{2,1,0:T(8,128)(2,1)} %param.5), kind=kOutput, calls=%fused_computation.4 | convolution fusion | flops 805830656 | bytes 4718592 | tf_op jit(solution)/shard_map/dot_general | solution.py:10
  25.9 0.3 copy.22
  26.4 3.0 %fusion.1 = bf16[1536,256]{0,1:T(8,128)(2,1)S(1)} fusion(bf16[1536,256]{1,0:T(8,128)(2,1)S(1)} %bitcast.237, bf16[3,512,1536]{2,1,0:T(8,128)(2,1)} %param.5), kind=kOutput, calls=%fused_computation.5 | convolution fusion | flops 805830656 | bytes 4718592 | tf_op jit(solution)/shard_map/dot_general | solution.py:10
  29.4 0.3 copy.29
  29.8 0.6 collective-permute-start.4
  30.4 0.6 fusion.72
  31.0 0.5 collective-permute-start.12
  31.9 1.6 %collective-permute-start.5 = (bf16[2,2,96,256]{3,2,0,1:T(8,128)(2,1)S(1)}, bf16[2,2,96,256]{3,2,0,1:T(8,128)(2,1)S(1)}, u32[]{:S(2)}, u32[]{:S(2)}) collective-permute-start(bf16[2,2,96,256]{3,2,0,1:T(8,128)(2,1)S(1)} %fusion.54), channel_id=1, source_target_pairs={{0,2},{1,3},{2,0},{3,1},{4,6},{5,7},{6,4},{7,5},{8,10},{9,11},{10,... | collective-permute-start | bytes 589832 | tf_op jit(solution)/shard_map/ppermute | solution.py:16
  33.6 0.6 collective-permute-start.13
  34.3 4.8 %collective-permute-done.5 = bf16[2,2,96,256]{3,2,0,1:T(8,128)(2,1)S(1)} collective-permute-done((bf16[2,2,96,256]{3,2,0,1:T(8,128)(2,1)S(1)}, bf16[2,2,96,256]{3,2,0,1:T(8,128)(2,1)S(1)}, u32[]{:S(2)}, u32[]{:S(2)}) %collective-permute-start.5) | collective-permute-done | bytes 196640 | tf_op jit(solution)/shard_map/ppermute | solution.py:16
  39.2 0.7 collective-permute-start.6
  39.9 0.7 collective-permute-done.13
  40.7 1.3 %collective-permute-start.14 = (bf16[2,96,256]{2,1,0:T(8,128)(2,1)S(1)}, bf16[2,96,256]{2,1,0:T(8,128)(2,1)S(1)}, u32[]{:S(2)}, u32[]{:S(2)}) collective-permute-start(bf16[2,96,256]{2,1,0:T(8,128)(2,1)S(1)} %fusion.59), channel_id=1, source_target_pairs={{0,2},{1,3},{2,0},{3,1},{4,6},{5,7},{6,4},{7,5},{8,10},{9,11},{10,... | collective-permute-start | bytes 294920 | tf_op jit(solution)/shard_map/ppermute | solution.py:16
  42.0 1.9 %collective-permute-done.6 = bf16[2,96,256]{2,1,0:T(8,128)(2,1)S(1)} collective-permute-done((bf16[2,96,256]{2,1,0:T(8,128)(2,1)S(1)}, bf16[2,96,256]{2,1,0:T(8,128)(2,1)S(1)}, u32[]{:S(2)}, u32[]{:S(2)}) %collective-permute-start.6) | collective-permute-done | bytes 98336 | tf_op jit(solution)/shard_map/ppermute | solution.py:16
  43.9 3.7 %collective-permute-start.7 = (bf16[2,96,256]{2,1,0:T(8,128)(2,1)S(1)}, bf16[2,96,256]{2,1,0:T(8,128)(2,1)S(1)}, u32[]{:S(2)}, u32[]{:S(2)}) collective-permute-start(bf16[2,96,256]{2,1,0:T(8,128)(2,1)S(1)} %fusion.62), channel_id=1, source_target_pairs={{0,8},{1,9},{2,10},{3,11},{4,12},{5,13},{6,14},{7,15},{8,0},{9,1},... | collective-permute-start | bytes 294920 | tf_op jit(solution)/shard_map/ppermute | solution.py:16
  47.7 1.0 collective-permute-start.15
  48.7 5.0 %collective-permute-done.7 = bf16[2,96,256]{2,1,0:T(8,128)(2,1)S(1)} collective-permute-done((bf16[2,96,256]{2,1,0:T(8,128)(2,1)S(1)}, bf16[2,96,256]{2,1,0:T(8,128)(2,1)S(1)}, u32[]{:S(2)}, u32[]{:S(2)}) %collective-permute-start.7) | collective-permute-done | bytes 98336 | tf_op jit(solution)/shard_map/ppermute | solution.py:16
  53.7 1.1 collective-permute-done.15
  55.0 1.6 %collective-permute-start.19 = (bf16[2,96,256]{2,1,0:T(8,128)(2,1)S(1)}, bf16[2,96,256]{2,1,0:T(8,128)(2,1)S(1)}, u32[]{:S(2)}, u32[]{:S(2)}) collective-permute-start(bf16[2,96,256]{2,1,0:T(8,128)(2,1)S(1)} %get-tuple-element.7), channel_id=1, source_target_pairs={{0,2},{1,3},{2,0},{3,1},{4,6},{5,7},{6,4},{7,5},{8,10},{9,11},{10,... | collective-permute-start | bytes 294920 | tf_op jit(solution)/shard_map/ppermute | solution.py:16
  56.6 3.0 %collective-permute-done.16 = bf16[2,96,256]{2,1,0:T(8,128)(2,1)S(1)} collective-permute-done((bf16[2,96,256]{2,1,0:T(8,128)(2,1)S(1)}, bf16[2,96,256]{2,1,0:T(8,128)(2,1)S(1)}, u32[]{:S(2)}, u32[]{:S(2)}) %collective-permute-start.16) | collective-permute-done | bytes 98336 | tf_op jit(solution)/shard_map/ppermute | solution.py:16
  59.7 1.6 %collective-permute-start.17 = (bf16[2,2,96,256]{3,2,0,1:T(8,128)(2,1)S(1)}, bf16[2,2,96,256]{3,2,0,1:T(8,128)(2,1)S(1)}, u32[]{:S(2)}, u32[]{:S(2)}) collective-permute-start(bf16[2,2,96,256]{3,2,0,1:T(8,128)(2,1)S(1)} %pad_maximum_fusion.10), channel_id=1, source_target_pairs={{0,2},{1,3},{2,0},{3,1},{4,6},{5,7},{6,4},{7,5},{8,10},{9,11},{10,... | collective-permute-start | bytes 589832 | tf_op jit(solution)/shard_map/ppermute | solution.py:16
  61.3 1.5 %collective-permute-start.20 = (bf16[2,2,96,256]{3,2,1,0:T(8,128)(2,1)S(1)}, bf16[2,2,96,256]{3,2,1,0:T(8,128)(2,1)S(1)}, u32[]{:S(2)}, u32[]{:S(2)}) collective-permute-start(bf16[2,2,96,256]{3,2,1,0:T(8,128)(2,1)S(1)} %pad_maximum_fusion.11), channel_id=1, source_target_pairs={{0,4},{1,5},{2,6},{3,7},{4,0},{5,1},{6,2},{7,3},{8,12},{9,13},{10,... | collective-permute-start | bytes 589832 | tf_op jit(solution)/shard_map/ppermute | solution.py:16
  62.8 2.6 %collective-permute-done.17 = bf16[2,2,96,256]{3,2,0,1:T(8,128)(2,1)S(1)} collective-permute-done((bf16[2,2,96,256]{3,2,0,1:T(8,128)(2,1)S(1)}, bf16[2,2,96,256]{3,2,0,1:T(8,128)(2,1)S(1)}, u32[]{:S(2)}, u32[]{:S(2)}) %collective-permute-start.17) | collective-permute-done | bytes 196640 | tf_op jit(solution)/shard_map/ppermute | solution.py:16
  65.6 1.5 %collective-permute-done.20 = bf16[2,2,96,256]{3,2,1,0:T(8,128)(2,1)S(1)} collective-permute-done((bf16[2,2,96,256]{3,2,1,0:T(8,128)(2,1)S(1)}, bf16[2,2,96,256]{3,2,1,0:T(8,128)(2,1)S(1)}, u32[]{:S(2)}, u32[]{:S(2)}) %collective-permute-start.20) | collective-permute-done | bytes 196640 | tf_op jit(solution)/shard_map/ppermute | solution.py:16
  67.4 0.2 multiply_reduce_fusion.1
  67.7 1.3 %collective-permute-done.21 = bf16[2,2,2,96,256]{4,3,2,1,0:T(8,128)(2,1)S(1)} collective-permute-done((bf16[2,2,2,96,256]{4,3,2,1,0:T(8,128)(2,1)S(1)}, bf16[2,2,2,96,256]{4,3,2,1,0:T(8,128)(2,1)S(1)}, u32[]{:S(2)}, u32[]{:S(2)}) %collective-permute-start.21) | collective-permute-done | bytes 393248 | tf_op jit(solution)/shard_map/ppermute | solution.py:16
  69.4 3.0 %fusion.3 = bf16[1536,256]{0,1:T(8,128)(2,1)S(1)} fusion(bf16[3,512,1536]{2,1,0:T(8,128)(2,1)} %param.5, bf16[1536,256]{1,0:T(8,128)(2,1)S(1)} %bitcast.235, f32[256]{0:T(256)S(1)} %add_rsqrt_fusion.1), kind=kOutput, calls=%fused_computation.7 | convolution fusion | flops 805961728 | bytes 4719616 | tf_op jit(solution)/shard_map/dot_general | solution.py:10
  72.4 0.3 copy.40
  73.0 3.0 %fusion.2 = bf16[1536,256]{0,1:T(8,128)(2,1)S(1)} fusion(bf16[3,512,1536]{2,1,0:T(8,128)(2,1)} %param.5, bf16[1536,256]{1,0:T(8,128)(2,1)S(1)} %bitcast.234, f32[256]{0:T(256)S(1)} %add_rsqrt_fusion.1), kind=kOutput, calls=%fused_computation.6 | convolution fusion | flops 805961728 | bytes 4719616 | tf_op jit(solution)/shard_map/dot_general | solution.py:10
  76.0 0.3 copy.38
  76.3 0.4 collective-permute-start.22
  76.7 0.8 bitcast_multiply_fusion
  77.7 1.5 %collective-permute-start.27 = (bf16[2,2,96,256]{3,2,0,1:T(8,128)(2,1)S(1)}, bf16[2,2,96,256]{3,2,0,1:T(8,128)(2,1)S(1)}, u32[]{:S(2)}, u32[]{:S(2)}) collective-permute-start(bf16[2,2,96,256]{3,2,0,1:T(8,128)(2,1)S(1)} %fusion.57), channel_id=1, source_target_pairs={{0,4},{1,5},{2,6},{3,7},{4,0},{5,1},{6,2},{7,3},{8,12},{9,13},{10,... | collective-permute-start | bytes 589832 | tf_op jit(solution)/shard_map/ppermute | solution.py:16
  79.3 1.6 %collective-permute-start.23 = (bf16[2,2,96,256]{3,2,1,0:T(8,128)(2,1)S(1)}, bf16[2,2,96,256]{3,2,1,0:T(8,128)(2,1)S(1)}, u32[]{:S(2)}, u32[]{:S(2)}) collective-permute-start(bf16[2,2,96,256]{3,2,1,0:T(8,128)(2,1)S(1)} %fusion.56), channel_id=1, source_target_pairs={{0,2},{1,3},{2,0},{3,1},{4,6},{5,7},{6,4},{7,5},{8,10},{9,11},{10,... | collective-permute-start | bytes 589832 | tf_op jit(solution)/shard_map/ppermute | solution.py:16
  80.9 3.8 %collective-permute-done.27 = bf16[2,2,96,256]{3,2,0,1:T(8,128)(2,1)S(1)} collective-permute-done((bf16[2,2,96,256]{3,2,0,1:T(8,128)(2,1)S(1)}, bf16[2,2,96,256]{3,2,0,1:T(8,128)(2,1)S(1)}, u32[]{:S(2)}, u32[]{:S(2)}) %collective-permute-start.27) | collective-permute-done | bytes 196640 | tf_op jit(solution)/shard_map/ppermute | solution.py:16
  84.7 1.3 %collective-permute-start.28 = (bf16[2,96,256]{2,1,0:T(8,128)(2,1)S(1)}, bf16[2,96,256]{2,1,0:T(8,128)(2,1)S(1)}, u32[]{:S(2)}, u32[]{:S(2)}) collective-permute-start(bf16[2,96,256]{2,1,0:T(8,128)(2,1)S(1)} %fusion.61), channel_id=1, source_target_pairs={{0,2},{1,3},{2,0},{3,1},{4,6},{5,7},{6,4},{7,5},{8,10},{9,11},{10,... | collective-permute-start | bytes 294920 | tf_op jit(solution)/shard_map/ppermute | solution.py:16
  86.1 1.8 %collective-permute-start.24 = (bf16[2,96,256]{2,1,0:T(8,128)(2,1)S(1)}, bf16[2,96,256]{2,1,0:T(8,128)(2,1)S(1)}, u32[]{:S(2)}, u32[]{:S(2)}) collective-permute-start(bf16[2,96,256]{2,1,0:T(8,128)(2,1)S(1)} %fusion.60), channel_id=1, source_target_pairs={{0,4},{1,5},{2,6},{3,7},{4,0},{5,1},{6,2},{7,3},{8,12},{9,13},{10,... | collective-permute-start | bytes 294920 | tf_op jit(solution)/shard_map/ppermute | solution.py:16
  87.9 1.5 %collective-permute-done.28 = bf16[2,96,256]{2,1,0:T(8,128)(2,1)S(1)} collective-permute-done((bf16[2,96,256]{2,1,0:T(8,128)(2,1)S(1)}, bf16[2,96,256]{2,1,0:T(8,128)(2,1)S(1)}, u32[]{:S(2)}, u32[]{:S(2)}) %collective-permute-start.28) | collective-permute-done | bytes 98336 | tf_op jit(solution)/shard_map/ppermute | solution.py:16
  89.5 2.6 %collective-permute-start.29 = (bf16[96,256]{1,0:T(8,128)(2,1)S(1)}, bf16[96,256]{1,0:T(8,128)(2,1)S(1)}, u32[]{:S(2)}, u32[]{:S(2)}) collective-permute-start(bf16[96,256]{1,0:T(8,128)(2,1)S(1)} %fusion.65), channel_id=1, source_target_pairs={{0,8},{1,9},{2,10},{3,11},{4,12},{5,13},{6,14},{7,15},{8,0},{9,1},... | collective-permute-start | bytes 147464 | tf_op jit(solution)/shard_map/ppermute | solution.py:16
  92.2 2.1 %collective-permute-start.25 = (bf16[96,256]{1,0:T(8,128)(2,1)S(1)}, bf16[96,256]{1,0:T(8,128)(2,1)S(1)}, u32[]{:S(2)}, u32[]{:S(2)}) collective-permute-start(bf16[96,256]{1,0:T(8,128)(2,1)S(1)} %fusion.64), channel_id=1, source_target_pairs={{0,8},{1,9},{2,10},{3,11},{4,12},{5,13},{6,14},{7,15},{8,0},{9,1},... | collective-permute-start | bytes 147464 | tf_op jit(solution)/shard_map/ppermute | solution.py:16
  94.4 1.3 %collective-permute-done.29 = bf16[96,256]{1,0:T(8,128)(2,1)S(1)} collective-permute-done((bf16[96,256]{1,0:T(8,128)(2,1)S(1)}, bf16[96,256]{1,0:T(8,128)(2,1)S(1)}, u32[]{:S(2)}, u32[]{:S(2)}) %collective-permute-start.29) | collective-permute-done | bytes 49184 | tf_op jit(solution)/shard_map/ppermute | solution.py:16
  95.7 2.1 %collective-permute-done.25 = bf16[96,256]{1,0:T(8,128)(2,1)S(1)} collective-permute-done((bf16[96,256]{1,0:T(8,128)(2,1)S(1)}, bf16[96,256]{1,0:T(8,128)(2,1)S(1)}, u32[]{:S(2)}, u32[]{:S(2)}) %collective-permute-start.25) | collective-permute-done | bytes 49184 | tf_op jit(solution)/shard_map/ppermute | solution.py:16
  98.0 1.3 %collective-permute-start.31 = (f32[256]{0:T(256)S(1)}, f32[256]{0:T(256)S(1)}, u32[]{:S(2)}, u32[]{:S(2)}) collective-permute-start(f32[256]{0:T(256)S(1)} %add.196), channel_id=1, source_target_pairs={{0,2},{1,3},{2,0},{3,1},{4,6},{5,7},{6,4},{7,5},{8,10},{9,11},{10,... | collective-permute-start | bytes 3080 | tf_op jit(solution)/shard_map/ppermute | solution.py:16
  99.3 0.5 collective-permute-start.30
  99.8 1.1 %collective-permute-done.32 = f32[256]{0:T(256)S(1)} collective-permute-done((f32[256]{0:T(256)S(1)}, f32[256]{0:T(256)S(1)}, u32[]{:S(2)}, u32[]{:S(2)}) %collective-permute-start.32) | collective-permute-done | bytes 1056 | tf_op jit(solution)/shard_map/ppermute | solution.py:16
  101.0 0.7 collective-permute-done.31
  101.6 0.9 collective-permute-start.35
  102.5 0.8 collective-permute-start.34
  103.3 2.8 %collective-permute-start.33 = (f32[256]{0:T(256)S(1)}, f32[256]{0:T(256)S(1)}, u32[]{:S(2)}, u32[]{:S(2)}) collective-permute-start(f32[256]{0:T(256)S(1)} %add_add_fusion), channel_id=1, source_target_pairs={{0,4},{1,5},{2,6},{3,7},{4,0},{5,1},{6,2},{7,3},{8,12},{9,13},{10,... | collective-permute-start | bytes 3080 | tf_op jit(solution)/shard_map/ppermute | solution.py:16
  106.1 1.0 collective-permute-done.35
  107.1 0.6 collective-permute-done.33
  107.6 0.7 broadcast_multiply_fusion
  (95 shorter events, 4.1 us)
Async XLA Ops:
  0.6 6.9 %collective-permute-start = (bf16[96,256]{1,0:T(8,128)(2,1)}, bf16[96,256]{1,0:T(8,128)(2,1)S(1)}, u32[]{:S(2)}, u32[]{:S(2)}) collective-permute-start(bf16[96,256]{1,0:T(8,128)(2,1)} %param.6), channel_id=1, source_target_pairs={{0,8},{1,9},{2,10},{3,11},{4,12},{5,13},{6,14},{7,15},{8,0},{9,1},... | collective-permute-start | bytes 147464 | tf_op jit(solution)/shard_map/ppermute | solution.py:16
  4.7 5.9 %collective-permute-start.8 = (bf16[96,256]{1,0:T(8,128)(2,1)}, bf16[96,256]{1,0:T(8,128)(2,1)S(1)}, u32[]{:S(2)}, u32[]{:S(2)}) collective-permute-start(bf16[96,256]{1,0:T(8,128)(2,1)} %param.7), channel_id=1, source_target_pairs={{0,8},{1,9},{2,10},{3,11},{4,12},{5,13},{6,14},{7,15},{8,0},{9,1},... | collective-permute-start | bytes 147464 | tf_op jit(solution)/shard_map/ppermute | solution.py:16
  8.4 5.1 %collective-permute-start.1 = (bf16[2,96,256]{2,1,0:T(8,128)(2,1)S(1)}, bf16[2,96,256]{2,1,0:T(8,128)(2,1)S(1)}, u32[]{:S(2)}, u32[]{:S(2)}) collective-permute-start(bf16[2,96,256]{2,1,0:T(8,128)(2,1)S(1)} %pad_maximum_fusion.12), channel_id=1, source_target_pairs={{0,4},{1,5},{2,6},{3,7},{4,0},{5,1},{6,2},{7,3},{8,12},{9,13},{10,... | collective-permute-start | bytes 294920 | tf_op jit(solution)/shard_map/ppermute | solution.py:16
  11.4 5.3 %collective-permute-start.9 = (bf16[2,96,256]{2,1,0:T(8,128)(2,1)S(1)}, bf16[2,96,256]{2,1,0:T(8,128)(2,1)S(1)}, u32[]{:S(2)}, u32[]{:S(2)}) collective-permute-start(bf16[2,96,256]{2,1,0:T(8,128)(2,1)S(1)} %pad_maximum_fusion.13), channel_id=1, source_target_pairs={{0,2},{1,3},{2,0},{3,1},{4,6},{5,7},{6,4},{7,5},{8,10},{9,11},{10,... | collective-permute-start | bytes 294920 | tf_op jit(solution)/shard_map/ppermute | solution.py:16
  13.5 7.0 %copy-start = (f32[2,1536]{1,0:T(2,128)S(1)}, f32[2,1536]{1,0:T(2,128)}, u32[]{:S(2)}) copy-start(f32[2,1536]{1,0:T(2,128)} %param.8) | copy-start | bytes 36868
  13.6 6.8 %collective-permute-start.2 = (bf16[2,2,96,256]{3,2,0,1:T(8,128)(2,1)S(1)}, bf16[2,2,96,256]{3,2,0,1:T(8,128)(2,1)S(1)}, u32[]{:S(2)}, u32[]{:S(2)}) collective-permute-start(bf16[2,2,96,256]{3,2,0,1:T(8,128)(2,1)S(1)} %pad_maximum_fusion.8), channel_id=1, source_target_pairs={{0,2},{1,3},{2,0},{3,1},{4,6},{5,7},{6,4},{7,5},{8,10},{9,11},{10,... | collective-permute-start | bytes 589832 | tf_op jit(solution)/shard_map/ppermute | solution.py:16
  16.8 5.7 %collective-permute-start.10 = (bf16[2,2,96,256]{3,2,1,0:T(8,128)(2,1)S(1)}, bf16[2,2,96,256]{3,2,1,0:T(8,128)(2,1)S(1)}, u32[]{:S(2)}, u32[]{:S(2)}) collective-permute-start(bf16[2,2,96,256]{3,2,1,0:T(8,128)(2,1)S(1)} %pad_maximum_fusion.9), channel_id=1, source_target_pairs={{0,4},{1,5},{2,6},{3,7},{4,0},{5,1},{6,2},{7,3},{8,12},{9,13},{10,... | collective-permute-start | bytes 589832 | tf_op jit(solution)/shard_map/ppermute | solution.py:16
  20.5 2.2 %collective-permute-start.3 = (bf16[2,2,2,96,256]{4,3,2,1,0:T(8,128)(2,1)S(1)}, bf16[2,2,2,96,256]{4,3,2,1,0:T(8,128)(2,1)S(1)}, u32[]{:S(2)}, u32[]{:S(2)}) collective-permute-start(bf16[2,2,2,96,256]{4,3,2,1,0:T(8,128)(2,1)S(1)} %copy.43), channel_id=1, source_target_pairs={{0,1},{1,0},{2,3},{3,2},{4,5},{5,4},{6,7},{7,6},{8,9},{9,8},{10,11... | collective-permute-start | bytes 1179656 | tf_op jit(solution)/shard_map/ppermute | solution.py:16
  22.6 3.6 %collective-permute-start.11 = (bf16[2,2,2,96,256]{4,3,2,0,1:T(8,128)(2,1)S(1)}, bf16[2,2,2,96,256]{4,3,2,0,1:T(8,128)(2,1)S(1)}, u32[]{:S(2)}, u32[]{:S(2)}) collective-permute-start(bf16[2,2,2,96,256]{4,3,2,0,1:T(8,128)(2,1)S(1)} %pad_maximum_fusion.5), channel_id=1, source_target_pairs={{0,1},{1,0},{2,3},{3,2},{4,5},{5,4},{6,7},{7,6},{8,9},{9,8},{10,11... | collective-permute-start | bytes 1179656 | tf_op jit(solution)/shard_map/ppermute | solution.py:16
  29.7 0.7 copy-start.1
  29.8 1.9 %collective-permute-start.4 = (bf16[2,2,2,96,256]{4,3,0,1,2:T(8,128)(2,1)S(1)}, bf16[2,2,2,96,256]{4,3,0,1,2:T(8,128)(2,1)S(1)}, u32[]{:S(2)}, u32[]{:S(2)}) collective-permute-start(bf16[2,2,2,96,256]{4,3,0,1,2:T(8,128)(2,1)S(1)} %bitcast.239), channel_id=1, source_target_pairs={{0,1},{1,0},{2,3},{3,2},{4,5},{5,4},{6,7},{7,6},{8,9},{9,8},{10,11... | collective-permute-start | bytes 1179656 | tf_op jit(solution)/shard_map/ppermute | solution.py:16
  31.0 2.5 %collective-permute-start.12 = (bf16[2,2,2,96,256]{4,3,0,2,1:T(8,128)(2,1)S(1)}, bf16[2,2,2,96,256]{4,3,0,2,1:T(8,128)(2,1)S(1)}, u32[]{:S(2)}, u32[]{:S(2)}) collective-permute-start(bf16[2,2,2,96,256]{4,3,0,2,1:T(8,128)(2,1)S(1)} %bitcast.238), channel_id=1, source_target_pairs={{0,1},{1,0},{2,3},{3,2},{4,5},{5,4},{6,7},{7,6},{8,9},{9,8},{10,11... | collective-permute-start | bytes 1179656 | tf_op jit(solution)/shard_map/ppermute | solution.py:16
  31.9 7.2 %collective-permute-start.5 = (bf16[2,2,96,256]{3,2,0,1:T(8,128)(2,1)S(1)}, bf16[2,2,96,256]{3,2,0,1:T(8,128)(2,1)S(1)}, u32[]{:S(2)}, u32[]{:S(2)}) collective-permute-start(bf16[2,2,96,256]{3,2,0,1:T(8,128)(2,1)S(1)} %fusion.54), channel_id=1, source_target_pairs={{0,2},{1,3},{2,0},{3,1},{4,6},{5,7},{6,4},{7,5},{8,10},{9,11},{10,... | collective-permute-start | bytes 589832 | tf_op jit(solution)/shard_map/ppermute | solution.py:16
  33.6 7.0 %collective-permute-start.13 = (bf16[2,2,96,256]{3,2,0,1:T(8,128)(2,1)S(1)}, bf16[2,2,96,256]{3,2,0,1:T(8,128)(2,1)S(1)}, u32[]{:S(2)}, u32[]{:S(2)}) collective-permute-start(bf16[2,2,96,256]{3,2,0,1:T(8,128)(2,1)S(1)} %fusion.55), channel_id=1, source_target_pairs={{0,4},{1,5},{2,6},{3,7},{4,0},{5,1},{6,2},{7,3},{8,12},{9,13},{10,... | collective-permute-start | bytes 589832 | tf_op jit(solution)/shard_map/ppermute | solution.py:16
  39.2 4.7 %collective-permute-start.6 = (bf16[2,96,256]{2,1,0:T(8,128)(2,1)S(1)}, bf16[2,96,256]{2,1,0:T(8,128)(2,1)S(1)}, u32[]{:S(2)}, u32[]{:S(2)}) collective-permute-start(bf16[2,96,256]{2,1,0:T(8,128)(2,1)S(1)} %fusion.58), channel_id=1, source_target_pairs={{0,4},{1,5},{2,6},{3,7},{4,0},{5,1},{6,2},{7,3},{8,12},{9,13},{10,... | collective-permute-start | bytes 294920 | tf_op jit(solution)/shard_map/ppermute | solution.py:16
  40.7 7.0 %collective-permute-start.14 = (bf16[2,96,256]{2,1,0:T(8,128)(2,1)S(1)}, bf16[2,96,256]{2,1,0:T(8,128)(2,1)S(1)}, u32[]{:S(2)}, u32[]{:S(2)}) collective-permute-start(bf16[2,96,256]{2,1,0:T(8,128)(2,1)S(1)} %fusion.59), channel_id=1, source_target_pairs={{0,2},{1,3},{2,0},{3,1},{4,6},{5,7},{6,4},{7,5},{8,10},{9,11},{10,... | collective-permute-start | bytes 294920 | tf_op jit(solution)/shard_map/ppermute | solution.py:16
  43.9 9.8 %collective-permute-start.7 = (bf16[2,96,256]{2,1,0:T(8,128)(2,1)S(1)}, bf16[2,96,256]{2,1,0:T(8,128)(2,1)S(1)}, u32[]{:S(2)}, u32[]{:S(2)}) collective-permute-start(bf16[2,96,256]{2,1,0:T(8,128)(2,1)S(1)} %fusion.62), channel_id=1, source_target_pairs={{0,8},{1,9},{2,10},{3,11},{4,12},{5,13},{6,14},{7,15},{8,0},{9,1},... | collective-permute-start | bytes 294920 | tf_op jit(solution)/shard_map/ppermute | solution.py:16
  47.7 7.1 %collective-permute-start.15 = (bf16[2,96,256]{2,1,0:T(8,128)(2,1)S(1)}, bf16[2,96,256]{2,1,0:T(8,128)(2,1)S(1)}, u32[]{:S(2)}, u32[]{:S(2)}) collective-permute-start(bf16[2,96,256]{2,1,0:T(8,128)(2,1)S(1)} %fusion.63), channel_id=1, source_target_pairs={{0,8},{1,9},{2,10},{3,11},{4,12},{5,13},{6,14},{7,15},{8,0},{9,1},... | collective-permute-start | bytes 294920 | tf_op jit(solution)/shard_map/ppermute | solution.py:16
  55.0 4.7 %collective-permute-start.16 = (bf16[2,96,256]{2,1,0:T(8,128)(2,1)S(1)}, bf16[2,96,256]{2,1,0:T(8,128)(2,1)S(1)}, u32[]{:S(2)}, u32[]{:S(2)}) collective-permute-start(bf16[2,96,256]{2,1,0:T(8,128)(2,1)S(1)} %get-tuple-element.6), channel_id=1, source_target_pairs={{0,4},{1,5},{2,6},{3,7},{4,0},{5,1},{6,2},{7,3},{8,12},{9,13},{10,... | collective-permute-start | bytes 294920 | tf_op jit(solution)/shard_map/ppermute | solution.py:16
  55.0 6.2 %collective-permute-start.19 = (bf16[2,96,256]{2,1,0:T(8,128)(2,1)S(1)}, bf16[2,96,256]{2,1,0:T(8,128)(2,1)S(1)}, u32[]{:S(2)}, u32[]{:S(2)}) collective-permute-start(bf16[2,96,256]{2,1,0:T(8,128)(2,1)S(1)} %get-tuple-element.7), channel_id=1, source_target_pairs={{0,2},{1,3},{2,0},{3,1},{4,6},{5,7},{6,4},{7,5},{8,10},{9,11},{10,... | collective-permute-start | bytes 294920 | tf_op jit(solution)/shard_map/ppermute | solution.py:16
  59.7 5.7 %collective-permute-start.17 = (bf16[2,2,96,256]{3,2,0,1:T(8,128)(2,1)S(1)}, bf16[2,2,96,256]{3,2,0,1:T(8,128)(2,1)S(1)}, u32[]{:S(2)}, u32[]{:S(2)}) collective-permute-start(bf16[2,2,96,256]{3,2,0,1:T(8,128)(2,1)S(1)} %pad_maximum_fusion.10), channel_id=1, source_target_pairs={{0,2},{1,3},{2,0},{3,1},{4,6},{5,7},{6,4},{7,5},{8,10},{9,11},{10,... | collective-permute-start | bytes 589832 | tf_op jit(solution)/shard_map/ppermute | solution.py:16
  61.3 5.7 %collective-permute-start.20 = (bf16[2,2,96,256]{3,2,1,0:T(8,128)(2,1)S(1)}, bf16[2,2,96,256]{3,2,1,0:T(8,128)(2,1)S(1)}, u32[]{:S(2)}, u32[]{:S(2)}) collective-permute-start(bf16[2,2,96,256]{3,2,1,0:T(8,128)(2,1)S(1)} %pad_maximum_fusion.11), channel_id=1, source_target_pairs={{0,4},{1,5},{2,6},{3,7},{4,0},{5,1},{6,2},{7,3},{8,12},{9,13},{10,... | collective-permute-start | bytes 589832 | tf_op jit(solution)/shard_map/ppermute | solution.py:16
  65.5 1.8 %collective-permute-start.18 = (bf16[2,2,2,96,256]{4,3,0,1,2:T(8,128)(2,1)S(1)}, bf16[2,2,2,96,256]{4,3,0,1,2:T(8,128)(2,1)S(1)}, u32[]{:S(2)}, u32[]{:S(2)}) collective-permute-start(bf16[2,2,2,96,256]{4,3,0,1,2:T(8,128)(2,1)S(1)} %pad_maximum_fusion.6), channel_id=1, source_target_pairs={{0,1},{1,0},{2,3},{3,2},{4,5},{5,4},{6,7},{7,6},{8,9},{9,8},{10,11... | collective-permute-start | bytes 1179656 | tf_op jit(solution)/shard_map/ppermute | solution.py:16
  67.1 1.8 %collective-permute-start.21 = (bf16[2,2,2,96,256]{4,3,2,1,0:T(8,128)(2,1)S(1)}, bf16[2,2,2,96,256]{4,3,2,1,0:T(8,128)(2,1)S(1)}, u32[]{:S(2)}, u32[]{:S(2)}) collective-permute-start(bf16[2,2,2,96,256]{4,3,2,1,0:T(8,128)(2,1)S(1)} %pad_maximum_fusion.7), channel_id=1, source_target_pairs={{0,1},{1,0},{2,3},{3,2},{4,5},{5,4},{6,7},{7,6},{8,9},{9,8},{10,11... | collective-permute-start | bytes 1179656 | tf_op jit(solution)/shard_map/ppermute | solution.py:16
  72.8 4.7 %collective-permute-start.26 = (bf16[2,2,2,96,256]{4,3,0,2,1:T(8,128)(2,1)S(1)}, bf16[2,2,2,96,256]{4,3,0,2,1:T(8,128)(2,1)S(1)}, u32[]{:S(2)}, u32[]{:S(2)}) collective-permute-start(bf16[2,2,2,96,256]{4,3,0,2,1:T(8,128)(2,1)S(1)} %bitcast.240), channel_id=1, source_target_pairs={{0,1},{1,0},{2,3},{3,2},{4,5},{5,4},{6,7},{7,6},{8,9},{9,8},{10,11... | collective-permute-start | bytes 1179656 | tf_op jit(solution)/shard_map/ppermute | solution.py:16
  76.3 2.9 %collective-permute-start.22 = (bf16[2,2,2,96,256]{4,3,2,1,0:T(8,128)(2,1)S(1)}, bf16[2,2,2,96,256]{4,3,2,1,0:T(8,128)(2,1)S(1)}, u32[]{:S(2)}, u32[]{:S(2)}) collective-permute-start(bf16[2,2,2,96,256]{4,3,2,1,0:T(8,128)(2,1)S(1)} %dynamic-slice_bitcast_fusion), channel_id=1, source_target_pairs={{0,1},{1,0},{2,3},{3,2},{4,5},{5,4},{6,7},{7,6},{8,9},{9,8},{10,11... | collective-permute-start | bytes 1179656 | tf_op jit(solution)/shard_map/ppermute | solution.py:16
  77.7 7.0 %collective-permute-start.27 = (bf16[2,2,96,256]{3,2,0,1:T(8,128)(2,1)S(1)}, bf16[2,2,96,256]{3,2,0,1:T(8,128)(2,1)S(1)}, u32[]{:S(2)}, u32[]{:S(2)}) collective-permute-start(bf16[2,2,96,256]{3,2,0,1:T(8,128)(2,1)S(1)} %fusion.57), channel_id=1, source_target_pairs={{0,4},{1,5},{2,6},{3,7},{4,0},{5,1},{6,2},{7,3},{8,12},{9,13},{10,... | collective-permute-start | bytes 589832 | tf_op jit(solution)/shard_map/ppermute | solution.py:16
  79.3 6.7 %collective-permute-start.23 = (bf16[2,2,96,256]{3,2,1,0:T(8,128)(2,1)S(1)}, bf16[2,2,96,256]{3,2,1,0:T(8,128)(2,1)S(1)}, u32[]{:S(2)}, u32[]{:S(2)}) collective-permute-start(bf16[2,2,96,256]{3,2,1,0:T(8,128)(2,1)S(1)} %fusion.56), channel_id=1, source_target_pairs={{0,2},{1,3},{2,0},{3,1},{4,6},{5,7},{6,4},{7,5},{8,10},{9,11},{10,... | collective-permute-start | bytes 589832 | tf_op jit(solution)/shard_map/ppermute | solution.py:16
  84.7 4.7 %collective-permute-start.28 = (bf16[2,96,256]{2,1,0:T(8,128)(2,1)S(1)}, bf16[2,96,256]{2,1,0:T(8,128)(2,1)S(1)}, u32[]{:S(2)}, u32[]{:S(2)}) collective-permute-start(bf16[2,96,256]{2,1,0:T(8,128)(2,1)S(1)} %fusion.61), channel_id=1, source_target_pairs={{0,2},{1,3},{2,0},{3,1},{4,6},{5,7},{6,4},{7,5},{8,10},{9,11},{10,... | collective-permute-start | bytes 294920 | tf_op jit(solution)/shard_map/ppermute | solution.py:16
  86.1 6.0 %collective-permute-start.24 = (bf16[2,96,256]{2,1,0:T(8,128)(2,1)S(1)}, bf16[2,96,256]{2,1,0:T(8,128)(2,1)S(1)}, u32[]{:S(2)}, u32[]{:S(2)}) collective-permute-start(bf16[2,96,256]{2,1,0:T(8,128)(2,1)S(1)} %fusion.60), channel_id=1, source_target_pairs={{0,4},{1,5},{2,6},{3,7},{4,0},{5,1},{6,2},{7,3},{8,12},{9,13},{10,... | collective-permute-start | bytes 294920 | tf_op jit(solution)/shard_map/ppermute | solution.py:16
  89.5 6.2 %collective-permute-start.29 = (bf16[96,256]{1,0:T(8,128)(2,1)S(1)}, bf16[96,256]{1,0:T(8,128)(2,1)S(1)}, u32[]{:S(2)}, u32[]{:S(2)}) collective-permute-start(bf16[96,256]{1,0:T(8,128)(2,1)S(1)} %fusion.65), channel_id=1, source_target_pairs={{0,8},{1,9},{2,10},{3,11},{4,12},{5,13},{6,14},{7,15},{8,0},{9,1},... | collective-permute-start | bytes 147464 | tf_op jit(solution)/shard_map/ppermute | solution.py:16
  92.2 5.6 %collective-permute-start.25 = (bf16[96,256]{1,0:T(8,128)(2,1)S(1)}, bf16[96,256]{1,0:T(8,128)(2,1)S(1)}, u32[]{:S(2)}, u32[]{:S(2)}) collective-permute-start(bf16[96,256]{1,0:T(8,128)(2,1)S(1)} %fusion.64), channel_id=1, source_target_pairs={{0,8},{1,9},{2,10},{3,11},{4,12},{5,13},{6,14},{7,15},{8,0},{9,1},... | collective-permute-start | bytes 147464 | tf_op jit(solution)/shard_map/ppermute | solution.py:16
  97.9 3.1 %collective-permute-start.32 = (f32[256]{0:T(256)S(1)}, f32[256]{0:T(256)S(1)}, u32[]{:S(2)}, u32[]{:S(2)}) collective-permute-start(f32[256]{0:T(256)S(1)} %add.196), channel_id=1, source_target_pairs={{0,3},{1,2},{2,1},{3,0},{4,7},{5,6},{6,5},{7,4},{8,11},{9,10},{10,... | collective-permute-start | bytes 3080 | tf_op jit(solution)/shard_map/ppermute | solution.py:16
  98.0 3.6 %collective-permute-start.31 = (f32[256]{0:T(256)S(1)}, f32[256]{0:T(256)S(1)}, u32[]{:S(2)}, u32[]{:S(2)}) collective-permute-start(f32[256]{0:T(256)S(1)} %add.196), channel_id=1, source_target_pairs={{0,2},{1,3},{2,0},{3,1},{4,6},{5,7},{6,4},{7,5},{8,10},{9,11},{10,... | collective-permute-start | bytes 3080 | tf_op jit(solution)/shard_map/ppermute | solution.py:16
  99.3 2.3 %collective-permute-start.30 = (f32[256]{0:T(256)S(1)}, f32[256]{0:T(256)S(1)}, u32[]{:S(2)}, u32[]{:S(2)}) collective-permute-start(f32[256]{0:T(256)S(1)} %add.196), channel_id=1, source_target_pairs={{0,1},{1,0},{2,3},{3,2},{4,5},{5,4},{6,7},{7,6},{8,9},{9,8},{10,11... | collective-permute-start | bytes 3080 | tf_op jit(solution)/shard_map/ppermute | solution.py:16
  101.6 5.4 %collective-permute-start.35 = (f32[256]{0:T(256)S(1)}, f32[256]{0:T(256)S(1)}, u32[]{:S(2)}, u32[]{:S(2)}) collective-permute-start(f32[256]{0:T(256)S(1)} %add_add_fusion), channel_id=1, source_target_pairs={{0,12},{1,13},{2,14},{3,15},{4,8},{5,9},{6,10},{7,11},{8,4},{9,5},... | collective-permute-start | bytes 3080 | tf_op jit(solution)/shard_map/ppermute | solution.py:16
  102.5 4.6 %collective-permute-start.34 = (f32[256]{0:T(256)S(1)}, f32[256]{0:T(256)S(1)}, u32[]{:S(2)}, u32[]{:S(2)}) collective-permute-start(f32[256]{0:T(256)S(1)} %add_add_fusion), channel_id=1, source_target_pairs={{0,8},{1,9},{2,10},{3,11},{4,12},{5,13},{6,14},{7,15},{8,0},{9,1},... | collective-permute-start | bytes 3080 | tf_op jit(solution)/shard_map/ppermute | solution.py:16
  103.3 4.3 %collective-permute-start.33 = (f32[256]{0:T(256)S(1)}, f32[256]{0:T(256)S(1)}, u32[]{:S(2)}, u32[]{:S(2)}) collective-permute-start(f32[256]{0:T(256)S(1)} %add_add_fusion), channel_id=1, source_target_pairs={{0,4},{1,5},{2,6},{3,7},{4,0},{5,1},{6,2},{7,3},{8,12},{9,13},{10,... | collective-permute-start | bytes 3080 | tf_op jit(solution)/shard_map/ppermute | solution.py:16

commit v19 on v18

--- a/solution.py
+++ b/solution.py
@@ -52,8 +52,9 @@
     return cur.reshape((-1, x.shape[-1]))
 
 
-def doubling_all_reduce(x, devices):
-    bits = devices.bit_length() - 1
+def doubling_all_reduce(x, devices, bits=None):
+    if bits is None:
+        bits = devices.bit_length() - 1
     low = 0
     while low < bits:
         width = 2 if low + 1 < bits else 1
@@ -92,14 +93,11 @@
                 contract_rows(panels[sector + 1], projected.astype(jnp.bfloat16)).astype(jnp.bfloat16)
             )
         last = sector + 1 == SECTORS
-        rot_amp = halving_reduce_scatter(halves[0], devices, order_amp, keep_pair=not last)
-        rot_der = halving_reduce_scatter(halves[1], devices, order_der, keep_pair=not last)
-        if last:
-            blocks = [first_row]
-        else:
-            pair_bit = order_amp[-1]
-            base = lax.axis_index("row") & ~(1 << pair_bit)
-            blocks = [base * chan_rows, (base | (1 << pair_bit)) * chan_rows]
+        rot_amp = halving_reduce_scatter(halves[0], devices, order_amp, keep_pair=True)
+        rot_der = halving_reduce_scatter(halves[1], devices, order_der, keep_pair=True)
+        pair_bit = order_amp[-1]
+        base = lax.axis_index("row") & ~(1 << pair_bit)
+        blocks = [base * chan_rows, (base | (1 << pair_bit)) * chan_rows]
         angle_rows = jnp.stack(
             [lax.dynamic_slice_in_dim(phase[sector], b, chan_rows, 0) for b in blocks]
         ).reshape(rot_amp.shape[:-1] + (1,))
@@ -122,8 +120,11 @@
             der_wide = der_full.astype(jnp.float32)
             norm = jnp.sum(amp_wide * amp_wide, axis=0) + jnp.sum(der_wide * der_wide, axis=0)
         else:
-            local_norm = jnp.sum(new_amp * new_amp, axis=0) + jnp.sum(new_der * new_der, axis=0)
-            norm = doubling_all_reduce(local_norm, devices)
+            local_norm = jnp.sum(new_amp * new_amp, axis=(0, 1)) + jnp.sum(new_der * new_der, axis=(0, 1))
+            norm = doubling_all_reduce(local_norm, devices, bits=pair_bit)
+            mine = (lax.axis_index("row") >> pair_bit) & 1
+            new_amp = lax.dynamic_index_in_dim(new_amp, mine, axis=0, keepdims=False)
+            new_der = lax.dynamic_index_in_dim(new_der, mine, axis=0, keepdims=False)
         scale = 1.0 / jnp.sqrt(norm / (2.0 * all_channels) + 1e-06)
     return (new_amp * scale[None, :], new_der * scale[None, :])
 

time: 109 us -> 109 us (level)
  waiting for transfers between devices: 43.6 us -> 48.9 us
  starting transfers between devices: 43.4 us -> 38.9 us
    ppermute x36 -> x34, waiting for transfers between devices: 43.6 us -> 48.9 us  [exchange(): return lax.ppermute(x, 'row', [(i, i ^ distance) for i in range(devices)])]
    ppermute x36 -> x34, starting transfers between devices: 43.4 us -> 38.9 us  [exchange(): return lax.ppermute(x, 'row', [(i, i ^ distance) for i in range(devices)])]
  transfers between devices with their start and end apart: 36 -> 34, of which waited for: 24 -> 24; matrix products, arithmetic and copies ran while one was open for 11% -> 10% of each run, Pallas kernels for 0% -> 0%
where the time goes in v19:
time: 109 us
  waiting for transfers between devices  48.9 us (45%)
  starting transfers between devices  38.9 us (36%)
  matrix products  11.9 us (11%)
  other arithmetic  4.9 us (4%)
  local copies, waits for them, and re-layouts  3.24 us (3%)
  between operations  1.23 us (1%)
    ppermute x34, waiting for transfers between devices, exchange(): return lax.ppermute(x, 'row', [(i, i ^ distance) for i in range(devices)])  48.9 us
    ppermute x34, starting transfers between devices, exchange(): return lax.ppermute(x, 'row', [(i, i ^ distance) for i in range(devices)])  38.9 us
    dot_general x4, matrix products, contract_rows(): lax.dot_general(left, right, (((0,), (0,)), ((), ())), preferred_element_...  11.9 us
    another operation x28, other arithmetic, doubling_all_gather(): jnp.stack([jnp.where(low, cur, other), jnp.where(low, other, cur)], axis=...  2.71 us
  transfers between devices with their start and end apart: 34, of which 24 were waited for; matrix products, arithmetic and copies ran while one was open for 10% of the time, Pallas kernels for 0%

profile of v19, /device:TPU:0, one launch (start us, length us, event | category | flops | bytes accessed | tf_op | source)
XLA Modules:
  0.0 109.0 jit_solution(17153391009325330150)
XLA Ops:
  0.6 4.1 %collective-permute-start = (bf16[96,256]{1,0:T(8,128)(2,1)}, bf16[96,256]{1,0:T(8,128)(2,1)S(1)}, u32[]{:S(2)}, u32[]{:S(2)}) collective-permute-start(bf16[96,256]{1,0:T(8,128)(2,1)} %param.6), channel_id=1, source_target_pairs={{0,8},{1,9},{2,10},{3,11},{4,12},{5,13},{6,14},{7,15},{8,0},{9,1},... | collective-permute-start | bytes 147464 | tf_op jit(solution)/shard_map/ppermute | solution.py:16
  4.8 2.7 %collective-permute-done = bf16[96,256]{1,0:T(8,128)(2,1)S(1)} collective-permute-done((bf16[96,256]{1,0:T(8,128)(2,1)}, bf16[96,256]{1,0:T(8,128)(2,1)S(1)}, u32[]{:S(2)}, u32[]{:S(2)}) %collective-permute-start) | collective-permute-done | bytes 49184 | tf_op jit(solution)/shard_map/ppermute | solution.py:16
  7.5 0.8 select_bitcast_fusion.27
  8.4 2.2 %collective-permute-start.1 = (bf16[2,96,256]{2,1,0:T(8,128)(2,1)S(1)}, bf16[2,96,256]{2,1,0:T(8,128)(2,1)S(1)}, u32[]{:S(2)}, u32[]{:S(2)}) collective-permute-start(bf16[2,96,256]{2,1,0:T(8,128)(2,1)S(1)} %pad_maximum_fusion.12), channel_id=1, source_target_pairs={{0,4},{1,5},{2,6},{3,7},{4,0},{5,1},{6,2},{7,3},{8,12},{9,13},{10,... | collective-permute-start | bytes 294920 | tf_op jit(solution)/shard_map/ppermute | solution.py:16
  10.6 0.8 select_bitcast_fusion.25
  11.4 1.6 %collective-permute-start.9 = (bf16[2,96,256]{2,1,0:T(8,128)(2,1)S(1)}, bf16[2,96,256]{2,1,0:T(8,128)(2,1)S(1)}, u32[]{:S(2)}, u32[]{:S(2)}) collective-permute-start(bf16[2,96,256]{2,1,0:T(8,128)(2,1)S(1)} %pad_maximum_fusion.13), channel_id=1, source_target_pairs={{0,2},{1,3},{2,0},{3,1},{4,6},{5,7},{6,4},{7,5},{8,10},{9,11},{10,... | collective-permute-start | bytes 294920 | tf_op jit(solution)/shard_map/ppermute | solution.py:16
  13.0 0.5 collective-permute-done.1
  13.6 1.6 %collective-permute-start.2 = (bf16[2,2,96,256]{3,2,0,1:T(8,128)(2,1)S(1)}, bf16[2,2,96,256]{3,2,0,1:T(8,128)(2,1)S(1)}, u32[]{:S(2)}, u32[]{:S(2)}) collective-permute-start(bf16[2,2,96,256]{3,2,0,1:T(8,128)(2,1)S(1)} %pad_maximum_fusion.8), channel_id=1, source_target_pairs={{0,2},{1,3},{2,0},{3,1},{4,6},{5,7},{6,4},{7,5},{8,10},{9,11},{10,... | collective-permute-start | bytes 589832 | tf_op jit(solution)/shard_map/ppermute | solution.py:16
  15.1 1.6 %collective-permute-done.9 = bf16[2,96,256]{2,1,0:T(8,128)(2,1)S(1)} collective-permute-done((bf16[2,96,256]{2,1,0:T(8,128)(2,1)S(1)}, bf16[2,96,256]{2,1,0:T(8,128)(2,1)S(1)}, u32[]{:S(2)}, u32[]{:S(2)}) %collective-permute-start.9) | collective-permute-done | bytes 98336 | tf_op jit(solution)/shard_map/ppermute | solution.py:16
  16.8 0.7 collective-permute-start.10
  17.5 2.9 %collective-permute-done.2 = bf16[2,2,96,256]{3,2,0,1:T(8,128)(2,1)S(1)} collective-permute-done((bf16[2,2,96,256]{3,2,0,1:T(8,128)(2,1)S(1)}, bf16[2,2,96,256]{3,2,0,1:T(8,128)(2,1)S(1)}, u32[]{:S(2)}, u32[]{:S(2)}) %collective-permute-start.2) | collective-permute-done | bytes 196640 | tf_op jit(solution)/shard_map/ppermute | solution.py:16
  20.6 1.9 %collective-permute-done.10 = bf16[2,2,96,256]{3,2,1,0:T(8,128)(2,1)S(1)} collective-permute-done((bf16[2,2,96,256]{3,2,1,0:T(8,128)(2,1)S(1)}, bf16[2,2,96,256]{3,2,1,0:T(8,128)(2,1)S(1)}, u32[]{:S(2)}, u32[]{:S(2)}) %collective-permute-start.10) | collective-permute-done | bytes 196640 | tf_op jit(solution)/shard_map/ppermute | solution.py:16
  22.7 0.2 select_bitcast_fusion.7
  22.9 3.0 %fusion = bf16[1536,256]{0,1:T(8,128)(2,1)S(1)} fusion(bf16[1536,256]{1,0:T(8,128)(2,1)S(1)} %bitcast.224, bf16[3,512,1536]{2,1,0:T(8,128)(2,1)} %param.5), kind=kOutput, calls=%fused_computation.4 | convolution fusion | flops 805830656 | bytes 4718592 | tf_op jit(solution)/shard_map/dot_general | solution.py:10
  25.9 0.3 copy.22
  26.4 3.0 %fusion.1 = bf16[1536,256]{0,1:T(8,128)(2,1)S(1)} fusion(bf16[1536,256]{1,0:T(8,128)(2,1)S(1)} %bitcast.226, bf16[3,512,1536]{2,1,0:T(8,128)(2,1)} %param.5), kind=kOutput, calls=%fused_computation.5 | convolution fusion | flops 805830656 | bytes 4718592 | tf_op jit(solution)/shard_map/dot_general | solution.py:10
  29.4 0.3 copy.29
  29.8 0.6 collective-permute-start.12
  30.4 0.6 constant_dynamic-slice_fusion.11
  31.1 0.5 collective-permute-start.4
  31.9 0.7 collective-permute-start.13
  32.6 0.4 collective-permute-done.4
  33.1 1.6 %collective-permute-start.5 = (bf16[2,2,96,256]{3,2,0,1:T(8,128)(2,1)S(1)}, bf16[2,2,96,256]{3,2,0,1:T(8,128)(2,1)S(1)}, u32[]{:S(2)}, u32[]{:S(2)}) collective-permute-start(bf16[2,2,96,256]{3,2,0,1:T(8,128)(2,1)S(1)} %fusion.54), channel_id=1, source_target_pairs={{0,2},{1,3},{2,0},{3,1},{4,6},{5,7},{6,4},{7,5},{8,10},{9,11},{10,... | collective-permute-start | bytes 589832 | tf_op jit(solution)/shard_map/ppermute | solution.py:16
  34.7 4.4 %collective-permute-done.13 = bf16[2,2,96,256]{3,2,0,1:T(8,128)(2,1)S(1)} collective-permute-done((bf16[2,2,96,256]{3,2,0,1:T(8,128)(2,1)S(1)}, bf16[2,2,96,256]{3,2,0,1:T(8,128)(2,1)S(1)}, u32[]{:S(2)}, u32[]{:S(2)}) %collective-permute-start.13) | collective-permute-done | bytes 196640 | tf_op jit(solution)/shard_map/ppermute | solution.py:16
  39.2 1.6 %collective-permute-start.14 = (bf16[2,96,256]{2,1,0:T(8,128)(2,1)S(1)}, bf16[2,96,256]{2,1,0:T(8,128)(2,1)S(1)}, u32[]{:S(2)}, u32[]{:S(2)}) collective-permute-start(bf16[2,96,256]{2,1,0:T(8,128)(2,1)S(1)} %fusion.59), channel_id=1, source_target_pairs={{0,2},{1,3},{2,0},{3,1},{4,6},{5,7},{6,4},{7,5},{8,10},{9,11},{10,... | collective-permute-start | bytes 294920 | tf_op jit(solution)/shard_map/ppermute | solution.py:16
  40.9 0.6 collective-permute-start.6
  41.5 2.3 %collective-permute-done.14 = bf16[2,96,256]{2,1,0:T(8,128)(2,1)S(1)} collective-permute-done((bf16[2,96,256]{2,1,0:T(8,128)(2,1)S(1)}, bf16[2,96,256]{2,1,0:T(8,128)(2,1)S(1)}, u32[]{:S(2)}, u32[]{:S(2)}) %collective-permute-start.14) | collective-permute-done | bytes 98336 | tf_op jit(solution)/shard_map/ppermute | solution.py:16
  43.9 3.3 %collective-permute-start.15 = (bf16[2,96,256]{2,1,0:T(8,128)(2,1)S(1)}, bf16[2,96,256]{2,1,0:T(8,128)(2,1)S(1)}, u32[]{:S(2)}, u32[]{:S(2)}) collective-permute-start(bf16[2,96,256]{2,1,0:T(8,128)(2,1)S(1)} %fusion.63), channel_id=1, source_target_pairs={{0,8},{1,9},{2,10},{3,11},{4,12},{5,13},{6,14},{7,15},{8,0},{9,1},... | collective-permute-start | bytes 294920 | tf_op jit(solution)/shard_map/ppermute | solution.py:16
  47.3 2.0 %collective-permute-start.7 = (bf16[2,96,256]{2,1,0:T(8,128)(2,1)S(1)}, bf16[2,96,256]{2,1,0:T(8,128)(2,1)S(1)}, u32[]{:S(2)}, u32[]{:S(2)}) collective-permute-start(bf16[2,96,256]{2,1,0:T(8,128)(2,1)S(1)} %fusion.62), channel_id=1, source_target_pairs={{0,8},{1,9},{2,10},{3,11},{4,12},{5,13},{6,14},{7,15},{8,0},{9,1},... | collective-permute-start | bytes 294920 | tf_op jit(solution)/shard_map/ppermute | solution.py:16
  49.4 4.5 %collective-permute-done.15 = bf16[2,96,256]{2,1,0:T(8,128)(2,1)S(1)} collective-permute-done((bf16[2,96,256]{2,1,0:T(8,128)(2,1)S(1)}, bf16[2,96,256]{2,1,0:T(8,128)(2,1)S(1)}, u32[]{:S(2)}, u32[]{:S(2)}) %collective-permute-start.15) | collective-permute-done | bytes 98336 | tf_op jit(solution)/shard_map/ppermute | solution.py:16
  53.9 1.1 collective-permute-done.7
  55.2 1.5 %collective-permute-start.19 = (bf16[2,96,256]{2,1,0:T(8,128)(2,1)S(1)}, bf16[2,96,256]{2,1,0:T(8,128)(2,1)S(1)}, u32[]{:S(2)}, u32[]{:S(2)}) collective-permute-start(bf16[2,96,256]{2,1,0:T(8,128)(2,1)S(1)} %get-tuple-element.9), channel_id=1, source_target_pairs={{0,2},{1,3},{2,0},{3,1},{4,6},{5,7},{6,4},{7,5},{8,10},{9,11},{10,... | collective-permute-start | bytes 294920 | tf_op jit(solution)/shard_map/ppermute | solution.py:16
  56.7 3.1 %collective-permute-done.16 = bf16[2,96,256]{2,1,0:T(8,128)(2,1)S(1)} collective-permute-done((bf16[2,96,256]{2,1,0:T(8,128)(2,1)S(1)}, bf16[2,96,256]{2,1,0:T(8,128)(2,1)S(1)}, u32[]{:S(2)}, u32[]{:S(2)}) %collective-permute-start.16) | collective-permute-done | bytes 98336 | tf_op jit(solution)/shard_map/ppermute | solution.py:16
  59.9 1.5 %collective-permute-start.17 = (bf16[2,2,96,256]{3,2,0,1:T(8,128)(2,1)S(1)}, bf16[2,2,96,256]{3,2,0,1:T(8,128)(2,1)S(1)}, u32[]{:S(2)}, u32[]{:S(2)}) collective-permute-start(bf16[2,2,96,256]{3,2,0,1:T(8,128)(2,1)S(1)} %pad_maximum_fusion.10), channel_id=1, source_target_pairs={{0,2},{1,3},{2,0},{3,1},{4,6},{5,7},{6,4},{7,5},{8,10},{9,11},{10,... | collective-permute-start | bytes 589832 | tf_op jit(solution)/shard_map/ppermute | solution.py:16
  61.4 1.6 %collective-permute-start.20 = (bf16[2,2,96,256]{3,2,1,0:T(8,128)(2,1)S(1)}, bf16[2,2,96,256]{3,2,1,0:T(8,128)(2,1)S(1)}, u32[]{:S(2)}, u32[]{:S(2)}) collective-permute-start(bf16[2,2,96,256]{3,2,1,0:T(8,128)(2,1)S(1)} %pad_maximum_fusion.11), channel_id=1, source_target_pairs={{0,4},{1,5},{2,6},{3,7},{4,0},{5,1},{6,2},{7,3},{8,12},{9,13},{10,... | collective-permute-start | bytes 589832 | tf_op jit(solution)/shard_map/ppermute | solution.py:16
  63.0 2.6 %collective-permute-done.17 = bf16[2,2,96,256]{3,2,0,1:T(8,128)(2,1)S(1)} collective-permute-done((bf16[2,2,96,256]{3,2,0,1:T(8,128)(2,1)S(1)}, bf16[2,2,96,256]{3,2,0,1:T(8,128)(2,1)S(1)}, u32[]{:S(2)}, u32[]{:S(2)}) %collective-permute-start.17) | collective-permute-done | bytes 196640 | tf_op jit(solution)/shard_map/ppermute | solution.py:16
  65.8 1.4 %collective-permute-done.20 = bf16[2,2,96,256]{3,2,1,0:T(8,128)(2,1)S(1)} collective-permute-done((bf16[2,2,96,256]{3,2,1,0:T(8,128)(2,1)S(1)}, bf16[2,2,96,256]{3,2,1,0:T(8,128)(2,1)S(1)}, u32[]{:S(2)}, u32[]{:S(2)}) %collective-permute-start.20) | collective-permute-done | bytes 196640 | tf_op jit(solution)/shard_map/ppermute | solution.py:16
  67.3 0.2 collective-permute-done.18
  67.5 0.2 multiply_reduce_fusion.1
  67.8 1.1 %collective-permute-done.21 = bf16[2,2,2,96,256]{4,3,2,1,0:T(8,128)(2,1)S(1)} collective-permute-done((bf16[2,2,2,96,256]{4,3,2,1,0:T(8,128)(2,1)S(1)}, bf16[2,2,2,96,256]{4,3,2,1,0:T(8,128)(2,1)S(1)}, u32[]{:S(2)}, u32[]{:S(2)}) %collective-permute-start.21) | collective-permute-done | bytes 393248 | tf_op jit(solution)/shard_map/ppermute | solution.py:16
  69.0 0.2 multiply_reduce_fusion
  69.4 3.0 %fusion.2 = bf16[1536,256]{0,1:T(8,128)(2,1)S(1)} fusion(bf16[3,512,1536]{2,1,0:T(8,128)(2,1)} %param.5, bf16[1536,256]{1,0:T(8,128)(2,1)S(1)} %bitcast.223, f32[256]{0:T(256)S(1)} %add_rsqrt_fusion.1), kind=kOutput, calls=%fused_computation.6 | convolution fusion | flops 805961728 | bytes 4719616 | tf_op jit(solution)/shard_map/dot_general | solution.py:10
  72.4 0.3 copy.38
  72.7 0.8 dynamic-slice_bitcast_fusion
  73.7 3.0 %fusion.3 = bf16[1536,256]{0,1:T(8,128)(2,1)S(1)} fusion(bf16[3,512,1536]{2,1,0:T(8,128)(2,1)} %param.5, bf16[1536,256]{1,0:T(8,128)(2,1)S(1)} %bitcast.225, f32[256]{0:T(256)S(1)} %add_rsqrt_fusion.1), kind=kOutput, calls=%fused_computation.7 | convolution fusion | flops 805961728 | bytes 4719616 | tf_op jit(solution)/shard_map/dot_general | solution.py:10
  76.6 0.3 copy.40
  77.0 0.5 collective-permute-start.26
  77.6 1.0 collective-permute-start.23
  78.6 0.2 collective-permute-done.26
  79.0 1.9 %collective-permute-start.27 = (bf16[2,2,96,256]{3,2,0,1:T(8,128)(2,1)S(1)}, bf16[2,2,96,256]{3,2,0,1:T(8,128)(2,1)S(1)}, u32[]{:S(2)}, u32[]{:S(2)}) collective-permute-start(bf16[2,2,96,256]{3,2,0,1:T(8,128)(2,1)S(1)} %fusion.57), channel_id=1, source_target_pairs={{0,4},{1,5},{2,6},{3,7},{4,0},{5,1},{6,2},{7,3},{8,12},{9,13},{10,... | collective-permute-start | bytes 589832 | tf_op jit(solution)/shard_map/ppermute | solution.py:16
  80.8 3.8 %collective-permute-done.23 = bf16[2,2,96,256]{3,2,1,0:T(8,128)(2,1)S(1)} collective-permute-done((bf16[2,2,96,256]{3,2,1,0:T(8,128)(2,1)S(1)}, bf16[2,2,96,256]{3,2,1,0:T(8,128)(2,1)S(1)}, u32[]{:S(2)}, u32[]{:S(2)}) %collective-permute-start.23) | collective-permute-done | bytes 196640 | tf_op jit(solution)/shard_map/ppermute | solution.py:16
  84.7 1.6 %collective-permute-start.24 = (bf16[2,96,256]{2,1,0:T(8,128)(2,1)S(1)}, bf16[2,96,256]{2,1,0:T(8,128)(2,1)S(1)}, u32[]{:S(2)}, u32[]{:S(2)}) collective-permute-start(bf16[2,96,256]{2,1,0:T(8,128)(2,1)S(1)} %fusion.60), channel_id=1, source_target_pairs={{0,4},{1,5},{2,6},{3,7},{4,0},{5,1},{6,2},{7,3},{8,12},{9,13},{10,... | collective-permute-start | bytes 294920 | tf_op jit(solution)/shard_map/ppermute | solution.py:16
  86.4 1.5 %collective-permute-start.28 = (bf16[2,96,256]{2,1,0:T(8,128)(2,1)S(1)}, bf16[2,96,256]{2,1,0:T(8,128)(2,1)S(1)}, u32[]{:S(2)}, u32[]{:S(2)}) collective-permute-start(bf16[2,96,256]{2,1,0:T(8,128)(2,1)S(1)} %fusion.61), channel_id=1, source_target_pairs={{0,2},{1,3},{2,0},{3,1},{4,6},{5,7},{6,4},{7,5},{8,10},{9,11},{10,... | collective-permute-start | bytes 294920 | tf_op jit(solution)/shard_map/ppermute | solution.py:16
  87.9 1.5 %collective-permute-done.24 = bf16[2,96,256]{2,1,0:T(8,128)(2,1)S(1)} collective-permute-done((bf16[2,96,256]{2,1,0:T(8,128)(2,1)S(1)}, bf16[2,96,256]{2,1,0:T(8,128)(2,1)S(1)}, u32[]{:S(2)}, u32[]{:S(2)}) %collective-permute-start.24) | collective-permute-done | bytes 98336 | tf_op jit(solution)/shard_map/ppermute | solution.py:16
  89.4 2.6 %collective-permute-start.25 = (bf16[2,96,256]{2,1,0:T(8,128)(2,1)S(1)}, bf16[2,96,256]{2,1,0:T(8,128)(2,1)S(1)}, u32[]{:S(2)}, u32[]{:S(2)}) collective-permute-start(bf16[2,96,256]{2,1,0:T(8,128)(2,1)S(1)} %fusion.64), channel_id=1, source_target_pairs={{0,8},{1,9},{2,10},{3,11},{4,12},{5,13},{6,14},{7,15},{8,0},{9,1},... | collective-permute-start | bytes 294920 | tf_op jit(solution)/shard_map/ppermute | solution.py:16
  92.0 1.6 %collective-permute-start.29 = (bf16[2,96,256]{2,1,0:T(8,128)(2,1)S(1)}, bf16[2,96,256]{2,1,0:T(8,128)(2,1)S(1)}, u32[]{:S(2)}, u32[]{:S(2)}) collective-permute-start(bf16[2,96,256]{2,1,0:T(8,128)(2,1)S(1)} %fusion.65), channel_id=1, source_target_pairs={{0,8},{1,9},{2,10},{3,11},{4,12},{5,13},{6,14},{7,15},{8,0},{9,1},... | collective-permute-start | bytes 294920 | tf_op jit(solution)/shard_map/ppermute | solution.py:16
  93.6 5.1 %collective-permute-done.25 = bf16[2,96,256]{2,1,0:T(8,128)(2,1)S(1)} collective-permute-done((bf16[2,96,256]{2,1,0:T(8,128)(2,1)S(1)}, bf16[2,96,256]{2,1,0:T(8,128)(2,1)S(1)}, u32[]{:S(2)}, u32[]{:S(2)}) %collective-permute-start.25) | collective-permute-done | bytes 98336 | tf_op jit(solution)/shard_map/ppermute | solution.py:16
  98.7 1.1 collective-permute-done.29
  99.7 0.2 multiply_reduce_fusion.2
  100.0 1.7 %collective-permute-start.31 = (f32[256]{0:T(256)S(1)}, f32[256]{0:T(256)S(1)}, u32[]{:S(2)}, u32[]{:S(2)}) collective-permute-start(f32[256]{0:T(256)S(1)} %add.183), channel_id=1, source_target_pairs={{0,2},{1,3},{2,0},{3,1},{4,6},{5,7},{6,4},{7,5},{8,10},{9,11},{10,... | collective-permute-start | bytes 3080 | tf_op jit(solution)/shard_map/ppermute | solution.py:16
  101.9 1.8 %collective-permute-done.31 = f32[256]{0:T(256)S(1)} collective-permute-done((f32[256]{0:T(256)S(1)}, f32[256]{0:T(256)S(1)}, u32[]{:S(2)}, u32[]{:S(2)}) %collective-permute-start.31) | collective-permute-done | bytes 1056 | tf_op jit(solution)/shard_map/ppermute | solution.py:16
  103.6 1.1 collective-permute-done.32
  104.7 3.6 %collective-permute-done.33 = f32[256]{0:T(256)S(1)} collective-permute-done((f32[256]{0:T(256)S(1)}, f32[256]{0:T(256)S(1)}, u32[]{:S(2)}, u32[]{:S(2)}) %collective-permute-start.33) | collective-permute-done | bytes 1056 | tf_op jit(solution)/shard_map/ppermute | solution.py:16
  108.3 0.7 bitcast_multiply_fusion
  (93 shorter events, 3.4 us)
Async XLA Ops:
  0.6 6.9 %collective-permute-start = (bf16[96,256]{1,0:T(8,128)(2,1)}, bf16[96,256]{1,0:T(8,128)(2,1)S(1)}, u32[]{:S(2)}, u32[]{:S(2)}) collective-permute-start(bf16[96,256]{1,0:T(8,128)(2,1)} %param.6), channel_id=1, source_target_pairs={{0,8},{1,9},{2,10},{3,11},{4,12},{5,13},{6,14},{7,15},{8,0},{9,1},... | collective-permute-start | bytes 147464 | tf_op jit(solution)/shard_map/ppermute | solution.py:16
  4.7 5.9 %collective-permute-start.8 = (bf16[96,256]{1,0:T(8,128)(2,1)}, bf16[96,256]{1,0:T(8,128)(2,1)S(1)}, u32[]{:S(2)}, u32[]{:S(2)}) collective-permute-start(bf16[96,256]{1,0:T(8,128)(2,1)} %param.7), channel_id=1, source_target_pairs={{0,8},{1,9},{2,10},{3,11},{4,12},{5,13},{6,14},{7,15},{8,0},{9,1},... | collective-permute-start | bytes 147464 | tf_op jit(solution)/shard_map/ppermute | solution.py:16
  8.4 5.1 %collective-permute-start.1 = (bf16[2,96,256]{2,1,0:T(8,128)(2,1)S(1)}, bf16[2,96,256]{2,1,0:T(8,128)(2,1)S(1)}, u32[]{:S(2)}, u32[]{:S(2)}) collective-permute-start(bf16[2,96,256]{2,1,0:T(8,128)(2,1)S(1)} %pad_maximum_fusion.12), channel_id=1, source_target_pairs={{0,4},{1,5},{2,6},{3,7},{4,0},{5,1},{6,2},{7,3},{8,12},{9,13},{10,... | collective-permute-start | bytes 294920 | tf_op jit(solution)/shard_map/ppermute | solution.py:16
  11.4 5.3 %collective-permute-start.9 = (bf16[2,96,256]{2,1,0:T(8,128)(2,1)S(1)}, bf16[2,96,256]{2,1,0:T(8,128)(2,1)S(1)}, u32[]{:S(2)}, u32[]{:S(2)}) collective-permute-start(bf16[2,96,256]{2,1,0:T(8,128)(2,1)S(1)} %pad_maximum_fusion.13), channel_id=1, source_target_pairs={{0,2},{1,3},{2,0},{3,1},{4,6},{5,7},{6,4},{7,5},{8,10},{9,11},{10,... | collective-permute-start | bytes 294920 | tf_op jit(solution)/shard_map/ppermute | solution.py:16
  13.5 7.0 %copy-start = (f32[2,1536]{1,0:T(2,128)S(1)}, f32[2,1536]{1,0:T(2,128)}, u32[]{:S(2)}) copy-start(f32[2,1536]{1,0:T(2,128)} %param.8) | copy-start | bytes 36868
  13.6 6.8 %collective-permute-start.2 = (bf16[2,2,96,256]{3,2,0,1:T(8,128)(2,1)S(1)}, bf16[2,2,96,256]{3,2,0,1:T(8,128)(2,1)S(1)}, u32[]{:S(2)}, u32[]{:S(2)}) collective-permute-start(bf16[2,2,96,256]{3,2,0,1:T(8,128)(2,1)S(1)} %pad_maximum_fusion.8), channel_id=1, source_target_pairs={{0,2},{1,3},{2,0},{3,1},{4,6},{5,7},{6,4},{7,5},{8,10},{9,11},{10,... | collective-permute-start | bytes 589832 | tf_op jit(solution)/shard_map/ppermute | solution.py:16
  16.8 5.7 %collective-permute-start.10 = (bf16[2,2,96,256]{3,2,1,0:T(8,128)(2,1)S(1)}, bf16[2,2,96,256]{3,2,1,0:T(8,128)(2,1)S(1)}, u32[]{:S(2)}, u32[]{:S(2)}) collective-permute-start(bf16[2,2,96,256]{3,2,1,0:T(8,128)(2,1)S(1)} %pad_maximum_fusion.9), channel_id=1, source_target_pairs={{0,4},{1,5},{2,6},{3,7},{4,0},{5,1},{6,2},{7,3},{8,12},{9,13},{10,... | collective-permute-start | bytes 589832 | tf_op jit(solution)/shard_map/ppermute | solution.py:16
  20.5 2.2 %collective-permute-start.3 = (bf16[2,2,2,96,256]{4,3,2,1,0:T(8,128)(2,1)S(1)}, bf16[2,2,2,96,256]{4,3,2,1,0:T(8,128)(2,1)S(1)}, u32[]{:S(2)}, u32[]{:S(2)}) collective-permute-start(bf16[2,2,2,96,256]{4,3,2,1,0:T(8,128)(2,1)S(1)} %copy.43), channel_id=1, source_target_pairs={{0,1},{1,0},{2,3},{3,2},{4,5},{5,4},{6,7},{7,6},{8,9},{9,8},{10,11... | collective-permute-start | bytes 1179656 | tf_op jit(solution)/shard_map/ppermute | solution.py:16
  22.6 3.6 %collective-permute-start.11 = (bf16[2,2,2,96,256]{4,3,2,0,1:T(8,128)(2,1)S(1)}, bf16[2,2,2,96,256]{4,3,2,0,1:T(8,128)(2,1)S(1)}, u32[]{:S(2)}, u32[]{:S(2)}) collective-permute-start(bf16[2,2,2,96,256]{4,3,2,0,1:T(8,128)(2,1)S(1)} %pad_maximum_fusion.5), channel_id=1, source_target_pairs={{0,1},{1,0},{2,3},{3,2},{4,5},{5,4},{6,7},{7,6},{8,9},{9,8},{10,11... | collective-permute-start | bytes 1179656 | tf_op jit(solution)/shard_map/ppermute | solution.py:16
  29.7 0.7 copy-start.1
  29.8 1.9 %collective-permute-start.12 = (bf16[2,2,2,96,256]{4,3,0,2,1:T(8,128)(2,1)S(1)}, bf16[2,2,2,96,256]{4,3,0,2,1:T(8,128)(2,1)S(1)}, u32[]{:S(2)}, u32[]{:S(2)}) collective-permute-start(bf16[2,2,2,96,256]{4,3,0,2,1:T(8,128)(2,1)S(1)} %bitcast.227), channel_id=1, source_target_pairs={{0,1},{1,0},{2,3},{3,2},{4,5},{5,4},{6,7},{7,6},{8,9},{9,8},{10,11... | collective-permute-start | bytes 1179656 | tf_op jit(solution)/shard_map/ppermute | solution.py:16
  31.1 1.9 %collective-permute-start.4 = (bf16[2,2,2,96,256]{4,3,0,1,2:T(8,128)(2,1)S(1)}, bf16[2,2,2,96,256]{4,3,0,1,2:T(8,128)(2,1)S(1)}, u32[]{:S(2)}, u32[]{:S(2)}) collective-permute-start(bf16[2,2,2,96,256]{4,3,0,1,2:T(8,128)(2,1)S(1)} %bitcast.228), channel_id=1, source_target_pairs={{0,1},{1,0},{2,3},{3,2},{4,5},{5,4},{6,7},{7,6},{8,9},{9,8},{10,11... | collective-permute-start | bytes 1179656 | tf_op jit(solution)/shard_map/ppermute | solution.py:16
  31.9 7.2 %collective-permute-start.13 = (bf16[2,2,96,256]{3,2,0,1:T(8,128)(2,1)S(1)}, bf16[2,2,96,256]{3,2,0,1:T(8,128)(2,1)S(1)}, u32[]{:S(2)}, u32[]{:S(2)}) collective-permute-start(bf16[2,2,96,256]{3,2,0,1:T(8,128)(2,1)S(1)} %fusion.55), channel_id=1, source_target_pairs={{0,4},{1,5},{2,6},{3,7},{4,0},{5,1},{6,2},{7,3},{8,12},{9,13},{10,... | collective-permute-start | bytes 589832 | tf_op jit(solution)/shard_map/ppermute | solution.py:16
  33.1 7.8 %collective-permute-start.5 = (bf16[2,2,96,256]{3,2,0,1:T(8,128)(2,1)S(1)}, bf16[2,2,96,256]{3,2,0,1:T(8,128)(2,1)S(1)}, u32[]{:S(2)}, u32[]{:S(2)}) collective-permute-start(bf16[2,2,96,256]{3,2,0,1:T(8,128)(2,1)S(1)} %fusion.54), channel_id=1, source_target_pairs={{0,2},{1,3},{2,0},{3,1},{4,6},{5,7},{6,4},{7,5},{8,10},{9,11},{10,... | collective-permute-start | bytes 589832 | tf_op jit(solution)/shard_map/ppermute | solution.py:16
  39.2 4.7 %collective-permute-start.14 = (bf16[2,96,256]{2,1,0:T(8,128)(2,1)S(1)}, bf16[2,96,256]{2,1,0:T(8,128)(2,1)S(1)}, u32[]{:S(2)}, u32[]{:S(2)}) collective-permute-start(bf16[2,96,256]{2,1,0:T(8,128)(2,1)S(1)} %fusion.59), channel_id=1, source_target_pairs={{0,2},{1,3},{2,0},{3,1},{4,6},{5,7},{6,4},{7,5},{8,10},{9,11},{10,... | collective-permute-start | bytes 294920 | tf_op jit(solution)/shard_map/ppermute | solution.py:16
  40.9 6.3 %collective-permute-start.6 = (bf16[2,96,256]{2,1,0:T(8,128)(2,1)S(1)}, bf16[2,96,256]{2,1,0:T(8,128)(2,1)S(1)}, u32[]{:S(2)}, u32[]{:S(2)}) collective-permute-start(bf16[2,96,256]{2,1,0:T(8,128)(2,1)S(1)} %fusion.58), channel_id=1, source_target_pairs={{0,4},{1,5},{2,6},{3,7},{4,0},{5,1},{6,2},{7,3},{8,12},{9,13},{10,... | collective-permute-start | bytes 294920 | tf_op jit(solution)/shard_map/ppermute | solution.py:16
  43.9 10.0 %collective-permute-start.15 = (bf16[2,96,256]{2,1,0:T(8,128)(2,1)S(1)}, bf16[2,96,256]{2,1,0:T(8,128)(2,1)S(1)}, u32[]{:S(2)}, u32[]{:S(2)}) collective-permute-start(bf16[2,96,256]{2,1,0:T(8,128)(2,1)S(1)} %fusion.63), channel_id=1, source_target_pairs={{0,8},{1,9},{2,10},{3,11},{4,12},{5,13},{6,14},{7,15},{8,0},{9,1},... | collective-permute-start | bytes 294920 | tf_op jit(solution)/shard_map/ppermute | solution.py:16
  47.3 7.7 %collective-permute-start.7 = (bf16[2,96,256]{2,1,0:T(8,128)(2,1)S(1)}, bf16[2,96,256]{2,1,0:T(8,128)(2,1)S(1)}, u32[]{:S(2)}, u32[]{:S(2)}) collective-permute-start(bf16[2,96,256]{2,1,0:T(8,128)(2,1)S(1)} %fusion.62), channel_id=1, source_target_pairs={{0,8},{1,9},{2,10},{3,11},{4,12},{5,13},{6,14},{7,15},{8,0},{9,1},... | collective-permute-start | bytes 294920 | tf_op jit(solution)/shard_map/ppermute | solution.py:16
  55.1 4.7 %collective-permute-start.16 = (bf16[2,96,256]{2,1,0:T(8,128)(2,1)S(1)}, bf16[2,96,256]{2,1,0:T(8,128)(2,1)S(1)}, u32[]{:S(2)}, u32[]{:S(2)}) collective-permute-start(bf16[2,96,256]{2,1,0:T(8,128)(2,1)S(1)} %get-tuple-element.8), channel_id=1, source_target_pairs={{0,4},{1,5},{2,6},{3,7},{4,0},{5,1},{6,2},{7,3},{8,12},{9,13},{10,... | collective-permute-start | bytes 294920 | tf_op jit(solution)/shard_map/ppermute | solution.py:16
  55.2 6.1 %collective-permute-start.19 = (bf16[2,96,256]{2,1,0:T(8,128)(2,1)S(1)}, bf16[2,96,256]{2,1,0:T(8,128)(2,1)S(1)}, u32[]{:S(2)}, u32[]{:S(2)}) collective-permute-start(bf16[2,96,256]{2,1,0:T(8,128)(2,1)S(1)} %get-tuple-element.9), channel_id=1, source_target_pairs={{0,2},{1,3},{2,0},{3,1},{4,6},{5,7},{6,4},{7,5},{8,10},{9,11},{10,... | collective-permute-start | bytes 294920 | tf_op jit(solution)/shard_map/ppermute | solution.py:16
  59.9 5.7 %collective-permute-start.17 = (bf16[2,2,96,256]{3,2,0,1:T(8,128)(2,1)S(1)}, bf16[2,2,96,256]{3,2,0,1:T(8,128)(2,1)S(1)}, u32[]{:S(2)}, u32[]{:S(2)}) collective-permute-start(bf16[2,2,96,256]{3,2,0,1:T(8,128)(2,1)S(1)} %pad_maximum_fusion.10), channel_id=1, source_target_pairs={{0,2},{1,3},{2,0},{3,1},{4,6},{5,7},{6,4},{7,5},{8,10},{9,11},{10,... | collective-permute-start | bytes 589832 | tf_op jit(solution)/shard_map/ppermute | solution.py:16
  61.4 5.7 %collective-permute-start.20 = (bf16[2,2,96,256]{3,2,1,0:T(8,128)(2,1)S(1)}, bf16[2,2,96,256]{3,2,1,0:T(8,128)(2,1)S(1)}, u32[]{:S(2)}, u32[]{:S(2)}) collective-permute-start(bf16[2,2,96,256]{3,2,1,0:T(8,128)(2,1)S(1)} %pad_maximum_fusion.11), channel_id=1, source_target_pairs={{0,4},{1,5},{2,6},{3,7},{4,0},{5,1},{6,2},{7,3},{8,12},{9,13},{10,... | collective-permute-start | bytes 589832 | tf_op jit(solution)/shard_map/ppermute | solution.py:16
  65.7 1.8 %collective-permute-start.18 = (bf16[2,2,2,96,256]{4,3,0,1,2:T(8,128)(2,1)S(1)}, bf16[2,2,2,96,256]{4,3,0,1,2:T(8,128)(2,1)S(1)}, u32[]{:S(2)}, u32[]{:S(2)}) collective-permute-start(bf16[2,2,2,96,256]{4,3,0,1,2:T(8,128)(2,1)S(1)} %pad_maximum_fusion.6), channel_id=1, source_target_pairs={{0,1},{1,0},{2,3},{3,2},{4,5},{5,4},{6,7},{7,6},{8,9},{9,8},{10,11... | collective-permute-start | bytes 1179656 | tf_op jit(solution)/shard_map/ppermute | solution.py:16
  67.2 1.8 %collective-permute-start.21 = (bf16[2,2,2,96,256]{4,3,2,1,0:T(8,128)(2,1)S(1)}, bf16[2,2,2,96,256]{4,3,2,1,0:T(8,128)(2,1)S(1)}, u32[]{:S(2)}, u32[]{:S(2)}) collective-permute-start(bf16[2,2,2,96,256]{4,3,2,1,0:T(8,128)(2,1)S(1)} %pad_maximum_fusion.7), channel_id=1, source_target_pairs={{0,1},{1,0},{2,3},{3,2},{4,5},{5,4},{6,7},{7,6},{8,9},{9,8},{10,11... | collective-permute-start | bytes 1179656 | tf_op jit(solution)/shard_map/ppermute | solution.py:16
  73.5 4.0 %collective-permute-start.22 = (bf16[2,2,2,96,256]{4,3,2,1,0:T(8,128)(2,1)}, bf16[2,2,2,96,256]{4,3,2,1,0:T(8,128)(2,1)S(1)}, u32[]{:S(2)}, u32[]{:S(2)}) collective-permute-start(bf16[2,2,2,96,256]{4,3,2,1,0:T(8,128)(2,1)} %dynamic-slice_bitcast_fusion), channel_id=1, source_target_pairs={{0,1},{1,0},{2,3},{3,2},{4,5},{5,4},{6,7},{7,6},{8,9},{9,8},{10,11... | collective-permute-start | bytes 1179656 | tf_op jit(solution)/shard_map/ppermute | solution.py:16
  77.0 1.8 %collective-permute-start.26 = (bf16[2,2,2,96,256]{4,3,0,2,1:T(8,128)(2,1)S(1)}, bf16[2,2,2,96,256]{4,3,0,2,1:T(8,128)(2,1)S(1)}, u32[]{:S(2)}, u32[]{:S(2)}) collective-permute-start(bf16[2,2,2,96,256]{4,3,0,2,1:T(8,128)(2,1)S(1)} %bitcast.229), channel_id=1, source_target_pairs={{0,1},{1,0},{2,3},{3,2},{4,5},{5,4},{6,7},{7,6},{8,9},{9,8},{10,11... | collective-permute-start | bytes 1179656 | tf_op jit(solution)/shard_map/ppermute | solution.py:16
  77.6 7.0 %collective-permute-start.23 = (bf16[2,2,96,256]{3,2,1,0:T(8,128)(2,1)S(1)}, bf16[2,2,96,256]{3,2,1,0:T(8,128)(2,1)S(1)}, u32[]{:S(2)}, u32[]{:S(2)}) collective-permute-start(bf16[2,2,96,256]{3,2,1,0:T(8,128)(2,1)S(1)} %fusion.56), channel_id=1, source_target_pairs={{0,2},{1,3},{2,0},{3,1},{4,6},{5,7},{6,4},{7,5},{8,10},{9,11},{10,... | collective-permute-start | bytes 589832 | tf_op jit(solution)/shard_map/ppermute | solution.py:16
  79.0 14.6 %copy-start.2 = (f32[1,96]{1,0:T(1,128)S(1)}, f32[1,96]{1,0:T(1,128)}, u32[]{:S(2)}) copy-start(f32[1,96]{1,0:T(1,128)} %get-tuple-element.68) | copy-start | bytes 1156
  79.0 14.6 %copy-start.3 = (f32[1,96]{1,0:T(1,128)S(1)}, f32[1,96]{1,0:T(1,128)}, u32[]{:S(2)}) copy-start(f32[1,96]{1,0:T(1,128)} %get-tuple-element.69) | copy-start | bytes 1156
  79.0 7.3 %collective-permute-start.27 = (bf16[2,2,96,256]{3,2,0,1:T(8,128)(2,1)S(1)}, bf16[2,2,96,256]{3,2,0,1:T(8,128)(2,1)S(1)}, u32[]{:S(2)}, u32[]{:S(2)}) collective-permute-start(bf16[2,2,96,256]{3,2,0,1:T(8,128)(2,1)S(1)} %fusion.57), channel_id=1, source_target_pairs={{0,4},{1,5},{2,6},{3,7},{4,0},{5,1},{6,2},{7,3},{8,12},{9,13},{10,... | collective-permute-start | bytes 589832 | tf_op jit(solution)/shard_map/ppermute | solution.py:16
  84.7 4.7 %collective-permute-start.24 = (bf16[2,96,256]{2,1,0:T(8,128)(2,1)S(1)}, bf16[2,96,256]{2,1,0:T(8,128)(2,1)S(1)}, u32[]{:S(2)}, u32[]{:S(2)}) collective-permute-start(bf16[2,96,256]{2,1,0:T(8,128)(2,1)S(1)} %fusion.60), channel_id=1, source_target_pairs={{0,4},{1,5},{2,6},{3,7},{4,0},{5,1},{6,2},{7,3},{8,12},{9,13},{10,... | collective-permute-start | bytes 294920 | tf_op jit(solution)/shard_map/ppermute | solution.py:16
  86.4 5.6 %collective-permute-start.28 = (bf16[2,96,256]{2,1,0:T(8,128)(2,1)S(1)}, bf16[2,96,256]{2,1,0:T(8,128)(2,1)S(1)}, u32[]{:S(2)}, u32[]{:S(2)}) collective-permute-start(bf16[2,96,256]{2,1,0:T(8,128)(2,1)S(1)} %fusion.61), channel_id=1, source_target_pairs={{0,2},{1,3},{2,0},{3,1},{4,6},{5,7},{6,4},{7,5},{8,10},{9,11},{10,... | collective-permute-start | bytes 294920 | tf_op jit(solution)/shard_map/ppermute | solution.py:16
  89.4 9.3 %collective-permute-start.25 = (bf16[2,96,256]{2,1,0:T(8,128)(2,1)S(1)}, bf16[2,96,256]{2,1,0:T(8,128)(2,1)S(1)}, u32[]{:S(2)}, u32[]{:S(2)}) collective-permute-start(bf16[2,96,256]{2,1,0:T(8,128)(2,1)S(1)} %fusion.64), channel_id=1, source_target_pairs={{0,8},{1,9},{2,10},{3,11},{4,12},{5,13},{6,14},{7,15},{8,0},{9,1},... | collective-permute-start | bytes 294920 | tf_op jit(solution)/shard_map/ppermute | solution.py:16
  92.0 7.8 %collective-permute-start.29 = (bf16[2,96,256]{2,1,0:T(8,128)(2,1)S(1)}, bf16[2,96,256]{2,1,0:T(8,128)(2,1)S(1)}, u32[]{:S(2)}, u32[]{:S(2)}) collective-permute-start(bf16[2,96,256]{2,1,0:T(8,128)(2,1)S(1)} %fusion.65), channel_id=1, source_target_pairs={{0,8},{1,9},{2,10},{3,11},{4,12},{5,13},{6,14},{7,15},{8,0},{9,1},... | collective-permute-start | bytes 294920 | tf_op jit(solution)/shard_map/ppermute | solution.py:16
  99.9 1.9 %collective-permute-start.30 = (f32[256]{0:T(256)S(1)}, f32[256]{0:T(256)S(1)}, u32[]{:S(2)}, u32[]{:S(2)}) collective-permute-start(f32[256]{0:T(256)S(1)} %add.183), channel_id=1, source_target_pairs={{0,1},{1,0},{2,3},{3,2},{4,5},{5,4},{6,7},{7,6},{8,9},{9,8},{10,11... | collective-permute-start | bytes 3080 | tf_op jit(solution)/shard_map/ppermute | solution.py:16
  100.0 3.6 %collective-permute-start.31 = (f32[256]{0:T(256)S(1)}, f32[256]{0:T(256)S(1)}, u32[]{:S(2)}, u32[]{:S(2)}) collective-permute-start(f32[256]{0:T(256)S(1)} %add.183), channel_id=1, source_target_pairs={{0,2},{1,3},{2,0},{3,1},{4,6},{5,7},{6,4},{7,5},{8,10},{9,11},{10,... | collective-permute-start | bytes 3080 | tf_op jit(solution)/shard_map/ppermute | solution.py:16
  101.7 3.0 %collective-permute-start.32 = (f32[256]{0:T(256)S(1)}, f32[256]{0:T(256)S(1)}, u32[]{:S(2)}, u32[]{:S(2)}) collective-permute-start(f32[256]{0:T(256)S(1)} %add.183), channel_id=1, source_target_pairs={{0,3},{1,2},{2,1},{3,0},{4,7},{5,6},{6,5},{7,4},{8,11},{9,10},{10,... | collective-permute-start | bytes 3080 | tf_op jit(solution)/shard_map/ppermute | solution.py:16
  104.7 3.6 %collective-permute-start.33 = (f32[256]{0:T(256)S(1)}, f32[256]{0:T(256)S(1)}, u32[]{:S(2)}, u32[]{:S(2)}) collective-permute-start(f32[256]{0:T(256)S(1)} %add_add_fusion), channel_id=1, source_target_pairs={{0,4},{1,5},{2,6},{3,7},{4,0},{5,1},{6,2},{7,3},{8,12},{9,13},{10,... | collective-permute-start | bytes 3080 | tf_op jit(solution)/shard_map/ppermute | solution.py:16
